TPU v7x, 32 devices: a whole 2x2x4 slice. The times are simulated.
32 devices in a mesh: gx: 8 (over z, y), gy: 4 (over x, core).
Axes of the slice: x: 2, y: 2, z: 4, core: 2. Of those that a mesh axis runs over, the one named last changes fastest.
Arguments:
- records: bfloat16 [128, 8, 8192], P('gx', 'gy')
- kept_bins: int32 [1024], replicated, may hold values from 1 to 4095, as said below
- pair_offsets: int32 [128], replicated, may hold values from 1 to 128, as said below
Outputs:
- correlation: bfloat16 [128, 128, 512], P('gy', 'gx')
Inputs may be any that keep to these rules, and one draw needn't show every extreme that they name: `kept_bins`: 1024 different bin indices in increasing order, both 1 and 4095 among them. `pair_offsets`: each offset from 1 to 128 exactly once, in any order.
All inputs are finite; a program needn't handle non-finite values.
Results may differ from a plain program's by a relative error of at most 0.0075.
Values may be sent and summed in bfloat16 or wider, within the bound.
No kernel may reach another device: no remote copies, remote signals or barrier semaphores. Data moves between devices by JAX's collectives and lax.ppermute only.
A program may use at most 64 MiB of HBM per device.

v0:
```python
import math

import jax
import jax.numpy as jnp
from jax import lax
from jax.sharding import PartitionSpec as P

SAMPLES = 8192
LAGS = 512


def forward_table(kept_bins, first_sample, sample_count):
    sample_index = first_sample + jnp.arange(sample_count, dtype=jnp.int32)
    angles = jnp.mod(sample_index[:, None] * kept_bins[None, :], SAMPLES).astype(jnp.float32) * (
        2.0 * math.pi / SAMPLES
    )
    return jnp.concatenate([jnp.cos(angles), -jnp.sin(angles)], axis=1).astype(jnp.bfloat16)


def inverse_table(kept_bins):
    lag_index = jnp.arange(LAGS, dtype=jnp.int32) - LAGS // 2
    angles = jnp.mod(kept_bins[:, None] * lag_index[None, :], SAMPLES).astype(jnp.float32) * (
        2.0 * math.pi / SAMPLES
    )
    return jnp.stack([jnp.cos(angles), -jnp.sin(angles)], axis=0).astype(jnp.bfloat16)


def whiten(spectra):
    mean_power = jnp.mean(spectra * spectra, axis=-1, keepdims=True)
    return (spectra * lax.rsqrt(mean_power + 1e-06)).astype(jnp.bfloat16)


def add_cross(running, window_block, my_offsets, own_count):
    group_size = math.gcd(8, my_offsets.shape[0])
    own_part = window_block[:, :own_count].astype(jnp.float32)

    def one_offset(shift_by):
        theirs = lax.dynamic_slice_in_dim(window_block, shift_by, own_count, 1).astype(jnp.float32)
        real_part = jnp.sum(
            own_part[:, :, 0] * theirs[:, :, 0] + own_part[:, :, 1] * theirs[:, :, 1], axis=0
        )
        imag_part = jnp.sum(
            own_part[:, :, 1] * theirs[:, :, 0] - own_part[:, :, 0] * theirs[:, :, 1], axis=0
        )
        return jnp.stack([real_part, imag_part], axis=1)

    def one_group(group_index, carried):
        chosen = lax.dynamic_slice_in_dim(my_offsets, group_index * group_size, group_size)
        update = jax.vmap(one_offset)(chosen)
        current = lax.dynamic_slice_in_dim(carried, group_index * group_size, group_size, 0)
        return lax.dynamic_update_slice_in_dim(
            carried, current + update, group_index * group_size, 0
        )

    return lax.fori_loop(0, my_offsets.shape[0] // group_size, one_group, running)


def local(records, kept_bins, pair_offsets):
    ch_dev, win_dev, samples = records.shape
    bin_count = kept_bins.shape[0]
    band_span = pair_offsets.shape[0]
    record_rows = jnp.transpose(records, (1, 0, 2)).reshape(win_dev * ch_dev, samples)
    block_len = math.gcd(samples, 1024)

    def add_block(running, block_index):
        first_sample = block_index * block_len
        sample_block = lax.dynamic_slice_in_dim(record_rows, first_sample, block_len, 1)
        table_block = forward_table(kept_bins, first_sample, block_len)
        return (
            running + jnp.dot(sample_block, table_block, preferred_element_type=jnp.float32),
            None,
        )

    spectra, _ = lax.scan(
        add_block,
        jnp.zeros((win_dev * ch_dev, 2 * bin_count), jnp.float32),
        jnp.arange(samples // block_len, dtype=jnp.int32),
    )
    white = whiten(spectra).reshape(win_dev, ch_dev, 2, bin_count)
    off_dev = band_span // lax.axis_size("gy")
    my_offsets = lax.dynamic_slice_in_dim(pair_offsets, lax.axis_index("gy") * off_dev, off_dev)
    inverse = inverse_table(kept_bins)
    norm_scale = 0.5 / math.sqrt(win_dev * lax.axis_size("gy") * bin_count)
    freq_white = lax.all_to_all(white, "gx", split_axis=3, concat_axis=1, tiled=True)
    all_channels = freq_white.shape[1]
    empty_sum = jnp.zeros((off_dev, all_channels, 2, freq_white.shape[3]), jnp.float32)
    window_block = lax.all_gather(freq_white, "gy", axis=0, tiled=True)
    widened = jnp.concatenate(
        [
            window_block,
            jnp.zeros(
                (window_block.shape[0], band_span, 2, window_block.shape[3]), window_block.dtype
            ),
        ],
        axis=1,
    )
    cross_sum = add_cross(empty_sum, widened, my_offsets, all_channels).astype(jnp.bfloat16)
    lagged = (
        jnp.einsum(
            "ocpk,pkl->ocl",
            lax.all_to_all(cross_sum, "gx", split_axis=1, concat_axis=3, tiled=True),
            inverse,
            preferred_element_type=jnp.float32,
        )
        * norm_scale
    )
    return lagged.astype(jnp.bfloat16)


def solution(mesh):
    return jax.shard_map(
        local,
        mesh=mesh,
        in_specs=(P("gx", "gy", None), P(), P()),
        out_specs=P("gy", "gx", None),
        check_vma=False,
    )
```

profile of v0, /device:TPU:0, one launch (start us, length us, event | category | flops | bytes accessed | tf_op | source)
XLA Modules:
  0.0 338.6 jit_solution(4817101264445600556)
XLA Ops:
  0.0 1.3 copy.25
  1.4 186.5 %while.27 = (s32[]{:T(128)}, f32[32,2048]{1,0:T(8,128)S(1)}, s32[8]{0:T(128)S(1)}, bf16[32,8192]{1,0:T(8,128)(2,1)S(1)}, s32[1024]{0:T(1024)}, /*index=5*/s32[]{:T(128)}, s32[1]{0:T(128)}, s32[]{:T(128)}, s32[]{:T(128)}) while((s32[]{:T(128)}, f32[32,2048]{1,0:T(8,128)S(1)}, s32[8]{0:T(128)S(1)}, bf16[32,8192]{1,0:T(8,128)(2,1)S(1)}, ...), condition=%wide.region_1.2_spmd.clone, body=%wide.region_0.1_spmd.clone.sunk | while | flops 160564224 | bytes 8990889 | solution.py:74
  2.6 19.6 %cosine_convert_fusion.3 = (bf16[1024,1024]{1,0:T(8,128)(2,1)S(1)}, bf16[1024,1024]{1,0:T(8,128)(2,1)}) fusion(s32[1024]{0:T(1024)} %get-tuple-element.329, s32[1024]{0:T(1024)S(1)} %iota_add_fusion.3), kind=kLoop, calls=%fused_computation.26.clone.1 | loop fusion | flops 17825792 | bytes 4202496 | tf_op jit(solution)/shard_map/convert
  22.2 2.4 fusion.33
  25.9 19.6 %cosine_convert_fusion.3 = (bf16[1024,1024]{1,0:T(8,128)(2,1)S(1)}, bf16[1024,1024]{1,0:T(8,128)(2,1)}) fusion(s32[1024]{0:T(1024)} %get-tuple-element.329, s32[1024]{0:T(1024)S(1)} %iota_add_fusion.3), kind=kLoop, calls=%fused_computation.26.clone.1 | loop fusion | flops 17825792 | bytes 4202496 | tf_op jit(solution)/shard_map/convert
  45.5 2.4 fusion.33
  49.2 19.6 %cosine_convert_fusion.3 = (bf16[1024,1024]{1,0:T(8,128)(2,1)S(1)}, bf16[1024,1024]{1,0:T(8,128)(2,1)}) fusion(s32[1024]{0:T(1024)} %get-tuple-element.329, s32[1024]{0:T(1024)S(1)} %iota_add_fusion.3), kind=kLoop, calls=%fused_computation.26.clone.1 | loop fusion | flops 17825792 | bytes 4202496 | tf_op jit(solution)/shard_map/convert
  68.8 2.4 fusion.33
  72.6 19.6 %cosine_convert_fusion.3 = (bf16[1024,1024]{1,0:T(8,128)(2,1)S(1)}, bf16[1024,1024]{1,0:T(8,128)(2,1)}) fusion(s32[1024]{0:T(1024)} %get-tuple-element.329, s32[1024]{0:T(1024)S(1)} %iota_add_fusion.3), kind=kLoop, calls=%fused_computation.26.clone.1 | loop fusion | flops 17825792 | bytes 4202496 | tf_op jit(solution)/shard_map/convert
  92.2 2.4 fusion.33
  95.9 19.6 %cosine_convert_fusion.3 = (bf16[1024,1024]{1,0:T(8,128)(2,1)S(1)}, bf16[1024,1024]{1,0:T(8,128)(2,1)}) fusion(s32[1024]{0:T(1024)} %get-tuple-element.329, s32[1024]{0:T(1024)S(1)} %iota_add_fusion.3), kind=kLoop, calls=%fused_computation.26.clone.1 | loop fusion | flops 17825792 | bytes 4202496 | tf_op jit(solution)/shard_map/convert
  115.5 2.4 fusion.33
  119.2 19.6 %cosine_convert_fusion.3 = (bf16[1024,1024]{1,0:T(8,128)(2,1)S(1)}, bf16[1024,1024]{1,0:T(8,128)(2,1)}) fusion(s32[1024]{0:T(1024)} %get-tuple-element.329, s32[1024]{0:T(1024)S(1)} %iota_add_fusion.3), kind=kLoop, calls=%fused_computation.26.clone.1 | loop fusion | flops 17825792 | bytes 4202496 | tf_op jit(solution)/shard_map/convert
  138.8 2.4 fusion.33
  142.5 19.6 %cosine_convert_fusion.3 = (bf16[1024,1024]{1,0:T(8,128)(2,1)S(1)}, bf16[1024,1024]{1,0:T(8,128)(2,1)}) fusion(s32[1024]{0:T(1024)} %get-tuple-element.329, s32[1024]{0:T(1024)S(1)} %iota_add_fusion.3), kind=kLoop, calls=%fused_computation.26.clone.1 | loop fusion | flops 17825792 | bytes 4202496 | tf_op jit(solution)/shard_map/convert
  162.1 2.4 fusion.33
  165.8 19.6 %cosine_convert_fusion.3 = (bf16[1024,1024]{1,0:T(8,128)(2,1)S(1)}, bf16[1024,1024]{1,0:T(8,128)(2,1)}) fusion(s32[1024]{0:T(1024)} %get-tuple-element.329, s32[1024]{0:T(1024)S(1)} %iota_add_fusion.3), kind=kLoop, calls=%fused_computation.26.clone.1 | loop fusion | flops 17825792 | bytes 4202496 | tf_op jit(solution)/shard_map/convert
  185.4 2.4 fusion.33
  189.0 1.7 reshape.170
  190.7 7.3 %all-to-all-start = ((bf16[8,2,4096]{2,1,0:T(2,128)(2,1)}), bf16[8,2,4096]{2,1,0:T(2,128)(2,1)S(1)}, u32[]{:S(2)}, u32[]{:S(2)}) async-start(bf16[8,2,4096]{2,1,0:T(2,128)(2,1)} %reshape.170), calls=%async_computation | async-start | bytes 262144 | tf_op jit(solution)/shard_map/all_to_all | solution.py:84
  198.1 7.3 %all-to-all-done = bf16[8,2,4096]{2,1,0:T(2,128)(2,1)S(1)} async-done(((bf16[8,2,4096]{2,1,0:T(2,128)(2,1)}), bf16[8,2,4096]{2,1,0:T(2,128)(2,1)S(1)}, u32[]{:S(2)}, u32[]{:S(2)}) %all-to-all-start) | async-done | bytes 131104 | tf_op jit(solution)/shard_map/all_to_all | solution.py:84
  207.4 7.4 %all_gather.3 = bf16[8,128,2,128]{3,1,2,0:T(8,128)(2,1)S(1)} all-gather(bf16[2,128,2,128]{3,1,2,0:T(8,128)(2,1)S(1)} %bitcast.72), channel_id=1, replica_groups=mesh['gx'=8,'gy'=4] {'gy'}, dimensions={0}, use_global_device_ids=true | all-gather | bytes 655360 | tf_op jit(solution)/shard_map/all_gather | solution.py:87
  215.5 4.0 %broadcast_in_dim.19.clone = f32[32,128,2,128]{3,2,0,1:T(2,128)} broadcast(f32[]{:T(128)} %constant.119.clone.1), dimensions={} | broadcast | bytes 4194308 | tf_op jit(solution)/shard_map/broadcast_in_dim | solution.py:86
  219.6 51.1 %while.26 = (s32[]{:T(128)}, f32[32,128,2,128]{3,2,0,1:T(2,128)}, f32[8,128,2,128]{3,0,1,2:T(8,128)S(1)}, s32[32]{0:T(128)S(1)}, bf16[8,256,2,128]{3,0,2,1:T(8,1...) while((s32[]{:T(128)}, f32[32,128,2,128]{3,2,0,1:T(2,128)}, ...), condition=%wide.region_6.7_spmd, body=%wide.region_3.6_spmd.sunk | while | flops 10747950 | bytes 38797656 | solution.py:55
  219.7 3.1 gather_fusion
  222.7 2.9 convert_element_type.68
  225.7 3.1 add_reduce_fusion.2
  228.8 1.3 constant_dynamic-slice_fusion.2
  230.1 2.2 copy_dynamic-update-slice_fusion.2
  232.4 3.1 gather_fusion
  235.5 2.9 convert_element_type.68
  238.5 3.1 add_reduce_fusion.2
  242.9 2.2 copy_dynamic-update-slice_fusion.2
  245.2 3.1 gather_fusion
  248.3 2.9 convert_element_type.68
  251.3 3.1 add_reduce_fusion.2
  255.7 2.2 copy_dynamic-update-slice_fusion.2
  257.9 3.1 gather_fusion
  261.0 2.9 convert_element_type.68
  264.0 3.1 add_reduce_fusion.2
  268.4 2.2 copy_dynamic-update-slice_fusion.2
  270.6 5.5 %convert_element_type.46 = bf16[32,128,2,128]{3,2,0,1:T(2,128)(2,1)} convert(f32[32,128,2,128]{3,2,0,1:T(2,128)} %get-tuple-element.166) | non-fusion elementwise | flops 1048576 | bytes 6291456 | tf_op jit(solution)/shard_map/convert_element_type | solution.py:97
  276.1 3.8 %all-to-all-start.1 = ((bf16[32,128,2,128]{3,2,0,1:T(2,128)(2,1)}), bf16[32,128,2,128]{3,2,0,1:T(2,128)(2,1)S(1)}, u32[]{:S(2)}, u32[]{:S(2)}) async-start(bf16[32,128,2,128]{3,2,0,1:T(2,128)(2,1)} %convert_element_type.46), calls=%async_computation.1 | async-start | bytes 4194304 | tf_op jit(solution)/shard_map/all_to_all | solution.py:101
  280.0 9.8 %cosine_convert_fusion.1 = (bf16[1,1024,512]{2,1,0:T(8,128)(2,1)S(1)}, bf16[1,1024,512]{2,1,0:T(8,128)(2,1)}) fusion(s32[512]{0:T(512)S(1)} %iota_add_fusion.1, s32[1024]{0:T(1024)S(1)} %copy-done), kind=kLoop, calls=%fused_computation.46 | loop fusion | flops 8912896 | bytes 2103296 | tf_op jit(solution)/shard_map/convert.2
  289.8 38.9 %all-to-all-done.1 = bf16[32,128,2,128]{3,2,0,1:T(2,128)(2,1)S(1)} async-done(((bf16[32,128,2,128]{3,2,0,1:T(2,128)(2,1)}), bf16[32,128,2,128]{3,2,0,1:T(2,128)(2,1)S(1)}, u32[]{:S(2)}, u32[]{:S(2)}) %all-to-all-start.1) | async-done | bytes 2097184 | tf_op jit(solution)/shard_map/all_to_all | solution.py:101
  328.7 3.8 %copy.43 = bf16[32,8,16,2,128]{4,1,2,3,0:T(8,128)(2,1)} copy(bf16[32,8,16,2,128]{4,3,0,2,1:T(2,128)(2,1)S(1)} %bitcast.68) | data formatting | bytes 4194304 | tf_op jit(solution)/shard_map/all_to_all | solution.py:101
  332.5 2.8 all_to_all.33
  335.3 3.3 fusion.23
  (45 shorter events, 13.5 us)
Async XLA Ops:
  1.3 196.6 %copy-start.1 = (s32[128]{0:T(128)S(1)}, s32[128]{0:T(128)}, u32[]{:S(2)}) copy-start(s32[128]{0:T(128)} %param.9) | copy-start | bytes 1540
  190.7 14.6 %all-to-all-start = ((bf16[8,2,4096]{2,1,0:T(2,128)(2,1)}), bf16[8,2,4096]{2,1,0:T(2,128)(2,1)S(1)}, u32[]{:S(2)}, u32[]{:S(2)}) async-start(bf16[8,2,4096]{2,1,0:T(2,128)(2,1)} %reshape.170), calls=%async_computation | async-start | bytes 262144 | tf_op jit(solution)/shard_map/all_to_all | solution.py:84
  270.6 9.3 %copy-start = (s32[1024]{0:T(1024)S(1)}, s32[1024]{0:T(1024)}, u32[]{:S(2)}) copy-start(s32[1024]{0:T(1024)} %get-tuple-element.363) | copy-start | bytes 12292
  276.1 52.6 %all-to-all-start.1 = ((bf16[32,128,2,128]{3,2,0,1:T(2,128)(2,1)}), bf16[32,128,2,128]{3,2,0,1:T(2,128)(2,1)S(1)}, u32[]{:S(2)}, u32[]{:S(2)}) async-start(bf16[32,128,2,128]{3,2,0,1:T(2,128)(2,1)} %convert_element_type.46), calls=%async_computation.1 | async-start | bytes 4194304 | tf_op jit(solution)/shard_map/all_to_all | solution.py:101
where the time goes:
time: 340 us; the launch traced here: 339 us
  other arithmetic  206 us (61%)
  waiting for transfers between devices  46.2 us (14%)
  local copies, waits for them, and re-layouts  40.2 us (12%)
  matrix products  22.8 us (7%)
  starting transfers between devices  11.1 us (3%)
  blocking collectives  7.35 us (2%)
  loops' own time  5.29 us (2%)
    another operation x9, other arithmetic  167 us
    all_to_all x1, waiting for transfers between devices, local(): lax.all_to_all(cross_sum, 'gx', split_axis=1, concat_axis=3, tiled=True)  38.9 us
    dot_general x8, matrix products, add_block(): jnp.dot(sample_block, table_block, preferred_element_type=jnp.float32)  19.5 us
    reduce_sum x4, other arithmetic, one_offset(): jnp.sum(own_part[:, :, 0] * theirs[:, :, 0] + own_part[:, :, 1] * theirs[...  12.3 us
    gather x4, local copies, waits for them, and re-layouts, one_offset(): lax.dynamic_slice_in_dim(window_block, shift_by, own_count, 1)  12.2 us
    convert_element_type x4, other arithmetic, one_offset(): lax.dynamic_slice_in_dim(window_block, shift_by, own_count, 1)  11.7 us
    dynamic_update_slice x4, other arithmetic, one_group(): lax.dynamic_update_slice_in_dim(carried, current + update, group_index *...  8.8 us
    all_gather x1, blocking collectives, local(): window_block = lax.all_gather(freq_white, 'gy', axis=0, tiled=True)  7.35 us
  transfers between devices with their start and end apart: 2, of which 2 were waited for; matrix products, arithmetic and copies ran while one was open for 3% of the time, Pallas kernels for 0%

commit v1 on v0

--- a/solution.py
+++ b/solution.py
@@ -7,14 +7,6 @@
 
 SAMPLES = 8192
 LAGS = 512
-
-
-def forward_table(kept_bins, first_sample, sample_count):
-    sample_index = first_sample + jnp.arange(sample_count, dtype=jnp.int32)
-    angles = jnp.mod(sample_index[:, None] * kept_bins[None, :], SAMPLES).astype(jnp.float32) * (
-        2.0 * math.pi / SAMPLES
-    )
-    return jnp.concatenate([jnp.cos(angles), -jnp.sin(angles)], axis=1).astype(jnp.bfloat16)
 
 
 def inverse_table(kept_bins):
@@ -55,27 +47,58 @@
     return lax.fori_loop(0, my_offsets.shape[0] // group_size, one_group, running)
 
 
+def small_table(kept_bins, rows):
+    fine_count = 1 << ((rows.bit_length() - 1) // 2)
+    coarse_count = rows // fine_count
+
+    def angles(step, count):
+        index = step * jnp.arange(count, dtype=jnp.int32)
+        return jnp.mod(index[:, None] * kept_bins[None, :], SAMPLES).astype(jnp.float32) * (
+            2.0 * math.pi / SAMPLES
+        )
+
+    fine = angles(1, fine_count)[None, :, :]
+    coarse = angles(fine_count, coarse_count)[:, None, :]
+    cos_f, sin_f, cos_c, sin_c = jnp.cos(fine), jnp.sin(fine), jnp.cos(coarse), jnp.sin(coarse)
+    cos_t = cos_f * cos_c - sin_f * sin_c
+    sin_t = sin_f * cos_c + cos_f * sin_c
+    table = jnp.concatenate([cos_t, -sin_t], axis=-1)
+    return table.reshape(rows, 2 * kept_bins.shape[0]).astype(jnp.bfloat16)
+
+
+def forward_spectra(record_rows, kept_bins):
+    row_count, samples = record_rows.shape
+    bin_count = kept_bins.shape[0]
+    block_len = math.gcd(samples, 1024)
+    block_count = samples // block_len
+    x = record_rows.reshape(row_count, block_count, block_len).astype(jnp.float32)
+    br = jnp.mod(
+        jnp.arange(block_count, dtype=jnp.int32)[:, None] * jnp.arange(block_count, dtype=jnp.int32)[None, :],
+        block_count,
+    ).astype(jnp.float32) * (2.0 * math.pi / block_count)
+    twiddle = jnp.stack([jnp.cos(br), -jnp.sin(br)], axis=0)
+    y = jnp.einsum("ubs,pbr->prus", x, twiddle, precision=lax.Precision.HIGHEST)
+    y_hi = y.astype(jnp.bfloat16)
+    y_lo = (y - y_hi.astype(jnp.float32)).astype(jnp.bfloat16)
+    lhs = jnp.stack([y_hi, y_lo], axis=0).reshape(-1, block_len)
+    prod = jnp.dot(lhs, small_table(kept_bins, block_len), preferred_element_type=jnp.float32)
+    prod = prod.reshape(2, 2, block_count, row_count, 2, bin_count)
+    prod = prod[0] + prod[1]
+    pick = (
+        jnp.mod(kept_bins, block_count)[None, None, :]
+        == jnp.arange(block_count, dtype=jnp.int32)[:, None, None]
+    ).astype(jnp.float32)
+    real_part = jnp.sum(pick * (prod[0, :, :, 0] - prod[1, :, :, 1]), axis=0)
+    imag_part = jnp.sum(pick * (prod[0, :, :, 1] + prod[1, :, :, 0]), axis=0)
+    return jnp.concatenate([real_part, imag_part], axis=-1)
+
+
 def local(records, kept_bins, pair_offsets):
     ch_dev, win_dev, samples = records.shape
     bin_count = kept_bins.shape[0]
     band_span = pair_offsets.shape[0]
     record_rows = jnp.transpose(records, (1, 0, 2)).reshape(win_dev * ch_dev, samples)
-    block_len = math.gcd(samples, 1024)
-
-    def add_block(running, block_index):
-        first_sample = block_index * block_len
-        sample_block = lax.dynamic_slice_in_dim(record_rows, first_sample, block_len, 1)
-        table_block = forward_table(kept_bins, first_sample, block_len)
-        return (
-            running + jnp.dot(sample_block, table_block, preferred_element_type=jnp.float32),
-            None,
-        )
-
-    spectra, _ = lax.scan(
-        add_block,
-        jnp.zeros((win_dev * ch_dev, 2 * bin_count), jnp.float32),
-        jnp.arange(samples // block_len, dtype=jnp.int32),
-    )
+    spectra = forward_spectra(record_rows, kept_bins)
     white = whiten(spectra).reshape(win_dev, ch_dev, 2, bin_count)
     off_dev = band_span // lax.axis_size("gy")
     my_offsets = lax.dynamic_slice_in_dim(pair_offsets, lax.axis_index("gy") * off_dev, off_dev)

time: 340 us -> 181 us (0.53)
  other arithmetic: 206 us -> 63.3 us
  matrix products: 22.8 us -> 8.83 us
  loops' own time: 5.29 us -> 0.1 us
    another operation x9 -> x3, other arithmetic: 167 us -> 11.5 us
    dot_general x8 -> x2, matrix products: 19.5 us -> 5.55 us  [the longest x1 4.55 us: forward_spectra(): jnp.dot(lhs, small_table(kept_bins, block_len), preferred_element_type=jn...]
    add x8 -> x2, other arithmetic: 0.03 us -> 9.55 us  [the longest x1 6.86 us: forward_spectra(): imag_part = jnp.sum(pick * (prod[0, :, :, 1] + prod[1, :, :, 0]), axis=0)]
    add x0 -> x1, local copies, waits for them, and re-layouts: none -> 6.59 us  [forward_spectra(): prod = prod[0] + prod[1]]
    another operation x1 -> x0, loops' own time: 5.19 us -> none  [local(): lax.scan(add_block, jnp.zeros((win_dev * ch_dev, 2 * bin_count), jnp.floa...]
    dynamic_slice x8 -> x0, local copies, waits for them, and re-layouts: 4.93 us -> none  [local(): lax.scan(add_block, jnp.zeros((win_dev * ch_dev, 2 * bin_count), jnp.floa...]
  transfers between devices with their start and end apart: 2 -> 2, of which waited for: 2 -> 2; matrix products, arithmetic and copies ran while one was open for 3% -> 5% of each run, Pallas kernels for 0% -> 0%
where the time goes in v1:
time: 181 us; the launch traced here: 180 us
  other arithmetic  63.3 us (35%)
  waiting for transfers between devices  46.1 us (25%)
  local copies, waits for them, and re-layouts  43.5 us (24%)
  starting transfers between devices  11.1 us (6%)
  matrix products  8.83 us (5%)
  blocking collectives  7.18 us (4%)
    all_to_all x1, waiting for transfers between devices, local(): lax.all_to_all(cross_sum, 'gx', split_axis=1, concat_axis=3, tiled=True)  38.9 us
    reduce_sum x4, other arithmetic, one_offset(): jnp.sum(own_part[:, :, 0] * theirs[:, :, 0] + own_part[:, :, 1] * theirs[...  12.3 us
    gather x4, local copies, waits for them, and re-layouts, one_offset(): lax.dynamic_slice_in_dim(window_block, shift_by, own_count, 1)  12.2 us
    convert_element_type x4, other arithmetic, one_offset(): lax.dynamic_slice_in_dim(window_block, shift_by, own_count, 1)  11.7 us
    another operation x2, other arithmetic  11.3 us
    dynamic_update_slice x4, other arithmetic, one_group(): lax.dynamic_update_slice_in_dim(carried, current + update, group_index *...  8.78 us
    all_to_all x1, starting transfers between devices, local(): lax.all_to_all(white, 'gx', split_axis=3, concat_axis=1, tiled=True)  7.27 us
    all_to_all x1, waiting for transfers between devices, local(): lax.all_to_all(white, 'gx', split_axis=3, concat_axis=1, tiled=True)  7.26 us
  transfers between devices with their start and end apart: 2, of which 2 were waited for; matrix products, arithmetic and copies ran while one was open for 5% of the time, Pallas kernels for 0%

profile of v1, /device:TPU:0, one launch (start us, length us, event | category | flops | bytes accessed | tf_op | source)
XLA Modules:
  0.0 180.3 jit_solution(6627129745590901906)
XLA Ops:
  0.1 0.7 add_select_fusion.4
  0.8 1.7 fusion.32
  2.5 1.3 copy.39
  4.1 1.0 convert_bitcast_fusion
  5.4 1.2 copy.40
  6.5 1.5 subtract_convert_fusion
  8.0 4.5 %fusion.2 = f32[1024,2048]{1,0:T(8,128)S(1)} fusion(bf16[1024,1024]{1,0:T(8,128)(2,1)S(1)} %bitcast.101, bf16[1024,1024]{1,0:T(8,128)(2,1)S(1)} %bitcast.103, bf16[1024,1024]{1,0:T(8,128)(2,1)S(1)} %bitcast.102), kind=kOutput, calls=%fused_computation.14 | convolution fusion | flops 4303355904 | bytes 14680064 | tf_op jit(solution)/shard_map/dot_general | solution.py:84
  12.6 2.7 %slice_add_fusion = f32[512,2048]{1,0:T(8,128)} fusion(f32[1024,2048]{1,0:T(8,128)S(1)} %fusion.2), kind=kLoop, calls=%fused_computation.13 | loop fusion | flops 1048576 | bytes 12582912 | tf_op jit(solution)/shard_map/add | solution.py:86
  15.2 6.6 %add.157 = f32[2,8,32,2,1024]{4,3,2,1,0:T(2,128)} reshape(f32[512,2048]{1,0:T(8,128)} %slice_add_fusion) | data formatting | bytes 8388608 | tf_op jit(solution)/shard_map/add | solution.py:86
  21.8 6.9 %slice_add_fusion.1 = (f32[1,8,32,1,1024]{4,3,2,1,0:T(1,128)S(1)}, f32[1,8,32,1,1024]{4,3,2,1,0:T(1,128)S(1)}, f32[1,8,32,1,1024]{4,3,2,1,0:T(1,128)S(1)}) fusion(f32[2,8,32,2,1024]{4,3,2,1,0:T(2,128)} %add.157), kind=kLoop, calls=%fused_computation.41 | loop fusion | flops 262144 | bytes 7340032 | tf_op jit(solution)/shard_map/add | solution.py:92
  28.7 0.8 fusion.18
  30.1 0.8 copy.43
  30.9 1.7 reshape.414
  32.7 7.3 %all-to-all-start = ((bf16[8,2,4096]{2,1,0:T(2,128)(2,1)}), bf16[8,2,4096]{2,1,0:T(2,128)(2,1)S(1)}, u32[]{:S(2)}, u32[]{:S(2)}) async-start(bf16[8,2,4096]{2,1,0:T(2,128)(2,1)} %reshape.414), calls=%async_computation | async-start | bytes 262144 | tf_op jit(solution)/shard_map/all_to_all | solution.py:107
  40.0 7.3 %all-to-all-done = bf16[8,2,4096]{2,1,0:T(2,128)(2,1)S(1)} async-done(((bf16[8,2,4096]{2,1,0:T(2,128)(2,1)}), bf16[8,2,4096]{2,1,0:T(2,128)(2,1)S(1)}, u32[]{:S(2)}, u32[]{:S(2)}) %all-to-all-start) | async-done | bytes 131104 | tf_op jit(solution)/shard_map/all_to_all | solution.py:107
  47.3 0.7 reshape.415
  48.0 1.3 copy.53
  49.3 7.2 %all_gather.3 = bf16[8,128,2,128]{3,1,2,0:T(8,128)(2,1)S(1)} all-gather(bf16[2,128,2,128]{3,1,2,0:T(8,128)(2,1)S(1)} %bitcast.105), channel_id=1, replica_groups=mesh['gx'=8,'gy'=4] {'gy'}, dimensions={0}, use_global_device_ids=true | all-gather | bytes 655360 | tf_op jit(solution)/shard_map/all_gather | solution.py:110
  56.5 0.3 copy.64
  57.3 4.0 %broadcast_in_dim.8.clone = f32[32,128,2,128]{3,2,0,1:T(2,128)} broadcast(f32[]{:T(128)} %constant.108.clone.1), dimensions={} | broadcast | bytes 4194308 | tf_op jit(solution)/shard_map/broadcast_in_dim | solution.py:109
  61.3 51.1 %while.13 = (s32[]{:T(128)}, f32[32,128,2,128]{3,2,0,1:T(2,128)}, f32[8,128,2,128]{3,0,1,2:T(8,128)S(1)}, s32[32]{0:T(128)S(1)}, bf16[8,256,2,128]{3,0,2,1:T(8,1...) while((s32[]{:T(128)}, f32[32,128,2,128]{3,2,0,1:T(2,128)}, ...), condition=%wide.region_6.7_spmd, body=%wide.region_3.6_spmd.sunk | while | flops 10747950 | bytes 38797656 | solution.py:47
  61.4 3.1 %gather_fusion = bf16[8,8,128,2,128]{4,1,3,2,0:T(8,128)(2,1)} fusion(bf16[8,256,2,128]{3,0,2,1:T(8,128)(2,1)S(1)} %get-tuple-element.219, s32[8]{0:T(128)S(1)} %fusion.52), kind=kCustom, calls=%fused_computation.clone.1 | custom fusion | bytes 8388736 | tf_op jit(solution)/shard_map/while/body/eval_jaxpr/vmap()/gather | solution.py:30
  64.5 2.9 %convert_element_type.142 = f32[8,8,128,2,128]{4,1,3,2,0:T(8,128)S(1)} convert(bf16[8,8,128,2,128]{4,1,3,2,0:T(8,128)(2,1)} %gather_fusion) | non-fusion elementwise | flops 2097152 | bytes 12582912 | tf_op jit(solution)/shard_map/while/body/eval_jaxpr/vmap()/convert_element_type | solution.py:30
  67.5 3.1 %add_reduce_fusion.2 = (f32[8,128,128]{2,1,0:T(8,128)S(1)}, f32[8,128,128]{2,1,0:T(8,128)S(1)}) fusion(f32[8,8,128,2,128]{4,1,3,2,0:T(8,128)S(1)} %convert_element_type.142, f32[8,128,128]{2,0,1:T(8,128)S(1)} %get-tuple-element.193, f32[8,128,128]{2,0,1:T(8,128)S(1)} %get-tuple-element.194), kind=kLoop, calls=%fused_computation.4.clone.1 | loop fusion | flops 8126464 | bytes 10485760 | tf_op jit(solution)/shard_map/while/body/eval_jaxpr/vmap()/reduce_sum | solution.py:31
  70.6 1.3 constant_dynamic-slice_fusion.2
  71.9 2.2 %copy_dynamic-update-slice_fusion.2 = f32[32,128,2,128]{3,2,0,1:T(2,128)} fusion(f32[32,128,2,128]{3,2,0,1:T(2,128)} %get-tuple-element.207, s32[]{:T(128)S(6)} %select_n.137, f32[8,128,1,128]{3,2,1,0:T(1,128)S(1)} %bitcast.95, f32[8,128,1,128]{3,2,1,0:T(1,128)S(1)} %bitcast.94, f32[8,128,2,128]{3,2,0,1:T(2,128)S(1)} %constant_dynamic-slice_fusion.2), kind=kLoop, calls=%fused_computation.6.clone.1 | loop fusion | flops 524288 | bytes 3145732 | tf_op jit(solution)/shard_map/while/body/eval_jaxpr/dynamic_update_slice | solution.py:43
  74.2 3.1 %gather_fusion = bf16[8,8,128,2,128]{4,1,3,2,0:T(8,128)(2,1)} fusion(bf16[8,256,2,128]{3,0,2,1:T(8,128)(2,1)S(1)} %get-tuple-element.219, s32[8]{0:T(128)S(1)} %fusion.52), kind=kCustom, calls=%fused_computation.clone.1 | custom fusion | bytes 8388736 | tf_op jit(solution)/shard_map/while/body/eval_jaxpr/vmap()/gather | solution.py:30
  77.2 2.9 %convert_element_type.142 = f32[8,8,128,2,128]{4,1,3,2,0:T(8,128)S(1)} convert(bf16[8,8,128,2,128]{4,1,3,2,0:T(8,128)(2,1)} %gather_fusion) | non-fusion elementwise | flops 2097152 | bytes 12582912 | tf_op jit(solution)/shard_map/while/body/eval_jaxpr/vmap()/convert_element_type | solution.py:30
  80.2 3.1 %add_reduce_fusion.2 = (f32[8,128,128]{2,1,0:T(8,128)S(1)}, f32[8,128,128]{2,1,0:T(8,128)S(1)}) fusion(f32[8,8,128,2,128]{4,1,3,2,0:T(8,128)S(1)} %convert_element_type.142, f32[8,128,128]{2,0,1:T(8,128)S(1)} %get-tuple-element.193, f32[8,128,128]{2,0,1:T(8,128)S(1)} %get-tuple-element.194), kind=kLoop, calls=%fused_computation.4.clone.1 | loop fusion | flops 8126464 | bytes 10485760 | tf_op jit(solution)/shard_map/while/body/eval_jaxpr/vmap()/reduce_sum | solution.py:31
  83.3 1.3 constant_dynamic-slice_fusion.2
  84.7 2.2 %copy_dynamic-update-slice_fusion.2 = f32[32,128,2,128]{3,2,0,1:T(2,128)} fusion(f32[32,128,2,128]{3,2,0,1:T(2,128)} %get-tuple-element.207, s32[]{:T(128)S(6)} %select_n.137, f32[8,128,1,128]{3,2,1,0:T(1,128)S(1)} %bitcast.95, f32[8,128,1,128]{3,2,1,0:T(1,128)S(1)} %bitcast.94, f32[8,128,2,128]{3,2,0,1:T(2,128)S(1)} %constant_dynamic-slice_fusion.2), kind=kLoop, calls=%fused_computation.6.clone.1 | loop fusion | flops 524288 | bytes 3145732 | tf_op jit(solution)/shard_map/while/body/eval_jaxpr/dynamic_update_slice | solution.py:43
  86.9 3.1 %gather_fusion = bf16[8,8,128,2,128]{4,1,3,2,0:T(8,128)(2,1)} fusion(bf16[8,256,2,128]{3,0,2,1:T(8,128)(2,1)S(1)} %get-tuple-element.219, s32[8]{0:T(128)S(1)} %fusion.52), kind=kCustom, calls=%fused_computation.clone.1 | custom fusion | bytes 8388736 | tf_op jit(solution)/shard_map/while/body/eval_jaxpr/vmap()/gather | solution.py:30
  90.0 2.9 %convert_element_type.142 = f32[8,8,128,2,128]{4,1,3,2,0:T(8,128)S(1)} convert(bf16[8,8,128,2,128]{4,1,3,2,0:T(8,128)(2,1)} %gather_fusion) | non-fusion elementwise | flops 2097152 | bytes 12582912 | tf_op jit(solution)/shard_map/while/body/eval_jaxpr/vmap()/convert_element_type | solution.py:30
  93.0 3.1 %add_reduce_fusion.2 = (f32[8,128,128]{2,1,0:T(8,128)S(1)}, f32[8,128,128]{2,1,0:T(8,128)S(1)}) fusion(f32[8,8,128,2,128]{4,1,3,2,0:T(8,128)S(1)} %convert_element_type.142, f32[8,128,128]{2,0,1:T(8,128)S(1)} %get-tuple-element.193, f32[8,128,128]{2,0,1:T(8,128)S(1)} %get-tuple-element.194), kind=kLoop, calls=%fused_computation.4.clone.1 | loop fusion | flops 8126464 | bytes 10485760 | tf_op jit(solution)/shard_map/while/body/eval_jaxpr/vmap()/reduce_sum | solution.py:31
  96.1 1.3 constant_dynamic-slice_fusion.2
  97.4 2.2 %copy_dynamic-update-slice_fusion.2 = f32[32,128,2,128]{3,2,0,1:T(2,128)} fusion(f32[32,128,2,128]{3,2,0,1:T(2,128)} %get-tuple-element.207, s32[]{:T(128)S(6)} %select_n.137, f32[8,128,1,128]{3,2,1,0:T(1,128)S(1)} %bitcast.95, f32[8,128,1,128]{3,2,1,0:T(1,128)S(1)} %bitcast.94, f32[8,128,2,128]{3,2,0,1:T(2,128)S(1)} %constant_dynamic-slice_fusion.2), kind=kLoop, calls=%fused_computation.6.clone.1 | loop fusion | flops 524288 | bytes 3145732 | tf_op jit(solution)/shard_map/while/body/eval_jaxpr/dynamic_update_slice | solution.py:43
  99.7 3.1 %gather_fusion = bf16[8,8,128,2,128]{4,1,3,2,0:T(8,128)(2,1)} fusion(bf16[8,256,2,128]{3,0,2,1:T(8,128)(2,1)S(1)} %get-tuple-element.219, s32[8]{0:T(128)S(1)} %fusion.52), kind=kCustom, calls=%fused_computation.clone.1 | custom fusion | bytes 8388736 | tf_op jit(solution)/shard_map/while/body/eval_jaxpr/vmap()/gather | solution.py:30
  102.8 2.9 %convert_element_type.142 = f32[8,8,128,2,128]{4,1,3,2,0:T(8,128)S(1)} convert(bf16[8,8,128,2,128]{4,1,3,2,0:T(8,128)(2,1)} %gather_fusion) | non-fusion elementwise | flops 2097152 | bytes 12582912 | tf_op jit(solution)/shard_map/while/body/eval_jaxpr/vmap()/convert_element_type | solution.py:30
  105.8 3.1 %add_reduce_fusion.2 = (f32[8,128,128]{2,1,0:T(8,128)S(1)}, f32[8,128,128]{2,1,0:T(8,128)S(1)}) fusion(f32[8,8,128,2,128]{4,1,3,2,0:T(8,128)S(1)} %convert_element_type.142, f32[8,128,128]{2,0,1:T(8,128)S(1)} %get-tuple-element.193, f32[8,128,128]{2,0,1:T(8,128)S(1)} %get-tuple-element.194), kind=kLoop, calls=%fused_computation.4.clone.1 | loop fusion | flops 8126464 | bytes 10485760 | tf_op jit(solution)/shard_map/while/body/eval_jaxpr/vmap()/reduce_sum | solution.py:31
  108.9 1.3 constant_dynamic-slice_fusion.2
  110.2 2.2 %copy_dynamic-update-slice_fusion.2 = f32[32,128,2,128]{3,2,0,1:T(2,128)} fusion(f32[32,128,2,128]{3,2,0,1:T(2,128)} %get-tuple-element.207, s32[]{:T(128)S(6)} %select_n.137, f32[8,128,1,128]{3,2,1,0:T(1,128)S(1)} %bitcast.95, f32[8,128,1,128]{3,2,1,0:T(1,128)S(1)} %bitcast.94, f32[8,128,2,128]{3,2,0,1:T(2,128)S(1)} %constant_dynamic-slice_fusion.2), kind=kLoop, calls=%fused_computation.6.clone.1 | loop fusion | flops 524288 | bytes 3145732 | tf_op jit(solution)/shard_map/while/body/eval_jaxpr/dynamic_update_slice | solution.py:43
  112.4 5.5 %convert_element_type.99 = bf16[32,128,2,128]{3,2,0,1:T(2,128)(2,1)} convert(f32[32,128,2,128]{3,2,0,1:T(2,128)} %get-tuple-element.99) | non-fusion elementwise | flops 1048576 | bytes 6291456 | tf_op jit(solution)/shard_map/convert_element_type | solution.py:120
  117.9 3.9 %all-to-all-start.1 = ((bf16[32,128,2,128]{3,2,0,1:T(2,128)(2,1)}), bf16[32,128,2,128]{3,2,0,1:T(2,128)(2,1)S(1)}, u32[]{:S(2)}, u32[]{:S(2)}) async-start(bf16[32,128,2,128]{3,2,0,1:T(2,128)(2,1)} %convert_element_type.99), calls=%async_computation.1 | async-start | bytes 4194304 | tf_op jit(solution)/shard_map/all_to_all | solution.py:124
  121.8 9.8 %cosine_convert_fusion = (bf16[1,1024,512]{2,1,0:T(8,128)(2,1)S(1)}, bf16[1,1024,512]{2,1,0:T(8,128)(2,1)}) fusion(s32[512]{0:T(512)S(1)} %iota_add_fusion, s32[1024]{0:T(1024)S(1)} %copy-done), kind=kLoop, calls=%fused_computation.35 | loop fusion | flops 8912896 | bytes 2103296 | tf_op jit(solution)/shard_map/convert
  131.6 38.9 %all-to-all-done.1 = bf16[32,128,2,128]{3,2,0,1:T(2,128)(2,1)S(1)} async-done(((bf16[32,128,2,128]{3,2,0,1:T(2,128)(2,1)}), bf16[32,128,2,128]{3,2,0,1:T(2,128)(2,1)S(1)}, u32[]{:S(2)}, u32[]{:S(2)}) %all-to-all-start.1) | async-done | bytes 2097184 | tf_op jit(solution)/shard_map/all_to_all | solution.py:124
  170.5 3.8 %copy.79 = bf16[32,8,16,2,128]{4,1,2,3,0:T(8,128)(2,1)} copy(bf16[32,8,16,2,128]{4,3,0,2,1:T(2,128)(2,1)S(1)} %bitcast.96) | data formatting | bytes 4194304 | tf_op jit(solution)/shard_map/all_to_all | solution.py:124
  174.2 2.8 %all_to_all.33 = bf16[32,16,2,1024]{3,1,2,0:T(8,128)(2,1)S(1)} reshape(bf16[32,16,2,8,128]{4,3,1,2,0:T(8,128)(2,1)} %bitcast.97) | data formatting | bytes 4194304 | tf_op jit(solution)/shard_map/all_to_all | solution.py:124
  177.1 3.3 %fusion.14 = bf16[32,16,512]{2,1,0:T(8,128)(2,1)} fusion(bf16[32,16,2,1024]{3,1,2,0:T(8,128)(2,1)S(1)} %all_to_all.33, bf16[1,1024,512]{2,1,0:T(8,128)(2,1)} %get-tuple-element.151, bf16[1,1024,512]{2,1,0:T(8,128)(2,1)S(1)} %get-tuple-element.150), kind=kOutput, calls=%fused_computation.39 | convolution fusion | flops 1075314688 | bytes 4718592 | tf_op jit(solution)/shard_map/ocpk,pkl->ocl/dot_general | solution.py:122
  (26 shorter events, 2.3 us)
Async XLA Ops:
  28.7 11.2 %copy-start.1 = (s32[128]{0:T(128)S(1)}, s32[128]{0:T(128)}, u32[]{:S(2)}) copy-start(s32[128]{0:T(128)} %param.7) | copy-start | bytes 1540
  32.7 14.6 %all-to-all-start = ((bf16[8,2,4096]{2,1,0:T(2,128)(2,1)}), bf16[8,2,4096]{2,1,0:T(2,128)(2,1)S(1)}, u32[]{:S(2)}, u32[]{:S(2)}) async-start(bf16[8,2,4096]{2,1,0:T(2,128)(2,1)} %reshape.414), calls=%async_computation | async-start | bytes 262144 | tf_op jit(solution)/shard_map/all_to_all | solution.py:107
  112.4 9.4 %copy-start = (s32[1024]{0:T(1024)S(1)}, s32[1024]{0:T(1024)}, u32[]{:S(2)}) copy-start(s32[1024]{0:T(1024)} %param.6) | copy-start | bytes 12292
  117.9 52.6 %all-to-all-start.1 = ((bf16[32,128,2,128]{3,2,0,1:T(2,128)(2,1)}), bf16[32,128,2,128]{3,2,0,1:T(2,128)(2,1)S(1)}, u32[]{:S(2)}, u32[]{:S(2)}) async-start(bf16[32,128,2,128]{3,2,0,1:T(2,128)(2,1)} %convert_element_type.99), calls=%async_computation.1 | async-start | bytes 4194304 | tf_op jit(solution)/shard_map/all_to_all | solution.py:124

commit v2 on v1

--- a/solution.py
+++ b/solution.py
@@ -69,14 +69,14 @@
 def forward_spectra(record_rows, kept_bins):
     row_count, samples = record_rows.shape
     bin_count = kept_bins.shape[0]
-    block_len = math.gcd(samples, 1024)
-    block_count = samples // block_len
+    block_count = 4
+    block_len = samples // block_count
     x = record_rows.reshape(row_count, block_count, block_len).astype(jnp.float32)
     br = jnp.mod(
         jnp.arange(block_count, dtype=jnp.int32)[:, None] * jnp.arange(block_count, dtype=jnp.int32)[None, :],
         block_count,
     ).astype(jnp.float32) * (2.0 * math.pi / block_count)
-    twiddle = jnp.stack([jnp.cos(br), -jnp.sin(br)], axis=0)
+    twiddle = jnp.round(jnp.stack([jnp.cos(br), -jnp.sin(br)], axis=0))
     y = jnp.einsum("ubs,pbr->prus", x, twiddle, precision=lax.Precision.HIGHEST)
     y_hi = y.astype(jnp.bfloat16)
     y_lo = (y - y_hi.astype(jnp.float32)).astype(jnp.bfloat16)

time: 181 us -> 177 us (0.978)
  local copies, waits for them, and re-layouts: 43.5 us -> 39.8 us
    add x1, local copies, waits for them, and re-layouts: 6.59 us -> 2.82 us  [forward_spectra(): prod = prod[0] + prod[1]]
    add x1, other arithmetic: 6.86 us -> 3.88 us  [forward_spectra(): imag_part = jnp.sum(pick * (prod[0, :, :, 1] + prod[1, :, :, 0]), axis=0)]
    another operation x2, other arithmetic: 11.3 us -> 13.8 us
    add x1, other arithmetic: 2.69 us -> 0.3 us  [forward_spectra(): prod = prod[0] + prod[1]]
  transfers between devices with their start and end apart: 2 -> 2, of which waited for: 2 -> 2; matrix products, arithmetic and copies ran while one was open for 5% -> 6% of each run, Pallas kernels for 0% -> 0%
where the time goes in v2:
time: 177 us; the launch traced here: 176 us
  other arithmetic  61.9 us (35%)
  waiting for transfers between devices  46.1 us (26%)
  local copies, waits for them, and re-layouts  39.8 us (22%)
  starting transfers between devices  11.1 us (6%)
  matrix products  9.67 us (5%)
  blocking collectives  7.4 us (4%)
    all_to_all x1, waiting for transfers between devices, local(): lax.all_to_all(cross_sum, 'gx', split_axis=1, concat_axis=3, tiled=True)  38.9 us
    another operation x2, other arithmetic  13.8 us
    reduce_sum x4, other arithmetic, one_offset(): jnp.sum(own_part[:, :, 0] * theirs[:, :, 0] + own_part[:, :, 1] * theirs[...  12.3 us
    gather x4, local copies, waits for them, and re-layouts, one_offset(): lax.dynamic_slice_in_dim(window_block, shift_by, own_count, 1)  12.2 us
    convert_element_type x4, other arithmetic, one_offset(): lax.dynamic_slice_in_dim(window_block, shift_by, own_count, 1)  11.7 us
    dynamic_update_slice x4, other arithmetic, one_group(): lax.dynamic_update_slice_in_dim(carried, current + update, group_index *...  8.8 us
    all_gather x1, blocking collectives, local(): window_block = lax.all_gather(freq_white, 'gy', axis=0, tiled=True)  7.4 us
    all_to_all x1, starting transfers between devices, local(): lax.all_to_all(white, 'gx', split_axis=3, concat_axis=1, tiled=True)  7.28 us
  transfers between devices with their start and end apart: 2, of which 2 were waited for; matrix products, arithmetic and copies ran while one was open for 6% of the time, Pallas kernels for 0%

profile of v2, /device:TPU:0, one launch (start us, length us, event | category | flops | bytes accessed | tf_op | source)
XLA Modules:
  0.0 176.3 jit_solution(10215648564440943071)
XLA Ops:
  0.1 1.2 fusion.32
  1.3 0.7 add_select_fusion.3
  2.0 1.3 copy.39
  3.3 0.4 reshape.410
  3.7 1.8 %convert_bitcast_fusion = (bf16[1,2,4,32,2048]{4,2,3,1,0:T(4,128)(2,1)S(1)}, bf16[1,2,4,32,2048]{4,2,3,1,0:T(4,128)(2,1)S(1)}) fusion(bf16[32,4,2048,1]{2,1,0,3:T(4,128)(2,1)S(1)} %reshape.410, f32[1,4,4]{1,2,0:T(4,128)S(1)} %get-tuple-element.156, f32[1,4,4]{1,2,0:T(4,128)S(1)} %get-tuple-element.157), kind=kOutput, calls=%fused_computation.48 | convolution fusion | flops 27263040 | bytes 2621568 | tf_op jit(solution)/shard_map/ubs,pbr->prus/dot_general | solution.py:80
  5.6 1.5 pad_maximum_fusion
  7.0 1.2 copy.40
  8.2 1.1 fusion.27
  9.3 4.0 %subtract_convert_fusion = (bf16[64,32,1024]{2,1,0:T(8,128)(2,1)S(1)}, bf16[64,32,1024]{2,1,0:T(8,128)(2,1)S(1)}) fusion(f32[64,1024]{1,0:T(8,128)S(1)} %get-tuple-element.153, f32[32,1024]{1,0:T(8,128)S(1)} %get-tuple-element.155, f32[64,1024]{1,0:T(8,128)S(1)} %get-tuple-element.152, f32[32,1024]{1,0:T(8,128)S(1)} %get-tuple-element.154), kind=kLoop, calls=%fused_computation.18 | loop fusion | flops 18874368 | bytes 9175040 | tf_op jit(solution)/shard_map/convert.5
  13.3 4.6 %fusion.2 = f32[512,2048]{1,0:T(8,128)S(1)} fusion(bf16[512,2048]{1,0:T(8,128)(2,1)S(1)} %bitcast.97, bf16[2048,1024]{1,0:T(8,128)(2,1)S(1)} %bitcast.96, bf16[2048,1024]{1,0:T(8,128)(2,1)S(1)} %bitcast.95), kind=kOutput, calls=%fused_computation.13 | convolution fusion | flops 4311744512 | bytes 14680064 | tf_op jit(solution)/shard_map/dot_general | solution.py:84
  18.2 2.8 %add.159 = f32[2,4,32,2,1024]{4,3,2,1,0:T(2,128)} reshape(f32[256,2048]{1,0:T(8,128)S(1)} %slice_add_fusion) | data formatting | bytes 4194304 | tf_op jit(solution)/shard_map/add | solution.py:86
  21.0 3.9 %slice_add_fusion.1 = (f32[1,4,32,1,1024]{4,3,2,1,0:T(1,128)S(1)}, f32[1,4,32,1,1024]{4,3,2,1,0:T(1,128)S(1)}, f32[1,4,32,1,1024]{4,3,2,1,0:T(1,128)S(1)}) fusion(f32[2,4,32,2,1024]{4,3,2,1,0:T(2,128)} %add.159), kind=kLoop, calls=%fused_computation.41 | loop fusion | flops 131072 | bytes 3670016 | tf_op jit(solution)/shard_map/add | solution.py:92
  25.9 0.8 copy.43
  26.7 1.7 reshape.414
  28.4 7.3 %all-to-all-start = ((bf16[8,2,4096]{2,1,0:T(2,128)(2,1)}), bf16[8,2,4096]{2,1,0:T(2,128)(2,1)S(1)}, u32[]{:S(2)}, u32[]{:S(2)}) async-start(bf16[8,2,4096]{2,1,0:T(2,128)(2,1)} %reshape.414), calls=%async_computation | async-start | bytes 262144 | tf_op jit(solution)/shard_map/all_to_all | solution.py:107
  35.8 7.3 %all-to-all-done = bf16[8,2,4096]{2,1,0:T(2,128)(2,1)S(1)} async-done(((bf16[8,2,4096]{2,1,0:T(2,128)(2,1)}), bf16[8,2,4096]{2,1,0:T(2,128)(2,1)S(1)}, u32[]{:S(2)}, u32[]{:S(2)}) %all-to-all-start) | async-done | bytes 131104 | tf_op jit(solution)/shard_map/all_to_all | solution.py:107
  43.1 0.7 reshape.415
  43.8 1.3 copy.53
  45.1 7.4 %all_gather.3 = bf16[8,128,2,128]{3,1,2,0:T(8,128)(2,1)S(1)} all-gather(bf16[2,128,2,128]{3,1,2,0:T(8,128)(2,1)S(1)} %bitcast.98), channel_id=1, replica_groups=mesh['gx'=8,'gy'=4] {'gy'}, dimensions={0}, use_global_device_ids=true | all-gather | bytes 655360 | tf_op jit(solution)/shard_map/all_gather | solution.py:110
  53.3 4.0 %broadcast_in_dim.8.clone = f32[32,128,2,128]{3,2,0,1:T(2,128)} broadcast(f32[]{:T(128)} %constant.112.clone.1), dimensions={} | broadcast | bytes 4194308 | tf_op jit(solution)/shard_map/broadcast_in_dim | solution.py:109
  57.3 51.1 %while.13 = (s32[]{:T(128)}, f32[32,128,2,128]{3,2,0,1:T(2,128)}, f32[8,128,2,128]{3,0,1,2:T(8,128)S(1)}, s32[32]{0:T(128)S(1)}, bf16[8,256,2,128]{3,0,2,1:T(8,1...) while((s32[]{:T(128)}, f32[32,128,2,128]{3,2,0,1:T(2,128)}, ...), condition=%wide.region_6.7_spmd, body=%wide.region_3.6_spmd.sunk | while | flops 10747950 | bytes 38797656 | solution.py:47
  57.4 3.1 %gather_fusion = bf16[8,8,128,2,128]{4,1,3,2,0:T(8,128)(2,1)} fusion(bf16[8,256,2,128]{3,0,2,1:T(8,128)(2,1)S(1)} %get-tuple-element.219, s32[8]{0:T(128)S(1)} %fusion.53), kind=kCustom, calls=%fused_computation.clone.1 | custom fusion | bytes 8388736 | tf_op jit(solution)/shard_map/while/body/eval_jaxpr/vmap()/gather | solution.py:30
  60.5 2.9 %convert_element_type.142 = f32[8,8,128,2,128]{4,1,3,2,0:T(8,128)S(1)} convert(bf16[8,8,128,2,128]{4,1,3,2,0:T(8,128)(2,1)} %gather_fusion) | non-fusion elementwise | flops 2097152 | bytes 12582912 | tf_op jit(solution)/shard_map/while/body/eval_jaxpr/vmap()/convert_element_type | solution.py:30
  63.5 3.1 %add_reduce_fusion.2 = (f32[8,128,128]{2,1,0:T(8,128)S(1)}, f32[8,128,128]{2,1,0:T(8,128)S(1)}) fusion(f32[8,8,128,2,128]{4,1,3,2,0:T(8,128)S(1)} %convert_element_type.142, f32[8,128,128]{2,0,1:T(8,128)S(1)} %get-tuple-element.193, f32[8,128,128]{2,0,1:T(8,128)S(1)} %get-tuple-element.194), kind=kLoop, calls=%fused_computation.4.clone.1 | loop fusion | flops 8126464 | bytes 10485760 | tf_op jit(solution)/shard_map/while/body/eval_jaxpr/vmap()/reduce_sum | solution.py:31
  66.6 1.3 constant_dynamic-slice_fusion.2
  67.9 2.2 %copy_dynamic-update-slice_fusion.2 = f32[32,128,2,128]{3,2,0,1:T(2,128)} fusion(f32[32,128,2,128]{3,2,0,1:T(2,128)} %get-tuple-element.207, s32[]{:T(128)S(6)} %select_n.139, f32[8,128,1,128]{3,2,1,0:T(1,128)S(1)} %bitcast.90, f32[8,128,1,128]{3,2,1,0:T(1,128)S(1)} %bitcast.89, f32[8,128,2,128]{3,2,0,1:T(2,128)S(1)} %constant_dynamic-slice_fusion.2), kind=kLoop, calls=%fused_computation.6.clone.1 | loop fusion | flops 524288 | bytes 3145732 | tf_op jit(solution)/shard_map/while/body/eval_jaxpr/dynamic_update_slice | solution.py:43
  70.2 3.1 %gather_fusion = bf16[8,8,128,2,128]{4,1,3,2,0:T(8,128)(2,1)} fusion(bf16[8,256,2,128]{3,0,2,1:T(8,128)(2,1)S(1)} %get-tuple-element.219, s32[8]{0:T(128)S(1)} %fusion.53), kind=kCustom, calls=%fused_computation.clone.1 | custom fusion | bytes 8388736 | tf_op jit(solution)/shard_map/while/body/eval_jaxpr/vmap()/gather | solution.py:30
  73.2 2.9 %convert_element_type.142 = f32[8,8,128,2,128]{4,1,3,2,0:T(8,128)S(1)} convert(bf16[8,8,128,2,128]{4,1,3,2,0:T(8,128)(2,1)} %gather_fusion) | non-fusion elementwise | flops 2097152 | bytes 12582912 | tf_op jit(solution)/shard_map/while/body/eval_jaxpr/vmap()/convert_element_type | solution.py:30
  76.3 3.1 %add_reduce_fusion.2 = (f32[8,128,128]{2,1,0:T(8,128)S(1)}, f32[8,128,128]{2,1,0:T(8,128)S(1)}) fusion(f32[8,8,128,2,128]{4,1,3,2,0:T(8,128)S(1)} %convert_element_type.142, f32[8,128,128]{2,0,1:T(8,128)S(1)} %get-tuple-element.193, f32[8,128,128]{2,0,1:T(8,128)S(1)} %get-tuple-element.194), kind=kLoop, calls=%fused_computation.4.clone.1 | loop fusion | flops 8126464 | bytes 10485760 | tf_op jit(solution)/shard_map/while/body/eval_jaxpr/vmap()/reduce_sum | solution.py:31
  79.4 1.3 constant_dynamic-slice_fusion.2
  80.7 2.2 %copy_dynamic-update-slice_fusion.2 = f32[32,128,2,128]{3,2,0,1:T(2,128)} fusion(f32[32,128,2,128]{3,2,0,1:T(2,128)} %get-tuple-element.207, s32[]{:T(128)S(6)} %select_n.139, f32[8,128,1,128]{3,2,1,0:T(1,128)S(1)} %bitcast.90, f32[8,128,1,128]{3,2,1,0:T(1,128)S(1)} %bitcast.89, f32[8,128,2,128]{3,2,0,1:T(2,128)S(1)} %constant_dynamic-slice_fusion.2), kind=kLoop, calls=%fused_computation.6.clone.1 | loop fusion | flops 524288 | bytes 3145732 | tf_op jit(solution)/shard_map/while/body/eval_jaxpr/dynamic_update_slice | solution.py:43
  83.0 3.1 %gather_fusion = bf16[8,8,128,2,128]{4,1,3,2,0:T(8,128)(2,1)} fusion(bf16[8,256,2,128]{3,0,2,1:T(8,128)(2,1)S(1)} %get-tuple-element.219, s32[8]{0:T(128)S(1)} %fusion.53), kind=kCustom, calls=%fused_computation.clone.1 | custom fusion | bytes 8388736 | tf_op jit(solution)/shard_map/while/body/eval_jaxpr/vmap()/gather | solution.py:30
  86.0 2.9 %convert_element_type.142 = f32[8,8,128,2,128]{4,1,3,2,0:T(8,128)S(1)} convert(bf16[8,8,128,2,128]{4,1,3,2,0:T(8,128)(2,1)} %gather_fusion) | non-fusion elementwise | flops 2097152 | bytes 12582912 | tf_op jit(solution)/shard_map/while/body/eval_jaxpr/vmap()/convert_element_type | solution.py:30
  89.0 3.1 %add_reduce_fusion.2 = (f32[8,128,128]{2,1,0:T(8,128)S(1)}, f32[8,128,128]{2,1,0:T(8,128)S(1)}) fusion(f32[8,8,128,2,128]{4,1,3,2,0:T(8,128)S(1)} %convert_element_type.142, f32[8,128,128]{2,0,1:T(8,128)S(1)} %get-tuple-element.193, f32[8,128,128]{2,0,1:T(8,128)S(1)} %get-tuple-element.194), kind=kLoop, calls=%fused_computation.4.clone.1 | loop fusion | flops 8126464 | bytes 10485760 | tf_op jit(solution)/shard_map/while/body/eval_jaxpr/vmap()/reduce_sum | solution.py:31
  92.1 1.3 constant_dynamic-slice_fusion.2
  93.5 2.2 %copy_dynamic-update-slice_fusion.2 = f32[32,128,2,128]{3,2,0,1:T(2,128)} fusion(f32[32,128,2,128]{3,2,0,1:T(2,128)} %get-tuple-element.207, s32[]{:T(128)S(6)} %select_n.139, f32[8,128,1,128]{3,2,1,0:T(1,128)S(1)} %bitcast.90, f32[8,128,1,128]{3,2,1,0:T(1,128)S(1)} %bitcast.89, f32[8,128,2,128]{3,2,0,1:T(2,128)S(1)} %constant_dynamic-slice_fusion.2), kind=kLoop, calls=%fused_computation.6.clone.1 | loop fusion | flops 524288 | bytes 3145732 | tf_op jit(solution)/shard_map/while/body/eval_jaxpr/dynamic_update_slice | solution.py:43
  95.7 3.1 %gather_fusion = bf16[8,8,128,2,128]{4,1,3,2,0:T(8,128)(2,1)} fusion(bf16[8,256,2,128]{3,0,2,1:T(8,128)(2,1)S(1)} %get-tuple-element.219, s32[8]{0:T(128)S(1)} %fusion.53), kind=kCustom, calls=%fused_computation.clone.1 | custom fusion | bytes 8388736 | tf_op jit(solution)/shard_map/while/body/eval_jaxpr/vmap()/gather | solution.py:30
  98.8 2.9 %convert_element_type.142 = f32[8,8,128,2,128]{4,1,3,2,0:T(8,128)S(1)} convert(bf16[8,8,128,2,128]{4,1,3,2,0:T(8,128)(2,1)} %gather_fusion) | non-fusion elementwise | flops 2097152 | bytes 12582912 | tf_op jit(solution)/shard_map/while/body/eval_jaxpr/vmap()/convert_element_type | solution.py:30
  101.8 3.1 %add_reduce_fusion.2 = (f32[8,128,128]{2,1,0:T(8,128)S(1)}, f32[8,128,128]{2,1,0:T(8,128)S(1)}) fusion(f32[8,8,128,2,128]{4,1,3,2,0:T(8,128)S(1)} %convert_element_type.142, f32[8,128,128]{2,0,1:T(8,128)S(1)} %get-tuple-element.193, f32[8,128,128]{2,0,1:T(8,128)S(1)} %get-tuple-element.194), kind=kLoop, calls=%fused_computation.4.clone.1 | loop fusion | flops 8126464 | bytes 10485760 | tf_op jit(solution)/shard_map/while/body/eval_jaxpr/vmap()/reduce_sum | solution.py:31
  104.9 1.3 constant_dynamic-slice_fusion.2
  106.2 2.2 %copy_dynamic-update-slice_fusion.2 = f32[32,128,2,128]{3,2,0,1:T(2,128)} fusion(f32[32,128,2,128]{3,2,0,1:T(2,128)} %get-tuple-element.207, s32[]{:T(128)S(6)} %select_n.139, f32[8,128,1,128]{3,2,1,0:T(1,128)S(1)} %bitcast.90, f32[8,128,1,128]{3,2,1,0:T(1,128)S(1)} %bitcast.89, f32[8,128,2,128]{3,2,0,1:T(2,128)S(1)} %constant_dynamic-slice_fusion.2), kind=kLoop, calls=%fused_computation.6.clone.1 | loop fusion | flops 524288 | bytes 3145732 | tf_op jit(solution)/shard_map/while/body/eval_jaxpr/dynamic_update_slice | solution.py:43
  108.4 5.5 %convert_element_type.99 = bf16[32,128,2,128]{3,2,0,1:T(2,128)(2,1)} convert(f32[32,128,2,128]{3,2,0,1:T(2,128)} %get-tuple-element.99) | non-fusion elementwise | flops 1048576 | bytes 6291456 | tf_op jit(solution)/shard_map/convert_element_type | solution.py:120
  113.9 3.9 %all-to-all-start.1 = ((bf16[32,128,2,128]{3,2,0,1:T(2,128)(2,1)}), bf16[32,128,2,128]{3,2,0,1:T(2,128)(2,1)S(1)}, u32[]{:S(2)}, u32[]{:S(2)}) async-start(bf16[32,128,2,128]{3,2,0,1:T(2,128)(2,1)} %convert_element_type.99), calls=%async_computation.1 | async-start | bytes 4194304 | tf_op jit(solution)/shard_map/all_to_all | solution.py:124
  117.8 9.8 %cosine_convert_fusion = (bf16[1,1024,512]{2,1,0:T(8,128)(2,1)S(1)}, bf16[1,1024,512]{2,1,0:T(8,128)(2,1)}) fusion(s32[512]{0:T(512)S(1)} %iota_add_fusion, s32[1024]{0:T(1024)S(1)} %copy-done), kind=kLoop, calls=%fused_computation.35 | loop fusion | flops 8912896 | bytes 2103296 | tf_op jit(solution)/shard_map/convert
  127.6 38.9 %all-to-all-done.1 = bf16[32,128,2,128]{3,2,0,1:T(2,128)(2,1)S(1)} async-done(((bf16[32,128,2,128]{3,2,0,1:T(2,128)(2,1)}), bf16[32,128,2,128]{3,2,0,1:T(2,128)(2,1)S(1)}, u32[]{:S(2)}, u32[]{:S(2)}) %all-to-all-start.1) | async-done | bytes 2097184 | tf_op jit(solution)/shard_map/all_to_all | solution.py:124
  166.4 3.8 %copy.78 = bf16[32,8,16,2,128]{4,1,2,3,0:T(8,128)(2,1)} copy(bf16[32,8,16,2,128]{4,3,0,2,1:T(2,128)(2,1)S(1)} %bitcast.91) | data formatting | bytes 4194304 | tf_op jit(solution)/shard_map/all_to_all | solution.py:124
  170.2 2.8 %all_to_all.33 = bf16[32,16,2,1024]{3,1,2,0:T(8,128)(2,1)S(1)} reshape(bf16[32,16,2,8,128]{4,3,1,2,0:T(8,128)(2,1)} %bitcast.92) | data formatting | bytes 4194304 | tf_op jit(solution)/shard_map/all_to_all | solution.py:124
  173.0 3.3 %fusion.14 = bf16[32,16,512]{2,1,0:T(8,128)(2,1)} fusion(bf16[32,16,2,1024]{3,1,2,0:T(8,128)(2,1)S(1)} %all_to_all.33, bf16[1,1024,512]{2,1,0:T(8,128)(2,1)} %get-tuple-element.151, bf16[1,1024,512]{2,1,0:T(8,128)(2,1)S(1)} %get-tuple-element.150), kind=kOutput, calls=%fused_computation.39 | convolution fusion | flops 1075314688 | bytes 4718592 | tf_op jit(solution)/shard_map/ocpk,pkl->ocl/dot_general | solution.py:122
  (27 shorter events, 2.8 us)
Async XLA Ops:
  5.5 2.7 %copy-start = (s32[1024]{0:T(1024)S(1)}, s32[1024]{0:T(1024)}, u32[]{:S(2)}) copy-start(s32[1024]{0:T(1024)} %param.6) | copy-start | bytes 12292
  21.0 14.7 %copy-start.1 = (s32[128]{0:T(128)S(1)}, s32[128]{0:T(128)}, u32[]{:S(2)}) copy-start(s32[128]{0:T(128)} %param.7) | copy-start | bytes 1540
  28.4 14.6 %all-to-all-start = ((bf16[8,2,4096]{2,1,0:T(2,128)(2,1)}), bf16[8,2,4096]{2,1,0:T(2,128)(2,1)S(1)}, u32[]{:S(2)}, u32[]{:S(2)}) async-start(bf16[8,2,4096]{2,1,0:T(2,128)(2,1)} %reshape.414), calls=%async_computation | async-start | bytes 262144 | tf_op jit(solution)/shard_map/all_to_all | solution.py:107
  113.9 52.6 %all-to-all-start.1 = ((bf16[32,128,2,128]{3,2,0,1:T(2,128)(2,1)}), bf16[32,128,2,128]{3,2,0,1:T(2,128)(2,1)S(1)}, u32[]{:S(2)}, u32[]{:S(2)}) async-start(bf16[32,128,2,128]{3,2,0,1:T(2,128)(2,1)} %convert_element_type.99), calls=%async_computation.1 | async-start | bytes 4194304 | tf_op jit(solution)/shard_map/all_to_all | solution.py:124

commit v3 on v2

--- a/solution.py
+++ b/solution.py
@@ -71,25 +71,21 @@
     bin_count = kept_bins.shape[0]
     block_count = 4
     block_len = samples // block_count
-    x = record_rows.reshape(row_count, block_count, block_len).astype(jnp.float32)
-    br = jnp.mod(
-        jnp.arange(block_count, dtype=jnp.int32)[:, None] * jnp.arange(block_count, dtype=jnp.int32)[None, :],
+    lhs = jnp.transpose(record_rows.reshape(row_count, block_count, block_len), (1, 0, 2))
+    prod = jnp.dot(
+        lhs.reshape(block_count * row_count, block_len),
+        small_table(kept_bins, block_len),
+        preferred_element_type=jnp.float32,
+    ).reshape(block_count, row_count, 2, bin_count)
+    turns = jnp.mod(
+        jnp.arange(block_count, dtype=jnp.int32)[:, None] * jnp.mod(kept_bins, block_count)[None, :],
         block_count,
     ).astype(jnp.float32) * (2.0 * math.pi / block_count)
-    twiddle = jnp.round(jnp.stack([jnp.cos(br), -jnp.sin(br)], axis=0))
-    y = jnp.einsum("ubs,pbr->prus", x, twiddle, precision=lax.Precision.HIGHEST)
-    y_hi = y.astype(jnp.bfloat16)
-    y_lo = (y - y_hi.astype(jnp.float32)).astype(jnp.bfloat16)
-    lhs = jnp.stack([y_hi, y_lo], axis=0).reshape(-1, block_len)
-    prod = jnp.dot(lhs, small_table(kept_bins, block_len), preferred_element_type=jnp.float32)
-    prod = prod.reshape(2, 2, block_count, row_count, 2, bin_count)
-    prod = prod[0] + prod[1]
-    pick = (
-        jnp.mod(kept_bins, block_count)[None, None, :]
-        == jnp.arange(block_count, dtype=jnp.int32)[:, None, None]
-    ).astype(jnp.float32)
-    real_part = jnp.sum(pick * (prod[0, :, :, 0] - prod[1, :, :, 1]), axis=0)
-    imag_part = jnp.sum(pick * (prod[0, :, :, 1] + prod[1, :, :, 0]), axis=0)
+    tw_re = jnp.round(jnp.cos(turns))[:, None, :]
+    tw_im = jnp.round(-jnp.sin(turns))[:, None, :]
+    p_re, p_im = prod[:, :, 0], prod[:, :, 1]
+    real_part = jnp.sum(tw_re * p_re - tw_im * p_im, axis=0)
+    imag_part = jnp.sum(tw_re * p_im + tw_im * p_re, axis=0)
     return jnp.concatenate([real_part, imag_part], axis=-1)
 
 

time: 177 us -> 166 us (0.938)
  other arithmetic: 61.9 us -> 56.5 us
  matrix products: 9.67 us -> 5.73 us
    add x2 -> x0, other arithmetic: 4.17 us -> none  [the longest x1 3.88 us: forward_spectra(): imag_part = jnp.sum(pick * (prod[0, :, :, 1] + prod[1, :, :, 0]), axis=0)]
    dot_general x2 -> x1, matrix products: 6.4 us -> 2.46 us  [forward_spectra(): jnp.dot(lhs.reshape(block_count * row_count, block_len), small_table(kept...]
    add x1 -> x0, local copies, waits for them, and re-layouts: 2.82 us -> none  [forward_spectra(): prod = prod[0] + prod[1]]
    another operation x3 -> x2, other arithmetic: 15.3 us -> 13.5 us
where the time goes in v3:
time: 166 us; the launch traced here: 165 us
  other arithmetic  56.5 us (34%)
  waiting for transfers between devices  46.2 us (28%)
  local copies, waits for them, and re-layouts  38.2 us (23%)
  starting transfers between devices  11.1 us (7%)
  blocking collectives  7.17 us (4%)
  matrix products  5.73 us (3%)
    all_to_all x1, waiting for transfers between devices, local(): lax.all_to_all(cross_sum, 'gx', split_axis=1, concat_axis=3, tiled=True)  38.9 us
    another operation x2, other arithmetic  13.5 us
    reduce_sum x4, other arithmetic, one_offset(): jnp.sum(own_part[:, :, 0] * theirs[:, :, 0] + own_part[:, :, 1] * theirs[...  12.3 us
    gather x4, local copies, waits for them, and re-layouts, one_offset(): lax.dynamic_slice_in_dim(window_block, shift_by, own_count, 1)  12.2 us
    convert_element_type x4, other arithmetic, one_offset(): lax.dynamic_slice_in_dim(window_block, shift_by, own_count, 1)  11.7 us
    dynamic_update_slice x4, other arithmetic, one_group(): lax.dynamic_update_slice_in_dim(carried, current + update, group_index *...  8.78 us
    all_to_all x1, starting transfers between devices, local(): lax.all_to_all(white, 'gx', split_axis=3, concat_axis=1, tiled=True)  7.28 us
    all_to_all x1, waiting for transfers between devices, local(): lax.all_to_all(white, 'gx', split_axis=3, concat_axis=1, tiled=True)  7.26 us
  transfers between devices with their start and end apart: 2, of which 2 were waited for; matrix products, arithmetic and copies ran while one was open for 6% of the time, Pallas kernels for 0%

profile of v3, /device:TPU:0, one launch (start us, length us, event | category | flops | bytes accessed | tf_op | source)
XLA Modules:
  0.0 165.2 jit_solution(18419957251662537689)
XLA Ops:
  0.0 1.2 fusion.34
  1.2 0.7 add_select_fusion.4
  1.9 1.8 %fusion.29 = (f32[64,1024]{1,0:T(8,128)S(1)}, f32[64,1024]{1,0:T(8,128)S(1)}) fusion(s32[1024]{0:T(1024)} %param.6, s32[64]{0:T(128)S(1)} %iota_multiply_fusion), kind=kLoop, calls=%fused_computation.63 | loop fusion | flops 917504 | bytes 528640 | tf_op jit(solution)/shard_map/cos | solution.py:62
  3.7 1.3 copy.37
  5.0 0.4 reshape_reshape.3
  5.7 3.7 %subtract_convert_fusion = (bf16[64,32,1024]{2,1,0:T(8,128)(2,1)S(1)}, bf16[64,32,1024]{2,1,0:T(8,128)(2,1)S(1)}) fusion(f32[64,1024]{1,0:T(8,128)S(1)} %get-tuple-element.150, f32[32,1024]{1,0:T(8,128)S(1)} %get-tuple-element.154, f32[64,1024]{1,0:T(8,128)S(1)} %get-tuple-element.149, f32[32,1024]{1,0:T(8,128)S(1)} %get-tuple-element.153), kind=kLoop, calls=%fused_computation.18 | loop fusion | flops 18874368 | bytes 9175040 | tf_op jit(solution)/shard_map/convert.5
  9.4 2.5 %fusion.6 = f32[128,2048]{0,1:T(8,128)S(1)} fusion(bf16[128,2048]{1,0:T(8,128)(2,1)S(1)} %bitcast.98, bf16[2048,1024]{1,0:T(8,128)(2,1)S(1)} %bitcast.94, bf16[2048,1024]{1,0:T(8,128)(2,1)S(1)} %bitcast.93), kind=kOutput, calls=%fused_computation.24 | convolution fusion | flops 1090519040 | bytes 9961472 | tf_op jit(solution)/shard_map/dot_general | solution.py:75
  11.9 0.3 copy.39
  12.2 0.9 reshape.346
  13.1 0.8 fusion.41
  15.0 0.8 copy.41
  15.8 1.7 %reshape.361 = bf16[8,2,4096]{2,1,0:T(2,128)(2,1)} reshape(bf16[1024,2,2,16]{3,2,1,0:T(2,128)(2,1)S(1)} %bitcast.91) | data formatting | bytes 262144
  17.5 7.3 %all-to-all-start = ((bf16[8,2,4096]{2,1,0:T(2,128)(2,1)}), bf16[8,2,4096]{2,1,0:T(2,128)(2,1)S(1)}, u32[]{:S(2)}, u32[]{:S(2)}) async-start(bf16[8,2,4096]{2,1,0:T(2,128)(2,1)} %reshape.361), calls=%async_computation | async-start | bytes 262144 | tf_op jit(solution)/shard_map/all_to_all | solution.py:103
  24.8 7.3 %all-to-all-done = bf16[8,2,4096]{2,1,0:T(2,128)(2,1)S(1)} async-done(((bf16[8,2,4096]{2,1,0:T(2,128)(2,1)}), bf16[8,2,4096]{2,1,0:T(2,128)(2,1)S(1)}, u32[]{:S(2)}, u32[]{:S(2)}) %all-to-all-start) | async-done | bytes 131104 | tf_op jit(solution)/shard_map/all_to_all | solution.py:103
  32.1 0.7 reshape.362
  32.8 1.3 copy.50
  34.1 7.2 %all_gather.3 = bf16[8,128,2,128]{3,1,2,0:T(8,128)(2,1)S(1)} all-gather(bf16[2,128,2,128]{3,1,2,0:T(8,128)(2,1)S(1)} %bitcast.96), channel_id=1, replica_groups=mesh['gx'=8,'gy'=4] {'gy'}, dimensions={0}, use_global_device_ids=true | all-gather | bytes 655360 | tf_op jit(solution)/shard_map/all_gather | solution.py:106
  41.3 0.3 copy.60
  41.6 0.3 copy.44
  42.1 4.0 %broadcast_in_dim.8.clone = f32[32,128,2,128]{3,2,0,1:T(2,128)} broadcast(f32[]{:T(128)} %constant.112.clone.1), dimensions={} | broadcast | bytes 4194308 | tf_op jit(solution)/shard_map/broadcast_in_dim | solution.py:105
  46.2 51.1 %while.13 = (s32[]{:T(128)}, f32[32,128,2,128]{3,2,0,1:T(2,128)}, f32[8,128,2,128]{3,0,1,2:T(8,128)S(1)}, s32[32]{0:T(128)S(1)}, bf16[8,256,2,128]{3,0,2,1:T(8,1...) while((s32[]{:T(128)}, f32[32,128,2,128]{3,2,0,1:T(2,128)}, ...), condition=%wide.region_6.7_spmd, body=%wide.region_3.6_spmd.sunk | while | flops 10747950 | bytes 38797656 | solution.py:47
  46.2 3.1 %gather_fusion = bf16[8,8,128,2,128]{4,1,3,2,0:T(8,128)(2,1)} fusion(bf16[8,256,2,128]{3,0,2,1:T(8,128)(2,1)S(1)} %get-tuple-element.216, s32[8]{0:T(128)S(1)} %fusion.45), kind=kCustom, calls=%fused_computation.clone.1 | custom fusion | bytes 8388736 | tf_op jit(solution)/shard_map/while/body/eval_jaxpr/vmap()/gather | solution.py:30
  49.3 2.9 %convert_element_type.105 = f32[8,8,128,2,128]{4,1,3,2,0:T(8,128)S(1)} convert(bf16[8,8,128,2,128]{4,1,3,2,0:T(8,128)(2,1)} %gather_fusion) | non-fusion elementwise | flops 2097152 | bytes 12582912 | tf_op jit(solution)/shard_map/while/body/eval_jaxpr/vmap()/convert_element_type | solution.py:30
  52.3 3.1 %add_reduce_fusion.2 = (f32[8,128,128]{2,1,0:T(8,128)S(1)}, f32[8,128,128]{2,1,0:T(8,128)S(1)}) fusion(f32[8,8,128,2,128]{4,1,3,2,0:T(8,128)S(1)} %convert_element_type.105, f32[8,128,128]{2,0,1:T(8,128)S(1)} %get-tuple-element.190, f32[8,128,128]{2,0,1:T(8,128)S(1)} %get-tuple-element.191), kind=kLoop, calls=%fused_computation.4.clone.1 | loop fusion | flops 8126464 | bytes 10485760 | tf_op jit(solution)/shard_map/while/body/eval_jaxpr/vmap()/reduce_sum | solution.py:31
  55.4 1.3 constant_dynamic-slice_fusion.2
  56.7 2.2 %copy_dynamic-update-slice_fusion.2 = f32[32,128,2,128]{3,2,0,1:T(2,128)} fusion(f32[32,128,2,128]{3,2,0,1:T(2,128)} %get-tuple-element.204, s32[]{:T(128)S(6)} %select_n.133, f32[8,128,1,128]{3,2,1,0:T(1,128)S(1)} %bitcast.88, f32[8,128,1,128]{3,2,1,0:T(1,128)S(1)} %bitcast.87, f32[8,128,2,128]{3,2,0,1:T(2,128)S(1)} %constant_dynamic-slice_fusion.2), kind=kLoop, calls=%fused_computation.6.clone.1 | loop fusion | flops 524288 | bytes 3145732 | tf_op jit(solution)/shard_map/while/body/eval_jaxpr/dynamic_update_slice | solution.py:43
  59.0 3.1 %gather_fusion = bf16[8,8,128,2,128]{4,1,3,2,0:T(8,128)(2,1)} fusion(bf16[8,256,2,128]{3,0,2,1:T(8,128)(2,1)S(1)} %get-tuple-element.216, s32[8]{0:T(128)S(1)} %fusion.45), kind=kCustom, calls=%fused_computation.clone.1 | custom fusion | bytes 8388736 | tf_op jit(solution)/shard_map/while/body/eval_jaxpr/vmap()/gather | solution.py:30
  62.0 2.9 %convert_element_type.105 = f32[8,8,128,2,128]{4,1,3,2,0:T(8,128)S(1)} convert(bf16[8,8,128,2,128]{4,1,3,2,0:T(8,128)(2,1)} %gather_fusion) | non-fusion elementwise | flops 2097152 | bytes 12582912 | tf_op jit(solution)/shard_map/while/body/eval_jaxpr/vmap()/convert_element_type | solution.py:30
  65.1 3.1 %add_reduce_fusion.2 = (f32[8,128,128]{2,1,0:T(8,128)S(1)}, f32[8,128,128]{2,1,0:T(8,128)S(1)}) fusion(f32[8,8,128,2,128]{4,1,3,2,0:T(8,128)S(1)} %convert_element_type.105, f32[8,128,128]{2,0,1:T(8,128)S(1)} %get-tuple-element.190, f32[8,128,128]{2,0,1:T(8,128)S(1)} %get-tuple-element.191), kind=kLoop, calls=%fused_computation.4.clone.1 | loop fusion | flops 8126464 | bytes 10485760 | tf_op jit(solution)/shard_map/while/body/eval_jaxpr/vmap()/reduce_sum | solution.py:31
  68.2 1.3 constant_dynamic-slice_fusion.2
  69.5 2.2 %copy_dynamic-update-slice_fusion.2 = f32[32,128,2,128]{3,2,0,1:T(2,128)} fusion(f32[32,128,2,128]{3,2,0,1:T(2,128)} %get-tuple-element.204, s32[]{:T(128)S(6)} %select_n.133, f32[8,128,1,128]{3,2,1,0:T(1,128)S(1)} %bitcast.88, f32[8,128,1,128]{3,2,1,0:T(1,128)S(1)} %bitcast.87, f32[8,128,2,128]{3,2,0,1:T(2,128)S(1)} %constant_dynamic-slice_fusion.2), kind=kLoop, calls=%fused_computation.6.clone.1 | loop fusion | flops 524288 | bytes 3145732 | tf_op jit(solution)/shard_map/while/body/eval_jaxpr/dynamic_update_slice | solution.py:43
  71.7 3.1 %gather_fusion = bf16[8,8,128,2,128]{4,1,3,2,0:T(8,128)(2,1)} fusion(bf16[8,256,2,128]{3,0,2,1:T(8,128)(2,1)S(1)} %get-tuple-element.216, s32[8]{0:T(128)S(1)} %fusion.45), kind=kCustom, calls=%fused_computation.clone.1 | custom fusion | bytes 8388736 | tf_op jit(solution)/shard_map/while/body/eval_jaxpr/vmap()/gather | solution.py:30
  74.8 2.9 %convert_element_type.105 = f32[8,8,128,2,128]{4,1,3,2,0:T(8,128)S(1)} convert(bf16[8,8,128,2,128]{4,1,3,2,0:T(8,128)(2,1)} %gather_fusion) | non-fusion elementwise | flops 2097152 | bytes 12582912 | tf_op jit(solution)/shard_map/while/body/eval_jaxpr/vmap()/convert_element_type | solution.py:30
  77.8 3.1 %add_reduce_fusion.2 = (f32[8,128,128]{2,1,0:T(8,128)S(1)}, f32[8,128,128]{2,1,0:T(8,128)S(1)}) fusion(f32[8,8,128,2,128]{4,1,3,2,0:T(8,128)S(1)} %convert_element_type.105, f32[8,128,128]{2,0,1:T(8,128)S(1)} %get-tuple-element.190, f32[8,128,128]{2,0,1:T(8,128)S(1)} %get-tuple-element.191), kind=kLoop, calls=%fused_computation.4.clone.1 | loop fusion | flops 8126464 | bytes 10485760 | tf_op jit(solution)/shard_map/while/body/eval_jaxpr/vmap()/reduce_sum | solution.py:31
  80.9 1.3 constant_dynamic-slice_fusion.2
  82.2 2.2 %copy_dynamic-update-slice_fusion.2 = f32[32,128,2,128]{3,2,0,1:T(2,128)} fusion(f32[32,128,2,128]{3,2,0,1:T(2,128)} %get-tuple-element.204, s32[]{:T(128)S(6)} %select_n.133, f32[8,128,1,128]{3,2,1,0:T(1,128)S(1)} %bitcast.88, f32[8,128,1,128]{3,2,1,0:T(1,128)S(1)} %bitcast.87, f32[8,128,2,128]{3,2,0,1:T(2,128)S(1)} %constant_dynamic-slice_fusion.2), kind=kLoop, calls=%fused_computation.6.clone.1 | loop fusion | flops 524288 | bytes 3145732 | tf_op jit(solution)/shard_map/while/body/eval_jaxpr/dynamic_update_slice | solution.py:43
  84.5 3.1 %gather_fusion = bf16[8,8,128,2,128]{4,1,3,2,0:T(8,128)(2,1)} fusion(bf16[8,256,2,128]{3,0,2,1:T(8,128)(2,1)S(1)} %get-tuple-element.216, s32[8]{0:T(128)S(1)} %fusion.45), kind=kCustom, calls=%fused_computation.clone.1 | custom fusion | bytes 8388736 | tf_op jit(solution)/shard_map/while/body/eval_jaxpr/vmap()/gather | solution.py:30
  87.6 2.9 %convert_element_type.105 = f32[8,8,128,2,128]{4,1,3,2,0:T(8,128)S(1)} convert(bf16[8,8,128,2,128]{4,1,3,2,0:T(8,128)(2,1)} %gather_fusion) | non-fusion elementwise | flops 2097152 | bytes 12582912 | tf_op jit(solution)/shard_map/while/body/eval_jaxpr/vmap()/convert_element_type | solution.py:30
  90.6 3.1 %add_reduce_fusion.2 = (f32[8,128,128]{2,1,0:T(8,128)S(1)}, f32[8,128,128]{2,1,0:T(8,128)S(1)}) fusion(f32[8,8,128,2,128]{4,1,3,2,0:T(8,128)S(1)} %convert_element_type.105, f32[8,128,128]{2,0,1:T(8,128)S(1)} %get-tuple-element.190, f32[8,128,128]{2,0,1:T(8,128)S(1)} %get-tuple-element.191), kind=kLoop, calls=%fused_computation.4.clone.1 | loop fusion | flops 8126464 | bytes 10485760 | tf_op jit(solution)/shard_map/while/body/eval_jaxpr/vmap()/reduce_sum | solution.py:31
  93.7 1.3 constant_dynamic-slice_fusion.2
  95.0 2.2 %copy_dynamic-update-slice_fusion.2 = f32[32,128,2,128]{3,2,0,1:T(2,128)} fusion(f32[32,128,2,128]{3,2,0,1:T(2,128)} %get-tuple-element.204, s32[]{:T(128)S(6)} %select_n.133, f32[8,128,1,128]{3,2,1,0:T(1,128)S(1)} %bitcast.88, f32[8,128,1,128]{3,2,1,0:T(1,128)S(1)} %bitcast.87, f32[8,128,2,128]{3,2,0,1:T(2,128)S(1)} %constant_dynamic-slice_fusion.2), kind=kLoop, calls=%fused_computation.6.clone.1 | loop fusion | flops 524288 | bytes 3145732 | tf_op jit(solution)/shard_map/while/body/eval_jaxpr/dynamic_update_slice | solution.py:43
  97.2 5.5 %convert_element_type.71 = bf16[32,128,2,128]{3,2,0,1:T(2,128)(2,1)} convert(f32[32,128,2,128]{3,2,0,1:T(2,128)} %get-tuple-element.99) | non-fusion elementwise | flops 1048576 | bytes 6291456 | tf_op jit(solution)/shard_map/convert_element_type | solution.py:116
  102.7 3.8 %all-to-all-start.1 = ((bf16[32,128,2,128]{3,2,0,1:T(2,128)(2,1)}), bf16[32,128,2,128]{3,2,0,1:T(2,128)(2,1)S(1)}, u32[]{:S(2)}, u32[]{:S(2)}) async-start(bf16[32,128,2,128]{3,2,0,1:T(2,128)(2,1)} %convert_element_type.71), calls=%async_computation.1 | async-start | bytes 4194304 | tf_op jit(solution)/shard_map/all_to_all | solution.py:120
  106.6 9.8 %cosine_convert_fusion = (bf16[1,1024,512]{2,1,0:T(8,128)(2,1)S(1)}, bf16[1,1024,512]{2,1,0:T(8,128)(2,1)}) fusion(s32[512]{0:T(512)S(1)} %iota_add_fusion, s32[1024]{0:T(1024)S(1)} %copy-done), kind=kLoop, calls=%fused_computation.34 | loop fusion | flops 8912896 | bytes 2103296 | tf_op jit(solution)/shard_map/convert
  116.4 38.9 %all-to-all-done.1 = bf16[32,128,2,128]{3,2,0,1:T(2,128)(2,1)S(1)} async-done(((bf16[32,128,2,128]{3,2,0,1:T(2,128)(2,1)}), bf16[32,128,2,128]{3,2,0,1:T(2,128)(2,1)S(1)}, u32[]{:S(2)}, u32[]{:S(2)}) %all-to-all-start.1) | async-done | bytes 2097184 | tf_op jit(solution)/shard_map/all_to_all | solution.py:120
  155.3 3.8 %copy.72 = bf16[32,8,16,2,128]{4,1,2,3,0:T(8,128)(2,1)} copy(bf16[32,8,16,2,128]{4,3,0,2,1:T(2,128)(2,1)S(1)} %bitcast.89) | data formatting | bytes 4194304 | tf_op jit(solution)/shard_map/all_to_all | solution.py:120
  159.1 2.8 %all_to_all.33 = bf16[32,16,2,1024]{3,1,2,0:T(8,128)(2,1)S(1)} reshape(bf16[32,16,2,8,128]{4,3,1,2,0:T(8,128)(2,1)} %bitcast.90) | data formatting | bytes 4194304 | tf_op jit(solution)/shard_map/all_to_all | solution.py:120
  161.9 3.3 %fusion.17 = bf16[32,16,512]{2,1,0:T(8,128)(2,1)} fusion(bf16[32,16,2,1024]{3,1,2,0:T(8,128)(2,1)S(1)} %all_to_all.33, bf16[1,1024,512]{2,1,0:T(8,128)(2,1)} %get-tuple-element.148, bf16[1,1024,512]{2,1,0:T(8,128)(2,1)S(1)} %get-tuple-element.147), kind=kOutput, calls=%fused_computation.37 | convolution fusion | flops 1075314688 | bytes 4718592 | tf_op jit(solution)/shard_map/ocpk,pkl->ocl/dot_general | solution.py:118
  (24 shorter events, 2.1 us)
Async XLA Ops:
  13.1 11.7 %copy-start.1 = (s32[128]{0:T(128)S(1)}, s32[128]{0:T(128)}, u32[]{:S(2)}) copy-start(s32[128]{0:T(128)} %param.7) | copy-start | bytes 1540
  17.5 14.6 %all-to-all-start = ((bf16[8,2,4096]{2,1,0:T(2,128)(2,1)}), bf16[8,2,4096]{2,1,0:T(2,128)(2,1)S(1)}, u32[]{:S(2)}, u32[]{:S(2)}) async-start(bf16[8,2,4096]{2,1,0:T(2,128)(2,1)} %reshape.361), calls=%async_computation | async-start | bytes 262144 | tf_op jit(solution)/shard_map/all_to_all | solution.py:103
  97.2 9.3 %copy-start = (s32[1024]{0:T(1024)S(1)}, s32[1024]{0:T(1024)}, u32[]{:S(2)}) copy-start(s32[1024]{0:T(1024)} %param.6) | copy-start | bytes 12292
  102.7 52.6 %all-to-all-start.1 = ((bf16[32,128,2,128]{3,2,0,1:T(2,128)(2,1)}), bf16[32,128,2,128]{3,2,0,1:T(2,128)(2,1)S(1)}, u32[]{:S(2)}, u32[]{:S(2)}) async-start(bf16[32,128,2,128]{3,2,0,1:T(2,128)(2,1)} %convert_element_type.71), calls=%async_computation.1 | async-start | bytes 4194304 | tf_op jit(solution)/shard_map/all_to_all | solution.py:120

commit v4 on v3

--- a/solution.py
+++ b/solution.py
@@ -1,8 +1,11 @@
+import functools
 import math
 
 import jax
 import jax.numpy as jnp
 from jax import lax
+from jax.experimental import pallas as pl
+from jax.experimental.pallas import tpu as pltpu
 from jax.sharding import PartitionSpec as P
 
 SAMPLES = 8192
@@ -22,29 +25,45 @@
     return (spectra * lax.rsqrt(mean_power + 1e-06)).astype(jnp.bfloat16)
 
 
-def add_cross(running, window_block, my_offsets, own_count):
-    group_size = math.gcd(8, my_offsets.shape[0])
-    own_part = window_block[:, :own_count].astype(jnp.float32)
+def cross_kernel(offsets_ref, base_ref, white_ref, out_ref, *, group, own_count, half):
+    step = pl.program_id(0)
+    base = base_ref[0]
+    own = [white_ref[base + c].astype(jnp.float32) for c in range(own_count)]
 
-    def one_offset(shift_by):
-        theirs = lax.dynamic_slice_in_dim(window_block, shift_by, own_count, 1).astype(jnp.float32)
-        real_part = jnp.sum(
-            own_part[:, :, 0] * theirs[:, :, 0] + own_part[:, :, 1] * theirs[:, :, 1], axis=0
-        )
-        imag_part = jnp.sum(
-            own_part[:, :, 1] * theirs[:, :, 0] - own_part[:, :, 0] * theirs[:, :, 1], axis=0
-        )
-        return jnp.stack([real_part, imag_part], axis=1)
+    def one_offset(i, carry):
+        shift = offsets_ref[step * group + i]
+        for c in range(own_count):
+            a = own[c]
+            b = white_ref[base + c + shift].astype(jnp.float32)
+            ar, ai, br, bi = a[:half], a[half:], b[:half], b[half:]
+            out_ref[i, 0, pl.ds(c, 1), :] = jnp.sum(ar * br + ai * bi, axis=0, keepdims=True)
+            out_ref[i, 1, pl.ds(c, 1), :] = jnp.sum(ai * br - ar * bi, axis=0, keepdims=True)
+        return carry
 
-    def one_group(group_index, carried):
-        chosen = lax.dynamic_slice_in_dim(my_offsets, group_index * group_size, group_size)
-        update = jax.vmap(one_offset)(chosen)
-        current = lax.dynamic_slice_in_dim(carried, group_index * group_size, group_size, 0)
-        return lax.dynamic_update_slice_in_dim(
-            carried, current + update, group_index * group_size, 0
-        )
+    lax.fori_loop(0, group, one_offset, 0)
 
-    return lax.fori_loop(0, my_offsets.shape[0] // group_size, one_group, running)
+
+def cross_spectra(white_all, pair_offsets, base, own_count):
+    rows, bins = white_all.shape[1], white_all.shape[2]
+    band_span = pair_offsets.shape[0]
+    group = math.gcd(band_span, 8)
+    kernel = functools.partial(cross_kernel, group=group, own_count=own_count, half=rows // 2)
+    return pl.pallas_call(
+        kernel,
+        grid_spec=pltpu.PrefetchScalarGridSpec(
+            num_scalar_prefetch=2,
+            grid=(band_span // group,),
+            in_specs=[pl.BlockSpec(white_all.shape, lambda g, offs, b: (0, 0, 0))],
+            out_specs=pl.BlockSpec((group, 2, own_count, bins), lambda g, offs, b: (g, 0, 0, 0)),
+        ),
+        out_shape=jax.ShapeDtypeStruct((band_span, 2, own_count, bins), jnp.float32),
+        compiler_params=pltpu.CompilerParams(vmem_limit_bytes=48 * 1024 * 1024),
+        cost_estimate=pl.CostEstimate(
+            flops=8 * band_span * own_count * rows * bins,
+            transcendentals=0,
+            bytes_accessed=white_all.size * 2 + band_span * 2 * own_count * bins * 4,
+        ),
+    )(pair_offsets, base, white_all)
 
 
 def small_table(kept_bins, rows):
@@ -96,32 +115,21 @@
     record_rows = jnp.transpose(records, (1, 0, 2)).reshape(win_dev * ch_dev, samples)
     spectra = forward_spectra(record_rows, kept_bins)
     white = whiten(spectra).reshape(win_dev, ch_dev, 2, bin_count)
-    off_dev = band_span // lax.axis_size("gy")
-    my_offsets = lax.dynamic_slice_in_dim(pair_offsets, lax.axis_index("gy") * off_dev, off_dev)
+    freq_white = lax.all_to_all(white, "gy", split_axis=3, concat_axis=0, tiled=True)
+    windows = freq_white.shape[0]
+    shard_bins = freq_white.shape[3]
+    rows_white = jnp.transpose(freq_white, (1, 2, 0, 3)).reshape(ch_dev, 2 * windows, shard_bins)
+    all_white = lax.all_gather(rows_white, "gx", axis=0, tiled=True)
+    padded = jnp.concatenate(
+        [all_white, jnp.zeros((band_span,) + all_white.shape[1:], all_white.dtype)], axis=0
+    )
+    base = (lax.axis_index("gx") * ch_dev).astype(jnp.int32).reshape(1)
+    cross = cross_spectra(padded, pair_offsets.astype(jnp.int32), base, ch_dev).astype(jnp.bfloat16)
+    cross = lax.all_to_all(cross, "gy", split_axis=0, concat_axis=3, tiled=True)
     inverse = inverse_table(kept_bins)
-    norm_scale = 0.5 / math.sqrt(win_dev * lax.axis_size("gy") * bin_count)
-    freq_white = lax.all_to_all(white, "gx", split_axis=3, concat_axis=1, tiled=True)
-    all_channels = freq_white.shape[1]
-    empty_sum = jnp.zeros((off_dev, all_channels, 2, freq_white.shape[3]), jnp.float32)
-    window_block = lax.all_gather(freq_white, "gy", axis=0, tiled=True)
-    widened = jnp.concatenate(
-        [
-            window_block,
-            jnp.zeros(
-                (window_block.shape[0], band_span, 2, window_block.shape[3]), window_block.dtype
-            ),
-        ],
-        axis=1,
-    )
-    cross_sum = add_cross(empty_sum, widened, my_offsets, all_channels).astype(jnp.bfloat16)
+    norm_scale = 0.5 / math.sqrt(windows * bin_count)
     lagged = (
-        jnp.einsum(
-            "ocpk,pkl->ocl",
-            lax.all_to_all(cross_sum, "gx", split_axis=1, concat_axis=3, tiled=True),
-            inverse,
-            preferred_element_type=jnp.float32,
-        )
-        * norm_scale
+        jnp.einsum("opck,pkl->ocl", cross, inverse, preferred_element_type=jnp.float32) * norm_scale
     )
     return lagged.astype(jnp.bfloat16)
 

time: 166 us -> 138 us (0.83)
  other arithmetic: 56.5 us -> 21.7 us
  local copies, waits for them, and re-layouts: 38.2 us -> 11.6 us
  Pallas kernels: 0 us -> 17.7 us
  between operations: 0.17 us -> 13.6 us
  waiting for transfers between devices: 46.2 us -> 56.5 us
  starting transfers between devices: 11.1 us -> 3.74 us
    all_gather x0 -> x1, waiting for transfers between devices: none -> 40.6 us  [local(): all_white = lax.all_gather(rows_white, 'gx', axis=0, tiled=True)]
    all_to_all x2 -> x1, waiting for transfers between devices: 46.2 us -> 15.8 us  [local(): cross = lax.all_to_all(cross, 'gy', split_axis=0, concat_axis=3, tiled=True)]
    pallas_call x0 -> x1, Pallas kernels: none -> 17.7 us  [cross_spectra(): pl.pallas_call(kernel, grid_spec=pltpu.PrefetchScalarGridSpec(num_scalar_...]
    convert_element_type x5 -> x1, other arithmetic: 17.2 us -> 3.85 us  [local(): cross_spectra(padded, pair_offsets.astype(jnp.int32), base, ch_dev)]
    reduce_sum x4 -> x0, other arithmetic: 12.3 us -> none  [one_offset(): jnp.sum(own_part[:, :, 0] * theirs[:, :, 0] + own_part[:, :, 1] * theirs[...]
    gather x4 -> x0, local copies, waits for them, and re-layouts: 12.2 us -> none  [one_offset(): lax.dynamic_slice_in_dim(window_block, shift_by, own_count, 1)]
    dynamic_update_slice x4 -> x0, other arithmetic: 8.78 us -> none  [one_group(): lax.dynamic_update_slice_in_dim(carried, current + update, group_index *...]
    all_to_all x0 -> x1, blocking collectives: none -> 8.64 us  [local(): lax.all_to_all(white, 'gy', split_axis=3, concat_axis=0, tiled=True)]
  transfers between devices with their start and end apart: 2 -> 2, of which waited for: 2 -> 2; matrix products, arithmetic and copies ran while one was open for 6% -> 7% of each run, Pallas kernels for 0% -> 0%
where the time goes in v4:
time: 138 us
  waiting for transfers between devices  56.5 us (41%)
  other arithmetic  21.7 us (16%)
  Pallas kernels  17.7 us (13%)
  between operations  13.6 us (10%)
  local copies, waits for them, and re-layouts  11.6 us (8%)
  blocking collectives  8.64 us (6%)
  matrix products  4.52 us (3%)
  starting transfers between devices  3.74 us (3%)
    all_gather x1, waiting for transfers between devices, local(): all_white = lax.all_gather(rows_white, 'gx', axis=0, tiled=True)  40.6 us
    pallas_call x1, Pallas kernels, cross_spectra(): pl.pallas_call(kernel, grid_spec=pltpu.PrefetchScalarGridSpec(num_scalar_...  17.7 us
    all_to_all x1, waiting for transfers between devices, local(): cross = lax.all_to_all(cross, 'gy', split_axis=0, concat_axis=3, tiled=True)  15.8 us
    another operation x2, other arithmetic  13.5 us
    all_to_all x1, blocking collectives, local(): lax.all_to_all(white, 'gy', split_axis=3, concat_axis=0, tiled=True)  8.64 us
    convert_element_type x1, other arithmetic, local(): cross_spectra(padded, pair_offsets.astype(jnp.int32), base, ch_dev)  3.85 us
    all_to_all x1, starting transfers between devices, local(): cross = lax.all_to_all(cross, 'gy', split_axis=0, concat_axis=3, tiled=True)  3.74 us
  transfers between devices with their start and end apart: 2, of which 2 were waited for; matrix products, arithmetic and copies ran while one was open for 7% of the time, Pallas kernels for 0%

profile of v4, /device:TPU:0, one launch (start us, length us, event | category | flops | bytes accessed | tf_op | source)
XLA Modules:
  0.0 138.0 jit_solution(11497124366807785811)
XLA Ops:
  6.5 0.0 all-gather.2.cloned.1.call-start
  6.5 1.2 fusion.32
  7.8 0.7 add_select_fusion.4
  8.5 1.8 %fusion.27 = (f32[64,1024]{1,0:T(8,128)S(1)}, f32[64,1024]{1,0:T(8,128)S(1)}) fusion(s32[1024]{0:T(1024)} %param.4, s32[64]{0:T(128)S(1)} %iota_multiply_fusion), kind=kLoop, calls=%fused_computation.50 | loop fusion | flops 917504 | bytes 528640 | tf_op jit(solution)/shard_map/cos | solution.py:81
  10.2 1.3 copy.35
  11.6 0.4 reshape_reshape.3
  12.0 0.3 copy.36
  12.3 3.7 %subtract_convert_fusion = (bf16[64,32,1024]{2,1,0:T(8,128)(2,1)S(1)}, bf16[64,32,1024]{2,1,0:T(8,128)(2,1)S(1)}) fusion(f32[64,1024]{1,0:T(8,128)S(1)} %get-tuple-element.16, f32[32,1024]{1,0:T(8,128)S(1)} %get-tuple-element.20, f32[64,1024]{1,0:T(8,128)S(1)} %get-tuple-element.15, f32[32,1024]{1,0:T(8,128)S(1)} %get-tuple-element.19), kind=kLoop, calls=%fused_computation.5 | loop fusion | flops 18874368 | bytes 9175040 | tf_op jit(solution)/shard_map/convert.5
  15.9 2.5 %fusion.4 = f32[128,2048]{0,1:T(8,128)S(1)} fusion(bf16[128,2048]{1,0:T(8,128)(2,1)S(1)} %bitcast.67, bf16[2048,1024]{1,0:T(8,128)(2,1)S(1)} %bitcast.62, bf16[2048,1024]{1,0:T(8,128)(2,1)S(1)} %bitcast.61), kind=kOutput, calls=%fused_computation.11 | convolution fusion | flops 1090519040 | bytes 9961472 | tf_op jit(solution)/shard_map/dot_general | solution.py:94
  18.4 0.3 copy.37
  18.7 0.9 reshape.351
  19.6 0.8 fusion.39
  20.4 0.2 cosine_round-nearest-even_fusion
  20.6 0.2 fusion.17
  20.9 0.1 multiply_reduce_fusion
  21.0 0.2 concatenate.15
  21.2 0.1 rsqrt.12
  21.3 0.2 multiply_convert_fusion
  21.5 0.8 copy.39
  22.3 1.1 reshape.355
  23.4 8.6 %all_to_all.36 = bf16[4,2,8192]{2,1,0:T(2,128)(2,1)S(1)} all-to-all(bf16[4,2,8192]{2,1,0:T(2,128)(2,1)S(1)} %reshape.355), channel_id=1, replica_groups=mesh['gx'=8,'gy'=4] {'gy'}, dimensions={0} | all-to-all | bytes 262144 | tf_op jit(solution)/shard_map/all_to_all | solution.py:118
  32.0 0.7 reshape.356
  32.7 1.4 %copy.45 = bf16[2,16,2,4,256]{4,3,1,2,0:T(4,128)(2,1)S(1)} copy(bf16[2,16,2,4,256]{1,2,0,4,3:T(2,128)(2,1)S(1)} %bitcast.60) | data formatting | bytes 262144 | tf_op jit(solution)/shard_map/all_to_all | solution.py:118
  34.1 0.0 copy-start
  34.1 0.7 copy.57
  34.9 0.0 all-gather.2.cloned.1.call-update
  34.9 40.6 %all-gather.2.cloned.1.call-done = bf16[128,16,256]{2,1,0:T(8,128)(2,1)} async-done(((bf16[16,16,256]{2,1,0:T(8,128)(2,1)}), bf16[128,16,256]{2,1,0:T(8,128)(2,1)}) %all-gather.2.cloned.1.call-update) | async-done | bytes 1048592 | tf_op jit(solution)/shard_map/all_gather | solution.py:122
  75.5 1.4 concatenate.16.white_ref
  76.9 0.0 copy-done
  76.9 17.7 %shard_map.37 = f32[128,2,16,256]{3,2,1,0:T(8,128)} custom-call(s32[128]{0:T(128)S(1)} %copy-done, s32[1]{0:T(128)} %bitcast.base_ref, bf16[256,16,256]{2,1,0:T(8,128)(2,1)S(1)} %concatenate.16.white_ref), custom_call_target="tpu_custom_call" | custom-call | flops 67108864 | bytes 6291456 | tf_op jit(solution)/shard_map/pallas_call | solution.py:51
  94.6 3.9 %convert_element_type.60 = bf16[128,2,16,256]{3,2,1,0:T(8,128)(2,1)} convert(f32[128,2,16,256]{3,2,1,0:T(8,128)} %shard_map.37) | non-fusion elementwise | flops 1048576 | bytes 6291456 | tf_op jit(solution)/shard_map/convert_element_type | solution.py:127
  98.4 0.0 copy-start.2
  98.4 3.7 %all-to-all-start.1 = ((bf16[128,2,16,256]{3,2,1,0:T(8,128)(2,1)}), bf16[128,2,16,256]{3,2,1,0:T(8,128)(2,1)S(1)}, u32[]{:S(2)}, u32[]{:S(2)}) async-start(bf16[128,2,16,256]{3,2,1,0:T(8,128)(2,1)} %convert_element_type.60), calls=%async_computation.1 | async-start | bytes 4194304 | tf_op jit(solution)/shard_map/all_to_all | solution.py:128
  102.2 0.0 copy-done.2
  102.2 9.8 %cosine_convert_fusion = (bf16[1,1024,512]{2,1,0:T(8,128)(2,1)S(1)}, bf16[1,1024,512]{2,1,0:T(8,128)(2,1)}) fusion(s32[512]{0:T(512)S(1)} %iota_add_fusion, s32[1024]{0:T(1024)S(1)} %copy-done.2), kind=kLoop, calls=%fused_computation.20 | loop fusion | flops 8912896 | bytes 2103296 | tf_op jit(solution)/shard_map/convert
  112.0 15.8 %all-to-all-done.1 = bf16[128,2,16,256]{3,2,1,0:T(8,128)(2,1)S(1)} async-done(((bf16[128,2,16,256]{3,2,1,0:T(8,128)(2,1)}), bf16[128,2,16,256]{3,2,1,0:T(8,128)(2,1)S(1)}, u32[]{:S(2)}, u32[]{:S(2)}) %all-to-all-start.1) | async-done | bytes 2097184 | tf_op jit(solution)/shard_map/all_to_all | solution.py:128
  127.8 0.0 copy-start.1
  127.8 0.3 copy.48
  128.1 0.9 copy-done.1
  129.1 2.1 %fusion.15 = bf16[32,16,512]{2,1,0:T(8,128)(2,1)} fusion(bf16[32,2,16,1024]{3,2,1,0:T(8,128)(2,1)S(1)} %bitcast.63, bf16[1,1024,512]{2,1,0:T(8,128)(2,1)S(1)} %copy-done.1, bf16[1,1024,512]{2,1,0:T(8,128)(2,1)S(1)} %get-tuple-element.13), kind=kOutput, calls=%fused_computation.23 | convolution fusion | flops 1075314688 | bytes 4718592 | tf_op jit(solution)/shard_map/opck,pkl->ocl/dot_general | solution.py:132
  (4 shorter events, 0.0 us)
Async XLA Ops:
  6.5 69.0 %all-gather.2.cloned.1.call-start = ((), (), s32[]{:S(2)}) async-start(), calls=%async_computation.2 | async-start | bytes 1179648 | tf_op jit(solution)/shard_map/all_gather | solution.py:122
  34.1 42.8 %copy-start = (s32[128]{0:T(128)S(1)}, s32[128]{0:T(128)}, u32[]{:S(2)}) copy-start(s32[128]{0:T(128)} %offsets_ref.1) | copy-start | bytes 1540
  98.4 3.8 %copy-start.2 = (s32[1024]{0:T(1024)S(1)}, s32[1024]{0:T(1024)}, u32[]{:S(2)}) copy-start(s32[1024]{0:T(1024)} %param.4) | copy-start | bytes 12292
  98.4 29.4 %all-to-all-start.1 = ((bf16[128,2,16,256]{3,2,1,0:T(8,128)(2,1)}), bf16[128,2,16,256]{3,2,1,0:T(8,128)(2,1)S(1)}, u32[]{:S(2)}, u32[]{:S(2)}) async-start(bf16[128,2,16,256]{3,2,1,0:T(8,128)(2,1)} %convert_element_type.60), calls=%async_computation.1 | async-start | bytes 4194304 | tf_op jit(solution)/shard_map/all_to_all | solution.py:128
  127.8 1.2 copy-start.1
Sparse Core Ops, SparseCore 0:
  35.0 40.4 all-gather.1

commit v5 on v4

--- a/solution.py
+++ b/solution.py
@@ -13,11 +13,20 @@
 
 
 def inverse_table(kept_bins):
-    lag_index = jnp.arange(LAGS, dtype=jnp.int32) - LAGS // 2
-    angles = jnp.mod(kept_bins[:, None] * lag_index[None, :], SAMPLES).astype(jnp.float32) * (
-        2.0 * math.pi / SAMPLES
-    )
-    return jnp.stack([jnp.cos(angles), -jnp.sin(angles)], axis=0).astype(jnp.bfloat16)
+    fine_count = 32
+    coarse_count = LAGS // fine_count
+
+    def angles(index):
+        return jnp.mod(kept_bins[:, None] * index[None, :], SAMPLES).astype(jnp.float32) * (
+            2.0 * math.pi / SAMPLES
+        )
+
+    fine = angles(jnp.arange(fine_count, dtype=jnp.int32))[:, None, :]
+    coarse = angles(fine_count * jnp.arange(coarse_count, dtype=jnp.int32) - LAGS // 2)[:, :, None]
+    cos_f, sin_f, cos_c, sin_c = jnp.cos(fine), jnp.sin(fine), jnp.cos(coarse), jnp.sin(coarse)
+    cos_t = (cos_f * cos_c - sin_f * sin_c).reshape(kept_bins.shape[0], LAGS)
+    sin_t = (sin_f * cos_c + cos_f * sin_c).reshape(kept_bins.shape[0], LAGS)
+    return jnp.stack([cos_t, -sin_t], axis=0).astype(jnp.bfloat16)
 
 
 def whiten(spectra):
@@ -124,8 +133,13 @@
         [all_white, jnp.zeros((band_span,) + all_white.shape[1:], all_white.dtype)], axis=0
     )
     base = (lax.axis_index("gx") * ch_dev).astype(jnp.int32).reshape(1)
-    cross = cross_spectra(padded, pair_offsets.astype(jnp.int32), base, ch_dev).astype(jnp.bfloat16)
-    cross = lax.all_to_all(cross, "gy", split_axis=0, concat_axis=3, tiled=True)
+    gy_count = lax.axis_size("gy")
+    halves = pair_offsets.astype(jnp.int32).reshape(gy_count, 2, band_span // (2 * gy_count))
+    parts = []
+    for h in range(2):
+        part = cross_spectra(padded, halves[:, h].reshape(-1), base, ch_dev).astype(jnp.bfloat16)
+        parts.append(lax.all_to_all(part, "gy", split_axis=0, concat_axis=3, tiled=True))
+    cross = jnp.concatenate(parts, axis=0)
     inverse = inverse_table(kept_bins)
     norm_scale = 0.5 / math.sqrt(windows * bin_count)
     lagged = (

time: 138 us -> 134 us (0.971)
  other arithmetic: 21.7 us -> 13 us
  waiting for transfers between devices: 56.5 us -> 52 us
  local copies, waits for them, and re-layouts: 11.6 us -> 15.6 us
  starting transfers between devices: 3.74 us -> 7.03 us
  matrix products: 4.52 us -> 6.06 us
    another operation x2, other arithmetic: 13.5 us -> 5.42 us
    all_to_all x1 -> x2, waiting for transfers between devices: 15.8 us -> 11.6 us  [local(): lax.all_to_all(part, 'gy', split_axis=0, concat_axis=3, tiled=True)]
    all_to_all x1 -> x2, starting transfers between devices: 3.74 us -> 7.03 us  [local(): lax.all_to_all(part, 'gy', split_axis=0, concat_axis=3, tiled=True)]
    sub x0 -> x1, local copies, waits for them, and re-layouts: none -> 2.29 us  [inverse_table(): cos_t = (cos_f * cos_c - sin_f * sin_c).reshape(kept_bins.shape[0], LAGS)]
    dot_general x1, matrix products: 2.06 us -> 3.6 us  [local(): jnp.einsum('opck,pkl->ocl', cross, inverse, preferred_element_type=jnp.fl...]
    convert_element_type x1 -> x2, other arithmetic: 3.85 us -> 2.35 us  [local(): cross_spectra(padded, halves[:, h].reshape(-1), base, ch_dev)]
    pallas_call x1 -> x2, Pallas kernels: 17.7 us -> 17.3 us  [cross_spectra(): pl.pallas_call(kernel, grid_spec=pltpu.PrefetchScalarGridSpec(num_scalar_...]
  transfers between devices with their start and end apart: 2 -> 3, of which waited for: 2 -> 3; matrix products, arithmetic and copies ran while one was open for 7% -> 7% of each run, Pallas kernels for 0% -> 6%
where the time goes in v5:
time: 134 us; the launch traced here: 133 us
  waiting for transfers between devices  52 us (39%)
  Pallas kernels  17.3 us (13%)
  local copies, waits for them, and re-layouts  15.6 us (12%)
  between operations  13.6 us (10%)
  other arithmetic  13 us (10%)
  blocking collectives  8.64 us (6%)
  starting transfers between devices  7.03 us (5%)
  matrix products  6.06 us (5%)
    all_gather x1, waiting for transfers between devices, local(): all_white = lax.all_gather(rows_white, 'gx', axis=0, tiled=True)  40.4 us
    pallas_call x2, Pallas kernels, cross_spectra(): pl.pallas_call(kernel, grid_spec=pltpu.PrefetchScalarGridSpec(num_scalar_...  17.3 us
    all_to_all x2, waiting for transfers between devices, local(): lax.all_to_all(part, 'gy', split_axis=0, concat_axis=3, tiled=True)  11.6 us
    all_to_all x1, blocking collectives, local(): lax.all_to_all(white, 'gy', split_axis=3, concat_axis=0, tiled=True)  8.64 us
    all_to_all x2, starting transfers between devices, local(): lax.all_to_all(part, 'gy', split_axis=0, concat_axis=3, tiled=True)  7.03 us
    another operation x2, other arithmetic  5.42 us
    dot_general x1, matrix products, local(): jnp.einsum('opck,pkl->ocl', cross, inverse, preferred_element_type=jnp.fl...  3.6 us
  transfers between devices with their start and end apart: 3, of which 3 were waited for; matrix products, arithmetic and copies ran while one was open for 7% of the time, Pallas kernels for 6%

profile of v5, /device:TPU:0, one launch (start us, length us, event | category | flops | bytes accessed | tf_op | source)
XLA Modules:
  0.0 133.3 jit_solution(5367254705532024818)
XLA Ops:
  6.5 0.0 all-gather.2.cloned.1.call-start
  6.5 1.2 fusion.45
  7.8 0.7 add_select_fusion.5
  8.5 1.8 %fusion.34 = (f32[64,1024]{1,0:T(8,128)S(1)}, f32[64,1024]{1,0:T(8,128)S(1)}) fusion(s32[1024]{0:T(1024)} %param.4, s32[64]{0:T(128)S(1)} %iota_multiply_fusion), kind=kLoop, calls=%fused_computation.52 | loop fusion | flops 917504 | bytes 528640 | tf_op jit(solution)/shard_map/cos | solution.py:90
  10.2 1.3 %copy.48 = bf16[2,16,8192]{2,1,0:T(8,128)(2,1)S(1)} copy(bf16[2,16,8192]{2,0,1:T(2,128)(2,1)} %bitcast.72) | data formatting | bytes 1048576 | tf_op jit(solution)/shard_map/transpose | solution.py:124
  11.6 0.4 reshape_reshape.3
  12.0 0.3 copy.49
  12.3 3.7 %subtract_convert_fusion = (bf16[64,32,1024]{2,1,0:T(8,128)(2,1)S(1)}, bf16[64,32,1024]{2,1,0:T(8,128)(2,1)S(1)}) fusion(f32[64,1024]{1,0:T(8,128)S(1)} %get-tuple-element.18, f32[32,1024]{1,0:T(8,128)S(1)} %get-tuple-element.24, f32[64,1024]{1,0:T(8,128)S(1)} %get-tuple-element.17, f32[32,1024]{1,0:T(8,128)S(1)} %get-tuple-element.23), kind=kLoop, calls=%fused_computation.5 | loop fusion | flops 18874368 | bytes 9175040 | tf_op jit(solution)/shard_map/convert.7
  15.9 2.5 %fusion.4 = f32[128,2048]{0,1:T(8,128)S(1)} fusion(bf16[128,2048]{1,0:T(8,128)(2,1)S(1)} %bitcast.73, bf16[2048,1024]{1,0:T(8,128)(2,1)S(1)} %bitcast.63, bf16[2048,1024]{1,0:T(8,128)(2,1)S(1)} %bitcast.62), kind=kOutput, calls=%fused_computation.6 | convolution fusion | flops 1090519040 | bytes 9961472 | tf_op jit(solution)/shard_map/dot_general | solution.py:103
  18.4 0.3 copy.50
  18.7 0.9 reshape.443
  19.6 0.8 fusion.54
  20.4 0.2 cosine_round-nearest-even_fusion
  20.6 0.0 copy-start.2
  20.6 0.2 fusion.19
  20.9 0.1 multiply_reduce_fusion
  21.0 0.2 concatenate.18
  21.2 0.1 rsqrt.12
  21.3 0.2 multiply_convert_fusion.1
  21.5 0.8 copy.52
  22.3 1.1 reshape.459
  23.4 8.6 %all_to_all.54 = bf16[4,2,8192]{2,1,0:T(2,128)(2,1)S(1)} all-to-all(bf16[4,2,8192]{2,1,0:T(2,128)(2,1)S(1)} %reshape.459), channel_id=1, replica_groups=mesh['gx'=8,'gy'=4] {'gy'}, dimensions={0} | all-to-all | bytes 262144 | tf_op jit(solution)/shard_map/all_to_all | solution.py:127
  32.0 0.7 reshape.460
  32.7 1.4 %copy.61 = bf16[2,16,2,4,256]{4,3,1,2,0:T(4,128)(2,1)S(1)} copy(bf16[2,16,2,4,256]{1,2,0,4,3:T(2,128)(2,1)S(1)} %bitcast.61) | data formatting | bytes 262144 | tf_op jit(solution)/shard_map/all_to_all | solution.py:127
  34.1 0.7 copy.74
  34.9 0.0 all-gather.2.cloned.1.call-update
  34.9 0.1 reshape.440
  35.0 0.1 reshape_squeeze.6.offsets_ref
  35.1 40.4 %all-gather.2.cloned.1.call-done = bf16[128,16,256]{2,1,0:T(8,128)(2,1)} async-done(((bf16[16,16,256]{2,1,0:T(8,128)(2,1)}), bf16[128,16,256]{2,1,0:T(8,128)(2,1)}) %all-gather.2.cloned.1.call-update) | async-done | bytes 1048592 | tf_op jit(solution)/shard_map/all_gather | solution.py:131
  75.5 1.4 %concatenate.19.white_ref = bf16[256,16,256]{2,1,0:T(8,128)(2,1)S(1)} pad(bf16[128,16,256]{2,1,0:T(8,128)(2,1)} %all-gather.2.cloned.1.call-done, bf16[]{:T(256)} %constant.90.clone.1), padding=0_128x0_0x0_0 | pad | bytes 3145730 | tf_op jit(solution)/shard_map/concatenate | solution.py:132
  76.9 8.7 %shard_map.37 = f32[64,2,16,256]{3,2,1,0:T(8,128)S(1)} custom-call(s32[64]{0:T(128)S(1)} %reshape_squeeze.6.offsets_ref, s32[1]{0:T(128)} %bitcast.base_ref, bf16[256,16,256]{2,1,0:T(8,128)(2,1)S(1)} %concatenate.19.white_ref), custom_call_target="tpu_custom_call" | custom-call | flops 33554432 | bytes 4194304 | tf_op jit(solution)/shard_map/pallas_call | solution.py:60
  85.6 1.2 convert_element_type.69
  86.8 3.5 %all-to-all-start.1 = ((bf16[64,2,16,256]{3,2,1,0:T(8,128)(2,1)}), bf16[64,2,16,256]{3,2,1,0:T(8,128)(2,1)S(1)}, u32[]{:S(2)}, u32[]{:S(2)}) async-start(bf16[64,2,16,256]{3,2,1,0:T(8,128)(2,1)} %convert_element_type.69), calls=%async_computation.1 | async-start | bytes 2097152 | tf_op jit(solution)/shard_map/all_to_all | solution.py:141
  90.3 0.1 reshape_squeeze.7.offsets_ref
  90.4 8.7 %shard_map.38 = f32[64,2,16,256]{3,2,1,0:T(8,128)S(1)} custom-call(s32[64]{0:T(128)S(1)} %reshape_squeeze.7.offsets_ref, s32[1]{0:T(128)} %bitcast.base_ref, bf16[256,16,256]{2,1,0:T(8,128)(2,1)S(1)} %concatenate.19.white_ref), custom_call_target="tpu_custom_call" | custom-call | flops 33554432 | bytes 4194304 | tf_op jit(solution)/shard_map/pallas_call | solution.py:60
  99.0 1.1 convert_element_type.70
  100.2 4.5 %all-to-all-done.1 = bf16[64,2,16,256]{3,2,1,0:T(8,128)(2,1)S(1)} async-done(((bf16[64,2,16,256]{3,2,1,0:T(8,128)(2,1)}), bf16[64,2,16,256]{3,2,1,0:T(8,128)(2,1)S(1)}, u32[]{:S(2)}, u32[]{:S(2)}) %all-to-all-start.1) | async-done | bytes 1048608 | tf_op jit(solution)/shard_map/all_to_all | solution.py:141
  104.7 3.5 %all-to-all-start.2 = ((bf16[64,2,16,256]{3,2,1,0:T(8,128)(2,1)}), bf16[64,2,16,256]{3,2,1,0:T(8,128)(2,1)S(1)}, u32[]{:S(2)}, u32[]{:S(2)}) async-start(bf16[64,2,16,256]{3,2,1,0:T(8,128)(2,1)} %convert_element_type.70), calls=%async_computation.2 | async-start | bytes 2097152 | tf_op jit(solution)/shard_map/all_to_all | solution.py:141
  108.3 0.3 fusion.47
  108.6 0.5 fusion.43
  109.1 1.8 %subtract_convert_fusion.1 = (bf16[1024,16,32]{0,2,1:T(8,128)(2,1)}, bf16[1024,16,32]{0,2,1:T(8,128)(2,1)S(1)}) fusion(f32[1024,16]{0,1:T(8,128)S(1)} %get-tuple-element.20, f32[1024,32]{0,1:T(8,128)S(1)} %get-tuple-element.26, f32[1024,16]{0,1:T(8,128)S(1)} %get-tuple-element.19, f32[1024,32]{0,1:T(8,128)S(1)} %get-tuple-element.25), kind=kLoop, calls=%fused_computation.15 | loop fusion | flops 4718592 | bytes 2490368 | tf_op jit(solution)/shard_map/convert.3
  110.9 2.3 %copy.58 = bf16[1,1024,512]{2,1,0:T(8,128)(2,1)} copy(bf16[1,1024,512]{1,2,0:T(8,128)(2,1)} %bitcast.67) | data formatting | bytes 2097152 | tf_op jit(solution)/shard_map/sub | solution.py:27
  113.2 1.3 %copy.59 = bf16[1,1024,512]{2,1,0:T(8,128)(2,1)} copy(bf16[1,1024,512]{1,2,0:T(8,128)(2,1)S(1)} %bitcast.66) | data formatting | bytes 2097152 | tf_op jit(solution)/shard_map/neg | solution.py:29
  114.5 1.1 copy.64
  115.7 7.0 %all-to-all-done.2 = bf16[64,2,16,256]{3,2,1,0:T(8,128)(2,1)S(1)} async-done(((bf16[64,2,16,256]{3,2,1,0:T(8,128)(2,1)}), bf16[64,2,16,256]{3,2,1,0:T(8,128)(2,1)S(1)}, u32[]{:S(2)}, u32[]{:S(2)}) %all-to-all-start.2) | async-done | bytes 1048608 | tf_op jit(solution)/shard_map/all_to_all | solution.py:141
  122.7 0.1 copy.65
  122.8 0.0 copy-done
  122.8 3.6 %multiply_convert_fusion = bf16[32,16,512]{2,1,0:T(8,128)(2,1)} fusion(bf16[1,1024,512]{2,1,0:T(8,128)(2,1)} %copy.59, bf16[1,1024,512]{2,1,0:T(8,128)(2,1)S(1)} %copy-done, bf16[16,2,16,1024]{3,2,1,0:T(8,128)(2,1)S(1)} %bitcast.70, bf16[16,2,16,1024]{3,2,1,0:T(8,128)(2,1)} %bitcast.69), kind=kOutput, calls=%fused_computation.17 | convolution fusion | flops 1076363264 | bytes 4718592 | tf_op jit(solution)/shard_map/opck,pkl->ocl/dot_general | solution.py:146
  (9 shorter events, 0.1 us)
Async XLA Ops:
  6.5 69.0 %all-gather.2.cloned.1.call-start = ((), (), s32[]{:S(2)}) async-start(), calls=%async_computation.3 | async-start | bytes 1179648 | tf_op jit(solution)/shard_map/all_gather | solution.py:131
  20.6 14.3 %copy-start.2 = (s32[128]{0:T(128)S(1)}, s32[128]{0:T(128)}, u32[]{:S(2)}) copy-start(s32[128]{0:T(128)} %param.5) | copy-start | bytes 1540
  86.8 18.0 %all-to-all-start.1 = ((bf16[64,2,16,256]{3,2,1,0:T(8,128)(2,1)}), bf16[64,2,16,256]{3,2,1,0:T(8,128)(2,1)S(1)}, u32[]{:S(2)}, u32[]{:S(2)}) async-start(bf16[64,2,16,256]{3,2,1,0:T(8,128)(2,1)} %convert_element_type.69), calls=%async_computation.1 | async-start | bytes 2097152 | tf_op jit(solution)/shard_map/all_to_all | solution.py:141
  90.4 17.9 %copy-start.1 = (s32[1024]{0:T(1024)S(1)}, s32[1024]{0:T(1024)}, u32[]{:S(2)}) copy-start(s32[1024]{0:T(1024)} %param.4) | copy-start | bytes 12292
  104.7 18.0 %all-to-all-start.2 = ((bf16[64,2,16,256]{3,2,1,0:T(8,128)(2,1)}), bf16[64,2,16,256]{3,2,1,0:T(8,128)(2,1)S(1)}, u32[]{:S(2)}, u32[]{:S(2)}) async-start(bf16[64,2,16,256]{3,2,1,0:T(8,128)(2,1)} %convert_element_type.70), calls=%async_computation.2 | async-start | bytes 2097152 | tf_op jit(solution)/shard_map/all_to_all | solution.py:141
  114.5 8.3 %copy-start = (bf16[1,1024,512]{2,1,0:T(8,128)(2,1)S(1)}, bf16[1,1024,512]{2,1,0:T(8,128)(2,1)}, u32[]{:S(2)}) copy-start(bf16[1,1024,512]{2,1,0:T(8,128)(2,1)} %copy.58) | copy-start | bytes 3145732
Sparse Core Ops, SparseCore 0:
  35.0 40.4 all-gather.1

commit v6 on v5

--- a/solution.py
+++ b/solution.py
@@ -128,19 +128,20 @@
     windows = freq_white.shape[0]
     shard_bins = freq_white.shape[3]
     rows_white = jnp.transpose(freq_white, (1, 2, 0, 3)).reshape(ch_dev, 2 * windows, shard_bins)
-    all_white = lax.all_gather(rows_white, "gx", axis=0, tiled=True)
-    padded = jnp.concatenate(
-        [all_white, jnp.zeros((band_span,) + all_white.shape[1:], all_white.dtype)], axis=0
-    )
     base = (lax.axis_index("gx") * ch_dev).astype(jnp.int32).reshape(1)
-    gy_count = lax.axis_size("gy")
-    halves = pair_offsets.astype(jnp.int32).reshape(gy_count, 2, band_span // (2 * gy_count))
+    half_bins = shard_bins // 2
     parts = []
     for h in range(2):
-        part = cross_spectra(padded, halves[:, h].reshape(-1), base, ch_dev).astype(jnp.bfloat16)
+        own_half = rows_white[:, :, h * half_bins:(h + 1) * half_bins]
+        all_white = lax.all_gather(own_half, "gx", axis=0, tiled=True)
+        padded = jnp.concatenate(
+            [all_white, jnp.zeros((band_span,) + all_white.shape[1:], all_white.dtype)], axis=0
+        )
+        part = cross_spectra(padded, pair_offsets.astype(jnp.int32), base, ch_dev).astype(jnp.bfloat16)
         parts.append(lax.all_to_all(part, "gy", split_axis=0, concat_axis=3, tiled=True))
-    cross = jnp.concatenate(parts, axis=0)
-    inverse = inverse_table(kept_bins)
+    cross = jnp.concatenate(parts, axis=3)
+    bin_order = jnp.transpose(kept_bins.reshape(-1, 2, half_bins), (1, 0, 2)).reshape(-1)
+    inverse = inverse_table(bin_order)
     norm_scale = 0.5 / math.sqrt(windows * bin_count)
     lagged = (
         jnp.einsum("opck,pkl->ocl", cross, inverse, preferred_element_type=jnp.float32) * norm_scale

time: 134 us -> 137 us (1.022)
  blocking collectives: 8.64 us -> 63.9 us
  waiting for transfers between devices: 52 us -> 11.5 us
  between operations: 13.6 us -> 0.25 us
  starting transfers between devices: 7.03 us -> 11.2 us
  Pallas kernels: 17.3 us -> 15.6 us
    all_gather x0 -> x2, blocking collectives: none -> 63.9 us  [local(): all_white = lax.all_gather(own_half, 'gx', axis=0, tiled=True)]
    all_gather x1 -> x0, waiting for transfers between devices: 40.4 us -> none  [local(): all_white = lax.all_gather(rows_white, 'gx', axis=0, tiled=True)]
    all_to_all x1 -> x0, blocking collectives: 8.64 us -> none  [local(): lax.all_to_all(white, 'gy', split_axis=3, concat_axis=0, tiled=True)]
    all_to_all x2, waiting for transfers between devices: 11.6 us -> 6.88 us  [local(): lax.all_to_all(part, 'gy', split_axis=0, concat_axis=3, tiled=True)]
    all_to_all x0 -> x1, waiting for transfers between devices: none -> 4.67 us  [local(): lax.all_to_all(white, 'gy', split_axis=3, concat_axis=0, tiled=True)]
    all_to_all x0 -> x1, starting transfers between devices: none -> 4.21 us  [local(): lax.all_to_all(white, 'gy', split_axis=3, concat_axis=0, tiled=True)]
    pallas_call x2, Pallas kernels: 17.3 us -> 15.6 us  [cross_spectra(): pl.pallas_call(kernel, grid_spec=pltpu.PrefetchScalarGridSpec(num_scalar_...]
  transfers between devices with their start and end apart: 3 -> 3, of which waited for: 3 -> 2; matrix products, arithmetic and copies ran while one was open for 7% -> 6% of each run, Pallas kernels for 6% -> 6%
where the time goes in v6:
time: 137 us; the launch traced here: 136 us
  blocking collectives  63.9 us (47%)
  Pallas kernels  15.6 us (11%)
  local copies, waits for them, and re-layouts  14.6 us (11%)
  other arithmetic  13.1 us (10%)
  waiting for transfers between devices  11.5 us (8%)
  starting transfers between devices  11.2 us (8%)
  matrix products  6.06 us (4%)
    all_gather x2, blocking collectives, local(): all_white = lax.all_gather(own_half, 'gx', axis=0, tiled=True)  63.9 us
    pallas_call x2, Pallas kernels, cross_spectra(): pl.pallas_call(kernel, grid_spec=pltpu.PrefetchScalarGridSpec(num_scalar_...  15.6 us
    all_to_all x2, starting transfers between devices, local(): lax.all_to_all(part, 'gy', split_axis=0, concat_axis=3, tiled=True)  7.03 us
    all_to_all x2, waiting for transfers between devices, local(): lax.all_to_all(part, 'gy', split_axis=0, concat_axis=3, tiled=True)  6.88 us
    another operation x2, other arithmetic  5.4 us
    all_to_all x1, waiting for transfers between devices, local(): lax.all_to_all(white, 'gy', split_axis=3, concat_axis=0, tiled=True)  4.67 us
    all_to_all x1, starting transfers between devices, local(): lax.all_to_all(white, 'gy', split_axis=3, concat_axis=0, tiled=True)  4.21 us
    dot_general x1, matrix products, local(): jnp.einsum('opck,pkl->ocl', cross, inverse, preferred_element_type=jnp.fl...  3.6 us
  transfers between devices with their start and end apart: 3, of which 2 were waited for; matrix products, arithmetic and copies ran while one was open for 6% of the time, Pallas kernels for 6%

profile of v6, /device:TPU:0, one launch (start us, length us, event | category | flops | bytes accessed | tf_op | source)
XLA Modules:
  0.0 136.4 jit_solution(4325900954099144669)
XLA Ops:
  0.0 1.2 fusion.45
  1.2 0.7 add_select_fusion.5
  1.9 1.8 %fusion.34 = (f32[64,1024]{1,0:T(8,128)S(1)}, f32[64,1024]{1,0:T(8,128)S(1)}) fusion(s32[1024]{0:T(1024)} %param.4, s32[64]{0:T(128)S(1)} %iota_multiply_fusion), kind=kLoop, calls=%fused_computation.54 | loop fusion | flops 917504 | bytes 528640 | tf_op jit(solution)/shard_map/cos | solution.py:90
  3.7 1.3 copy.51
  5.0 0.4 reshape_reshape.3
  5.4 0.3 copy.52
  5.7 3.7 %subtract_convert_fusion = (bf16[64,32,1024]{2,1,0:T(8,128)(2,1)S(1)}, bf16[64,32,1024]{2,1,0:T(8,128)(2,1)S(1)}) fusion(f32[64,1024]{1,0:T(8,128)S(1)} %get-tuple-element.18, f32[32,1024]{1,0:T(8,128)S(1)} %get-tuple-element.24, f32[64,1024]{1,0:T(8,128)S(1)} %get-tuple-element.17, f32[32,1024]{1,0:T(8,128)S(1)} %get-tuple-element.23), kind=kLoop, calls=%fused_computation.5 | loop fusion | flops 18874368 | bytes 9175040 | tf_op jit(solution)/shard_map/convert.7
  9.4 2.5 %fusion.4 = f32[128,2048]{0,1:T(8,128)S(1)} fusion(bf16[128,2048]{1,0:T(8,128)(2,1)S(1)} %bitcast.81, bf16[2048,1024]{1,0:T(8,128)(2,1)S(1)} %bitcast.71, bf16[2048,1024]{1,0:T(8,128)(2,1)S(1)} %bitcast.70), kind=kOutput, calls=%fused_computation.6 | convolution fusion | flops 1090519040 | bytes 9961472 | tf_op jit(solution)/shard_map/dot_general | solution.py:103
  11.9 0.3 copy.53
  12.2 0.9 reshape.457
  13.1 0.8 fusion.54
  13.9 0.2 cosine_round-nearest-even_fusion
  14.1 0.2 fusion.19
  14.3 0.1 multiply_reduce_fusion
  14.5 0.2 concatenate.21
  14.7 0.0 copy-start
  14.7 0.1 rsqrt.12
  14.8 0.2 multiply_convert_fusion.1
  15.0 0.8 copy.55
  15.8 1.7 %reshape.462 = bf16[4,2,8192]{2,1,0:T(2,128)(2,1)} reshape(bf16[1024,2,2,16]{3,2,1,0:T(2,128)(2,1)S(1)} %bitcast.68) | data formatting | bytes 262144
  17.5 4.2 %all-to-all-start = ((bf16[4,2,8192]{2,1,0:T(2,128)(2,1)}), bf16[4,2,8192]{2,1,0:T(2,128)(2,1)S(1)}, u32[]{:S(2)}, u32[]{:S(2)}) async-start(bf16[4,2,8192]{2,1,0:T(2,128)(2,1)} %reshape.462), calls=%async_computation | async-start | bytes 262144 | tf_op jit(solution)/shard_map/all_to_all | solution.py:127
  21.7 4.7 %all-to-all-done = bf16[4,2,8192]{2,1,0:T(2,128)(2,1)S(1)} async-done(((bf16[4,2,8192]{2,1,0:T(2,128)(2,1)}), bf16[4,2,8192]{2,1,0:T(2,128)(2,1)S(1)}, u32[]{:S(2)}, u32[]{:S(2)}) %all-to-all-start) | async-done | bytes 131104 | tf_op jit(solution)/shard_map/all_to_all | solution.py:127
  26.4 0.7 reshape.463
  27.1 1.4 %copy.65 = bf16[2,16,2,4,256]{4,3,1,2,0:T(4,128)(2,1)S(1)} copy(bf16[2,16,2,4,256]{1,2,0,4,3:T(2,128)(2,1)S(1)} %bitcast.69) | data formatting | bytes 262144 | tf_op jit(solution)/shard_map/all_to_all | solution.py:127
  28.5 0.1 copy.82
  28.6 32.5 %all_gather.6 = bf16[128,16,128]{2,1,0:T(8,128)(2,1)S(1)} all-gather(bf16[16,16,128]{2,1,0:T(8,128)(2,1)S(1)} %get-tuple-element.15), channel_id=1, replica_groups=mesh['gx'=8,'gy'=4] {'gx'}, dimensions={0}, use_global_device_ids=true | all-gather | bytes 589824 | tf_op jit(solution)/shard_map/all_gather | solution.py:136
  61.1 0.1 concatenate.22.white_ref
  61.3 0.0 copy-done
  61.3 7.8 %shard_map.37 = f32[128,2,16,128]{3,2,1,0:T(8,128)S(1)} custom-call(s32[128]{0:T(128)S(1)} %copy-done, s32[1]{0:T(128)} %bitcast.base_ref, bf16[256,16,128]{2,1,0:T(8,128)(2,1)S(1)} %concatenate.22.white_ref), custom_call_target="tpu_custom_call" | custom-call | flops 33554432 | bytes 3145728 | tf_op jit(solution)/shard_map/pallas_call | solution.py:60
  69.1 1.2 convert_element_type.69
  70.3 3.5 %all-to-all-start.1 = ((bf16[128,2,16,128]{3,2,1,0:T(8,128)(2,1)}), bf16[128,2,16,128]{3,2,1,0:T(8,128)(2,1)S(1)}, u32[]{:S(2)}, u32[]{:S(2)}) async-start(bf16[128,2,16,128]{3,2,1,0:T(8,128)(2,1)} %convert_element_type.69), calls=%async_computation.1 | async-start | bytes 2097152 | tf_op jit(solution)/shard_map/all_to_all | solution.py:141
  73.8 31.5 %all_gather.7 = bf16[128,16,128]{2,1,0:T(8,128)(2,1)S(1)} all-gather(bf16[16,16,128]{2,1,0:T(8,128)(2,1)S(1)} %get-tuple-element.16), channel_id=1, replica_groups=mesh['gx'=8,'gy'=4] {'gx'}, dimensions={0}, use_global_device_ids=true | all-gather | bytes 589824 | tf_op jit(solution)/shard_map/all_gather | solution.py:136
  105.3 0.1 concatenate.23.white_ref
  105.5 0.0 copy-start.2
  105.5 7.8 %shard_map.38 = f32[128,2,16,128]{3,2,1,0:T(8,128)S(1)} custom-call(s32[128]{0:T(128)S(1)} %copy-done, s32[1]{0:T(128)} %bitcast.base_ref, bf16[256,16,128]{2,1,0:T(8,128)(2,1)S(1)} %concatenate.23.white_ref), custom_call_target="tpu_custom_call" | custom-call | flops 33554432 | bytes 3145728 | tf_op jit(solution)/shard_map/pallas_call | solution.py:60
  113.3 1.2 convert_element_type.70
  114.5 0.0 all-to-all-done.1
  114.5 3.5 %all-to-all-start.2 = ((bf16[128,2,16,128]{3,2,1,0:T(8,128)(2,1)}), bf16[128,2,16,128]{3,2,1,0:T(8,128)(2,1)S(1)}, u32[]{:S(2)}, u32[]{:S(2)}) async-start(bf16[128,2,16,128]{3,2,1,0:T(8,128)(2,1)} %convert_element_type.70), calls=%async_computation.2 | async-start | bytes 2097152 | tf_op jit(solution)/shard_map/all_to_all | solution.py:141
  118.0 0.3 fusion.47
  118.4 0.5 fusion.43
  118.9 1.7 %subtract_convert_fusion.1 = (bf16[1024,16,32]{0,2,1:T(8,128)(2,1)}, bf16[1024,16,32]{0,2,1:T(8,128)(2,1)S(1)}) fusion(f32[1024,16]{0,1:T(8,128)S(1)} %get-tuple-element.20, f32[1024,32]{0,1:T(8,128)S(1)} %get-tuple-element.26, f32[1024,16]{0,1:T(8,128)S(1)} %get-tuple-element.19, f32[1024,32]{0,1:T(8,128)S(1)} %get-tuple-element.25), kind=kLoop, calls=%fused_computation.15 | loop fusion | flops 4718592 | bytes 2490368 | tf_op jit(solution)/shard_map/convert.3
  120.7 2.3 %copy.62 = bf16[1,1024,512]{2,1,0:T(8,128)(2,1)} copy(bf16[1,1024,512]{1,2,0:T(8,128)(2,1)} %bitcast.75) | data formatting | bytes 2097152 | tf_op jit(solution)/shard_map/sub | solution.py:27
  122.9 1.3 copy.63
  124.3 1.3 copy.81
  125.6 6.9 %all-to-all-done.2 = bf16[128,2,16,128]{3,2,1,0:T(8,128)(2,1)S(1)} async-done(((bf16[128,2,16,128]{3,2,1,0:T(8,128)(2,1)}), bf16[128,2,16,128]{3,2,1,0:T(8,128)(2,1)S(1)}, u32[]{:S(2)}, u32[]{:S(2)}) %all-to-all-start.2) | async-done | bytes 1048608 | tf_op jit(solution)/shard_map/all_to_all | solution.py:141
  132.4 0.3 copy.80
  132.7 0.0 copy-done.1
  132.8 3.6 %multiply_convert_fusion = bf16[32,16,512]{2,1,0:T(8,128)(2,1)} fusion(bf16[1,1024,512]{2,1,0:T(8,128)(2,1)} %copy.63, bf16[1,1024,512]{2,1,0:T(8,128)(2,1)S(1)} %copy-done.1, bf16[32,2,16,512]{3,2,1,0:T(8,128)(2,1)S(1)} %bitcast.78, bf16[32,2,16,512]{3,2,1,0:T(8,128)(2,1)} %bitcast.77), kind=kOutput, calls=%fused_computation.19 | convolution fusion | flops 1079508992 | bytes 4718592 | tf_op jit(solution)/shard_map/opck,pkl->ocl/dot_general | solution.py:147
  (8 shorter events, 0.1 us)
Async XLA Ops:
  14.7 46.6 %copy-start = (s32[128]{0:T(128)S(1)}, s32[128]{0:T(128)}, u32[]{:S(2)}) copy-start(s32[128]{0:T(128)} %offsets_ref.3) | copy-start | bytes 1540
  17.5 8.9 %all-to-all-start = ((bf16[4,2,8192]{2,1,0:T(2,128)(2,1)}), bf16[4,2,8192]{2,1,0:T(2,128)(2,1)S(1)}, u32[]{:S(2)}, u32[]{:S(2)}) async-start(bf16[4,2,8192]{2,1,0:T(2,128)(2,1)} %reshape.462), calls=%async_computation | async-start | bytes 262144 | tf_op jit(solution)/shard_map/all_to_all | solution.py:127
  70.3 44.2 %all-to-all-start.1 = ((bf16[128,2,16,128]{3,2,1,0:T(8,128)(2,1)}), bf16[128,2,16,128]{3,2,1,0:T(8,128)(2,1)S(1)}, u32[]{:S(2)}, u32[]{:S(2)}) async-start(bf16[128,2,16,128]{3,2,1,0:T(8,128)(2,1)} %convert_element_type.69), calls=%async_computation.1 | async-start | bytes 2097152 | tf_op jit(solution)/shard_map/all_to_all | solution.py:141
  105.5 12.6 %copy-start.2 = (s32[1024]{0:T(1024)S(1)}, s32[1024]{0:T(1024)}, u32[]{:S(2)}) copy-start(s32[1024]{0:T(1024)} %param.4) | copy-start | bytes 12292
  114.5 18.0 %all-to-all-start.2 = ((bf16[128,2,16,128]{3,2,1,0:T(8,128)(2,1)}), bf16[128,2,16,128]{3,2,1,0:T(8,128)(2,1)S(1)}, u32[]{:S(2)}, u32[]{:S(2)}) async-start(bf16[128,2,16,128]{3,2,1,0:T(8,128)(2,1)} %convert_element_type.70), calls=%async_computation.2 | async-start | bytes 2097152 | tf_op jit(solution)/shard_map/all_to_all | solution.py:141
  124.3 8.5 %copy-start.1 = (bf16[1,1024,512]{2,1,0:T(8,128)(2,1)S(1)}, bf16[1,1024,512]{2,1,0:T(8,128)(2,1)}, u32[]{:S(2)}) copy-start(bf16[1,1024,512]{2,1,0:T(8,128)(2,1)} %copy.62) | copy-start | bytes 3145732

commit v7 on v5

--- a/solution.py
+++ b/solution.py
@@ -128,11 +128,17 @@
     windows = freq_white.shape[0]
     shard_bins = freq_white.shape[3]
     rows_white = jnp.transpose(freq_white, (1, 2, 0, 3)).reshape(ch_dev, 2 * windows, shard_bins)
-    all_white = lax.all_gather(rows_white, "gx", axis=0, tiled=True)
-    padded = jnp.concatenate(
-        [all_white, jnp.zeros((band_span,) + all_white.shape[1:], all_white.dtype)], axis=0
-    )
-    base = (lax.axis_index("gx") * ch_dev).astype(jnp.int32).reshape(1)
+    gx_count = lax.axis_size("gx")
+    needed = -(-band_span // ch_dev)
+    blocks = [rows_white]
+    for shift in range(1, min(needed, gx_count - 1) + 1):
+        pairs = [(src, src - shift) for src in range(shift, gx_count)]
+        blocks.append(lax.ppermute(rows_white, "gx", perm=pairs))
+    missing = needed + 1 - len(blocks)
+    if missing > 0:
+        blocks.append(jnp.zeros((missing * ch_dev,) + rows_white.shape[1:], rows_white.dtype))
+    padded = jnp.concatenate(blocks, axis=0)
+    base = jnp.zeros((1,), jnp.int32)
     gy_count = lax.axis_size("gy")
     halves = pair_offsets.astype(jnp.int32).reshape(gy_count, 2, band_span // (2 * gy_count))
     parts = []

time: 134 us -> 110 us (0.82)
  waiting for transfers between devices: 52 us -> 38.3 us
  starting transfers between devices: 7.03 us -> 20.3 us
  between operations: 13.6 us -> 0.37 us
  blocking collectives: 8.64 us -> 0 us
  matrix products: 6.06 us -> 4.52 us
    all_gather x1 -> x0, waiting for transfers between devices: 40.4 us -> none  [local(): all_white = lax.all_gather(rows_white, 'gx', axis=0, tiled=True)]
    ppermute x0 -> x7, waiting for transfers between devices: none -> 22.2 us  [local(): blocks.append(lax.ppermute(rows_white, 'gx', perm=pairs))]
    ppermute x0 -> x7, starting transfers between devices: none -> 9.02 us  [local(): blocks.append(lax.ppermute(rows_white, 'gx', perm=pairs))]
    all_to_all x1 -> x0, blocking collectives: 8.64 us -> none  [local(): lax.all_to_all(white, 'gy', split_axis=3, concat_axis=0, tiled=True)]
    all_to_all x0 -> x1, waiting for transfers between devices: none -> 4.47 us  [local(): lax.all_to_all(white, 'gy', split_axis=3, concat_axis=0, tiled=True)]
    all_to_all x0 -> x1, starting transfers between devices: none -> 4.21 us  [local(): lax.all_to_all(white, 'gy', split_axis=3, concat_axis=0, tiled=True)]
    unnamed x8 -> x20, local copies, waits for them, and re-layouts: 1.78 us -> 3.68 us
    dot_general x1, matrix products: 3.6 us -> 2.07 us  [local(): jnp.einsum('opck,pkl->ocl', cross, inverse, preferred_element_type=jnp.fl...]
  transfers between devices with their start and end apart: 3 -> 10, of which waited for: 3 -> 8; matrix products, arithmetic and copies ran while one was open for 7% -> 8% of each run, Pallas kernels for 6% -> 8%
where the time goes in v7:
time: 110 us; the launch traced here: 109 us
  waiting for transfers between devices  38.3 us (35%)
  starting transfers between devices  20.3 us (18%)
  Pallas kernels  17.3 us (16%)
  local copies, waits for them, and re-layouts  15.4 us (14%)
  other arithmetic  12.9 us (12%)
  matrix products  4.52 us (4%)
    ppermute x7, waiting for transfers between devices, local(): blocks.append(lax.ppermute(rows_white, 'gx', perm=pairs))  22.2 us
    pallas_call x2, Pallas kernels, cross_spectra(): pl.pallas_call(kernel, grid_spec=pltpu.PrefetchScalarGridSpec(num_scalar_...  17.3 us
    all_to_all x2, waiting for transfers between devices, local(): lax.all_to_all(part, 'gy', split_axis=0, concat_axis=3, tiled=True)  11.6 us
    ppermute x7, starting transfers between devices, local(): blocks.append(lax.ppermute(rows_white, 'gx', perm=pairs))  9.02 us
    all_to_all x2, starting transfers between devices, local(): lax.all_to_all(part, 'gy', split_axis=0, concat_axis=3, tiled=True)  7.03 us
    another operation x2, other arithmetic  5.37 us
    all_to_all x1, waiting for transfers between devices, local(): lax.all_to_all(white, 'gy', split_axis=3, concat_axis=0, tiled=True)  4.47 us
    all_to_all x1, starting transfers between devices, local(): lax.all_to_all(white, 'gy', split_axis=3, concat_axis=0, tiled=True)  4.21 us
  transfers between devices with their start and end apart: 10, of which 8 were waited for; matrix products, arithmetic and copies ran while one was open for 8% of the time, Pallas kernels for 8%

profile of v7, /device:TPU:0, one launch (start us, length us, event | category | flops | bytes accessed | tf_op | source)
XLA Modules:
  0.0 109.1 jit_solution(5435730996613546815)
XLA Ops:
  0.0 1.2 %fusion.45 = (f32[32,1024]{1,0:T(8,128)S(1)}, f32[32,1024]{1,0:T(8,128)S(1)}) fusion(s32[1024]{0:T(1024)} %param.4), kind=kLoop, calls=%fused_computation.69 | loop fusion | flops 458752 | bytes 266240 | tf_op jit(solution)/shard_map/cos | solution.py:90
  1.2 0.7 add_select_fusion.5
  1.9 1.8 %fusion.34 = (f32[64,1024]{1,0:T(8,128)S(1)}, f32[64,1024]{1,0:T(8,128)S(1)}) fusion(s32[1024]{0:T(1024)} %param.4, s32[64]{0:T(128)S(1)} %iota_multiply_fusion), kind=kLoop, calls=%fused_computation.52 | loop fusion | flops 917504 | bytes 528640 | tf_op jit(solution)/shard_map/cos | solution.py:90
  3.7 1.3 %copy.37 = bf16[2,16,8192]{2,1,0:T(8,128)(2,1)S(1)} copy(bf16[2,16,8192]{2,0,1:T(2,128)(2,1)} %bitcast.75) | data formatting | bytes 1048576 | tf_op jit(solution)/shard_map/transpose | solution.py:124
  5.0 0.4 reshape_reshape.3
  5.4 0.3 copy.38
  5.7 3.7 %subtract_convert_fusion = (bf16[64,32,1024]{2,1,0:T(8,128)(2,1)S(1)}, bf16[64,32,1024]{2,1,0:T(8,128)(2,1)S(1)}) fusion(f32[64,1024]{1,0:T(8,128)S(1)} %get-tuple-element.18, f32[32,1024]{1,0:T(8,128)S(1)} %get-tuple-element.24, f32[64,1024]{1,0:T(8,128)S(1)} %get-tuple-element.17, f32[32,1024]{1,0:T(8,128)S(1)} %get-tuple-element.23), kind=kLoop, calls=%fused_computation.5 | loop fusion | flops 18874368 | bytes 9175040 | tf_op jit(solution)/shard_map/convert.7
  9.4 2.5 %fusion.4 = f32[128,2048]{0,1:T(8,128)S(1)} fusion(bf16[128,2048]{1,0:T(8,128)(2,1)S(1)} %bitcast.76, bf16[2048,1024]{1,0:T(8,128)(2,1)S(1)} %bitcast.64, bf16[2048,1024]{1,0:T(8,128)(2,1)S(1)} %bitcast.63), kind=kOutput, calls=%fused_computation.6 | convolution fusion | flops 1090519040 | bytes 9961472 | tf_op jit(solution)/shard_map/dot_general | solution.py:103
  11.9 0.3 copy.39
  12.2 0.9 reshape.439
  13.1 0.8 fusion.54
  14.1 0.2 fusion.19
  14.5 0.2 concatenate.18
  14.8 0.2 multiply_convert_fusion.1
  14.9 0.8 copy.41
  15.8 1.7 %reshape.455 = bf16[4,2,8192]{2,1,0:T(2,128)(2,1)} reshape(bf16[1024,2,2,16]{3,2,1,0:T(2,128)(2,1)S(1)} %bitcast.61) | data formatting | bytes 262144
  17.5 4.2 %all-to-all-start = ((bf16[4,2,8192]{2,1,0:T(2,128)(2,1)}), bf16[4,2,8192]{2,1,0:T(2,128)(2,1)S(1)}, u32[]{:S(2)}, u32[]{:S(2)}) async-start(bf16[4,2,8192]{2,1,0:T(2,128)(2,1)} %reshape.455), calls=%async_computation | async-start | bytes 262144 | tf_op jit(solution)/shard_map/all_to_all | solution.py:127
  21.9 4.5 %all-to-all-done = bf16[4,2,8192]{2,1,0:T(2,128)(2,1)S(1)} async-done(((bf16[4,2,8192]{2,1,0:T(2,128)(2,1)}), bf16[4,2,8192]{2,1,0:T(2,128)(2,1)S(1)}, u32[]{:S(2)}, u32[]{:S(2)}) %all-to-all-start) | async-done | bytes 131104 | tf_op jit(solution)/shard_map/all_to_all | solution.py:127
  26.4 0.7 reshape.456
  27.1 1.4 %copy.50 = bf16[2,16,2,4,256]{4,3,1,2,0:T(4,128)(2,1)S(1)} copy(bf16[2,16,2,4,256]{1,2,0,4,3:T(2,128)(2,1)S(1)} %bitcast.62) | data formatting | bytes 262144 | tf_op jit(solution)/shard_map/all_to_all | solution.py:127
  28.6 1.3 %collective-permute-start = (bf16[16,16,256]{2,1,0:T(8,128)(2,1)S(1)}, bf16[16,16,256]{2,1,0:T(8,128)(2,1)S(1)}, u32[]{:S(2)}, u32[]{:S(2)}) collective-permute-start(bf16[16,16,256]{2,1,0:T(8,128)(2,1)S(1)} %bitcast.77), channel_id=1, source_target_pairs={{4,0},{8,4},{12,8},{16,12},{20,16},{24,20},{28,24},{5,1},{9,5},{13... | collective-permute-start | bytes 393224 | tf_op jit(solution)/shard_map/ppermute | solution.py:136
  29.9 1.3 %collective-permute-start.1 = (bf16[16,16,256]{2,1,0:T(8,128)(2,1)S(1)}, bf16[16,16,256]{2,1,0:T(8,128)(2,1)S(1)}, u32[]{:S(2)}, u32[]{:S(2)}) collective-permute-start(bf16[16,16,256]{2,1,0:T(8,128)(2,1)S(1)} %bitcast.78), channel_id=1, source_target_pairs={{8,0},{12,4},{16,8},{20,12},{24,16},{28,20},{9,1},{13,5},{17,9},{2... | collective-permute-start | bytes 393224 | tf_op jit(solution)/shard_map/ppermute | solution.py:136
  31.3 1.3 %collective-permute-start.2 = (bf16[16,16,256]{2,1,0:T(8,128)(2,1)S(1)}, bf16[16,16,256]{2,1,0:T(8,128)(2,1)S(1)}, u32[]{:S(2)}, u32[]{:S(2)}) collective-permute-start(bf16[16,16,256]{2,1,0:T(8,128)(2,1)S(1)} %bitcast.79), channel_id=1, source_target_pairs={{12,0},{16,4},{20,8},{24,12},{28,16},{13,1},{17,5},{21,9},{25,13},... | collective-permute-start | bytes 393224 | tf_op jit(solution)/shard_map/ppermute | solution.py:136
  32.6 1.3 %collective-permute-start.3 = (bf16[16,16,256]{2,1,0:T(8,128)(2,1)S(1)}, bf16[16,16,256]{2,1,0:T(8,128)(2,1)S(1)}, u32[]{:S(2)}, u32[]{:S(2)}) collective-permute-start(bf16[16,16,256]{2,1,0:T(8,128)(2,1)S(1)} %bitcast.80), channel_id=1, source_target_pairs={{16,0},{20,4},{24,8},{28,12},{17,1},{21,5},{25,9},{29,13},{18,2},{... | collective-permute-start | bytes 393224 | tf_op jit(solution)/shard_map/ppermute | solution.py:136
  33.9 1.3 %collective-permute-start.4 = (bf16[16,16,256]{2,1,0:T(8,128)(2,1)S(1)}, bf16[16,16,256]{2,1,0:T(8,128)(2,1)S(1)}, u32[]{:S(2)}, u32[]{:S(2)}) collective-permute-start(bf16[16,16,256]{2,1,0:T(8,128)(2,1)S(1)} %bitcast.81), channel_id=1, source_target_pairs={{20,0},{24,4},{28,8},{21,1},{25,5},{29,9},{22,2},{26,6},{30,10},{2... | collective-permute-start | bytes 393224 | tf_op jit(solution)/shard_map/ppermute | solution.py:136
  35.2 0.5 collective-permute-done
  35.6 1.3 %collective-permute-start.5 = (bf16[16,16,256]{2,1,0:T(8,128)(2,1)S(1)}, bf16[16,16,256]{2,1,0:T(8,128)(2,1)S(1)}, u32[]{:S(2)}, u32[]{:S(2)}) collective-permute-start(bf16[16,16,256]{2,1,0:T(8,128)(2,1)S(1)} %bitcast.82), channel_id=1, source_target_pairs={{24,0},{28,4},{25,1},{29,5},{26,2},{30,6},{27,3},{31,7}} | collective-permute-start | bytes 393224 | tf_op jit(solution)/shard_map/ppermute | solution.py:136
  36.9 2.8 %collective-permute-done.1 = bf16[16,16,256]{2,1,0:T(8,128)(2,1)S(1)} collective-permute-done((bf16[16,16,256]{2,1,0:T(8,128)(2,1)S(1)}, bf16[16,16,256]{2,1,0:T(8,128)(2,1)S(1)}, u32[]{:S(2)}, u32[]{:S(2)}) %collective-permute-start.1) | collective-permute-done | bytes 131104 | tf_op jit(solution)/shard_map/ppermute | solution.py:136
  39.7 1.3 %collective-permute-start.6 = (bf16[16,16,256]{2,1,0:T(8,128)(2,1)S(1)}, bf16[16,16,256]{2,1,0:T(8,128)(2,1)S(1)}, u32[]{:S(2)}, u32[]{:S(2)}) collective-permute-start(bf16[16,16,256]{2,1,0:T(8,128)(2,1)S(1)} %bitcast.83), channel_id=1, source_target_pairs={{28,0},{29,1},{30,2},{31,3}} | collective-permute-start | bytes 393224 | tf_op jit(solution)/shard_map/ppermute | solution.py:136
  41.0 0.7 collective-permute-done.2
  41.7 15.9 %collective-permute-done.3 = bf16[16,16,256]{2,1,0:T(8,128)(2,1)S(1)} collective-permute-done((bf16[16,16,256]{2,1,0:T(8,128)(2,1)S(1)}, bf16[16,16,256]{2,1,0:T(8,128)(2,1)S(1)}, u32[]{:S(2)}, u32[]{:S(2)}) %collective-permute-start.3) | collective-permute-done | bytes 131104 | tf_op jit(solution)/shard_map/ppermute | solution.py:136
  57.6 2.4 %collective-permute-done.4 = bf16[16,16,256]{2,1,0:T(8,128)(2,1)S(1)} collective-permute-done((bf16[16,16,256]{2,1,0:T(8,128)(2,1)S(1)}, bf16[16,16,256]{2,1,0:T(8,128)(2,1)S(1)}, u32[]{:S(2)}, u32[]{:S(2)}) %collective-permute-start.4) | collective-permute-done | bytes 131104 | tf_op jit(solution)/shard_map/ppermute | solution.py:136
  60.1 8.7 %shard_map.37 = f32[64,2,16,256]{3,2,1,0:T(8,128)S(1)} custom-call(s32[64]{0:T(128)S(1)} %reshape_squeeze.6.offsets_ref, s32[1]{0:T(128)} %constant.72.clone.1.base_ref, bf16[144,16,256]{2,1,0:T(8,128)(2,1)S(1)} %broadcast_dynamic-update-slice_fusion.white_ref), custom_call_target="tpu_custom_call" | custom-call | flops 33554432 | bytes 3276800 | tf_op jit(solution)/shard_map/pallas_call | solution.py:60
  68.8 1.2 %convert_element_type.69 = bf16[64,2,16,256]{3,2,1,0:T(8,128)(2,1)} convert(f32[64,2,16,256]{3,2,1,0:T(8,128)S(1)} %shard_map.37) | non-fusion elementwise | flops 524288 | bytes 3145728 | tf_op jit(solution)/shard_map/convert_element_type | solution.py:146
  69.9 3.5 %all-to-all-start.1 = ((bf16[64,2,16,256]{3,2,1,0:T(8,128)(2,1)}), bf16[64,2,16,256]{3,2,1,0:T(8,128)(2,1)S(1)}, u32[]{:S(2)}, u32[]{:S(2)}) async-start(bf16[64,2,16,256]{3,2,1,0:T(8,128)(2,1)} %convert_element_type.69), calls=%async_computation.1 | async-start | bytes 2097152 | tf_op jit(solution)/shard_map/all_to_all | solution.py:147
  73.5 8.7 %shard_map.38 = f32[64,2,16,256]{3,2,1,0:T(8,128)S(1)} custom-call(s32[64]{0:T(128)S(1)} %reshape_squeeze.7.offsets_ref, s32[1]{0:T(128)} %constant.72.clone.1.base_ref, bf16[144,16,256]{2,1,0:T(8,128)(2,1)S(1)} %broadcast_dynamic-update-slice_fusion.white_ref), custom_call_target="tpu_custom_call" | custom-call | flops 33554432 | bytes 3276800 | tf_op jit(solution)/shard_map/pallas_call | solution.py:60
  82.2 1.2 %convert_element_type.70 = bf16[64,2,16,256]{3,2,1,0:T(8,128)(2,1)} convert(f32[64,2,16,256]{3,2,1,0:T(8,128)S(1)} %shard_map.38) | non-fusion elementwise | flops 524288 | bytes 3145728 | tf_op jit(solution)/shard_map/convert_element_type | solution.py:146
  83.4 4.5 %all-to-all-done.1 = bf16[64,2,16,256]{3,2,1,0:T(8,128)(2,1)S(1)} async-done(((bf16[64,2,16,256]{3,2,1,0:T(8,128)(2,1)}), bf16[64,2,16,256]{3,2,1,0:T(8,128)(2,1)S(1)}, u32[]{:S(2)}, u32[]{:S(2)}) %all-to-all-start.1) | async-done | bytes 1048608 | tf_op jit(solution)/shard_map/all_to_all | solution.py:147
  87.9 3.5 %all-to-all-start.2 = ((bf16[64,2,16,256]{3,2,1,0:T(8,128)(2,1)}), bf16[64,2,16,256]{3,2,1,0:T(8,128)(2,1)S(1)}, u32[]{:S(2)}, u32[]{:S(2)}) async-start(bf16[64,2,16,256]{3,2,1,0:T(8,128)(2,1)} %convert_element_type.70), calls=%async_computation.2 | async-start | bytes 2097152 | tf_op jit(solution)/shard_map/all_to_all | solution.py:147
  91.4 0.3 fusion.47
  91.8 0.5 fusion.43
  92.3 1.7 %subtract_convert_fusion.1 = (bf16[1024,16,32]{0,2,1:T(8,128)(2,1)}, bf16[1024,16,32]{0,2,1:T(8,128)(2,1)S(1)}) fusion(f32[1024,16]{0,1:T(8,128)S(1)} %get-tuple-element.20, f32[1024,32]{0,1:T(8,128)S(1)} %get-tuple-element.26, f32[1024,16]{0,1:T(8,128)S(1)} %get-tuple-element.19, f32[1024,32]{0,1:T(8,128)S(1)} %get-tuple-element.25), kind=kLoop, calls=%fused_computation.15 | loop fusion | flops 4718592 | bytes 2490368 | tf_op jit(solution)/shard_map/convert.3
  94.0 2.3 %copy.47 = bf16[1,1024,512]{2,1,0:T(8,128)(2,1)} copy(bf16[1,1024,512]{1,2,0:T(8,128)(2,1)} %bitcast.68) | data formatting | bytes 2097152 | tf_op jit(solution)/shard_map/sub | solution.py:27
  96.3 1.3 %copy.48 = bf16[1,1024,512]{2,1,0:T(8,128)(2,1)} copy(bf16[1,1024,512]{1,2,0:T(8,128)(2,1)S(1)} %bitcast.67) | data formatting | bytes 2097152 | tf_op jit(solution)/shard_map/neg | solution.py:29
  97.6 1.1 %copy.53 = bf16[4,16,2,2,8,256]{5,4,0,3,2,1:T(8,128)(2,1)} copy(bf16[4,16,2,2,8,256]{5,4,3,2,1,0:T(8,128)(2,1)S(1)} %bitcast.65) | data formatting | bytes 2097152 | tf_op jit(solution)/shard_map/all_to_all | solution.py:147
  98.7 7.1 %all-to-all-done.2 = bf16[64,2,16,256]{3,2,1,0:T(8,128)(2,1)S(1)} async-done(((bf16[64,2,16,256]{3,2,1,0:T(8,128)(2,1)}), bf16[64,2,16,256]{3,2,1,0:T(8,128)(2,1)S(1)}, u32[]{:S(2)}, u32[]{:S(2)}) %all-to-all-start.2) | async-done | bytes 1048608 | tf_op jit(solution)/shard_map/all_to_all | solution.py:147
  106.0 1.1 copy-done.2
  107.1 2.1 %multiply_convert_fusion = bf16[32,16,512]{2,1,0:T(8,128)(2,1)} fusion(bf16[1,1024,512]{2,1,0:T(8,128)(2,1)S(1)} %copy-done.1, bf16[1,1024,512]{2,1,0:T(8,128)(2,1)S(1)} %copy-done, bf16[16,2,16,1024]{3,2,1,0:T(8,128)(2,1)S(1)} %bitcast.73, bf16[16,2,16,1024]{3,2,1,0:T(8,128)(2,1)S(1)} %bitcast.72), kind=kOutput, calls=%fused_computation.17 | convolution fusion | flops 1076363264 | bytes 4718592 | tf_op jit(solution)/shard_map/opck,pkl->ocl/dot_general | solution.py:152
  (33 shorter events, 1.1 us)
Async XLA Ops:
  14.3 7.4 %copy-start.4 = (s32[128]{0:T(128)S(1)}, s32[128]{0:T(128)}, u32[]{:S(2)}) copy-start(s32[128]{0:T(128)} %param.5) | copy-start | bytes 1540
  17.5 8.9 %all-to-all-start = ((bf16[4,2,8192]{2,1,0:T(2,128)(2,1)}), bf16[4,2,8192]{2,1,0:T(2,128)(2,1)S(1)}, u32[]{:S(2)}, u32[]{:S(2)}) async-start(bf16[4,2,8192]{2,1,0:T(2,128)(2,1)} %reshape.455), calls=%async_computation | async-start | bytes 262144 | tf_op jit(solution)/shard_map/all_to_all | solution.py:127
  28.6 7.1 %collective-permute-start = (bf16[16,16,256]{2,1,0:T(8,128)(2,1)S(1)}, bf16[16,16,256]{2,1,0:T(8,128)(2,1)S(1)}, u32[]{:S(2)}, u32[]{:S(2)}) collective-permute-start(bf16[16,16,256]{2,1,0:T(8,128)(2,1)S(1)} %bitcast.77), channel_id=1, source_target_pairs={{4,0},{8,4},{12,8},{16,12},{20,16},{24,20},{28,24},{5,1},{9,5},{13... | collective-permute-start | bytes 393224 | tf_op jit(solution)/shard_map/ppermute | solution.py:136
  29.9 9.8 %collective-permute-start.1 = (bf16[16,16,256]{2,1,0:T(8,128)(2,1)S(1)}, bf16[16,16,256]{2,1,0:T(8,128)(2,1)S(1)}, u32[]{:S(2)}, u32[]{:S(2)}) collective-permute-start(bf16[16,16,256]{2,1,0:T(8,128)(2,1)S(1)} %bitcast.78), channel_id=1, source_target_pairs={{8,0},{12,4},{16,8},{20,12},{24,16},{28,20},{9,1},{13,5},{17,9},{2... | collective-permute-start | bytes 393224 | tf_op jit(solution)/shard_map/ppermute | solution.py:136
  31.3 10.4 %collective-permute-start.2 = (bf16[16,16,256]{2,1,0:T(8,128)(2,1)S(1)}, bf16[16,16,256]{2,1,0:T(8,128)(2,1)S(1)}, u32[]{:S(2)}, u32[]{:S(2)}) collective-permute-start(bf16[16,16,256]{2,1,0:T(8,128)(2,1)S(1)} %bitcast.79), channel_id=1, source_target_pairs={{12,0},{16,4},{20,8},{24,12},{28,16},{13,1},{17,5},{21,9},{25,13},... | collective-permute-start | bytes 393224 | tf_op jit(solution)/shard_map/ppermute | solution.py:136
  32.6 25.0 %collective-permute-start.3 = (bf16[16,16,256]{2,1,0:T(8,128)(2,1)S(1)}, bf16[16,16,256]{2,1,0:T(8,128)(2,1)S(1)}, u32[]{:S(2)}, u32[]{:S(2)}) collective-permute-start(bf16[16,16,256]{2,1,0:T(8,128)(2,1)S(1)} %bitcast.80), channel_id=1, source_target_pairs={{16,0},{20,4},{24,8},{28,12},{17,1},{21,5},{25,9},{29,13},{18,2},{... | collective-permute-start | bytes 393224 | tf_op jit(solution)/shard_map/ppermute | solution.py:136
  33.9 26.1 %collective-permute-start.4 = (bf16[16,16,256]{2,1,0:T(8,128)(2,1)S(1)}, bf16[16,16,256]{2,1,0:T(8,128)(2,1)S(1)}, u32[]{:S(2)}, u32[]{:S(2)}) collective-permute-start(bf16[16,16,256]{2,1,0:T(8,128)(2,1)S(1)} %bitcast.81), channel_id=1, source_target_pairs={{20,0},{24,4},{28,8},{21,1},{25,5},{29,9},{22,2},{26,6},{30,10},{2... | collective-permute-start | bytes 393224 | tf_op jit(solution)/shard_map/ppermute | solution.py:136
  35.6 24.4 %collective-permute-start.5 = (bf16[16,16,256]{2,1,0:T(8,128)(2,1)S(1)}, bf16[16,16,256]{2,1,0:T(8,128)(2,1)S(1)}, u32[]{:S(2)}, u32[]{:S(2)}) collective-permute-start(bf16[16,16,256]{2,1,0:T(8,128)(2,1)S(1)} %bitcast.82), channel_id=1, source_target_pairs={{24,0},{28,4},{25,1},{29,5},{26,2},{30,6},{27,3},{31,7}} | collective-permute-start | bytes 393224 | tf_op jit(solution)/shard_map/ppermute | solution.py:136
  39.7 20.3 %collective-permute-start.6 = (bf16[16,16,256]{2,1,0:T(8,128)(2,1)S(1)}, bf16[16,16,256]{2,1,0:T(8,128)(2,1)S(1)}, u32[]{:S(2)}, u32[]{:S(2)}) collective-permute-start(bf16[16,16,256]{2,1,0:T(8,128)(2,1)S(1)} %bitcast.83), channel_id=1, source_target_pairs={{28,0},{29,1},{30,2},{31,3}} | collective-permute-start | bytes 393224 | tf_op jit(solution)/shard_map/ppermute | solution.py:136
  69.9 18.0 %all-to-all-start.1 = ((bf16[64,2,16,256]{3,2,1,0:T(8,128)(2,1)}), bf16[64,2,16,256]{3,2,1,0:T(8,128)(2,1)S(1)}, u32[]{:S(2)}, u32[]{:S(2)}) async-start(bf16[64,2,16,256]{3,2,1,0:T(8,128)(2,1)} %convert_element_type.69), calls=%async_computation.1 | async-start | bytes 2097152 | tf_op jit(solution)/shard_map/all_to_all | solution.py:147
  82.2 9.2 %copy-start.3 = (s32[1024]{0:T(1024)S(1)}, s32[1024]{0:T(1024)}, u32[]{:S(2)}) copy-start(s32[1024]{0:T(1024)} %param.4) | copy-start | bytes 12292
  87.9 18.0 %all-to-all-start.2 = ((bf16[64,2,16,256]{3,2,1,0:T(8,128)(2,1)}), bf16[64,2,16,256]{3,2,1,0:T(8,128)(2,1)S(1)}, u32[]{:S(2)}, u32[]{:S(2)}) async-start(bf16[64,2,16,256]{3,2,1,0:T(8,128)(2,1)} %convert_element_type.70), calls=%async_computation.2 | async-start | bytes 2097152 | tf_op jit(solution)/shard_map/all_to_all | solution.py:147
  97.6 8.4 %copy-start = (bf16[1,1024,512]{2,1,0:T(8,128)(2,1)S(1)}, bf16[1,1024,512]{2,1,0:T(8,128)(2,1)}, u32[]{:S(2)}) copy-start(bf16[1,1024,512]{2,1,0:T(8,128)(2,1)} %copy.47) | copy-start | bytes 3145732
  98.7 7.2 %copy-start.1 = (bf16[1,1024,512]{2,1,0:T(8,128)(2,1)S(1)}, bf16[1,1024,512]{2,1,0:T(8,128)(2,1)}, u32[]{:S(2)}) copy-start(bf16[1,1024,512]{2,1,0:T(8,128)(2,1)} %copy.48) | copy-start | bytes 3145732
  105.8 1.2 %copy-start.2 = (bf16[4,16,2,2,8,256]{5,4,0,3,2,1:T(8,128)(2,1)S(1)}, bf16[4,16,2,2,8,256]{5,4,0,3,2,1:T(8,128)(2,1)}, u32[]{:S(2)}) copy-start(bf16[4,16,2,2,8,256]{5,4,0,3,2,1:T(8,128)(2,1)} %copy.53) | copy-start | bytes 3145732

commit v8 on v7

--- a/solution.py
+++ b/solution.py
@@ -34,45 +34,53 @@
     return (spectra * lax.rsqrt(mean_power + 1e-06)).astype(jnp.bfloat16)
 
 
-def cross_kernel(offsets_ref, base_ref, white_ref, out_ref, *, group, own_count, half):
+def cross_kernel(offsets_ref, white_ref, out_ref, *, group, own_count, windows):
     step = pl.program_id(0)
-    base = base_ref[0]
-    own = [white_ref[base + c].astype(jnp.float32) for c in range(own_count)]
+    bins = white_ref.shape[2]
+
+    span = own_count + 16
 
     def one_offset(i, carry):
         shift = offsets_ref[step * group + i]
-        for c in range(own_count):
-            a = own[c]
-            b = white_ref[base + c + shift].astype(jnp.float32)
-            ar, ai, br, bi = a[:half], a[half:], b[:half], b[half:]
-            out_ref[i, 0, pl.ds(c, 1), :] = jnp.sum(ar * br + ai * bi, axis=0, keepdims=True)
-            out_ref[i, 1, pl.ds(c, 1), :] = jnp.sum(ai * br - ar * bi, axis=0, keepdims=True)
+        start = pl.multiple_of((shift // 8) * 8, 8)
+        turn = (span - shift % 8) % span
+        real_sum = jnp.zeros((own_count, bins), jnp.float32)
+        imag_sum = jnp.zeros((own_count, bins), jnp.float32)
+        for w in range(windows):
+            ar = white_ref[w, pl.ds(0, own_count), :]
+            ai = white_ref[windows + w, pl.ds(0, own_count), :]
+            br = pltpu.roll(white_ref[w, pl.ds(start, span), :], turn, 0)[:own_count]
+            bi = pltpu.roll(white_ref[windows + w, pl.ds(start, span), :], turn, 0)[:own_count]
+            real_sum = real_sum + (ar * br + ai * bi)
+            imag_sum = imag_sum + (ai * br - ar * bi)
+        out_ref[i, 0] = real_sum
+        out_ref[i, 1] = imag_sum
         return carry
 
     lax.fori_loop(0, group, one_offset, 0)
 
 
-def cross_spectra(white_all, pair_offsets, base, own_count):
-    rows, bins = white_all.shape[1], white_all.shape[2]
+def cross_spectra(white_rows, pair_offsets, own_count):
+    rows, channels, bins = white_rows.shape
     band_span = pair_offsets.shape[0]
     group = math.gcd(band_span, 8)
-    kernel = functools.partial(cross_kernel, group=group, own_count=own_count, half=rows // 2)
+    kernel = functools.partial(cross_kernel, group=group, own_count=own_count, windows=rows // 2)
     return pl.pallas_call(
         kernel,
         grid_spec=pltpu.PrefetchScalarGridSpec(
-            num_scalar_prefetch=2,
+            num_scalar_prefetch=1,
             grid=(band_span // group,),
-            in_specs=[pl.BlockSpec(white_all.shape, lambda g, offs, b: (0, 0, 0))],
-            out_specs=pl.BlockSpec((group, 2, own_count, bins), lambda g, offs, b: (g, 0, 0, 0)),
+            in_specs=[pl.BlockSpec(white_rows.shape, lambda g, offs: (0, 0, 0))],
+            out_specs=pl.BlockSpec((group, 2, own_count, bins), lambda g, offs: (g, 0, 0, 0)),
         ),
         out_shape=jax.ShapeDtypeStruct((band_span, 2, own_count, bins), jnp.float32),
         compiler_params=pltpu.CompilerParams(vmem_limit_bytes=48 * 1024 * 1024),
         cost_estimate=pl.CostEstimate(
             flops=8 * band_span * own_count * rows * bins,
             transcendentals=0,
-            bytes_accessed=white_all.size * 2 + band_span * 2 * own_count * bins * 4,
+            bytes_accessed=white_rows.size * 4 + band_span * 2 * own_count * bins * 4,
         ),
-    )(pair_offsets, base, white_all)
+    )(pair_offsets, white_rows)
 
 
 def small_table(kept_bins, rows):
@@ -134,16 +142,15 @@
     for shift in range(1, min(needed, gx_count - 1) + 1):
         pairs = [(src, src - shift) for src in range(shift, gx_count)]
         blocks.append(lax.ppermute(rows_white, "gx", perm=pairs))
-    missing = needed + 1 - len(blocks)
+    missing = needed + 2 - len(blocks)
     if missing > 0:
         blocks.append(jnp.zeros((missing * ch_dev,) + rows_white.shape[1:], rows_white.dtype))
-    padded = jnp.concatenate(blocks, axis=0)
-    base = jnp.zeros((1,), jnp.int32)
+    padded = jnp.transpose(jnp.concatenate(blocks, axis=0), (1, 0, 2)).astype(jnp.float32)
     gy_count = lax.axis_size("gy")
     halves = pair_offsets.astype(jnp.int32).reshape(gy_count, 2, band_span // (2 * gy_count))
     parts = []
     for h in range(2):
-        part = cross_spectra(padded, halves[:, h].reshape(-1), base, ch_dev).astype(jnp.bfloat16)
+        part = cross_spectra(padded, halves[:, h].reshape(-1), ch_dev).astype(jnp.bfloat16)
         parts.append(lax.all_to_all(part, "gy", split_axis=0, concat_axis=3, tiled=True))
     cross = jnp.concatenate(parts, axis=0)
     inverse = inverse_table(kept_bins)

time: 110 us -> 112 us (1.018)
  Pallas kernels: 17.3 us -> 18.7 us
    pallas_call x2, Pallas kernels: 17.3 us -> 18.7 us  [cross_spectra(): pl.pallas_call(kernel, grid_spec=pltpu.PrefetchScalarGridSpec(num_scalar_...]
    all_to_all x2, local copies, waits for them, and re-layouts: 1.25 us -> 2.57 us  [local(): lax.all_to_all(part, 'gy', split_axis=0, concat_axis=3, tiled=True)]
    convert_element_type x2 -> x3, other arithmetic: 2.32 us -> 2.58 us  [the longest x2 2.31 us: local(): cross_spectra(padded, halves[:, h].reshape(-1), ch_dev).astype(jnp.bfloat16)]
    unnamed x20 -> x18, local copies, waits for them, and re-layouts: 3.68 us -> 3.61 us
  transfers between devices with their start and end apart: 10 -> 10, of which waited for: 8 -> 8; matrix products, arithmetic and copies ran while one was open for 8% -> 7% of each run, Pallas kernels for 8% -> 8%
where the time goes in v8:
time: 112 us; the launch traced here: 111 us
  waiting for transfers between devices  39.2 us (35%)
  starting transfers between devices  21 us (19%)
  Pallas kernels  18.7 us (17%)
  local copies, waits for them, and re-layouts  14.9 us (13%)
  other arithmetic  12.3 us (11%)
  matrix products  4.52 us (4%)
    ppermute x7, waiting for transfers between devices, local(): blocks.append(lax.ppermute(rows_white, 'gx', perm=pairs))  22.3 us
    pallas_call x2, Pallas kernels, cross_spectra(): pl.pallas_call(kernel, grid_spec=pltpu.PrefetchScalarGridSpec(num_scalar_...  18.7 us
    all_to_all x2, waiting for transfers between devices, local(): lax.all_to_all(part, 'gy', split_axis=0, concat_axis=3, tiled=True)  12.3 us
    ppermute x7, starting transfers between devices, local(): blocks.append(lax.ppermute(rows_white, 'gx', perm=pairs))  9.01 us
    all_to_all x2, starting transfers between devices, local(): lax.all_to_all(part, 'gy', split_axis=0, concat_axis=3, tiled=True)  7.75 us
    all_to_all x1, waiting for transfers between devices, local(): lax.all_to_all(white, 'gy', split_axis=3, concat_axis=0, tiled=True)  4.58 us
    another operation x2, other arithmetic  4.43 us
    all_to_all x1, starting transfers between devices, local(): lax.all_to_all(white, 'gy', split_axis=3, concat_axis=0, tiled=True)  4.21 us
  transfers between devices with their start and end apart: 10, of which 8 were waited for; matrix products, arithmetic and copies ran while one was open for 7% of the time, Pallas kernels for 8%

profile of v8, /device:TPU:0, one launch (start us, length us, event | category | flops | bytes accessed | tf_op | source)
XLA Modules:
  0.0 110.9 jit_solution(9908515272428540777)
XLA Ops:
  0.0 1.2 %fusion.45 = (f32[32,1024]{1,0:T(8,128)S(1)}, f32[32,1024]{1,0:T(8,128)S(1)}) fusion(s32[1024]{0:T(1024)} %param.4), kind=kLoop, calls=%fused_computation.69 | loop fusion | flops 458752 | bytes 266240 | tf_op jit(solution)/shard_map/cos | solution.py:98
  1.2 0.7 add_select_fusion.5
  1.9 1.8 %fusion.34 = (f32[64,1024]{1,0:T(8,128)S(1)}, f32[64,1024]{1,0:T(8,128)S(1)}) fusion(s32[1024]{0:T(1024)} %param.4, s32[64]{0:T(128)S(1)} %iota_multiply_fusion), kind=kLoop, calls=%fused_computation.53 | loop fusion | flops 917504 | bytes 528640 | tf_op jit(solution)/shard_map/cos | solution.py:98
  3.7 1.3 %copy.37 = bf16[2,16,8192]{2,1,0:T(8,128)(2,1)S(1)} copy(bf16[2,16,8192]{2,0,1:T(2,128)(2,1)} %bitcast.71) | data formatting | bytes 1048576 | tf_op jit(solution)/shard_map/transpose | solution.py:132
  5.0 0.4 reshape_reshape.3
  5.4 0.3 copy.38
  5.7 3.7 %subtract_convert_fusion = (bf16[64,32,1024]{2,1,0:T(8,128)(2,1)S(1)}, bf16[64,32,1024]{2,1,0:T(8,128)(2,1)S(1)}) fusion(f32[64,1024]{1,0:T(8,128)S(1)} %get-tuple-element.18, f32[32,1024]{1,0:T(8,128)S(1)} %get-tuple-element.24, f32[64,1024]{1,0:T(8,128)S(1)} %get-tuple-element.17, f32[32,1024]{1,0:T(8,128)S(1)} %get-tuple-element.23), kind=kLoop, calls=%fused_computation.5 | loop fusion | flops 18874368 | bytes 9175040 | tf_op jit(solution)/shard_map/convert.8
  9.4 2.5 %fusion.4 = f32[128,2048]{0,1:T(8,128)S(1)} fusion(bf16[128,2048]{1,0:T(8,128)(2,1)S(1)} %bitcast.72, bf16[2048,1024]{1,0:T(8,128)(2,1)S(1)} %bitcast.63, bf16[2048,1024]{1,0:T(8,128)(2,1)S(1)} %bitcast.62), kind=kOutput, calls=%fused_computation.7 | convolution fusion | flops 1090519040 | bytes 9961472 | tf_op jit(solution)/shard_map/dot_general | solution.py:111
  11.9 0.3 copy.39
  12.2 0.9 reshape.439
  13.1 0.8 fusion.54
  14.1 0.2 fusion.19
  14.5 0.2 concatenate.18
  14.9 0.8 copy.41
  15.8 1.7 %reshape.455 = bf16[4,2,8192]{2,1,0:T(2,128)(2,1)} reshape(bf16[1024,2,2,16]{3,2,1,0:T(2,128)(2,1)S(1)} %bitcast.60) | data formatting | bytes 262144
  17.5 4.2 %all-to-all-start = ((bf16[4,2,8192]{2,1,0:T(2,128)(2,1)}), bf16[4,2,8192]{2,1,0:T(2,128)(2,1)S(1)}, u32[]{:S(2)}, u32[]{:S(2)}) async-start(bf16[4,2,8192]{2,1,0:T(2,128)(2,1)} %reshape.455), calls=%async_computation | async-start | bytes 262144 | tf_op jit(solution)/shard_map/all_to_all | solution.py:135
  21.8 4.6 %all-to-all-done = bf16[4,2,8192]{2,1,0:T(2,128)(2,1)S(1)} async-done(((bf16[4,2,8192]{2,1,0:T(2,128)(2,1)}), bf16[4,2,8192]{2,1,0:T(2,128)(2,1)S(1)}, u32[]{:S(2)}, u32[]{:S(2)}) %all-to-all-start) | async-done | bytes 131104 | tf_op jit(solution)/shard_map/all_to_all | solution.py:135
  26.4 0.7 reshape.456
  27.1 1.4 %copy.50 = bf16[2,16,2,4,256]{4,3,1,2,0:T(4,128)(2,1)S(1)} copy(bf16[2,16,2,4,256]{1,2,0,4,3:T(2,128)(2,1)S(1)} %bitcast.61) | data formatting | bytes 262144 | tf_op jit(solution)/shard_map/all_to_all | solution.py:135
  28.5 1.3 %collective-permute-start = (bf16[16,16,256]{2,0,1:T(8,128)(2,1)S(1)}, bf16[16,16,256]{2,0,1:T(8,128)(2,1)S(1)}, u32[]{:S(2)}, u32[]{:S(2)}) collective-permute-start(bf16[16,16,256]{2,0,1:T(8,128)(2,1)S(1)} %bitcast.73), channel_id=1, source_target_pairs={{4,0},{8,4},{12,8},{16,12},{20,16},{24,20},{28,24},{5,1},{9,5},{13... | collective-permute-start | bytes 393224 | tf_op jit(solution)/shard_map/ppermute | solution.py:144
  29.9 1.3 %collective-permute-start.1 = (bf16[16,16,256]{2,0,1:T(8,128)(2,1)S(1)}, bf16[16,16,256]{2,0,1:T(8,128)(2,1)S(1)}, u32[]{:S(2)}, u32[]{:S(2)}) collective-permute-start(bf16[16,16,256]{2,0,1:T(8,128)(2,1)S(1)} %bitcast.74), channel_id=1, source_target_pairs={{8,0},{12,4},{16,8},{20,12},{24,16},{28,20},{9,1},{13,5},{17,9},{2... | collective-permute-start | bytes 393224 | tf_op jit(solution)/shard_map/ppermute | solution.py:144
  31.2 1.3 %collective-permute-start.2 = (bf16[16,16,256]{2,0,1:T(8,128)(2,1)S(1)}, bf16[16,16,256]{2,0,1:T(8,128)(2,1)S(1)}, u32[]{:S(2)}, u32[]{:S(2)}) collective-permute-start(bf16[16,16,256]{2,0,1:T(8,128)(2,1)S(1)} %bitcast.76), channel_id=1, source_target_pairs={{12,0},{16,4},{20,8},{24,12},{28,16},{13,1},{17,5},{21,9},{25,13},... | collective-permute-start | bytes 393224 | tf_op jit(solution)/shard_map/ppermute | solution.py:144
  32.5 1.3 %collective-permute-start.3 = (bf16[16,16,256]{2,0,1:T(8,128)(2,1)S(1)}, bf16[16,16,256]{2,0,1:T(8,128)(2,1)S(1)}, u32[]{:S(2)}, u32[]{:S(2)}) collective-permute-start(bf16[16,16,256]{2,0,1:T(8,128)(2,1)S(1)} %bitcast.77), channel_id=1, source_target_pairs={{16,0},{20,4},{24,8},{28,12},{17,1},{21,5},{25,9},{29,13},{18,2},{... | collective-permute-start | bytes 393224 | tf_op jit(solution)/shard_map/ppermute | solution.py:144
  33.8 1.3 %collective-permute-start.4 = (bf16[16,16,256]{2,0,1:T(8,128)(2,1)S(1)}, bf16[16,16,256]{2,0,1:T(8,128)(2,1)S(1)}, u32[]{:S(2)}, u32[]{:S(2)}) collective-permute-start(bf16[16,16,256]{2,0,1:T(8,128)(2,1)S(1)} %bitcast.78), channel_id=1, source_target_pairs={{20,0},{24,4},{28,8},{21,1},{25,5},{29,9},{22,2},{26,6},{30,10},{2... | collective-permute-start | bytes 393224 | tf_op jit(solution)/shard_map/ppermute | solution.py:144
  35.1 0.4 collective-permute-done
  35.5 1.3 %collective-permute-start.5 = (bf16[16,16,256]{2,0,1:T(8,128)(2,1)S(1)}, bf16[16,16,256]{2,0,1:T(8,128)(2,1)S(1)}, u32[]{:S(2)}, u32[]{:S(2)}) collective-permute-start(bf16[16,16,256]{2,0,1:T(8,128)(2,1)S(1)} %bitcast.79), channel_id=1, source_target_pairs={{24,0},{28,4},{25,1},{29,5},{26,2},{30,6},{27,3},{31,7}} | collective-permute-start | bytes 393224 | tf_op jit(solution)/shard_map/ppermute | solution.py:144
  36.9 2.9 %collective-permute-done.1 = bf16[16,16,256]{2,0,1:T(8,128)(2,1)S(1)} collective-permute-done((bf16[16,16,256]{2,0,1:T(8,128)(2,1)S(1)}, bf16[16,16,256]{2,0,1:T(8,128)(2,1)S(1)}, u32[]{:S(2)}, u32[]{:S(2)}) %collective-permute-start.1) | collective-permute-done | bytes 131104 | tf_op jit(solution)/shard_map/ppermute | solution.py:144
  39.7 1.3 %collective-permute-start.6 = (bf16[16,16,256]{2,0,1:T(8,128)(2,1)S(1)}, bf16[16,16,256]{2,0,1:T(8,128)(2,1)S(1)}, u32[]{:S(2)}, u32[]{:S(2)}) collective-permute-start(bf16[16,16,256]{2,0,1:T(8,128)(2,1)S(1)} %bitcast.80), channel_id=1, source_target_pairs={{28,0},{29,1},{30,2},{31,3}} | collective-permute-start | bytes 393224 | tf_op jit(solution)/shard_map/ppermute | solution.py:144
  41.0 0.7 collective-permute-done.2
  41.7 15.8 %collective-permute-done.3 = bf16[16,16,256]{2,0,1:T(8,128)(2,1)S(1)} collective-permute-done((bf16[16,16,256]{2,0,1:T(8,128)(2,1)S(1)}, bf16[16,16,256]{2,0,1:T(8,128)(2,1)S(1)}, u32[]{:S(2)}, u32[]{:S(2)}) %collective-permute-start.3) | collective-permute-done | bytes 131104 | tf_op jit(solution)/shard_map/ppermute | solution.py:144
  57.5 2.5 %collective-permute-done.4 = bf16[16,16,256]{2,0,1:T(8,128)(2,1)S(1)} collective-permute-done((bf16[16,16,256]{2,0,1:T(8,128)(2,1)S(1)}, bf16[16,16,256]{2,0,1:T(8,128)(2,1)S(1)}, u32[]{:S(2)}, u32[]{:S(2)}) %collective-permute-start.4) | collective-permute-done | bytes 131104 | tf_op jit(solution)/shard_map/ppermute | solution.py:144
  60.1 0.3 convert_bitcast_fusion.white_ref
  60.4 9.3 %shard_map.37 = f32[64,2,16,256]{3,2,1,0:T(8,128)S(1)} custom-call(s32[64]{0:T(128)S(1)} %reshape_squeeze.6.offsets_ref, f32[16,160,256]{2,1,0:T(8,128)S(1)} %convert_bitcast_fusion.white_ref), custom_call_target="tpu_custom_call" | custom-call | flops 33554432 | bytes 4718592 | tf_op jit(solution)/shard_map/pallas_call | solution.py:68
  69.7 1.1 %convert_element_type.76 = bf16[64,2,16,256]{3,2,1,0:T(8,128)(2,1)} convert(f32[64,2,16,256]{3,2,1,0:T(8,128)S(1)} %shard_map.37) | non-fusion elementwise | flops 524288 | bytes 3145728 | tf_op jit(solution)/shard_map/convert_element_type | solution.py:153
  70.9 4.2 %all-to-all-start.1 = ((bf16[64,2,16,256]{3,2,1,0:T(8,128)(2,1)}), bf16[64,2,16,256]{3,2,1,0:T(8,128)(2,1)}, u32[]{:S(2)}, u32[]{:S(2)}) async-start(bf16[64,2,16,256]{3,2,1,0:T(8,128)(2,1)} %convert_element_type.76), calls=%async_computation.1 | async-start | bytes 2097152 | tf_op jit(solution)/shard_map/all_to_all | solution.py:154
  75.2 9.4 %shard_map.38 = f32[64,2,16,256]{3,2,1,0:T(8,128)S(1)} custom-call(s32[64]{0:T(128)S(1)} %reshape_squeeze.7.offsets_ref, f32[16,160,256]{2,1,0:T(8,128)S(1)} %convert_bitcast_fusion.white_ref), custom_call_target="tpu_custom_call" | custom-call | flops 33554432 | bytes 4718592 | tf_op jit(solution)/shard_map/pallas_call | solution.py:68
  84.6 1.2 %convert_element_type.77 = bf16[64,2,16,256]{3,2,1,0:T(8,128)(2,1)} convert(f32[64,2,16,256]{3,2,1,0:T(8,128)S(1)} %shard_map.38) | non-fusion elementwise | flops 524288 | bytes 3145728 | tf_op jit(solution)/shard_map/convert_element_type | solution.py:153
  85.7 3.9 %all-to-all-done.1 = bf16[64,2,16,256]{3,2,1,0:T(8,128)(2,1)} async-done(((bf16[64,2,16,256]{3,2,1,0:T(8,128)(2,1)}), bf16[64,2,16,256]{3,2,1,0:T(8,128)(2,1)}, u32[]{:S(2)}, u32[]{:S(2)}) %all-to-all-start.1) | async-done | bytes 1048608 | tf_op jit(solution)/shard_map/all_to_all | solution.py:154
  89.6 3.5 %all-to-all-start.2 = ((bf16[64,2,16,256]{3,2,1,0:T(8,128)(2,1)}), bf16[64,2,16,256]{3,2,1,0:T(8,128)(2,1)S(1)}, u32[]{:S(2)}, u32[]{:S(2)}) async-start(bf16[64,2,16,256]{3,2,1,0:T(8,128)(2,1)} %convert_element_type.77), calls=%async_computation.2 | async-start | bytes 2097152 | tf_op jit(solution)/shard_map/all_to_all | solution.py:154
  93.2 0.3 fusion.47
  93.5 0.5 fusion.43
  94.1 0.8 subtract_convert_fusion.1
  94.8 1.3 %copy.47 = bf16[1,1024,512]{2,1,0:T(8,128)(2,1)} copy(bf16[1,1024,512]{1,2,0:T(8,128)(2,1)S(1)} %bitcast.66) | data formatting | bytes 2097152 | tf_op jit(solution)/shard_map/sub | solution.py:27
  96.2 0.5 copy.48
  96.7 2.4 %copy.54 = bf16[4,16,2,2,8,256]{5,4,0,3,2,1:T(8,128)(2,1)} copy(bf16[4,16,2,2,8,256]{5,4,3,2,1,0:T(8,128)(2,1)} %bitcast.27) | data formatting | bytes 2097152 | tf_op jit(solution)/shard_map/all_to_all | solution.py:154
  99.2 8.4 %all-to-all-done.2 = bf16[64,2,16,256]{3,2,1,0:T(8,128)(2,1)S(1)} async-done(((bf16[64,2,16,256]{3,2,1,0:T(8,128)(2,1)}), bf16[64,2,16,256]{3,2,1,0:T(8,128)(2,1)S(1)}, u32[]{:S(2)}, u32[]{:S(2)}) %all-to-all-start.2) | async-done | bytes 1048608 | tf_op jit(solution)/shard_map/all_to_all | solution.py:154
  107.7 1.1 copy-done.1
  108.8 2.1 %multiply_convert_fusion = bf16[32,16,512]{2,1,0:T(8,128)(2,1)} fusion(bf16[1,1024,512]{2,1,0:T(8,128)(2,1)S(1)} %copy.48, bf16[1,1024,512]{2,1,0:T(8,128)(2,1)S(1)} %copy-done, bf16[16,2,16,1024]{3,2,1,0:T(8,128)(2,1)S(1)} %bitcast.69, bf16[16,2,16,1024]{3,2,1,0:T(8,128)(2,1)S(1)} %bitcast.68), kind=kOutput, calls=%fused_computation.18 | convolution fusion | flops 1076363264 | bytes 4718592 | tf_op jit(solution)/shard_map/opck,pkl->ocl/dot_general | solution.py:159
  (31 shorter events, 1.1 us)
Async XLA Ops:
  14.3 7.4 %copy-start.3 = (s32[128]{0:T(128)S(1)}, s32[128]{0:T(128)}, u32[]{:S(2)}) copy-start(s32[128]{0:T(128)} %param.5) | copy-start | bytes 1540
  17.5 8.9 %all-to-all-start = ((bf16[4,2,8192]{2,1,0:T(2,128)(2,1)}), bf16[4,2,8192]{2,1,0:T(2,128)(2,1)S(1)}, u32[]{:S(2)}, u32[]{:S(2)}) async-start(bf16[4,2,8192]{2,1,0:T(2,128)(2,1)} %reshape.455), calls=%async_computation | async-start | bytes 262144 | tf_op jit(solution)/shard_map/all_to_all | solution.py:135
  28.5 7.1 %collective-permute-start = (bf16[16,16,256]{2,0,1:T(8,128)(2,1)S(1)}, bf16[16,16,256]{2,0,1:T(8,128)(2,1)S(1)}, u32[]{:S(2)}, u32[]{:S(2)}) collective-permute-start(bf16[16,16,256]{2,0,1:T(8,128)(2,1)S(1)} %bitcast.73), channel_id=1, source_target_pairs={{4,0},{8,4},{12,8},{16,12},{20,16},{24,20},{28,24},{5,1},{9,5},{13... | collective-permute-start | bytes 393224 | tf_op jit(solution)/shard_map/ppermute | solution.py:144
  29.9 9.8 %collective-permute-start.1 = (bf16[16,16,256]{2,0,1:T(8,128)(2,1)S(1)}, bf16[16,16,256]{2,0,1:T(8,128)(2,1)S(1)}, u32[]{:S(2)}, u32[]{:S(2)}) collective-permute-start(bf16[16,16,256]{2,0,1:T(8,128)(2,1)S(1)} %bitcast.74), channel_id=1, source_target_pairs={{8,0},{12,4},{16,8},{20,12},{24,16},{28,20},{9,1},{13,5},{17,9},{2... | collective-permute-start | bytes 393224 | tf_op jit(solution)/shard_map/ppermute | solution.py:144
  31.2 10.5 %collective-permute-start.2 = (bf16[16,16,256]{2,0,1:T(8,128)(2,1)S(1)}, bf16[16,16,256]{2,0,1:T(8,128)(2,1)S(1)}, u32[]{:S(2)}, u32[]{:S(2)}) collective-permute-start(bf16[16,16,256]{2,0,1:T(8,128)(2,1)S(1)} %bitcast.76), channel_id=1, source_target_pairs={{12,0},{16,4},{20,8},{24,12},{28,16},{13,1},{17,5},{21,9},{25,13},... | collective-permute-start | bytes 393224 | tf_op jit(solution)/shard_map/ppermute | solution.py:144
  32.5 25.0 %collective-permute-start.3 = (bf16[16,16,256]{2,0,1:T(8,128)(2,1)S(1)}, bf16[16,16,256]{2,0,1:T(8,128)(2,1)S(1)}, u32[]{:S(2)}, u32[]{:S(2)}) collective-permute-start(bf16[16,16,256]{2,0,1:T(8,128)(2,1)S(1)} %bitcast.77), channel_id=1, source_target_pairs={{16,0},{20,4},{24,8},{28,12},{17,1},{21,5},{25,9},{29,13},{18,2},{... | collective-permute-start | bytes 393224 | tf_op jit(solution)/shard_map/ppermute | solution.py:144
  33.8 26.2 %collective-permute-start.4 = (bf16[16,16,256]{2,0,1:T(8,128)(2,1)S(1)}, bf16[16,16,256]{2,0,1:T(8,128)(2,1)S(1)}, u32[]{:S(2)}, u32[]{:S(2)}) collective-permute-start(bf16[16,16,256]{2,0,1:T(8,128)(2,1)S(1)} %bitcast.78), channel_id=1, source_target_pairs={{20,0},{24,4},{28,8},{21,1},{25,5},{29,9},{22,2},{26,6},{30,10},{2... | collective-permute-start | bytes 393224 | tf_op jit(solution)/shard_map/ppermute | solution.py:144
  35.5 24.5 %collective-permute-start.5 = (bf16[16,16,256]{2,0,1:T(8,128)(2,1)S(1)}, bf16[16,16,256]{2,0,1:T(8,128)(2,1)S(1)}, u32[]{:S(2)}, u32[]{:S(2)}) collective-permute-start(bf16[16,16,256]{2,0,1:T(8,128)(2,1)S(1)} %bitcast.79), channel_id=1, source_target_pairs={{24,0},{28,4},{25,1},{29,5},{26,2},{30,6},{27,3},{31,7}} | collective-permute-start | bytes 393224 | tf_op jit(solution)/shard_map/ppermute | solution.py:144
  39.7 20.3 %collective-permute-start.6 = (bf16[16,16,256]{2,0,1:T(8,128)(2,1)S(1)}, bf16[16,16,256]{2,0,1:T(8,128)(2,1)S(1)}, u32[]{:S(2)}, u32[]{:S(2)}) collective-permute-start(bf16[16,16,256]{2,0,1:T(8,128)(2,1)S(1)} %bitcast.80), channel_id=1, source_target_pairs={{28,0},{29,1},{30,2},{31,3}} | collective-permute-start | bytes 393224 | tf_op jit(solution)/shard_map/ppermute | solution.py:144
  70.9 18.8 %all-to-all-start.1 = ((bf16[64,2,16,256]{3,2,1,0:T(8,128)(2,1)}), bf16[64,2,16,256]{3,2,1,0:T(8,128)(2,1)}, u32[]{:S(2)}, u32[]{:S(2)}) async-start(bf16[64,2,16,256]{3,2,1,0:T(8,128)(2,1)} %convert_element_type.76), calls=%async_computation.1 | async-start | bytes 2097152 | tf_op jit(solution)/shard_map/all_to_all | solution.py:154
  84.6 8.6 %copy-start.2 = (s32[1024]{0:T(1024)S(1)}, s32[1024]{0:T(1024)}, u32[]{:S(2)}) copy-start(s32[1024]{0:T(1024)} %param.4) | copy-start | bytes 12292
  89.6 18.0 %all-to-all-start.2 = ((bf16[64,2,16,256]{3,2,1,0:T(8,128)(2,1)}), bf16[64,2,16,256]{3,2,1,0:T(8,128)(2,1)S(1)}, u32[]{:S(2)}, u32[]{:S(2)}) async-start(bf16[64,2,16,256]{3,2,1,0:T(8,128)(2,1)} %convert_element_type.77), calls=%async_computation.2 | async-start | bytes 2097152 | tf_op jit(solution)/shard_map/all_to_all | solution.py:154
  96.7 11.0 %copy-start = (bf16[1,1024,512]{2,1,0:T(8,128)(2,1)S(1)}, bf16[1,1024,512]{2,1,0:T(8,128)(2,1)}, u32[]{:S(2)}) copy-start(bf16[1,1024,512]{2,1,0:T(8,128)(2,1)} %copy.47) | copy-start | bytes 3145732
  107.6 1.2 %copy-start.1 = (bf16[4,16,2,2,8,256]{5,4,0,3,2,1:T(8,128)(2,1)S(1)}, bf16[4,16,2,2,8,256]{5,4,0,3,2,1:T(8,128)(2,1)}, u32[]{:S(2)}) copy-start(bf16[4,16,2,2,8,256]{5,4,0,3,2,1:T(8,128)(2,1)} %copy.54) | copy-start | bytes 3145732

commit v9 on v7

--- a/solution.py
+++ b/solution.py
@@ -140,9 +140,10 @@
     padded = jnp.concatenate(blocks, axis=0)
     base = jnp.zeros((1,), jnp.int32)
     gy_count = lax.axis_size("gy")
-    halves = pair_offsets.astype(jnp.int32).reshape(gy_count, 2, band_span // (2 * gy_count))
+    part_count = 4
+    halves = pair_offsets.astype(jnp.int32).reshape(gy_count, part_count, band_span // (part_count * gy_count))
     parts = []
-    for h in range(2):
+    for h in range(part_count):
         part = cross_spectra(padded, halves[:, h].reshape(-1), base, ch_dev).astype(jnp.bfloat16)
         parts.append(lax.all_to_all(part, "gy", split_axis=0, concat_axis=3, tiled=True))
     cross = jnp.concatenate(parts, axis=0)

time: 110 us -> 121 us (1.10)
  starting transfers between devices: 20.3 us -> 27.8 us
    all_to_all x2 -> x4, starting transfers between devices: 7.03 us -> 14.5 us  [local(): lax.all_to_all(part, 'gy', split_axis=0, concat_axis=3, tiled=True)]
    all_to_all x2 -> x4, local copies, waits for them, and re-layouts: 1.25 us -> 3.68 us  [local(): lax.all_to_all(part, 'gy', split_axis=0, concat_axis=3, tiled=True)]
    convert_element_type x2 -> x4, other arithmetic: 2.32 us -> 3.47 us  [local(): cross_spectra(padded, halves[:, h].reshape(-1), base, ch_dev)]
    pallas_call x2 -> x4, Pallas kernels: 17.3 us -> 18.5 us  [cross_spectra(): pl.pallas_call(kernel, grid_spec=pltpu.PrefetchScalarGridSpec(num_scalar_...]
    unnamed x20 -> x24, local copies, waits for them, and re-layouts: 3.68 us -> 2.61 us
    all_to_all x2 -> x4, waiting for transfers between devices: 11.6 us -> 11.7 us  [local(): lax.all_to_all(part, 'gy', split_axis=0, concat_axis=3, tiled=True)]
  transfers between devices with their start and end apart: 10 -> 12, of which waited for: 8 -> 10; matrix products, arithmetic and copies ran while one was open for 8% -> 8% of each run, Pallas kernels for 8% -> 12%
where the time goes in v9:
time: 121 us; the launch traced here: 120 us
  waiting for transfers between devices  38.3 us (32%)
  starting transfers between devices  27.8 us (23%)
  Pallas kernels  18.5 us (15%)
  local copies, waits for them, and re-layouts  16.1 us (13%)
  other arithmetic  13.2 us (11%)
  matrix products  5.71 us (5%)
    ppermute x7, waiting for transfers between devices, local(): blocks.append(lax.ppermute(rows_white, 'gx', perm=pairs))  22.2 us
    pallas_call x4, Pallas kernels, cross_spectra(): pl.pallas_call(kernel, grid_spec=pltpu.PrefetchScalarGridSpec(num_scalar_...  18.5 us
    all_to_all x4, starting transfers between devices, local(): lax.all_to_all(part, 'gy', split_axis=0, concat_axis=3, tiled=True)  14.5 us
    all_to_all x4, waiting for transfers between devices, local(): lax.all_to_all(part, 'gy', split_axis=0, concat_axis=3, tiled=True)  11.7 us
    ppermute x7, starting transfers between devices, local(): blocks.append(lax.ppermute(rows_white, 'gx', perm=pairs))  9.02 us
    all_to_all x1, waiting for transfers between devices, local(): lax.all_to_all(white, 'gy', split_axis=3, concat_axis=0, tiled=True)  4.45 us
    another operation x2, other arithmetic  4.43 us
    all_to_all x1, starting transfers between devices, local(): lax.all_to_all(white, 'gy', split_axis=3, concat_axis=0, tiled=True)  4.21 us
  transfers between devices with their start and end apart: 12, of which 10 were waited for; matrix products, arithmetic and copies ran while one was open for 8% of the time, Pallas kernels for 12%

profile of v9, /device:TPU:0, one launch (start us, length us, event | category | flops | bytes accessed | tf_op | source)
XLA Modules:
  0.0 119.9 jit_solution(17843521577694686611)
XLA Ops:
  0.0 1.2 %fusion.49 = (f32[32,1024]{1,0:T(8,128)S(1)}, f32[32,1024]{1,0:T(8,128)S(1)}) fusion(s32[1024]{0:T(1024)} %param.4), kind=kLoop, calls=%fused_computation.73 | loop fusion | flops 458752 | bytes 266240 | tf_op jit(solution)/shard_map/cos | solution.py:90
  1.2 0.7 add_select_fusion.5
  1.9 1.8 %fusion.38 = (f32[64,1024]{1,0:T(8,128)S(1)}, f32[64,1024]{1,0:T(8,128)S(1)}) fusion(s32[1024]{0:T(1024)} %param.4, s32[64]{0:T(128)S(1)} %iota_multiply_fusion), kind=kLoop, calls=%fused_computation.56 | loop fusion | flops 917504 | bytes 528640 | tf_op jit(solution)/shard_map/cos | solution.py:90
  3.7 1.3 %copy.45 = bf16[2,16,8192]{2,1,0:T(8,128)(2,1)S(1)} copy(bf16[2,16,8192]{2,0,1:T(2,128)(2,1)} %bitcast.84) | data formatting | bytes 1048576 | tf_op jit(solution)/shard_map/transpose | solution.py:124
  5.7 3.7 %subtract_convert_fusion = (bf16[64,32,1024]{2,1,0:T(8,128)(2,1)S(1)}, bf16[64,32,1024]{2,1,0:T(8,128)(2,1)S(1)}) fusion(f32[64,1024]{1,0:T(8,128)S(1)} %get-tuple-element.20, f32[32,1024]{1,0:T(8,128)S(1)} %get-tuple-element.26, f32[64,1024]{1,0:T(8,128)S(1)} %get-tuple-element.19, f32[32,1024]{1,0:T(8,128)S(1)} %get-tuple-element.25), kind=kLoop, calls=%fused_computation.5 | loop fusion | flops 18874368 | bytes 9175040 | tf_op jit(solution)/shard_map/convert.7
  9.4 2.5 %fusion.4 = f32[128,2048]{0,1:T(8,128)S(1)} fusion(bf16[128,2048]{1,0:T(8,128)(2,1)S(1)} %bitcast.88, bf16[2048,1024]{1,0:T(8,128)(2,1)S(1)} %bitcast.74, bf16[2048,1024]{1,0:T(8,128)(2,1)S(1)} %bitcast.73), kind=kOutput, calls=%fused_computation.6 | convolution fusion | flops 1090519040 | bytes 9961472 | tf_op jit(solution)/shard_map/dot_general | solution.py:103
  12.2 0.9 reshape.439
  13.1 0.8 fusion.58
  14.9 0.8 copy.49
  15.8 1.7 %reshape.465 = bf16[4,2,8192]{2,1,0:T(2,128)(2,1)} reshape(bf16[1024,2,2,16]{3,2,1,0:T(2,128)(2,1)S(1)} %bitcast.71) | data formatting | bytes 262144
  17.5 4.2 %all-to-all-start = ((bf16[4,2,8192]{2,1,0:T(2,128)(2,1)}), bf16[4,2,8192]{2,1,0:T(2,128)(2,1)S(1)}, u32[]{:S(2)}, u32[]{:S(2)}) async-start(bf16[4,2,8192]{2,1,0:T(2,128)(2,1)} %reshape.465), calls=%async_computation | async-start | bytes 262144 | tf_op jit(solution)/shard_map/all_to_all | solution.py:127
  21.9 4.4 %all-to-all-done = bf16[4,2,8192]{2,1,0:T(2,128)(2,1)S(1)} async-done(((bf16[4,2,8192]{2,1,0:T(2,128)(2,1)}), bf16[4,2,8192]{2,1,0:T(2,128)(2,1)S(1)}, u32[]{:S(2)}, u32[]{:S(2)}) %all-to-all-start) | async-done | bytes 131104 | tf_op jit(solution)/shard_map/all_to_all | solution.py:127
  26.4 0.7 reshape.466
  27.1 1.4 %copy.60 = bf16[2,16,2,4,256]{4,3,1,2,0:T(4,128)(2,1)S(1)} copy(bf16[2,16,2,4,256]{1,2,0,4,3:T(2,128)(2,1)S(1)} %bitcast.72) | data formatting | bytes 262144 | tf_op jit(solution)/shard_map/all_to_all | solution.py:127
  28.6 1.3 %collective-permute-start = (bf16[16,16,256]{2,1,0:T(8,128)(2,1)S(1)}, bf16[16,16,256]{2,1,0:T(8,128)(2,1)S(1)}, u32[]{:S(2)}, u32[]{:S(2)}) collective-permute-start(bf16[16,16,256]{2,1,0:T(8,128)(2,1)S(1)} %bitcast.90), channel_id=1, source_target_pairs={{4,0},{8,4},{12,8},{16,12},{20,16},{24,20},{28,24},{5,1},{9,5},{13... | collective-permute-start | bytes 393224 | tf_op jit(solution)/shard_map/ppermute | solution.py:136
  29.9 1.3 %collective-permute-start.1 = (bf16[16,16,256]{2,1,0:T(8,128)(2,1)S(1)}, bf16[16,16,256]{2,1,0:T(8,128)(2,1)S(1)}, u32[]{:S(2)}, u32[]{:S(2)}) collective-permute-start(bf16[16,16,256]{2,1,0:T(8,128)(2,1)S(1)} %bitcast.91), channel_id=1, source_target_pairs={{8,0},{12,4},{16,8},{20,12},{24,16},{28,20},{9,1},{13,5},{17,9},{2... | collective-permute-start | bytes 393224 | tf_op jit(solution)/shard_map/ppermute | solution.py:136
  31.3 1.3 %collective-permute-start.2 = (bf16[16,16,256]{2,1,0:T(8,128)(2,1)S(1)}, bf16[16,16,256]{2,1,0:T(8,128)(2,1)S(1)}, u32[]{:S(2)}, u32[]{:S(2)}) collective-permute-start(bf16[16,16,256]{2,1,0:T(8,128)(2,1)S(1)} %bitcast.92), channel_id=1, source_target_pairs={{12,0},{16,4},{20,8},{24,12},{28,16},{13,1},{17,5},{21,9},{25,13},... | collective-permute-start | bytes 393224 | tf_op jit(solution)/shard_map/ppermute | solution.py:136
  32.6 1.3 %collective-permute-start.3 = (bf16[16,16,256]{2,1,0:T(8,128)(2,1)S(1)}, bf16[16,16,256]{2,1,0:T(8,128)(2,1)S(1)}, u32[]{:S(2)}, u32[]{:S(2)}) collective-permute-start(bf16[16,16,256]{2,1,0:T(8,128)(2,1)S(1)} %bitcast.93), channel_id=1, source_target_pairs={{16,0},{20,4},{24,8},{28,12},{17,1},{21,5},{25,9},{29,13},{18,2},{... | collective-permute-start | bytes 393224 | tf_op jit(solution)/shard_map/ppermute | solution.py:136
  33.9 1.3 %collective-permute-start.4 = (bf16[16,16,256]{2,1,0:T(8,128)(2,1)S(1)}, bf16[16,16,256]{2,1,0:T(8,128)(2,1)S(1)}, u32[]{:S(2)}, u32[]{:S(2)}) collective-permute-start(bf16[16,16,256]{2,1,0:T(8,128)(2,1)S(1)} %bitcast.94), channel_id=1, source_target_pairs={{20,0},{24,4},{28,8},{21,1},{25,5},{29,9},{22,2},{26,6},{30,10},{2... | collective-permute-start | bytes 393224 | tf_op jit(solution)/shard_map/ppermute | solution.py:136
  35.6 1.3 %collective-permute-start.5 = (bf16[16,16,256]{2,1,0:T(8,128)(2,1)S(1)}, bf16[16,16,256]{2,1,0:T(8,128)(2,1)S(1)}, u32[]{:S(2)}, u32[]{:S(2)}) collective-permute-start(bf16[16,16,256]{2,1,0:T(8,128)(2,1)S(1)} %bitcast.95), channel_id=1, source_target_pairs={{24,0},{28,4},{25,1},{29,5},{26,2},{30,6},{27,3},{31,7}} | collective-permute-start | bytes 393224 | tf_op jit(solution)/shard_map/ppermute | solution.py:136
  36.9 2.8 %collective-permute-done.1 = bf16[16,16,256]{2,1,0:T(8,128)(2,1)S(1)} collective-permute-done((bf16[16,16,256]{2,1,0:T(8,128)(2,1)S(1)}, bf16[16,16,256]{2,1,0:T(8,128)(2,1)S(1)}, u32[]{:S(2)}, u32[]{:S(2)}) %collective-permute-start.1) | collective-permute-done | bytes 131104 | tf_op jit(solution)/shard_map/ppermute | solution.py:136
  39.7 1.3 %collective-permute-start.6 = (bf16[16,16,256]{2,1,0:T(8,128)(2,1)S(1)}, bf16[16,16,256]{2,1,0:T(8,128)(2,1)S(1)}, u32[]{:S(2)}, u32[]{:S(2)}) collective-permute-start(bf16[16,16,256]{2,1,0:T(8,128)(2,1)S(1)} %bitcast.96), channel_id=1, source_target_pairs={{28,0},{29,1},{30,2},{31,3}} | collective-permute-start | bytes 393224 | tf_op jit(solution)/shard_map/ppermute | solution.py:136
  41.7 15.9 %collective-permute-done.3 = bf16[16,16,256]{2,1,0:T(8,128)(2,1)S(1)} collective-permute-done((bf16[16,16,256]{2,1,0:T(8,128)(2,1)S(1)}, bf16[16,16,256]{2,1,0:T(8,128)(2,1)S(1)}, u32[]{:S(2)}, u32[]{:S(2)}) %collective-permute-start.3) | collective-permute-done | bytes 131104 | tf_op jit(solution)/shard_map/ppermute | solution.py:136
  57.6 2.4 %collective-permute-done.4 = bf16[16,16,256]{2,1,0:T(8,128)(2,1)S(1)} collective-permute-done((bf16[16,16,256]{2,1,0:T(8,128)(2,1)S(1)}, bf16[16,16,256]{2,1,0:T(8,128)(2,1)S(1)}, u32[]{:S(2)}, u32[]{:S(2)}) %collective-permute-start.4) | collective-permute-done | bytes 131104 | tf_op jit(solution)/shard_map/ppermute | solution.py:136
  60.1 4.6 %shard_map.37 = f32[32,2,16,256]{3,2,1,0:T(8,128)S(1)} custom-call(s32[32]{0:T(128)S(1)} %reshape_squeeze.12.offsets_ref, s32[1]{0:T(128)} %constant.72.clone.1.base_ref, bf16[144,16,256]{2,1,0:T(8,128)(2,1)S(1)} %broadcast_dynamic-update-slice_fusion.white_ref), custom_call_target="tpu_custom_call" | custom-call | flops 16777216 | bytes 2228224 | tf_op jit(solution)/shard_map/pallas_call | solution.py:60
  64.7 0.9 convert_element_type.75
  65.6 3.5 %all-to-all-start.1 = ((bf16[32,2,16,256]{3,2,1,0:T(8,128)(2,1)}), bf16[32,2,16,256]{3,2,1,0:T(8,128)(2,1)S(1)}, u32[]{:S(2)}, u32[]{:S(2)}) async-start(bf16[32,2,16,256]{3,2,1,0:T(8,128)(2,1)} %convert_element_type.75), calls=%async_computation.1 | async-start | bytes 1048576 | tf_op jit(solution)/shard_map/all_to_all | solution.py:148
  69.1 4.6 %shard_map.38 = f32[32,2,16,256]{3,2,1,0:T(8,128)S(1)} custom-call(s32[32]{0:T(128)S(1)} %reshape_squeeze.13.offsets_ref, s32[1]{0:T(128)} %constant.72.clone.1.base_ref, bf16[144,16,256]{2,1,0:T(8,128)(2,1)S(1)} %broadcast_dynamic-update-slice_fusion.white_ref), custom_call_target="tpu_custom_call" | custom-call | flops 16777216 | bytes 2228224 | tf_op jit(solution)/shard_map/pallas_call | solution.py:60
  73.8 0.9 convert_element_type.76
  74.6 3.2 %all-to-all-done.1 = bf16[32,2,16,256]{3,2,1,0:T(8,128)(2,1)S(1)} async-done(((bf16[32,2,16,256]{3,2,1,0:T(8,128)(2,1)}), bf16[32,2,16,256]{3,2,1,0:T(8,128)(2,1)S(1)}, u32[]{:S(2)}, u32[]{:S(2)}) %all-to-all-start.1) | async-done | bytes 524320 | tf_op jit(solution)/shard_map/all_to_all | solution.py:148
  77.9 3.5 %all-to-all-start.2 = ((bf16[32,2,16,256]{3,2,1,0:T(8,128)(2,1)}), bf16[32,2,16,256]{3,2,1,0:T(8,128)(2,1)S(1)}, u32[]{:S(2)}, u32[]{:S(2)}) async-start(bf16[32,2,16,256]{3,2,1,0:T(8,128)(2,1)} %convert_element_type.76), calls=%async_computation.2 | async-start | bytes 1048576 | tf_op jit(solution)/shard_map/all_to_all | solution.py:148
  81.4 4.6 %shard_map.39 = f32[32,2,16,256]{3,2,1,0:T(8,128)S(1)} custom-call(s32[32]{0:T(128)S(1)} %reshape_squeeze.14.offsets_ref, s32[1]{0:T(128)} %constant.72.clone.1.base_ref, bf16[144,16,256]{2,1,0:T(8,128)(2,1)S(1)} %broadcast_dynamic-update-slice_fusion.white_ref), custom_call_target="tpu_custom_call" | custom-call | flops 16777216 | bytes 2228224 | tf_op jit(solution)/shard_map/pallas_call | solution.py:60
  86.1 0.9 convert_element_type.77
  86.9 3.2 %all-to-all-done.2 = bf16[32,2,16,256]{3,2,1,0:T(8,128)(2,1)S(1)} async-done(((bf16[32,2,16,256]{3,2,1,0:T(8,128)(2,1)}), bf16[32,2,16,256]{3,2,1,0:T(8,128)(2,1)S(1)}, u32[]{:S(2)}, u32[]{:S(2)}) %all-to-all-start.2) | async-done | bytes 524320 | tf_op jit(solution)/shard_map/all_to_all | solution.py:148
  90.2 3.5 %all-to-all-start.3 = ((bf16[32,2,16,256]{3,2,1,0:T(8,128)(2,1)}), bf16[32,2,16,256]{3,2,1,0:T(8,128)(2,1)S(1)}, u32[]{:S(2)}, u32[]{:S(2)}) async-start(bf16[32,2,16,256]{3,2,1,0:T(8,128)(2,1)} %convert_element_type.77), calls=%async_computation.3 | async-start | bytes 1048576 | tf_op jit(solution)/shard_map/all_to_all | solution.py:148
  94.3 4.6 %shard_map.40 = f32[32,2,16,256]{3,2,1,0:T(8,128)S(1)} custom-call(s32[32]{0:T(128)S(1)} %reshape_squeeze.15.offsets_ref, s32[1]{0:T(128)} %constant.72.clone.1.base_ref, bf16[144,16,256]{2,1,0:T(8,128)(2,1)S(1)} %broadcast_dynamic-update-slice_fusion.white_ref), custom_call_target="tpu_custom_call" | custom-call | flops 16777216 | bytes 2228224 | tf_op jit(solution)/shard_map/pallas_call | solution.py:60
  98.9 0.9 convert_element_type.78
  99.8 2.7 %all-to-all-done.3 = bf16[32,2,16,256]{3,2,1,0:T(8,128)(2,1)S(1)} async-done(((bf16[32,2,16,256]{3,2,1,0:T(8,128)(2,1)}), bf16[32,2,16,256]{3,2,1,0:T(8,128)(2,1)S(1)}, u32[]{:S(2)}, u32[]{:S(2)}) %all-to-all-start.3) | async-done | bytes 524320 | tf_op jit(solution)/shard_map/all_to_all | solution.py:148
  102.4 4.1 %all-to-all-start.4 = ((bf16[32,2,16,256]{3,2,1,0:T(8,128)(2,1)}), bf16[32,2,16,256]{3,2,1,0:T(8,128)(2,1)}, u32[]{:S(2)}, u32[]{:S(2)}) async-start(bf16[32,2,16,256]{3,2,1,0:T(8,128)(2,1)} %convert_element_type.78), calls=%async_computation.4 | async-start | bytes 1048576 | tf_op jit(solution)/shard_map/all_to_all | solution.py:148
  106.9 0.8 subtract_convert_fusion.1
  107.7 1.3 %copy.57 = bf16[1,1024,512]{2,1,0:T(8,128)(2,1)} copy(bf16[1,1024,512]{1,2,0:T(8,128)(2,1)S(1)} %bitcast.76) | data formatting | bytes 2097152 | tf_op jit(solution)/shard_map/sub | solution.py:27
  109.1 1.3 %copy.58 = bf16[1,1024,512]{2,1,0:T(8,128)(2,1)} copy(bf16[1,1024,512]{1,2,0:T(8,128)(2,1)S(1)} %bitcast.75) | data formatting | bytes 2097152 | tf_op jit(solution)/shard_map/neg | solution.py:29
  110.4 0.9 copy.63
  111.3 0.9 copy.64
  112.1 0.9 copy.65
  113.0 2.5 %all-to-all-done.4 = bf16[32,2,16,256]{3,2,1,0:T(8,128)(2,1)} async-done(((bf16[32,2,16,256]{3,2,1,0:T(8,128)(2,1)}), bf16[32,2,16,256]{3,2,1,0:T(8,128)(2,1)}, u32[]{:S(2)}, u32[]{:S(2)}) %all-to-all-start.4) | async-done | bytes 524320 | tf_op jit(solution)/shard_map/all_to_all | solution.py:148
  115.5 1.1 copy.66
  116.6 3.3 %multiply_convert_fusion = bf16[32,16,512]{2,1,0:T(8,128)(2,1)} fusion(bf16[1,1024,512]{2,1,0:T(8,128)(2,1)S(1)} %copy-done.3, bf16[1,1024,512]{2,1,0:T(8,128)(2,1)S(1)} %copy-done.2, bf16[8,2,16,1024]{3,2,1,0:T(8,128)(2,1)S(1)} %bitcast.89, bf16[8,2,16,1024]{3,2,1,0:T(8,128)(2,1)} %bitcast.87, bf16[8,2,16,1024]{3,2,1,0:T(8,128)(2,1)} %bitcast.86, ...), kind=kOutput, calls=%fused_computation.21 | convolution fusion | flops 1078460416 | bytes 4718592 | tf_op jit(solution)/shard_map/opck,pkl->ocl/dot_general | solution.py:153
  (49 shorter events, 4.8 us)
Async XLA Ops:
  14.3 7.4 %copy-start.6 = (s32[128]{0:T(128)S(1)}, s32[128]{0:T(128)}, u32[]{:S(2)}) copy-start(s32[128]{0:T(128)} %param.5) | copy-start | bytes 1540
  17.5 8.9 %all-to-all-start = ((bf16[4,2,8192]{2,1,0:T(2,128)(2,1)}), bf16[4,2,8192]{2,1,0:T(2,128)(2,1)S(1)}, u32[]{:S(2)}, u32[]{:S(2)}) async-start(bf16[4,2,8192]{2,1,0:T(2,128)(2,1)} %reshape.465), calls=%async_computation | async-start | bytes 262144 | tf_op jit(solution)/shard_map/all_to_all | solution.py:127
  28.6 7.1 %collective-permute-start = (bf16[16,16,256]{2,1,0:T(8,128)(2,1)S(1)}, bf16[16,16,256]{2,1,0:T(8,128)(2,1)S(1)}, u32[]{:S(2)}, u32[]{:S(2)}) collective-permute-start(bf16[16,16,256]{2,1,0:T(8,128)(2,1)S(1)} %bitcast.90), channel_id=1, source_target_pairs={{4,0},{8,4},{12,8},{16,12},{20,16},{24,20},{28,24},{5,1},{9,5},{13... | collective-permute-start | bytes 393224 | tf_op jit(solution)/shard_map/ppermute | solution.py:136
  29.9 9.8 %collective-permute-start.1 = (bf16[16,16,256]{2,1,0:T(8,128)(2,1)S(1)}, bf16[16,16,256]{2,1,0:T(8,128)(2,1)S(1)}, u32[]{:S(2)}, u32[]{:S(2)}) collective-permute-start(bf16[16,16,256]{2,1,0:T(8,128)(2,1)S(1)} %bitcast.91), channel_id=1, source_target_pairs={{8,0},{12,4},{16,8},{20,12},{24,16},{28,20},{9,1},{13,5},{17,9},{2... | collective-permute-start | bytes 393224 | tf_op jit(solution)/shard_map/ppermute | solution.py:136
  31.3 10.4 %collective-permute-start.2 = (bf16[16,16,256]{2,1,0:T(8,128)(2,1)S(1)}, bf16[16,16,256]{2,1,0:T(8,128)(2,1)S(1)}, u32[]{:S(2)}, u32[]{:S(2)}) collective-permute-start(bf16[16,16,256]{2,1,0:T(8,128)(2,1)S(1)} %bitcast.92), channel_id=1, source_target_pairs={{12,0},{16,4},{20,8},{24,12},{28,16},{13,1},{17,5},{21,9},{25,13},... | collective-permute-start | bytes 393224 | tf_op jit(solution)/shard_map/ppermute | solution.py:136
  32.6 25.0 %collective-permute-start.3 = (bf16[16,16,256]{2,1,0:T(8,128)(2,1)S(1)}, bf16[16,16,256]{2,1,0:T(8,128)(2,1)S(1)}, u32[]{:S(2)}, u32[]{:S(2)}) collective-permute-start(bf16[16,16,256]{2,1,0:T(8,128)(2,1)S(1)} %bitcast.93), channel_id=1, source_target_pairs={{16,0},{20,4},{24,8},{28,12},{17,1},{21,5},{25,9},{29,13},{18,2},{... | collective-permute-start | bytes 393224 | tf_op jit(solution)/shard_map/ppermute | solution.py:136
  33.9 26.1 %collective-permute-start.4 = (bf16[16,16,256]{2,1,0:T(8,128)(2,1)S(1)}, bf16[16,16,256]{2,1,0:T(8,128)(2,1)S(1)}, u32[]{:S(2)}, u32[]{:S(2)}) collective-permute-start(bf16[16,16,256]{2,1,0:T(8,128)(2,1)S(1)} %bitcast.94), channel_id=1, source_target_pairs={{20,0},{24,4},{28,8},{21,1},{25,5},{29,9},{22,2},{26,6},{30,10},{2... | collective-permute-start | bytes 393224 | tf_op jit(solution)/shard_map/ppermute | solution.py:136
  35.6 24.4 %collective-permute-start.5 = (bf16[16,16,256]{2,1,0:T(8,128)(2,1)S(1)}, bf16[16,16,256]{2,1,0:T(8,128)(2,1)S(1)}, u32[]{:S(2)}, u32[]{:S(2)}) collective-permute-start(bf16[16,16,256]{2,1,0:T(8,128)(2,1)S(1)} %bitcast.95), channel_id=1, source_target_pairs={{24,0},{28,4},{25,1},{29,5},{26,2},{30,6},{27,3},{31,7}} | collective-permute-start | bytes 393224 | tf_op jit(solution)/shard_map/ppermute | solution.py:136
  39.7 20.3 %collective-permute-start.6 = (bf16[16,16,256]{2,1,0:T(8,128)(2,1)S(1)}, bf16[16,16,256]{2,1,0:T(8,128)(2,1)S(1)}, u32[]{:S(2)}, u32[]{:S(2)}) collective-permute-start(bf16[16,16,256]{2,1,0:T(8,128)(2,1)S(1)} %bitcast.96), channel_id=1, source_target_pairs={{28,0},{29,1},{30,2},{31,3}} | collective-permute-start | bytes 393224 | tf_op jit(solution)/shard_map/ppermute | solution.py:136
  65.6 12.3 %all-to-all-start.1 = ((bf16[32,2,16,256]{3,2,1,0:T(8,128)(2,1)}), bf16[32,2,16,256]{3,2,1,0:T(8,128)(2,1)S(1)}, u32[]{:S(2)}, u32[]{:S(2)}) async-start(bf16[32,2,16,256]{3,2,1,0:T(8,128)(2,1)} %convert_element_type.75), calls=%async_computation.1 | async-start | bytes 1048576 | tf_op jit(solution)/shard_map/all_to_all | solution.py:148
  77.9 12.3 %all-to-all-start.2 = ((bf16[32,2,16,256]{3,2,1,0:T(8,128)(2,1)}), bf16[32,2,16,256]{3,2,1,0:T(8,128)(2,1)S(1)}, u32[]{:S(2)}, u32[]{:S(2)}) async-start(bf16[32,2,16,256]{3,2,1,0:T(8,128)(2,1)} %convert_element_type.76), calls=%async_computation.2 | async-start | bytes 1048576 | tf_op jit(solution)/shard_map/all_to_all | solution.py:148
  81.4 12.3 %copy-start.5 = (s32[1024]{0:T(1024)S(1)}, s32[1024]{0:T(1024)}, u32[]{:S(2)}) copy-start(s32[1024]{0:T(1024)} %param.4) | copy-start | bytes 12292
  90.2 12.3 %all-to-all-start.3 = ((bf16[32,2,16,256]{3,2,1,0:T(8,128)(2,1)}), bf16[32,2,16,256]{3,2,1,0:T(8,128)(2,1)S(1)}, u32[]{:S(2)}, u32[]{:S(2)}) async-start(bf16[32,2,16,256]{3,2,1,0:T(8,128)(2,1)} %convert_element_type.77), calls=%async_computation.3 | async-start | bytes 1048576 | tf_op jit(solution)/shard_map/all_to_all | solution.py:148
  102.4 4.5 %copy-start = (bf16[32,2,16,256]{3,2,1,0:T(8,128)(2,1)}, bf16[32,2,16,256]{3,2,1,0:T(8,128)(2,1)S(1)}, u32[]{:S(2)}) copy-start(bf16[32,2,16,256]{3,2,1,0:T(8,128)(2,1)S(1)} %all-to-all-done.3) | copy-start | bytes 1572868
  102.4 13.1 %all-to-all-start.4 = ((bf16[32,2,16,256]{3,2,1,0:T(8,128)(2,1)}), bf16[32,2,16,256]{3,2,1,0:T(8,128)(2,1)}, u32[]{:S(2)}, u32[]{:S(2)}) async-start(bf16[32,2,16,256]{3,2,1,0:T(8,128)(2,1)} %convert_element_type.78), calls=%async_computation.4 | async-start | bytes 1048576 | tf_op jit(solution)/shard_map/all_to_all | solution.py:148
  109.1 3.1 %copy-start.1 = (bf16[32,2,16,256]{3,2,1,0:T(8,128)(2,1)S(1)}, bf16[32,2,16,256]{3,2,1,0:T(8,128)(2,1)}, u32[]{:S(2)}) copy-start(bf16[32,2,16,256]{3,2,1,0:T(8,128)(2,1)} %copy-done) | copy-start | bytes 1572868
  110.4 6.2 %copy-start.2 = (bf16[1,1024,512]{2,1,0:T(8,128)(2,1)S(1)}, bf16[1,1024,512]{2,1,0:T(8,128)(2,1)}, u32[]{:S(2)}) copy-start(bf16[1,1024,512]{2,1,0:T(8,128)(2,1)} %copy.57) | copy-start | bytes 3145732
  111.3 5.4 %copy-start.3 = (bf16[1,1024,512]{2,1,0:T(8,128)(2,1)S(1)}, bf16[1,1024,512]{2,1,0:T(8,128)(2,1)}, u32[]{:S(2)}) copy-start(bf16[1,1024,512]{2,1,0:T(8,128)(2,1)} %copy.58) | copy-start | bytes 3145732
  112.1 4.5 %copy-start.4 = (bf16[4,8,2,2,8,256]{5,4,0,3,2,1:T(8,128)(2,1)S(1)}, bf16[4,8,2,2,8,256]{5,4,0,3,2,1:T(8,128)(2,1)}, u32[]{:S(2)}) copy-start(bf16[4,8,2,2,8,256]{5,4,0,3,2,1:T(8,128)(2,1)} %copy.63) | copy-start | bytes 1572868

commit v10 on v7

--- a/solution.py
+++ b/solution.py
@@ -140,17 +140,25 @@
     padded = jnp.concatenate(blocks, axis=0)
     base = jnp.zeros((1,), jnp.int32)
     gy_count = lax.axis_size("gy")
-    halves = pair_offsets.astype(jnp.int32).reshape(gy_count, 2, band_span // (2 * gy_count))
-    parts = []
-    for h in range(2):
-        part = cross_spectra(padded, halves[:, h].reshape(-1), base, ch_dev).astype(jnp.bfloat16)
-        parts.append(lax.all_to_all(part, "gy", split_axis=0, concat_axis=3, tiled=True))
-    cross = jnp.concatenate(parts, axis=0)
+    off_dev = band_span // gy_count
+    me = lax.axis_index("gy")
+    offsets = pair_offsets.astype(jnp.int32)
     inverse = inverse_table(kept_bins)
     norm_scale = 0.5 / math.sqrt(windows * bin_count)
-    lagged = (
-        jnp.einsum("opck,pkl->ocl", cross, inverse, preferred_element_type=jnp.float32) * norm_scale
-    )
+    lagged = None
+    for shift in list(range(1, gy_count)) + [0]:
+        dest = lax.rem(me + shift, gy_count)
+        part = cross_spectra(
+            padded, lax.dynamic_slice_in_dim(offsets, dest * off_dev, off_dev), base, ch_dev
+        ).astype(jnp.bfloat16)
+        if shift:
+            pairs = [(src, (src + shift) % gy_count) for src in range(gy_count)]
+            part = lax.ppermute(part, "gy", perm=pairs)
+        origin = lax.rem(me + gy_count - shift, gy_count)
+        rows = lax.dynamic_slice_in_dim(inverse, origin * shard_bins, shard_bins, 1)
+        term = jnp.einsum("opck,pkl->ocl", part, rows, preferred_element_type=jnp.float32)
+        lagged = term if lagged is None else lagged + term
+    lagged = lagged * norm_scale
     return lagged.astype(jnp.bfloat16)
 
 

time: 110 us -> 91.6 us (0.83)
  waiting for transfers between devices: 38.3 us -> 26.5 us
  starting transfers between devices: 20.3 us -> 14.2 us
  local copies, waits for them, and re-layouts: 15.4 us -> 11.4 us
  matrix products: 4.52 us -> 7.11 us
  Pallas kernels: 17.3 us -> 18.5 us
    all_to_all x2 -> x0, waiting for transfers between devices: 11.6 us -> none  [local(): lax.all_to_all(part, 'gy', split_axis=0, concat_axis=3, tiled=True)]
    all_to_all x2 -> x0, starting transfers between devices: 7.03 us -> none  [local(): lax.all_to_all(part, 'gy', split_axis=0, concat_axis=3, tiled=True)]
    dot_general x1 -> x4, matrix products: 2.07 us -> 4.66 us  [local(): jnp.einsum('opck,pkl->ocl', part, rows, preferred_element_type=jnp.float32)]
    sub x1, local copies, waits for them, and re-layouts: 2.28 us -> 0.53 us  [inverse_table(): cos_t = (cos_f * cos_c - sin_f * sin_c).reshape(kept_bins.shape[0], LAGS)]
    all_to_all x2 -> x0, local copies, waits for them, and re-layouts: 1.25 us -> none  [local(): lax.all_to_all(part, 'gy', split_axis=0, concat_axis=3, tiled=True)]
    pallas_call x2 -> x4, Pallas kernels: 17.3 us -> 18.5 us  [cross_spectra(): pl.pallas_call(kernel, grid_spec=pltpu.PrefetchScalarGridSpec(num_scalar_...]
    unnamed x20 -> x14, local copies, waits for them, and re-layouts: 3.68 us -> 2.6 us
    convert_element_type x2 -> x3, other arithmetic: 2.32 us -> 1.86 us  [local(): part = cross_spectra(padded, lax.dynamic_slice_in_dim(offsets, dest * off...]
  transfers between devices with their start and end apart: 10 -> 11, of which waited for: 8 -> 7; matrix products, arithmetic and copies ran while one was open for 8% -> 10% of each run, Pallas kernels for 8% -> 15%
where the time goes in v10:
time: 91.6 us; the launch traced here: 90.5 us
  waiting for transfers between devices  26.5 us (29%)
  Pallas kernels  18.5 us (20%)
  starting transfers between devices  14.2 us (16%)
  other arithmetic  12.4 us (14%)
  local copies, waits for them, and re-layouts  11.4 us (12%)
  matrix products  7.11 us (8%)
    ppermute x7, waiting for transfers between devices, local(): blocks.append(lax.ppermute(rows_white, 'gx', perm=pairs))  22.2 us
    pallas_call x4, Pallas kernels, cross_spectra(): pl.pallas_call(kernel, grid_spec=pltpu.PrefetchScalarGridSpec(num_scalar_...  18.5 us
    ppermute x7, starting transfers between devices, local(): blocks.append(lax.ppermute(rows_white, 'gx', perm=pairs))  9.02 us
    another operation x2, other arithmetic  5.32 us
    dot_general x4, matrix products, local(): jnp.einsum('opck,pkl->ocl', part, rows, preferred_element_type=jnp.float32)  4.66 us
    all_to_all x1, starting transfers between devices, local(): lax.all_to_all(white, 'gy', split_axis=3, concat_axis=0, tiled=True)  4.21 us
    all_to_all x1, waiting for transfers between devices, local(): lax.all_to_all(white, 'gy', split_axis=3, concat_axis=0, tiled=True)  4.02 us
    unnamed x14, local copies, waits for them, and re-layouts  2.6 us
  transfers between devices with their start and end apart: 11, of which 7 were waited for; matrix products, arithmetic and copies ran while one was open for 10% of the time, Pallas kernels for 15%

profile of v10, /device:TPU:0, one launch (start us, length us, event | category | flops | bytes accessed | tf_op | source)
XLA Modules:
  0.0 90.5 jit_solution(14241505732062854455)
XLA Ops:
  0.0 1.2 %fusion.52 = (f32[32,1024]{1,0:T(8,128)S(1)}, f32[32,1024]{1,0:T(8,128)S(1)}) fusion(s32[1024]{0:T(1024)} %param.4), kind=kLoop, calls=%fused_computation.86 | loop fusion | flops 458752 | bytes 266240 | tf_op jit(solution)/shard_map/cos | solution.py:90
  1.2 0.7 add_select_fusion.5
  1.9 1.8 %fusion.41 = (f32[64,1024]{1,0:T(8,128)S(1)}, f32[64,1024]{1,0:T(8,128)S(1)}) fusion(s32[1024]{0:T(1024)} %param.4, s32[64]{0:T(128)S(1)} %iota_multiply_fusion), kind=kLoop, calls=%fused_computation.69 | loop fusion | flops 917504 | bytes 528640 | tf_op jit(solution)/shard_map/cos | solution.py:90
  3.7 1.3 %copy.29 = bf16[2,16,8192]{2,1,0:T(8,128)(2,1)S(1)} copy(bf16[2,16,8192]{2,0,1:T(2,128)(2,1)} %bitcast.86) | data formatting | bytes 1048576 | tf_op jit(solution)/shard_map/transpose | solution.py:124
  5.0 0.4 reshape_reshape.3
  5.4 0.3 copy.30
  5.7 3.7 %subtract_convert_fusion = (bf16[64,32,1024]{2,1,0:T(8,128)(2,1)S(1)}, bf16[64,32,1024]{2,1,0:T(8,128)(2,1)S(1)}) fusion(f32[64,1024]{1,0:T(8,128)S(1)} %get-tuple-element.16, f32[32,1024]{1,0:T(8,128)S(1)} %get-tuple-element.22, f32[64,1024]{1,0:T(8,128)S(1)} %get-tuple-element.15, f32[32,1024]{1,0:T(8,128)S(1)} %get-tuple-element.21), kind=kLoop, calls=%fused_computation.5 | loop fusion | flops 18874368 | bytes 9175040 | tf_op jit(solution)/shard_map/convert.7
  9.4 2.5 %fusion.4 = f32[128,2048]{0,1:T(8,128)S(1)} fusion(bf16[128,2048]{1,0:T(8,128)(2,1)S(1)} %bitcast.87, bf16[2048,1024]{1,0:T(8,128)(2,1)S(1)} %bitcast.79, bf16[2048,1024]{1,0:T(8,128)(2,1)S(1)} %bitcast.78), kind=kOutput, calls=%fused_computation.14 | convolution fusion | flops 1090519040 | bytes 9961472 | tf_op jit(solution)/shard_map/dot_general | solution.py:103
  11.9 0.3 copy.31
  12.2 0.9 reshape.435
  13.1 0.8 fusion.68
  14.1 0.2 fusion.25
  15.0 0.8 copy.33
  15.8 1.7 %reshape.445 = bf16[4,2,8192]{2,1,0:T(2,128)(2,1)} reshape(bf16[1024,2,2,16]{3,2,1,0:T(2,128)(2,1)S(1)} %bitcast.76) | data formatting | bytes 262144
  17.5 4.2 %all-to-all-start = ((bf16[4,2,8192]{2,1,0:T(2,128)(2,1)}), bf16[4,2,8192]{2,1,0:T(2,128)(2,1)S(1)}, u32[]{:S(2)}, u32[]{:S(2)}) async-start(bf16[4,2,8192]{2,1,0:T(2,128)(2,1)} %reshape.445), calls=%async_computation | async-start | bytes 262144 | tf_op jit(solution)/shard_map/all_to_all | solution.py:127
  21.7 0.5 fusion.50
  22.4 4.0 %all-to-all-done = bf16[4,2,8192]{2,1,0:T(2,128)(2,1)S(1)} async-done(((bf16[4,2,8192]{2,1,0:T(2,128)(2,1)}), bf16[4,2,8192]{2,1,0:T(2,128)(2,1)S(1)}, u32[]{:S(2)}, u32[]{:S(2)}) %all-to-all-start) | async-done | bytes 131104 | tf_op jit(solution)/shard_map/all_to_all | solution.py:127
  26.4 0.7 reshape.446
  27.1 1.4 %copy.43 = bf16[2,16,2,4,256]{4,3,1,2,0:T(4,128)(2,1)S(1)} copy(bf16[2,16,2,4,256]{1,2,0,4,3:T(2,128)(2,1)S(1)} %bitcast.77) | data formatting | bytes 262144 | tf_op jit(solution)/shard_map/all_to_all | solution.py:127
  28.6 1.3 %collective-permute-start = (bf16[16,16,256]{2,1,0:T(8,128)(2,1)S(1)}, bf16[16,16,256]{2,1,0:T(8,128)(2,1)S(1)}, u32[]{:S(2)}, u32[]{:S(2)}) collective-permute-start(bf16[16,16,256]{2,1,0:T(8,128)(2,1)S(1)} %bitcast.88), channel_id=1, source_target_pairs={{4,0},{8,4},{12,8},{16,12},{20,16},{24,20},{28,24},{5,1},{9,5},{13... | collective-permute-start | bytes 393224 | tf_op jit(solution)/shard_map/ppermute | solution.py:136
  29.9 1.3 %collective-permute-start.1 = (bf16[16,16,256]{2,1,0:T(8,128)(2,1)S(1)}, bf16[16,16,256]{2,1,0:T(8,128)(2,1)S(1)}, u32[]{:S(2)}, u32[]{:S(2)}) collective-permute-start(bf16[16,16,256]{2,1,0:T(8,128)(2,1)S(1)} %bitcast.89), channel_id=1, source_target_pairs={{8,0},{12,4},{16,8},{20,12},{24,16},{28,20},{9,1},{13,5},{17,9},{2... | collective-permute-start | bytes 393224 | tf_op jit(solution)/shard_map/ppermute | solution.py:136
  31.3 1.3 %collective-permute-start.2 = (bf16[16,16,256]{2,1,0:T(8,128)(2,1)S(1)}, bf16[16,16,256]{2,1,0:T(8,128)(2,1)S(1)}, u32[]{:S(2)}, u32[]{:S(2)}) collective-permute-start(bf16[16,16,256]{2,1,0:T(8,128)(2,1)S(1)} %bitcast.90), channel_id=1, source_target_pairs={{12,0},{16,4},{20,8},{24,12},{28,16},{13,1},{17,5},{21,9},{25,13},... | collective-permute-start | bytes 393224 | tf_op jit(solution)/shard_map/ppermute | solution.py:136
  32.6 1.3 %collective-permute-start.3 = (bf16[16,16,256]{2,1,0:T(8,128)(2,1)S(1)}, bf16[16,16,256]{2,1,0:T(8,128)(2,1)S(1)}, u32[]{:S(2)}, u32[]{:S(2)}) collective-permute-start(bf16[16,16,256]{2,1,0:T(8,128)(2,1)S(1)} %bitcast.91), channel_id=1, source_target_pairs={{16,0},{20,4},{24,8},{28,12},{17,1},{21,5},{25,9},{29,13},{18,2},{... | collective-permute-start | bytes 393224 | tf_op jit(solution)/shard_map/ppermute | solution.py:136
  33.9 1.3 %collective-permute-start.4 = (bf16[16,16,256]{2,1,0:T(8,128)(2,1)S(1)}, bf16[16,16,256]{2,1,0:T(8,128)(2,1)S(1)}, u32[]{:S(2)}, u32[]{:S(2)}) collective-permute-start(bf16[16,16,256]{2,1,0:T(8,128)(2,1)S(1)} %bitcast.92), channel_id=1, source_target_pairs={{20,0},{24,4},{28,8},{21,1},{25,5},{29,9},{22,2},{26,6},{30,10},{2... | collective-permute-start | bytes 393224 | tf_op jit(solution)/shard_map/ppermute | solution.py:136
  35.2 0.5 collective-permute-done
  35.6 1.3 %collective-permute-start.5 = (bf16[16,16,256]{2,1,0:T(8,128)(2,1)S(1)}, bf16[16,16,256]{2,1,0:T(8,128)(2,1)S(1)}, u32[]{:S(2)}, u32[]{:S(2)}) collective-permute-start(bf16[16,16,256]{2,1,0:T(8,128)(2,1)S(1)} %bitcast.93), channel_id=1, source_target_pairs={{24,0},{28,4},{25,1},{29,5},{26,2},{30,6},{27,3},{31,7}} | collective-permute-start | bytes 393224 | tf_op jit(solution)/shard_map/ppermute | solution.py:136
  37.0 2.8 %collective-permute-done.1 = bf16[16,16,256]{2,1,0:T(8,128)(2,1)S(1)} collective-permute-done((bf16[16,16,256]{2,1,0:T(8,128)(2,1)S(1)}, bf16[16,16,256]{2,1,0:T(8,128)(2,1)S(1)}, u32[]{:S(2)}, u32[]{:S(2)}) %collective-permute-start.1) | collective-permute-done | bytes 131104 | tf_op jit(solution)/shard_map/ppermute | solution.py:136
  39.7 1.3 %collective-permute-start.6 = (bf16[16,16,256]{2,1,0:T(8,128)(2,1)S(1)}, bf16[16,16,256]{2,1,0:T(8,128)(2,1)S(1)}, u32[]{:S(2)}, u32[]{:S(2)}) collective-permute-start(bf16[16,16,256]{2,1,0:T(8,128)(2,1)S(1)} %bitcast.94), channel_id=1, source_target_pairs={{28,0},{29,1},{30,2},{31,3}} | collective-permute-start | bytes 393224 | tf_op jit(solution)/shard_map/ppermute | solution.py:136
  41.0 0.7 collective-permute-done.2
  41.7 15.9 %collective-permute-done.3 = bf16[16,16,256]{2,1,0:T(8,128)(2,1)S(1)} collective-permute-done((bf16[16,16,256]{2,1,0:T(8,128)(2,1)S(1)}, bf16[16,16,256]{2,1,0:T(8,128)(2,1)S(1)}, u32[]{:S(2)}, u32[]{:S(2)}) %collective-permute-start.3) | collective-permute-done | bytes 131104 | tf_op jit(solution)/shard_map/ppermute | solution.py:136
  57.6 2.4 %collective-permute-done.4 = bf16[16,16,256]{2,1,0:T(8,128)(2,1)S(1)} collective-permute-done((bf16[16,16,256]{2,1,0:T(8,128)(2,1)S(1)}, bf16[16,16,256]{2,1,0:T(8,128)(2,1)S(1)}, u32[]{:S(2)}, u32[]{:S(2)}) %collective-permute-start.4) | collective-permute-done | bytes 131104 | tf_op jit(solution)/shard_map/ppermute | solution.py:136
  60.1 4.6 %shard_map.38 = f32[32,2,16,256]{3,2,1,0:T(8,128)S(1)} custom-call(s32[32]{0:T(128)S(1)} %get-tuple-element.26.offsets_ref, s32[1]{0:T(128)} %constant.111.clone.1.base_ref, bf16[144,16,256]{2,1,0:T(8,128)(2,1)S(1)} %broadcast_dynamic-update-slice_fusion.white_ref), custom_call_target="tpu_custom_call" | custom-call | flops 16777216 | bytes 2228224 | tf_op jit(solution)/shard_map/pallas_call | solution.py:60
  64.7 0.9 %convert_element_type.78 = bf16[32,2,16,256]{3,2,1,0:T(8,128)(2,1)} convert(f32[32,2,16,256]{3,2,1,0:T(8,128)S(1)} %shard_map.38) | non-fusion elementwise | flops 262144 | bytes 1572864 | tf_op jit(solution)/shard_map/convert_element_type | solution.py:153
  65.6 0.4 collective-permute-start.8
  66.0 0.3 fusion.54
  66.3 4.6 %shard_map.39 = f32[32,2,16,256]{3,2,1,0:T(8,128)S(1)} custom-call(s32[32]{0:T(128)S(1)} %get-tuple-element.28.offsets_ref, s32[1]{0:T(128)} %constant.111.clone.1.base_ref, bf16[144,16,256]{2,1,0:T(8,128)(2,1)S(1)} %broadcast_dynamic-update-slice_fusion.white_ref), custom_call_target="tpu_custom_call" | custom-call | flops 16777216 | bytes 2228224 | tf_op jit(solution)/shard_map/pallas_call | solution.py:60
  71.0 0.9 convert_element_type.79
  71.9 1.7 %negate_convert_fusion.1 = (bf16[1024,16,32]{0,2,1:T(8,128)(2,1)}, bf16[1024,16,32]{0,2,1:T(8,128)(2,1)S(1)}) fusion(f32[1024,16]{0,1:T(8,128)S(1)} %get-tuple-element.18, f32[1024,32]{0,1:T(8,128)S(1)} %get-tuple-element.24, f32[1024,16]{0,1:T(8,128)S(1)} %get-tuple-element.17, f32[1024,32]{0,1:T(8,128)S(1)} %get-tuple-element.23), kind=kLoop, calls=%fused_computation.15 | loop fusion | flops 4718592 | bytes 2490368 | tf_op jit(solution)/shard_map/convert.2
  73.5 0.5 copy.37
  74.1 1.5 %copy.38 = bf16[1,1024,512]{2,1,0:T(8,128)(2,1)S(1)} copy(bf16[1,1024,512]{1,2,0:T(8,128)(2,1)} %bitcast.80) | data formatting | bytes 2097152 | tf_op jit(solution)/shard_map/neg | solution.py:29
  75.6 4.6 %shard_map.37 = f32[32,2,16,256]{3,2,1,0:T(8,128)S(1)} custom-call(s32[32]{0:T(128)S(1)} %get-tuple-element.25.offsets_ref, s32[1]{0:T(128)} %constant.111.clone.1.base_ref, bf16[144,16,256]{2,1,0:T(8,128)(2,1)S(1)} %broadcast_dynamic-update-slice_fusion.white_ref), custom_call_target="tpu_custom_call" | custom-call | flops 16777216 | bytes 2228224 | tf_op jit(solution)/shard_map/pallas_call | solution.py:60
  80.3 0.6 collective-permute-start.7
  80.8 4.6 %shard_map.40 = f32[32,2,16,256]{3,2,1,0:T(8,128)S(1)} custom-call(s32[32]{0:T(128)S(1)} %get-tuple-element.27.offsets_ref, s32[1]{0:T(128)} %constant.111.clone.1.base_ref, bf16[144,16,256]{2,1,0:T(8,128)(2,1)S(1)} %broadcast_dynamic-update-slice_fusion.white_ref), custom_call_target="tpu_custom_call" | custom-call | flops 16777216 | bytes 2228224 | tf_op jit(solution)/shard_map/pallas_call | solution.py:60
  85.5 0.4 convolution_bitcast_fusion
  85.9 1.5 %convolution_bitcast_fusion.2 = f32[32,16,512]{2,1,0:T(8,128)S(1)} fusion(bf16[32,2,16,256]{3,2,1,0:T(8,128)(2,1)} %collective-permute-done.8, s32[]{:T(128)S(6)} %select_n.105, bf16[1,1024,512]{2,1,0:T(8,128)(2,1)S(1)} %copy.37, bf16[1,1024,512]{2,1,0:T(8,128)(2,1)S(1)} %copy.38), kind=kOutput, calls=%fused_computation.19 | convolution fusion | flops 269484032 | bytes 3670020 | tf_op jit(solution)/shard_map/opck,pkl->ocl/dot_general | solution.py:159
  87.4 1.5 %convolution_bitcast_fusion.1 = f32[32,16,512]{2,1,0:T(8,128)S(1)} fusion(bf16[32,2,16,256]{3,2,1,0:T(8,128)(2,1)} %collective-permute-done.9, s32[]{:T(128)S(6)} %select_n.107, bf16[1,1024,512]{2,1,0:T(8,128)(2,1)S(1)} %copy.37, bf16[1,1024,512]{2,1,0:T(8,128)(2,1)S(1)} %copy.38), kind=kOutput, calls=%fused_computation.18 | convolution fusion | flops 269484032 | bytes 3670020 | tf_op jit(solution)/shard_map/opck,pkl->ocl/dot_general | solution.py:159
  88.9 0.3 collective-permute-done.7
  89.2 1.3 %fusion.11 = bf16[32,16,512]{2,1,0:T(8,128)(2,1)} fusion(f32[32,16,512]{2,1,0:T(8,128)S(1)} %convolution_bitcast_fusion, f32[32,16,512]{2,1,0:T(8,128)S(1)} %convolution_bitcast_fusion.1, f32[32,16,512]{2,1,0:T(8,128)S(1)} %convolution_bitcast_fusion.2, bf16[32,2,16,256]{3,2,1,0:T(8,128)(2,1)S(1)} %collective-permute-done.7, s32[]{:T(128)S(6)} %select_n.103, ...), kind=kOutput, calls=%fused_computation.25 | convolution fusion | flops 270794752 | bytes 6291460 | tf_op jit(solution)/shard_map/opck,pkl->ocl/dot_general | solution.py:159
  (30 shorter events, 1.2 us)
Async XLA Ops:
  14.3 7.4 %copy-start = (s32[1024]{0:T(1024)S(1)}, s32[1024]{0:T(1024)}, u32[]{:S(2)}) copy-start(s32[1024]{0:T(1024)} %param.4) | copy-start | bytes 12292
  14.3 7.9 %copy-start.1 = (s32[128]{0:T(128)S(1)}, s32[128]{0:T(128)}, u32[]{:S(2)}) copy-start(s32[128]{0:T(128)} %param.5) | copy-start | bytes 1540
  17.5 8.9 %all-to-all-start = ((bf16[4,2,8192]{2,1,0:T(2,128)(2,1)}), bf16[4,2,8192]{2,1,0:T(2,128)(2,1)S(1)}, u32[]{:S(2)}, u32[]{:S(2)}) async-start(bf16[4,2,8192]{2,1,0:T(2,128)(2,1)} %reshape.445), calls=%async_computation | async-start | bytes 262144 | tf_op jit(solution)/shard_map/all_to_all | solution.py:127
  28.6 7.1 %collective-permute-start = (bf16[16,16,256]{2,1,0:T(8,128)(2,1)S(1)}, bf16[16,16,256]{2,1,0:T(8,128)(2,1)S(1)}, u32[]{:S(2)}, u32[]{:S(2)}) collective-permute-start(bf16[16,16,256]{2,1,0:T(8,128)(2,1)S(1)} %bitcast.88), channel_id=1, source_target_pairs={{4,0},{8,4},{12,8},{16,12},{20,16},{24,20},{28,24},{5,1},{9,5},{13... | collective-permute-start | bytes 393224 | tf_op jit(solution)/shard_map/ppermute | solution.py:136
  29.9 9.8 %collective-permute-start.1 = (bf16[16,16,256]{2,1,0:T(8,128)(2,1)S(1)}, bf16[16,16,256]{2,1,0:T(8,128)(2,1)S(1)}, u32[]{:S(2)}, u32[]{:S(2)}) collective-permute-start(bf16[16,16,256]{2,1,0:T(8,128)(2,1)S(1)} %bitcast.89), channel_id=1, source_target_pairs={{8,0},{12,4},{16,8},{20,12},{24,16},{28,20},{9,1},{13,5},{17,9},{2... | collective-permute-start | bytes 393224 | tf_op jit(solution)/shard_map/ppermute | solution.py:136
  31.3 10.4 %collective-permute-start.2 = (bf16[16,16,256]{2,1,0:T(8,128)(2,1)S(1)}, bf16[16,16,256]{2,1,0:T(8,128)(2,1)S(1)}, u32[]{:S(2)}, u32[]{:S(2)}) collective-permute-start(bf16[16,16,256]{2,1,0:T(8,128)(2,1)S(1)} %bitcast.90), channel_id=1, source_target_pairs={{12,0},{16,4},{20,8},{24,12},{28,16},{13,1},{17,5},{21,9},{25,13},... | collective-permute-start | bytes 393224 | tf_op jit(solution)/shard_map/ppermute | solution.py:136
  32.6 25.0 %collective-permute-start.3 = (bf16[16,16,256]{2,1,0:T(8,128)(2,1)S(1)}, bf16[16,16,256]{2,1,0:T(8,128)(2,1)S(1)}, u32[]{:S(2)}, u32[]{:S(2)}) collective-permute-start(bf16[16,16,256]{2,1,0:T(8,128)(2,1)S(1)} %bitcast.91), channel_id=1, source_target_pairs={{16,0},{20,4},{24,8},{28,12},{17,1},{21,5},{25,9},{29,13},{18,2},{... | collective-permute-start | bytes 393224 | tf_op jit(solution)/shard_map/ppermute | solution.py:136
  33.9 26.1 %collective-permute-start.4 = (bf16[16,16,256]{2,1,0:T(8,128)(2,1)S(1)}, bf16[16,16,256]{2,1,0:T(8,128)(2,1)S(1)}, u32[]{:S(2)}, u32[]{:S(2)}) collective-permute-start(bf16[16,16,256]{2,1,0:T(8,128)(2,1)S(1)} %bitcast.92), channel_id=1, source_target_pairs={{20,0},{24,4},{28,8},{21,1},{25,5},{29,9},{22,2},{26,6},{30,10},{2... | collective-permute-start | bytes 393224 | tf_op jit(solution)/shard_map/ppermute | solution.py:136
  35.6 24.4 %collective-permute-start.5 = (bf16[16,16,256]{2,1,0:T(8,128)(2,1)S(1)}, bf16[16,16,256]{2,1,0:T(8,128)(2,1)S(1)}, u32[]{:S(2)}, u32[]{:S(2)}) collective-permute-start(bf16[16,16,256]{2,1,0:T(8,128)(2,1)S(1)} %bitcast.93), channel_id=1, source_target_pairs={{24,0},{28,4},{25,1},{29,5},{26,2},{30,6},{27,3},{31,7}} | collective-permute-start | bytes 393224 | tf_op jit(solution)/shard_map/ppermute | solution.py:136
  39.7 20.3 %collective-permute-start.6 = (bf16[16,16,256]{2,1,0:T(8,128)(2,1)S(1)}, bf16[16,16,256]{2,1,0:T(8,128)(2,1)S(1)}, u32[]{:S(2)}, u32[]{:S(2)}) collective-permute-start(bf16[16,16,256]{2,1,0:T(8,128)(2,1)S(1)} %bitcast.94), channel_id=1, source_target_pairs={{28,0},{29,1},{30,2},{31,3}} | collective-permute-start | bytes 393224 | tf_op jit(solution)/shard_map/ppermute | solution.py:136
  65.6 20.3 %collective-permute-start.8 = (bf16[32,2,16,256]{3,2,1,0:T(8,128)(2,1)}, bf16[32,2,16,256]{3,2,1,0:T(8,128)(2,1)}, u32[]{:S(2)}, u32[]{:S(2)}) collective-permute-start(bf16[32,2,16,256]{3,2,1,0:T(8,128)(2,1)} %convert_element_type.78), channel_id=1, source_target_pairs={{0,2},{1,3},{2,0},{3,1},{4,6},{5,7},{6,4},{7,5},{8,10},{9,11},{10,... | collective-permute-start | bytes 1572872 | tf_op jit(solution)/shard_map/ppermute | solution.py:156
  71.8 15.6 %collective-permute-start.9 = (bf16[32,2,16,256]{3,2,1,0:T(8,128)(2,1)}, bf16[32,2,16,256]{3,2,1,0:T(8,128)(2,1)}, u32[]{:S(2)}, u32[]{:S(2)}) collective-permute-start(bf16[32,2,16,256]{3,2,1,0:T(8,128)(2,1)} %convert_element_type.79), channel_id=1, source_target_pairs={{0,3},{1,0},{2,1},{3,2},{4,7},{5,4},{6,5},{7,6},{8,11},{9,8},{10,9... | collective-permute-start | bytes 1572872 | tf_op jit(solution)/shard_map/ppermute | solution.py:156
  80.3 8.9 %collective-permute-start.7 = (bf16[32,2,16,256]{3,2,1,0:T(8,128)(2,1)S(1)}, bf16[32,2,16,256]{3,2,1,0:T(8,128)(2,1)S(1)}, u32[]{:S(2)}, u32[]{:S(2)}) collective-permute-start(bf16[32,2,16,256]{3,2,1,0:T(8,128)(2,1)S(1)} %convert_element_type.75), channel_id=1, source_target_pairs={{0,1},{1,2},{2,3},{3,0},{4,5},{5,6},{6,7},{7,4},{8,9},{9,10},{10,1... | collective-permute-start | bytes 1572872 | tf_op jit(solution)/shard_map/ppermute | solution.py:156

commit v11 on v5

--- a/solution.py
+++ b/solution.py
@@ -128,23 +128,45 @@
     windows = freq_white.shape[0]
     shard_bins = freq_white.shape[3]
     rows_white = jnp.transpose(freq_white, (1, 2, 0, 3)).reshape(ch_dev, 2 * windows, shard_bins)
-    all_white = lax.all_gather(rows_white, "gx", axis=0, tiled=True)
-    padded = jnp.concatenate(
-        [all_white, jnp.zeros((band_span,) + all_white.shape[1:], all_white.dtype)], axis=0
-    )
-    base = (lax.axis_index("gx") * ch_dev).astype(jnp.int32).reshape(1)
+    gx_count = lax.axis_size("gx")
     gy_count = lax.axis_size("gy")
-    halves = pair_offsets.astype(jnp.int32).reshape(gy_count, 2, band_span // (2 * gy_count))
-    parts = []
-    for h in range(2):
-        part = cross_spectra(padded, halves[:, h].reshape(-1), base, ch_dev).astype(jnp.bfloat16)
-        parts.append(lax.all_to_all(part, "gy", split_axis=0, concat_axis=3, tiled=True))
-    cross = jnp.concatenate(parts, axis=0)
+    needed = -(-band_span // ch_dev)
+    off_dev = band_span // gy_count
+    me = lax.axis_index("gy")
+    offsets = pair_offsets.astype(jnp.int32)
     inverse = inverse_table(kept_bins)
     norm_scale = 0.5 / math.sqrt(windows * bin_count)
-    lagged = (
-        jnp.einsum("opck,pkl->ocl", cross, inverse, preferred_element_type=jnp.float32) * norm_scale
-    )
+    base = jnp.zeros((1,), jnp.int32)
+    half_bins = shard_bins // 2
+
+    def gather_above(own_rows):
+        blocks = [own_rows]
+        for shift in range(1, min(needed, gx_count - 1) + 1):
+            pairs = [(src, src - shift) for src in range(shift, gx_count)]
+            blocks.append(lax.ppermute(own_rows, "gx", perm=pairs))
+        missing = needed + 1 - len(blocks)
+        if missing > 0:
+            blocks.append(jnp.zeros((missing * ch_dev,) + own_rows.shape[1:], own_rows.dtype))
+        return jnp.concatenate(blocks, axis=0)
+
+    first_half = gather_above(rows_white[:, :, :half_bins])
+    second_own, first_half = lax.optimization_barrier((rows_white[:, :, half_bins:], first_half))
+    second_half = gather_above(second_own)
+    lagged = None
+    for h, padded in enumerate([first_half, second_half]):
+        for shift in list(range(1, gy_count)) + [0]:
+            dest = lax.rem(me + shift, gy_count)
+            part = cross_spectra(
+                padded, lax.dynamic_slice_in_dim(offsets, dest * off_dev, off_dev), base, ch_dev
+            ).astype(jnp.bfloat16)
+            if shift:
+                pairs = [(src, (src + shift) % gy_count) for src in range(gy_count)]
+                part = lax.ppermute(part, "gy", perm=pairs)
+            origin = lax.rem(me + gy_count - shift, gy_count)
+            rows = lax.dynamic_slice_in_dim(inverse, origin * shard_bins + h * half_bins, half_bins, 1)
+            term = jnp.einsum("opck,pkl->ocl", part, rows, preferred_element_type=jnp.float32)
+            lagged = term if lagged is None else lagged + term
+    lagged = lagged * norm_scale
     return lagged.astype(jnp.bfloat16)
 
 

time: 134 us -> 98.9 us (0.74)
  waiting for transfers between devices: 52 us -> 28 us
  starting transfers between devices: 7.03 us -> 24.7 us
  between operations: 13.6 us -> 0.72 us
  blocking collectives: 8.64 us -> 0 us
  local copies, waits for them, and re-layouts: 15.6 us -> 10.5 us
  other arithmetic: 13 us -> 9.44 us
  Pallas kernels: 17.3 us -> 19 us
    all_gather x1 -> x0, waiting for transfers between devices: 40.4 us -> none  [local(): all_white = lax.all_gather(rows_white, 'gx', axis=0, tiled=True)]
    ppermute x0 -> x20, waiting for transfers between devices: none -> 26.2 us  [the longest x14 21.8 us: gather_above(): blocks.append(lax.ppermute(own_rows, 'gx', perm=pairs))]
    ppermute x0 -> x20, starting transfers between devices: none -> 20.5 us  [the longest x14 18.1 us: gather_above(): blocks.append(lax.ppermute(own_rows, 'gx', perm=pairs))]
    all_to_all x2 -> x1, waiting for transfers between devices: 11.6 us -> 1.81 us  [local(): lax.all_to_all(white, 'gy', split_axis=3, concat_axis=0, tiled=True)]
    all_to_all x1 -> x0, blocking collectives: 8.64 us -> none  [local(): lax.all_to_all(white, 'gy', split_axis=3, concat_axis=0, tiled=True)]
    all_to_all x2 -> x1, starting transfers between devices: 7.03 us -> 4.21 us  [local(): lax.all_to_all(white, 'gy', split_axis=3, concat_axis=0, tiled=True)]
    convert_element_type x2 -> x6, other arithmetic: 2.35 us -> 0.23 us  [local(): part = cross_spectra(padded, lax.dynamic_slice_in_dim(offsets, dest * off...]
    sub x1, local copies, waits for them, and re-layouts: 2.29 us -> 0.54 us  [inverse_table(): cos_t = (cos_f * cos_c - sin_f * sin_c).reshape(kept_bins.shape[0], LAGS)]
  transfers between devices with their start and end apart: 3 -> 21, of which waited for: 3 -> 9; matrix products, arithmetic and copies ran while one was open for 7% -> 5% of each run, Pallas kernels for 6% -> 19%
where the time goes in v11:
time: 98.9 us; the launch traced here: 98.3 us
  waiting for transfers between devices  28 us (28%)
  starting transfers between devices  24.7 us (25%)
  Pallas kernels  19 us (19%)
  local copies, waits for them, and re-layouts  10.5 us (11%)
  other arithmetic  9.44 us (10%)
  matrix products  5.87 us (6%)
    ppermute x14, waiting for transfers between devices, gather_above(): blocks.append(lax.ppermute(own_rows, 'gx', perm=pairs))  21.8 us
    pallas_call x8, Pallas kernels, cross_spectra(): pl.pallas_call(kernel, grid_spec=pltpu.PrefetchScalarGridSpec(num_scalar_...  19 us
    ppermute x14, starting transfers between devices, gather_above(): blocks.append(lax.ppermute(own_rows, 'gx', perm=pairs))  18.1 us
    another operation x2, other arithmetic  4.56 us
    ppermute x6, waiting for transfers between devices, local(): part = lax.ppermute(part, 'gy', perm=pairs)  4.37 us
    all_to_all x1, starting transfers between devices, local(): lax.all_to_all(white, 'gy', split_axis=3, concat_axis=0, tiled=True)  4.21 us
    dot_general x8, matrix products, local(): jnp.einsum('opck,pkl->ocl', part, rows, preferred_element_type=jnp.float32)  3.41 us
    unnamed x21, local copies, waits for them, and re-layouts  2.63 us
  transfers between devices with their start and end apart: 21, of which 9 were waited for; matrix products, arithmetic and copies ran while one was open for 5% of the time, Pallas kernels for 19%

profile of v11, /device:TPU:0, one launch (start us, length us, event | category | flops | bytes accessed | tf_op | source)
XLA Modules:
  0.0 98.3 jit_solution(6627851858165540480)
XLA Ops:
  0.0 1.3 %fusion.69 = (f32[32,1024]{1,0:T(8,128)S(1)}, f32[32,1024]{1,0:T(8,128)S(1)}) fusion(s32[1024]{0:T(1024)} %param.4), kind=kLoop, calls=%fused_computation.110 | loop fusion | flops 458752 | bytes 266240 | tf_op jit(solution)/shard_map/cos | solution.py:90
  1.3 0.7 add_select_fusion.5
  2.0 1.3 %copy.29 = bf16[2,16,8192]{2,1,0:T(8,128)(2,1)S(1)} copy(bf16[2,16,8192]{2,0,1:T(2,128)(2,1)} %bitcast.117) | data formatting | bytes 1048576 | tf_op jit(solution)/shard_map/transpose | solution.py:124
  4.0 1.1 %fusion.58 = (f32[64,1024]{1,0:T(8,128)S(1)}, f32[64,1024]{1,0:T(8,128)S(1)}) fusion(s32[1024]{0:T(1024)S(1)} %copy-done, s32[64]{0:T(128)S(1)} %iota_multiply_fusion), kind=kLoop, calls=%fused_computation.94 | loop fusion | flops 917504 | bytes 528640 | tf_op jit(solution)/shard_map/cos | solution.py:90
  5.1 3.8 %subtract_convert_fusion = (bf16[64,32,1024]{2,1,0:T(8,128)(2,1)S(1)}, bf16[64,32,1024]{2,1,0:T(8,128)(2,1)S(1)}) fusion(f32[64,1024]{1,0:T(8,128)S(1)} %get-tuple-element.25, f32[32,1024]{1,0:T(8,128)S(1)} %get-tuple-element.31, f32[64,1024]{1,0:T(8,128)S(1)} %get-tuple-element.24, f32[32,1024]{1,0:T(8,128)S(1)} %get-tuple-element.30), kind=kLoop, calls=%fused_computation.5 | loop fusion | flops 18874368 | bytes 9175040 | tf_op jit(solution)/shard_map/convert.7
  8.9 2.5 %fusion.4 = f32[128,2048]{0,1:T(8,128)S(1)} fusion(bf16[128,2048]{1,0:T(8,128)(2,1)S(1)} %bitcast.118, bf16[2048,1024]{1,0:T(8,128)(2,1)S(1)} %bitcast.112, bf16[2048,1024]{1,0:T(8,128)(2,1)S(1)} %bitcast.111), kind=kOutput, calls=%fused_computation.22 | convolution fusion | flops 1090519040 | bytes 9961472 | tf_op jit(solution)/shard_map/dot_general | solution.py:103
  11.7 0.9 reshape.435
  12.6 0.8 fusion.93
  14.5 0.8 copy.33
  15.3 1.7 %reshape.453 = bf16[4,2,8192]{2,1,0:T(2,128)(2,1)} reshape(bf16[1024,2,2,16]{3,2,1,0:T(2,128)(2,1)S(1)} %bitcast.109) | data formatting | bytes 262144
  17.0 4.2 %all-to-all-start = ((bf16[4,2,8192]{2,1,0:T(2,128)(2,1)}), bf16[4,2,8192]{2,1,0:T(2,128)(2,1)S(1)}, u32[]{:S(2)}, u32[]{:S(2)}) async-start(bf16[4,2,8192]{2,1,0:T(2,128)(2,1)} %reshape.453), calls=%async_computation | async-start | bytes 262144 | tf_op jit(solution)/shard_map/all_to_all | solution.py:127
  22.1 0.7 negate_convert_fusion.1
  24.1 1.8 %all-to-all-done = bf16[4,2,8192]{2,1,0:T(2,128)(2,1)S(1)} async-done(((bf16[4,2,8192]{2,1,0:T(2,128)(2,1)}), bf16[4,2,8192]{2,1,0:T(2,128)(2,1)S(1)}, u32[]{:S(2)}, u32[]{:S(2)}) %all-to-all-start) | async-done | bytes 131104 | tf_op jit(solution)/shard_map/all_to_all | solution.py:127
  25.9 0.7 reshape.454
  26.6 1.4 %copy.47 = bf16[2,16,2,4,256]{4,3,1,2,0:T(4,128)(2,1)S(1)} copy(bf16[2,16,2,4,256]{1,2,0,4,3:T(2,128)(2,1)S(1)} %bitcast.110) | data formatting | bytes 262144 | tf_op jit(solution)/shard_map/all_to_all | solution.py:127
  28.2 1.3 %collective-permute-start = (bf16[16,16,128]{2,1,0:T(8,128)(2,1)S(1)}, bf16[16,16,128]{2,1,0:T(8,128)(2,1)S(1)}, u32[]{:S(2)}, u32[]{:S(2)}) collective-permute-start(bf16[16,16,128]{2,1,0:T(8,128)(2,1)S(1)} %get-tuple-element.19), channel_id=1, source_target_pairs={{4,0},{8,4},{12,8},{16,12},{20,16},{24,20},{28,24},{5,1},{9,5},{13... | collective-permute-start | bytes 196616 | tf_op jit(solution)/shard_map/ppermute | solution.py:146
  29.6 1.3 %collective-permute-start.1 = (bf16[16,16,128]{2,1,0:T(8,128)(2,1)S(1)}, bf16[16,16,128]{2,1,0:T(8,128)(2,1)S(1)}, u32[]{:S(2)}, u32[]{:S(2)}) collective-permute-start(bf16[16,16,128]{2,1,0:T(8,128)(2,1)S(1)} %get-tuple-element.19), channel_id=1, source_target_pairs={{8,0},{12,4},{16,8},{20,12},{24,16},{28,20},{9,1},{13,5},{17,9},{2... | collective-permute-start | bytes 196616 | tf_op jit(solution)/shard_map/ppermute | solution.py:146
  30.8 1.3 %collective-permute-start.2 = (bf16[16,16,128]{2,1,0:T(8,128)(2,1)S(1)}, bf16[16,16,128]{2,1,0:T(8,128)(2,1)S(1)}, u32[]{:S(2)}, u32[]{:S(2)}) collective-permute-start(bf16[16,16,128]{2,1,0:T(8,128)(2,1)S(1)} %get-tuple-element.19), channel_id=1, source_target_pairs={{12,0},{16,4},{20,8},{24,12},{28,16},{13,1},{17,5},{21,9},{25,13},... | collective-permute-start | bytes 196616 | tf_op jit(solution)/shard_map/ppermute | solution.py:146
  32.1 1.3 %collective-permute-start.3 = (bf16[16,16,128]{2,1,0:T(8,128)(2,1)S(1)}, bf16[16,16,128]{2,1,0:T(8,128)(2,1)S(1)}, u32[]{:S(2)}, u32[]{:S(2)}) collective-permute-start(bf16[16,16,128]{2,1,0:T(8,128)(2,1)S(1)} %get-tuple-element.19), channel_id=1, source_target_pairs={{16,0},{20,4},{24,8},{28,12},{17,1},{21,5},{25,9},{29,13},{18,2},{... | collective-permute-start | bytes 196616 | tf_op jit(solution)/shard_map/ppermute | solution.py:146
  33.4 1.3 %collective-permute-start.4 = (bf16[16,16,128]{2,1,0:T(8,128)(2,1)S(1)}, bf16[16,16,128]{2,1,0:T(8,128)(2,1)S(1)}, u32[]{:S(2)}, u32[]{:S(2)}) collective-permute-start(bf16[16,16,128]{2,1,0:T(8,128)(2,1)S(1)} %get-tuple-element.19), channel_id=1, source_target_pairs={{20,0},{24,4},{28,8},{21,1},{25,5},{29,9},{22,2},{26,6},{30,10},{2... | collective-permute-start | bytes 196616 | tf_op jit(solution)/shard_map/ppermute | solution.py:146
  34.8 1.3 %collective-permute-start.5 = (bf16[16,16,128]{2,1,0:T(8,128)(2,1)S(1)}, bf16[16,16,128]{2,1,0:T(8,128)(2,1)S(1)}, u32[]{:S(2)}, u32[]{:S(2)}) collective-permute-start(bf16[16,16,128]{2,1,0:T(8,128)(2,1)S(1)} %get-tuple-element.19), channel_id=1, source_target_pairs={{24,0},{28,4},{25,1},{29,5},{26,2},{30,6},{27,3},{31,7}} | collective-permute-start | bytes 196616 | tf_op jit(solution)/shard_map/ppermute | solution.py:146
  36.1 1.7 %collective-permute-done.1 = bf16[16,16,128]{2,1,0:T(8,128)(2,1)S(1)} collective-permute-done((bf16[16,16,128]{2,1,0:T(8,128)(2,1)S(1)}, bf16[16,16,128]{2,1,0:T(8,128)(2,1)S(1)}, u32[]{:S(2)}, u32[]{:S(2)}) %collective-permute-start.1) | collective-permute-done | bytes 65568 | tf_op jit(solution)/shard_map/ppermute | solution.py:146
  37.8 1.3 %collective-permute-start.6 = (bf16[16,16,128]{2,1,0:T(8,128)(2,1)S(1)}, bf16[16,16,128]{2,1,0:T(8,128)(2,1)S(1)}, u32[]{:S(2)}, u32[]{:S(2)}) collective-permute-start(bf16[16,16,128]{2,1,0:T(8,128)(2,1)S(1)} %get-tuple-element.19), channel_id=1, source_target_pairs={{28,0},{29,1},{30,2},{31,3}} | collective-permute-start | bytes 196616 | tf_op jit(solution)/shard_map/ppermute | solution.py:146
  39.1 0.7 collective-permute-done.2
  39.8 7.9 %collective-permute-done.3 = bf16[16,16,128]{2,1,0:T(8,128)(2,1)S(1)} collective-permute-done((bf16[16,16,128]{2,1,0:T(8,128)(2,1)S(1)}, bf16[16,16,128]{2,1,0:T(8,128)(2,1)S(1)}, u32[]{:S(2)}, u32[]{:S(2)}) %collective-permute-start.3) | collective-permute-done | bytes 65568 | tf_op jit(solution)/shard_map/ppermute | solution.py:146
  47.7 2.3 %collective-permute-done.4 = bf16[16,16,128]{2,1,0:T(8,128)(2,1)S(1)} collective-permute-done((bf16[16,16,128]{2,1,0:T(8,128)(2,1)S(1)}, bf16[16,16,128]{2,1,0:T(8,128)(2,1)S(1)}, u32[]{:S(2)}, u32[]{:S(2)}) %collective-permute-start.4) | collective-permute-done | bytes 65568 | tf_op jit(solution)/shard_map/ppermute | solution.py:146
  50.1 1.3 %collective-permute-start.10 = (bf16[16,16,128]{2,1,0:T(8,128)(2,1)S(1)}, bf16[16,16,128]{2,1,0:T(8,128)(2,1)S(1)}, u32[]{:S(2)}, u32[]{:S(2)}) collective-permute-start(bf16[16,16,128]{2,1,0:T(8,128)(2,1)S(1)} %get-tuple-element.8), channel_id=1, source_target_pairs={{4,0},{8,4},{12,8},{16,12},{20,16},{24,20},{28,24},{5,1},{9,5},{13... | collective-permute-start | bytes 196616 | tf_op jit(solution)/shard_map/ppermute | solution.py:146
  51.4 1.3 %collective-permute-start.11 = (bf16[16,16,128]{2,1,0:T(8,128)(2,1)S(1)}, bf16[16,16,128]{2,1,0:T(8,128)(2,1)S(1)}, u32[]{:S(2)}, u32[]{:S(2)}) collective-permute-start(bf16[16,16,128]{2,1,0:T(8,128)(2,1)S(1)} %get-tuple-element.8), channel_id=1, source_target_pairs={{8,0},{12,4},{16,8},{20,12},{24,16},{28,20},{9,1},{13,5},{17,9},{2... | collective-permute-start | bytes 196616 | tf_op jit(solution)/shard_map/ppermute | solution.py:146
  52.7 1.3 %collective-permute-start.12 = (bf16[16,16,128]{2,1,0:T(8,128)(2,1)S(1)}, bf16[16,16,128]{2,1,0:T(8,128)(2,1)S(1)}, u32[]{:S(2)}, u32[]{:S(2)}) collective-permute-start(bf16[16,16,128]{2,1,0:T(8,128)(2,1)S(1)} %get-tuple-element.8), channel_id=1, source_target_pairs={{12,0},{16,4},{20,8},{24,12},{28,16},{13,1},{17,5},{21,9},{25,13},... | collective-permute-start | bytes 196616 | tf_op jit(solution)/shard_map/ppermute | solution.py:146
  54.0 1.3 %collective-permute-start.13 = (bf16[16,16,128]{2,1,0:T(8,128)(2,1)S(1)}, bf16[16,16,128]{2,1,0:T(8,128)(2,1)S(1)}, u32[]{:S(2)}, u32[]{:S(2)}) collective-permute-start(bf16[16,16,128]{2,1,0:T(8,128)(2,1)S(1)} %get-tuple-element.8), channel_id=1, source_target_pairs={{16,0},{20,4},{24,8},{28,12},{17,1},{21,5},{25,9},{29,13},{18,2},{... | collective-permute-start | bytes 196616 | tf_op jit(solution)/shard_map/ppermute | solution.py:146
  55.3 1.3 %collective-permute-start.14 = (bf16[16,16,128]{2,1,0:T(8,128)(2,1)S(1)}, bf16[16,16,128]{2,1,0:T(8,128)(2,1)S(1)}, u32[]{:S(2)}, u32[]{:S(2)}) collective-permute-start(bf16[16,16,128]{2,1,0:T(8,128)(2,1)S(1)} %get-tuple-element.8), channel_id=1, source_target_pairs={{20,0},{24,4},{28,8},{21,1},{25,5},{29,9},{22,2},{26,6},{30,10},{2... | collective-permute-start | bytes 196616 | tf_op jit(solution)/shard_map/ppermute | solution.py:146
  56.6 2.4 %shard_map.40 = f32[32,2,16,128]{3,2,1,0:T(8,128)S(1)} custom-call(s32[32]{0:T(128)S(1)} %get-tuple-element.34.offsets_ref, s32[1]{0:T(128)} %constant.115.clone.1.base_ref, bf16[144,16,128]{2,1,0:T(8,128)(2,1)S(1)} %constant_dynamic-update-slice_fusion.white_ref), custom_call_target="tpu_custom_call" | custom-call | flops 8388608 | bytes 1114112 | tf_op jit(solution)/shard_map/pallas_call | solution.py:60
  59.0 2.4 %shard_map.39 = f32[32,2,16,128]{3,2,1,0:T(8,128)S(1)} custom-call(s32[32]{0:T(128)S(1)} %get-tuple-element.35.offsets_ref, s32[1]{0:T(128)} %constant.115.clone.1.base_ref, bf16[144,16,128]{2,1,0:T(8,128)(2,1)S(1)} %constant_dynamic-update-slice_fusion.white_ref), custom_call_target="tpu_custom_call" | custom-call | flops 8388608 | bytes 1114112 | tf_op jit(solution)/shard_map/pallas_call | solution.py:60
  61.4 2.4 %shard_map.38 = f32[32,2,16,128]{3,2,1,0:T(8,128)S(1)} custom-call(s32[32]{0:T(128)S(1)} %get-tuple-element.33.offsets_ref, s32[1]{0:T(128)} %constant.115.clone.1.base_ref, bf16[144,16,128]{2,1,0:T(8,128)(2,1)S(1)} %constant_dynamic-update-slice_fusion.white_ref), custom_call_target="tpu_custom_call" | custom-call | flops 8388608 | bytes 1114112 | tf_op jit(solution)/shard_map/pallas_call | solution.py:60
  63.9 2.4 %shard_map.37 = f32[32,2,16,128]{3,2,1,0:T(8,128)S(1)} custom-call(s32[32]{0:T(128)S(1)} %get-tuple-element.32.offsets_ref, s32[1]{0:T(128)} %constant.115.clone.1.base_ref, bf16[144,16,128]{2,1,0:T(8,128)(2,1)S(1)} %constant_dynamic-update-slice_fusion.white_ref), custom_call_target="tpu_custom_call" | custom-call | flops 8388608 | bytes 1114112 | tf_op jit(solution)/shard_map/pallas_call | solution.py:60
  66.6 1.3 %collective-permute-start.15 = (bf16[16,16,128]{2,1,0:T(8,128)(2,1)S(1)}, bf16[16,16,128]{2,1,0:T(8,128)(2,1)S(1)}, u32[]{:S(2)}, u32[]{:S(2)}) collective-permute-start(bf16[16,16,128]{2,1,0:T(8,128)(2,1)S(1)} %get-tuple-element.8), channel_id=1, source_target_pairs={{24,0},{28,4},{25,1},{29,5},{26,2},{30,6},{27,3},{31,7}} | collective-permute-start | bytes 196616 | tf_op jit(solution)/shard_map/ppermute | solution.py:146
  67.9 1.3 %collective-permute-start.16 = (bf16[16,16,128]{2,1,0:T(8,128)(2,1)S(1)}, bf16[16,16,128]{2,1,0:T(8,128)(2,1)S(1)}, u32[]{:S(2)}, u32[]{:S(2)}) collective-permute-start(bf16[16,16,128]{2,1,0:T(8,128)(2,1)S(1)} %get-tuple-element.8), channel_id=1, source_target_pairs={{28,0},{29,1},{30,2},{31,3}} | collective-permute-start | bytes 196616 | tf_op jit(solution)/shard_map/ppermute | solution.py:146
  69.4 0.9 collective-permute-start.8
  70.6 7.3 %collective-permute-done.15 = bf16[16,16,128]{2,1,0:T(8,128)(2,1)S(1)} collective-permute-done((bf16[16,16,128]{2,1,0:T(8,128)(2,1)S(1)}, bf16[16,16,128]{2,1,0:T(8,128)(2,1)S(1)}, u32[]{:S(2)}, u32[]{:S(2)}) %collective-permute-start.15) | collective-permute-done | bytes 65568 | tf_op jit(solution)/shard_map/ppermute | solution.py:146
  77.9 2.0 %collective-permute-done.16 = bf16[16,16,128]{2,1,0:T(8,128)(2,1)S(1)} collective-permute-done((bf16[16,16,128]{2,1,0:T(8,128)(2,1)S(1)}, bf16[16,16,128]{2,1,0:T(8,128)(2,1)S(1)}, u32[]{:S(2)}, u32[]{:S(2)}) %collective-permute-start.16) | collective-permute-done | bytes 65568 | tf_op jit(solution)/shard_map/ppermute | solution.py:146
  79.8 2.4 %shard_map.43 = f32[32,2,16,128]{3,2,1,0:T(8,128)S(1)} custom-call(s32[32]{0:T(128)S(1)} %get-tuple-element.35.offsets_ref, s32[1]{0:T(128)} %constant.115.clone.1.base_ref, bf16[144,16,128]{2,1,0:T(8,128)(2,1)S(1)} %constant_dynamic-update-slice_fusion.9.white_ref), custom_call_target="tpu_custom_call" | custom-call | flops 8388608 | bytes 1114112 | tf_op jit(solution)/shard_map/pallas_call | solution.py:60
  82.3 2.4 %shard_map.42 = f32[32,2,16,128]{3,2,1,0:T(8,128)S(1)} custom-call(s32[32]{0:T(128)S(1)} %get-tuple-element.33.offsets_ref, s32[1]{0:T(128)} %constant.115.clone.1.base_ref, bf16[144,16,128]{2,1,0:T(8,128)(2,1)S(1)} %constant_dynamic-update-slice_fusion.9.white_ref), custom_call_target="tpu_custom_call" | custom-call | flops 8388608 | bytes 1114112 | tf_op jit(solution)/shard_map/pallas_call | solution.py:60
  84.8 0.9 collective-permute-start.18
  85.7 2.4 %shard_map.41 = f32[32,2,16,128]{3,2,1,0:T(8,128)S(1)} custom-call(s32[32]{0:T(128)S(1)} %get-tuple-element.32.offsets_ref, s32[1]{0:T(128)} %constant.115.clone.1.base_ref, bf16[144,16,128]{2,1,0:T(8,128)(2,1)S(1)} %constant_dynamic-update-slice_fusion.9.white_ref), custom_call_target="tpu_custom_call" | custom-call | flops 8388608 | bytes 1114112 | tf_op jit(solution)/shard_map/pallas_call | solution.py:60
  88.1 2.4 %shard_map.44 = f32[32,2,16,128]{3,2,1,0:T(8,128)S(1)} custom-call(s32[32]{0:T(128)S(1)} %get-tuple-element.34.offsets_ref, s32[1]{0:T(128)} %constant.115.clone.1.base_ref, bf16[144,16,128]{2,1,0:T(8,128)(2,1)S(1)} %constant_dynamic-update-slice_fusion.9.white_ref), custom_call_target="tpu_custom_call" | custom-call | flops 8388608 | bytes 1114112 | tf_op jit(solution)/shard_map/pallas_call | solution.py:60
  92.0 1.6 %collective-permute-done.18 = bf16[32,2,16,128]{3,2,1,0:T(8,128)(2,1)S(1)} collective-permute-done((bf16[32,2,16,128]{3,2,1,0:T(8,128)(2,1)S(1)}, bf16[32,2,16,128]{3,2,1,0:T(8,128)(2,1)S(1)}, u32[]{:S(2)}, u32[]{:S(2)}) %collective-permute-start.18) | collective-permute-done | bytes 262176 | tf_op jit(solution)/shard_map/ppermute | solution.py:164
  93.8 2.8 %collective-permute-done.17 = bf16[32,2,16,128]{3,2,1,0:T(8,128)(2,1)S(1)} collective-permute-done((bf16[32,2,16,128]{3,2,1,0:T(8,128)(2,1)S(1)}, bf16[32,2,16,128]{3,2,1,0:T(8,128)(2,1)S(1)}, u32[]{:S(2)}, u32[]{:S(2)}) %collective-permute-start.17) | collective-permute-done | bytes 262176 | tf_op jit(solution)/shard_map/ppermute | solution.py:164
  96.9 1.3 %fusion.15 = bf16[32,16,512]{2,1,0:T(8,128)(2,1)} fusion(f32[32,16,512]{2,1,0:T(8,128)S(1)} %convolution_bitcast_fusion, f32[32,16,512]{2,1,0:T(8,128)S(1)} %convolution_bitcast_fusion.1, f32[32,16,512]{2,1,0:T(8,128)S(1)} %convolution_bitcast_fusion.2, f32[32,16,512]{2,1,0:T(8,128)S(1)} %convolution_bitcast_fusion.3, ...), kind=kOutput, calls=%fused_computation.41 | convolution fusion | flops 137101312 | bytes 10223620 | tf_op jit(solution)/shard_map/opck,pkl->ocl/dot_general | solution.py:167
  (70 shorter events, 7.4 us)
Async XLA Ops:
  0.0 4.0 %copy-start = (s32[1024]{0:T(1024)S(1)}, s32[1024]{0:T(1024)}, u32[]{:S(2)}) copy-start(s32[1024]{0:T(1024)} %param.4) | copy-start | bytes 12292
  17.0 8.9 %all-to-all-start = ((bf16[4,2,8192]{2,1,0:T(2,128)(2,1)}), bf16[4,2,8192]{2,1,0:T(2,128)(2,1)S(1)}, u32[]{:S(2)}, u32[]{:S(2)}) async-start(bf16[4,2,8192]{2,1,0:T(2,128)(2,1)} %reshape.453), calls=%async_computation | async-start | bytes 262144 | tf_op jit(solution)/shard_map/all_to_all | solution.py:127
  24.0 5.5 %copy-start.1 = (s32[128]{0:T(128)S(1)}, s32[128]{0:T(128)}, u32[]{:S(2)}) copy-start(s32[128]{0:T(128)} %param.5) | copy-start | bytes 1540
  28.2 6.6 %collective-permute-start = (bf16[16,16,128]{2,1,0:T(8,128)(2,1)S(1)}, bf16[16,16,128]{2,1,0:T(8,128)(2,1)S(1)}, u32[]{:S(2)}, u32[]{:S(2)}) collective-permute-start(bf16[16,16,128]{2,1,0:T(8,128)(2,1)S(1)} %get-tuple-element.19), channel_id=1, source_target_pairs={{4,0},{8,4},{12,8},{16,12},{20,16},{24,20},{28,24},{5,1},{9,5},{13... | collective-permute-start | bytes 196616 | tf_op jit(solution)/shard_map/ppermute | solution.py:146
  29.6 8.2 %collective-permute-start.1 = (bf16[16,16,128]{2,1,0:T(8,128)(2,1)S(1)}, bf16[16,16,128]{2,1,0:T(8,128)(2,1)S(1)}, u32[]{:S(2)}, u32[]{:S(2)}) collective-permute-start(bf16[16,16,128]{2,1,0:T(8,128)(2,1)S(1)} %get-tuple-element.19), channel_id=1, source_target_pairs={{8,0},{12,4},{16,8},{20,12},{24,16},{28,20},{9,1},{13,5},{17,9},{2... | collective-permute-start | bytes 196616 | tf_op jit(solution)/shard_map/ppermute | solution.py:146
  30.8 8.9 %collective-permute-start.2 = (bf16[16,16,128]{2,1,0:T(8,128)(2,1)S(1)}, bf16[16,16,128]{2,1,0:T(8,128)(2,1)S(1)}, u32[]{:S(2)}, u32[]{:S(2)}) collective-permute-start(bf16[16,16,128]{2,1,0:T(8,128)(2,1)S(1)} %get-tuple-element.19), channel_id=1, source_target_pairs={{12,0},{16,4},{20,8},{24,12},{28,16},{13,1},{17,5},{21,9},{25,13},... | collective-permute-start | bytes 196616 | tf_op jit(solution)/shard_map/ppermute | solution.py:146
  32.1 15.5 %collective-permute-start.3 = (bf16[16,16,128]{2,1,0:T(8,128)(2,1)S(1)}, bf16[16,16,128]{2,1,0:T(8,128)(2,1)S(1)}, u32[]{:S(2)}, u32[]{:S(2)}) collective-permute-start(bf16[16,16,128]{2,1,0:T(8,128)(2,1)S(1)} %get-tuple-element.19), channel_id=1, source_target_pairs={{16,0},{20,4},{24,8},{28,12},{17,1},{21,5},{25,9},{29,13},{18,2},{... | collective-permute-start | bytes 196616 | tf_op jit(solution)/shard_map/ppermute | solution.py:146
  33.4 16.6 %collective-permute-start.4 = (bf16[16,16,128]{2,1,0:T(8,128)(2,1)S(1)}, bf16[16,16,128]{2,1,0:T(8,128)(2,1)S(1)}, u32[]{:S(2)}, u32[]{:S(2)}) collective-permute-start(bf16[16,16,128]{2,1,0:T(8,128)(2,1)S(1)} %get-tuple-element.19), channel_id=1, source_target_pairs={{20,0},{24,4},{28,8},{21,1},{25,5},{29,9},{22,2},{26,6},{30,10},{2... | collective-permute-start | bytes 196616 | tf_op jit(solution)/shard_map/ppermute | solution.py:146
  34.8 15.3 %collective-permute-start.5 = (bf16[16,16,128]{2,1,0:T(8,128)(2,1)S(1)}, bf16[16,16,128]{2,1,0:T(8,128)(2,1)S(1)}, u32[]{:S(2)}, u32[]{:S(2)}) collective-permute-start(bf16[16,16,128]{2,1,0:T(8,128)(2,1)S(1)} %get-tuple-element.19), channel_id=1, source_target_pairs={{24,0},{28,4},{25,1},{29,5},{26,2},{30,6},{27,3},{31,7}} | collective-permute-start | bytes 196616 | tf_op jit(solution)/shard_map/ppermute | solution.py:146
  37.8 12.3 %collective-permute-start.6 = (bf16[16,16,128]{2,1,0:T(8,128)(2,1)S(1)}, bf16[16,16,128]{2,1,0:T(8,128)(2,1)S(1)}, u32[]{:S(2)}, u32[]{:S(2)}) collective-permute-start(bf16[16,16,128]{2,1,0:T(8,128)(2,1)S(1)} %get-tuple-element.19), channel_id=1, source_target_pairs={{28,0},{29,1},{30,2},{31,3}} | collective-permute-start | bytes 196616 | tf_op jit(solution)/shard_map/ppermute | solution.py:146
  50.1 16.5 %collective-permute-start.10 = (bf16[16,16,128]{2,1,0:T(8,128)(2,1)S(1)}, bf16[16,16,128]{2,1,0:T(8,128)(2,1)S(1)}, u32[]{:S(2)}, u32[]{:S(2)}) collective-permute-start(bf16[16,16,128]{2,1,0:T(8,128)(2,1)S(1)} %get-tuple-element.8), channel_id=1, source_target_pairs={{4,0},{8,4},{12,8},{16,12},{20,16},{24,20},{28,24},{5,1},{9,5},{13... | collective-permute-start | bytes 196616 | tf_op jit(solution)/shard_map/ppermute | solution.py:146
  51.4 16.5 %collective-permute-start.11 = (bf16[16,16,128]{2,1,0:T(8,128)(2,1)S(1)}, bf16[16,16,128]{2,1,0:T(8,128)(2,1)S(1)}, u32[]{:S(2)}, u32[]{:S(2)}) collective-permute-start(bf16[16,16,128]{2,1,0:T(8,128)(2,1)S(1)} %get-tuple-element.8), channel_id=1, source_target_pairs={{8,0},{12,4},{16,8},{20,12},{24,16},{28,20},{9,1},{13,5},{17,9},{2... | collective-permute-start | bytes 196616 | tf_op jit(solution)/shard_map/ppermute | solution.py:146
  52.7 16.6 %collective-permute-start.12 = (bf16[16,16,128]{2,1,0:T(8,128)(2,1)S(1)}, bf16[16,16,128]{2,1,0:T(8,128)(2,1)S(1)}, u32[]{:S(2)}, u32[]{:S(2)}) collective-permute-start(bf16[16,16,128]{2,1,0:T(8,128)(2,1)S(1)} %get-tuple-element.8), channel_id=1, source_target_pairs={{12,0},{16,4},{20,8},{24,12},{28,16},{13,1},{17,5},{21,9},{25,13},... | collective-permute-start | bytes 196616 | tf_op jit(solution)/shard_map/ppermute | solution.py:146
  54.0 15.4 %collective-permute-start.13 = (bf16[16,16,128]{2,1,0:T(8,128)(2,1)S(1)}, bf16[16,16,128]{2,1,0:T(8,128)(2,1)S(1)}, u32[]{:S(2)}, u32[]{:S(2)}) collective-permute-start(bf16[16,16,128]{2,1,0:T(8,128)(2,1)S(1)} %get-tuple-element.8), channel_id=1, source_target_pairs={{16,0},{20,4},{24,8},{28,12},{17,1},{21,5},{25,9},{29,13},{18,2},{... | collective-permute-start | bytes 196616 | tf_op jit(solution)/shard_map/ppermute | solution.py:146
  55.3 15.0 %collective-permute-start.14 = (bf16[16,16,128]{2,1,0:T(8,128)(2,1)S(1)}, bf16[16,16,128]{2,1,0:T(8,128)(2,1)S(1)}, u32[]{:S(2)}, u32[]{:S(2)}) collective-permute-start(bf16[16,16,128]{2,1,0:T(8,128)(2,1)S(1)} %get-tuple-element.8), channel_id=1, source_target_pairs={{20,0},{24,4},{28,8},{21,1},{25,5},{29,9},{22,2},{26,6},{30,10},{2... | collective-permute-start | bytes 196616 | tf_op jit(solution)/shard_map/ppermute | solution.py:146
  66.6 11.2 %collective-permute-start.15 = (bf16[16,16,128]{2,1,0:T(8,128)(2,1)S(1)}, bf16[16,16,128]{2,1,0:T(8,128)(2,1)S(1)}, u32[]{:S(2)}, u32[]{:S(2)}) collective-permute-start(bf16[16,16,128]{2,1,0:T(8,128)(2,1)S(1)} %get-tuple-element.8), channel_id=1, source_target_pairs={{24,0},{28,4},{25,1},{29,5},{26,2},{30,6},{27,3},{31,7}} | collective-permute-start | bytes 196616 | tf_op jit(solution)/shard_map/ppermute | solution.py:146
  67.9 11.9 %collective-permute-start.16 = (bf16[16,16,128]{2,1,0:T(8,128)(2,1)S(1)}, bf16[16,16,128]{2,1,0:T(8,128)(2,1)S(1)}, u32[]{:S(2)}, u32[]{:S(2)}) collective-permute-start(bf16[16,16,128]{2,1,0:T(8,128)(2,1)S(1)} %get-tuple-element.8), channel_id=1, source_target_pairs={{28,0},{29,1},{30,2},{31,3}} | collective-permute-start | bytes 196616 | tf_op jit(solution)/shard_map/ppermute | solution.py:146
  69.3 21.5 %collective-permute-start.9 = (bf16[32,2,16,128]{3,2,1,0:T(8,128)(2,1)S(1)}, bf16[32,2,16,128]{3,2,1,0:T(8,128)(2,1)S(1)}, u32[]{:S(2)}, u32[]{:S(2)}) collective-permute-start(bf16[32,2,16,128]{3,2,1,0:T(8,128)(2,1)S(1)} %convert_element_type.91), channel_id=1, source_target_pairs={{0,3},{1,0},{2,1},{3,2},{4,7},{5,4},{6,5},{7,6},{8,11},{9,8},{10,9... | collective-permute-start | bytes 786440 | tf_op jit(solution)/shard_map/ppermute | solution.py:164
  69.4 22.0 %collective-permute-start.8 = (bf16[32,2,16,128]{3,2,1,0:T(8,128)(2,1)S(1)}, bf16[32,2,16,128]{3,2,1,0:T(8,128)(2,1)S(1)}, u32[]{:S(2)}, u32[]{:S(2)}) collective-permute-start(bf16[32,2,16,128]{3,2,1,0:T(8,128)(2,1)S(1)} %convert_element_type.90), channel_id=1, source_target_pairs={{0,2},{1,3},{2,0},{3,1},{4,6},{5,7},{6,4},{7,5},{8,10},{9,11},{10,... | collective-permute-start | bytes 786440 | tf_op jit(solution)/shard_map/ppermute | solution.py:164
  70.3 26.6 %collective-permute-start.7 = (bf16[32,2,16,128]{3,2,1,0:T(8,128)(2,1)S(1)}, bf16[32,2,16,128]{3,2,1,0:T(8,128)(2,1)S(1)}, u32[]{:S(2)}, u32[]{:S(2)}) collective-permute-start(bf16[32,2,16,128]{3,2,1,0:T(8,128)(2,1)S(1)} %convert_element_type.87), channel_id=1, source_target_pairs={{0,1},{1,2},{2,3},{3,0},{4,5},{5,6},{6,7},{7,4},{8,9},{9,10},{10,1... | collective-permute-start | bytes 786440 | tf_op jit(solution)/shard_map/ppermute | solution.py:164
  82.3 9.4 %collective-permute-start.19 = (bf16[32,2,16,128]{3,2,1,0:T(8,128)(2,1)S(1)}, bf16[32,2,16,128]{3,2,1,0:T(8,128)(2,1)S(1)}, u32[]{:S(2)}, u32[]{:S(2)}) collective-permute-start(bf16[32,2,16,128]{3,2,1,0:T(8,128)(2,1)S(1)} %convert_element_type.95), channel_id=1, source_target_pairs={{0,3},{1,0},{2,1},{3,2},{4,7},{5,4},{6,5},{7,6},{8,11},{9,8},{10,9... | collective-permute-start | bytes 786440 | tf_op jit(solution)/shard_map/ppermute | solution.py:164
  84.8 8.8 %collective-permute-start.18 = (bf16[32,2,16,128]{3,2,1,0:T(8,128)(2,1)S(1)}, bf16[32,2,16,128]{3,2,1,0:T(8,128)(2,1)S(1)}, u32[]{:S(2)}, u32[]{:S(2)}) collective-permute-start(bf16[32,2,16,128]{3,2,1,0:T(8,128)(2,1)S(1)} %convert_element_type.94), channel_id=1, source_target_pairs={{0,2},{1,3},{2,0},{3,1},{4,6},{5,7},{6,4},{7,5},{8,10},{9,11},{10,... | collective-permute-start | bytes 786440 | tf_op jit(solution)/shard_map/ppermute | solution.py:164
  90.8 5.8 %collective-permute-start.17 = (bf16[32,2,16,128]{3,2,1,0:T(8,128)(2,1)S(1)}, bf16[32,2,16,128]{3,2,1,0:T(8,128)(2,1)S(1)}, u32[]{:S(2)}, u32[]{:S(2)}) collective-permute-start(bf16[32,2,16,128]{3,2,1,0:T(8,128)(2,1)S(1)} %convert_element_type.93), channel_id=1, source_target_pairs={{0,1},{1,2},{2,3},{3,0},{4,5},{5,6},{6,7},{7,4},{8,9},{9,10},{10,1... | collective-permute-start | bytes 786440 | tf_op jit(solution)/shard_map/ppermute | solution.py:164

commit v12 on v10

--- a/solution.py
+++ b/solution.py
@@ -34,45 +34,70 @@
     return (spectra * lax.rsqrt(mean_power + 1e-06)).astype(jnp.bfloat16)
 
 
-def cross_kernel(offsets_ref, base_ref, white_ref, out_ref, *, group, own_count, half):
+def cross_kernel(offsets_ref, white_ref, *rest, group, own_count, half, first_row, end_row):
+    if len(rest) == 2:
+        earlier_ref, out_ref = rest
+    else:
+        earlier_ref, (out_ref,) = None, rest
     step = pl.program_id(0)
-    base = base_ref[0]
-    own = [white_ref[base + c].astype(jnp.float32) for c in range(own_count)]
+    own = [white_ref[c].astype(jnp.float32) for c in range(own_count)]
 
     def one_offset(i, carry):
         shift = offsets_ref[step * group + i]
-        for c in range(own_count):
-            a = own[c]
-            b = white_ref[base + c + shift].astype(jnp.float32)
-            ar, ai, br, bi = a[:half], a[half:], b[:half], b[half:]
-            out_ref[i, 0, pl.ds(c, 1), :] = jnp.sum(ar * br + ai * bi, axis=0, keepdims=True)
-            out_ref[i, 1, pl.ds(c, 1), :] = jnp.sum(ai * br - ar * bi, axis=0, keepdims=True)
+        meets = jnp.logical_and(shift + own_count > first_row, shift < end_row)
+
+        @pl.when(meets)
+        def _():
+            for c in range(own_count):
+                a = own[c]
+                b = white_ref[c + shift].astype(jnp.float32)
+                ar, ai, br, bi = a[:half], a[half:], b[:half], b[half:]
+                real_part = jnp.sum(ar * br + ai * bi, axis=0, keepdims=True)
+                imag_part = jnp.sum(ai * br - ar * bi, axis=0, keepdims=True)
+                if earlier_ref is not None:
+                    real_part = real_part + earlier_ref[i, 0, pl.ds(c, 1), :]
+                    imag_part = imag_part + earlier_ref[i, 1, pl.ds(c, 1), :]
+                out_ref[i, 0, pl.ds(c, 1), :] = real_part
+                out_ref[i, 1, pl.ds(c, 1), :] = imag_part
+
+        @pl.when(jnp.logical_not(meets))
+        def _():
+            if earlier_ref is None:
+                out_ref[i] = jnp.zeros(out_ref.shape[1:], out_ref.dtype)
+            else:
+                out_ref[i] = earlier_ref[i]
+
         return carry
 
     lax.fori_loop(0, group, one_offset, 0)
 
 
-def cross_spectra(white_all, pair_offsets, base, own_count):
+def cross_spectra(white_all, pair_offsets, own_count, first_row, end_row, earlier=None):
     rows, bins = white_all.shape[1], white_all.shape[2]
     band_span = pair_offsets.shape[0]
     group = math.gcd(band_span, 8)
-    kernel = functools.partial(cross_kernel, group=group, own_count=own_count, half=rows // 2)
+    kernel = functools.partial(
+        cross_kernel, group=group, own_count=own_count, half=rows // 2, first_row=first_row, end_row=end_row
+    )
+    block = pl.BlockSpec((group, 2, own_count, bins), lambda g, offs: (g, 0, 0, 0))
+    operands = [pair_offsets, white_all] + ([] if earlier is None else [earlier])
     return pl.pallas_call(
         kernel,
         grid_spec=pltpu.PrefetchScalarGridSpec(
-            num_scalar_prefetch=2,
+            num_scalar_prefetch=1,
             grid=(band_span // group,),
-            in_specs=[pl.BlockSpec(white_all.shape, lambda g, offs, b: (0, 0, 0))],
-            out_specs=pl.BlockSpec((group, 2, own_count, bins), lambda g, offs, b: (g, 0, 0, 0)),
+            in_specs=[pl.BlockSpec(white_all.shape, lambda g, offs: (0, 0, 0))]
+            + ([] if earlier is None else [block]),
+            out_specs=block,
         ),
         out_shape=jax.ShapeDtypeStruct((band_span, 2, own_count, bins), jnp.float32),
         compiler_params=pltpu.CompilerParams(vmem_limit_bytes=48 * 1024 * 1024),
         cost_estimate=pl.CostEstimate(
-            flops=8 * band_span * own_count * rows * bins,
+            flops=1024 * band_span * own_count * rows * bins,
             transcendentals=0,
-            bytes_accessed=white_all.size * 2 + band_span * 2 * own_count * bins * 4,
+            bytes_accessed=white_all.size * 2 + band_span * 2 * own_count * bins * 8,
         ),
-    )(pair_offsets, base, white_all)
+    )(*operands)
 
 
 def small_table(kept_bins, rows):
@@ -130,27 +155,35 @@
     rows_white = jnp.transpose(freq_white, (1, 2, 0, 3)).reshape(ch_dev, 2 * windows, shard_bins)
     gx_count = lax.axis_size("gx")
     needed = -(-band_span // ch_dev)
+    real_count = min(needed, gx_count - 1) + 1
+    near_count = min(4, real_count)
     blocks = [rows_white]
-    for shift in range(1, min(needed, gx_count - 1) + 1):
+    source = rows_white
+    for shift in range(1, real_count):
+        if shift == near_count:
+            source, _ = lax.optimization_barrier((rows_white, blocks))
         pairs = [(src, src - shift) for src in range(shift, gx_count)]
-        blocks.append(lax.ppermute(rows_white, "gx", perm=pairs))
-    missing = needed + 1 - len(blocks)
-    if missing > 0:
-        blocks.append(jnp.zeros((missing * ch_dev,) + rows_white.shape[1:], rows_white.dtype))
-    padded = jnp.concatenate(blocks, axis=0)
-    base = jnp.zeros((1,), jnp.int32)
+        blocks.append(lax.ppermute(source, "gx", perm=pairs))
+    zero_block = jnp.zeros_like(rows_white)
+    blocks += [zero_block] * (needed + 1 - len(blocks))
+    near = jnp.concatenate(blocks[:near_count] + [zero_block] * (len(blocks) - near_count), axis=0)
+    far = jnp.concatenate([rows_white] + [zero_block] * (near_count - 1) + blocks[near_count:], axis=0)
+    split_row = near_count * ch_dev
+    end_row = len(blocks) * ch_dev
     gy_count = lax.axis_size("gy")
     off_dev = band_span // gy_count
     me = lax.axis_index("gy")
     offsets = pair_offsets.astype(jnp.int32)
     inverse = inverse_table(kept_bins)
     norm_scale = 0.5 / math.sqrt(windows * bin_count)
+    shifts = list(range(1, gy_count)) + [0]
+    dest_offsets = [
+        lax.dynamic_slice_in_dim(offsets, lax.rem(me + shift, gy_count) * off_dev, off_dev) for shift in shifts
+    ]
+    near_parts = [cross_spectra(near, offs, ch_dev, 0, split_row) for offs in dest_offsets]
     lagged = None
-    for shift in list(range(1, gy_count)) + [0]:
-        dest = lax.rem(me + shift, gy_count)
-        part = cross_spectra(
-            padded, lax.dynamic_slice_in_dim(offsets, dest * off_dev, off_dev), base, ch_dev
-        ).astype(jnp.bfloat16)
+    for shift, offs, near_part in zip(shifts, dest_offsets, near_parts):
+        part = cross_spectra(far, offs, ch_dev, split_row, end_row, near_part).astype(jnp.bfloat16)
         if shift:
             pairs = [(src, (src + shift) % gy_count) for src in range(gy_count)]
             part = lax.ppermute(part, "gy", perm=pairs)

time: 91.6 us -> 97.8 us (1.068)
  Pallas kernels: 18.5 us -> 26.8 us
  other arithmetic: 12.4 us -> 9.87 us
  matrix products: 7.11 us -> 5.03 us
  starting transfers between devices: 14.2 us -> 15.8 us
  waiting for transfers between devices: 26.5 us -> 27.8 us
    ppermute x3, waiting for transfers between devices: 0.31 us -> 9.28 us  [local(): part = lax.ppermute(part, 'gy', perm=pairs)]
    pallas_call x4 -> x8, Pallas kernels: 18.5 us -> 26.8 us  [cross_spectra(): pl.pallas_call(kernel, grid_spec=pltpu.PrefetchScalarGridSpec(num_scalar_...]
    ppermute x7, waiting for transfers between devices: 22.2 us -> 16.7 us  [local(): blocks.append(lax.ppermute(source, 'gx', perm=pairs))]
    all_to_all x1, waiting for transfers between devices: 4.02 us -> 1.76 us  [local(): lax.all_to_all(white, 'gy', split_axis=3, concat_axis=0, tiled=True)]
    dot_general x4, matrix products: 4.66 us -> 2.57 us  [local(): jnp.einsum('opck,pkl->ocl', part, rows, preferred_element_type=jnp.float32)]
    convert_element_type x3, other arithmetic: 1.86 us -> 0.23 us  [local(): cross_spectra(far, offs, ch_dev, split_row, end_row, near_part)]
    ppermute x3, starting transfers between devices: 0.93 us -> 2.54 us  [local(): part = lax.ppermute(part, 'gy', perm=pairs)]
    unnamed x14 -> x16, local copies, waits for them, and re-layouts: 2.6 us -> 2.7 us
  transfers between devices with their start and end apart: 11 -> 11, of which waited for: 7 -> 7; matrix products, arithmetic and copies ran while one was open for 10% -> 5% of each run, Pallas kernels for 15% -> 24%
where the time goes in v12:
time: 97.8 us; the launch traced here: 96.4 us
  waiting for transfers between devices  27.8 us (28%)
  Pallas kernels  26.8 us (27%)
  starting transfers between devices  15.8 us (16%)
  local copies, waits for them, and re-layouts  10.6 us (11%)
  other arithmetic  9.87 us (10%)
  matrix products  5.03 us (5%)
    pallas_call x8, Pallas kernels, cross_spectra(): pl.pallas_call(kernel, grid_spec=pltpu.PrefetchScalarGridSpec(num_scalar_...  26.8 us
    ppermute x7, waiting for transfers between devices, local(): blocks.append(lax.ppermute(source, 'gx', perm=pairs))  16.7 us
    ppermute x3, waiting for transfers between devices, local(): part = lax.ppermute(part, 'gy', perm=pairs)  9.28 us
    ppermute x7, starting transfers between devices, local(): blocks.append(lax.ppermute(source, 'gx', perm=pairs))  9.03 us
    another operation x2, other arithmetic  4.39 us
    all_to_all x1, starting transfers between devices, local(): lax.all_to_all(white, 'gy', split_axis=3, concat_axis=0, tiled=True)  4.21 us
    unnamed x16, local copies, waits for them, and re-layouts  2.7 us
    dot_general x4, matrix products, local(): jnp.einsum('opck,pkl->ocl', part, rows, preferred_element_type=jnp.float32)  2.57 us
  transfers between devices with their start and end apart: 11, of which 7 were waited for; matrix products, arithmetic and copies ran while one was open for 5% of the time, Pallas kernels for 24%

profile of v12, /device:TPU:0, one launch (start us, length us, event | category | flops | bytes accessed | tf_op | source)
XLA Modules:
  0.0 96.4 jit_solution(882063477949314104)
XLA Ops:
  0.0 1.2 %fusion.52 = (f32[32,1024]{1,0:T(8,128)S(1)}, f32[32,1024]{1,0:T(8,128)S(1)}) fusion(s32[1024]{0:T(1024)} %param.4), kind=kLoop, calls=%fused_computation.88 | loop fusion | flops 458752 | bytes 266240 | tf_op jit(solution)/shard_map/cos | solution.py:115
  1.2 0.7 add_select_fusion.5
  1.9 1.8 %fusion.41 = (f32[64,1024]{1,0:T(8,128)S(1)}, f32[64,1024]{1,0:T(8,128)S(1)}) fusion(s32[1024]{0:T(1024)} %param.4, s32[64]{0:T(128)S(1)} %iota_multiply_fusion), kind=kLoop, calls=%fused_computation.71 | loop fusion | flops 917504 | bytes 528640 | tf_op jit(solution)/shard_map/cos | solution.py:115
  3.7 1.3 %copy.29 = bf16[2,16,8192]{2,1,0:T(8,128)(2,1)S(1)} copy(bf16[2,16,8192]{2,0,1:T(2,128)(2,1)} %bitcast.88) | data formatting | bytes 1048576 | tf_op jit(solution)/shard_map/transpose | solution.py:149
  5.0 0.4 reshape_reshape.3
  5.4 0.3 copy.30
  5.7 3.7 %subtract_convert_fusion = (bf16[64,32,1024]{2,1,0:T(8,128)(2,1)S(1)}, bf16[64,32,1024]{2,1,0:T(8,128)(2,1)S(1)}) fusion(f32[64,1024]{1,0:T(8,128)S(1)} %get-tuple-element.18, f32[32,1024]{1,0:T(8,128)S(1)} %get-tuple-element.24, f32[64,1024]{1,0:T(8,128)S(1)} %get-tuple-element.17, f32[32,1024]{1,0:T(8,128)S(1)} %get-tuple-element.23), kind=kLoop, calls=%fused_computation.5 | loop fusion | flops 18874368 | bytes 9175040 | tf_op jit(solution)/shard_map/convert.7
  9.4 2.5 %fusion.4 = f32[128,2048]{0,1:T(8,128)S(1)} fusion(bf16[128,2048]{1,0:T(8,128)(2,1)S(1)} %bitcast.89, bf16[2048,1024]{1,0:T(8,128)(2,1)S(1)} %bitcast.81, bf16[2048,1024]{1,0:T(8,128)(2,1)S(1)} %bitcast.80), kind=kOutput, calls=%fused_computation.14 | convolution fusion | flops 1090519040 | bytes 9961472 | tf_op jit(solution)/shard_map/dot_general | solution.py:128
  11.9 0.3 copy.31
  12.2 0.9 reshape.435
  13.1 0.8 fusion.68
  14.9 0.8 copy.33
  15.8 1.7 %reshape.445 = bf16[4,2,8192]{2,1,0:T(2,128)(2,1)} reshape(bf16[1024,2,2,16]{3,2,1,0:T(2,128)(2,1)S(1)} %bitcast.78) | data formatting | bytes 262144
  17.5 4.2 %all-to-all-start = ((bf16[4,2,8192]{2,1,0:T(2,128)(2,1)}), bf16[4,2,8192]{2,1,0:T(2,128)(2,1)S(1)}, u32[]{:S(2)}, u32[]{:S(2)}) async-start(bf16[4,2,8192]{2,1,0:T(2,128)(2,1)} %reshape.445), calls=%async_computation | async-start | bytes 262144 | tf_op jit(solution)/shard_map/all_to_all | solution.py:152
  21.7 0.5 fusion.50
  22.3 0.3 fusion.54
  22.6 0.7 negate_convert_fusion.1
  23.4 0.5 copy.37
  23.9 0.5 copy.38
  24.6 1.8 %all-to-all-done = bf16[4,2,8192]{2,1,0:T(2,128)(2,1)S(1)} async-done(((bf16[4,2,8192]{2,1,0:T(2,128)(2,1)}), bf16[4,2,8192]{2,1,0:T(2,128)(2,1)S(1)}, u32[]{:S(2)}, u32[]{:S(2)}) %all-to-all-start) | async-done | bytes 131104 | tf_op jit(solution)/shard_map/all_to_all | solution.py:152
  26.4 0.7 reshape.446
  27.1 1.4 %copy.43 = bf16[2,16,2,4,256]{4,3,1,2,0:T(4,128)(2,1)S(1)} copy(bf16[2,16,2,4,256]{1,2,0,4,3:T(2,128)(2,1)S(1)} %bitcast.79) | data formatting | bytes 262144 | tf_op jit(solution)/shard_map/all_to_all | solution.py:152
  28.6 1.3 %collective-permute-start = (bf16[16,16,256]{2,1,0:T(8,128)(2,1)S(1)}, bf16[16,16,256]{2,1,0:T(8,128)(2,1)S(1)}, u32[]{:S(2)}, u32[]{:S(2)}) collective-permute-start(bf16[16,16,256]{2,1,0:T(8,128)(2,1)S(1)} %bitcast.90), channel_id=1, source_target_pairs={{4,0},{8,4},{12,8},{16,12},{20,16},{24,20},{28,24},{5,1},{9,5},{13... | collective-permute-start | bytes 393224 | tf_op jit(solution)/shard_map/ppermute | solution.py:166
  29.9 1.3 %collective-permute-start.1 = (bf16[16,16,256]{2,1,0:T(8,128)(2,1)S(1)}, bf16[16,16,256]{2,1,0:T(8,128)(2,1)S(1)}, u32[]{:S(2)}, u32[]{:S(2)}) collective-permute-start(bf16[16,16,256]{2,1,0:T(8,128)(2,1)S(1)} %bitcast.91), channel_id=1, source_target_pairs={{8,0},{12,4},{16,8},{20,12},{24,16},{28,20},{9,1},{13,5},{17,9},{2... | collective-permute-start | bytes 393224 | tf_op jit(solution)/shard_map/ppermute | solution.py:166
  31.2 1.3 %collective-permute-start.2 = (bf16[16,16,256]{2,1,0:T(8,128)(2,1)S(1)}, bf16[16,16,256]{2,1,0:T(8,128)(2,1)S(1)}, u32[]{:S(2)}, u32[]{:S(2)}) collective-permute-start(bf16[16,16,256]{2,1,0:T(8,128)(2,1)S(1)} %bitcast.92), channel_id=1, source_target_pairs={{12,0},{16,4},{20,8},{24,12},{28,16},{13,1},{17,5},{21,9},{25,13},... | collective-permute-start | bytes 393224 | tf_op jit(solution)/shard_map/ppermute | solution.py:166
  32.7 2.9 %collective-permute-done = bf16[16,16,256]{2,1,0:T(8,128)(2,1)S(1)} collective-permute-done((bf16[16,16,256]{2,1,0:T(8,128)(2,1)S(1)}, bf16[16,16,256]{2,1,0:T(8,128)(2,1)S(1)}, u32[]{:S(2)}, u32[]{:S(2)}) %collective-permute-start) | collective-permute-done | bytes 131104 | tf_op jit(solution)/shard_map/ppermute | solution.py:166
  35.6 4.1 %collective-permute-done.1 = bf16[16,16,256]{2,1,0:T(8,128)(2,1)S(1)} collective-permute-done((bf16[16,16,256]{2,1,0:T(8,128)(2,1)S(1)}, bf16[16,16,256]{2,1,0:T(8,128)(2,1)S(1)}, u32[]{:S(2)}, u32[]{:S(2)}) %collective-permute-start.1) | collective-permute-done | bytes 131104 | tf_op jit(solution)/shard_map/ppermute | solution.py:166
  39.7 2.0 %collective-permute-done.2 = bf16[16,16,256]{2,1,0:T(8,128)(2,1)S(1)} collective-permute-done((bf16[16,16,256]{2,1,0:T(8,128)(2,1)S(1)}, bf16[16,16,256]{2,1,0:T(8,128)(2,1)S(1)}, u32[]{:S(2)}, u32[]{:S(2)}) %collective-permute-start.2) | collective-permute-done | bytes 131104 | tf_op jit(solution)/shard_map/ppermute | solution.py:166
  41.7 1.3 %collective-permute-start.3 = (bf16[16,16,256]{2,1,0:T(8,128)(2,1)S(1)}, bf16[16,16,256]{2,1,0:T(8,128)(2,1)S(1)}, u32[]{:S(2)}, u32[]{:S(2)}) collective-permute-start(bf16[16,16,256]{2,1,0:T(8,128)(2,1)S(1)} %bitcast.93), channel_id=1, source_target_pairs={{16,0},{20,4},{24,8},{28,12},{17,1},{21,5},{25,9},{29,13},{18,2},{... | collective-permute-start | bytes 393224 | tf_op jit(solution)/shard_map/ppermute | solution.py:166
  43.0 1.3 %collective-permute-start.4 = (bf16[16,16,256]{2,1,0:T(8,128)(2,1)S(1)}, bf16[16,16,256]{2,1,0:T(8,128)(2,1)S(1)}, u32[]{:S(2)}, u32[]{:S(2)}) collective-permute-start(bf16[16,16,256]{2,1,0:T(8,128)(2,1)S(1)} %bitcast.94), channel_id=1, source_target_pairs={{20,0},{24,4},{28,8},{21,1},{25,5},{29,9},{22,2},{26,6},{30,10},{2... | collective-permute-start | bytes 393224 | tf_op jit(solution)/shard_map/ppermute | solution.py:166
  44.3 1.3 %collective-permute-start.5 = (bf16[16,16,256]{2,1,0:T(8,128)(2,1)S(1)}, bf16[16,16,256]{2,1,0:T(8,128)(2,1)S(1)}, u32[]{:S(2)}, u32[]{:S(2)}) collective-permute-start(bf16[16,16,256]{2,1,0:T(8,128)(2,1)S(1)} %bitcast.95), channel_id=1, source_target_pairs={{24,0},{28,4},{25,1},{29,5},{26,2},{30,6},{27,3},{31,7}} | collective-permute-start | bytes 393224 | tf_op jit(solution)/shard_map/ppermute | solution.py:166
  45.6 1.3 %collective-permute-start.6 = (bf16[16,16,256]{2,1,0:T(8,128)(2,1)S(1)}, bf16[16,16,256]{2,1,0:T(8,128)(2,1)S(1)}, u32[]{:S(2)}, u32[]{:S(2)}) collective-permute-start(bf16[16,16,256]{2,1,0:T(8,128)(2,1)S(1)} %bitcast.96), channel_id=1, source_target_pairs={{28,0},{29,1},{30,2},{31,3}} | collective-permute-start | bytes 393224 | tf_op jit(solution)/shard_map/ppermute | solution.py:166
  47.0 2.6 %shard_map.37.rest_0_ = f32[32,2,16,256]{3,2,1,0:T(8,128)S(1)} custom-call(s32[32]{0:T(128)S(1)} %get-tuple-element.27.offsets_ref, bf16[144,16,256]{2,1,0:T(8,128)(2,1)S(1)} %broadcast_dynamic-update-slice_fusion.white_ref), custom_call_target="tpu_custom_call" | custom-call | flops 2147483648 | bytes 3276800 | tf_op jit(solution)/shard_map/pallas_call | solution.py:84
  49.6 2.8 %shard_map.39.rest_0_ = f32[32,2,16,256]{3,2,1,0:T(8,128)S(1)} custom-call(s32[32]{0:T(128)S(1)} %get-tuple-element.28.offsets_ref, bf16[144,16,256]{2,1,0:T(8,128)(2,1)S(1)} %broadcast_dynamic-update-slice_fusion.white_ref), custom_call_target="tpu_custom_call" | custom-call | flops 2147483648 | bytes 3276800 | tf_op jit(solution)/shard_map/pallas_call | solution.py:84
  52.4 3.3 %shard_map.41.rest_0_ = f32[32,2,16,256]{3,2,1,0:T(8,128)S(1)} custom-call(s32[32]{0:T(128)S(1)} %get-tuple-element.30.offsets_ref, bf16[144,16,256]{2,1,0:T(8,128)(2,1)S(1)} %broadcast_dynamic-update-slice_fusion.white_ref), custom_call_target="tpu_custom_call" | custom-call | flops 2147483648 | bytes 3276800 | tf_op jit(solution)/shard_map/pallas_call | solution.py:84
  55.6 3.4 %shard_map.43.rest_0_ = f32[32,2,16,256]{3,2,1,0:T(8,128)S(1)} custom-call(s32[32]{0:T(128)S(1)} %get-tuple-element.29.offsets_ref, bf16[144,16,256]{2,1,0:T(8,128)(2,1)S(1)} %broadcast_dynamic-update-slice_fusion.white_ref), custom_call_target="tpu_custom_call" | custom-call | flops 2147483648 | bytes 3276800 | tf_op jit(solution)/shard_map/pallas_call | solution.py:84
  59.0 7.7 %collective-permute-done.4 = bf16[16,16,256]{2,1,0:T(8,128)(2,1)S(1)} collective-permute-done((bf16[16,16,256]{2,1,0:T(8,128)(2,1)S(1)}, bf16[16,16,256]{2,1,0:T(8,128)(2,1)S(1)}, u32[]{:S(2)}, u32[]{:S(2)}) %collective-permute-start.4) | collective-permute-done | bytes 131104 | tf_op jit(solution)/shard_map/ppermute | solution.py:166
  66.8 4.1 %shard_map.38 = f32[32,2,16,256]{3,2,1,0:T(8,128)S(1)} custom-call(s32[32]{0:T(128)S(1)} %get-tuple-element.27.offsets_ref, bf16[144,16,256]{2,1,0:T(8,128)(2,1)S(1)} %broadcast_dynamic-update-slice_fusion.2.white_ref, f32[32,2,16,256]{3,2,1,0:T(8,128)S(1)} %shard_map.37.rest_0_), custom_call_target="tpu_custom_call" | custom-call | flops 2147483648 | bytes 3276800 | tf_op jit(solution)/shard_map/pallas_call | solution.py:84
  71.1 4.0 %shard_map.40 = f32[32,2,16,256]{3,2,1,0:T(8,128)S(1)} custom-call(s32[32]{0:T(128)S(1)} %get-tuple-element.28.offsets_ref, bf16[144,16,256]{2,1,0:T(8,128)(2,1)S(1)} %broadcast_dynamic-update-slice_fusion.2.white_ref, f32[32,2,16,256]{3,2,1,0:T(8,128)S(1)} %shard_map.39.rest_0_), custom_call_target="tpu_custom_call" | custom-call | flops 2147483648 | bytes 3276800 | tf_op jit(solution)/shard_map/pallas_call | solution.py:84
  75.2 3.5 %shard_map.42 = f32[32,2,16,256]{3,2,1,0:T(8,128)S(1)} custom-call(s32[32]{0:T(128)S(1)} %get-tuple-element.30.offsets_ref, bf16[144,16,256]{2,1,0:T(8,128)(2,1)S(1)} %broadcast_dynamic-update-slice_fusion.2.white_ref, f32[32,2,16,256]{3,2,1,0:T(8,128)S(1)} %shard_map.41.rest_0_), custom_call_target="tpu_custom_call" | custom-call | flops 2147483648 | bytes 3276800 | tf_op jit(solution)/shard_map/pallas_call | solution.py:84
  78.8 2.4 %collective-permute-start.9 = (bf16[32,2,16,256]{3,2,1,0:T(8,128)(2,1)S(1)}, bf16[32,2,16,256]{3,2,1,0:T(8,128)(2,1)S(1)}, u32[]{:S(2)}, u32[]{:S(2)}) collective-permute-start(bf16[32,2,16,256]{3,2,1,0:T(8,128)(2,1)S(1)} %convert_element_type.79), channel_id=1, source_target_pairs={{0,3},{1,0},{2,1},{3,2},{4,7},{5,4},{6,5},{7,6},{8,11},{9,8},{10,9... | collective-permute-start | bytes 1572872 | tf_op jit(solution)/shard_map/ppermute | solution.py:189
  81.2 3.3 %shard_map.44 = f32[32,2,16,256]{3,2,1,0:T(8,128)S(1)} custom-call(s32[32]{0:T(128)S(1)} %get-tuple-element.29.offsets_ref, bf16[144,16,256]{2,1,0:T(8,128)(2,1)S(1)} %broadcast_dynamic-update-slice_fusion.2.white_ref, f32[32,2,16,256]{3,2,1,0:T(8,128)S(1)} %shard_map.43.rest_0_), custom_call_target="tpu_custom_call" | custom-call | flops 2147483648 | bytes 3276800 | tf_op jit(solution)/shard_map/pallas_call | solution.py:84
  84.5 0.4 convolution_bitcast_fusion
  85.0 5.1 %collective-permute-done.8 = bf16[32,2,16,256]{3,2,1,0:T(8,128)(2,1)S(1)} collective-permute-done((bf16[32,2,16,256]{3,2,1,0:T(8,128)(2,1)S(1)}, bf16[32,2,16,256]{3,2,1,0:T(8,128)(2,1)S(1)}, u32[]{:S(2)}, u32[]{:S(2)}) %collective-permute-start.8) | collective-permute-done | bytes 524320 | tf_op jit(solution)/shard_map/ppermute | solution.py:189
  90.1 0.4 convolution_bitcast_fusion.2
  90.5 4.2 %collective-permute-done.9 = bf16[32,2,16,256]{3,2,1,0:T(8,128)(2,1)S(1)} collective-permute-done((bf16[32,2,16,256]{3,2,1,0:T(8,128)(2,1)S(1)}, bf16[32,2,16,256]{3,2,1,0:T(8,128)(2,1)S(1)}, u32[]{:S(2)}, u32[]{:S(2)}) %collective-permute-start.9) | collective-permute-done | bytes 524320 | tf_op jit(solution)/shard_map/ppermute | solution.py:189
  94.7 0.4 convolution_bitcast_fusion.1
  95.1 1.3 %fusion.11 = bf16[32,16,512]{2,1,0:T(8,128)(2,1)} fusion(f32[32,16,512]{2,1,0:T(8,128)S(1)} %convolution_bitcast_fusion, f32[32,16,512]{2,1,0:T(8,128)S(1)} %convolution_bitcast_fusion.1, f32[32,16,512]{2,1,0:T(8,128)S(1)} %convolution_bitcast_fusion.2, bf16[32,2,16,256]{3,2,1,0:T(8,128)(2,1)S(1)} %collective-permute-done.7, s32[]{:T(128)S(6)} %select_n.103, ...), kind=kOutput, calls=%fused_computation.25 | convolution fusion | flops 270794752 | bytes 6291460 | tf_op jit(solution)/shard_map/opck,pkl->ocl/dot_general | solution.py:192
  (37 shorter events, 1.9 us)
Async XLA Ops:
  14.3 7.4 %copy-start = (s32[1024]{0:T(1024)S(1)}, s32[1024]{0:T(1024)}, u32[]{:S(2)}) copy-start(s32[1024]{0:T(1024)} %param.4) | copy-start | bytes 12292
  17.5 8.9 %all-to-all-start = ((bf16[4,2,8192]{2,1,0:T(2,128)(2,1)}), bf16[4,2,8192]{2,1,0:T(2,128)(2,1)S(1)}, u32[]{:S(2)}, u32[]{:S(2)}) async-start(bf16[4,2,8192]{2,1,0:T(2,128)(2,1)} %reshape.445), calls=%async_computation | async-start | bytes 262144 | tf_op jit(solution)/shard_map/all_to_all | solution.py:152
  23.3 1.2 %copy-start.1 = (s32[128]{0:T(128)S(1)}, s32[128]{0:T(128)}, u32[]{:S(2)}) copy-start(s32[128]{0:T(128)} %param.5) | copy-start | bytes 1540
  28.6 7.1 %collective-permute-start = (bf16[16,16,256]{2,1,0:T(8,128)(2,1)S(1)}, bf16[16,16,256]{2,1,0:T(8,128)(2,1)S(1)}, u32[]{:S(2)}, u32[]{:S(2)}) collective-permute-start(bf16[16,16,256]{2,1,0:T(8,128)(2,1)S(1)} %bitcast.90), channel_id=1, source_target_pairs={{4,0},{8,4},{12,8},{16,12},{20,16},{24,20},{28,24},{5,1},{9,5},{13... | collective-permute-start | bytes 393224 | tf_op jit(solution)/shard_map/ppermute | solution.py:166
  29.9 9.8 %collective-permute-start.1 = (bf16[16,16,256]{2,1,0:T(8,128)(2,1)S(1)}, bf16[16,16,256]{2,1,0:T(8,128)(2,1)S(1)}, u32[]{:S(2)}, u32[]{:S(2)}) collective-permute-start(bf16[16,16,256]{2,1,0:T(8,128)(2,1)S(1)} %bitcast.91), channel_id=1, source_target_pairs={{8,0},{12,4},{16,8},{20,12},{24,16},{28,20},{9,1},{13,5},{17,9},{2... | collective-permute-start | bytes 393224 | tf_op jit(solution)/shard_map/ppermute | solution.py:166
  31.2 10.5 %collective-permute-start.2 = (bf16[16,16,256]{2,1,0:T(8,128)(2,1)S(1)}, bf16[16,16,256]{2,1,0:T(8,128)(2,1)S(1)}, u32[]{:S(2)}, u32[]{:S(2)}) collective-permute-start(bf16[16,16,256]{2,1,0:T(8,128)(2,1)S(1)} %bitcast.92), channel_id=1, source_target_pairs={{12,0},{16,4},{20,8},{24,12},{28,16},{13,1},{17,5},{21,9},{25,13},... | collective-permute-start | bytes 393224 | tf_op jit(solution)/shard_map/ppermute | solution.py:166
  41.7 17.3 %collective-permute-start.3 = (bf16[16,16,256]{2,1,0:T(8,128)(2,1)S(1)}, bf16[16,16,256]{2,1,0:T(8,128)(2,1)S(1)}, u32[]{:S(2)}, u32[]{:S(2)}) collective-permute-start(bf16[16,16,256]{2,1,0:T(8,128)(2,1)S(1)} %bitcast.93), channel_id=1, source_target_pairs={{16,0},{20,4},{24,8},{28,12},{17,1},{21,5},{25,9},{29,13},{18,2},{... | collective-permute-start | bytes 393224 | tf_op jit(solution)/shard_map/ppermute | solution.py:166
  43.0 23.8 %collective-permute-start.4 = (bf16[16,16,256]{2,1,0:T(8,128)(2,1)S(1)}, bf16[16,16,256]{2,1,0:T(8,128)(2,1)S(1)}, u32[]{:S(2)}, u32[]{:S(2)}) collective-permute-start(bf16[16,16,256]{2,1,0:T(8,128)(2,1)S(1)} %bitcast.94), channel_id=1, source_target_pairs={{20,0},{24,4},{28,8},{21,1},{25,5},{29,9},{22,2},{26,6},{30,10},{2... | collective-permute-start | bytes 393224 | tf_op jit(solution)/shard_map/ppermute | solution.py:166
  44.3 22.5 %collective-permute-start.5 = (bf16[16,16,256]{2,1,0:T(8,128)(2,1)S(1)}, bf16[16,16,256]{2,1,0:T(8,128)(2,1)S(1)}, u32[]{:S(2)}, u32[]{:S(2)}) collective-permute-start(bf16[16,16,256]{2,1,0:T(8,128)(2,1)S(1)} %bitcast.95), channel_id=1, source_target_pairs={{24,0},{28,4},{25,1},{29,5},{26,2},{30,6},{27,3},{31,7}} | collective-permute-start | bytes 393224 | tf_op jit(solution)/shard_map/ppermute | solution.py:166
  45.6 21.2 %collective-permute-start.6 = (bf16[16,16,256]{2,1,0:T(8,128)(2,1)S(1)}, bf16[16,16,256]{2,1,0:T(8,128)(2,1)S(1)}, u32[]{:S(2)}, u32[]{:S(2)}) collective-permute-start(bf16[16,16,256]{2,1,0:T(8,128)(2,1)S(1)} %bitcast.96), channel_id=1, source_target_pairs={{28,0},{29,1},{30,2},{31,3}} | collective-permute-start | bytes 393224 | tf_op jit(solution)/shard_map/ppermute | solution.py:166
  71.0 24.1 %collective-permute-start.7 = (bf16[32,2,16,256]{3,2,1,0:T(8,128)(2,1)S(1)}, bf16[32,2,16,256]{3,2,1,0:T(8,128)(2,1)S(1)}, u32[]{:S(2)}, u32[]{:S(2)}) collective-permute-start(bf16[32,2,16,256]{3,2,1,0:T(8,128)(2,1)S(1)} %convert_element_type.75), channel_id=1, source_target_pairs={{0,1},{1,2},{2,3},{3,0},{4,5},{5,6},{6,7},{7,4},{8,9},{9,10},{10,1... | collective-permute-start | bytes 1572872 | tf_op jit(solution)/shard_map/ppermute | solution.py:189
  75.1 14.9 %collective-permute-start.8 = (bf16[32,2,16,256]{3,2,1,0:T(8,128)(2,1)S(1)}, bf16[32,2,16,256]{3,2,1,0:T(8,128)(2,1)S(1)}, u32[]{:S(2)}, u32[]{:S(2)}) collective-permute-start(bf16[32,2,16,256]{3,2,1,0:T(8,128)(2,1)S(1)} %convert_element_type.78), channel_id=1, source_target_pairs={{0,2},{1,3},{2,0},{3,1},{4,6},{5,7},{6,4},{7,5},{8,10},{9,11},{10,... | collective-permute-start | bytes 1572872 | tf_op jit(solution)/shard_map/ppermute | solution.py:189
  78.8 15.9 %collective-permute-start.9 = (bf16[32,2,16,256]{3,2,1,0:T(8,128)(2,1)S(1)}, bf16[32,2,16,256]{3,2,1,0:T(8,128)(2,1)S(1)}, u32[]{:S(2)}, u32[]{:S(2)}) collective-permute-start(bf16[32,2,16,256]{3,2,1,0:T(8,128)(2,1)S(1)} %convert_element_type.79), channel_id=1, source_target_pairs={{0,3},{1,0},{2,1},{3,2},{4,7},{5,4},{6,5},{7,6},{8,11},{9,8},{10,9... | collective-permute-start | bytes 1572872 | tf_op jit(solution)/shard_map/ppermute | solution.py:189

commit v13 on v10

--- a/solution.py
+++ b/solution.py
@@ -37,16 +37,25 @@
 def cross_kernel(offsets_ref, base_ref, white_ref, out_ref, *, group, own_count, half):
     step = pl.program_id(0)
     base = base_ref[0]
-    own = [white_ref[base + c].astype(jnp.float32) for c in range(own_count)]
+    bins = white_ref.shape[2]
+    row_of = lax.broadcasted_iota(jnp.int32, (own_count, own_count * half), 1) // half
+    pick = (row_of == lax.broadcasted_iota(jnp.int32, (own_count, own_count * half), 0)).astype(jnp.float32)
+
+    def window_sum(products):
+        return jnp.dot(
+            pick,
+            products.reshape(own_count * half, bins),
+            precision=lax.Precision.HIGHEST,
+            preferred_element_type=jnp.float32,
+        )
 
     def one_offset(i, carry):
         shift = offsets_ref[step * group + i]
-        for c in range(own_count):
-            a = own[c]
-            b = white_ref[base + c + shift].astype(jnp.float32)
-            ar, ai, br, bi = a[:half], a[half:], b[:half], b[half:]
-            out_ref[i, 0, pl.ds(c, 1), :] = jnp.sum(ar * br + ai * bi, axis=0, keepdims=True)
-            out_ref[i, 1, pl.ds(c, 1), :] = jnp.sum(ai * br - ar * bi, axis=0, keepdims=True)
+        a = white_ref[pl.ds(base, own_count)].astype(jnp.float32)
+        b = white_ref[pl.ds(base + shift, own_count)].astype(jnp.float32)
+        ar, ai, br, bi = a[:, :half], a[:, half:], b[:, :half], b[:, half:]
+        out_ref[i, 0] = window_sum(ar * br + ai * bi)
+        out_ref[i, 1] = window_sum(ai * br - ar * bi)
         return carry
 
     lax.fori_loop(0, group, one_offset, 0)

time: 91.6 us -> 113 us (1.23)
  Pallas kernels: 18.5 us -> 40.3 us
    pallas_call x4, Pallas kernels: 18.5 us -> 40.3 us  [cross_spectra(): pl.pallas_call(kernel, grid_spec=pltpu.PrefetchScalarGridSpec(num_scalar_...]
  transfers between devices with their start and end apart: 11 -> 11, of which waited for: 7 -> 6; matrix products, arithmetic and copies ran while one was open for 10% -> 8% of each run, Pallas kernels for 15% -> 27%
where the time goes in v13:
time: 113 us; the launch traced here: 112 us
  Pallas kernels  40.3 us (36%)
  waiting for transfers between devices  26.2 us (23%)
  starting transfers between devices  14.2 us (13%)
  other arithmetic  12.4 us (11%)
  local copies, waits for them, and re-layouts  11.4 us (10%)
  matrix products  7.12 us (6%)
    pallas_call x4, Pallas kernels, cross_spectra(): pl.pallas_call(kernel, grid_spec=pltpu.PrefetchScalarGridSpec(num_scalar_...  40.3 us
    ppermute x7, waiting for transfers between devices, local(): blocks.append(lax.ppermute(rows_white, 'gx', perm=pairs))  22.2 us
    ppermute x7, starting transfers between devices, local(): blocks.append(lax.ppermute(rows_white, 'gx', perm=pairs))  9.02 us
    another operation x2, other arithmetic  5.32 us
    dot_general x4, matrix products, local(): jnp.einsum('opck,pkl->ocl', part, rows, preferred_element_type=jnp.float32)  4.67 us
    all_to_all x1, starting transfers between devices, local(): lax.all_to_all(white, 'gy', split_axis=3, concat_axis=0, tiled=True)  4.21 us
    all_to_all x1, waiting for transfers between devices, local(): lax.all_to_all(white, 'gy', split_axis=3, concat_axis=0, tiled=True)  4.02 us
    unnamed x14, local copies, waits for them, and re-layouts  2.6 us
  transfers between devices with their start and end apart: 11, of which 6 were waited for; matrix products, arithmetic and copies ran while one was open for 8% of the time, Pallas kernels for 27%

profile of v13, /device:TPU:0, one launch (start us, length us, event | category | flops | bytes accessed | tf_op | source)
XLA Modules:
  0.0 112.0 jit_solution(2888030399375071332)
XLA Ops:
  0.0 1.2 %fusion.52 = (f32[32,1024]{1,0:T(8,128)S(1)}, f32[32,1024]{1,0:T(8,128)S(1)}) fusion(s32[1024]{0:T(1024)} %param.4), kind=kLoop, calls=%fused_computation.86 | loop fusion | flops 458752 | bytes 266240 | tf_op jit(solution)/shard_map/cos | solution.py:99
  1.2 0.7 add_select_fusion.5
  1.9 1.8 %fusion.41 = (f32[64,1024]{1,0:T(8,128)S(1)}, f32[64,1024]{1,0:T(8,128)S(1)}) fusion(s32[1024]{0:T(1024)} %param.4, s32[64]{0:T(128)S(1)} %iota_multiply_fusion), kind=kLoop, calls=%fused_computation.69 | loop fusion | flops 917504 | bytes 528640 | tf_op jit(solution)/shard_map/cos | solution.py:99
  3.7 1.3 %copy.29 = bf16[2,16,8192]{2,1,0:T(8,128)(2,1)S(1)} copy(bf16[2,16,8192]{2,0,1:T(2,128)(2,1)} %bitcast.86) | data formatting | bytes 1048576 | tf_op jit(solution)/shard_map/transpose | solution.py:133
  5.0 0.4 reshape_reshape.3
  5.4 0.3 copy.30
  5.7 3.7 %subtract_convert_fusion = (bf16[64,32,1024]{2,1,0:T(8,128)(2,1)S(1)}, bf16[64,32,1024]{2,1,0:T(8,128)(2,1)S(1)}) fusion(f32[64,1024]{1,0:T(8,128)S(1)} %get-tuple-element.16, f32[32,1024]{1,0:T(8,128)S(1)} %get-tuple-element.22, f32[64,1024]{1,0:T(8,128)S(1)} %get-tuple-element.15, f32[32,1024]{1,0:T(8,128)S(1)} %get-tuple-element.21), kind=kLoop, calls=%fused_computation.5 | loop fusion | flops 18874368 | bytes 9175040 | tf_op jit(solution)/shard_map/convert.7
  9.4 2.5 %fusion.4 = f32[128,2048]{0,1:T(8,128)S(1)} fusion(bf16[128,2048]{1,0:T(8,128)(2,1)S(1)} %bitcast.87, bf16[2048,1024]{1,0:T(8,128)(2,1)S(1)} %bitcast.79, bf16[2048,1024]{1,0:T(8,128)(2,1)S(1)} %bitcast.78), kind=kOutput, calls=%fused_computation.14 | convolution fusion | flops 1090519040 | bytes 9961472 | tf_op jit(solution)/shard_map/dot_general | solution.py:112
  11.9 0.3 copy.31
  12.2 0.9 reshape.435
  13.1 0.8 fusion.68
  14.1 0.2 fusion.25
  14.5 0.2 concatenate.15
  15.0 0.8 copy.33
  15.8 1.7 %reshape.445 = bf16[4,2,8192]{2,1,0:T(2,128)(2,1)} reshape(bf16[1024,2,2,16]{3,2,1,0:T(2,128)(2,1)S(1)} %bitcast.76) | data formatting | bytes 262144
  17.5 4.2 %all-to-all-start = ((bf16[4,2,8192]{2,1,0:T(2,128)(2,1)}), bf16[4,2,8192]{2,1,0:T(2,128)(2,1)S(1)}, u32[]{:S(2)}, u32[]{:S(2)}) async-start(bf16[4,2,8192]{2,1,0:T(2,128)(2,1)} %reshape.445), calls=%async_computation | async-start | bytes 262144 | tf_op jit(solution)/shard_map/all_to_all | solution.py:136
  21.7 0.5 fusion.50
  22.4 4.0 %all-to-all-done = bf16[4,2,8192]{2,1,0:T(2,128)(2,1)S(1)} async-done(((bf16[4,2,8192]{2,1,0:T(2,128)(2,1)}), bf16[4,2,8192]{2,1,0:T(2,128)(2,1)S(1)}, u32[]{:S(2)}, u32[]{:S(2)}) %all-to-all-start) | async-done | bytes 131104 | tf_op jit(solution)/shard_map/all_to_all | solution.py:136
  26.4 0.7 reshape.446
  27.1 1.4 %copy.43 = bf16[2,16,2,4,256]{4,3,1,2,0:T(4,128)(2,1)S(1)} copy(bf16[2,16,2,4,256]{1,2,0,4,3:T(2,128)(2,1)S(1)} %bitcast.77) | data formatting | bytes 262144 | tf_op jit(solution)/shard_map/all_to_all | solution.py:136
  28.6 1.3 %collective-permute-start = (bf16[16,16,256]{2,1,0:T(8,128)(2,1)S(1)}, bf16[16,16,256]{2,1,0:T(8,128)(2,1)S(1)}, u32[]{:S(2)}, u32[]{:S(2)}) collective-permute-start(bf16[16,16,256]{2,1,0:T(8,128)(2,1)S(1)} %bitcast.88), channel_id=1, source_target_pairs={{4,0},{8,4},{12,8},{16,12},{20,16},{24,20},{28,24},{5,1},{9,5},{13... | collective-permute-start | bytes 393224 | tf_op jit(solution)/shard_map/ppermute | solution.py:145
  29.9 1.3 %collective-permute-start.1 = (bf16[16,16,256]{2,1,0:T(8,128)(2,1)S(1)}, bf16[16,16,256]{2,1,0:T(8,128)(2,1)S(1)}, u32[]{:S(2)}, u32[]{:S(2)}) collective-permute-start(bf16[16,16,256]{2,1,0:T(8,128)(2,1)S(1)} %bitcast.89), channel_id=1, source_target_pairs={{8,0},{12,4},{16,8},{20,12},{24,16},{28,20},{9,1},{13,5},{17,9},{2... | collective-permute-start | bytes 393224 | tf_op jit(solution)/shard_map/ppermute | solution.py:145
  31.3 1.3 %collective-permute-start.2 = (bf16[16,16,256]{2,1,0:T(8,128)(2,1)S(1)}, bf16[16,16,256]{2,1,0:T(8,128)(2,1)S(1)}, u32[]{:S(2)}, u32[]{:S(2)}) collective-permute-start(bf16[16,16,256]{2,1,0:T(8,128)(2,1)S(1)} %bitcast.90), channel_id=1, source_target_pairs={{12,0},{16,4},{20,8},{24,12},{28,16},{13,1},{17,5},{21,9},{25,13},... | collective-permute-start | bytes 393224 | tf_op jit(solution)/shard_map/ppermute | solution.py:145
  32.6 1.3 %collective-permute-start.3 = (bf16[16,16,256]{2,1,0:T(8,128)(2,1)S(1)}, bf16[16,16,256]{2,1,0:T(8,128)(2,1)S(1)}, u32[]{:S(2)}, u32[]{:S(2)}) collective-permute-start(bf16[16,16,256]{2,1,0:T(8,128)(2,1)S(1)} %bitcast.91), channel_id=1, source_target_pairs={{16,0},{20,4},{24,8},{28,12},{17,1},{21,5},{25,9},{29,13},{18,2},{... | collective-permute-start | bytes 393224 | tf_op jit(solution)/shard_map/ppermute | solution.py:145
  33.9 1.3 %collective-permute-start.4 = (bf16[16,16,256]{2,1,0:T(8,128)(2,1)S(1)}, bf16[16,16,256]{2,1,0:T(8,128)(2,1)S(1)}, u32[]{:S(2)}, u32[]{:S(2)}) collective-permute-start(bf16[16,16,256]{2,1,0:T(8,128)(2,1)S(1)} %bitcast.92), channel_id=1, source_target_pairs={{20,0},{24,4},{28,8},{21,1},{25,5},{29,9},{22,2},{26,6},{30,10},{2... | collective-permute-start | bytes 393224 | tf_op jit(solution)/shard_map/ppermute | solution.py:145
  35.2 0.5 collective-permute-done
  35.6 1.3 %collective-permute-start.5 = (bf16[16,16,256]{2,1,0:T(8,128)(2,1)S(1)}, bf16[16,16,256]{2,1,0:T(8,128)(2,1)S(1)}, u32[]{:S(2)}, u32[]{:S(2)}) collective-permute-start(bf16[16,16,256]{2,1,0:T(8,128)(2,1)S(1)} %bitcast.93), channel_id=1, source_target_pairs={{24,0},{28,4},{25,1},{29,5},{26,2},{30,6},{27,3},{31,7}} | collective-permute-start | bytes 393224 | tf_op jit(solution)/shard_map/ppermute | solution.py:145
  37.0 2.8 %collective-permute-done.1 = bf16[16,16,256]{2,1,0:T(8,128)(2,1)S(1)} collective-permute-done((bf16[16,16,256]{2,1,0:T(8,128)(2,1)S(1)}, bf16[16,16,256]{2,1,0:T(8,128)(2,1)S(1)}, u32[]{:S(2)}, u32[]{:S(2)}) %collective-permute-start.1) | collective-permute-done | bytes 131104 | tf_op jit(solution)/shard_map/ppermute | solution.py:145
  39.7 1.3 %collective-permute-start.6 = (bf16[16,16,256]{2,1,0:T(8,128)(2,1)S(1)}, bf16[16,16,256]{2,1,0:T(8,128)(2,1)S(1)}, u32[]{:S(2)}, u32[]{:S(2)}) collective-permute-start(bf16[16,16,256]{2,1,0:T(8,128)(2,1)S(1)} %bitcast.94), channel_id=1, source_target_pairs={{28,0},{29,1},{30,2},{31,3}} | collective-permute-start | bytes 393224 | tf_op jit(solution)/shard_map/ppermute | solution.py:145
  41.0 0.7 collective-permute-done.2
  41.7 15.9 %collective-permute-done.3 = bf16[16,16,256]{2,1,0:T(8,128)(2,1)S(1)} collective-permute-done((bf16[16,16,256]{2,1,0:T(8,128)(2,1)S(1)}, bf16[16,16,256]{2,1,0:T(8,128)(2,1)S(1)}, u32[]{:S(2)}, u32[]{:S(2)}) %collective-permute-start.3) | collective-permute-done | bytes 131104 | tf_op jit(solution)/shard_map/ppermute | solution.py:145
  57.6 2.4 %collective-permute-done.4 = bf16[16,16,256]{2,1,0:T(8,128)(2,1)S(1)} collective-permute-done((bf16[16,16,256]{2,1,0:T(8,128)(2,1)S(1)}, bf16[16,16,256]{2,1,0:T(8,128)(2,1)S(1)}, u32[]{:S(2)}, u32[]{:S(2)}) %collective-permute-start.4) | collective-permute-done | bytes 131104 | tf_op jit(solution)/shard_map/ppermute | solution.py:145
  60.1 10.1 %shard_map.38 = f32[32,2,16,256]{3,2,1,0:T(8,128)S(1)} custom-call(s32[32]{0:T(128)S(1)} %get-tuple-element.26.offsets_ref, s32[1]{0:T(128)} %constant.111.clone.1.base_ref, bf16[144,16,256]{2,1,0:T(8,128)(2,1)S(1)} %broadcast_dynamic-update-slice_fusion.white_ref), custom_call_target="tpu_custom_call" | custom-call | flops 16777216 | bytes 2228224 | tf_op jit(solution)/shard_map/pallas_call | solution.py:69
  70.2 0.9 convert_element_type.78
  71.1 0.4 collective-permute-start.8
  71.5 0.3 fusion.54
  71.8 10.1 %shard_map.39 = f32[32,2,16,256]{3,2,1,0:T(8,128)S(1)} custom-call(s32[32]{0:T(128)S(1)} %get-tuple-element.28.offsets_ref, s32[1]{0:T(128)} %constant.111.clone.1.base_ref, bf16[144,16,256]{2,1,0:T(8,128)(2,1)S(1)} %broadcast_dynamic-update-slice_fusion.white_ref), custom_call_target="tpu_custom_call" | custom-call | flops 16777216 | bytes 2228224 | tf_op jit(solution)/shard_map/pallas_call | solution.py:69
  81.9 0.9 convert_element_type.79
  82.8 1.7 %negate_convert_fusion.1 = (bf16[1024,16,32]{0,2,1:T(8,128)(2,1)}, bf16[1024,16,32]{0,2,1:T(8,128)(2,1)S(1)}) fusion(f32[1024,16]{0,1:T(8,128)S(1)} %get-tuple-element.18, f32[1024,32]{0,1:T(8,128)S(1)} %get-tuple-element.24, f32[1024,16]{0,1:T(8,128)S(1)} %get-tuple-element.17, f32[1024,32]{0,1:T(8,128)S(1)} %get-tuple-element.23), kind=kLoop, calls=%fused_computation.15 | loop fusion | flops 4718592 | bytes 2490368 | tf_op jit(solution)/shard_map/convert.2
  84.4 0.5 copy.37
  85.0 1.5 %copy.38 = bf16[1,1024,512]{2,1,0:T(8,128)(2,1)S(1)} copy(bf16[1,1024,512]{1,2,0:T(8,128)(2,1)} %bitcast.80) | data formatting | bytes 2097152 | tf_op jit(solution)/shard_map/neg | solution.py:29
  86.5 10.1 %shard_map.37 = f32[32,2,16,256]{3,2,1,0:T(8,128)S(1)} custom-call(s32[32]{0:T(128)S(1)} %get-tuple-element.25.offsets_ref, s32[1]{0:T(128)} %constant.111.clone.1.base_ref, bf16[144,16,256]{2,1,0:T(8,128)(2,1)S(1)} %broadcast_dynamic-update-slice_fusion.white_ref), custom_call_target="tpu_custom_call" | custom-call | flops 16777216 | bytes 2228224 | tf_op jit(solution)/shard_map/pallas_call | solution.py:69
  96.7 0.6 collective-permute-start.7
  97.2 10.1 %shard_map.40 = f32[32,2,16,256]{3,2,1,0:T(8,128)S(1)} custom-call(s32[32]{0:T(128)S(1)} %get-tuple-element.27.offsets_ref, s32[1]{0:T(128)} %constant.111.clone.1.base_ref, bf16[144,16,256]{2,1,0:T(8,128)(2,1)S(1)} %broadcast_dynamic-update-slice_fusion.white_ref), custom_call_target="tpu_custom_call" | custom-call | flops 16777216 | bytes 2228224 | tf_op jit(solution)/shard_map/pallas_call | solution.py:69
  107.3 0.4 convolution_bitcast_fusion
  107.7 1.5 %convolution_bitcast_fusion.2 = f32[32,16,512]{2,1,0:T(8,128)S(1)} fusion(bf16[32,2,16,256]{3,2,1,0:T(8,128)(2,1)} %collective-permute-done.8, s32[]{:T(128)S(6)} %select_n.105, bf16[1,1024,512]{2,1,0:T(8,128)(2,1)S(1)} %copy.37, bf16[1,1024,512]{2,1,0:T(8,128)(2,1)S(1)} %copy.38), kind=kOutput, calls=%fused_computation.19 | convolution fusion | flops 269484032 | bytes 3670020 | tf_op jit(solution)/shard_map/opck,pkl->ocl/dot_general | solution.py:168
  109.2 1.5 %convolution_bitcast_fusion.1 = f32[32,16,512]{2,1,0:T(8,128)S(1)} fusion(bf16[32,2,16,256]{3,2,1,0:T(8,128)(2,1)} %collective-permute-done.9, s32[]{:T(128)S(6)} %select_n.107, bf16[1,1024,512]{2,1,0:T(8,128)(2,1)S(1)} %copy.37, bf16[1,1024,512]{2,1,0:T(8,128)(2,1)S(1)} %copy.38), kind=kOutput, calls=%fused_computation.18 | convolution fusion | flops 269484032 | bytes 3670020 | tf_op jit(solution)/shard_map/opck,pkl->ocl/dot_general | solution.py:168
  110.7 1.3 %fusion.11 = bf16[32,16,512]{2,1,0:T(8,128)(2,1)} fusion(f32[32,16,512]{2,1,0:T(8,128)S(1)} %convolution_bitcast_fusion, f32[32,16,512]{2,1,0:T(8,128)S(1)} %convolution_bitcast_fusion.1, f32[32,16,512]{2,1,0:T(8,128)S(1)} %convolution_bitcast_fusion.2, bf16[32,2,16,256]{3,2,1,0:T(8,128)(2,1)S(1)} %collective-permute-done.7, s32[]{:T(128)S(6)} %select_n.103, ...), kind=kOutput, calls=%fused_computation.25 | convolution fusion | flops 270794752 | bytes 6291460 | tf_op jit(solution)/shard_map/opck,pkl->ocl/dot_general | solution.py:168
  (30 shorter events, 1.0 us)
Async XLA Ops:
  14.3 7.4 %copy-start = (s32[1024]{0:T(1024)S(1)}, s32[1024]{0:T(1024)}, u32[]{:S(2)}) copy-start(s32[1024]{0:T(1024)} %param.4) | copy-start | bytes 12292
  14.3 7.9 %copy-start.1 = (s32[128]{0:T(128)S(1)}, s32[128]{0:T(128)}, u32[]{:S(2)}) copy-start(s32[128]{0:T(128)} %param.5) | copy-start | bytes 1540
  17.5 8.9 %all-to-all-start = ((bf16[4,2,8192]{2,1,0:T(2,128)(2,1)}), bf16[4,2,8192]{2,1,0:T(2,128)(2,1)S(1)}, u32[]{:S(2)}, u32[]{:S(2)}) async-start(bf16[4,2,8192]{2,1,0:T(2,128)(2,1)} %reshape.445), calls=%async_computation | async-start | bytes 262144 | tf_op jit(solution)/shard_map/all_to_all | solution.py:136
  28.6 7.1 %collective-permute-start = (bf16[16,16,256]{2,1,0:T(8,128)(2,1)S(1)}, bf16[16,16,256]{2,1,0:T(8,128)(2,1)S(1)}, u32[]{:S(2)}, u32[]{:S(2)}) collective-permute-start(bf16[16,16,256]{2,1,0:T(8,128)(2,1)S(1)} %bitcast.88), channel_id=1, source_target_pairs={{4,0},{8,4},{12,8},{16,12},{20,16},{24,20},{28,24},{5,1},{9,5},{13... | collective-permute-start | bytes 393224 | tf_op jit(solution)/shard_map/ppermute | solution.py:145
  29.9 9.8 %collective-permute-start.1 = (bf16[16,16,256]{2,1,0:T(8,128)(2,1)S(1)}, bf16[16,16,256]{2,1,0:T(8,128)(2,1)S(1)}, u32[]{:S(2)}, u32[]{:S(2)}) collective-permute-start(bf16[16,16,256]{2,1,0:T(8,128)(2,1)S(1)} %bitcast.89), channel_id=1, source_target_pairs={{8,0},{12,4},{16,8},{20,12},{24,16},{28,20},{9,1},{13,5},{17,9},{2... | collective-permute-start | bytes 393224 | tf_op jit(solution)/shard_map/ppermute | solution.py:145
  31.3 10.4 %collective-permute-start.2 = (bf16[16,16,256]{2,1,0:T(8,128)(2,1)S(1)}, bf16[16,16,256]{2,1,0:T(8,128)(2,1)S(1)}, u32[]{:S(2)}, u32[]{:S(2)}) collective-permute-start(bf16[16,16,256]{2,1,0:T(8,128)(2,1)S(1)} %bitcast.90), channel_id=1, source_target_pairs={{12,0},{16,4},{20,8},{24,12},{28,16},{13,1},{17,5},{21,9},{25,13},... | collective-permute-start | bytes 393224 | tf_op jit(solution)/shard_map/ppermute | solution.py:145
  32.6 25.0 %collective-permute-start.3 = (bf16[16,16,256]{2,1,0:T(8,128)(2,1)S(1)}, bf16[16,16,256]{2,1,0:T(8,128)(2,1)S(1)}, u32[]{:S(2)}, u32[]{:S(2)}) collective-permute-start(bf16[16,16,256]{2,1,0:T(8,128)(2,1)S(1)} %bitcast.91), channel_id=1, source_target_pairs={{16,0},{20,4},{24,8},{28,12},{17,1},{21,5},{25,9},{29,13},{18,2},{... | collective-permute-start | bytes 393224 | tf_op jit(solution)/shard_map/ppermute | solution.py:145
  33.9 26.1 %collective-permute-start.4 = (bf16[16,16,256]{2,1,0:T(8,128)(2,1)S(1)}, bf16[16,16,256]{2,1,0:T(8,128)(2,1)S(1)}, u32[]{:S(2)}, u32[]{:S(2)}) collective-permute-start(bf16[16,16,256]{2,1,0:T(8,128)(2,1)S(1)} %bitcast.92), channel_id=1, source_target_pairs={{20,0},{24,4},{28,8},{21,1},{25,5},{29,9},{22,2},{26,6},{30,10},{2... | collective-permute-start | bytes 393224 | tf_op jit(solution)/shard_map/ppermute | solution.py:145
  35.6 24.4 %collective-permute-start.5 = (bf16[16,16,256]{2,1,0:T(8,128)(2,1)S(1)}, bf16[16,16,256]{2,1,0:T(8,128)(2,1)S(1)}, u32[]{:S(2)}, u32[]{:S(2)}) collective-permute-start(bf16[16,16,256]{2,1,0:T(8,128)(2,1)S(1)} %bitcast.93), channel_id=1, source_target_pairs={{24,0},{28,4},{25,1},{29,5},{26,2},{30,6},{27,3},{31,7}} | collective-permute-start | bytes 393224 | tf_op jit(solution)/shard_map/ppermute | solution.py:145
  39.7 20.3 %collective-permute-start.6 = (bf16[16,16,256]{2,1,0:T(8,128)(2,1)S(1)}, bf16[16,16,256]{2,1,0:T(8,128)(2,1)S(1)}, u32[]{:S(2)}, u32[]{:S(2)}) collective-permute-start(bf16[16,16,256]{2,1,0:T(8,128)(2,1)S(1)} %bitcast.94), channel_id=1, source_target_pairs={{28,0},{29,1},{30,2},{31,3}} | collective-permute-start | bytes 393224 | tf_op jit(solution)/shard_map/ppermute | solution.py:145
  71.1 36.6 %collective-permute-start.8 = (bf16[32,2,16,256]{3,2,1,0:T(8,128)(2,1)}, bf16[32,2,16,256]{3,2,1,0:T(8,128)(2,1)}, u32[]{:S(2)}, u32[]{:S(2)}) collective-permute-start(bf16[32,2,16,256]{3,2,1,0:T(8,128)(2,1)} %convert_element_type.78), channel_id=1, source_target_pairs={{0,2},{1,3},{2,0},{3,1},{4,6},{5,7},{6,4},{7,5},{8,10},{9,11},{10,... | collective-permute-start | bytes 1572872 | tf_op jit(solution)/shard_map/ppermute | solution.py:165
  82.8 26.5 %collective-permute-start.9 = (bf16[32,2,16,256]{3,2,1,0:T(8,128)(2,1)}, bf16[32,2,16,256]{3,2,1,0:T(8,128)(2,1)}, u32[]{:S(2)}, u32[]{:S(2)}) collective-permute-start(bf16[32,2,16,256]{3,2,1,0:T(8,128)(2,1)} %convert_element_type.79), channel_id=1, source_target_pairs={{0,3},{1,0},{2,1},{3,2},{4,7},{5,4},{6,5},{7,6},{8,11},{9,8},{10,9... | collective-permute-start | bytes 1572872 | tf_op jit(solution)/shard_map/ppermute | solution.py:165
  96.7 14.1 %collective-permute-start.7 = (bf16[32,2,16,256]{3,2,1,0:T(8,128)(2,1)S(1)}, bf16[32,2,16,256]{3,2,1,0:T(8,128)(2,1)S(1)}, u32[]{:S(2)}, u32[]{:S(2)}) collective-permute-start(bf16[32,2,16,256]{3,2,1,0:T(8,128)(2,1)S(1)} %convert_element_type.75), channel_id=1, source_target_pairs={{0,1},{1,2},{2,3},{3,0},{4,5},{5,6},{6,7},{7,4},{8,9},{9,10},{10,1... | collective-permute-start | bytes 1572872 | tf_op jit(solution)/shard_map/ppermute | solution.py:165

commit v14 on v10

--- a/solution.py
+++ b/solution.py
@@ -99,21 +99,20 @@
     bin_count = kept_bins.shape[0]
     block_count = 4
     block_len = samples // block_count
-    lhs = jnp.transpose(record_rows.reshape(row_count, block_count, block_len), (1, 0, 2))
     prod = jnp.dot(
-        lhs.reshape(block_count * row_count, block_len),
+        record_rows.reshape(row_count * block_count, block_len),
         small_table(kept_bins, block_len),
         preferred_element_type=jnp.float32,
-    ).reshape(block_count, row_count, 2, bin_count)
+    ).reshape(row_count, block_count, 2, bin_count)
     turns = jnp.mod(
         jnp.arange(block_count, dtype=jnp.int32)[:, None] * jnp.mod(kept_bins, block_count)[None, :],
         block_count,
     ).astype(jnp.float32) * (2.0 * math.pi / block_count)
-    tw_re = jnp.round(jnp.cos(turns))[:, None, :]
-    tw_im = jnp.round(-jnp.sin(turns))[:, None, :]
+    tw_re = jnp.round(jnp.cos(turns))[None]
+    tw_im = jnp.round(-jnp.sin(turns))[None]
     p_re, p_im = prod[:, :, 0], prod[:, :, 1]
-    real_part = jnp.sum(tw_re * p_re - tw_im * p_im, axis=0)
-    imag_part = jnp.sum(tw_re * p_im + tw_im * p_re, axis=0)
+    real_part = jnp.sum(tw_re * p_re - tw_im * p_im, axis=1)
+    imag_part = jnp.sum(tw_re * p_im + tw_im * p_re, axis=1)
     return jnp.concatenate([real_part, imag_part], axis=-1)
 
 
@@ -121,13 +120,12 @@
     ch_dev, win_dev, samples = records.shape
     bin_count = kept_bins.shape[0]
     band_span = pair_offsets.shape[0]
-    record_rows = jnp.transpose(records, (1, 0, 2)).reshape(win_dev * ch_dev, samples)
-    spectra = forward_spectra(record_rows, kept_bins)
-    white = whiten(spectra).reshape(win_dev, ch_dev, 2, bin_count)
-    freq_white = lax.all_to_all(white, "gy", split_axis=3, concat_axis=0, tiled=True)
-    windows = freq_white.shape[0]
+    spectra = forward_spectra(records.reshape(ch_dev * win_dev, samples), kept_bins)
+    white = whiten(spectra).reshape(ch_dev, win_dev, 2, bin_count)
+    freq_white = lax.all_to_all(white, "gy", split_axis=3, concat_axis=1, tiled=True)
+    windows = freq_white.shape[1]
     shard_bins = freq_white.shape[3]
-    rows_white = jnp.transpose(freq_white, (1, 2, 0, 3)).reshape(ch_dev, 2 * windows, shard_bins)
+    rows_white = jnp.transpose(freq_white, (0, 2, 1, 3)).reshape(ch_dev, 2 * windows, shard_bins)
     gx_count = lax.axis_size("gx")
     needed = -(-band_span // ch_dev)
     blocks = [rows_white]

time: 91.6 us -> 91.6 us (level)
    transpose x3 -> x1, local copies, waits for them, and re-layouts: 1.71 us -> 0.08 us  [local(): jnp.transpose(freq_white, (0, 2, 1, 3))]
where the time goes in v14:
time: 91.6 us; the launch traced here: 90.5 us
  waiting for transfers between devices  26.5 us (29%)
  Pallas kernels  18.5 us (20%)
  starting transfers between devices  14.2 us (16%)
  other arithmetic  13 us (14%)
  local copies, waits for them, and re-layouts  10.9 us (12%)
  matrix products  7.12 us (8%)
    ppermute x7, waiting for transfers between devices, local(): blocks.append(lax.ppermute(rows_white, 'gx', perm=pairs))  22.2 us
    pallas_call x4, Pallas kernels, cross_spectra(): pl.pallas_call(kernel, grid_spec=pltpu.PrefetchScalarGridSpec(num_scalar_...  18.5 us
    ppermute x7, starting transfers between devices, local(): blocks.append(lax.ppermute(rows_white, 'gx', perm=pairs))  9.02 us
    another operation x2, other arithmetic  5.32 us
    dot_general x4, matrix products, local(): jnp.einsum('opck,pkl->ocl', part, rows, preferred_element_type=jnp.float32)  4.66 us
    all_to_all x1, starting transfers between devices, local(): lax.all_to_all(white, 'gy', split_axis=3, concat_axis=1, tiled=True)  4.21 us
    all_to_all x1, waiting for transfers between devices, local(): lax.all_to_all(white, 'gy', split_axis=3, concat_axis=1, tiled=True)  4.02 us
    unnamed x14, local copies, waits for them, and re-layouts  2.6 us
  transfers between devices with their start and end apart: 11, of which 7 were waited for; matrix products, arithmetic and copies ran while one was open for 10% of the time, Pallas kernels for 15%

profile of v14, /device:TPU:0, one launch (start us, length us, event | category | flops | bytes accessed | tf_op | source)
XLA Modules:
  0.0 90.5 jit_solution(16553068493189408691)
XLA Ops:
  0.0 1.2 %fusion.52 = (f32[32,1024]{1,0:T(8,128)S(1)}, f32[32,1024]{1,0:T(8,128)S(1)}) fusion(s32[1024]{0:T(1024)} %param.4), kind=kLoop, calls=%fused_computation.86 | loop fusion | flops 458752 | bytes 266240 | tf_op jit(solution)/shard_map/cos | solution.py:90
  1.2 0.7 add_select_fusion.5
  1.9 1.8 %fusion.41 = (f32[64,1024]{1,0:T(8,128)S(1)}, f32[64,1024]{1,0:T(8,128)S(1)}) fusion(s32[1024]{0:T(1024)} %param.4, s32[64]{0:T(128)S(1)} %iota_multiply_fusion), kind=kLoop, calls=%fused_computation.69 | loop fusion | flops 917504 | bytes 528640 | tf_op jit(solution)/shard_map/cos | solution.py:90
  3.7 1.2 %reshape_reshape.3 = bf16[128,2048]{1,0:T(8,128)(2,1)S(1)} reshape(bf16[16,2,8192]{2,1,0:T(2,128)(2,1)} %param.3) | data formatting | bytes 1048576 | tf_op jit(solution)/shard_map/reshape;reshape | solution.py:103
  4.9 3.7 %subtract_convert_fusion = (bf16[64,32,1024]{2,1,0:T(8,128)(2,1)S(1)}, bf16[64,32,1024]{2,1,0:T(8,128)(2,1)S(1)}) fusion(f32[64,1024]{1,0:T(8,128)S(1)} %get-tuple-element.16, f32[32,1024]{1,0:T(8,128)S(1)} %get-tuple-element.22, f32[64,1024]{1,0:T(8,128)S(1)} %get-tuple-element.15, f32[32,1024]{1,0:T(8,128)S(1)} %get-tuple-element.21), kind=kLoop, calls=%fused_computation.5 | loop fusion | flops 18874368 | bytes 9175040 | tf_op jit(solution)/shard_map/convert.7
  8.5 2.5 %fusion.4 = f32[128,2048]{0,1:T(8,128)S(1)} fusion(bf16[128,2048]{1,0:T(8,128)(2,1)S(1)} %reshape_reshape.3, bf16[2048,1024]{1,0:T(8,128)(2,1)S(1)} %bitcast.76, bf16[2048,1024]{1,0:T(8,128)(2,1)S(1)} %bitcast.75), kind=kOutput, calls=%fused_computation.14 | convolution fusion | flops 1090519040 | bytes 9961472 | tf_op jit(solution)/shard_map/dot_general | solution.py:102
  11.0 0.3 copy.24
  11.3 0.9 reshape.439
  12.2 1.2 %fusion.68 = (f32[32,4,1,1024]{3,2,1,0:T(1,128)S(1)}, f32[32,4,1,1024]{3,2,1,0:T(1,128)S(1)}) fusion(f32[32,4,2,1024]{3,2,1,0:T(2,128)S(1)} %reshape.439), kind=kLoop, calls=%fused_computation.121 | loop fusion | bytes 2097152 | tf_op jit(solution)/shard_map/slice | solution.py:113
  13.6 0.8 fusion.25
  14.5 0.2 concatenate.15
  14.8 0.2 multiply_convert_fusion
  15.0 0.8 copy.26
  15.8 1.7 %reshape.449 = bf16[4,2,8192]{2,1,0:T(2,128)(2,1)} reshape(bf16[1024,2,2,16]{3,2,1,0:T(2,128)(2,1)S(1)} %bitcast.73) | data formatting | bytes 262144
  17.5 4.2 %all-to-all-start = ((bf16[4,2,8192]{2,1,0:T(2,128)(2,1)}), bf16[4,2,8192]{2,1,0:T(2,128)(2,1)S(1)}, u32[]{:S(2)}, u32[]{:S(2)}) async-start(bf16[4,2,8192]{2,1,0:T(2,128)(2,1)} %reshape.449), calls=%async_computation | async-start | bytes 262144 | tf_op jit(solution)/shard_map/all_to_all | solution.py:125
  21.7 0.5 fusion.50
  22.4 4.0 %all-to-all-done = bf16[4,2,8192]{2,1,0:T(2,128)(2,1)S(1)} async-done(((bf16[4,2,8192]{2,1,0:T(2,128)(2,1)}), bf16[4,2,8192]{2,1,0:T(2,128)(2,1)S(1)}, u32[]{:S(2)}, u32[]{:S(2)}) %all-to-all-start) | async-done | bytes 131104 | tf_op jit(solution)/shard_map/all_to_all | solution.py:125
  26.4 0.7 reshape.450
  27.1 1.4 %copy.36 = bf16[16,2,2,4,256]{4,3,0,2,1:T(4,128)(2,1)S(1)} copy(bf16[16,2,2,4,256]{0,2,1,4,3:T(2,128)(2,1)S(1)} %bitcast.74) | data formatting | bytes 262144 | tf_op jit(solution)/shard_map/all_to_all | solution.py:125
  28.6 1.3 %collective-permute-start = (bf16[16,16,256]{2,1,0:T(8,128)(2,1)S(1)}, bf16[16,16,256]{2,1,0:T(8,128)(2,1)S(1)}, u32[]{:S(2)}, u32[]{:S(2)}) collective-permute-start(bf16[16,16,256]{2,1,0:T(8,128)(2,1)S(1)} %bitcast.82), channel_id=1, source_target_pairs={{4,0},{8,4},{12,8},{16,12},{20,16},{24,20},{28,24},{5,1},{9,5},{13... | collective-permute-start | bytes 393224 | tf_op jit(solution)/shard_map/ppermute | solution.py:134
  29.9 1.3 %collective-permute-start.1 = (bf16[16,16,256]{2,1,0:T(8,128)(2,1)S(1)}, bf16[16,16,256]{2,1,0:T(8,128)(2,1)S(1)}, u32[]{:S(2)}, u32[]{:S(2)}) collective-permute-start(bf16[16,16,256]{2,1,0:T(8,128)(2,1)S(1)} %bitcast.83), channel_id=1, source_target_pairs={{8,0},{12,4},{16,8},{20,12},{24,16},{28,20},{9,1},{13,5},{17,9},{2... | collective-permute-start | bytes 393224 | tf_op jit(solution)/shard_map/ppermute | solution.py:134
  31.3 1.3 %collective-permute-start.2 = (bf16[16,16,256]{2,1,0:T(8,128)(2,1)S(1)}, bf16[16,16,256]{2,1,0:T(8,128)(2,1)S(1)}, u32[]{:S(2)}, u32[]{:S(2)}) collective-permute-start(bf16[16,16,256]{2,1,0:T(8,128)(2,1)S(1)} %bitcast.84), channel_id=1, source_target_pairs={{12,0},{16,4},{20,8},{24,12},{28,16},{13,1},{17,5},{21,9},{25,13},... | collective-permute-start | bytes 393224 | tf_op jit(solution)/shard_map/ppermute | solution.py:134
  32.6 1.3 %collective-permute-start.3 = (bf16[16,16,256]{2,1,0:T(8,128)(2,1)S(1)}, bf16[16,16,256]{2,1,0:T(8,128)(2,1)S(1)}, u32[]{:S(2)}, u32[]{:S(2)}) collective-permute-start(bf16[16,16,256]{2,1,0:T(8,128)(2,1)S(1)} %bitcast.85), channel_id=1, source_target_pairs={{16,0},{20,4},{24,8},{28,12},{17,1},{21,5},{25,9},{29,13},{18,2},{... | collective-permute-start | bytes 393224 | tf_op jit(solution)/shard_map/ppermute | solution.py:134
  33.9 1.3 %collective-permute-start.4 = (bf16[16,16,256]{2,1,0:T(8,128)(2,1)S(1)}, bf16[16,16,256]{2,1,0:T(8,128)(2,1)S(1)}, u32[]{:S(2)}, u32[]{:S(2)}) collective-permute-start(bf16[16,16,256]{2,1,0:T(8,128)(2,1)S(1)} %bitcast.86), channel_id=1, source_target_pairs={{20,0},{24,4},{28,8},{21,1},{25,5},{29,9},{22,2},{26,6},{30,10},{2... | collective-permute-start | bytes 393224 | tf_op jit(solution)/shard_map/ppermute | solution.py:134
  35.2 0.5 collective-permute-done
  35.7 1.3 %collective-permute-start.5 = (bf16[16,16,256]{2,1,0:T(8,128)(2,1)S(1)}, bf16[16,16,256]{2,1,0:T(8,128)(2,1)S(1)}, u32[]{:S(2)}, u32[]{:S(2)}) collective-permute-start(bf16[16,16,256]{2,1,0:T(8,128)(2,1)S(1)} %bitcast.87), channel_id=1, source_target_pairs={{24,0},{28,4},{25,1},{29,5},{26,2},{30,6},{27,3},{31,7}} | collective-permute-start | bytes 393224 | tf_op jit(solution)/shard_map/ppermute | solution.py:134
  37.0 2.8 %collective-permute-done.1 = bf16[16,16,256]{2,1,0:T(8,128)(2,1)S(1)} collective-permute-done((bf16[16,16,256]{2,1,0:T(8,128)(2,1)S(1)}, bf16[16,16,256]{2,1,0:T(8,128)(2,1)S(1)}, u32[]{:S(2)}, u32[]{:S(2)}) %collective-permute-start.1) | collective-permute-done | bytes 131104 | tf_op jit(solution)/shard_map/ppermute | solution.py:134
  39.7 1.3 %collective-permute-start.6 = (bf16[16,16,256]{2,1,0:T(8,128)(2,1)S(1)}, bf16[16,16,256]{2,1,0:T(8,128)(2,1)S(1)}, u32[]{:S(2)}, u32[]{:S(2)}) collective-permute-start(bf16[16,16,256]{2,1,0:T(8,128)(2,1)S(1)} %bitcast.88), channel_id=1, source_target_pairs={{28,0},{29,1},{30,2},{31,3}} | collective-permute-start | bytes 393224 | tf_op jit(solution)/shard_map/ppermute | solution.py:134
  41.1 0.7 collective-permute-done.2
  41.7 15.9 %collective-permute-done.3 = bf16[16,16,256]{2,1,0:T(8,128)(2,1)S(1)} collective-permute-done((bf16[16,16,256]{2,1,0:T(8,128)(2,1)S(1)}, bf16[16,16,256]{2,1,0:T(8,128)(2,1)S(1)}, u32[]{:S(2)}, u32[]{:S(2)}) %collective-permute-start.3) | collective-permute-done | bytes 131104 | tf_op jit(solution)/shard_map/ppermute | solution.py:134
  57.6 2.4 %collective-permute-done.4 = bf16[16,16,256]{2,1,0:T(8,128)(2,1)S(1)} collective-permute-done((bf16[16,16,256]{2,1,0:T(8,128)(2,1)S(1)}, bf16[16,16,256]{2,1,0:T(8,128)(2,1)S(1)}, u32[]{:S(2)}, u32[]{:S(2)}) %collective-permute-start.4) | collective-permute-done | bytes 131104 | tf_op jit(solution)/shard_map/ppermute | solution.py:134
  60.1 4.6 %shard_map.38 = f32[32,2,16,256]{3,2,1,0:T(8,128)S(1)} custom-call(s32[32]{0:T(128)S(1)} %get-tuple-element.26.offsets_ref, s32[1]{0:T(128)} %constant.111.clone.1.base_ref, bf16[144,16,256]{2,1,0:T(8,128)(2,1)S(1)} %broadcast_dynamic-update-slice_fusion.white_ref), custom_call_target="tpu_custom_call" | custom-call | flops 16777216 | bytes 2228224 | tf_op jit(solution)/shard_map/pallas_call | solution.py:60
  64.7 0.9 %convert_element_type.78 = bf16[32,2,16,256]{3,2,1,0:T(8,128)(2,1)} convert(f32[32,2,16,256]{3,2,1,0:T(8,128)S(1)} %shard_map.38) | non-fusion elementwise | flops 262144 | bytes 1572864 | tf_op jit(solution)/shard_map/convert_element_type | solution.py:151
  65.6 0.4 collective-permute-start.8
  66.0 0.3 fusion.54
  66.4 4.6 %shard_map.39 = f32[32,2,16,256]{3,2,1,0:T(8,128)S(1)} custom-call(s32[32]{0:T(128)S(1)} %get-tuple-element.28.offsets_ref, s32[1]{0:T(128)} %constant.111.clone.1.base_ref, bf16[144,16,256]{2,1,0:T(8,128)(2,1)S(1)} %broadcast_dynamic-update-slice_fusion.white_ref), custom_call_target="tpu_custom_call" | custom-call | flops 16777216 | bytes 2228224 | tf_op jit(solution)/shard_map/pallas_call | solution.py:60
  71.0 0.9 convert_element_type.79
  71.9 1.7 %negate_convert_fusion.1 = (bf16[1024,16,32]{0,2,1:T(8,128)(2,1)}, bf16[1024,16,32]{0,2,1:T(8,128)(2,1)S(1)}) fusion(f32[1024,16]{0,1:T(8,128)S(1)} %get-tuple-element.18, f32[1024,32]{0,1:T(8,128)S(1)} %get-tuple-element.24, f32[1024,16]{0,1:T(8,128)S(1)} %get-tuple-element.17, f32[1024,32]{0,1:T(8,128)S(1)} %get-tuple-element.23), kind=kLoop, calls=%fused_computation.15 | loop fusion | flops 4718592 | bytes 2490368 | tf_op jit(solution)/shard_map/convert.2
  73.5 0.5 copy.30
  74.1 1.5 %copy.31 = bf16[1,1024,512]{2,1,0:T(8,128)(2,1)S(1)} copy(bf16[1,1024,512]{1,2,0:T(8,128)(2,1)} %bitcast.77) | data formatting | bytes 2097152 | tf_op jit(solution)/shard_map/neg | solution.py:29
  75.6 4.6 %shard_map.37 = f32[32,2,16,256]{3,2,1,0:T(8,128)S(1)} custom-call(s32[32]{0:T(128)S(1)} %get-tuple-element.25.offsets_ref, s32[1]{0:T(128)} %constant.111.clone.1.base_ref, bf16[144,16,256]{2,1,0:T(8,128)(2,1)S(1)} %broadcast_dynamic-update-slice_fusion.white_ref), custom_call_target="tpu_custom_call" | custom-call | flops 16777216 | bytes 2228224 | tf_op jit(solution)/shard_map/pallas_call | solution.py:60
  80.3 0.6 collective-permute-start.7
  80.9 4.6 %shard_map.40 = f32[32,2,16,256]{3,2,1,0:T(8,128)S(1)} custom-call(s32[32]{0:T(128)S(1)} %get-tuple-element.27.offsets_ref, s32[1]{0:T(128)} %constant.111.clone.1.base_ref, bf16[144,16,256]{2,1,0:T(8,128)(2,1)S(1)} %broadcast_dynamic-update-slice_fusion.white_ref), custom_call_target="tpu_custom_call" | custom-call | flops 16777216 | bytes 2228224 | tf_op jit(solution)/shard_map/pallas_call | solution.py:60
  85.5 0.4 convolution_bitcast_fusion
  85.9 1.5 %convolution_bitcast_fusion.2 = f32[32,16,512]{2,1,0:T(8,128)S(1)} fusion(bf16[32,2,16,256]{3,2,1,0:T(8,128)(2,1)} %collective-permute-done.8, s32[]{:T(128)S(6)} %select_n.105, bf16[1,1024,512]{2,1,0:T(8,128)(2,1)S(1)} %copy.30, bf16[1,1024,512]{2,1,0:T(8,128)(2,1)S(1)} %copy.31), kind=kOutput, calls=%fused_computation.19 | convolution fusion | flops 269484032 | bytes 3670020 | tf_op jit(solution)/shard_map/opck,pkl->ocl/dot_general | solution.py:157
  87.4 1.5 %convolution_bitcast_fusion.1 = f32[32,16,512]{2,1,0:T(8,128)S(1)} fusion(bf16[32,2,16,256]{3,2,1,0:T(8,128)(2,1)} %collective-permute-done.9, s32[]{:T(128)S(6)} %select_n.107, bf16[1,1024,512]{2,1,0:T(8,128)(2,1)S(1)} %copy.30, bf16[1,1024,512]{2,1,0:T(8,128)(2,1)S(1)} %copy.31), kind=kOutput, calls=%fused_computation.18 | convolution fusion | flops 269484032 | bytes 3670020 | tf_op jit(solution)/shard_map/opck,pkl->ocl/dot_general | solution.py:157
  88.9 0.3 collective-permute-done.7
  89.2 1.3 %fusion.11 = bf16[32,16,512]{2,1,0:T(8,128)(2,1)} fusion(f32[32,16,512]{2,1,0:T(8,128)S(1)} %convolution_bitcast_fusion, f32[32,16,512]{2,1,0:T(8,128)S(1)} %convolution_bitcast_fusion.1, f32[32,16,512]{2,1,0:T(8,128)S(1)} %convolution_bitcast_fusion.2, bf16[32,2,16,256]{3,2,1,0:T(8,128)(2,1)S(1)} %collective-permute-done.7, s32[]{:T(128)S(6)} %select_n.103, ...), kind=kOutput, calls=%fused_computation.25 | convolution fusion | flops 270794752 | bytes 6291460 | tf_op jit(solution)/shard_map/opck,pkl->ocl/dot_general | solution.py:157
  (28 shorter events, 0.8 us)
Async XLA Ops:
  14.3 7.4 %copy-start = (s32[1024]{0:T(1024)S(1)}, s32[1024]{0:T(1024)}, u32[]{:S(2)}) copy-start(s32[1024]{0:T(1024)} %param.4) | copy-start | bytes 12292
  14.3 7.9 %copy-start.1 = (s32[128]{0:T(128)S(1)}, s32[128]{0:T(128)}, u32[]{:S(2)}) copy-start(s32[128]{0:T(128)} %param.5) | copy-start | bytes 1540
  17.5 8.9 %all-to-all-start = ((bf16[4,2,8192]{2,1,0:T(2,128)(2,1)}), bf16[4,2,8192]{2,1,0:T(2,128)(2,1)S(1)}, u32[]{:S(2)}, u32[]{:S(2)}) async-start(bf16[4,2,8192]{2,1,0:T(2,128)(2,1)} %reshape.449), calls=%async_computation | async-start | bytes 262144 | tf_op jit(solution)/shard_map/all_to_all | solution.py:125
  28.6 7.1 %collective-permute-start = (bf16[16,16,256]{2,1,0:T(8,128)(2,1)S(1)}, bf16[16,16,256]{2,1,0:T(8,128)(2,1)S(1)}, u32[]{:S(2)}, u32[]{:S(2)}) collective-permute-start(bf16[16,16,256]{2,1,0:T(8,128)(2,1)S(1)} %bitcast.82), channel_id=1, source_target_pairs={{4,0},{8,4},{12,8},{16,12},{20,16},{24,20},{28,24},{5,1},{9,5},{13... | collective-permute-start | bytes 393224 | tf_op jit(solution)/shard_map/ppermute | solution.py:134
  29.9 9.8 %collective-permute-start.1 = (bf16[16,16,256]{2,1,0:T(8,128)(2,1)S(1)}, bf16[16,16,256]{2,1,0:T(8,128)(2,1)S(1)}, u32[]{:S(2)}, u32[]{:S(2)}) collective-permute-start(bf16[16,16,256]{2,1,0:T(8,128)(2,1)S(1)} %bitcast.83), channel_id=1, source_target_pairs={{8,0},{12,4},{16,8},{20,12},{24,16},{28,20},{9,1},{13,5},{17,9},{2... | collective-permute-start | bytes 393224 | tf_op jit(solution)/shard_map/ppermute | solution.py:134
  31.3 10.4 %collective-permute-start.2 = (bf16[16,16,256]{2,1,0:T(8,128)(2,1)S(1)}, bf16[16,16,256]{2,1,0:T(8,128)(2,1)S(1)}, u32[]{:S(2)}, u32[]{:S(2)}) collective-permute-start(bf16[16,16,256]{2,1,0:T(8,128)(2,1)S(1)} %bitcast.84), channel_id=1, source_target_pairs={{12,0},{16,4},{20,8},{24,12},{28,16},{13,1},{17,5},{21,9},{25,13},... | collective-permute-start | bytes 393224 | tf_op jit(solution)/shard_map/ppermute | solution.py:134
  32.6 25.0 %collective-permute-start.3 = (bf16[16,16,256]{2,1,0:T(8,128)(2,1)S(1)}, bf16[16,16,256]{2,1,0:T(8,128)(2,1)S(1)}, u32[]{:S(2)}, u32[]{:S(2)}) collective-permute-start(bf16[16,16,256]{2,1,0:T(8,128)(2,1)S(1)} %bitcast.85), channel_id=1, source_target_pairs={{16,0},{20,4},{24,8},{28,12},{17,1},{21,5},{25,9},{29,13},{18,2},{... | collective-permute-start | bytes 393224 | tf_op jit(solution)/shard_map/ppermute | solution.py:134
  33.9 26.1 %collective-permute-start.4 = (bf16[16,16,256]{2,1,0:T(8,128)(2,1)S(1)}, bf16[16,16,256]{2,1,0:T(8,128)(2,1)S(1)}, u32[]{:S(2)}, u32[]{:S(2)}) collective-permute-start(bf16[16,16,256]{2,1,0:T(8,128)(2,1)S(1)} %bitcast.86), channel_id=1, source_target_pairs={{20,0},{24,4},{28,8},{21,1},{25,5},{29,9},{22,2},{26,6},{30,10},{2... | collective-permute-start | bytes 393224 | tf_op jit(solution)/shard_map/ppermute | solution.py:134
  35.7 24.4 %collective-permute-start.5 = (bf16[16,16,256]{2,1,0:T(8,128)(2,1)S(1)}, bf16[16,16,256]{2,1,0:T(8,128)(2,1)S(1)}, u32[]{:S(2)}, u32[]{:S(2)}) collective-permute-start(bf16[16,16,256]{2,1,0:T(8,128)(2,1)S(1)} %bitcast.87), channel_id=1, source_target_pairs={{24,0},{28,4},{25,1},{29,5},{26,2},{30,6},{27,3},{31,7}} | collective-permute-start | bytes 393224 | tf_op jit(solution)/shard_map/ppermute | solution.py:134
  39.7 20.3 %collective-permute-start.6 = (bf16[16,16,256]{2,1,0:T(8,128)(2,1)S(1)}, bf16[16,16,256]{2,1,0:T(8,128)(2,1)S(1)}, u32[]{:S(2)}, u32[]{:S(2)}) collective-permute-start(bf16[16,16,256]{2,1,0:T(8,128)(2,1)S(1)} %bitcast.88), channel_id=1, source_target_pairs={{28,0},{29,1},{30,2},{31,3}} | collective-permute-start | bytes 393224 | tf_op jit(solution)/shard_map/ppermute | solution.py:134
  65.6 20.3 %collective-permute-start.8 = (bf16[32,2,16,256]{3,2,1,0:T(8,128)(2,1)}, bf16[32,2,16,256]{3,2,1,0:T(8,128)(2,1)}, u32[]{:S(2)}, u32[]{:S(2)}) collective-permute-start(bf16[32,2,16,256]{3,2,1,0:T(8,128)(2,1)} %convert_element_type.78), channel_id=1, source_target_pairs={{0,2},{1,3},{2,0},{3,1},{4,6},{5,7},{6,4},{7,5},{8,10},{9,11},{10,... | collective-permute-start | bytes 1572872 | tf_op jit(solution)/shard_map/ppermute | solution.py:154
  71.9 15.6 %collective-permute-start.9 = (bf16[32,2,16,256]{3,2,1,0:T(8,128)(2,1)}, bf16[32,2,16,256]{3,2,1,0:T(8,128)(2,1)}, u32[]{:S(2)}, u32[]{:S(2)}) collective-permute-start(bf16[32,2,16,256]{3,2,1,0:T(8,128)(2,1)} %convert_element_type.79), channel_id=1, source_target_pairs={{0,3},{1,0},{2,1},{3,2},{4,7},{5,4},{6,5},{7,6},{8,11},{9,8},{10,9... | collective-permute-start | bytes 1572872 | tf_op jit(solution)/shard_map/ppermute | solution.py:154
  80.3 8.9 %collective-permute-start.7 = (bf16[32,2,16,256]{3,2,1,0:T(8,128)(2,1)S(1)}, bf16[32,2,16,256]{3,2,1,0:T(8,128)(2,1)S(1)}, u32[]{:S(2)}, u32[]{:S(2)}) collective-permute-start(bf16[32,2,16,256]{3,2,1,0:T(8,128)(2,1)S(1)} %convert_element_type.75), channel_id=1, source_target_pairs={{0,1},{1,2},{2,3},{3,0},{4,5},{5,6},{6,7},{7,4},{8,9},{9,10},{10,1... | collective-permute-start | bytes 1572872 | tf_op jit(solution)/shard_map/ppermute | solution.py:154

commit v15 on v14

--- a/solution.py
+++ b/solution.py
@@ -128,10 +128,22 @@
     rows_white = jnp.transpose(freq_white, (0, 2, 1, 3)).reshape(ch_dev, 2 * windows, shard_bins)
     gx_count = lax.axis_size("gx")
     needed = -(-band_span // ch_dev)
+    hop = 4
+    top = min(needed, gx_count - 1)
     blocks = [rows_white]
-    for shift in range(1, min(needed, gx_count - 1) + 1):
-        pairs = [(src, src - shift) for src in range(shift, gx_count)]
-        blocks.append(lax.ppermute(rows_white, "gx", perm=pairs))
+    relayed = None
+    for shift in range(1, top + 1):
+        if shift < hop:
+            pairs = [(src, src - shift) for src in range(shift, gx_count)]
+            blocks.append(lax.ppermute(rows_white, "gx", perm=pairs))
+        elif shift == hop:
+            pairs = [(src, src - hop) for src in range(hop, gx_count)]
+            relayed = lax.ppermute(rows_white, "gx", perm=pairs)
+            blocks.append(relayed)
+        else:
+            step = shift - hop
+            pairs = [(src, src - step) for src in range(step, gx_count - hop)]
+            blocks.append(lax.ppermute(relayed, "gx", perm=pairs))
     missing = needed + 1 - len(blocks)
     if missing > 0:
         blocks.append(jnp.zeros((missing * ch_dev,) + rows_white.shape[1:], rows_white.dtype))

time: 91.6 us -> 95.3 us (1.040)
  waiting for transfers between devices: 26.5 us -> 28.1 us
  matrix products: 7.12 us -> 8.15 us
    ppermute x0 -> x4, waiting for transfers between devices: none -> 24 us  [the longest x1 16.4 us: local(): relayed = lax.ppermute(rows_white, 'gx', perm=pairs)]
    ppermute x7 -> x3, waiting for transfers between devices: 22.2 us -> 0.01 us  [local(): blocks.append(lax.ppermute(rows_white, 'gx', perm=pairs))]
    ppermute x0 -> x4, starting transfers between devices: none -> 5.16 us  [the longest x3 3.86 us: local(): blocks.append(lax.ppermute(relayed, 'gx', perm=pairs))]
    ppermute x7 -> x3, starting transfers between devices: 9.02 us -> 3.88 us  [local(): blocks.append(lax.ppermute(rows_white, 'gx', perm=pairs))]
    dot_general x4, matrix products: 4.66 us -> 5.69 us  [local(): jnp.einsum('opck,pkl->ocl', part, rows, preferred_element_type=jnp.float32)]
  transfers between devices with their start and end apart: 11 -> 11, of which waited for: 7 -> 5; matrix products, arithmetic and copies ran while one was open for 10% -> 10% of each run, Pallas kernels for 15% -> 15%
where the time goes in v15:
time: 95.3 us; the launch traced here: 93.9 us
  waiting for transfers between devices  28.1 us (29%)
  Pallas kernels  18.5 us (19%)
  starting transfers between devices  14.2 us (15%)
  other arithmetic  13.8 us (14%)
  local copies, waits for them, and re-layouts  10.9 us (11%)
  matrix products  8.15 us (9%)
    pallas_call x4, Pallas kernels, cross_spectra(): pl.pallas_call(kernel, grid_spec=pltpu.PrefetchScalarGridSpec(num_scalar_...  18.5 us
    ppermute x1, waiting for transfers between devices, local(): relayed = lax.ppermute(rows_white, 'gx', perm=pairs)  16.4 us
    ppermute x3, waiting for transfers between devices, local(): blocks.append(lax.ppermute(relayed, 'gx', perm=pairs))  7.61 us
    dot_general x4, matrix products, local(): jnp.einsum('opck,pkl->ocl', part, rows, preferred_element_type=jnp.float32)  5.69 us
    another operation x2, other arithmetic  5.32 us
    all_to_all x1, starting transfers between devices, local(): lax.all_to_all(white, 'gy', split_axis=3, concat_axis=1, tiled=True)  4.21 us
    all_to_all x1, waiting for transfers between devices, local(): lax.all_to_all(white, 'gy', split_axis=3, concat_axis=1, tiled=True)  4.02 us
    ppermute x3, starting transfers between devices, local(): blocks.append(lax.ppermute(rows_white, 'gx', perm=pairs))  3.88 us
  transfers between devices with their start and end apart: 11, of which 5 were waited for; matrix products, arithmetic and copies ran while one was open for 10% of the time, Pallas kernels for 15%

profile of v15, /device:TPU:0, one launch (start us, length us, event | category | flops | bytes accessed | tf_op | source)
XLA Modules:
  0.0 93.9 jit_solution(9220768683045705283)
XLA Ops:
  0.0 1.2 %fusion.52 = (f32[32,1024]{1,0:T(8,128)S(1)}, f32[32,1024]{1,0:T(8,128)S(1)}) fusion(s32[1024]{0:T(1024)} %param.4), kind=kLoop, calls=%fused_computation.86 | loop fusion | flops 458752 | bytes 266240 | tf_op jit(solution)/shard_map/cos | solution.py:90
  1.2 0.7 add_select_fusion.5
  1.9 1.8 %fusion.41 = (f32[64,1024]{1,0:T(8,128)S(1)}, f32[64,1024]{1,0:T(8,128)S(1)}) fusion(s32[1024]{0:T(1024)} %param.4, s32[64]{0:T(128)S(1)} %iota_multiply_fusion), kind=kLoop, calls=%fused_computation.69 | loop fusion | flops 917504 | bytes 528640 | tf_op jit(solution)/shard_map/cos | solution.py:90
  3.7 1.2 %reshape_reshape.3 = bf16[128,2048]{1,0:T(8,128)(2,1)S(1)} reshape(bf16[16,2,8192]{2,1,0:T(2,128)(2,1)} %param.3) | data formatting | bytes 1048576 | tf_op jit(solution)/shard_map/reshape;reshape | solution.py:103
  4.9 3.7 %subtract_convert_fusion = (bf16[64,32,1024]{2,1,0:T(8,128)(2,1)S(1)}, bf16[64,32,1024]{2,1,0:T(8,128)(2,1)S(1)}) fusion(f32[64,1024]{1,0:T(8,128)S(1)} %get-tuple-element.18, f32[32,1024]{1,0:T(8,128)S(1)} %get-tuple-element.24, f32[64,1024]{1,0:T(8,128)S(1)} %get-tuple-element.17, f32[32,1024]{1,0:T(8,128)S(1)} %get-tuple-element.23), kind=kLoop, calls=%fused_computation.5 | loop fusion | flops 18874368 | bytes 9175040 | tf_op jit(solution)/shard_map/convert.7
  8.5 2.5 %fusion.4 = f32[128,2048]{0,1:T(8,128)S(1)} fusion(bf16[128,2048]{1,0:T(8,128)(2,1)S(1)} %reshape_reshape.3, bf16[2048,1024]{1,0:T(8,128)(2,1)S(1)} %bitcast.76, bf16[2048,1024]{1,0:T(8,128)(2,1)S(1)} %bitcast.75), kind=kOutput, calls=%fused_computation.14 | convolution fusion | flops 1090519040 | bytes 9961472 | tf_op jit(solution)/shard_map/dot_general | solution.py:102
  11.0 0.3 copy.24
  11.3 0.9 reshape.439
  12.2 1.2 %fusion.68 = (f32[32,4,1,1024]{3,2,1,0:T(1,128)S(1)}, f32[32,4,1,1024]{3,2,1,0:T(1,128)S(1)}) fusion(f32[32,4,2,1024]{3,2,1,0:T(2,128)S(1)} %reshape.439), kind=kLoop, calls=%fused_computation.121 | loop fusion | bytes 2097152 | tf_op jit(solution)/shard_map/slice | solution.py:113
  13.4 0.2 cosine_round-nearest-even_fusion
  13.6 0.8 fusion.25
  14.5 0.2 concatenate.15
  14.8 0.2 multiply_convert_fusion
  15.0 0.8 copy.26
  15.8 1.7 %reshape.449 = bf16[4,2,8192]{2,1,0:T(2,128)(2,1)} reshape(bf16[1024,2,2,16]{3,2,1,0:T(2,128)(2,1)S(1)} %bitcast.73) | data formatting | bytes 262144
  17.5 4.2 %all-to-all-start = ((bf16[4,2,8192]{2,1,0:T(2,128)(2,1)}), bf16[4,2,8192]{2,1,0:T(2,128)(2,1)S(1)}, u32[]{:S(2)}, u32[]{:S(2)}) async-start(bf16[4,2,8192]{2,1,0:T(2,128)(2,1)} %reshape.449), calls=%async_computation | async-start | bytes 262144 | tf_op jit(solution)/shard_map/all_to_all | solution.py:125
  21.7 0.5 fusion.50
  22.4 4.0 %all-to-all-done = bf16[4,2,8192]{2,1,0:T(2,128)(2,1)S(1)} async-done(((bf16[4,2,8192]{2,1,0:T(2,128)(2,1)}), bf16[4,2,8192]{2,1,0:T(2,128)(2,1)S(1)}, u32[]{:S(2)}, u32[]{:S(2)}) %all-to-all-start) | async-done | bytes 131104 | tf_op jit(solution)/shard_map/all_to_all | solution.py:125
  26.4 0.7 reshape.450
  27.1 1.4 %copy.36 = bf16[16,2,2,4,256]{4,3,0,2,1:T(4,128)(2,1)S(1)} copy(bf16[16,2,2,4,256]{0,2,1,4,3:T(2,128)(2,1)S(1)} %bitcast.74) | data formatting | bytes 262144 | tf_op jit(solution)/shard_map/all_to_all | solution.py:125
  28.6 1.3 %collective-permute-start = (bf16[16,16,256]{2,1,0:T(8,128)(2,1)S(1)}, bf16[16,16,256]{2,1,0:T(8,128)(2,1)S(1)}, u32[]{:S(2)}, u32[]{:S(2)}) collective-permute-start(bf16[16,16,256]{2,1,0:T(8,128)(2,1)S(1)} %bitcast.82), channel_id=1, source_target_pairs={{4,0},{8,4},{12,8},{16,12},{20,16},{24,20},{28,24},{5,1},{9,5},{13... | collective-permute-start | bytes 393224 | tf_op jit(solution)/shard_map/ppermute | solution.py:138
  29.9 1.3 %collective-permute-start.1 = (bf16[16,16,256]{2,1,0:T(8,128)(2,1)S(1)}, bf16[16,16,256]{2,1,0:T(8,128)(2,1)S(1)}, u32[]{:S(2)}, u32[]{:S(2)}) collective-permute-start(bf16[16,16,256]{2,1,0:T(8,128)(2,1)S(1)} %bitcast.83), channel_id=1, source_target_pairs={{8,0},{12,4},{16,8},{20,12},{24,16},{28,20},{9,1},{13,5},{17,9},{2... | collective-permute-start | bytes 393224 | tf_op jit(solution)/shard_map/ppermute | solution.py:138
  31.2 1.3 %collective-permute-start.3 = (bf16[16,16,256]{2,1,0:T(8,128)(2,1)S(1)}, bf16[16,16,256]{2,1,0:T(8,128)(2,1)S(1)}, u32[]{:S(2)}, u32[]{:S(2)}) collective-permute-start(bf16[16,16,256]{2,1,0:T(8,128)(2,1)S(1)} %bitcast.84), channel_id=1, source_target_pairs={{16,0},{20,4},{24,8},{28,12},{17,1},{21,5},{25,9},{29,13},{18,2},{... | collective-permute-start | bytes 393224 | tf_op jit(solution)/shard_map/ppermute | solution.py:141
  32.6 1.3 %collective-permute-start.2 = (bf16[16,16,256]{2,1,0:T(8,128)(2,1)S(1)}, bf16[16,16,256]{2,1,0:T(8,128)(2,1)S(1)}, u32[]{:S(2)}, u32[]{:S(2)}) collective-permute-start(bf16[16,16,256]{2,1,0:T(8,128)(2,1)S(1)} %bitcast.85), channel_id=1, source_target_pairs={{12,0},{16,4},{20,8},{24,12},{28,16},{13,1},{17,5},{21,9},{25,13},... | collective-permute-start | bytes 393224 | tf_op jit(solution)/shard_map/ppermute | solution.py:138
  33.9 16.4 %collective-permute-done.3 = bf16[16,16,256]{2,1,0:T(8,128)(2,1)S(1)} collective-permute-done((bf16[16,16,256]{2,1,0:T(8,128)(2,1)S(1)}, bf16[16,16,256]{2,1,0:T(8,128)(2,1)S(1)}, u32[]{:S(2)}, u32[]{:S(2)}) %collective-permute-start.3) | collective-permute-done | bytes 131104 | tf_op jit(solution)/shard_map/ppermute | solution.py:141
  50.3 1.3 %collective-permute-start.4 = (bf16[16,16,256]{2,1,0:T(8,128)(2,1)S(1)}, bf16[16,16,256]{2,1,0:T(8,128)(2,1)S(1)}, u32[]{:S(2)}, u32[]{:S(2)}) collective-permute-start(bf16[16,16,256]{2,1,0:T(8,128)(2,1)S(1)} %collective-permute-done.3), channel_id=1, source_target_pairs={{4,0},{8,4},{12,8},{5,1},{9,5},{13,9},{6,2},{10,6},{14,10},{7,3},{... | collective-permute-start | bytes 393224 | tf_op jit(solution)/shard_map/ppermute | solution.py:146
  51.6 1.3 %collective-permute-start.5 = (bf16[16,16,256]{2,1,0:T(8,128)(2,1)S(1)}, bf16[16,16,256]{2,1,0:T(8,128)(2,1)S(1)}, u32[]{:S(2)}, u32[]{:S(2)}) collective-permute-start(bf16[16,16,256]{2,1,0:T(8,128)(2,1)S(1)} %collective-permute-done.3), channel_id=1, source_target_pairs={{8,0},{12,4},{9,1},{13,5},{10,2},{14,6},{11,3},{15,7}} | collective-permute-start | bytes 393224 | tf_op jit(solution)/shard_map/ppermute | solution.py:146
  52.9 1.3 %collective-permute-start.6 = (bf16[16,16,256]{2,1,0:T(8,128)(2,1)S(1)}, bf16[16,16,256]{2,1,0:T(8,128)(2,1)S(1)}, u32[]{:S(2)}, u32[]{:S(2)}) collective-permute-start(bf16[16,16,256]{2,1,0:T(8,128)(2,1)S(1)} %collective-permute-done.3), channel_id=1, source_target_pairs={{12,0},{13,1},{14,2},{15,3}} | collective-permute-start | bytes 393224 | tf_op jit(solution)/shard_map/ppermute | solution.py:146
  54.3 2.9 %collective-permute-done.4 = bf16[16,16,256]{2,1,0:T(8,128)(2,1)S(1)} collective-permute-done((bf16[16,16,256]{2,1,0:T(8,128)(2,1)S(1)}, bf16[16,16,256]{2,1,0:T(8,128)(2,1)S(1)}, u32[]{:S(2)}, u32[]{:S(2)}) %collective-permute-start.4) | collective-permute-done | bytes 131104 | tf_op jit(solution)/shard_map/ppermute | solution.py:146
  57.2 1.3 %collective-permute-done.5 = bf16[16,16,256]{2,1,0:T(8,128)(2,1)S(1)} collective-permute-done((bf16[16,16,256]{2,1,0:T(8,128)(2,1)S(1)}, bf16[16,16,256]{2,1,0:T(8,128)(2,1)S(1)}, u32[]{:S(2)}, u32[]{:S(2)}) %collective-permute-start.5) | collective-permute-done | bytes 131104 | tf_op jit(solution)/shard_map/ppermute | solution.py:146
  58.5 3.5 %collective-permute-done.6 = bf16[16,16,256]{2,1,0:T(8,128)(2,1)S(1)} collective-permute-done((bf16[16,16,256]{2,1,0:T(8,128)(2,1)S(1)}, bf16[16,16,256]{2,1,0:T(8,128)(2,1)S(1)}, u32[]{:S(2)}, u32[]{:S(2)}) %collective-permute-start.6) | collective-permute-done | bytes 131104 | tf_op jit(solution)/shard_map/ppermute | solution.py:146
  62.0 4.6 %shard_map.38 = f32[32,2,16,256]{3,2,1,0:T(8,128)S(1)} custom-call(s32[32]{0:T(128)S(1)} %get-tuple-element.26.offsets_ref, s32[1]{0:T(128)} %constant.111.clone.1.base_ref, bf16[144,16,256]{2,1,0:T(8,128)(2,1)S(1)} %broadcast_dynamic-update-slice_fusion.white_ref), custom_call_target="tpu_custom_call" | custom-call | flops 16777216 | bytes 2228224 | tf_op jit(solution)/shard_map/pallas_call | solution.py:60
  66.6 0.9 convert_element_type.78
  67.5 0.4 collective-permute-start.8
  67.9 4.6 %shard_map.39 = f32[32,2,16,256]{3,2,1,0:T(8,128)S(1)} custom-call(s32[32]{0:T(128)S(1)} %get-tuple-element.28.offsets_ref, s32[1]{0:T(128)} %constant.111.clone.1.base_ref, bf16[144,16,256]{2,1,0:T(8,128)(2,1)S(1)} %broadcast_dynamic-update-slice_fusion.white_ref), custom_call_target="tpu_custom_call" | custom-call | flops 16777216 | bytes 2228224 | tf_op jit(solution)/shard_map/pallas_call | solution.py:60
  72.5 0.9 convert_element_type.79
  73.4 0.3 fusion.54
  73.8 4.6 %shard_map.37 = f32[32,2,16,256]{3,2,1,0:T(8,128)S(1)} custom-call(s32[32]{0:T(128)S(1)} %get-tuple-element.27.offsets_ref, s32[1]{0:T(128)} %constant.111.clone.1.base_ref, bf16[144,16,256]{2,1,0:T(8,128)(2,1)S(1)} %broadcast_dynamic-update-slice_fusion.white_ref), custom_call_target="tpu_custom_call" | custom-call | flops 16777216 | bytes 2228224 | tf_op jit(solution)/shard_map/pallas_call | solution.py:60
  78.4 0.9 convert_element_type.75
  79.3 0.5 collective-permute-start.7
  79.8 1.7 %negate_convert_fusion.1 = (bf16[1024,16,32]{0,2,1:T(8,128)(2,1)}, bf16[1024,16,32]{0,2,1:T(8,128)(2,1)S(1)}) fusion(f32[1024,16]{0,1:T(8,128)S(1)} %get-tuple-element.16, f32[1024,32]{0,1:T(8,128)S(1)} %get-tuple-element.20, f32[1024,16]{0,1:T(8,128)S(1)} %get-tuple-element.15, f32[1024,32]{0,1:T(8,128)S(1)} %get-tuple-element.19), kind=kLoop, calls=%fused_computation.15 | loop fusion | flops 4718592 | bytes 2490368 | tf_op jit(solution)/shard_map/convert.2
  81.5 0.5 copy.30
  82.0 1.5 %copy.31 = bf16[1,1024,512]{2,1,0:T(8,128)(2,1)S(1)} copy(bf16[1,1024,512]{1,2,0:T(8,128)(2,1)} %bitcast.77) | data formatting | bytes 2097152 | tf_op jit(solution)/shard_map/neg | solution.py:29
  83.5 4.6 %shard_map.40 = f32[32,2,16,256]{3,2,1,0:T(8,128)S(1)} custom-call(s32[32]{0:T(128)S(1)} %get-tuple-element.25.offsets_ref, s32[1]{0:T(128)} %constant.111.clone.1.base_ref, bf16[144,16,256]{2,1,0:T(8,128)(2,1)S(1)} %broadcast_dynamic-update-slice_fusion.white_ref), custom_call_target="tpu_custom_call" | custom-call | flops 16777216 | bytes 2228224 | tf_op jit(solution)/shard_map/pallas_call | solution.py:60
  88.2 1.5 %convolution_bitcast_fusion.2 = f32[32,16,512]{2,1,0:T(8,128)S(1)} fusion(bf16[32,2,16,256]{3,2,1,0:T(8,128)(2,1)} %collective-permute-done.8, s32[]{:T(128)S(6)} %select_n.105, bf16[1,1024,512]{2,1,0:T(8,128)(2,1)S(1)} %copy.30, bf16[1,1024,512]{2,1,0:T(8,128)(2,1)S(1)} %copy.31), kind=kOutput, calls=%fused_computation.19 | convolution fusion | flops 269484032 | bytes 3670020 | tf_op jit(solution)/shard_map/opck,pkl->ocl/dot_general | solution.py:169
  89.7 1.5 %convolution_bitcast_fusion.1 = f32[32,16,512]{2,1,0:T(8,128)S(1)} fusion(bf16[32,2,16,256]{3,2,1,0:T(8,128)(2,1)} %collective-permute-done.9, s32[]{:T(128)S(6)} %select_n.107, bf16[1,1024,512]{2,1,0:T(8,128)(2,1)S(1)} %copy.30, bf16[1,1024,512]{2,1,0:T(8,128)(2,1)S(1)} %copy.31), kind=kOutput, calls=%fused_computation.18 | convolution fusion | flops 269484032 | bytes 3670020 | tf_op jit(solution)/shard_map/opck,pkl->ocl/dot_general | solution.py:169
  91.2 1.5 %fusion.8 = f32[32,16,512]{2,1,0:T(8,128)S(1)} fusion(f32[32,16,512]{2,1,0:T(8,128)S(1)} %convolution_bitcast_fusion.1, f32[32,16,512]{2,1,0:T(8,128)S(1)} %convolution_bitcast_fusion.2, bf16[32,2,16,256]{3,2,1,0:T(8,128)(2,1)} %collective-permute-done.7, s32[]{:T(128)S(6)} %select_n.103, bf16[1,1024,512]{2,1,0:T(8,128)(2,1)S(1)} %copy.30, ...), kind=kOutput, calls=%fused_computation.22 | convolution fusion | flops 270008320 | bytes 5767172 | tf_op jit(solution)/shard_map/opck,pkl->ocl/dot_general | solution.py:169
  92.7 1.2 %fusion.11 = bf16[32,16,512]{2,1,0:T(8,128)(2,1)} fusion(f32[32,16,512]{2,1,0:T(8,128)S(1)} %fusion.8, s32[]{:T(128)S(6)} %select_n.109, bf16[1,1024,512]{2,1,0:T(8,128)(2,1)S(1)} %copy.30, bf16[1,1024,512]{2,1,0:T(8,128)(2,1)S(1)} %copy.31, f32[32,2,16,256]{3,2,1,0:T(8,128)S(1)} %shard_map.40), kind=kOutput, calls=%fused_computation.25 | convolution fusion | flops 270532608 | bytes 4718596 | tf_op jit(solution)/shard_map/opck,pkl->ocl/dot_general | solution.py:169
  (28 shorter events, 0.6 us)
Async XLA Ops:
  14.3 7.4 %copy-start = (s32[1024]{0:T(1024)S(1)}, s32[1024]{0:T(1024)}, u32[]{:S(2)}) copy-start(s32[1024]{0:T(1024)} %param.4) | copy-start | bytes 12292
  14.3 7.9 %copy-start.1 = (s32[128]{0:T(128)S(1)}, s32[128]{0:T(128)}, u32[]{:S(2)}) copy-start(s32[128]{0:T(128)} %param.5) | copy-start | bytes 1540
  17.5 8.9 %all-to-all-start = ((bf16[4,2,8192]{2,1,0:T(2,128)(2,1)}), bf16[4,2,8192]{2,1,0:T(2,128)(2,1)S(1)}, u32[]{:S(2)}, u32[]{:S(2)}) async-start(bf16[4,2,8192]{2,1,0:T(2,128)(2,1)} %reshape.449), calls=%async_computation | async-start | bytes 262144 | tf_op jit(solution)/shard_map/all_to_all | solution.py:125
  28.6 24.3 %collective-permute-start = (bf16[16,16,256]{2,1,0:T(8,128)(2,1)S(1)}, bf16[16,16,256]{2,1,0:T(8,128)(2,1)S(1)}, u32[]{:S(2)}, u32[]{:S(2)}) collective-permute-start(bf16[16,16,256]{2,1,0:T(8,128)(2,1)S(1)} %bitcast.82), channel_id=1, source_target_pairs={{4,0},{8,4},{12,8},{16,12},{20,16},{24,20},{28,24},{5,1},{9,5},{13... | collective-permute-start | bytes 393224 | tf_op jit(solution)/shard_map/ppermute | solution.py:138
  29.9 24.3 %collective-permute-start.1 = (bf16[16,16,256]{2,1,0:T(8,128)(2,1)S(1)}, bf16[16,16,256]{2,1,0:T(8,128)(2,1)S(1)}, u32[]{:S(2)}, u32[]{:S(2)}) collective-permute-start(bf16[16,16,256]{2,1,0:T(8,128)(2,1)S(1)} %bitcast.83), channel_id=1, source_target_pairs={{8,0},{12,4},{16,8},{20,12},{24,16},{28,20},{9,1},{13,5},{17,9},{2... | collective-permute-start | bytes 393224 | tf_op jit(solution)/shard_map/ppermute | solution.py:138
  31.2 19.1 %collective-permute-start.3 = (bf16[16,16,256]{2,1,0:T(8,128)(2,1)S(1)}, bf16[16,16,256]{2,1,0:T(8,128)(2,1)S(1)}, u32[]{:S(2)}, u32[]{:S(2)}) collective-permute-start(bf16[16,16,256]{2,1,0:T(8,128)(2,1)S(1)} %bitcast.84), channel_id=1, source_target_pairs={{16,0},{20,4},{24,8},{28,12},{17,1},{21,5},{25,9},{29,13},{18,2},{... | collective-permute-start | bytes 393224 | tf_op jit(solution)/shard_map/ppermute | solution.py:141
  32.6 21.7 %collective-permute-start.2 = (bf16[16,16,256]{2,1,0:T(8,128)(2,1)S(1)}, bf16[16,16,256]{2,1,0:T(8,128)(2,1)S(1)}, u32[]{:S(2)}, u32[]{:S(2)}) collective-permute-start(bf16[16,16,256]{2,1,0:T(8,128)(2,1)S(1)} %bitcast.85), channel_id=1, source_target_pairs={{12,0},{16,4},{20,8},{24,12},{28,16},{13,1},{17,5},{21,9},{25,13},... | collective-permute-start | bytes 393224 | tf_op jit(solution)/shard_map/ppermute | solution.py:138
  50.3 6.8 %collective-permute-start.4 = (bf16[16,16,256]{2,1,0:T(8,128)(2,1)S(1)}, bf16[16,16,256]{2,1,0:T(8,128)(2,1)S(1)}, u32[]{:S(2)}, u32[]{:S(2)}) collective-permute-start(bf16[16,16,256]{2,1,0:T(8,128)(2,1)S(1)} %collective-permute-done.3), channel_id=1, source_target_pairs={{4,0},{8,4},{12,8},{5,1},{9,5},{13,9},{6,2},{10,6},{14,10},{7,3},{... | collective-permute-start | bytes 393224 | tf_op jit(solution)/shard_map/ppermute | solution.py:146
  51.6 6.9 %collective-permute-start.5 = (bf16[16,16,256]{2,1,0:T(8,128)(2,1)S(1)}, bf16[16,16,256]{2,1,0:T(8,128)(2,1)S(1)}, u32[]{:S(2)}, u32[]{:S(2)}) collective-permute-start(bf16[16,16,256]{2,1,0:T(8,128)(2,1)S(1)} %collective-permute-done.3), channel_id=1, source_target_pairs={{8,0},{12,4},{9,1},{13,5},{10,2},{14,6},{11,3},{15,7}} | collective-permute-start | bytes 393224 | tf_op jit(solution)/shard_map/ppermute | solution.py:146
  52.9 9.0 %collective-permute-start.6 = (bf16[16,16,256]{2,1,0:T(8,128)(2,1)S(1)}, bf16[16,16,256]{2,1,0:T(8,128)(2,1)S(1)}, u32[]{:S(2)}, u32[]{:S(2)}) collective-permute-start(bf16[16,16,256]{2,1,0:T(8,128)(2,1)S(1)} %collective-permute-done.3), channel_id=1, source_target_pairs={{12,0},{13,1},{14,2},{15,3}} | collective-permute-start | bytes 393224 | tf_op jit(solution)/shard_map/ppermute | solution.py:146
  67.5 20.7 %collective-permute-start.8 = (bf16[32,2,16,256]{3,2,1,0:T(8,128)(2,1)}, bf16[32,2,16,256]{3,2,1,0:T(8,128)(2,1)}, u32[]{:S(2)}, u32[]{:S(2)}) collective-permute-start(bf16[32,2,16,256]{3,2,1,0:T(8,128)(2,1)} %convert_element_type.78), channel_id=1, source_target_pairs={{0,2},{1,3},{2,0},{3,1},{4,6},{5,7},{6,4},{7,5},{8,10},{9,11},{10,... | collective-permute-start | bytes 1572872 | tf_op jit(solution)/shard_map/ppermute | solution.py:166
  73.4 16.2 %collective-permute-start.9 = (bf16[32,2,16,256]{3,2,1,0:T(8,128)(2,1)}, bf16[32,2,16,256]{3,2,1,0:T(8,128)(2,1)}, u32[]{:S(2)}, u32[]{:S(2)}) collective-permute-start(bf16[32,2,16,256]{3,2,1,0:T(8,128)(2,1)} %convert_element_type.79), channel_id=1, source_target_pairs={{0,3},{1,0},{2,1},{3,2},{4,7},{5,4},{6,5},{7,6},{8,11},{9,8},{10,9... | collective-permute-start | bytes 1572872 | tf_op jit(solution)/shard_map/ppermute | solution.py:166
  79.3 11.9 %collective-permute-start.7 = (bf16[32,2,16,256]{3,2,1,0:T(8,128)(2,1)}, bf16[32,2,16,256]{3,2,1,0:T(8,128)(2,1)}, u32[]{:S(2)}, u32[]{:S(2)}) collective-permute-start(bf16[32,2,16,256]{3,2,1,0:T(8,128)(2,1)} %convert_element_type.75), channel_id=1, source_target_pairs={{0,1},{1,2},{2,3},{3,0},{4,5},{5,6},{6,7},{7,4},{8,9},{9,10},{10,1... | collective-permute-start | bytes 1572872 | tf_op jit(solution)/shard_map/ppermute | solution.py:166

commit v16 on v12

--- a/solution.py
+++ b/solution.py
@@ -160,14 +160,11 @@
     blocks = [rows_white]
     source = rows_white
     for shift in range(1, real_count):
-        if shift == near_count:
-            source, _ = lax.optimization_barrier((rows_white, blocks))
         pairs = [(src, src - shift) for src in range(shift, gx_count)]
         blocks.append(lax.ppermute(source, "gx", perm=pairs))
     zero_block = jnp.zeros_like(rows_white)
     blocks += [zero_block] * (needed + 1 - len(blocks))
     near = jnp.concatenate(blocks[:near_count] + [zero_block] * (len(blocks) - near_count), axis=0)
-    far = jnp.concatenate([rows_white] + [zero_block] * (near_count - 1) + blocks[near_count:], axis=0)
     split_row = near_count * ch_dev
     end_row = len(blocks) * ch_dev
     gy_count = lax.axis_size("gy")
@@ -181,6 +178,8 @@
         lax.dynamic_slice_in_dim(offsets, lax.rem(me + shift, gy_count) * off_dev, off_dev) for shift in shifts
     ]
     near_parts = [cross_spectra(near, offs, ch_dev, 0, split_row) for offs in dest_offsets]
+    far_blocks, near_parts = lax.optimization_barrier((blocks[near_count:], near_parts))
+    far = jnp.concatenate([rows_white] + [zero_block] * (near_count - 1) + list(far_blocks), axis=0)
     lagged = None
     for shift, offs, near_part in zip(shifts, dest_offsets, near_parts):
         part = cross_spectra(far, offs, ch_dev, split_row, end_row, near_part).astype(jnp.bfloat16)

time: 97.8 us -> 98.7 us (level)
  the two profiles are of different devices: /device:TPU:0 before, /device:TPU:5 now
where the time goes in v16:
time: 98.7 us; the launch traced here: 98.4 us
  Pallas kernels  26.8 us (27%)
  waiting for transfers between devices  26.3 us (27%)
  starting transfers between devices  19.2 us (19%)
  local copies, waits for them, and re-layouts  10.6 us (11%)
  other arithmetic  9.87 us (10%)
  matrix products  5.03 us (5%)
    pallas_call x8, Pallas kernels, cross_spectra(): pl.pallas_call(kernel, grid_spec=pltpu.PrefetchScalarGridSpec(num_scalar_...  26.8 us
    ppermute x7, waiting for transfers between devices, local(): blocks.append(lax.ppermute(source, 'gx', perm=pairs))  15.8 us
    ppermute x3, waiting for transfers between devices, local(): part = lax.ppermute(part, 'gy', perm=pairs)  9.83 us
    ppermute x7, starting transfers between devices, local(): blocks.append(lax.ppermute(source, 'gx', perm=pairs))  9.05 us
    ppermute x3, starting transfers between devices, local(): part = lax.ppermute(part, 'gy', perm=pairs)  6.14 us
    another operation x2, other arithmetic  4.39 us
    all_to_all x1, starting transfers between devices, local(): lax.all_to_all(white, 'gy', split_axis=3, concat_axis=0, tiled=True)  3.97 us
    unnamed x16, local copies, waits for them, and re-layouts  2.7 us
  transfers between devices with their start and end apart: 11, of which 4 were waited for; matrix products, arithmetic and copies ran while one was open for 5% of the time, Pallas kernels for 24%

profile of v16, /device:TPU:5, one launch (start us, length us, event | category | flops | bytes accessed | tf_op | source)
XLA Modules:
  0.0 98.4 jit_solution(16625556972590273047)
XLA Ops:
  0.0 1.2 %fusion.52 = (f32[32,1024]{1,0:T(8,128)S(1)}, f32[32,1024]{1,0:T(8,128)S(1)}) fusion(s32[1024]{0:T(1024)} %param.4), kind=kLoop, calls=%fused_computation.87 | loop fusion | flops 458752 | bytes 266240 | tf_op jit(solution)/shard_map/cos | solution.py:115
  1.2 0.7 add_select_fusion.5
  1.9 1.8 %fusion.41 = (f32[64,1024]{1,0:T(8,128)S(1)}, f32[64,1024]{1,0:T(8,128)S(1)}) fusion(s32[1024]{0:T(1024)} %param.4, s32[64]{0:T(128)S(1)} %iota_multiply_fusion), kind=kLoop, calls=%fused_computation.71 | loop fusion | flops 917504 | bytes 528640 | tf_op jit(solution)/shard_map/cos | solution.py:115
  3.7 1.3 %copy.29 = bf16[2,16,8192]{2,1,0:T(8,128)(2,1)S(1)} copy(bf16[2,16,8192]{2,0,1:T(2,128)(2,1)} %bitcast.88) | data formatting | bytes 1048576 | tf_op jit(solution)/shard_map/transpose | solution.py:149
  5.0 0.4 reshape_reshape.3
  5.4 0.3 copy.30
  5.7 3.7 %subtract_convert_fusion = (bf16[64,32,1024]{2,1,0:T(8,128)(2,1)S(1)}, bf16[64,32,1024]{2,1,0:T(8,128)(2,1)S(1)}) fusion(f32[64,1024]{1,0:T(8,128)S(1)} %get-tuple-element.34, f32[32,1024]{1,0:T(8,128)S(1)} %get-tuple-element.40, f32[64,1024]{1,0:T(8,128)S(1)} %get-tuple-element.33, f32[32,1024]{1,0:T(8,128)S(1)} %get-tuple-element.39), kind=kLoop, calls=%fused_computation.5 | loop fusion | flops 18874368 | bytes 9175040 | tf_op jit(solution)/shard_map/convert.7
  9.4 2.5 %fusion.4 = f32[128,2048]{0,1:T(8,128)S(1)} fusion(bf16[128,2048]{1,0:T(8,128)(2,1)S(1)} %bitcast.89, bf16[2048,1024]{1,0:T(8,128)(2,1)S(1)} %bitcast.81, bf16[2048,1024]{1,0:T(8,128)(2,1)S(1)} %bitcast.80), kind=kOutput, calls=%fused_computation.14 | convolution fusion | flops 1090519040 | bytes 9961472 | tf_op jit(solution)/shard_map/dot_general | solution.py:128
  11.8 0.3 copy.31
  12.2 0.9 reshape.435
  13.1 0.8 fusion.68
  14.1 0.2 fusion.25
  14.5 0.2 concatenate.24
  14.9 0.8 copy.33
  15.8 1.7 %reshape.445 = bf16[4,2,8192]{2,1,0:T(2,128)(2,1)} reshape(bf16[1024,2,2,16]{3,2,1,0:T(2,128)(2,1)S(1)} %bitcast.78) | data formatting | bytes 262144
  17.5 4.0 %all-to-all-start = ((bf16[4,2,8192]{2,1,0:T(2,128)(2,1)}), bf16[4,2,8192]{2,1,0:T(2,128)(2,1)S(1)}, u32[]{:S(2)}, u32[]{:S(2)}) async-start(bf16[4,2,8192]{2,1,0:T(2,128)(2,1)} %reshape.445), calls=%async_computation | async-start | bytes 262144 | tf_op jit(solution)/shard_map/all_to_all | solution.py:152
  21.5 0.5 fusion.50
  22.0 0.3 fusion.54
  22.4 0.7 negate_convert_fusion.1
  23.1 0.5 copy.37
  23.7 0.5 copy.38
  24.4 0.7 all-to-all-done
  25.1 0.7 reshape.446
  25.8 1.4 %copy.43 = bf16[2,16,2,4,256]{4,3,1,2,0:T(4,128)(2,1)S(1)} copy(bf16[2,16,2,4,256]{1,2,0,4,3:T(2,128)(2,1)S(1)} %bitcast.79) | data formatting | bytes 262144 | tf_op jit(solution)/shard_map/all_to_all | solution.py:152
  27.3 1.9 %collective-permute-start.4 = (bf16[16,16,256]{2,1,0:T(8,128)(2,1)S(1)}, bf16[16,16,256]{2,1,0:T(8,128)(2,1)S(1)}, u32[]{:S(2)}, u32[]{:S(2)}) collective-permute-start(bf16[16,16,256]{2,1,0:T(8,128)(2,1)S(1)} %bitcast.90), channel_id=1, source_target_pairs={{4,0},{8,4},{12,8},{16,12},{20,16},{24,20},{28,24},{5,1},{9,5},{13... | collective-permute-start | bytes 393224 | tf_op jit(solution)/shard_map/ppermute | solution.py:164
  29.3 1.3 %collective-permute-start.5 = (bf16[16,16,256]{2,1,0:T(8,128)(2,1)S(1)}, bf16[16,16,256]{2,1,0:T(8,128)(2,1)S(1)}, u32[]{:S(2)}, u32[]{:S(2)}) collective-permute-start(bf16[16,16,256]{2,1,0:T(8,128)(2,1)S(1)} %bitcast.91), channel_id=1, source_target_pairs={{8,0},{12,4},{16,8},{20,12},{24,16},{28,20},{9,1},{13,5},{17,9},{2... | collective-permute-start | bytes 393224 | tf_op jit(solution)/shard_map/ppermute | solution.py:164
  30.6 1.3 %collective-permute-start.6 = (bf16[16,16,256]{2,1,0:T(8,128)(2,1)S(1)}, bf16[16,16,256]{2,1,0:T(8,128)(2,1)S(1)}, u32[]{:S(2)}, u32[]{:S(2)}) collective-permute-start(bf16[16,16,256]{2,1,0:T(8,128)(2,1)S(1)} %bitcast.92), channel_id=1, source_target_pairs={{12,0},{16,4},{20,8},{24,12},{28,16},{13,1},{17,5},{21,9},{25,13},... | collective-permute-start | bytes 393224 | tf_op jit(solution)/shard_map/ppermute | solution.py:164
  31.9 1.3 %collective-permute-start = (bf16[16,16,256]{2,1,0:T(8,128)(2,1)S(1)}, bf16[16,16,256]{2,1,0:T(8,128)(2,1)S(1)}, u32[]{:S(2)}, u32[]{:S(2)}) collective-permute-start(bf16[16,16,256]{2,1,0:T(8,128)(2,1)S(1)} %bitcast.93), channel_id=1, source_target_pairs={{16,0},{20,4},{24,8},{28,12},{17,1},{21,5},{25,9},{29,13},{18,2},{... | collective-permute-start | bytes 393224 | tf_op jit(solution)/shard_map/ppermute | solution.py:164
  33.2 1.3 %collective-permute-start.1 = (bf16[16,16,256]{2,1,0:T(8,128)(2,1)S(1)}, bf16[16,16,256]{2,1,0:T(8,128)(2,1)S(1)}, u32[]{:S(2)}, u32[]{:S(2)}) collective-permute-start(bf16[16,16,256]{2,1,0:T(8,128)(2,1)S(1)} %bitcast.94), channel_id=1, source_target_pairs={{20,0},{24,4},{28,8},{21,1},{25,5},{29,9},{22,2},{26,6},{30,10},{2... | collective-permute-start | bytes 393224 | tf_op jit(solution)/shard_map/ppermute | solution.py:164
  34.6 1.3 %collective-permute-start.2 = (bf16[16,16,256]{2,1,0:T(8,128)(2,1)S(1)}, bf16[16,16,256]{2,1,0:T(8,128)(2,1)S(1)}, u32[]{:S(2)}, u32[]{:S(2)}) collective-permute-start(bf16[16,16,256]{2,1,0:T(8,128)(2,1)S(1)} %bitcast.95), channel_id=1, source_target_pairs={{24,0},{28,4},{25,1},{29,5},{26,2},{30,6},{27,3},{31,7}} | collective-permute-start | bytes 393224 | tf_op jit(solution)/shard_map/ppermute | solution.py:164
  35.9 0.7 collective-permute-start.3
  36.6 15.8 %collective-permute-done.6 = bf16[16,16,256]{2,1,0:T(8,128)(2,1)S(1)} collective-permute-done((bf16[16,16,256]{2,1,0:T(8,128)(2,1)S(1)}, bf16[16,16,256]{2,1,0:T(8,128)(2,1)S(1)}, u32[]{:S(2)}, u32[]{:S(2)}) %collective-permute-start.6) | collective-permute-done | bytes 131104 | tf_op jit(solution)/shard_map/ppermute | solution.py:164
  52.5 3.3 %shard_map.38.rest_0_ = f32[32,2,16,256]{3,2,1,0:T(8,128)S(1)} custom-call(s32[32]{0:T(128)S(1)} %get-tuple-element.44.offsets_ref, bf16[144,16,256]{2,1,0:T(8,128)(2,1)S(1)} %broadcast_dynamic-update-slice_fusion.white_ref), custom_call_target="tpu_custom_call" | custom-call | flops 2147483648 | bytes 3276800 | tf_op jit(solution)/shard_map/pallas_call | solution.py:84
  55.8 3.3 %shard_map.39.rest_0_ = f32[32,2,16,256]{3,2,1,0:T(8,128)S(1)} custom-call(s32[32]{0:T(128)S(1)} %get-tuple-element.43.offsets_ref, bf16[144,16,256]{2,1,0:T(8,128)(2,1)S(1)} %broadcast_dynamic-update-slice_fusion.white_ref), custom_call_target="tpu_custom_call" | custom-call | flops 2147483648 | bytes 3276800 | tf_op jit(solution)/shard_map/pallas_call | solution.py:84
  59.0 2.5 %shard_map.40.rest_0_ = f32[32,2,16,256]{3,2,1,0:T(8,128)S(1)} custom-call(s32[32]{0:T(128)S(1)} %get-tuple-element.46.offsets_ref, bf16[144,16,256]{2,1,0:T(8,128)(2,1)S(1)} %broadcast_dynamic-update-slice_fusion.white_ref), custom_call_target="tpu_custom_call" | custom-call | flops 2147483648 | bytes 3276800 | tf_op jit(solution)/shard_map/pallas_call | solution.py:84
  61.5 3.0 %shard_map.37.rest_0_ = f32[32,2,16,256]{3,2,1,0:T(8,128)S(1)} custom-call(s32[32]{0:T(128)S(1)} %get-tuple-element.45.offsets_ref, bf16[144,16,256]{2,1,0:T(8,128)(2,1)S(1)} %broadcast_dynamic-update-slice_fusion.white_ref), custom_call_target="tpu_custom_call" | custom-call | flops 2147483648 | bytes 3276800 | tf_op jit(solution)/shard_map/pallas_call | solution.py:84
  64.7 3.3 %shard_map.41 = f32[32,2,16,256]{3,2,1,0:T(8,128)S(1)} custom-call(s32[32]{0:T(128)S(1)} %get-tuple-element.45.offsets_ref, bf16[144,16,256]{2,1,0:T(8,128)(2,1)S(1)} %constant_dynamic-update-slice_fusion.4.white_ref, f32[32,2,16,256]{3,2,1,0:T(8,128)S(1)} %shard_map.37.rest_0_), custom_call_target="tpu_custom_call" | custom-call | flops 2147483648 | bytes 3276800 | tf_op jit(solution)/shard_map/pallas_call | solution.py:84
  68.1 2.9 %collective-permute-start.7 = (bf16[32,2,16,256]{3,2,1,0:T(8,128)(2,1)S(1)}, bf16[32,2,16,256]{3,2,1,0:T(8,128)(2,1)S(1)}, u32[]{:S(2)}, u32[]{:S(2)}) collective-permute-start(bf16[32,2,16,256]{3,2,1,0:T(8,128)(2,1)S(1)} %convert_element_type.75), channel_id=1, source_target_pairs={{0,1},{1,2},{2,3},{3,0},{4,5},{5,6},{6,7},{7,4},{8,9},{9,10},{10,1... | collective-permute-start | bytes 1572872 | tf_op jit(solution)/shard_map/ppermute | solution.py:188
  71.0 3.6 %shard_map.42 = f32[32,2,16,256]{3,2,1,0:T(8,128)S(1)} custom-call(s32[32]{0:T(128)S(1)} %get-tuple-element.44.offsets_ref, bf16[144,16,256]{2,1,0:T(8,128)(2,1)S(1)} %constant_dynamic-update-slice_fusion.4.white_ref, f32[32,2,16,256]{3,2,1,0:T(8,128)S(1)} %shard_map.38.rest_0_), custom_call_target="tpu_custom_call" | custom-call | flops 2147483648 | bytes 3276800 | tf_op jit(solution)/shard_map/pallas_call | solution.py:84
  74.7 3.2 %collective-permute-start.8 = (bf16[32,2,16,256]{3,2,1,0:T(8,128)(2,1)S(1)}, bf16[32,2,16,256]{3,2,1,0:T(8,128)(2,1)S(1)}, u32[]{:S(2)}, u32[]{:S(2)}) collective-permute-start(bf16[32,2,16,256]{3,2,1,0:T(8,128)(2,1)S(1)} %convert_element_type.78), channel_id=1, source_target_pairs={{0,2},{1,3},{2,0},{3,1},{4,6},{5,7},{6,4},{7,5},{8,10},{9,11},{10,... | collective-permute-start | bytes 1572872 | tf_op jit(solution)/shard_map/ppermute | solution.py:188
  77.9 3.5 %shard_map.43 = f32[32,2,16,256]{3,2,1,0:T(8,128)S(1)} custom-call(s32[32]{0:T(128)S(1)} %get-tuple-element.43.offsets_ref, bf16[144,16,256]{2,1,0:T(8,128)(2,1)S(1)} %constant_dynamic-update-slice_fusion.4.white_ref, f32[32,2,16,256]{3,2,1,0:T(8,128)S(1)} %shard_map.39.rest_0_), custom_call_target="tpu_custom_call" | custom-call | flops 2147483648 | bytes 3276800 | tf_op jit(solution)/shard_map/pallas_call | solution.py:84
  81.5 4.5 %shard_map.44 = f32[32,2,16,256]{3,2,1,0:T(8,128)S(1)} custom-call(s32[32]{0:T(128)S(1)} %get-tuple-element.46.offsets_ref, bf16[144,16,256]{2,1,0:T(8,128)(2,1)S(1)} %constant_dynamic-update-slice_fusion.4.white_ref, f32[32,2,16,256]{3,2,1,0:T(8,128)S(1)} %shard_map.40.rest_0_), custom_call_target="tpu_custom_call" | custom-call | flops 2147483648 | bytes 3276800 | tf_op jit(solution)/shard_map/pallas_call | solution.py:84
  86.0 0.4 convolution_bitcast_fusion
  86.4 6.1 %collective-permute-done.8 = bf16[32,2,16,256]{3,2,1,0:T(8,128)(2,1)S(1)} collective-permute-done((bf16[32,2,16,256]{3,2,1,0:T(8,128)(2,1)S(1)}, bf16[32,2,16,256]{3,2,1,0:T(8,128)(2,1)S(1)}, u32[]{:S(2)}, u32[]{:S(2)}) %collective-permute-start.8) | collective-permute-done | bytes 524320 | tf_op jit(solution)/shard_map/ppermute | solution.py:188
  92.5 0.4 convolution_bitcast_fusion.2
  93.0 3.7 %collective-permute-done.9 = bf16[32,2,16,256]{3,2,1,0:T(8,128)(2,1)S(1)} collective-permute-done((bf16[32,2,16,256]{3,2,1,0:T(8,128)(2,1)S(1)}, bf16[32,2,16,256]{3,2,1,0:T(8,128)(2,1)S(1)}, u32[]{:S(2)}, u32[]{:S(2)}) %collective-permute-start.9) | collective-permute-done | bytes 524320 | tf_op jit(solution)/shard_map/ppermute | solution.py:188
  96.7 0.4 convolution_bitcast_fusion.1
  97.1 1.3 %fusion.11 = bf16[32,16,512]{2,1,0:T(8,128)(2,1)} fusion(f32[32,16,512]{2,1,0:T(8,128)S(1)} %convolution_bitcast_fusion, f32[32,16,512]{2,1,0:T(8,128)S(1)} %convolution_bitcast_fusion.1, f32[32,16,512]{2,1,0:T(8,128)S(1)} %convolution_bitcast_fusion.2, bf16[32,2,16,256]{3,2,1,0:T(8,128)(2,1)S(1)} %collective-permute-done.7, s32[]{:T(128)S(6)} %select_n.106, ...), kind=kOutput, calls=%fused_computation.25 | convolution fusion | flops 270794752 | bytes 6291460 | tf_op jit(solution)/shard_map/opck,pkl->ocl/dot_general | solution.py:191
  (38 shorter events, 1.4 us)
Async XLA Ops:
  14.3 7.1 %copy-start = (s32[1024]{0:T(1024)S(1)}, s32[1024]{0:T(1024)}, u32[]{:S(2)}) copy-start(s32[1024]{0:T(1024)} %param.4) | copy-start | bytes 12292
  17.5 7.6 %all-to-all-start = ((bf16[4,2,8192]{2,1,0:T(2,128)(2,1)}), bf16[4,2,8192]{2,1,0:T(2,128)(2,1)S(1)}, u32[]{:S(2)}, u32[]{:S(2)}) async-start(bf16[4,2,8192]{2,1,0:T(2,128)(2,1)} %reshape.445), calls=%async_computation | async-start | bytes 262144 | tf_op jit(solution)/shard_map/all_to_all | solution.py:152
  23.1 1.2 %copy-start.1 = (s32[128]{0:T(128)S(1)}, s32[128]{0:T(128)}, u32[]{:S(2)}) copy-start(s32[128]{0:T(128)} %param.5) | copy-start | bytes 1540
  27.3 7.3 %collective-permute-start.4 = (bf16[16,16,256]{2,1,0:T(8,128)(2,1)S(1)}, bf16[16,16,256]{2,1,0:T(8,128)(2,1)S(1)}, u32[]{:S(2)}, u32[]{:S(2)}) collective-permute-start(bf16[16,16,256]{2,1,0:T(8,128)(2,1)S(1)} %bitcast.90), channel_id=1, source_target_pairs={{4,0},{8,4},{12,8},{16,12},{20,16},{24,20},{28,24},{5,1},{9,5},{13... | collective-permute-start | bytes 393224 | tf_op jit(solution)/shard_map/ppermute | solution.py:164
  29.3 6.7 %collective-permute-start.5 = (bf16[16,16,256]{2,1,0:T(8,128)(2,1)S(1)}, bf16[16,16,256]{2,1,0:T(8,128)(2,1)S(1)}, u32[]{:S(2)}, u32[]{:S(2)}) collective-permute-start(bf16[16,16,256]{2,1,0:T(8,128)(2,1)S(1)} %bitcast.91), channel_id=1, source_target_pairs={{8,0},{12,4},{16,8},{20,12},{24,16},{28,20},{9,1},{13,5},{17,9},{2... | collective-permute-start | bytes 393224 | tf_op jit(solution)/shard_map/ppermute | solution.py:164
  30.6 21.8 %collective-permute-start.6 = (bf16[16,16,256]{2,1,0:T(8,128)(2,1)S(1)}, bf16[16,16,256]{2,1,0:T(8,128)(2,1)S(1)}, u32[]{:S(2)}, u32[]{:S(2)}) collective-permute-start(bf16[16,16,256]{2,1,0:T(8,128)(2,1)S(1)} %bitcast.92), channel_id=1, source_target_pairs={{12,0},{16,4},{20,8},{24,12},{28,16},{13,1},{17,5},{21,9},{25,13},... | collective-permute-start | bytes 393224 | tf_op jit(solution)/shard_map/ppermute | solution.py:164
  31.9 32.6 %collective-permute-start = (bf16[16,16,256]{2,1,0:T(8,128)(2,1)S(1)}, bf16[16,16,256]{2,1,0:T(8,128)(2,1)S(1)}, u32[]{:S(2)}, u32[]{:S(2)}) collective-permute-start(bf16[16,16,256]{2,1,0:T(8,128)(2,1)S(1)} %bitcast.93), channel_id=1, source_target_pairs={{16,0},{20,4},{24,8},{28,12},{17,1},{21,5},{25,9},{29,13},{18,2},{... | collective-permute-start | bytes 393224 | tf_op jit(solution)/shard_map/ppermute | solution.py:164
  33.2 31.3 %collective-permute-start.1 = (bf16[16,16,256]{2,1,0:T(8,128)(2,1)S(1)}, bf16[16,16,256]{2,1,0:T(8,128)(2,1)S(1)}, u32[]{:S(2)}, u32[]{:S(2)}) collective-permute-start(bf16[16,16,256]{2,1,0:T(8,128)(2,1)S(1)} %bitcast.94), channel_id=1, source_target_pairs={{20,0},{24,4},{28,8},{21,1},{25,5},{29,9},{22,2},{26,6},{30,10},{2... | collective-permute-start | bytes 393224 | tf_op jit(solution)/shard_map/ppermute | solution.py:164
  34.6 29.9 %collective-permute-start.2 = (bf16[16,16,256]{2,1,0:T(8,128)(2,1)S(1)}, bf16[16,16,256]{2,1,0:T(8,128)(2,1)S(1)}, u32[]{:S(2)}, u32[]{:S(2)}) collective-permute-start(bf16[16,16,256]{2,1,0:T(8,128)(2,1)S(1)} %bitcast.95), channel_id=1, source_target_pairs={{24,0},{28,4},{25,1},{29,5},{26,2},{30,6},{27,3},{31,7}} | collective-permute-start | bytes 393224 | tf_op jit(solution)/shard_map/ppermute | solution.py:164
  35.9 28.6 %collective-permute-start.3 = (bf16[16,16,256]{2,1,0:T(8,128)(2,1)S(1)}, bf16[16,16,256]{2,1,0:T(8,128)(2,1)S(1)}, u32[]{:S(2)}, u32[]{:S(2)}) collective-permute-start(bf16[16,16,256]{2,1,0:T(8,128)(2,1)S(1)} %bitcast.96), channel_id=1, source_target_pairs={{28,0},{29,1},{30,2},{31,3}} | collective-permute-start | bytes 393224 | tf_op jit(solution)/shard_map/ppermute | solution.py:164
  68.1 29.0 %collective-permute-start.7 = (bf16[32,2,16,256]{3,2,1,0:T(8,128)(2,1)S(1)}, bf16[32,2,16,256]{3,2,1,0:T(8,128)(2,1)S(1)}, u32[]{:S(2)}, u32[]{:S(2)}) collective-permute-start(bf16[32,2,16,256]{3,2,1,0:T(8,128)(2,1)S(1)} %convert_element_type.75), channel_id=1, source_target_pairs={{0,1},{1,2},{2,3},{3,0},{4,5},{5,6},{6,7},{7,4},{8,9},{9,10},{10,1... | collective-permute-start | bytes 1572872 | tf_op jit(solution)/shard_map/ppermute | solution.py:188
  74.7 17.8 %collective-permute-start.8 = (bf16[32,2,16,256]{3,2,1,0:T(8,128)(2,1)S(1)}, bf16[32,2,16,256]{3,2,1,0:T(8,128)(2,1)S(1)}, u32[]{:S(2)}, u32[]{:S(2)}) collective-permute-start(bf16[32,2,16,256]{3,2,1,0:T(8,128)(2,1)S(1)} %convert_element_type.78), channel_id=1, source_target_pairs={{0,2},{1,3},{2,0},{3,1},{4,6},{5,7},{6,4},{7,5},{8,10},{9,11},{10,... | collective-permute-start | bytes 1572872 | tf_op jit(solution)/shard_map/ppermute | solution.py:188
  81.4 15.3 %collective-permute-start.9 = (bf16[32,2,16,256]{3,2,1,0:T(8,128)(2,1)S(1)}, bf16[32,2,16,256]{3,2,1,0:T(8,128)(2,1)S(1)}, u32[]{:S(2)}, u32[]{:S(2)}) collective-permute-start(bf16[32,2,16,256]{3,2,1,0:T(8,128)(2,1)S(1)} %convert_element_type.79), channel_id=1, source_target_pairs={{0,3},{1,0},{2,1},{3,2},{4,7},{5,4},{6,5},{7,6},{8,11},{9,8},{10,9... | collective-permute-start | bytes 1572872 | tf_op jit(solution)/shard_map/ppermute | solution.py:188

commit v17 on v14

--- a/solution.py
+++ b/solution.py
@@ -122,9 +122,18 @@
     band_span = pair_offsets.shape[0]
     spectra = forward_spectra(records.reshape(ch_dev * win_dev, samples), kept_bins)
     white = whiten(spectra).reshape(ch_dev, win_dev, 2, bin_count)
-    freq_white = lax.all_to_all(white, "gy", split_axis=3, concat_axis=1, tiled=True)
+    gy_count = lax.axis_size("gy")
+    shard_bins = bin_count // gy_count
+    me = lax.axis_index("gy")
+    slots = []
+    for shift in range(gy_count):
+        dest = lax.rem(me + shift, gy_count)
+        piece = lax.dynamic_slice_in_dim(white, dest * shard_bins, shard_bins, 3)
+        if shift:
+            piece = lax.ppermute(piece, "gy", perm=[(src, (src + shift) % gy_count) for src in range(gy_count)])
+        slots.append(piece)
+    freq_white = jnp.concatenate(slots, axis=1)
     windows = freq_white.shape[1]
-    shard_bins = freq_white.shape[3]
     rows_white = jnp.transpose(freq_white, (0, 2, 1, 3)).reshape(ch_dev, 2 * windows, shard_bins)
     gx_count = lax.axis_size("gx")
     needed = -(-band_span // ch_dev)

time: 91.6 us -> 85.5 us (0.933)
  local copies, waits for them, and re-layouts: 10.9 us -> 6.19 us
  waiting for transfers between devices: 26.5 us -> 24 us
  starting transfers between devices: 14.2 us -> 15.7 us
    ppermute x0 -> x3, starting transfers between devices: none -> 4.46 us  [local(): lax.ppermute(piece, 'gy', perm=[(src, (src + shift) % gy_count) for src i...]
    all_to_all x1 -> x0, starting transfers between devices: 4.21 us -> none  [local(): lax.all_to_all(white, 'gy', split_axis=3, concat_axis=1, tiled=True)]
    all_to_all x1 -> x0, waiting for transfers between devices: 4.02 us -> none  [local(): lax.all_to_all(white, 'gy', split_axis=3, concat_axis=1, tiled=True)]
    unnamed x14 -> x12, local copies, waits for them, and re-layouts: 2.6 us -> 0.1 us
    all_to_all x2 -> x0, local copies, waits for them, and re-layouts: 1.41 us -> none  [local(): lax.all_to_all(white, 'gy', split_axis=3, concat_axis=1, tiled=True)]
    ppermute x3, starting transfers between devices: 0.93 us -> 2.05 us  [local(): part = lax.ppermute(part, 'gy', perm=pairs)]
    ppermute x0 -> x3, waiting for transfers between devices: none -> 0.94 us  [local(): lax.ppermute(piece, 'gy', perm=[(src, (src + shift) % gy_count) for src i...]
  transfers between devices with their start and end apart: 11 -> 13, of which waited for: 7 -> 7; matrix products, arithmetic and copies ran while one was open for 10% -> 11% of each run, Pallas kernels for 15% -> 16%
where the time goes in v17:
time: 85.5 us; the launch traced here: 85 us
  waiting for transfers between devices  24 us (28%)
  Pallas kernels  18.5 us (22%)
  starting transfers between devices  15.7 us (18%)
  other arithmetic  13.1 us (15%)
  matrix products  7.12 us (8%)
  local copies, waits for them, and re-layouts  6.19 us (7%)
    ppermute x7, waiting for transfers between devices, local(): blocks.append(lax.ppermute(rows_white, 'gx', perm=pairs))  22.4 us
    pallas_call x4, Pallas kernels, cross_spectra(): pl.pallas_call(kernel, grid_spec=pltpu.PrefetchScalarGridSpec(num_scalar_...  18.5 us
    ppermute x7, starting transfers between devices, local(): blocks.append(lax.ppermute(rows_white, 'gx', perm=pairs))  9.2 us
    another operation x2, other arithmetic  5.34 us
    dot_general x4, matrix products, local(): jnp.einsum('opck,pkl->ocl', part, rows, preferred_element_type=jnp.float32)  4.66 us
    ppermute x3, starting transfers between devices, local(): lax.ppermute(piece, 'gy', perm=[(src, (src + shift) % gy_count) for src i...  4.46 us
    dot_general x1, matrix products, forward_spectra(): jnp.dot(record_rows.reshape(row_count * block_count, block_len), small_ta...  2.46 us
    ppermute x3, starting transfers between devices, local(): part = lax.ppermute(part, 'gy', perm=pairs)  2.05 us
  transfers between devices with their start and end apart: 13, of which 7 were waited for; matrix products, arithmetic and copies ran while one was open for 11% of the time, Pallas kernels for 16%

profile of v17, /device:TPU:0, one launch (start us, length us, event | category | flops | bytes accessed | tf_op | source)
XLA Modules:
  0.0 85.0 jit_solution(10499058576475644976)
XLA Ops:
  0.0 1.2 %fusion.52 = (f32[32,1024]{1,0:T(8,128)S(1)}, f32[32,1024]{1,0:T(8,128)S(1)}) fusion(s32[1024]{0:T(1024)} %param.4), kind=kLoop, calls=%fused_computation.87 | loop fusion | flops 458752 | bytes 266240 | tf_op jit(solution)/shard_map/cos | solution.py:90
  1.2 0.7 add_select_fusion.5
  1.9 1.8 %fusion.41 = (f32[64,1024]{1,0:T(8,128)S(1)}, f32[64,1024]{1,0:T(8,128)S(1)}) fusion(s32[1024]{0:T(1024)} %param.4, s32[64]{0:T(128)S(1)} %iota_multiply_fusion), kind=kLoop, calls=%fused_computation.70 | loop fusion | flops 917504 | bytes 528640 | tf_op jit(solution)/shard_map/cos | solution.py:90
  3.7 1.2 %reshape_reshape.3 = bf16[128,2048]{1,0:T(8,128)(2,1)S(1)} reshape(bf16[16,2,8192]{2,1,0:T(2,128)(2,1)} %param.3) | data formatting | bytes 1048576 | tf_op jit(solution)/shard_map/reshape;reshape | solution.py:103
  4.9 3.7 %subtract_convert_fusion = (bf16[64,32,1024]{2,1,0:T(8,128)(2,1)S(1)}, bf16[64,32,1024]{2,1,0:T(8,128)(2,1)S(1)}) fusion(f32[64,1024]{1,0:T(8,128)S(1)} %get-tuple-element.20, f32[32,1024]{1,0:T(8,128)S(1)} %get-tuple-element.26, f32[64,1024]{1,0:T(8,128)S(1)} %get-tuple-element.19, f32[32,1024]{1,0:T(8,128)S(1)} %get-tuple-element.25), kind=kLoop, calls=%fused_computation.5 | loop fusion | flops 18874368 | bytes 9175040 | tf_op jit(solution)/shard_map/convert.7
  8.5 2.5 %fusion.4 = f32[128,2048]{0,1:T(8,128)S(1)} fusion(bf16[128,2048]{1,0:T(8,128)(2,1)S(1)} %reshape_reshape.3, bf16[2048,1024]{1,0:T(8,128)(2,1)S(1)} %bitcast.69, bf16[2048,1024]{1,0:T(8,128)(2,1)S(1)} %bitcast.68), kind=kOutput, calls=%fused_computation.14 | convolution fusion | flops 1090519040 | bytes 9961472 | tf_op jit(solution)/shard_map/dot_general | solution.py:102
  11.0 0.3 copy.4
  11.3 0.9 %reshape.439 = f32[32,4,2,1024]{3,2,1,0:T(2,128)S(1)} reshape(f32[128,2048]{1,0:T(8,128)S(1)} %copy.4) | data formatting | bytes 2097152 | tf_op jit(solution)/shard_map/reshape | solution.py:106
  12.2 1.2 %fusion.68 = (f32[32,4,1,1024]{3,2,1,0:T(1,128)S(1)}, f32[32,4,1,1024]{3,2,1,0:T(1,128)S(1)}) fusion(f32[32,4,2,1024]{3,2,1,0:T(2,128)S(1)} %reshape.439), kind=kLoop, calls=%fused_computation.126 | loop fusion | bytes 2097152 | tf_op jit(solution)/shard_map/slice | solution.py:113
  13.4 0.2 cosine_round-nearest-even_fusion
  13.6 0.8 fusion.25
  14.5 0.2 concatenate.18
  14.8 0.2 multiply_convert_fusion
  15.1 0.5 collective-permute-start
  15.6 2.6 %collective-permute-start.1 = (bf16[16,2,2,256]{3,2,1,0:T(2,128)(2,1)S(1)}, bf16[16,2,2,256]{3,2,1,0:T(2,128)(2,1)S(1)}, u32[]{:S(2)}, u32[]{:S(2)}) collective-permute-start(bf16[16,2,2,256]{3,2,1,0:T(2,128)(2,1)S(1)} %get-tuple-element.17), channel_id=1, source_target_pairs={{0,2},{1,3},{2,0},{3,1},{4,6},{5,7},{6,4},{7,5},{8,10},{9,11},{10,... | collective-permute-start | bytes 98312 | tf_op jit(solution)/shard_map/ppermute | solution.py:133
  18.2 1.4 %collective-permute-start.2 = (bf16[16,2,2,256]{3,2,1,0:T(2,128)(2,1)S(1)}, bf16[16,2,2,256]{3,2,1,0:T(2,128)(2,1)S(1)}, u32[]{:S(2)}, u32[]{:S(2)}) collective-permute-start(bf16[16,2,2,256]{3,2,1,0:T(2,128)(2,1)S(1)} %get-tuple-element.16), channel_id=1, source_target_pairs={{0,3},{1,0},{2,1},{3,2},{4,7},{5,4},{6,5},{7,6},{8,11},{9,8},{10,9... | collective-permute-start | bytes 98312 | tf_op jit(solution)/shard_map/ppermute | solution.py:133
  19.5 0.5 fusion.50
  20.2 0.9 %collective-permute-done.2 = bf16[16,2,2,256]{3,2,1,0:T(2,128)(2,1)S(1)} collective-permute-done((bf16[16,2,2,256]{3,2,1,0:T(2,128)(2,1)S(1)}, bf16[16,2,2,256]{3,2,1,0:T(2,128)(2,1)S(1)}, u32[]{:S(2)}, u32[]{:S(2)}) %collective-permute-start.2) | collective-permute-done | bytes 32800 | tf_op jit(solution)/shard_map/ppermute | solution.py:133
  21.1 0.2 maximum_bitcast_fusion
  21.4 1.3 %collective-permute-start.3 = (bf16[16,16,256]{2,1,0:T(8,128)(2,1)S(1)}, bf16[16,16,256]{2,1,0:T(8,128)(2,1)S(1)}, u32[]{:S(2)}, u32[]{:S(2)}) collective-permute-start(bf16[16,16,256]{2,1,0:T(8,128)(2,1)S(1)} %bitcast.72), channel_id=1, source_target_pairs={{4,0},{8,4},{12,8},{16,12},{20,16},{24,20},{28,24},{5,1},{9,5},{13... | collective-permute-start | bytes 393224 | tf_op jit(solution)/shard_map/ppermute | solution.py:143
  22.7 1.3 %collective-permute-start.4 = (bf16[16,16,256]{2,1,0:T(8,128)(2,1)S(1)}, bf16[16,16,256]{2,1,0:T(8,128)(2,1)S(1)}, u32[]{:S(2)}, u32[]{:S(2)}) collective-permute-start(bf16[16,16,256]{2,1,0:T(8,128)(2,1)S(1)} %bitcast.73), channel_id=1, source_target_pairs={{8,0},{12,4},{16,8},{20,12},{24,16},{28,20},{9,1},{13,5},{17,9},{2... | collective-permute-start | bytes 393224 | tf_op jit(solution)/shard_map/ppermute | solution.py:143
  24.0 1.3 %collective-permute-start.5 = (bf16[16,16,256]{2,1,0:T(8,128)(2,1)S(1)}, bf16[16,16,256]{2,1,0:T(8,128)(2,1)S(1)}, u32[]{:S(2)}, u32[]{:S(2)}) collective-permute-start(bf16[16,16,256]{2,1,0:T(8,128)(2,1)S(1)} %bitcast.74), channel_id=1, source_target_pairs={{12,0},{16,4},{20,8},{24,12},{28,16},{13,1},{17,5},{21,9},{25,13},... | collective-permute-start | bytes 393224 | tf_op jit(solution)/shard_map/ppermute | solution.py:143
  25.3 1.3 %collective-permute-start.6 = (bf16[16,16,256]{2,1,0:T(8,128)(2,1)S(1)}, bf16[16,16,256]{2,1,0:T(8,128)(2,1)S(1)}, u32[]{:S(2)}, u32[]{:S(2)}) collective-permute-start(bf16[16,16,256]{2,1,0:T(8,128)(2,1)S(1)} %bitcast.75), channel_id=1, source_target_pairs={{16,0},{20,4},{24,8},{28,12},{17,1},{21,5},{25,9},{29,13},{18,2},{... | collective-permute-start | bytes 393224 | tf_op jit(solution)/shard_map/ppermute | solution.py:143
  26.6 1.3 %collective-permute-start.7 = (bf16[16,16,256]{2,1,0:T(8,128)(2,1)S(1)}, bf16[16,16,256]{2,1,0:T(8,128)(2,1)S(1)}, u32[]{:S(2)}, u32[]{:S(2)}) collective-permute-start(bf16[16,16,256]{2,1,0:T(8,128)(2,1)S(1)} %bitcast.76), channel_id=1, source_target_pairs={{20,0},{24,4},{28,8},{21,1},{25,5},{29,9},{22,2},{26,6},{30,10},{2... | collective-permute-start | bytes 393224 | tf_op jit(solution)/shard_map/ppermute | solution.py:143
  27.9 1.2 %collective-permute-done.3 = bf16[16,16,256]{2,1,0:T(8,128)(2,1)S(1)} collective-permute-done((bf16[16,16,256]{2,1,0:T(8,128)(2,1)S(1)}, bf16[16,16,256]{2,1,0:T(8,128)(2,1)S(1)}, u32[]{:S(2)}, u32[]{:S(2)}) %collective-permute-start.3) | collective-permute-done | bytes 131104 | tf_op jit(solution)/shard_map/ppermute | solution.py:143
  29.1 1.3 %collective-permute-start.8 = (bf16[16,16,256]{2,1,0:T(8,128)(2,1)S(1)}, bf16[16,16,256]{2,1,0:T(8,128)(2,1)S(1)}, u32[]{:S(2)}, u32[]{:S(2)}) collective-permute-start(bf16[16,16,256]{2,1,0:T(8,128)(2,1)S(1)} %bitcast.77), channel_id=1, source_target_pairs={{24,0},{28,4},{25,1},{29,5},{26,2},{30,6},{27,3},{31,7}} | collective-permute-start | bytes 393224 | tf_op jit(solution)/shard_map/ppermute | solution.py:143
  30.4 2.7 %collective-permute-done.4 = bf16[16,16,256]{2,1,0:T(8,128)(2,1)S(1)} collective-permute-done((bf16[16,16,256]{2,1,0:T(8,128)(2,1)S(1)}, bf16[16,16,256]{2,1,0:T(8,128)(2,1)S(1)}, u32[]{:S(2)}, u32[]{:S(2)}) %collective-permute-start.4) | collective-permute-done | bytes 131104 | tf_op jit(solution)/shard_map/ppermute | solution.py:143
  33.1 1.5 %collective-permute-start.9 = (bf16[16,16,256]{2,1,0:T(8,128)(2,1)S(1)}, bf16[16,16,256]{2,1,0:T(8,128)(2,1)S(1)}, u32[]{:S(2)}, u32[]{:S(2)}) collective-permute-start(bf16[16,16,256]{2,1,0:T(8,128)(2,1)S(1)} %bitcast.78), channel_id=1, source_target_pairs={{28,0},{29,1},{30,2},{31,3}} | collective-permute-start | bytes 393224 | tf_op jit(solution)/shard_map/ppermute | solution.py:143
  34.6 0.5 collective-permute-done.5
  35.1 15.9 %collective-permute-done.6 = bf16[16,16,256]{2,1,0:T(8,128)(2,1)S(1)} collective-permute-done((bf16[16,16,256]{2,1,0:T(8,128)(2,1)S(1)}, bf16[16,16,256]{2,1,0:T(8,128)(2,1)S(1)}, u32[]{:S(2)}, u32[]{:S(2)}) %collective-permute-start.6) | collective-permute-done | bytes 131104 | tf_op jit(solution)/shard_map/ppermute | solution.py:143
  50.9 2.1 %collective-permute-done.7 = bf16[16,16,256]{2,1,0:T(8,128)(2,1)S(1)} collective-permute-done((bf16[16,16,256]{2,1,0:T(8,128)(2,1)S(1)}, bf16[16,16,256]{2,1,0:T(8,128)(2,1)S(1)}, u32[]{:S(2)}, u32[]{:S(2)}) %collective-permute-start.7) | collective-permute-done | bytes 131104 | tf_op jit(solution)/shard_map/ppermute | solution.py:143
  53.2 4.6 %shard_map.38 = f32[32,2,16,256]{3,2,1,0:T(8,128)S(1)} custom-call(s32[32]{0:T(128)S(1)} %get-tuple-element.30.offsets_ref, s32[1]{0:T(128)} %constant.111.clone.1.base_ref, bf16[144,16,256]{2,1,0:T(8,128)(2,1)S(1)} %broadcast_dynamic-update-slice_fusion.white_ref), custom_call_target="tpu_custom_call" | custom-call | flops 16777216 | bytes 2228224 | tf_op jit(solution)/shard_map/pallas_call | solution.py:60
  57.8 0.9 %convert_element_type.78 = bf16[32,2,16,256]{3,2,1,0:T(8,128)(2,1)} convert(f32[32,2,16,256]{3,2,1,0:T(8,128)S(1)} %shard_map.38) | non-fusion elementwise | flops 262144 | bytes 1572864 | tf_op jit(solution)/shard_map/convert_element_type | solution.py:160
  58.7 1.5 %collective-permute-start.11 = (bf16[32,2,16,256]{3,2,1,0:T(8,128)(2,1)}, bf16[32,2,16,256]{3,2,1,0:T(8,128)(2,1)}, u32[]{:S(2)}, u32[]{:S(2)}) collective-permute-start(bf16[32,2,16,256]{3,2,1,0:T(8,128)(2,1)} %convert_element_type.78), channel_id=1, source_target_pairs={{0,2},{1,3},{2,0},{3,1},{4,6},{5,7},{6,4},{7,5},{8,10},{9,11},{10,... | collective-permute-start | bytes 1572872 | tf_op jit(solution)/shard_map/ppermute | solution.py:163
  60.2 0.3 fusion.54
  60.5 4.6 %shard_map.39 = f32[32,2,16,256]{3,2,1,0:T(8,128)S(1)} custom-call(s32[32]{0:T(128)S(1)} %get-tuple-element.32.offsets_ref, s32[1]{0:T(128)} %constant.111.clone.1.base_ref, bf16[144,16,256]{2,1,0:T(8,128)(2,1)S(1)} %broadcast_dynamic-update-slice_fusion.white_ref), custom_call_target="tpu_custom_call" | custom-call | flops 16777216 | bytes 2228224 | tf_op jit(solution)/shard_map/pallas_call | solution.py:60
  65.1 0.9 %convert_element_type.79 = bf16[32,2,16,256]{3,2,1,0:T(8,128)(2,1)} convert(f32[32,2,16,256]{3,2,1,0:T(8,128)S(1)} %shard_map.39) | non-fusion elementwise | flops 262144 | bytes 1572864 | tf_op jit(solution)/shard_map/convert_element_type | solution.py:160
  66.0 1.7 %negate_convert_fusion.1 = (bf16[1024,16,32]{0,2,1:T(8,128)(2,1)}, bf16[1024,16,32]{0,2,1:T(8,128)(2,1)S(1)}) fusion(f32[1024,16]{0,1:T(8,128)S(1)} %get-tuple-element.22, f32[1024,32]{0,1:T(8,128)S(1)} %get-tuple-element.28, f32[1024,16]{0,1:T(8,128)S(1)} %get-tuple-element.21, f32[1024,32]{0,1:T(8,128)S(1)} %get-tuple-element.27), kind=kLoop, calls=%fused_computation.15 | loop fusion | flops 4718592 | bytes 2490368 | tf_op jit(solution)/shard_map/convert.2
  67.7 0.5 copy.7
  68.2 1.5 %copy.8 = bf16[1,1024,512]{2,1,0:T(8,128)(2,1)S(1)} copy(bf16[1,1024,512]{1,2,0:T(8,128)(2,1)} %bitcast.70) | data formatting | bytes 2097152 | tf_op jit(solution)/shard_map/neg | solution.py:29
  69.7 4.6 %shard_map.37 = f32[32,2,16,256]{3,2,1,0:T(8,128)S(1)} custom-call(s32[32]{0:T(128)S(1)} %get-tuple-element.29.offsets_ref, s32[1]{0:T(128)} %constant.111.clone.1.base_ref, bf16[144,16,256]{2,1,0:T(8,128)(2,1)S(1)} %broadcast_dynamic-update-slice_fusion.white_ref), custom_call_target="tpu_custom_call" | custom-call | flops 16777216 | bytes 2228224 | tf_op jit(solution)/shard_map/pallas_call | solution.py:60
  74.5 0.6 collective-permute-start.10
  75.0 4.6 %shard_map.40 = f32[32,2,16,256]{3,2,1,0:T(8,128)S(1)} custom-call(s32[32]{0:T(128)S(1)} %get-tuple-element.31.offsets_ref, s32[1]{0:T(128)} %constant.111.clone.1.base_ref, bf16[144,16,256]{2,1,0:T(8,128)(2,1)S(1)} %broadcast_dynamic-update-slice_fusion.white_ref), custom_call_target="tpu_custom_call" | custom-call | flops 16777216 | bytes 2228224 | tf_op jit(solution)/shard_map/pallas_call | solution.py:60
  79.6 0.4 convolution_bitcast_fusion
  80.1 1.5 %convolution_bitcast_fusion.2 = f32[32,16,512]{2,1,0:T(8,128)S(1)} fusion(bf16[32,2,16,256]{3,2,1,0:T(8,128)(2,1)} %collective-permute-done.11, s32[]{:T(128)S(6)} %select_n.109, bf16[1,1024,512]{2,1,0:T(8,128)(2,1)S(1)} %copy.7, bf16[1,1024,512]{2,1,0:T(8,128)(2,1)S(1)} %copy.8), kind=kOutput, calls=%fused_computation.19 | convolution fusion | flops 269484032 | bytes 3670020 | tf_op jit(solution)/shard_map/opck,pkl->ocl/dot_general | solution.py:166
  81.6 1.5 %convolution_bitcast_fusion.1 = f32[32,16,512]{2,1,0:T(8,128)S(1)} fusion(bf16[32,2,16,256]{3,2,1,0:T(8,128)(2,1)} %collective-permute-done.12, s32[]{:T(128)S(6)} %select_n.108, bf16[1,1024,512]{2,1,0:T(8,128)(2,1)S(1)} %copy.7, bf16[1,1024,512]{2,1,0:T(8,128)(2,1)S(1)} %copy.8), kind=kOutput, calls=%fused_computation.18 | convolution fusion | flops 269484032 | bytes 3670020 | tf_op jit(solution)/shard_map/opck,pkl->ocl/dot_general | solution.py:166
  83.1 0.7 collective-permute-done.10
  83.7 1.3 %fusion.11 = bf16[32,16,512]{2,1,0:T(8,128)(2,1)} fusion(f32[32,16,512]{2,1,0:T(8,128)S(1)} %convolution_bitcast_fusion, f32[32,16,512]{2,1,0:T(8,128)S(1)} %convolution_bitcast_fusion.1, f32[32,16,512]{2,1,0:T(8,128)S(1)} %convolution_bitcast_fusion.2, bf16[32,2,16,256]{3,2,1,0:T(8,128)(2,1)S(1)} %collective-permute-done.10, s32[]{:T(128)S(6)} %select_n.110, ...), kind=kOutput, calls=%fused_computation.25 | convolution fusion | flops 270794752 | bytes 6291460 | tf_op jit(solution)/shard_map/opck,pkl->ocl/dot_general | solution.py:166
  (29 shorter events, 0.6 us)
Async XLA Ops:
  13.4 6.1 %copy-start = (s32[1024]{0:T(1024)S(1)}, s32[1024]{0:T(1024)}, u32[]{:S(2)}) copy-start(s32[1024]{0:T(1024)} %param.4) | copy-start | bytes 12292
  13.4 6.7 %copy-start.1 = (s32[128]{0:T(128)S(1)}, s32[128]{0:T(128)}, u32[]{:S(2)}) copy-start(s32[128]{0:T(128)} %param.5) | copy-start | bytes 1540
  15.1 5.1 %collective-permute-start = (bf16[16,2,2,256]{3,2,1,0:T(2,128)(2,1)S(1)}, bf16[16,2,2,256]{3,2,1,0:T(2,128)(2,1)S(1)}, u32[]{:S(2)}, u32[]{:S(2)}) collective-permute-start(bf16[16,2,2,256]{3,2,1,0:T(2,128)(2,1)S(1)} %get-tuple-element.18), channel_id=1, source_target_pairs={{0,1},{1,2},{2,3},{3,0},{4,5},{5,6},{6,7},{7,4},{8,9},{9,10},{10,1... | collective-permute-start | bytes 98312 | tf_op jit(solution)/shard_map/ppermute | solution.py:133
  15.6 4.6 %collective-permute-start.1 = (bf16[16,2,2,256]{3,2,1,0:T(2,128)(2,1)S(1)}, bf16[16,2,2,256]{3,2,1,0:T(2,128)(2,1)S(1)}, u32[]{:S(2)}, u32[]{:S(2)}) collective-permute-start(bf16[16,2,2,256]{3,2,1,0:T(2,128)(2,1)S(1)} %get-tuple-element.17), channel_id=1, source_target_pairs={{0,2},{1,3},{2,0},{3,1},{4,6},{5,7},{6,4},{7,5},{8,10},{9,11},{10,... | collective-permute-start | bytes 98312 | tf_op jit(solution)/shard_map/ppermute | solution.py:133
  18.2 3.0 %collective-permute-start.2 = (bf16[16,2,2,256]{3,2,1,0:T(2,128)(2,1)S(1)}, bf16[16,2,2,256]{3,2,1,0:T(2,128)(2,1)S(1)}, u32[]{:S(2)}, u32[]{:S(2)}) collective-permute-start(bf16[16,2,2,256]{3,2,1,0:T(2,128)(2,1)S(1)} %get-tuple-element.16), channel_id=1, source_target_pairs={{0,3},{1,0},{2,1},{3,2},{4,7},{5,4},{6,5},{7,6},{8,11},{9,8},{10,9... | collective-permute-start | bytes 98312 | tf_op jit(solution)/shard_map/ppermute | solution.py:133
  21.4 7.7 %collective-permute-start.3 = (bf16[16,16,256]{2,1,0:T(8,128)(2,1)S(1)}, bf16[16,16,256]{2,1,0:T(8,128)(2,1)S(1)}, u32[]{:S(2)}, u32[]{:S(2)}) collective-permute-start(bf16[16,16,256]{2,1,0:T(8,128)(2,1)S(1)} %bitcast.72), channel_id=1, source_target_pairs={{4,0},{8,4},{12,8},{16,12},{20,16},{24,20},{28,24},{5,1},{9,5},{13... | collective-permute-start | bytes 393224 | tf_op jit(solution)/shard_map/ppermute | solution.py:143
  22.7 10.4 %collective-permute-start.4 = (bf16[16,16,256]{2,1,0:T(8,128)(2,1)S(1)}, bf16[16,16,256]{2,1,0:T(8,128)(2,1)S(1)}, u32[]{:S(2)}, u32[]{:S(2)}) collective-permute-start(bf16[16,16,256]{2,1,0:T(8,128)(2,1)S(1)} %bitcast.73), channel_id=1, source_target_pairs={{8,0},{12,4},{16,8},{20,12},{24,16},{28,20},{9,1},{13,5},{17,9},{2... | collective-permute-start | bytes 393224 | tf_op jit(solution)/shard_map/ppermute | solution.py:143
  24.0 11.1 %collective-permute-start.5 = (bf16[16,16,256]{2,1,0:T(8,128)(2,1)S(1)}, bf16[16,16,256]{2,1,0:T(8,128)(2,1)S(1)}, u32[]{:S(2)}, u32[]{:S(2)}) collective-permute-start(bf16[16,16,256]{2,1,0:T(8,128)(2,1)S(1)} %bitcast.74), channel_id=1, source_target_pairs={{12,0},{16,4},{20,8},{24,12},{28,16},{13,1},{17,5},{21,9},{25,13},... | collective-permute-start | bytes 393224 | tf_op jit(solution)/shard_map/ppermute | solution.py:143
  25.3 25.6 %collective-permute-start.6 = (bf16[16,16,256]{2,1,0:T(8,128)(2,1)S(1)}, bf16[16,16,256]{2,1,0:T(8,128)(2,1)S(1)}, u32[]{:S(2)}, u32[]{:S(2)}) collective-permute-start(bf16[16,16,256]{2,1,0:T(8,128)(2,1)S(1)} %bitcast.75), channel_id=1, source_target_pairs={{16,0},{20,4},{24,8},{28,12},{17,1},{21,5},{25,9},{29,13},{18,2},{... | collective-permute-start | bytes 393224 | tf_op jit(solution)/shard_map/ppermute | solution.py:143
  26.6 26.5 %collective-permute-start.7 = (bf16[16,16,256]{2,1,0:T(8,128)(2,1)S(1)}, bf16[16,16,256]{2,1,0:T(8,128)(2,1)S(1)}, u32[]{:S(2)}, u32[]{:S(2)}) collective-permute-start(bf16[16,16,256]{2,1,0:T(8,128)(2,1)S(1)} %bitcast.76), channel_id=1, source_target_pairs={{20,0},{24,4},{28,8},{21,1},{25,5},{29,9},{22,2},{26,6},{30,10},{2... | collective-permute-start | bytes 393224 | tf_op jit(solution)/shard_map/ppermute | solution.py:143
  29.1 24.0 %collective-permute-start.8 = (bf16[16,16,256]{2,1,0:T(8,128)(2,1)S(1)}, bf16[16,16,256]{2,1,0:T(8,128)(2,1)S(1)}, u32[]{:S(2)}, u32[]{:S(2)}) collective-permute-start(bf16[16,16,256]{2,1,0:T(8,128)(2,1)S(1)} %bitcast.77), channel_id=1, source_target_pairs={{24,0},{28,4},{25,1},{29,5},{26,2},{30,6},{27,3},{31,7}} | collective-permute-start | bytes 393224 | tf_op jit(solution)/shard_map/ppermute | solution.py:143
  33.1 20.1 %collective-permute-start.9 = (bf16[16,16,256]{2,1,0:T(8,128)(2,1)S(1)}, bf16[16,16,256]{2,1,0:T(8,128)(2,1)S(1)}, u32[]{:S(2)}, u32[]{:S(2)}) collective-permute-start(bf16[16,16,256]{2,1,0:T(8,128)(2,1)S(1)} %bitcast.78), channel_id=1, source_target_pairs={{28,0},{29,1},{30,2},{31,3}} | collective-permute-start | bytes 393224 | tf_op jit(solution)/shard_map/ppermute | solution.py:143
  58.7 21.4 %collective-permute-start.11 = (bf16[32,2,16,256]{3,2,1,0:T(8,128)(2,1)}, bf16[32,2,16,256]{3,2,1,0:T(8,128)(2,1)}, u32[]{:S(2)}, u32[]{:S(2)}) collective-permute-start(bf16[32,2,16,256]{3,2,1,0:T(8,128)(2,1)} %convert_element_type.78), channel_id=1, source_target_pairs={{0,2},{1,3},{2,0},{3,1},{4,6},{5,7},{6,4},{7,5},{8,10},{9,11},{10,... | collective-permute-start | bytes 1572872 | tf_op jit(solution)/shard_map/ppermute | solution.py:163
  66.0 15.6 %collective-permute-start.12 = (bf16[32,2,16,256]{3,2,1,0:T(8,128)(2,1)}, bf16[32,2,16,256]{3,2,1,0:T(8,128)(2,1)}, u32[]{:S(2)}, u32[]{:S(2)}) collective-permute-start(bf16[32,2,16,256]{3,2,1,0:T(8,128)(2,1)} %convert_element_type.79), channel_id=1, source_target_pairs={{0,3},{1,0},{2,1},{3,2},{4,7},{5,4},{6,5},{7,6},{8,11},{9,8},{10,9... | collective-permute-start | bytes 1572872 | tf_op jit(solution)/shard_map/ppermute | solution.py:163
  74.5 9.3 %collective-permute-start.10 = (bf16[32,2,16,256]{3,2,1,0:T(8,128)(2,1)S(1)}, bf16[32,2,16,256]{3,2,1,0:T(8,128)(2,1)S(1)}, u32[]{:S(2)}, u32[]{:S(2)}) collective-permute-start(bf16[32,2,16,256]{3,2,1,0:T(8,128)(2,1)S(1)} %convert_element_type.75), channel_id=1, source_target_pairs={{0,1},{1,2},{2,3},{3,0},{4,5},{5,6},{6,7},{7,4},{8,9},{9,10},{10,1... | collective-permute-start | bytes 1572872 | tf_op jit(solution)/shard_map/ppermute | solution.py:163

commit v18 on v17

--- a/solution.py
+++ b/solution.py
@@ -150,7 +150,6 @@
     off_dev = band_span // gy_count
     me = lax.axis_index("gy")
     offsets = pair_offsets.astype(jnp.int32)
-    inverse = inverse_table(kept_bins)
     norm_scale = 0.5 / math.sqrt(windows * bin_count)
     lagged = None
     for shift in list(range(1, gy_count)) + [0]:
@@ -162,7 +161,7 @@
             pairs = [(src, (src + shift) % gy_count) for src in range(gy_count)]
             part = lax.ppermute(part, "gy", perm=pairs)
         origin = lax.rem(me + gy_count - shift, gy_count)
-        rows = lax.dynamic_slice_in_dim(inverse, origin * shard_bins, shard_bins, 1)
+        rows = inverse_table(lax.dynamic_slice_in_dim(kept_bins, origin * shard_bins, shard_bins))
         term = jnp.einsum("opck,pkl->ocl", part, rows, preferred_element_type=jnp.float32)
         lagged = term if lagged is None else lagged + term
     lagged = lagged * norm_scale

time: 85.5 us -> 87.2 us (1.020)
  waiting for transfers between devices: 24 us -> 26.5 us
    ppermute x3, waiting for transfers between devices: 0.68 us -> 4.94 us  [local(): part = lax.ppermute(part, 'gy', perm=pairs)]
    another operation x1, local copies, waits for them, and re-layouts: 1.16 us -> 0.12 us  [forward_spectra(): record_rows.reshape(row_count * block_count, block_len)]
    ppermute x3, waiting for transfers between devices: 0.94 us -> 0.01 us  [local(): lax.ppermute(piece, 'gy', perm=[(src, (src + shift) % gy_count) for src i...]
    another operation x2 -> x5, other arithmetic: 5.34 us -> 4.43 us
where the time goes in v18:
time: 87.2 us; the launch traced here: 86.7 us
  waiting for transfers between devices  26.5 us (30%)
  Pallas kernels  18.5 us (21%)
  starting transfers between devices  15.1 us (17%)
  other arithmetic  13.5 us (15%)
  matrix products  7.12 us (8%)
  local copies, waits for them, and re-layouts  5.55 us (6%)
    ppermute x7, waiting for transfers between devices, local(): blocks.append(lax.ppermute(rows_white, 'gx', perm=pairs))  21.6 us
    pallas_call x4, Pallas kernels, cross_spectra(): pl.pallas_call(kernel, grid_spec=pltpu.PrefetchScalarGridSpec(num_scalar_...  18.5 us
    ppermute x7, starting transfers between devices, local(): blocks.append(lax.ppermute(rows_white, 'gx', perm=pairs))  9.2 us
    ppermute x3, waiting for transfers between devices, local(): part = lax.ppermute(part, 'gy', perm=pairs)  4.94 us
    dot_general x4, matrix products, local(): jnp.einsum('opck,pkl->ocl', part, rows, preferred_element_type=jnp.float32)  4.66 us
    ppermute x3, starting transfers between devices, local(): lax.ppermute(piece, 'gy', perm=[(src, (src + shift) % gy_count) for src i...  4.46 us
    another operation x5, other arithmetic  4.43 us
    dot_general x1, matrix products, forward_spectra(): jnp.dot(record_rows.reshape(row_count * block_count, block_len), small_ta...  2.46 us
  transfers between devices with their start and end apart: 13, of which 7 were waited for; matrix products, arithmetic and copies ran while one was open for 11% of the time, Pallas kernels for 16%

profile of v18, /device:TPU:0, one launch (start us, length us, event | category | flops | bytes accessed | tf_op | source)
XLA Modules:
  0.0 86.7 jit_solution(7076221380312923263)
XLA Ops:
  0.0 1.3 %fusion.37 = (f32[32,1024]{1,0:T(8,128)S(1)}, f32[32,1024]{1,0:T(8,128)S(1)}) fusion(s32[1024]{0:T(1024)} %param.4), kind=kLoop, calls=%fused_computation.70 | loop fusion | flops 458752 | bytes 266240 | tf_op jit(solution)/shard_map/cos | solution.py:90
  1.3 0.7 add_select_fusion.11
  2.0 1.8 %fusion.32 = (f32[64,1024]{1,0:T(8,128)S(1)}, f32[64,1024]{1,0:T(8,128)S(1)}) fusion(s32[1024]{0:T(1024)} %param.4, s32[64]{0:T(128)S(1)} %iota_multiply_fusion), kind=kLoop, calls=%fused_computation.64 | loop fusion | flops 917504 | bytes 528640 | tf_op jit(solution)/shard_map/cos | solution.py:90
  3.9 3.7 %subtract_convert_fusion = (bf16[64,32,1024]{2,1,0:T(8,128)(2,1)S(1)}, bf16[64,32,1024]{2,1,0:T(8,128)(2,1)S(1)}) fusion(f32[64,1024]{1,0:T(8,128)S(1)} %get-tuple-element.26, f32[32,1024]{1,0:T(8,128)S(1)} %get-tuple-element.34, f32[64,1024]{1,0:T(8,128)S(1)} %get-tuple-element.25, f32[32,1024]{1,0:T(8,128)S(1)} %get-tuple-element.33), kind=kLoop, calls=%fused_computation.5 | loop fusion | flops 18874368 | bytes 9175040 | tf_op jit(solution)/shard_map/convert.19
  7.6 2.5 %fusion.4 = f32[128,2048]{0,1:T(8,128)S(1)} fusion(bf16[128,2048]{1,0:T(8,128)(2,1)S(1)} %reshape_reshape.3, bf16[2048,1024]{1,0:T(8,128)(2,1)S(1)} %bitcast.75, bf16[2048,1024]{1,0:T(8,128)(2,1)S(1)} %bitcast.74), kind=kOutput, calls=%fused_computation.6 | convolution fusion | flops 1090519040 | bytes 9961472 | tf_op jit(solution)/shard_map/dot_general | solution.py:102
  10.0 0.3 copy.4
  10.4 0.9 %reshape.1081 = f32[32,4,2,1024]{3,2,1,0:T(2,128)S(1)} reshape(f32[128,2048]{1,0:T(8,128)S(1)} %copy.4) | data formatting | bytes 2097152 | tf_op jit(solution)/shard_map/reshape | solution.py:106
  11.3 1.2 %fusion.99 = (f32[32,4,1,1024]{3,2,1,0:T(1,128)S(1)}, f32[32,4,1,1024]{3,2,1,0:T(1,128)S(1)}) fusion(f32[32,4,2,1024]{3,2,1,0:T(2,128)S(1)} %reshape.1081), kind=kLoop, calls=%fused_computation.187 | loop fusion | bytes 2097152 | tf_op jit(solution)/shard_map/slice | solution.py:113
  12.6 0.8 fusion.21
  13.5 0.2 concatenate.18
  14.1 0.5 collective-permute-start
  14.6 2.6 %collective-permute-start.1 = (bf16[16,2,2,256]{3,2,1,0:T(2,128)(2,1)S(1)}, bf16[16,2,2,256]{3,2,1,0:T(2,128)(2,1)S(1)}, u32[]{:S(2)}, u32[]{:S(2)}) collective-permute-start(bf16[16,2,2,256]{3,2,1,0:T(2,128)(2,1)S(1)} %get-tuple-element.15), channel_id=1, source_target_pairs={{0,2},{1,3},{2,0},{3,1},{4,6},{5,7},{6,4},{7,5},{8,10},{9,11},{10,... | collective-permute-start | bytes 98312 | tf_op jit(solution)/shard_map/ppermute | solution.py:133
  17.2 1.4 %collective-permute-start.2 = (bf16[16,2,2,256]{3,2,1,0:T(2,128)(2,1)S(1)}, bf16[16,2,2,256]{3,2,1,0:T(2,128)(2,1)S(1)}, u32[]{:S(2)}, u32[]{:S(2)}) collective-permute-start(bf16[16,2,2,256]{3,2,1,0:T(2,128)(2,1)S(1)} %get-tuple-element.14), channel_id=1, source_target_pairs={{0,3},{1,0},{2,1},{3,2},{4,7},{5,4},{6,5},{7,6},{8,11},{9,8},{10,9... | collective-permute-start | bytes 98312 | tf_op jit(solution)/shard_map/ppermute | solution.py:133
  18.6 0.3 fusion.78
  18.9 0.9 %fusion.82 = (f32[256,32]{0,1:T(8,128)S(1)}, f32[256,32]{0,1:T(8,128)S(1)}, f32[256,32]{0,1:T(8,128)}, f32[256,32]{0,1:T(8,128)}) fusion(s32[256]{0:T(256)S(1)} %get-tuple-element.28, s32[256]{0:T(256)S(1)} %get-tuple-element.27), kind=kLoop, calls=%fused_computation.158 | loop fusion | flops 229376 | bytes 133120 | tf_op jit(solution)/shard_map/cos | solution.py:26
  19.8 0.9 %fusion.92 = (f32[256,16]{0,1:T(8,128)}, f32[256,16]{0,1:T(8,128)}, f32[256,16]{0,1:T(8,128)S(1)}, f32[256,16]{0,1:T(8,128)S(1)}, f32[256,16]{0,1:T(8,128)S(1)},...) fusion(s32[16]{0:T(128)S(1)} %multiply_add_fusion, s32[256]{0:T(256)S(1)} %get-tuple-element.27, ...), kind=kLoop, calls=%fused_computation.170 | loop fusion | flops 229376 | bytes 135232 | tf_op jit(solution)/shard_map/cos | solution.py:26
  20.7 0.2 subtract_convert_fusion.2
  20.9 0.2 subtract_convert_fusion.3
  21.2 0.2 maximum_bitcast_fusion.8
  21.5 1.3 %collective-permute-start.3 = (bf16[16,16,256]{2,1,0:T(8,128)(2,1)S(1)}, bf16[16,16,256]{2,1,0:T(8,128)(2,1)S(1)}, u32[]{:S(2)}, u32[]{:S(2)}) collective-permute-start(bf16[16,16,256]{2,1,0:T(8,128)(2,1)S(1)} %bitcast.84), channel_id=1, source_target_pairs={{4,0},{8,4},{12,8},{16,12},{20,16},{24,20},{28,24},{5,1},{9,5},{13... | collective-permute-start | bytes 393224 | tf_op jit(solution)/shard_map/ppermute | solution.py:143
  22.8 1.3 %collective-permute-start.4 = (bf16[16,16,256]{2,1,0:T(8,128)(2,1)S(1)}, bf16[16,16,256]{2,1,0:T(8,128)(2,1)S(1)}, u32[]{:S(2)}, u32[]{:S(2)}) collective-permute-start(bf16[16,16,256]{2,1,0:T(8,128)(2,1)S(1)} %bitcast.85), channel_id=1, source_target_pairs={{8,0},{12,4},{16,8},{20,12},{24,16},{28,20},{9,1},{13,5},{17,9},{2... | collective-permute-start | bytes 393224 | tf_op jit(solution)/shard_map/ppermute | solution.py:143
  24.1 1.3 %collective-permute-start.5 = (bf16[16,16,256]{2,1,0:T(8,128)(2,1)S(1)}, bf16[16,16,256]{2,1,0:T(8,128)(2,1)S(1)}, u32[]{:S(2)}, u32[]{:S(2)}) collective-permute-start(bf16[16,16,256]{2,1,0:T(8,128)(2,1)S(1)} %bitcast.86), channel_id=1, source_target_pairs={{12,0},{16,4},{20,8},{24,12},{28,16},{13,1},{17,5},{21,9},{25,13},... | collective-permute-start | bytes 393224 | tf_op jit(solution)/shard_map/ppermute | solution.py:143
  25.4 1.5 %collective-permute-start.6 = (bf16[16,16,256]{2,1,0:T(8,128)(2,1)S(1)}, bf16[16,16,256]{2,1,0:T(8,128)(2,1)S(1)}, u32[]{:S(2)}, u32[]{:S(2)}) collective-permute-start(bf16[16,16,256]{2,1,0:T(8,128)(2,1)S(1)} %bitcast.87), channel_id=1, source_target_pairs={{16,0},{20,4},{24,8},{28,12},{17,1},{21,5},{25,9},{29,13},{18,2},{... | collective-permute-start | bytes 393224 | tf_op jit(solution)/shard_map/ppermute | solution.py:143
  26.9 1.3 %collective-permute-start.7 = (bf16[16,16,256]{2,1,0:T(8,128)(2,1)S(1)}, bf16[16,16,256]{2,1,0:T(8,128)(2,1)S(1)}, u32[]{:S(2)}, u32[]{:S(2)}) collective-permute-start(bf16[16,16,256]{2,1,0:T(8,128)(2,1)S(1)} %bitcast.88), channel_id=1, source_target_pairs={{20,0},{24,4},{28,8},{21,1},{25,5},{29,9},{22,2},{26,6},{30,10},{2... | collective-permute-start | bytes 393224 | tf_op jit(solution)/shard_map/ppermute | solution.py:143
  28.3 1.3 %collective-permute-start.8 = (bf16[16,16,256]{2,1,0:T(8,128)(2,1)S(1)}, bf16[16,16,256]{2,1,0:T(8,128)(2,1)S(1)}, u32[]{:S(2)}, u32[]{:S(2)}) collective-permute-start(bf16[16,16,256]{2,1,0:T(8,128)(2,1)S(1)} %bitcast.89), channel_id=1, source_target_pairs={{24,0},{28,4},{25,1},{29,5},{26,2},{30,6},{27,3},{31,7}} | collective-permute-start | bytes 393224 | tf_op jit(solution)/shard_map/ppermute | solution.py:143
  29.6 2.5 %collective-permute-done.4 = bf16[16,16,256]{2,1,0:T(8,128)(2,1)S(1)} collective-permute-done((bf16[16,16,256]{2,1,0:T(8,128)(2,1)S(1)}, bf16[16,16,256]{2,1,0:T(8,128)(2,1)S(1)}, u32[]{:S(2)}, u32[]{:S(2)}) %collective-permute-start.4) | collective-permute-done | bytes 131104 | tf_op jit(solution)/shard_map/ppermute | solution.py:143
  32.1 1.3 %collective-permute-start.9 = (bf16[16,16,256]{2,1,0:T(8,128)(2,1)S(1)}, bf16[16,16,256]{2,1,0:T(8,128)(2,1)S(1)}, u32[]{:S(2)}, u32[]{:S(2)}) collective-permute-start(bf16[16,16,256]{2,1,0:T(8,128)(2,1)S(1)} %bitcast.90), channel_id=1, source_target_pairs={{28,0},{29,1},{30,2},{31,3}} | collective-permute-start | bytes 393224 | tf_op jit(solution)/shard_map/ppermute | solution.py:143
  33.4 1.5 %collective-permute-done.5 = bf16[16,16,256]{2,1,0:T(8,128)(2,1)S(1)} collective-permute-done((bf16[16,16,256]{2,1,0:T(8,128)(2,1)S(1)}, bf16[16,16,256]{2,1,0:T(8,128)(2,1)S(1)}, u32[]{:S(2)}, u32[]{:S(2)}) %collective-permute-start.5) | collective-permute-done | bytes 131104 | tf_op jit(solution)/shard_map/ppermute | solution.py:143
  35.0 15.0 %collective-permute-done.6 = bf16[16,16,256]{2,1,0:T(8,128)(2,1)S(1)} collective-permute-done((bf16[16,16,256]{2,1,0:T(8,128)(2,1)S(1)}, bf16[16,16,256]{2,1,0:T(8,128)(2,1)S(1)}, u32[]{:S(2)}, u32[]{:S(2)}) %collective-permute-start.6) | collective-permute-done | bytes 131104 | tf_op jit(solution)/shard_map/ppermute | solution.py:143
  50.0 2.4 %collective-permute-done.7 = bf16[16,16,256]{2,1,0:T(8,128)(2,1)S(1)} collective-permute-done((bf16[16,16,256]{2,1,0:T(8,128)(2,1)S(1)}, bf16[16,16,256]{2,1,0:T(8,128)(2,1)S(1)}, u32[]{:S(2)}, u32[]{:S(2)}) %collective-permute-start.7) | collective-permute-done | bytes 131104 | tf_op jit(solution)/shard_map/ppermute | solution.py:143
  52.5 4.6 %shard_map.39 = f32[32,2,16,256]{3,2,1,0:T(8,128)S(1)} custom-call(s32[32]{0:T(128)S(1)} %get-tuple-element.60.offsets_ref, s32[1]{0:T(128)} %constant.141.clone.1.base_ref, bf16[144,16,256]{2,1,0:T(8,128)(2,1)S(1)} %broadcast_dynamic-update-slice_fusion.white_ref), custom_call_target="tpu_custom_call" | custom-call | flops 16777216 | bytes 2228224 | tf_op jit(solution)/shard_map/pallas_call | solution.py:60
  57.1 0.9 convert_element_type.144
  58.0 0.2 collective-permute-start.12
  58.5 0.9 copy.12
  60.0 4.6 %shard_map.38 = f32[32,2,16,256]{3,2,1,0:T(8,128)S(1)} custom-call(s32[32]{0:T(128)S(1)} %get-tuple-element.58.offsets_ref, s32[1]{0:T(128)} %constant.141.clone.1.base_ref, bf16[144,16,256]{2,1,0:T(8,128)(2,1)S(1)} %broadcast_dynamic-update-slice_fusion.white_ref), custom_call_target="tpu_custom_call" | custom-call | flops 16777216 | bytes 2228224 | tf_op jit(solution)/shard_map/pallas_call | solution.py:60
  64.7 0.9 %convert_element_type.141 = bf16[32,2,16,256]{3,2,1,0:T(8,128)(2,1)} convert(f32[32,2,16,256]{3,2,1,0:T(8,128)S(1)} %shard_map.38) | non-fusion elementwise | flops 262144 | bytes 1572864 | tf_op jit(solution)/shard_map/convert_element_type | solution.py:159
  65.5 1.0 %collective-permute-start.11 = (bf16[32,2,16,256]{3,2,1,0:T(8,128)(2,1)}, bf16[32,2,16,256]{3,2,1,0:T(8,128)(2,1)}, u32[]{:S(2)}, u32[]{:S(2)}) collective-permute-start(bf16[32,2,16,256]{3,2,1,0:T(8,128)(2,1)} %convert_element_type.141), channel_id=1, source_target_pairs={{0,2},{1,3},{2,0},{3,1},{4,6},{5,7},{6,4},{7,5},{8,10},{9,11},{10,... | collective-permute-start | bytes 1572872 | tf_op jit(solution)/shard_map/ppermute | solution.py:162
  66.5 0.2 subtract_convert_fusion.4
  67.0 4.6 %shard_map.37 = f32[32,2,16,256]{3,2,1,0:T(8,128)S(1)} custom-call(s32[32]{0:T(128)S(1)} %get-tuple-element.57.offsets_ref, s32[1]{0:T(128)} %constant.141.clone.1.base_ref, bf16[144,16,256]{2,1,0:T(8,128)(2,1)S(1)} %broadcast_dynamic-update-slice_fusion.white_ref), custom_call_target="tpu_custom_call" | custom-call | flops 16777216 | bytes 2228224 | tf_op jit(solution)/shard_map/pallas_call | solution.py:60
  71.7 0.3 collective-permute-start.10
  72.0 4.6 %shard_map.40 = f32[32,2,16,256]{3,2,1,0:T(8,128)S(1)} custom-call(s32[32]{0:T(128)S(1)} %get-tuple-element.59.offsets_ref, s32[1]{0:T(128)} %constant.141.clone.1.base_ref, bf16[144,16,256]{2,1,0:T(8,128)(2,1)S(1)} %broadcast_dynamic-update-slice_fusion.white_ref), custom_call_target="tpu_custom_call" | custom-call | flops 16777216 | bytes 2228224 | tf_op jit(solution)/shard_map/pallas_call | solution.py:60
  76.6 0.4 convolution_bitcast_fusion
  77.1 0.5 copy-done
  77.6 1.5 %convolution_bitcast_fusion.1 = f32[32,16,512]{2,1,0:T(8,128)S(1)} fusion(bf16[32,2,16,256]{3,2,1,0:T(8,128)(2,1)} %collective-permute-done.12, bf16[1,256,512]{2,1,0:T(8,128)(2,1)S(1)} %copy-done, bf16[1,256,512]{2,1,0:T(8,128)(2,1)S(1)} %copy.11), kind=kOutput, calls=%fused_computation.8 | convolution fusion | flops 268697600 | bytes 2097152 | tf_op jit(solution)/shard_map/opck,pkl->ocl/dot_general | solution.py:165
  79.1 1.5 %collective-permute-done.11 = bf16[32,2,16,256]{3,2,1,0:T(8,128)(2,1)} collective-permute-done((bf16[32,2,16,256]{3,2,1,0:T(8,128)(2,1)}, bf16[32,2,16,256]{3,2,1,0:T(8,128)(2,1)}, u32[]{:S(2)}, u32[]{:S(2)}) %collective-permute-start.11) | collective-permute-done | bytes 524320 | tf_op jit(solution)/shard_map/ppermute | solution.py:162
  80.6 1.5 %convolution_bitcast_fusion.2 = f32[32,16,512]{2,1,0:T(8,128)S(1)} fusion(bf16[32,2,16,256]{3,2,1,0:T(8,128)(2,1)} %collective-permute-done.11, bf16[1,256,512]{2,1,0:T(8,128)(2,1)S(1)} %copy.10, bf16[1,256,512]{2,1,0:T(8,128)(2,1)S(1)} %copy.9), kind=kOutput, calls=%fused_computation.9 | convolution fusion | flops 268697600 | bytes 2097152 | tf_op jit(solution)/shard_map/opck,pkl->ocl/dot_general | solution.py:165
  82.1 3.4 %collective-permute-done.10 = bf16[32,2,16,256]{3,2,1,0:T(8,128)(2,1)S(1)} collective-permute-done((bf16[32,2,16,256]{3,2,1,0:T(8,128)(2,1)S(1)}, bf16[32,2,16,256]{3,2,1,0:T(8,128)(2,1)S(1)}, u32[]{:S(2)}, u32[]{:S(2)}) %collective-permute-start.10) | collective-permute-done | bytes 524320 | tf_op jit(solution)/shard_map/ppermute | solution.py:162
  85.5 1.3 %fusion.11 = bf16[32,16,512]{2,1,0:T(8,128)(2,1)} fusion(f32[32,16,512]{2,1,0:T(8,128)S(1)} %convolution_bitcast_fusion, f32[32,16,512]{2,1,0:T(8,128)S(1)} %convolution_bitcast_fusion.1, f32[32,16,512]{2,1,0:T(8,128)S(1)} %convolution_bitcast_fusion.2, bf16[32,2,16,256]{3,2,1,0:T(8,128)(2,1)S(1)} %collective-permute-done.10, ...), kind=kOutput, calls=%fused_computation.15 | convolution fusion | flops 270008320 | bytes 4718592 | tf_op jit(solution)/shard_map/opck,pkl->ocl/dot_general | solution.py:165
  (52 shorter events, 2.5 us)
Async XLA Ops:
  0.0 3.8 %copy-start.1 = (bf16[16,2,8192]{2,1,0:T(2,128)(2,1)S(1)}, bf16[16,2,8192]{2,1,0:T(2,128)(2,1)}, u32[]{:S(2)}) copy-start(bf16[16,2,8192]{2,1,0:T(2,128)(2,1)} %param.3) | copy-start | bytes 1572868
  13.3 5.2 %copy-start.4 = (s32[1024]{0:T(1024)S(1)}, s32[1024]{0:T(1024)}, u32[]{:S(2)}) copy-start(s32[1024]{0:T(1024)} %param.4) | copy-start | bytes 12292
  13.8 7.3 %copy-start.7 = (s32[128]{0:T(128)S(1)}, s32[128]{0:T(128)}, u32[]{:S(2)}) copy-start(s32[128]{0:T(128)} %param.5) | copy-start | bytes 1540
  14.1 7.1 %collective-permute-start = (bf16[16,2,2,256]{3,2,1,0:T(2,128)(2,1)S(1)}, bf16[16,2,2,256]{3,2,1,0:T(2,128)(2,1)S(1)}, u32[]{:S(2)}, u32[]{:S(2)}) collective-permute-start(bf16[16,2,2,256]{3,2,1,0:T(2,128)(2,1)S(1)} %get-tuple-element.16), channel_id=1, source_target_pairs={{0,1},{1,2},{2,3},{3,0},{4,5},{5,6},{6,7},{7,4},{8,9},{9,10},{10,1... | collective-permute-start | bytes 98312 | tf_op jit(solution)/shard_map/ppermute | solution.py:133
  14.6 6.6 %collective-permute-start.1 = (bf16[16,2,2,256]{3,2,1,0:T(2,128)(2,1)S(1)}, bf16[16,2,2,256]{3,2,1,0:T(2,128)(2,1)S(1)}, u32[]{:S(2)}, u32[]{:S(2)}) collective-permute-start(bf16[16,2,2,256]{3,2,1,0:T(2,128)(2,1)S(1)} %get-tuple-element.15), channel_id=1, source_target_pairs={{0,2},{1,3},{2,0},{3,1},{4,6},{5,7},{6,4},{7,5},{8,10},{9,11},{10,... | collective-permute-start | bytes 98312 | tf_op jit(solution)/shard_map/ppermute | solution.py:133
  17.2 4.1 %collective-permute-start.2 = (bf16[16,2,2,256]{3,2,1,0:T(2,128)(2,1)S(1)}, bf16[16,2,2,256]{3,2,1,0:T(2,128)(2,1)S(1)}, u32[]{:S(2)}, u32[]{:S(2)}) collective-permute-start(bf16[16,2,2,256]{3,2,1,0:T(2,128)(2,1)S(1)} %get-tuple-element.14), channel_id=1, source_target_pairs={{0,3},{1,0},{2,1},{3,2},{4,7},{5,4},{6,5},{7,6},{8,11},{9,8},{10,9... | collective-permute-start | bytes 98312 | tf_op jit(solution)/shard_map/ppermute | solution.py:133
  21.5 6.9 %collective-permute-start.3 = (bf16[16,16,256]{2,1,0:T(8,128)(2,1)S(1)}, bf16[16,16,256]{2,1,0:T(8,128)(2,1)S(1)}, u32[]{:S(2)}, u32[]{:S(2)}) collective-permute-start(bf16[16,16,256]{2,1,0:T(8,128)(2,1)S(1)} %bitcast.84), channel_id=1, source_target_pairs={{4,0},{8,4},{12,8},{16,12},{20,16},{24,20},{28,24},{5,1},{9,5},{13... | collective-permute-start | bytes 393224 | tf_op jit(solution)/shard_map/ppermute | solution.py:143
  22.8 9.3 %collective-permute-start.4 = (bf16[16,16,256]{2,1,0:T(8,128)(2,1)S(1)}, bf16[16,16,256]{2,1,0:T(8,128)(2,1)S(1)}, u32[]{:S(2)}, u32[]{:S(2)}) collective-permute-start(bf16[16,16,256]{2,1,0:T(8,128)(2,1)S(1)} %bitcast.85), channel_id=1, source_target_pairs={{8,0},{12,4},{16,8},{20,12},{24,16},{28,20},{9,1},{13,5},{17,9},{2... | collective-permute-start | bytes 393224 | tf_op jit(solution)/shard_map/ppermute | solution.py:143
  24.1 10.9 %collective-permute-start.5 = (bf16[16,16,256]{2,1,0:T(8,128)(2,1)S(1)}, bf16[16,16,256]{2,1,0:T(8,128)(2,1)S(1)}, u32[]{:S(2)}, u32[]{:S(2)}) collective-permute-start(bf16[16,16,256]{2,1,0:T(8,128)(2,1)S(1)} %bitcast.86), channel_id=1, source_target_pairs={{12,0},{16,4},{20,8},{24,12},{28,16},{13,1},{17,5},{21,9},{25,13},... | collective-permute-start | bytes 393224 | tf_op jit(solution)/shard_map/ppermute | solution.py:143
  25.4 24.6 %collective-permute-start.6 = (bf16[16,16,256]{2,1,0:T(8,128)(2,1)S(1)}, bf16[16,16,256]{2,1,0:T(8,128)(2,1)S(1)}, u32[]{:S(2)}, u32[]{:S(2)}) collective-permute-start(bf16[16,16,256]{2,1,0:T(8,128)(2,1)S(1)} %bitcast.87), channel_id=1, source_target_pairs={{16,0},{20,4},{24,8},{28,12},{17,1},{21,5},{25,9},{29,13},{18,2},{... | collective-permute-start | bytes 393224 | tf_op jit(solution)/shard_map/ppermute | solution.py:143
  26.9 25.5 %collective-permute-start.7 = (bf16[16,16,256]{2,1,0:T(8,128)(2,1)S(1)}, bf16[16,16,256]{2,1,0:T(8,128)(2,1)S(1)}, u32[]{:S(2)}, u32[]{:S(2)}) collective-permute-start(bf16[16,16,256]{2,1,0:T(8,128)(2,1)S(1)} %bitcast.88), channel_id=1, source_target_pairs={{20,0},{24,4},{28,8},{21,1},{25,5},{29,9},{22,2},{26,6},{30,10},{2... | collective-permute-start | bytes 393224 | tf_op jit(solution)/shard_map/ppermute | solution.py:143
  28.3 24.1 %collective-permute-start.8 = (bf16[16,16,256]{2,1,0:T(8,128)(2,1)S(1)}, bf16[16,16,256]{2,1,0:T(8,128)(2,1)S(1)}, u32[]{:S(2)}, u32[]{:S(2)}) collective-permute-start(bf16[16,16,256]{2,1,0:T(8,128)(2,1)S(1)} %bitcast.89), channel_id=1, source_target_pairs={{24,0},{28,4},{25,1},{29,5},{26,2},{30,6},{27,3},{31,7}} | collective-permute-start | bytes 393224 | tf_op jit(solution)/shard_map/ppermute | solution.py:143
  32.1 20.3 %collective-permute-start.9 = (bf16[16,16,256]{2,1,0:T(8,128)(2,1)S(1)}, bf16[16,16,256]{2,1,0:T(8,128)(2,1)S(1)}, u32[]{:S(2)}, u32[]{:S(2)}) collective-permute-start(bf16[16,16,256]{2,1,0:T(8,128)(2,1)S(1)} %bitcast.90), channel_id=1, source_target_pairs={{28,0},{29,1},{30,2},{31,3}} | collective-permute-start | bytes 393224 | tf_op jit(solution)/shard_map/ppermute | solution.py:143
  58.0 19.1 %collective-permute-start.12 = (bf16[32,2,16,256]{3,2,1,0:T(8,128)(2,1)}, bf16[32,2,16,256]{3,2,1,0:T(8,128)(2,1)}, u32[]{:S(2)}, u32[]{:S(2)}) collective-permute-start(bf16[32,2,16,256]{3,2,1,0:T(8,128)(2,1)} %convert_element_type.144), channel_id=1, source_target_pairs={{0,3},{1,0},{2,1},{3,2},{4,7},{5,4},{6,5},{7,6},{8,11},{9,8},{10,9... | collective-permute-start | bytes 1572872 | tf_op jit(solution)/shard_map/ppermute | solution.py:162
  64.6 1.9 %copy-start.2 = (f32[256,32]{0,1:T(8,128)S(1)}, f32[256,32]{0,1:T(8,128)}, u32[]{:S(2)}) copy-start(f32[256,32]{0,1:T(8,128)} %get-tuple-element.63) | copy-start | bytes 98308
  64.6 1.9 %copy-start.3 = (f32[256,32]{0,1:T(8,128)S(1)}, f32[256,32]{0,1:T(8,128)}, u32[]{:S(2)}) copy-start(f32[256,32]{0,1:T(8,128)} %get-tuple-element.64) | copy-start | bytes 98308
  64.6 1.9 %copy-start.5 = (f32[256,16]{0,1:T(8,128)S(1)}, f32[256,16]{0,1:T(8,128)}, u32[]{:S(2)}) copy-start(f32[256,16]{0,1:T(8,128)} %get-tuple-element.35) | copy-start | bytes 49156
  64.6 1.9 %copy-start.6 = (f32[256,16]{0,1:T(8,128)S(1)}, f32[256,16]{0,1:T(8,128)}, u32[]{:S(2)}) copy-start(f32[256,16]{0,1:T(8,128)} %get-tuple-element.36) | copy-start | bytes 49156
  65.5 15.1 %collective-permute-start.11 = (bf16[32,2,16,256]{3,2,1,0:T(8,128)(2,1)}, bf16[32,2,16,256]{3,2,1,0:T(8,128)(2,1)}, u32[]{:S(2)}, u32[]{:S(2)}) collective-permute-start(bf16[32,2,16,256]{3,2,1,0:T(8,128)(2,1)} %convert_element_type.141), channel_id=1, source_target_pairs={{0,2},{1,3},{2,0},{3,1},{4,6},{5,7},{6,4},{7,5},{8,10},{9,11},{10,... | collective-permute-start | bytes 1572872 | tf_op jit(solution)/shard_map/ppermute | solution.py:162
  71.7 13.7 %collective-permute-start.10 = (bf16[32,2,16,256]{3,2,1,0:T(8,128)(2,1)S(1)}, bf16[32,2,16,256]{3,2,1,0:T(8,128)(2,1)S(1)}, u32[]{:S(2)}, u32[]{:S(2)}) collective-permute-start(bf16[32,2,16,256]{3,2,1,0:T(8,128)(2,1)S(1)} %convert_element_type.138), channel_id=1, source_target_pairs={{0,1},{1,2},{2,3},{3,0},{4,5},{5,6},{6,7},{7,4},{8,9},{9,10},{10,1... | collective-permute-start | bytes 1572872 | tf_op jit(solution)/shard_map/ppermute | solution.py:162
  76.6 1.0 %copy-start = (bf16[1,256,512]{2,1,0:T(8,128)(2,1)S(1)}, bf16[1,256,512]{2,1,0:T(8,128)(2,1)}, u32[]{:S(2)}) copy-start(bf16[1,256,512]{2,1,0:T(8,128)(2,1)} %copy.12) | copy-start | bytes 786436

commit v19 on v17

--- a/solution.py
+++ b/solution.py
@@ -70,7 +70,7 @@
         cost_estimate=pl.CostEstimate(
             flops=8 * band_span * own_count * rows * bins,
             transcendentals=0,
-            bytes_accessed=white_all.size * 2 + band_span * 2 * own_count * bins * 4,
+            bytes_accessed=white_all.size * 4 + band_span * 2 * own_count * bins * 4,
         ),
     )(pair_offsets, base, white_all)
 
@@ -144,7 +144,7 @@
     missing = needed + 1 - len(blocks)
     if missing > 0:
         blocks.append(jnp.zeros((missing * ch_dev,) + rows_white.shape[1:], rows_white.dtype))
-    padded = jnp.concatenate(blocks, axis=0)
+    padded = jnp.concatenate(blocks, axis=0).astype(jnp.float32)
     base = jnp.zeros((1,), jnp.int32)
     gy_count = lax.axis_size("gy")
     off_dev = band_span // gy_count

time: 85.5 us -> 85.1 us (level)
  Pallas kernels: 18.5 us -> 15.5 us
  local copies, waits for them, and re-layouts: 6.19 us -> 7.97 us
    pallas_call x4, Pallas kernels: 18.5 us -> 15.5 us  [cross_spectra(): pl.pallas_call(kernel, grid_spec=pltpu.PrefetchScalarGridSpec(num_scalar_...]
    sub x1, local copies, waits for them, and re-layouts: 0.53 us -> 1.49 us  [inverse_table(): cos_t = (cos_f * cos_c - sin_f * sin_c).reshape(kept_bins.shape[0], LAGS)]
  transfers between devices with their start and end apart: 13 -> 13, of which waited for: 7 -> 7; matrix products, arithmetic and copies ran while one was open for 11% -> 13% of each run, Pallas kernels for 16% -> 14%
where the time goes in v19:
time: 85.1 us; the launch traced here: 84.6 us
  waiting for transfers between devices  24.1 us (28%)
  starting transfers between devices  15.7 us (18%)
  Pallas kernels  15.5 us (18%)
  other arithmetic  13.8 us (16%)
  local copies, waits for them, and re-layouts  7.97 us (9%)
  matrix products  7.12 us (8%)
    ppermute x7, waiting for transfers between devices, local(): blocks.append(lax.ppermute(rows_white, 'gx', perm=pairs))  22.4 us
    pallas_call x4, Pallas kernels, cross_spectra(): pl.pallas_call(kernel, grid_spec=pltpu.PrefetchScalarGridSpec(num_scalar_...  15.5 us
    ppermute x7, starting transfers between devices, local(): blocks.append(lax.ppermute(rows_white, 'gx', perm=pairs))  9.2 us
    another operation x2, other arithmetic  5.69 us
    dot_general x4, matrix products, local(): jnp.einsum('opck,pkl->ocl', part, rows, preferred_element_type=jnp.float32)  4.66 us
    ppermute x3, starting transfers between devices, local(): lax.ppermute(piece, 'gy', perm=[(src, (src + shift) % gy_count) for src i...  4.46 us
    dot_general x1, matrix products, forward_spectra(): jnp.dot(record_rows.reshape(row_count * block_count, block_len), small_ta...  2.46 us
    neg x1, local copies, waits for them, and re-layouts, inverse_table(): return jnp.stack([cos_t, -sin_t], axis=0).astype(jnp.bfloat16)  2.31 us
  transfers between devices with their start and end apart: 13, of which 7 were waited for; matrix products, arithmetic and copies ran while one was open for 13% of the time, Pallas kernels for 14%

profile of v19, /device:TPU:0, one launch (start us, length us, event | category | flops | bytes accessed | tf_op | source)
XLA Modules:
  0.0 84.6 jit_solution(1979279377849395003)
XLA Ops:
  0.0 1.2 %fusion.52 = (f32[32,1024]{1,0:T(8,128)S(1)}, f32[32,1024]{1,0:T(8,128)S(1)}) fusion(s32[1024]{0:T(1024)} %param.4), kind=kLoop, calls=%fused_computation.87 | loop fusion | flops 458752 | bytes 266240 | tf_op jit(solution)/shard_map/cos | solution.py:90
  1.2 0.7 add_select_fusion.5
  1.9 1.8 %fusion.41 = (f32[64,1024]{1,0:T(8,128)S(1)}, f32[64,1024]{1,0:T(8,128)S(1)}) fusion(s32[1024]{0:T(1024)} %param.4, s32[64]{0:T(128)S(1)} %iota_multiply_fusion), kind=kLoop, calls=%fused_computation.70 | loop fusion | flops 917504 | bytes 528640 | tf_op jit(solution)/shard_map/cos | solution.py:90
  3.7 1.2 %reshape_reshape.3 = bf16[128,2048]{1,0:T(8,128)(2,1)S(1)} reshape(bf16[16,2,8192]{2,1,0:T(2,128)(2,1)} %param.3) | data formatting | bytes 1048576 | tf_op jit(solution)/shard_map/reshape;reshape | solution.py:103
  4.9 3.7 %subtract_convert_fusion = (bf16[64,32,1024]{2,1,0:T(8,128)(2,1)S(1)}, bf16[64,32,1024]{2,1,0:T(8,128)(2,1)S(1)}) fusion(f32[64,1024]{1,0:T(8,128)S(1)} %get-tuple-element.20, f32[32,1024]{1,0:T(8,128)S(1)} %get-tuple-element.26, f32[64,1024]{1,0:T(8,128)S(1)} %get-tuple-element.19, f32[32,1024]{1,0:T(8,128)S(1)} %get-tuple-element.25), kind=kLoop, calls=%fused_computation.5 | loop fusion | flops 18874368 | bytes 9175040 | tf_op jit(solution)/shard_map/convert.7
  8.5 2.5 %fusion.4 = f32[128,2048]{0,1:T(8,128)S(1)} fusion(bf16[128,2048]{1,0:T(8,128)(2,1)S(1)} %reshape_reshape.3, bf16[2048,1024]{1,0:T(8,128)(2,1)S(1)} %bitcast.69, bf16[2048,1024]{1,0:T(8,128)(2,1)S(1)} %bitcast.68), kind=kOutput, calls=%fused_computation.14 | convolution fusion | flops 1090519040 | bytes 9961472 | tf_op jit(solution)/shard_map/dot_general | solution.py:102
  11.0 0.3 copy.4
  11.3 0.9 %reshape.439 = f32[32,4,2,1024]{3,2,1,0:T(2,128)S(1)} reshape(f32[128,2048]{1,0:T(8,128)S(1)} %copy.4) | data formatting | bytes 2097152 | tf_op jit(solution)/shard_map/reshape | solution.py:106
  12.2 1.2 %fusion.68 = (f32[32,4,1,1024]{3,2,1,0:T(1,128)S(1)}, f32[32,4,1,1024]{3,2,1,0:T(1,128)S(1)}) fusion(f32[32,4,2,1024]{3,2,1,0:T(2,128)S(1)} %reshape.439), kind=kLoop, calls=%fused_computation.126 | loop fusion | bytes 2097152 | tf_op jit(solution)/shard_map/slice | solution.py:113
  13.6 0.8 fusion.25
  14.5 0.2 concatenate.18
  14.8 0.2 multiply_convert_fusion
  15.1 0.5 collective-permute-start
  15.6 2.6 %collective-permute-start.1 = (bf16[16,2,2,256]{3,2,1,0:T(2,128)(2,1)S(1)}, bf16[16,2,2,256]{3,2,1,0:T(2,128)(2,1)S(1)}, u32[]{:S(2)}, u32[]{:S(2)}) collective-permute-start(bf16[16,2,2,256]{3,2,1,0:T(2,128)(2,1)S(1)} %get-tuple-element.17), channel_id=1, source_target_pairs={{0,2},{1,3},{2,0},{3,1},{4,6},{5,7},{6,4},{7,5},{8,10},{9,11},{10,... | collective-permute-start | bytes 98312 | tf_op jit(solution)/shard_map/ppermute | solution.py:133
  18.2 1.4 %collective-permute-start.2 = (bf16[16,2,2,256]{3,2,1,0:T(2,128)(2,1)S(1)}, bf16[16,2,2,256]{3,2,1,0:T(2,128)(2,1)S(1)}, u32[]{:S(2)}, u32[]{:S(2)}) collective-permute-start(bf16[16,2,2,256]{3,2,1,0:T(2,128)(2,1)S(1)} %get-tuple-element.16), channel_id=1, source_target_pairs={{0,3},{1,0},{2,1},{3,2},{4,7},{5,4},{6,5},{7,6},{8,11},{9,8},{10,9... | collective-permute-start | bytes 98312 | tf_op jit(solution)/shard_map/ppermute | solution.py:133
  19.5 0.5 fusion.50
  20.2 0.9 %collective-permute-done.2 = bf16[16,2,2,256]{3,2,1,0:T(2,128)(2,1)S(1)} collective-permute-done((bf16[16,2,2,256]{3,2,1,0:T(2,128)(2,1)S(1)}, bf16[16,2,2,256]{3,2,1,0:T(2,128)(2,1)S(1)}, u32[]{:S(2)}, u32[]{:S(2)}) %collective-permute-start.2) | collective-permute-done | bytes 32800 | tf_op jit(solution)/shard_map/ppermute | solution.py:133
  21.1 0.2 maximum_bitcast_fusion
  21.4 1.3 %collective-permute-start.3 = (bf16[16,16,256]{2,1,0:T(8,128)(2,1)S(1)}, bf16[16,16,256]{2,1,0:T(8,128)(2,1)S(1)}, u32[]{:S(2)}, u32[]{:S(2)}) collective-permute-start(bf16[16,16,256]{2,1,0:T(8,128)(2,1)S(1)} %bitcast.72), channel_id=1, source_target_pairs={{4,0},{8,4},{12,8},{16,12},{20,16},{24,20},{28,24},{5,1},{9,5},{13... | collective-permute-start | bytes 393224 | tf_op jit(solution)/shard_map/ppermute | solution.py:143
  22.7 1.3 %collective-permute-start.4 = (bf16[16,16,256]{2,1,0:T(8,128)(2,1)S(1)}, bf16[16,16,256]{2,1,0:T(8,128)(2,1)S(1)}, u32[]{:S(2)}, u32[]{:S(2)}) collective-permute-start(bf16[16,16,256]{2,1,0:T(8,128)(2,1)S(1)} %bitcast.73), channel_id=1, source_target_pairs={{8,0},{12,4},{16,8},{20,12},{24,16},{28,20},{9,1},{13,5},{17,9},{2... | collective-permute-start | bytes 393224 | tf_op jit(solution)/shard_map/ppermute | solution.py:143
  24.0 1.3 %collective-permute-start.5 = (bf16[16,16,256]{2,1,0:T(8,128)(2,1)S(1)}, bf16[16,16,256]{2,1,0:T(8,128)(2,1)S(1)}, u32[]{:S(2)}, u32[]{:S(2)}) collective-permute-start(bf16[16,16,256]{2,1,0:T(8,128)(2,1)S(1)} %bitcast.74), channel_id=1, source_target_pairs={{12,0},{16,4},{20,8},{24,12},{28,16},{13,1},{17,5},{21,9},{25,13},... | collective-permute-start | bytes 393224 | tf_op jit(solution)/shard_map/ppermute | solution.py:143
  25.3 1.3 %collective-permute-start.6 = (bf16[16,16,256]{2,1,0:T(8,128)(2,1)S(1)}, bf16[16,16,256]{2,1,0:T(8,128)(2,1)S(1)}, u32[]{:S(2)}, u32[]{:S(2)}) collective-permute-start(bf16[16,16,256]{2,1,0:T(8,128)(2,1)S(1)} %bitcast.75), channel_id=1, source_target_pairs={{16,0},{20,4},{24,8},{28,12},{17,1},{21,5},{25,9},{29,13},{18,2},{... | collective-permute-start | bytes 393224 | tf_op jit(solution)/shard_map/ppermute | solution.py:143
  26.6 1.3 %collective-permute-start.7 = (bf16[16,16,256]{2,1,0:T(8,128)(2,1)S(1)}, bf16[16,16,256]{2,1,0:T(8,128)(2,1)S(1)}, u32[]{:S(2)}, u32[]{:S(2)}) collective-permute-start(bf16[16,16,256]{2,1,0:T(8,128)(2,1)S(1)} %bitcast.76), channel_id=1, source_target_pairs={{20,0},{24,4},{28,8},{21,1},{25,5},{29,9},{22,2},{26,6},{30,10},{2... | collective-permute-start | bytes 393224 | tf_op jit(solution)/shard_map/ppermute | solution.py:143
  27.9 1.2 %collective-permute-done.3 = bf16[16,16,256]{2,1,0:T(8,128)(2,1)S(1)} collective-permute-done((bf16[16,16,256]{2,1,0:T(8,128)(2,1)S(1)}, bf16[16,16,256]{2,1,0:T(8,128)(2,1)S(1)}, u32[]{:S(2)}, u32[]{:S(2)}) %collective-permute-start.3) | collective-permute-done | bytes 131104 | tf_op jit(solution)/shard_map/ppermute | solution.py:143
  29.1 1.3 %collective-permute-start.8 = (bf16[16,16,256]{2,1,0:T(8,128)(2,1)S(1)}, bf16[16,16,256]{2,1,0:T(8,128)(2,1)S(1)}, u32[]{:S(2)}, u32[]{:S(2)}) collective-permute-start(bf16[16,16,256]{2,1,0:T(8,128)(2,1)S(1)} %bitcast.77), channel_id=1, source_target_pairs={{24,0},{28,4},{25,1},{29,5},{26,2},{30,6},{27,3},{31,7}} | collective-permute-start | bytes 393224 | tf_op jit(solution)/shard_map/ppermute | solution.py:143
  30.4 2.7 %collective-permute-done.4 = bf16[16,16,256]{2,1,0:T(8,128)(2,1)S(1)} collective-permute-done((bf16[16,16,256]{2,1,0:T(8,128)(2,1)S(1)}, bf16[16,16,256]{2,1,0:T(8,128)(2,1)S(1)}, u32[]{:S(2)}, u32[]{:S(2)}) %collective-permute-start.4) | collective-permute-done | bytes 131104 | tf_op jit(solution)/shard_map/ppermute | solution.py:143
  33.1 1.5 %collective-permute-start.9 = (bf16[16,16,256]{2,1,0:T(8,128)(2,1)S(1)}, bf16[16,16,256]{2,1,0:T(8,128)(2,1)S(1)}, u32[]{:S(2)}, u32[]{:S(2)}) collective-permute-start(bf16[16,16,256]{2,1,0:T(8,128)(2,1)S(1)} %bitcast.78), channel_id=1, source_target_pairs={{28,0},{29,1},{30,2},{31,3}} | collective-permute-start | bytes 393224 | tf_op jit(solution)/shard_map/ppermute | solution.py:143
  34.6 0.5 collective-permute-done.5
  35.1 15.9 %collective-permute-done.6 = bf16[16,16,256]{2,1,0:T(8,128)(2,1)S(1)} collective-permute-done((bf16[16,16,256]{2,1,0:T(8,128)(2,1)S(1)}, bf16[16,16,256]{2,1,0:T(8,128)(2,1)S(1)}, u32[]{:S(2)}, u32[]{:S(2)}) %collective-permute-start.6) | collective-permute-done | bytes 131104 | tf_op jit(solution)/shard_map/ppermute | solution.py:143
  50.9 2.1 %collective-permute-done.7 = bf16[16,16,256]{2,1,0:T(8,128)(2,1)S(1)} collective-permute-done((bf16[16,16,256]{2,1,0:T(8,128)(2,1)S(1)}, bf16[16,16,256]{2,1,0:T(8,128)(2,1)S(1)}, u32[]{:S(2)}, u32[]{:S(2)}) %collective-permute-start.7) | collective-permute-done | bytes 131104 | tf_op jit(solution)/shard_map/ppermute | solution.py:143
  53.2 0.3 convert_element_type.78.white_ref
  53.5 3.9 %shard_map.38 = f32[32,2,16,256]{3,2,1,0:T(8,128)S(1)} custom-call(s32[32]{0:T(128)S(1)} %get-tuple-element.30.offsets_ref, s32[1]{0:T(128)} %constant.111.clone.1.base_ref, f32[144,16,256]{2,1,0:T(8,128)S(1)} %convert_element_type.78.white_ref), custom_call_target="tpu_custom_call" | custom-call | flops 16777216 | bytes 3407872 | tf_op jit(solution)/shard_map/pallas_call | solution.py:60
  57.4 0.9 %convert_element_type.82 = bf16[32,2,16,256]{3,2,1,0:T(8,128)(2,1)} convert(f32[32,2,16,256]{3,2,1,0:T(8,128)S(1)} %shard_map.38) | non-fusion elementwise | flops 262144 | bytes 1572864 | tf_op jit(solution)/shard_map/convert_element_type | solution.py:160
  58.3 1.5 %collective-permute-start.11 = (bf16[32,2,16,256]{3,2,1,0:T(8,128)(2,1)}, bf16[32,2,16,256]{3,2,1,0:T(8,128)(2,1)}, u32[]{:S(2)}, u32[]{:S(2)}) collective-permute-start(bf16[32,2,16,256]{3,2,1,0:T(8,128)(2,1)} %convert_element_type.82), channel_id=1, source_target_pairs={{0,2},{1,3},{2,0},{3,1},{4,6},{5,7},{6,4},{7,5},{8,10},{9,11},{10,... | collective-permute-start | bytes 1572872 | tf_op jit(solution)/shard_map/ppermute | solution.py:163
  59.8 0.3 fusion.54
  60.1 3.9 %shard_map.39 = f32[32,2,16,256]{3,2,1,0:T(8,128)S(1)} custom-call(s32[32]{0:T(128)S(1)} %get-tuple-element.32.offsets_ref, s32[1]{0:T(128)} %constant.111.clone.1.base_ref, f32[144,16,256]{2,1,0:T(8,128)S(1)} %convert_element_type.78.white_ref), custom_call_target="tpu_custom_call" | custom-call | flops 16777216 | bytes 3407872 | tf_op jit(solution)/shard_map/pallas_call | solution.py:60
  64.0 0.9 %convert_element_type.83 = bf16[32,2,16,256]{3,2,1,0:T(8,128)(2,1)} convert(f32[32,2,16,256]{3,2,1,0:T(8,128)S(1)} %shard_map.39) | non-fusion elementwise | flops 262144 | bytes 1572864 | tf_op jit(solution)/shard_map/convert_element_type | solution.py:160
  64.9 2.0 %negate_convert_fusion.1 = (bf16[1024,16,32]{0,2,1:T(8,128)(2,1)}, bf16[1024,16,32]{0,2,1:T(8,128)(2,1)}) fusion(f32[1024,16]{0,1:T(8,128)S(1)} %get-tuple-element.22, f32[1024,32]{0,1:T(8,128)S(1)} %get-tuple-element.28, f32[1024,16]{0,1:T(8,128)S(1)} %get-tuple-element.21, f32[1024,32]{0,1:T(8,128)S(1)} %get-tuple-element.27), kind=kLoop, calls=%fused_computation.15 | loop fusion | flops 4718592 | bytes 2490368 | tf_op jit(solution)/shard_map/convert.2
  66.9 1.5 %copy.7 = bf16[1,1024,512]{2,1,0:T(8,128)(2,1)S(1)} copy(bf16[1,1024,512]{1,2,0:T(8,128)(2,1)} %bitcast.71) | data formatting | bytes 2097152 | tf_op jit(solution)/shard_map/sub | solution.py:27
  68.4 2.3 %copy.8 = bf16[1,1024,512]{2,1,0:T(8,128)(2,1)} copy(bf16[1,1024,512]{1,2,0:T(8,128)(2,1)} %bitcast.70) | data formatting | bytes 2097152 | tf_op jit(solution)/shard_map/neg | solution.py:29
  70.7 3.9 %shard_map.37 = f32[32,2,16,256]{3,2,1,0:T(8,128)S(1)} custom-call(s32[32]{0:T(128)S(1)} %get-tuple-element.29.offsets_ref, s32[1]{0:T(128)} %constant.111.clone.1.base_ref, f32[144,16,256]{2,1,0:T(8,128)S(1)} %convert_element_type.78.white_ref), custom_call_target="tpu_custom_call" | custom-call | flops 16777216 | bytes 3407872 | tf_op jit(solution)/shard_map/pallas_call | solution.py:60
  74.7 0.6 collective-permute-start.10
  75.2 3.9 %shard_map.40 = f32[32,2,16,256]{3,2,1,0:T(8,128)S(1)} custom-call(s32[32]{0:T(128)S(1)} %get-tuple-element.31.offsets_ref, s32[1]{0:T(128)} %constant.111.clone.1.base_ref, f32[144,16,256]{2,1,0:T(8,128)S(1)} %convert_element_type.78.white_ref), custom_call_target="tpu_custom_call" | custom-call | flops 16777216 | bytes 3407872 | tf_op jit(solution)/shard_map/pallas_call | solution.py:60
  79.1 0.4 convolution_bitcast_fusion
  79.6 1.5 %convolution_bitcast_fusion.2 = f32[32,16,512]{2,1,0:T(8,128)S(1)} fusion(bf16[32,2,16,256]{3,2,1,0:T(8,128)(2,1)} %collective-permute-done.11, s32[]{:T(128)S(6)} %select_n.109, bf16[1,1024,512]{2,1,0:T(8,128)(2,1)S(1)} %copy.7, bf16[1,1024,512]{2,1,0:T(8,128)(2,1)S(1)} %copy-done), kind=kOutput, calls=%fused_computation.19 | convolution fusion | flops 269484032 | bytes 3670020 | tf_op jit(solution)/shard_map/opck,pkl->ocl/dot_general | solution.py:166
  81.1 1.5 %convolution_bitcast_fusion.1 = f32[32,16,512]{2,1,0:T(8,128)S(1)} fusion(bf16[32,2,16,256]{3,2,1,0:T(8,128)(2,1)} %collective-permute-done.12, s32[]{:T(128)S(6)} %select_n.108, bf16[1,1024,512]{2,1,0:T(8,128)(2,1)S(1)} %copy.7, bf16[1,1024,512]{2,1,0:T(8,128)(2,1)S(1)} %copy-done), kind=kOutput, calls=%fused_computation.18 | convolution fusion | flops 269484032 | bytes 3670020 | tf_op jit(solution)/shard_map/opck,pkl->ocl/dot_general | solution.py:166
  82.6 0.8 collective-permute-done.10
  83.3 1.3 %fusion.11 = bf16[32,16,512]{2,1,0:T(8,128)(2,1)} fusion(f32[32,16,512]{2,1,0:T(8,128)S(1)} %convolution_bitcast_fusion, f32[32,16,512]{2,1,0:T(8,128)S(1)} %convolution_bitcast_fusion.1, f32[32,16,512]{2,1,0:T(8,128)S(1)} %convolution_bitcast_fusion.2, bf16[32,2,16,256]{3,2,1,0:T(8,128)(2,1)S(1)} %collective-permute-done.10, s32[]{:T(128)S(6)} %select_n.110, ...), kind=kOutput, calls=%fused_computation.25 | convolution fusion | flops 270794752 | bytes 6291460 | tf_op jit(solution)/shard_map/opck,pkl->ocl/dot_general | solution.py:166
  (32 shorter events, 0.8 us)
Async XLA Ops:
  13.4 6.1 %copy-start.1 = (s32[1024]{0:T(1024)S(1)}, s32[1024]{0:T(1024)}, u32[]{:S(2)}) copy-start(s32[1024]{0:T(1024)} %param.4) | copy-start | bytes 12292
  13.4 6.7 %copy-start.2 = (s32[128]{0:T(128)S(1)}, s32[128]{0:T(128)}, u32[]{:S(2)}) copy-start(s32[128]{0:T(128)} %param.5) | copy-start | bytes 1540
  15.1 5.1 %collective-permute-start = (bf16[16,2,2,256]{3,2,1,0:T(2,128)(2,1)S(1)}, bf16[16,2,2,256]{3,2,1,0:T(2,128)(2,1)S(1)}, u32[]{:S(2)}, u32[]{:S(2)}) collective-permute-start(bf16[16,2,2,256]{3,2,1,0:T(2,128)(2,1)S(1)} %get-tuple-element.18), channel_id=1, source_target_pairs={{0,1},{1,2},{2,3},{3,0},{4,5},{5,6},{6,7},{7,4},{8,9},{9,10},{10,1... | collective-permute-start | bytes 98312 | tf_op jit(solution)/shard_map/ppermute | solution.py:133
  15.6 4.6 %collective-permute-start.1 = (bf16[16,2,2,256]{3,2,1,0:T(2,128)(2,1)S(1)}, bf16[16,2,2,256]{3,2,1,0:T(2,128)(2,1)S(1)}, u32[]{:S(2)}, u32[]{:S(2)}) collective-permute-start(bf16[16,2,2,256]{3,2,1,0:T(2,128)(2,1)S(1)} %get-tuple-element.17), channel_id=1, source_target_pairs={{0,2},{1,3},{2,0},{3,1},{4,6},{5,7},{6,4},{7,5},{8,10},{9,11},{10,... | collective-permute-start | bytes 98312 | tf_op jit(solution)/shard_map/ppermute | solution.py:133
  18.2 3.0 %collective-permute-start.2 = (bf16[16,2,2,256]{3,2,1,0:T(2,128)(2,1)S(1)}, bf16[16,2,2,256]{3,2,1,0:T(2,128)(2,1)S(1)}, u32[]{:S(2)}, u32[]{:S(2)}) collective-permute-start(bf16[16,2,2,256]{3,2,1,0:T(2,128)(2,1)S(1)} %get-tuple-element.16), channel_id=1, source_target_pairs={{0,3},{1,0},{2,1},{3,2},{4,7},{5,4},{6,5},{7,6},{8,11},{9,8},{10,9... | collective-permute-start | bytes 98312 | tf_op jit(solution)/shard_map/ppermute | solution.py:133
  21.4 7.7 %collective-permute-start.3 = (bf16[16,16,256]{2,1,0:T(8,128)(2,1)S(1)}, bf16[16,16,256]{2,1,0:T(8,128)(2,1)S(1)}, u32[]{:S(2)}, u32[]{:S(2)}) collective-permute-start(bf16[16,16,256]{2,1,0:T(8,128)(2,1)S(1)} %bitcast.72), channel_id=1, source_target_pairs={{4,0},{8,4},{12,8},{16,12},{20,16},{24,20},{28,24},{5,1},{9,5},{13... | collective-permute-start | bytes 393224 | tf_op jit(solution)/shard_map/ppermute | solution.py:143
  22.7 10.4 %collective-permute-start.4 = (bf16[16,16,256]{2,1,0:T(8,128)(2,1)S(1)}, bf16[16,16,256]{2,1,0:T(8,128)(2,1)S(1)}, u32[]{:S(2)}, u32[]{:S(2)}) collective-permute-start(bf16[16,16,256]{2,1,0:T(8,128)(2,1)S(1)} %bitcast.73), channel_id=1, source_target_pairs={{8,0},{12,4},{16,8},{20,12},{24,16},{28,20},{9,1},{13,5},{17,9},{2... | collective-permute-start | bytes 393224 | tf_op jit(solution)/shard_map/ppermute | solution.py:143
  24.0 11.1 %collective-permute-start.5 = (bf16[16,16,256]{2,1,0:T(8,128)(2,1)S(1)}, bf16[16,16,256]{2,1,0:T(8,128)(2,1)S(1)}, u32[]{:S(2)}, u32[]{:S(2)}) collective-permute-start(bf16[16,16,256]{2,1,0:T(8,128)(2,1)S(1)} %bitcast.74), channel_id=1, source_target_pairs={{12,0},{16,4},{20,8},{24,12},{28,16},{13,1},{17,5},{21,9},{25,13},... | collective-permute-start | bytes 393224 | tf_op jit(solution)/shard_map/ppermute | solution.py:143
  25.3 25.6 %collective-permute-start.6 = (bf16[16,16,256]{2,1,0:T(8,128)(2,1)S(1)}, bf16[16,16,256]{2,1,0:T(8,128)(2,1)S(1)}, u32[]{:S(2)}, u32[]{:S(2)}) collective-permute-start(bf16[16,16,256]{2,1,0:T(8,128)(2,1)S(1)} %bitcast.75), channel_id=1, source_target_pairs={{16,0},{20,4},{24,8},{28,12},{17,1},{21,5},{25,9},{29,13},{18,2},{... | collective-permute-start | bytes 393224 | tf_op jit(solution)/shard_map/ppermute | solution.py:143
  26.6 26.5 %collective-permute-start.7 = (bf16[16,16,256]{2,1,0:T(8,128)(2,1)S(1)}, bf16[16,16,256]{2,1,0:T(8,128)(2,1)S(1)}, u32[]{:S(2)}, u32[]{:S(2)}) collective-permute-start(bf16[16,16,256]{2,1,0:T(8,128)(2,1)S(1)} %bitcast.76), channel_id=1, source_target_pairs={{20,0},{24,4},{28,8},{21,1},{25,5},{29,9},{22,2},{26,6},{30,10},{2... | collective-permute-start | bytes 393224 | tf_op jit(solution)/shard_map/ppermute | solution.py:143
  29.1 24.0 %collective-permute-start.8 = (bf16[16,16,256]{2,1,0:T(8,128)(2,1)S(1)}, bf16[16,16,256]{2,1,0:T(8,128)(2,1)S(1)}, u32[]{:S(2)}, u32[]{:S(2)}) collective-permute-start(bf16[16,16,256]{2,1,0:T(8,128)(2,1)S(1)} %bitcast.77), channel_id=1, source_target_pairs={{24,0},{28,4},{25,1},{29,5},{26,2},{30,6},{27,3},{31,7}} | collective-permute-start | bytes 393224 | tf_op jit(solution)/shard_map/ppermute | solution.py:143
  33.1 20.1 %collective-permute-start.9 = (bf16[16,16,256]{2,1,0:T(8,128)(2,1)S(1)}, bf16[16,16,256]{2,1,0:T(8,128)(2,1)S(1)}, u32[]{:S(2)}, u32[]{:S(2)}) collective-permute-start(bf16[16,16,256]{2,1,0:T(8,128)(2,1)S(1)} %bitcast.78), channel_id=1, source_target_pairs={{28,0},{29,1},{30,2},{31,3}} | collective-permute-start | bytes 393224 | tf_op jit(solution)/shard_map/ppermute | solution.py:143
  58.3 21.3 %collective-permute-start.11 = (bf16[32,2,16,256]{3,2,1,0:T(8,128)(2,1)}, bf16[32,2,16,256]{3,2,1,0:T(8,128)(2,1)}, u32[]{:S(2)}, u32[]{:S(2)}) collective-permute-start(bf16[32,2,16,256]{3,2,1,0:T(8,128)(2,1)} %convert_element_type.82), channel_id=1, source_target_pairs={{0,2},{1,3},{2,0},{3,1},{4,6},{5,7},{6,4},{7,5},{8,10},{9,11},{10,... | collective-permute-start | bytes 1572872 | tf_op jit(solution)/shard_map/ppermute | solution.py:163
  64.8 16.2 %collective-permute-start.12 = (bf16[32,2,16,256]{3,2,1,0:T(8,128)(2,1)}, bf16[32,2,16,256]{3,2,1,0:T(8,128)(2,1)}, u32[]{:S(2)}, u32[]{:S(2)}) collective-permute-start(bf16[32,2,16,256]{3,2,1,0:T(8,128)(2,1)} %convert_element_type.83), channel_id=1, source_target_pairs={{0,3},{1,0},{2,1},{3,2},{4,7},{5,4},{6,5},{7,6},{8,11},{9,8},{10,9... | collective-permute-start | bytes 1572872 | tf_op jit(solution)/shard_map/ppermute | solution.py:163
  74.7 4.5 %copy-start = (bf16[1,1024,512]{2,1,0:T(8,128)(2,1)S(1)}, bf16[1,1024,512]{2,1,0:T(8,128)(2,1)}, u32[]{:S(2)}) copy-start(bf16[1,1024,512]{2,1,0:T(8,128)(2,1)} %copy.8) | copy-start | bytes 3145732
  74.7 8.7 %collective-permute-start.10 = (bf16[32,2,16,256]{3,2,1,0:T(8,128)(2,1)S(1)}, bf16[32,2,16,256]{3,2,1,0:T(8,128)(2,1)S(1)}, u32[]{:S(2)}, u32[]{:S(2)}) collective-permute-start(bf16[32,2,16,256]{3,2,1,0:T(8,128)(2,1)S(1)} %convert_element_type.79), channel_id=1, source_target_pairs={{0,1},{1,2},{2,3},{3,0},{4,5},{5,6},{6,7},{7,4},{8,9},{9,10},{10,1... | collective-permute-start | bytes 1572872 | tf_op jit(solution)/shard_map/ppermute | solution.py:163

commit v20 on v19

--- a/solution.py
+++ b/solution.py
@@ -150,7 +150,7 @@
     off_dev = band_span // gy_count
     me = lax.axis_index("gy")
     offsets = pair_offsets.astype(jnp.int32)
-    inverse = inverse_table(kept_bins)
+    inverse, padded = lax.optimization_barrier((inverse_table(kept_bins), padded))
     norm_scale = 0.5 / math.sqrt(windows * bin_count)
     lagged = None
     for shift in list(range(1, gy_count)) + [0]:

time: 85.1 us -> 85.9 us (level)
  waiting for transfers between devices: 24.1 us -> 28.5 us
  local copies, waits for them, and re-layouts: 7.97 us -> 5.25 us
  starting transfers between devices: 15.7 us -> 14.6 us
    ppermute x3, waiting for transfers between devices: 0.78 us -> 6.7 us  [local(): part = lax.ppermute(part, 'gy', perm=pairs)]
    neg x1, local copies, waits for them, and re-layouts: 2.31 us -> 0.54 us  [inverse_table(): return jnp.stack([cos_t, -sin_t], axis=0).astype(jnp.bfloat16)]
    sub x1, local copies, waits for them, and re-layouts: 1.49 us -> 0.54 us  [inverse_table(): cos_t = (cos_f * cos_c - sin_f * sin_c).reshape(kept_bins.shape[0], LAGS)]
    ppermute x3, waiting for transfers between devices: 0.94 us -> 0.01 us  [local(): lax.ppermute(piece, 'gy', perm=[(src, (src + shift) % gy_count) for src i...]
    ppermute x3, starting transfers between devices: 2.05 us -> 1.13 us  [local(): part = lax.ppermute(part, 'gy', perm=pairs)]
    another operation x2 -> x3, other arithmetic: 5.69 us -> 5.96 us
  transfers between devices with their start and end apart: 13 -> 13, of which waited for: 7 -> 7; matrix products, arithmetic and copies ran while one was open for 13% -> 10% of each run, Pallas kernels for 14% -> 14%
where the time goes in v20:
time: 85.9 us; the launch traced here: 85.4 us
  waiting for transfers between devices  28.5 us (33%)
  Pallas kernels  15.5 us (18%)
  starting transfers between devices  14.6 us (17%)
  other arithmetic  14.1 us (16%)
  matrix products  7.11 us (8%)
  local copies, waits for them, and re-layouts  5.25 us (6%)
    ppermute x7, waiting for transfers between devices, local(): blocks.append(lax.ppermute(rows_white, 'gx', perm=pairs))  21.8 us
    pallas_call x4, Pallas kernels, cross_spectra(): pl.pallas_call(kernel, grid_spec=pltpu.PrefetchScalarGridSpec(num_scalar_...  15.5 us
    ppermute x7, starting transfers between devices, local(): blocks.append(lax.ppermute(rows_white, 'gx', perm=pairs))  9.02 us
    ppermute x3, waiting for transfers between devices, local(): part = lax.ppermute(part, 'gy', perm=pairs)  6.7 us
    dot_general x4, matrix products, local(): jnp.einsum('opck,pkl->ocl', part, rows, preferred_element_type=jnp.float32)  4.65 us
    ppermute x3, starting transfers between devices, local(): lax.ppermute(piece, 'gy', perm=[(src, (src + shift) % gy_count) for src i...  4.46 us
    another operation x2, other arithmetic  4.43 us
    dot_general x1, matrix products, forward_spectra(): jnp.dot(record_rows.reshape(row_count * block_count, block_len), small_ta...  2.46 us
  transfers between devices with their start and end apart: 13, of which 7 were waited for; matrix products, arithmetic and copies ran while one was open for 10% of the time, Pallas kernels for 14%

profile of v20, /device:TPU:0, one launch (start us, length us, event | category | flops | bytes accessed | tf_op | source)
XLA Modules:
  0.0 85.4 jit_solution(17720423409061785085)
XLA Ops:
  0.0 1.2 %fusion.46 = (f32[32,1024]{1,0:T(8,128)S(1)}, f32[32,1024]{1,0:T(8,128)S(1)}) fusion(s32[1024]{0:T(1024)} %param.4), kind=kLoop, calls=%fused_computation.78 | loop fusion | flops 458752 | bytes 266240 | tf_op jit(solution)/shard_map/cos | solution.py:90
  1.2 0.7 add_select_fusion.5
  1.9 1.8 %fusion.35 = (f32[64,1024]{1,0:T(8,128)S(1)}, f32[64,1024]{1,0:T(8,128)S(1)}) fusion(s32[1024]{0:T(1024)} %param.4, s32[64]{0:T(128)S(1)} %iota_multiply_fusion), kind=kLoop, calls=%fused_computation.61 | loop fusion | flops 917504 | bytes 528640 | tf_op jit(solution)/shard_map/cos | solution.py:90
  3.7 1.2 %reshape_reshape.3 = bf16[128,2048]{1,0:T(8,128)(2,1)S(1)} reshape(bf16[16,2,8192]{2,1,0:T(2,128)(2,1)} %param.3) | data formatting | bytes 1048576 | tf_op jit(solution)/shard_map/reshape;reshape | solution.py:103
  4.9 3.7 %subtract_convert_fusion = (bf16[64,32,1024]{2,1,0:T(8,128)(2,1)S(1)}, bf16[64,32,1024]{2,1,0:T(8,128)(2,1)S(1)}) fusion(f32[64,1024]{1,0:T(8,128)S(1)} %get-tuple-element.24, f32[32,1024]{1,0:T(8,128)S(1)} %get-tuple-element.30, f32[64,1024]{1,0:T(8,128)S(1)} %get-tuple-element.23, f32[32,1024]{1,0:T(8,128)S(1)} %get-tuple-element.29), kind=kLoop, calls=%fused_computation.5 | loop fusion | flops 18874368 | bytes 9175040 | tf_op jit(solution)/shard_map/convert.3
  8.5 2.5 %fusion.4 = f32[128,2048]{0,1:T(8,128)S(1)} fusion(bf16[128,2048]{1,0:T(8,128)(2,1)S(1)} %reshape_reshape.3, bf16[2048,1024]{1,0:T(8,128)(2,1)S(1)} %bitcast.69, bf16[2048,1024]{1,0:T(8,128)(2,1)S(1)} %bitcast.68), kind=kOutput, calls=%fused_computation.6 | convolution fusion | flops 1090519040 | bytes 9961472 | tf_op jit(solution)/shard_map/dot_general | solution.py:102
  11.0 0.3 copy.6
  11.3 0.9 %reshape.439 = f32[32,4,2,1024]{3,2,1,0:T(2,128)S(1)} reshape(f32[128,2048]{1,0:T(8,128)S(1)} %copy.6) | data formatting | bytes 2097152 | tf_op jit(solution)/shard_map/reshape | solution.py:106
  12.2 1.2 %fusion.60 = (f32[32,4,1,1024]{3,2,1,0:T(1,128)S(1)}, f32[32,4,1,1024]{3,2,1,0:T(1,128)S(1)}) fusion(f32[32,4,2,1024]{3,2,1,0:T(2,128)S(1)} %reshape.439), kind=kLoop, calls=%fused_computation.115 | loop fusion | bytes 2097152 | tf_op jit(solution)/shard_map/slice | solution.py:113
  13.6 0.8 fusion.13
  14.5 0.2 concatenate.18
  15.1 0.5 collective-permute-start
  15.6 2.6 %collective-permute-start.1 = (bf16[16,2,2,256]{3,2,1,0:T(2,128)(2,1)S(1)}, bf16[16,2,2,256]{3,2,1,0:T(2,128)(2,1)S(1)}, u32[]{:S(2)}, u32[]{:S(2)}) collective-permute-start(bf16[16,2,2,256]{3,2,1,0:T(2,128)(2,1)S(1)} %get-tuple-element.21), channel_id=1, source_target_pairs={{0,2},{1,3},{2,0},{3,1},{4,6},{5,7},{6,4},{7,5},{8,10},{9,11},{10,... | collective-permute-start | bytes 98312 | tf_op jit(solution)/shard_map/ppermute | solution.py:133
  18.1 1.4 %collective-permute-start.2 = (bf16[16,2,2,256]{3,2,1,0:T(2,128)(2,1)S(1)}, bf16[16,2,2,256]{3,2,1,0:T(2,128)(2,1)S(1)}, u32[]{:S(2)}, u32[]{:S(2)}) collective-permute-start(bf16[16,2,2,256]{3,2,1,0:T(2,128)(2,1)S(1)} %get-tuple-element.20), channel_id=1, source_target_pairs={{0,3},{1,0},{2,1},{3,2},{4,7},{5,4},{6,5},{7,6},{8,11},{9,8},{10,9... | collective-permute-start | bytes 98312 | tf_op jit(solution)/shard_map/ppermute | solution.py:133
  19.5 0.5 fusion.48
  20.1 0.3 fusion.50
  20.4 0.8 subtract_convert_fusion.1
  21.2 0.5 copy.4
  21.8 0.5 copy.5
  22.3 1.5 %pad_maximum_fusion = bf16[2,1024,512]{2,1,0:T(8,128)(2,1)} fusion(bf16[1,1024,512]{2,1,0:T(8,128)(2,1)S(1)} %copy.5, bf16[1,1024,512]{2,1,0:T(8,128)(2,1)S(1)} %copy.4), kind=kLoop, calls=%fused_computation.7 | loop fusion | flops 1048576 | bytes 4194304 | tf_op jit(solution)/shard_map/stack | solution.py:29
  24.0 0.2 maximum_bitcast_fusion
  24.2 1.3 %collective-permute-start.3 = (bf16[16,16,256]{2,1,0:T(8,128)(2,1)S(1)}, bf16[16,16,256]{2,1,0:T(8,128)(2,1)S(1)}, u32[]{:S(2)}, u32[]{:S(2)}) collective-permute-start(bf16[16,16,256]{2,1,0:T(8,128)(2,1)S(1)} %bitcast.72), channel_id=1, source_target_pairs={{4,0},{8,4},{12,8},{16,12},{20,16},{24,20},{28,24},{5,1},{9,5},{13... | collective-permute-start | bytes 393224 | tf_op jit(solution)/shard_map/ppermute | solution.py:143
  25.5 1.3 %collective-permute-start.4 = (bf16[16,16,256]{2,1,0:T(8,128)(2,1)S(1)}, bf16[16,16,256]{2,1,0:T(8,128)(2,1)S(1)}, u32[]{:S(2)}, u32[]{:S(2)}) collective-permute-start(bf16[16,16,256]{2,1,0:T(8,128)(2,1)S(1)} %bitcast.73), channel_id=1, source_target_pairs={{8,0},{12,4},{16,8},{20,12},{24,16},{28,20},{9,1},{13,5},{17,9},{2... | collective-permute-start | bytes 393224 | tf_op jit(solution)/shard_map/ppermute | solution.py:143
  26.8 1.3 %collective-permute-start.5 = (bf16[16,16,256]{2,1,0:T(8,128)(2,1)S(1)}, bf16[16,16,256]{2,1,0:T(8,128)(2,1)S(1)}, u32[]{:S(2)}, u32[]{:S(2)}) collective-permute-start(bf16[16,16,256]{2,1,0:T(8,128)(2,1)S(1)} %bitcast.74), channel_id=1, source_target_pairs={{12,0},{16,4},{20,8},{24,12},{28,16},{13,1},{17,5},{21,9},{25,13},... | collective-permute-start | bytes 393224 | tf_op jit(solution)/shard_map/ppermute | solution.py:143
  28.1 1.3 %collective-permute-start.6 = (bf16[16,16,256]{2,1,0:T(8,128)(2,1)S(1)}, bf16[16,16,256]{2,1,0:T(8,128)(2,1)S(1)}, u32[]{:S(2)}, u32[]{:S(2)}) collective-permute-start(bf16[16,16,256]{2,1,0:T(8,128)(2,1)S(1)} %bitcast.75), channel_id=1, source_target_pairs={{16,0},{20,4},{24,8},{28,12},{17,1},{21,5},{25,9},{29,13},{18,2},{... | collective-permute-start | bytes 393224 | tf_op jit(solution)/shard_map/ppermute | solution.py:143
  29.4 1.3 %collective-permute-start.7 = (bf16[16,16,256]{2,1,0:T(8,128)(2,1)S(1)}, bf16[16,16,256]{2,1,0:T(8,128)(2,1)S(1)}, u32[]{:S(2)}, u32[]{:S(2)}) collective-permute-start(bf16[16,16,256]{2,1,0:T(8,128)(2,1)S(1)} %bitcast.76), channel_id=1, source_target_pairs={{20,0},{24,4},{28,8},{21,1},{25,5},{29,9},{22,2},{26,6},{30,10},{2... | collective-permute-start | bytes 393224 | tf_op jit(solution)/shard_map/ppermute | solution.py:143
  30.7 0.3 collective-permute-done.3
  31.1 1.3 %collective-permute-start.8 = (bf16[16,16,256]{2,1,0:T(8,128)(2,1)S(1)}, bf16[16,16,256]{2,1,0:T(8,128)(2,1)S(1)}, u32[]{:S(2)}, u32[]{:S(2)}) collective-permute-start(bf16[16,16,256]{2,1,0:T(8,128)(2,1)S(1)} %bitcast.77), channel_id=1, source_target_pairs={{24,0},{28,4},{25,1},{29,5},{26,2},{30,6},{27,3},{31,7}} | collective-permute-start | bytes 393224 | tf_op jit(solution)/shard_map/ppermute | solution.py:143
  32.4 2.6 %collective-permute-done.4 = bf16[16,16,256]{2,1,0:T(8,128)(2,1)S(1)} collective-permute-done((bf16[16,16,256]{2,1,0:T(8,128)(2,1)S(1)}, bf16[16,16,256]{2,1,0:T(8,128)(2,1)S(1)}, u32[]{:S(2)}, u32[]{:S(2)}) %collective-permute-start.4) | collective-permute-done | bytes 131104 | tf_op jit(solution)/shard_map/ppermute | solution.py:143
  35.0 1.3 %collective-permute-start.9 = (bf16[16,16,256]{2,1,0:T(8,128)(2,1)S(1)}, bf16[16,16,256]{2,1,0:T(8,128)(2,1)S(1)}, u32[]{:S(2)}, u32[]{:S(2)}) collective-permute-start(bf16[16,16,256]{2,1,0:T(8,128)(2,1)S(1)} %bitcast.78), channel_id=1, source_target_pairs={{28,0},{29,1},{30,2},{31,3}} | collective-permute-start | bytes 393224 | tf_op jit(solution)/shard_map/ppermute | solution.py:143
  36.3 1.1 %collective-permute-done.5 = bf16[16,16,256]{2,1,0:T(8,128)(2,1)S(1)} collective-permute-done((bf16[16,16,256]{2,1,0:T(8,128)(2,1)S(1)}, bf16[16,16,256]{2,1,0:T(8,128)(2,1)S(1)}, u32[]{:S(2)}, u32[]{:S(2)}) %collective-permute-start.5) | collective-permute-done | bytes 131104 | tf_op jit(solution)/shard_map/ppermute | solution.py:143
  37.3 15.3 %collective-permute-done.6 = bf16[16,16,256]{2,1,0:T(8,128)(2,1)S(1)} collective-permute-done((bf16[16,16,256]{2,1,0:T(8,128)(2,1)S(1)}, bf16[16,16,256]{2,1,0:T(8,128)(2,1)S(1)}, u32[]{:S(2)}, u32[]{:S(2)}) %collective-permute-start.6) | collective-permute-done | bytes 131104 | tf_op jit(solution)/shard_map/ppermute | solution.py:143
  52.7 2.4 %collective-permute-done.7 = bf16[16,16,256]{2,1,0:T(8,128)(2,1)S(1)} collective-permute-done((bf16[16,16,256]{2,1,0:T(8,128)(2,1)S(1)}, bf16[16,16,256]{2,1,0:T(8,128)(2,1)S(1)}, u32[]{:S(2)}, u32[]{:S(2)}) %collective-permute-start.7) | collective-permute-done | bytes 131104 | tf_op jit(solution)/shard_map/ppermute | solution.py:143
  55.2 0.3 convert_element_type.80.white_ref
  55.5 3.9 %shard_map.38 = f32[32,2,16,256]{3,2,1,0:T(8,128)S(1)} custom-call(s32[32]{0:T(128)S(1)} %get-tuple-element.34.offsets_ref, s32[1]{0:T(128)} %constant.111.clone.1.base_ref, f32[144,16,256]{2,1,0:T(8,128)S(1)} %convert_element_type.80.white_ref), custom_call_target="tpu_custom_call" | custom-call | flops 16777216 | bytes 3407872 | tf_op jit(solution)/shard_map/pallas_call | solution.py:60
  59.5 0.6 collective-permute-start.11
  60.1 3.9 %shard_map.39 = f32[32,2,16,256]{3,2,1,0:T(8,128)S(1)} custom-call(s32[32]{0:T(128)S(1)} %get-tuple-element.36.offsets_ref, s32[1]{0:T(128)} %constant.111.clone.1.base_ref, f32[144,16,256]{2,1,0:T(8,128)S(1)} %convert_element_type.80.white_ref), custom_call_target="tpu_custom_call" | custom-call | flops 16777216 | bytes 3407872 | tf_op jit(solution)/shard_map/pallas_call | solution.py:60
  64.0 0.9 %convert_element_type.83 = bf16[32,2,16,256]{3,2,1,0:T(8,128)(2,1)} convert(f32[32,2,16,256]{3,2,1,0:T(8,128)S(1)} %shard_map.39) | non-fusion elementwise | flops 262144 | bytes 1572864 | tf_op jit(solution)/shard_map/convert_element_type | solution.py:160
  64.9 3.9 %shard_map.37 = f32[32,2,16,256]{3,2,1,0:T(8,128)S(1)} custom-call(s32[32]{0:T(128)S(1)} %get-tuple-element.33.offsets_ref, s32[1]{0:T(128)} %constant.111.clone.1.base_ref, f32[144,16,256]{2,1,0:T(8,128)S(1)} %convert_element_type.80.white_ref), custom_call_target="tpu_custom_call" | custom-call | flops 16777216 | bytes 3407872 | tf_op jit(solution)/shard_map/pallas_call | solution.py:60
  68.7 0.9 %convert_element_type.81 = bf16[32,2,16,256]{3,2,1,0:T(8,128)(2,1)} convert(f32[32,2,16,256]{3,2,1,0:T(8,128)S(1)} %shard_map.37) | non-fusion elementwise | flops 262144 | bytes 1572864 | tf_op jit(solution)/shard_map/convert_element_type | solution.py:160
  69.6 0.5 collective-permute-start.10
  70.1 3.9 %shard_map.40 = f32[32,2,16,256]{3,2,1,0:T(8,128)S(1)} custom-call(s32[32]{0:T(128)S(1)} %get-tuple-element.35.offsets_ref, s32[1]{0:T(128)} %constant.111.clone.1.base_ref, f32[144,16,256]{2,1,0:T(8,128)S(1)} %convert_element_type.80.white_ref), custom_call_target="tpu_custom_call" | custom-call | flops 16777216 | bytes 3407872 | tf_op jit(solution)/shard_map/pallas_call | solution.py:60
  74.0 0.4 convolution_bitcast_fusion
  74.5 0.4 convolution_bitcast_fusion.2
  74.9 4.3 %collective-permute-done.12 = bf16[32,2,16,256]{3,2,1,0:T(8,128)(2,1)} collective-permute-done((bf16[32,2,16,256]{3,2,1,0:T(8,128)(2,1)}, bf16[32,2,16,256]{3,2,1,0:T(8,128)(2,1)}, u32[]{:S(2)}, u32[]{:S(2)}) %collective-permute-start.12) | collective-permute-done | bytes 524320 | tf_op jit(solution)/shard_map/ppermute | solution.py:163
  79.2 1.5 %convolution_bitcast_fusion.1 = f32[32,16,512]{2,1,0:T(8,128)S(1)} fusion(bf16[32,2,16,256]{3,2,1,0:T(8,128)(2,1)} %collective-permute-done.12, bf16[2,1024,512]{2,1,0:T(8,128)(2,1)S(1)} %copy-done, s32[]{:T(128)S(6)} %select_n.110), kind=kOutput, calls=%fused_computation.11 | convolution fusion | flops 268435456 | bytes 2097156 | tf_op jit(solution)/shard_map/opck,pkl->ocl/dot_general | solution.py:166
  80.7 2.4 %collective-permute-done.10 = bf16[32,2,16,256]{3,2,1,0:T(8,128)(2,1)} collective-permute-done((bf16[32,2,16,256]{3,2,1,0:T(8,128)(2,1)}, bf16[32,2,16,256]{3,2,1,0:T(8,128)(2,1)}, u32[]{:S(2)}, u32[]{:S(2)}) %collective-permute-start.10) | collective-permute-done | bytes 524320 | tf_op jit(solution)/shard_map/ppermute | solution.py:163
  83.1 2.3 %fusion.11 = bf16[32,16,512]{2,1,0:T(8,128)(2,1)} fusion(f32[32,16,512]{2,1,0:T(8,128)S(1)} %convolution_bitcast_fusion, f32[32,16,512]{2,1,0:T(8,128)S(1)} %convolution_bitcast_fusion.1, f32[32,16,512]{2,1,0:T(8,128)S(1)} %convolution_bitcast_fusion.2, bf16[32,2,16,256]{3,2,1,0:T(8,128)(2,1)} %collective-permute-done.10, ...), kind=kOutput, calls=%fused_computation.18 | convolution fusion | flops 269746176 | bytes 4718596 | tf_op jit(solution)/shard_map/opck,pkl->ocl/dot_general | solution.py:166
  (33 shorter events, 1.0 us)
Async XLA Ops:
  12.2 7.3 %copy-start.1 = (s32[1024]{0:T(1024)S(1)}, s32[1024]{0:T(1024)}, u32[]{:S(2)}) copy-start(s32[1024]{0:T(1024)} %param.4) | copy-start | bytes 12292
  15.1 8.9 %collective-permute-start = (bf16[16,2,2,256]{3,2,1,0:T(2,128)(2,1)S(1)}, bf16[16,2,2,256]{3,2,1,0:T(2,128)(2,1)S(1)}, u32[]{:S(2)}, u32[]{:S(2)}) collective-permute-start(bf16[16,2,2,256]{3,2,1,0:T(2,128)(2,1)S(1)} %get-tuple-element.22), channel_id=1, source_target_pairs={{0,1},{1,2},{2,3},{3,0},{4,5},{5,6},{6,7},{7,4},{8,9},{9,10},{10,1... | collective-permute-start | bytes 98312 | tf_op jit(solution)/shard_map/ppermute | solution.py:133
  15.6 8.4 %collective-permute-start.1 = (bf16[16,2,2,256]{3,2,1,0:T(2,128)(2,1)S(1)}, bf16[16,2,2,256]{3,2,1,0:T(2,128)(2,1)S(1)}, u32[]{:S(2)}, u32[]{:S(2)}) collective-permute-start(bf16[16,2,2,256]{3,2,1,0:T(2,128)(2,1)S(1)} %get-tuple-element.21), channel_id=1, source_target_pairs={{0,2},{1,3},{2,0},{3,1},{4,6},{5,7},{6,4},{7,5},{8,10},{9,11},{10,... | collective-permute-start | bytes 98312 | tf_op jit(solution)/shard_map/ppermute | solution.py:133
  18.1 5.8 %collective-permute-start.2 = (bf16[16,2,2,256]{3,2,1,0:T(2,128)(2,1)S(1)}, bf16[16,2,2,256]{3,2,1,0:T(2,128)(2,1)S(1)}, u32[]{:S(2)}, u32[]{:S(2)}) collective-permute-start(bf16[16,2,2,256]{3,2,1,0:T(2,128)(2,1)S(1)} %get-tuple-element.20), channel_id=1, source_target_pairs={{0,3},{1,0},{2,1},{3,2},{4,7},{5,4},{6,5},{7,6},{8,11},{9,8},{10,9... | collective-permute-start | bytes 98312 | tf_op jit(solution)/shard_map/ppermute | solution.py:133
  22.3 1.5 %copy-start.2 = (s32[128]{0:T(128)S(1)}, s32[128]{0:T(128)}, u32[]{:S(2)}) copy-start(s32[128]{0:T(128)} %param.5) | copy-start | bytes 1540
  24.2 6.9 %collective-permute-start.3 = (bf16[16,16,256]{2,1,0:T(8,128)(2,1)S(1)}, bf16[16,16,256]{2,1,0:T(8,128)(2,1)S(1)}, u32[]{:S(2)}, u32[]{:S(2)}) collective-permute-start(bf16[16,16,256]{2,1,0:T(8,128)(2,1)S(1)} %bitcast.72), channel_id=1, source_target_pairs={{4,0},{8,4},{12,8},{16,12},{20,16},{24,20},{28,24},{5,1},{9,5},{13... | collective-permute-start | bytes 393224 | tf_op jit(solution)/shard_map/ppermute | solution.py:143
  25.5 9.5 %collective-permute-start.4 = (bf16[16,16,256]{2,1,0:T(8,128)(2,1)S(1)}, bf16[16,16,256]{2,1,0:T(8,128)(2,1)S(1)}, u32[]{:S(2)}, u32[]{:S(2)}) collective-permute-start(bf16[16,16,256]{2,1,0:T(8,128)(2,1)S(1)} %bitcast.73), channel_id=1, source_target_pairs={{8,0},{12,4},{16,8},{20,12},{24,16},{28,20},{9,1},{13,5},{17,9},{2... | collective-permute-start | bytes 393224 | tf_op jit(solution)/shard_map/ppermute | solution.py:143
  26.8 10.5 %collective-permute-start.5 = (bf16[16,16,256]{2,1,0:T(8,128)(2,1)S(1)}, bf16[16,16,256]{2,1,0:T(8,128)(2,1)S(1)}, u32[]{:S(2)}, u32[]{:S(2)}) collective-permute-start(bf16[16,16,256]{2,1,0:T(8,128)(2,1)S(1)} %bitcast.74), channel_id=1, source_target_pairs={{12,0},{16,4},{20,8},{24,12},{28,16},{13,1},{17,5},{21,9},{25,13},... | collective-permute-start | bytes 393224 | tf_op jit(solution)/shard_map/ppermute | solution.py:143
  28.1 24.6 %collective-permute-start.6 = (bf16[16,16,256]{2,1,0:T(8,128)(2,1)S(1)}, bf16[16,16,256]{2,1,0:T(8,128)(2,1)S(1)}, u32[]{:S(2)}, u32[]{:S(2)}) collective-permute-start(bf16[16,16,256]{2,1,0:T(8,128)(2,1)S(1)} %bitcast.75), channel_id=1, source_target_pairs={{16,0},{20,4},{24,8},{28,12},{17,1},{21,5},{25,9},{29,13},{18,2},{... | collective-permute-start | bytes 393224 | tf_op jit(solution)/shard_map/ppermute | solution.py:143
  29.4 25.7 %collective-permute-start.7 = (bf16[16,16,256]{2,1,0:T(8,128)(2,1)S(1)}, bf16[16,16,256]{2,1,0:T(8,128)(2,1)S(1)}, u32[]{:S(2)}, u32[]{:S(2)}) collective-permute-start(bf16[16,16,256]{2,1,0:T(8,128)(2,1)S(1)} %bitcast.76), channel_id=1, source_target_pairs={{20,0},{24,4},{28,8},{21,1},{25,5},{29,9},{22,2},{26,6},{30,10},{2... | collective-permute-start | bytes 393224 | tf_op jit(solution)/shard_map/ppermute | solution.py:143
  31.1 24.1 %collective-permute-start.8 = (bf16[16,16,256]{2,1,0:T(8,128)(2,1)S(1)}, bf16[16,16,256]{2,1,0:T(8,128)(2,1)S(1)}, u32[]{:S(2)}, u32[]{:S(2)}) collective-permute-start(bf16[16,16,256]{2,1,0:T(8,128)(2,1)S(1)} %bitcast.77), channel_id=1, source_target_pairs={{24,0},{28,4},{25,1},{29,5},{26,2},{30,6},{27,3},{31,7}} | collective-permute-start | bytes 393224 | tf_op jit(solution)/shard_map/ppermute | solution.py:143
  35.0 20.2 %collective-permute-start.9 = (bf16[16,16,256]{2,1,0:T(8,128)(2,1)S(1)}, bf16[16,16,256]{2,1,0:T(8,128)(2,1)S(1)}, u32[]{:S(2)}, u32[]{:S(2)}) collective-permute-start(bf16[16,16,256]{2,1,0:T(8,128)(2,1)S(1)} %bitcast.78), channel_id=1, source_target_pairs={{28,0},{29,1},{30,2},{31,3}} | collective-permute-start | bytes 393224 | tf_op jit(solution)/shard_map/ppermute | solution.py:143
  59.5 15.0 %collective-permute-start.11 = (bf16[32,2,16,256]{3,2,1,0:T(8,128)(2,1)S(1)}, bf16[32,2,16,256]{3,2,1,0:T(8,128)(2,1)S(1)}, u32[]{:S(2)}, u32[]{:S(2)}) collective-permute-start(bf16[32,2,16,256]{3,2,1,0:T(8,128)(2,1)S(1)} %convert_element_type.82), channel_id=1, source_target_pairs={{0,2},{1,3},{2,0},{3,1},{4,6},{5,7},{6,4},{7,5},{8,10},{9,11},{10,... | collective-permute-start | bytes 1572872 | tf_op jit(solution)/shard_map/ppermute | solution.py:163
  64.9 14.3 %collective-permute-start.12 = (bf16[32,2,16,256]{3,2,1,0:T(8,128)(2,1)}, bf16[32,2,16,256]{3,2,1,0:T(8,128)(2,1)}, u32[]{:S(2)}, u32[]{:S(2)}) collective-permute-start(bf16[32,2,16,256]{3,2,1,0:T(8,128)(2,1)} %convert_element_type.83), channel_id=1, source_target_pairs={{0,3},{1,0},{2,1},{3,2},{4,7},{5,4},{6,5},{7,6},{8,11},{9,8},{10,9... | collective-permute-start | bytes 1572872 | tf_op jit(solution)/shard_map/ppermute | solution.py:163
  69.6 13.5 %collective-permute-start.10 = (bf16[32,2,16,256]{3,2,1,0:T(8,128)(2,1)}, bf16[32,2,16,256]{3,2,1,0:T(8,128)(2,1)}, u32[]{:S(2)}, u32[]{:S(2)}) collective-permute-start(bf16[32,2,16,256]{3,2,1,0:T(8,128)(2,1)} %convert_element_type.81), channel_id=1, source_target_pairs={{0,1},{1,2},{2,3},{3,0},{4,5},{5,6},{6,7},{7,4},{8,9},{9,10},{10,1... | collective-permute-start | bytes 1572872 | tf_op jit(solution)/shard_map/ppermute | solution.py:163
  70.1 3.9 %copy-start = (bf16[2,1024,512]{2,1,0:T(8,128)(2,1)S(1)}, bf16[2,1024,512]{2,1,0:T(8,128)(2,1)}, u32[]{:S(2)}) copy-start(bf16[2,1024,512]{2,1,0:T(8,128)(2,1)} %pad_maximum_fusion) | copy-start | bytes 6291460

commit v21 on v19

--- a/solution.py
+++ b/solution.py
@@ -55,7 +55,7 @@
 def cross_spectra(white_all, pair_offsets, base, own_count):
     rows, bins = white_all.shape[1], white_all.shape[2]
     band_span = pair_offsets.shape[0]
-    group = math.gcd(band_span, 8)
+    group = math.gcd(band_span, 32)
     kernel = functools.partial(cross_kernel, group=group, own_count=own_count, half=rows // 2)
     return pl.pallas_call(
         kernel,

time: 85.1 us -> 85 us (level)
  transfers between devices with their start and end apart: 13 -> 13, of which waited for: 7 -> 7; matrix products, arithmetic and copies ran while one was open for 13% -> 13% of each run, Pallas kernels for 14% -> 13%
where the time goes in v21:
time: 85 us; the launch traced here: 84.5 us
  waiting for transfers between devices  24.4 us (29%)
  starting transfers between devices  15.7 us (18%)
  Pallas kernels  15.1 us (18%)
  other arithmetic  13.8 us (16%)
  local copies, waits for them, and re-layouts  7.97 us (9%)
  matrix products  7.12 us (8%)
    ppermute x7, waiting for transfers between devices, local(): blocks.append(lax.ppermute(rows_white, 'gx', perm=pairs))  22.4 us
    pallas_call x4, Pallas kernels, cross_spectra(): pl.pallas_call(kernel, grid_spec=pltpu.PrefetchScalarGridSpec(num_scalar_...  15.1 us
    ppermute x7, starting transfers between devices, local(): blocks.append(lax.ppermute(rows_white, 'gx', perm=pairs))  9.2 us
    another operation x2, other arithmetic  5.69 us
    dot_general x4, matrix products, local(): jnp.einsum('opck,pkl->ocl', part, rows, preferred_element_type=jnp.float32)  4.66 us
    ppermute x3, starting transfers between devices, local(): lax.ppermute(piece, 'gy', perm=[(src, (src + shift) % gy_count) for src i...  4.46 us
    dot_general x1, matrix products, forward_spectra(): jnp.dot(record_rows.reshape(row_count * block_count, block_len), small_ta...  2.46 us
    neg x1, local copies, waits for them, and re-layouts, inverse_table(): return jnp.stack([cos_t, -sin_t], axis=0).astype(jnp.bfloat16)  2.31 us
  transfers between devices with their start and end apart: 13, of which 7 were waited for; matrix products, arithmetic and copies ran while one was open for 13% of the time, Pallas kernels for 13%

profile of v21, /device:TPU:0, one launch (start us, length us, event | category | flops | bytes accessed | tf_op | source)
XLA Modules:
  0.0 84.5 jit_solution(10050077940875925562)
XLA Ops:
  0.0 1.2 %fusion.52 = (f32[32,1024]{1,0:T(8,128)S(1)}, f32[32,1024]{1,0:T(8,128)S(1)}) fusion(s32[1024]{0:T(1024)} %param.4), kind=kLoop, calls=%fused_computation.87 | loop fusion | flops 458752 | bytes 266240 | tf_op jit(solution)/shard_map/cos | solution.py:90
  1.2 0.7 add_select_fusion.5
  1.9 1.8 %fusion.41 = (f32[64,1024]{1,0:T(8,128)S(1)}, f32[64,1024]{1,0:T(8,128)S(1)}) fusion(s32[1024]{0:T(1024)} %param.4, s32[64]{0:T(128)S(1)} %iota_multiply_fusion), kind=kLoop, calls=%fused_computation.70 | loop fusion | flops 917504 | bytes 528640 | tf_op jit(solution)/shard_map/cos | solution.py:90
  3.7 1.2 %reshape_reshape.3 = bf16[128,2048]{1,0:T(8,128)(2,1)S(1)} reshape(bf16[16,2,8192]{2,1,0:T(2,128)(2,1)} %param.3) | data formatting | bytes 1048576 | tf_op jit(solution)/shard_map/reshape;reshape | solution.py:103
  4.9 3.7 %subtract_convert_fusion = (bf16[64,32,1024]{2,1,0:T(8,128)(2,1)S(1)}, bf16[64,32,1024]{2,1,0:T(8,128)(2,1)S(1)}) fusion(f32[64,1024]{1,0:T(8,128)S(1)} %get-tuple-element.20, f32[32,1024]{1,0:T(8,128)S(1)} %get-tuple-element.26, f32[64,1024]{1,0:T(8,128)S(1)} %get-tuple-element.19, f32[32,1024]{1,0:T(8,128)S(1)} %get-tuple-element.25), kind=kLoop, calls=%fused_computation.5 | loop fusion | flops 18874368 | bytes 9175040 | tf_op jit(solution)/shard_map/convert.7
  8.5 2.5 %fusion.4 = f32[128,2048]{0,1:T(8,128)S(1)} fusion(bf16[128,2048]{1,0:T(8,128)(2,1)S(1)} %reshape_reshape.3, bf16[2048,1024]{1,0:T(8,128)(2,1)S(1)} %bitcast.69, bf16[2048,1024]{1,0:T(8,128)(2,1)S(1)} %bitcast.68), kind=kOutput, calls=%fused_computation.14 | convolution fusion | flops 1090519040 | bytes 9961472 | tf_op jit(solution)/shard_map/dot_general | solution.py:102
  11.0 0.3 copy.4
  11.3 0.9 %reshape.439 = f32[32,4,2,1024]{3,2,1,0:T(2,128)S(1)} reshape(f32[128,2048]{1,0:T(8,128)S(1)} %copy.4) | data formatting | bytes 2097152 | tf_op jit(solution)/shard_map/reshape | solution.py:106
  12.2 1.2 %fusion.68 = (f32[32,4,1,1024]{3,2,1,0:T(1,128)S(1)}, f32[32,4,1,1024]{3,2,1,0:T(1,128)S(1)}) fusion(f32[32,4,2,1024]{3,2,1,0:T(2,128)S(1)} %reshape.439), kind=kLoop, calls=%fused_computation.126 | loop fusion | bytes 2097152 | tf_op jit(solution)/shard_map/slice | solution.py:113
  13.6 0.8 fusion.25
  14.5 0.2 concatenate.18
  14.8 0.2 multiply_convert_fusion
  15.1 0.5 collective-permute-start
  15.6 2.6 %collective-permute-start.1 = (bf16[16,2,2,256]{3,2,1,0:T(2,128)(2,1)S(1)}, bf16[16,2,2,256]{3,2,1,0:T(2,128)(2,1)S(1)}, u32[]{:S(2)}, u32[]{:S(2)}) collective-permute-start(bf16[16,2,2,256]{3,2,1,0:T(2,128)(2,1)S(1)} %get-tuple-element.17), channel_id=1, source_target_pairs={{0,2},{1,3},{2,0},{3,1},{4,6},{5,7},{6,4},{7,5},{8,10},{9,11},{10,... | collective-permute-start | bytes 98312 | tf_op jit(solution)/shard_map/ppermute | solution.py:133
  18.2 1.4 %collective-permute-start.2 = (bf16[16,2,2,256]{3,2,1,0:T(2,128)(2,1)S(1)}, bf16[16,2,2,256]{3,2,1,0:T(2,128)(2,1)S(1)}, u32[]{:S(2)}, u32[]{:S(2)}) collective-permute-start(bf16[16,2,2,256]{3,2,1,0:T(2,128)(2,1)S(1)} %get-tuple-element.16), channel_id=1, source_target_pairs={{0,3},{1,0},{2,1},{3,2},{4,7},{5,4},{6,5},{7,6},{8,11},{9,8},{10,9... | collective-permute-start | bytes 98312 | tf_op jit(solution)/shard_map/ppermute | solution.py:133
  19.5 0.5 fusion.50
  20.2 0.9 %collective-permute-done.2 = bf16[16,2,2,256]{3,2,1,0:T(2,128)(2,1)S(1)} collective-permute-done((bf16[16,2,2,256]{3,2,1,0:T(2,128)(2,1)S(1)}, bf16[16,2,2,256]{3,2,1,0:T(2,128)(2,1)S(1)}, u32[]{:S(2)}, u32[]{:S(2)}) %collective-permute-start.2) | collective-permute-done | bytes 32800 | tf_op jit(solution)/shard_map/ppermute | solution.py:133
  21.1 0.2 maximum_bitcast_fusion
  21.4 1.3 %collective-permute-start.3 = (bf16[16,16,256]{2,1,0:T(8,128)(2,1)S(1)}, bf16[16,16,256]{2,1,0:T(8,128)(2,1)S(1)}, u32[]{:S(2)}, u32[]{:S(2)}) collective-permute-start(bf16[16,16,256]{2,1,0:T(8,128)(2,1)S(1)} %bitcast.72), channel_id=1, source_target_pairs={{4,0},{8,4},{12,8},{16,12},{20,16},{24,20},{28,24},{5,1},{9,5},{13... | collective-permute-start | bytes 393224 | tf_op jit(solution)/shard_map/ppermute | solution.py:143
  22.7 1.3 %collective-permute-start.4 = (bf16[16,16,256]{2,1,0:T(8,128)(2,1)S(1)}, bf16[16,16,256]{2,1,0:T(8,128)(2,1)S(1)}, u32[]{:S(2)}, u32[]{:S(2)}) collective-permute-start(bf16[16,16,256]{2,1,0:T(8,128)(2,1)S(1)} %bitcast.73), channel_id=1, source_target_pairs={{8,0},{12,4},{16,8},{20,12},{24,16},{28,20},{9,1},{13,5},{17,9},{2... | collective-permute-start | bytes 393224 | tf_op jit(solution)/shard_map/ppermute | solution.py:143
  24.0 1.3 %collective-permute-start.5 = (bf16[16,16,256]{2,1,0:T(8,128)(2,1)S(1)}, bf16[16,16,256]{2,1,0:T(8,128)(2,1)S(1)}, u32[]{:S(2)}, u32[]{:S(2)}) collective-permute-start(bf16[16,16,256]{2,1,0:T(8,128)(2,1)S(1)} %bitcast.74), channel_id=1, source_target_pairs={{12,0},{16,4},{20,8},{24,12},{28,16},{13,1},{17,5},{21,9},{25,13},... | collective-permute-start | bytes 393224 | tf_op jit(solution)/shard_map/ppermute | solution.py:143
  25.3 1.3 %collective-permute-start.6 = (bf16[16,16,256]{2,1,0:T(8,128)(2,1)S(1)}, bf16[16,16,256]{2,1,0:T(8,128)(2,1)S(1)}, u32[]{:S(2)}, u32[]{:S(2)}) collective-permute-start(bf16[16,16,256]{2,1,0:T(8,128)(2,1)S(1)} %bitcast.75), channel_id=1, source_target_pairs={{16,0},{20,4},{24,8},{28,12},{17,1},{21,5},{25,9},{29,13},{18,2},{... | collective-permute-start | bytes 393224 | tf_op jit(solution)/shard_map/ppermute | solution.py:143
  26.6 1.3 %collective-permute-start.7 = (bf16[16,16,256]{2,1,0:T(8,128)(2,1)S(1)}, bf16[16,16,256]{2,1,0:T(8,128)(2,1)S(1)}, u32[]{:S(2)}, u32[]{:S(2)}) collective-permute-start(bf16[16,16,256]{2,1,0:T(8,128)(2,1)S(1)} %bitcast.76), channel_id=1, source_target_pairs={{20,0},{24,4},{28,8},{21,1},{25,5},{29,9},{22,2},{26,6},{30,10},{2... | collective-permute-start | bytes 393224 | tf_op jit(solution)/shard_map/ppermute | solution.py:143
  27.9 1.2 %collective-permute-done.3 = bf16[16,16,256]{2,1,0:T(8,128)(2,1)S(1)} collective-permute-done((bf16[16,16,256]{2,1,0:T(8,128)(2,1)S(1)}, bf16[16,16,256]{2,1,0:T(8,128)(2,1)S(1)}, u32[]{:S(2)}, u32[]{:S(2)}) %collective-permute-start.3) | collective-permute-done | bytes 131104 | tf_op jit(solution)/shard_map/ppermute | solution.py:143
  29.1 1.3 %collective-permute-start.8 = (bf16[16,16,256]{2,1,0:T(8,128)(2,1)S(1)}, bf16[16,16,256]{2,1,0:T(8,128)(2,1)S(1)}, u32[]{:S(2)}, u32[]{:S(2)}) collective-permute-start(bf16[16,16,256]{2,1,0:T(8,128)(2,1)S(1)} %bitcast.77), channel_id=1, source_target_pairs={{24,0},{28,4},{25,1},{29,5},{26,2},{30,6},{27,3},{31,7}} | collective-permute-start | bytes 393224 | tf_op jit(solution)/shard_map/ppermute | solution.py:143
  30.4 2.7 %collective-permute-done.4 = bf16[16,16,256]{2,1,0:T(8,128)(2,1)S(1)} collective-permute-done((bf16[16,16,256]{2,1,0:T(8,128)(2,1)S(1)}, bf16[16,16,256]{2,1,0:T(8,128)(2,1)S(1)}, u32[]{:S(2)}, u32[]{:S(2)}) %collective-permute-start.4) | collective-permute-done | bytes 131104 | tf_op jit(solution)/shard_map/ppermute | solution.py:143
  33.1 1.5 %collective-permute-start.9 = (bf16[16,16,256]{2,1,0:T(8,128)(2,1)S(1)}, bf16[16,16,256]{2,1,0:T(8,128)(2,1)S(1)}, u32[]{:S(2)}, u32[]{:S(2)}) collective-permute-start(bf16[16,16,256]{2,1,0:T(8,128)(2,1)S(1)} %bitcast.78), channel_id=1, source_target_pairs={{28,0},{29,1},{30,2},{31,3}} | collective-permute-start | bytes 393224 | tf_op jit(solution)/shard_map/ppermute | solution.py:143
  34.6 0.5 collective-permute-done.5
  35.1 15.9 %collective-permute-done.6 = bf16[16,16,256]{2,1,0:T(8,128)(2,1)S(1)} collective-permute-done((bf16[16,16,256]{2,1,0:T(8,128)(2,1)S(1)}, bf16[16,16,256]{2,1,0:T(8,128)(2,1)S(1)}, u32[]{:S(2)}, u32[]{:S(2)}) %collective-permute-start.6) | collective-permute-done | bytes 131104 | tf_op jit(solution)/shard_map/ppermute | solution.py:143
  50.9 2.1 %collective-permute-done.7 = bf16[16,16,256]{2,1,0:T(8,128)(2,1)S(1)} collective-permute-done((bf16[16,16,256]{2,1,0:T(8,128)(2,1)S(1)}, bf16[16,16,256]{2,1,0:T(8,128)(2,1)S(1)}, u32[]{:S(2)}, u32[]{:S(2)}) %collective-permute-start.7) | collective-permute-done | bytes 131104 | tf_op jit(solution)/shard_map/ppermute | solution.py:143
  53.2 0.3 convert_element_type.78.white_ref
  53.5 3.8 %shard_map.38 = f32[32,2,16,256]{3,2,1,0:T(8,128)S(1)} custom-call(s32[32]{0:T(128)S(1)} %get-tuple-element.30.offsets_ref, s32[1]{0:T(128)} %constant.111.clone.1.base_ref, f32[144,16,256]{2,1,0:T(8,128)S(1)} %convert_element_type.78.white_ref), custom_call_target="tpu_custom_call" | custom-call | flops 16777216 | bytes 3407872 | tf_op jit(solution)/shard_map/pallas_call | solution.py:60
  57.3 0.9 %convert_element_type.82 = bf16[32,2,16,256]{3,2,1,0:T(8,128)(2,1)} convert(f32[32,2,16,256]{3,2,1,0:T(8,128)S(1)} %shard_map.38) | non-fusion elementwise | flops 262144 | bytes 1572864 | tf_op jit(solution)/shard_map/convert_element_type | solution.py:160
  58.2 1.5 %collective-permute-start.11 = (bf16[32,2,16,256]{3,2,1,0:T(8,128)(2,1)}, bf16[32,2,16,256]{3,2,1,0:T(8,128)(2,1)}, u32[]{:S(2)}, u32[]{:S(2)}) collective-permute-start(bf16[32,2,16,256]{3,2,1,0:T(8,128)(2,1)} %convert_element_type.82), channel_id=1, source_target_pairs={{0,2},{1,3},{2,0},{3,1},{4,6},{5,7},{6,4},{7,5},{8,10},{9,11},{10,... | collective-permute-start | bytes 1572872 | tf_op jit(solution)/shard_map/ppermute | solution.py:163
  59.6 0.3 fusion.54
  60.0 3.8 %shard_map.39 = f32[32,2,16,256]{3,2,1,0:T(8,128)S(1)} custom-call(s32[32]{0:T(128)S(1)} %get-tuple-element.32.offsets_ref, s32[1]{0:T(128)} %constant.111.clone.1.base_ref, f32[144,16,256]{2,1,0:T(8,128)S(1)} %convert_element_type.78.white_ref), custom_call_target="tpu_custom_call" | custom-call | flops 16777216 | bytes 3407872 | tf_op jit(solution)/shard_map/pallas_call | solution.py:60
  63.8 0.9 %convert_element_type.83 = bf16[32,2,16,256]{3,2,1,0:T(8,128)(2,1)} convert(f32[32,2,16,256]{3,2,1,0:T(8,128)S(1)} %shard_map.39) | non-fusion elementwise | flops 262144 | bytes 1572864 | tf_op jit(solution)/shard_map/convert_element_type | solution.py:160
  64.6 2.0 %negate_convert_fusion.1 = (bf16[1024,16,32]{0,2,1:T(8,128)(2,1)}, bf16[1024,16,32]{0,2,1:T(8,128)(2,1)}) fusion(f32[1024,16]{0,1:T(8,128)S(1)} %get-tuple-element.22, f32[1024,32]{0,1:T(8,128)S(1)} %get-tuple-element.28, f32[1024,16]{0,1:T(8,128)S(1)} %get-tuple-element.21, f32[1024,32]{0,1:T(8,128)S(1)} %get-tuple-element.27), kind=kLoop, calls=%fused_computation.15 | loop fusion | flops 4718592 | bytes 2490368 | tf_op jit(solution)/shard_map/convert.2
  66.7 1.5 %copy.7 = bf16[1,1024,512]{2,1,0:T(8,128)(2,1)S(1)} copy(bf16[1,1024,512]{1,2,0:T(8,128)(2,1)} %bitcast.71) | data formatting | bytes 2097152 | tf_op jit(solution)/shard_map/sub | solution.py:27
  68.2 2.3 %copy.8 = bf16[1,1024,512]{2,1,0:T(8,128)(2,1)} copy(bf16[1,1024,512]{1,2,0:T(8,128)(2,1)} %bitcast.70) | data formatting | bytes 2097152 | tf_op jit(solution)/shard_map/neg | solution.py:29
  70.5 3.8 %shard_map.37 = f32[32,2,16,256]{3,2,1,0:T(8,128)S(1)} custom-call(s32[32]{0:T(128)S(1)} %get-tuple-element.29.offsets_ref, s32[1]{0:T(128)} %constant.111.clone.1.base_ref, f32[144,16,256]{2,1,0:T(8,128)S(1)} %convert_element_type.78.white_ref), custom_call_target="tpu_custom_call" | custom-call | flops 16777216 | bytes 3407872 | tf_op jit(solution)/shard_map/pallas_call | solution.py:60
  74.4 0.6 collective-permute-start.10
  74.9 3.8 %shard_map.40 = f32[32,2,16,256]{3,2,1,0:T(8,128)S(1)} custom-call(s32[32]{0:T(128)S(1)} %get-tuple-element.31.offsets_ref, s32[1]{0:T(128)} %constant.111.clone.1.base_ref, f32[144,16,256]{2,1,0:T(8,128)S(1)} %convert_element_type.78.white_ref), custom_call_target="tpu_custom_call" | custom-call | flops 16777216 | bytes 3407872 | tf_op jit(solution)/shard_map/pallas_call | solution.py:60
  78.7 0.4 convolution_bitcast_fusion
  79.2 1.5 %convolution_bitcast_fusion.2 = f32[32,16,512]{2,1,0:T(8,128)S(1)} fusion(bf16[32,2,16,256]{3,2,1,0:T(8,128)(2,1)} %collective-permute-done.11, s32[]{:T(128)S(6)} %select_n.109, bf16[1,1024,512]{2,1,0:T(8,128)(2,1)S(1)} %copy.7, bf16[1,1024,512]{2,1,0:T(8,128)(2,1)S(1)} %copy-done), kind=kOutput, calls=%fused_computation.19 | convolution fusion | flops 269484032 | bytes 3670020 | tf_op jit(solution)/shard_map/opck,pkl->ocl/dot_general | solution.py:166
  80.6 1.5 %convolution_bitcast_fusion.1 = f32[32,16,512]{2,1,0:T(8,128)S(1)} fusion(bf16[32,2,16,256]{3,2,1,0:T(8,128)(2,1)} %collective-permute-done.12, s32[]{:T(128)S(6)} %select_n.108, bf16[1,1024,512]{2,1,0:T(8,128)(2,1)S(1)} %copy.7, bf16[1,1024,512]{2,1,0:T(8,128)(2,1)S(1)} %copy-done), kind=kOutput, calls=%fused_computation.18 | convolution fusion | flops 269484032 | bytes 3670020 | tf_op jit(solution)/shard_map/opck,pkl->ocl/dot_general | solution.py:166
  82.1 1.1 %collective-permute-done.10 = bf16[32,2,16,256]{3,2,1,0:T(8,128)(2,1)S(1)} collective-permute-done((bf16[32,2,16,256]{3,2,1,0:T(8,128)(2,1)S(1)}, bf16[32,2,16,256]{3,2,1,0:T(8,128)(2,1)S(1)}, u32[]{:S(2)}, u32[]{:S(2)}) %collective-permute-start.10) | collective-permute-done | bytes 524320 | tf_op jit(solution)/shard_map/ppermute | solution.py:163
  83.2 1.3 %fusion.11 = bf16[32,16,512]{2,1,0:T(8,128)(2,1)} fusion(f32[32,16,512]{2,1,0:T(8,128)S(1)} %convolution_bitcast_fusion, f32[32,16,512]{2,1,0:T(8,128)S(1)} %convolution_bitcast_fusion.1, f32[32,16,512]{2,1,0:T(8,128)S(1)} %convolution_bitcast_fusion.2, bf16[32,2,16,256]{3,2,1,0:T(8,128)(2,1)S(1)} %collective-permute-done.10, s32[]{:T(128)S(6)} %select_n.110, ...), kind=kOutput, calls=%fused_computation.25 | convolution fusion | flops 270794752 | bytes 6291460 | tf_op jit(solution)/shard_map/opck,pkl->ocl/dot_general | solution.py:166
  (32 shorter events, 0.8 us)
Async XLA Ops:
  13.4 6.1 %copy-start.1 = (s32[1024]{0:T(1024)S(1)}, s32[1024]{0:T(1024)}, u32[]{:S(2)}) copy-start(s32[1024]{0:T(1024)} %param.4) | copy-start | bytes 12292
  13.4 6.7 %copy-start.2 = (s32[128]{0:T(128)S(1)}, s32[128]{0:T(128)}, u32[]{:S(2)}) copy-start(s32[128]{0:T(128)} %param.5) | copy-start | bytes 1540
  15.1 5.1 %collective-permute-start = (bf16[16,2,2,256]{3,2,1,0:T(2,128)(2,1)S(1)}, bf16[16,2,2,256]{3,2,1,0:T(2,128)(2,1)S(1)}, u32[]{:S(2)}, u32[]{:S(2)}) collective-permute-start(bf16[16,2,2,256]{3,2,1,0:T(2,128)(2,1)S(1)} %get-tuple-element.18), channel_id=1, source_target_pairs={{0,1},{1,2},{2,3},{3,0},{4,5},{5,6},{6,7},{7,4},{8,9},{9,10},{10,1... | collective-permute-start | bytes 98312 | tf_op jit(solution)/shard_map/ppermute | solution.py:133
  15.6 4.6 %collective-permute-start.1 = (bf16[16,2,2,256]{3,2,1,0:T(2,128)(2,1)S(1)}, bf16[16,2,2,256]{3,2,1,0:T(2,128)(2,1)S(1)}, u32[]{:S(2)}, u32[]{:S(2)}) collective-permute-start(bf16[16,2,2,256]{3,2,1,0:T(2,128)(2,1)S(1)} %get-tuple-element.17), channel_id=1, source_target_pairs={{0,2},{1,3},{2,0},{3,1},{4,6},{5,7},{6,4},{7,5},{8,10},{9,11},{10,... | collective-permute-start | bytes 98312 | tf_op jit(solution)/shard_map/ppermute | solution.py:133
  18.2 3.0 %collective-permute-start.2 = (bf16[16,2,2,256]{3,2,1,0:T(2,128)(2,1)S(1)}, bf16[16,2,2,256]{3,2,1,0:T(2,128)(2,1)S(1)}, u32[]{:S(2)}, u32[]{:S(2)}) collective-permute-start(bf16[16,2,2,256]{3,2,1,0:T(2,128)(2,1)S(1)} %get-tuple-element.16), channel_id=1, source_target_pairs={{0,3},{1,0},{2,1},{3,2},{4,7},{5,4},{6,5},{7,6},{8,11},{9,8},{10,9... | collective-permute-start | bytes 98312 | tf_op jit(solution)/shard_map/ppermute | solution.py:133
  21.4 7.7 %collective-permute-start.3 = (bf16[16,16,256]{2,1,0:T(8,128)(2,1)S(1)}, bf16[16,16,256]{2,1,0:T(8,128)(2,1)S(1)}, u32[]{:S(2)}, u32[]{:S(2)}) collective-permute-start(bf16[16,16,256]{2,1,0:T(8,128)(2,1)S(1)} %bitcast.72), channel_id=1, source_target_pairs={{4,0},{8,4},{12,8},{16,12},{20,16},{24,20},{28,24},{5,1},{9,5},{13... | collective-permute-start | bytes 393224 | tf_op jit(solution)/shard_map/ppermute | solution.py:143
  22.7 10.4 %collective-permute-start.4 = (bf16[16,16,256]{2,1,0:T(8,128)(2,1)S(1)}, bf16[16,16,256]{2,1,0:T(8,128)(2,1)S(1)}, u32[]{:S(2)}, u32[]{:S(2)}) collective-permute-start(bf16[16,16,256]{2,1,0:T(8,128)(2,1)S(1)} %bitcast.73), channel_id=1, source_target_pairs={{8,0},{12,4},{16,8},{20,12},{24,16},{28,20},{9,1},{13,5},{17,9},{2... | collective-permute-start | bytes 393224 | tf_op jit(solution)/shard_map/ppermute | solution.py:143
  24.0 11.1 %collective-permute-start.5 = (bf16[16,16,256]{2,1,0:T(8,128)(2,1)S(1)}, bf16[16,16,256]{2,1,0:T(8,128)(2,1)S(1)}, u32[]{:S(2)}, u32[]{:S(2)}) collective-permute-start(bf16[16,16,256]{2,1,0:T(8,128)(2,1)S(1)} %bitcast.74), channel_id=1, source_target_pairs={{12,0},{16,4},{20,8},{24,12},{28,16},{13,1},{17,5},{21,9},{25,13},... | collective-permute-start | bytes 393224 | tf_op jit(solution)/shard_map/ppermute | solution.py:143
  25.3 25.6 %collective-permute-start.6 = (bf16[16,16,256]{2,1,0:T(8,128)(2,1)S(1)}, bf16[16,16,256]{2,1,0:T(8,128)(2,1)S(1)}, u32[]{:S(2)}, u32[]{:S(2)}) collective-permute-start(bf16[16,16,256]{2,1,0:T(8,128)(2,1)S(1)} %bitcast.75), channel_id=1, source_target_pairs={{16,0},{20,4},{24,8},{28,12},{17,1},{21,5},{25,9},{29,13},{18,2},{... | collective-permute-start | bytes 393224 | tf_op jit(solution)/shard_map/ppermute | solution.py:143
  26.6 26.5 %collective-permute-start.7 = (bf16[16,16,256]{2,1,0:T(8,128)(2,1)S(1)}, bf16[16,16,256]{2,1,0:T(8,128)(2,1)S(1)}, u32[]{:S(2)}, u32[]{:S(2)}) collective-permute-start(bf16[16,16,256]{2,1,0:T(8,128)(2,1)S(1)} %bitcast.76), channel_id=1, source_target_pairs={{20,0},{24,4},{28,8},{21,1},{25,5},{29,9},{22,2},{26,6},{30,10},{2... | collective-permute-start | bytes 393224 | tf_op jit(solution)/shard_map/ppermute | solution.py:143
  29.1 24.0 %collective-permute-start.8 = (bf16[16,16,256]{2,1,0:T(8,128)(2,1)S(1)}, bf16[16,16,256]{2,1,0:T(8,128)(2,1)S(1)}, u32[]{:S(2)}, u32[]{:S(2)}) collective-permute-start(bf16[16,16,256]{2,1,0:T(8,128)(2,1)S(1)} %bitcast.77), channel_id=1, source_target_pairs={{24,0},{28,4},{25,1},{29,5},{26,2},{30,6},{27,3},{31,7}} | collective-permute-start | bytes 393224 | tf_op jit(solution)/shard_map/ppermute | solution.py:143
  33.1 20.1 %collective-permute-start.9 = (bf16[16,16,256]{2,1,0:T(8,128)(2,1)S(1)}, bf16[16,16,256]{2,1,0:T(8,128)(2,1)S(1)}, u32[]{:S(2)}, u32[]{:S(2)}) collective-permute-start(bf16[16,16,256]{2,1,0:T(8,128)(2,1)S(1)} %bitcast.78), channel_id=1, source_target_pairs={{28,0},{29,1},{30,2},{31,3}} | collective-permute-start | bytes 393224 | tf_op jit(solution)/shard_map/ppermute | solution.py:143
  58.2 21.0 %collective-permute-start.11 = (bf16[32,2,16,256]{3,2,1,0:T(8,128)(2,1)}, bf16[32,2,16,256]{3,2,1,0:T(8,128)(2,1)}, u32[]{:S(2)}, u32[]{:S(2)}) collective-permute-start(bf16[32,2,16,256]{3,2,1,0:T(8,128)(2,1)} %convert_element_type.82), channel_id=1, source_target_pairs={{0,2},{1,3},{2,0},{3,1},{4,6},{5,7},{6,4},{7,5},{8,10},{9,11},{10,... | collective-permute-start | bytes 1572872 | tf_op jit(solution)/shard_map/ppermute | solution.py:163
  64.6 16.0 %collective-permute-start.12 = (bf16[32,2,16,256]{3,2,1,0:T(8,128)(2,1)}, bf16[32,2,16,256]{3,2,1,0:T(8,128)(2,1)}, u32[]{:S(2)}, u32[]{:S(2)}) collective-permute-start(bf16[32,2,16,256]{3,2,1,0:T(8,128)(2,1)} %convert_element_type.83), channel_id=1, source_target_pairs={{0,3},{1,0},{2,1},{3,2},{4,7},{5,4},{6,5},{7,6},{8,11},{9,8},{10,9... | collective-permute-start | bytes 1572872 | tf_op jit(solution)/shard_map/ppermute | solution.py:163
  74.3 4.3 %copy-start = (bf16[1,1024,512]{2,1,0:T(8,128)(2,1)S(1)}, bf16[1,1024,512]{2,1,0:T(8,128)(2,1)}, u32[]{:S(2)}) copy-start(bf16[1,1024,512]{2,1,0:T(8,128)(2,1)} %copy.8) | copy-start | bytes 3145732
  74.4 8.9 %collective-permute-start.10 = (bf16[32,2,16,256]{3,2,1,0:T(8,128)(2,1)S(1)}, bf16[32,2,16,256]{3,2,1,0:T(8,128)(2,1)S(1)}, u32[]{:S(2)}, u32[]{:S(2)}) collective-permute-start(bf16[32,2,16,256]{3,2,1,0:T(8,128)(2,1)S(1)} %convert_element_type.79), channel_id=1, source_target_pairs={{0,1},{1,2},{2,3},{3,0},{4,5},{5,6},{6,7},{7,4},{8,9},{9,10},{10,1... | collective-permute-start | bytes 1572872 | tf_op jit(solution)/shard_map/ppermute | solution.py:163

commit v22 on v19

--- a/solution.py
+++ b/solution.py
@@ -153,7 +153,8 @@
     inverse = inverse_table(kept_bins)
     norm_scale = 0.5 / math.sqrt(windows * bin_count)
     lagged = None
-    for shift in list(range(1, gy_count)) + [0]:
+    far_shift = gy_count // 2
+    for shift in [far_shift] + [s for s in range(1, gy_count) if s != far_shift] + [0]:
         dest = lax.rem(me + shift, gy_count)
         part = cross_spectra(
             padded, lax.dynamic_slice_in_dim(offsets, dest * off_dev, off_dev), base, ch_dev

time: 85.1 us -> 90.5 us (1.063)
  waiting for transfers between devices: 24.1 us -> 28.2 us
  starting transfers between devices: 15.7 us -> 17 us
    ppermute x3, waiting for transfers between devices: 0.78 us -> 4.88 us  [local(): part = lax.ppermute(part, 'gy', perm=pairs)]
    ppermute x3, starting transfers between devices: 2.05 us -> 3.3 us  [local(): part = lax.ppermute(part, 'gy', perm=pairs)]
  transfers between devices with their start and end apart: 13 -> 13, of which waited for: 7 -> 7; matrix products, arithmetic and copies ran while one was open for 13% -> 12% of each run, Pallas kernels for 14% -> 13%
where the time goes in v22:
time: 90.5 us; the launch traced here: 89.9 us
  waiting for transfers between devices  28.2 us (31%)
  starting transfers between devices  17 us (19%)
  Pallas kernels  15.5 us (17%)
  other arithmetic  13.8 us (15%)
  local copies, waits for them, and re-layouts  7.97 us (9%)
  matrix products  7.12 us (8%)
    ppermute x7, waiting for transfers between devices, local(): blocks.append(lax.ppermute(rows_white, 'gx', perm=pairs))  22.4 us
    pallas_call x4, Pallas kernels, cross_spectra(): pl.pallas_call(kernel, grid_spec=pltpu.PrefetchScalarGridSpec(num_scalar_...  15.5 us
    ppermute x7, starting transfers between devices, local(): blocks.append(lax.ppermute(rows_white, 'gx', perm=pairs))  9.2 us
    another operation x2, other arithmetic  5.69 us
    ppermute x3, waiting for transfers between devices, local(): part = lax.ppermute(part, 'gy', perm=pairs)  4.88 us
    dot_general x4, matrix products, local(): jnp.einsum('opck,pkl->ocl', part, rows, preferred_element_type=jnp.float32)  4.66 us
    ppermute x3, starting transfers between devices, local(): lax.ppermute(piece, 'gy', perm=[(src, (src + shift) % gy_count) for src i...  4.46 us
    ppermute x3, starting transfers between devices, local(): part = lax.ppermute(part, 'gy', perm=pairs)  3.3 us
  transfers between devices with their start and end apart: 13, of which 7 were waited for; matrix products, arithmetic and copies ran while one was open for 12% of the time, Pallas kernels for 13%

profile of v22, /device:TPU:0, one launch (start us, length us, event | category | flops | bytes accessed | tf_op | source)
XLA Modules:
  0.0 89.9 jit_solution(12499321463066625446)
XLA Ops:
  0.0 1.2 %fusion.52 = (f32[32,1024]{1,0:T(8,128)S(1)}, f32[32,1024]{1,0:T(8,128)S(1)}) fusion(s32[1024]{0:T(1024)} %param.4), kind=kLoop, calls=%fused_computation.87 | loop fusion | flops 458752 | bytes 266240 | tf_op jit(solution)/shard_map/cos | solution.py:90
  1.2 0.7 add_select_fusion.5
  1.9 1.8 %fusion.41 = (f32[64,1024]{1,0:T(8,128)S(1)}, f32[64,1024]{1,0:T(8,128)S(1)}) fusion(s32[1024]{0:T(1024)} %param.4, s32[64]{0:T(128)S(1)} %iota_multiply_fusion), kind=kLoop, calls=%fused_computation.70 | loop fusion | flops 917504 | bytes 528640 | tf_op jit(solution)/shard_map/cos | solution.py:90
  3.7 1.2 %reshape_reshape.3 = bf16[128,2048]{1,0:T(8,128)(2,1)S(1)} reshape(bf16[16,2,8192]{2,1,0:T(2,128)(2,1)} %param.3) | data formatting | bytes 1048576 | tf_op jit(solution)/shard_map/reshape;reshape | solution.py:103
  4.9 3.7 %subtract_convert_fusion = (bf16[64,32,1024]{2,1,0:T(8,128)(2,1)S(1)}, bf16[64,32,1024]{2,1,0:T(8,128)(2,1)S(1)}) fusion(f32[64,1024]{1,0:T(8,128)S(1)} %get-tuple-element.20, f32[32,1024]{1,0:T(8,128)S(1)} %get-tuple-element.26, f32[64,1024]{1,0:T(8,128)S(1)} %get-tuple-element.19, f32[32,1024]{1,0:T(8,128)S(1)} %get-tuple-element.25), kind=kLoop, calls=%fused_computation.5 | loop fusion | flops 18874368 | bytes 9175040 | tf_op jit(solution)/shard_map/convert.7
  8.5 2.5 %fusion.4 = f32[128,2048]{0,1:T(8,128)S(1)} fusion(bf16[128,2048]{1,0:T(8,128)(2,1)S(1)} %reshape_reshape.3, bf16[2048,1024]{1,0:T(8,128)(2,1)S(1)} %bitcast.69, bf16[2048,1024]{1,0:T(8,128)(2,1)S(1)} %bitcast.68), kind=kOutput, calls=%fused_computation.14 | convolution fusion | flops 1090519040 | bytes 9961472 | tf_op jit(solution)/shard_map/dot_general | solution.py:102
  11.0 0.3 copy.4
  11.3 0.9 reshape.439
  12.2 1.2 %fusion.68 = (f32[32,4,1,1024]{3,2,1,0:T(1,128)S(1)}, f32[32,4,1,1024]{3,2,1,0:T(1,128)S(1)}) fusion(f32[32,4,2,1024]{3,2,1,0:T(2,128)S(1)} %reshape.439), kind=kLoop, calls=%fused_computation.126 | loop fusion | bytes 2097152 | tf_op jit(solution)/shard_map/slice | solution.py:113
  13.6 0.8 fusion.25
  14.5 0.2 concatenate.18
  14.8 0.2 multiply_convert_fusion
  15.1 0.5 collective-permute-start
  15.6 2.6 %collective-permute-start.1 = (bf16[16,2,2,256]{3,2,1,0:T(2,128)(2,1)S(1)}, bf16[16,2,2,256]{3,2,1,0:T(2,128)(2,1)S(1)}, u32[]{:S(2)}, u32[]{:S(2)}) collective-permute-start(bf16[16,2,2,256]{3,2,1,0:T(2,128)(2,1)S(1)} %get-tuple-element.17), channel_id=1, source_target_pairs={{0,2},{1,3},{2,0},{3,1},{4,6},{5,7},{6,4},{7,5},{8,10},{9,11},{10,... | collective-permute-start | bytes 98312 | tf_op jit(solution)/shard_map/ppermute | solution.py:133
  18.2 1.4 %collective-permute-start.2 = (bf16[16,2,2,256]{3,2,1,0:T(2,128)(2,1)S(1)}, bf16[16,2,2,256]{3,2,1,0:T(2,128)(2,1)S(1)}, u32[]{:S(2)}, u32[]{:S(2)}) collective-permute-start(bf16[16,2,2,256]{3,2,1,0:T(2,128)(2,1)S(1)} %get-tuple-element.16), channel_id=1, source_target_pairs={{0,3},{1,0},{2,1},{3,2},{4,7},{5,4},{6,5},{7,6},{8,11},{9,8},{10,9... | collective-permute-start | bytes 98312 | tf_op jit(solution)/shard_map/ppermute | solution.py:133
  19.5 0.5 fusion.50
  20.2 0.9 %collective-permute-done.2 = bf16[16,2,2,256]{3,2,1,0:T(2,128)(2,1)S(1)} collective-permute-done((bf16[16,2,2,256]{3,2,1,0:T(2,128)(2,1)S(1)}, bf16[16,2,2,256]{3,2,1,0:T(2,128)(2,1)S(1)}, u32[]{:S(2)}, u32[]{:S(2)}) %collective-permute-start.2) | collective-permute-done | bytes 32800 | tf_op jit(solution)/shard_map/ppermute | solution.py:133
  21.1 0.2 maximum_bitcast_fusion
  21.4 1.3 %collective-permute-start.3 = (bf16[16,16,256]{2,1,0:T(8,128)(2,1)S(1)}, bf16[16,16,256]{2,1,0:T(8,128)(2,1)S(1)}, u32[]{:S(2)}, u32[]{:S(2)}) collective-permute-start(bf16[16,16,256]{2,1,0:T(8,128)(2,1)S(1)} %bitcast.72), channel_id=1, source_target_pairs={{4,0},{8,4},{12,8},{16,12},{20,16},{24,20},{28,24},{5,1},{9,5},{13... | collective-permute-start | bytes 393224 | tf_op jit(solution)/shard_map/ppermute | solution.py:143
  22.7 1.3 %collective-permute-start.4 = (bf16[16,16,256]{2,1,0:T(8,128)(2,1)S(1)}, bf16[16,16,256]{2,1,0:T(8,128)(2,1)S(1)}, u32[]{:S(2)}, u32[]{:S(2)}) collective-permute-start(bf16[16,16,256]{2,1,0:T(8,128)(2,1)S(1)} %bitcast.73), channel_id=1, source_target_pairs={{8,0},{12,4},{16,8},{20,12},{24,16},{28,20},{9,1},{13,5},{17,9},{2... | collective-permute-start | bytes 393224 | tf_op jit(solution)/shard_map/ppermute | solution.py:143
  24.0 1.3 %collective-permute-start.5 = (bf16[16,16,256]{2,1,0:T(8,128)(2,1)S(1)}, bf16[16,16,256]{2,1,0:T(8,128)(2,1)S(1)}, u32[]{:S(2)}, u32[]{:S(2)}) collective-permute-start(bf16[16,16,256]{2,1,0:T(8,128)(2,1)S(1)} %bitcast.74), channel_id=1, source_target_pairs={{12,0},{16,4},{20,8},{24,12},{28,16},{13,1},{17,5},{21,9},{25,13},... | collective-permute-start | bytes 393224 | tf_op jit(solution)/shard_map/ppermute | solution.py:143
  25.3 1.3 %collective-permute-start.6 = (bf16[16,16,256]{2,1,0:T(8,128)(2,1)S(1)}, bf16[16,16,256]{2,1,0:T(8,128)(2,1)S(1)}, u32[]{:S(2)}, u32[]{:S(2)}) collective-permute-start(bf16[16,16,256]{2,1,0:T(8,128)(2,1)S(1)} %bitcast.75), channel_id=1, source_target_pairs={{16,0},{20,4},{24,8},{28,12},{17,1},{21,5},{25,9},{29,13},{18,2},{... | collective-permute-start | bytes 393224 | tf_op jit(solution)/shard_map/ppermute | solution.py:143
  26.6 1.3 %collective-permute-start.7 = (bf16[16,16,256]{2,1,0:T(8,128)(2,1)S(1)}, bf16[16,16,256]{2,1,0:T(8,128)(2,1)S(1)}, u32[]{:S(2)}, u32[]{:S(2)}) collective-permute-start(bf16[16,16,256]{2,1,0:T(8,128)(2,1)S(1)} %bitcast.76), channel_id=1, source_target_pairs={{20,0},{24,4},{28,8},{21,1},{25,5},{29,9},{22,2},{26,6},{30,10},{2... | collective-permute-start | bytes 393224 | tf_op jit(solution)/shard_map/ppermute | solution.py:143
  27.9 1.2 %collective-permute-done.3 = bf16[16,16,256]{2,1,0:T(8,128)(2,1)S(1)} collective-permute-done((bf16[16,16,256]{2,1,0:T(8,128)(2,1)S(1)}, bf16[16,16,256]{2,1,0:T(8,128)(2,1)S(1)}, u32[]{:S(2)}, u32[]{:S(2)}) %collective-permute-start.3) | collective-permute-done | bytes 131104 | tf_op jit(solution)/shard_map/ppermute | solution.py:143
  29.1 1.3 %collective-permute-start.8 = (bf16[16,16,256]{2,1,0:T(8,128)(2,1)S(1)}, bf16[16,16,256]{2,1,0:T(8,128)(2,1)S(1)}, u32[]{:S(2)}, u32[]{:S(2)}) collective-permute-start(bf16[16,16,256]{2,1,0:T(8,128)(2,1)S(1)} %bitcast.77), channel_id=1, source_target_pairs={{24,0},{28,4},{25,1},{29,5},{26,2},{30,6},{27,3},{31,7}} | collective-permute-start | bytes 393224 | tf_op jit(solution)/shard_map/ppermute | solution.py:143
  30.4 2.7 %collective-permute-done.4 = bf16[16,16,256]{2,1,0:T(8,128)(2,1)S(1)} collective-permute-done((bf16[16,16,256]{2,1,0:T(8,128)(2,1)S(1)}, bf16[16,16,256]{2,1,0:T(8,128)(2,1)S(1)}, u32[]{:S(2)}, u32[]{:S(2)}) %collective-permute-start.4) | collective-permute-done | bytes 131104 | tf_op jit(solution)/shard_map/ppermute | solution.py:143
  33.1 1.5 %collective-permute-start.9 = (bf16[16,16,256]{2,1,0:T(8,128)(2,1)S(1)}, bf16[16,16,256]{2,1,0:T(8,128)(2,1)S(1)}, u32[]{:S(2)}, u32[]{:S(2)}) collective-permute-start(bf16[16,16,256]{2,1,0:T(8,128)(2,1)S(1)} %bitcast.78), channel_id=1, source_target_pairs={{28,0},{29,1},{30,2},{31,3}} | collective-permute-start | bytes 393224 | tf_op jit(solution)/shard_map/ppermute | solution.py:143
  34.6 0.5 collective-permute-done.5
  35.1 15.9 %collective-permute-done.6 = bf16[16,16,256]{2,1,0:T(8,128)(2,1)S(1)} collective-permute-done((bf16[16,16,256]{2,1,0:T(8,128)(2,1)S(1)}, bf16[16,16,256]{2,1,0:T(8,128)(2,1)S(1)}, u32[]{:S(2)}, u32[]{:S(2)}) %collective-permute-start.6) | collective-permute-done | bytes 131104 | tf_op jit(solution)/shard_map/ppermute | solution.py:143
  50.9 2.1 %collective-permute-done.7 = bf16[16,16,256]{2,1,0:T(8,128)(2,1)S(1)} collective-permute-done((bf16[16,16,256]{2,1,0:T(8,128)(2,1)S(1)}, bf16[16,16,256]{2,1,0:T(8,128)(2,1)S(1)}, u32[]{:S(2)}, u32[]{:S(2)}) %collective-permute-start.7) | collective-permute-done | bytes 131104 | tf_op jit(solution)/shard_map/ppermute | solution.py:143
  53.2 0.3 convert_element_type.78.white_ref
  53.5 3.9 %shard_map.38 = f32[32,2,16,256]{3,2,1,0:T(8,128)S(1)} custom-call(s32[32]{0:T(128)S(1)} %get-tuple-element.30.offsets_ref, s32[1]{0:T(128)} %constant.111.clone.1.base_ref, f32[144,16,256]{2,1,0:T(8,128)S(1)} %convert_element_type.78.white_ref), custom_call_target="tpu_custom_call" | custom-call | flops 16777216 | bytes 3407872 | tf_op jit(solution)/shard_map/pallas_call | solution.py:60
  57.4 0.9 convert_element_type.82
  58.3 0.3 fusion.54
  58.6 3.9 %shard_map.39 = f32[32,2,16,256]{3,2,1,0:T(8,128)S(1)} custom-call(s32[32]{0:T(128)S(1)} %get-tuple-element.32.offsets_ref, s32[1]{0:T(128)} %constant.111.clone.1.base_ref, f32[144,16,256]{2,1,0:T(8,128)S(1)} %convert_element_type.78.white_ref), custom_call_target="tpu_custom_call" | custom-call | flops 16777216 | bytes 3407872 | tf_op jit(solution)/shard_map/pallas_call | solution.py:60
  62.5 0.9 convert_element_type.83
  63.4 1.7 %collective-permute-start.12 = (bf16[32,2,16,256]{3,2,1,0:T(8,128)(2,1)}, bf16[32,2,16,256]{3,2,1,0:T(8,128)(2,1)}, u32[]{:S(2)}, u32[]{:S(2)}) collective-permute-start(bf16[32,2,16,256]{3,2,1,0:T(8,128)(2,1)} %convert_element_type.83), channel_id=1, source_target_pairs={{0,3},{1,0},{2,1},{3,2},{4,7},{5,4},{6,5},{7,6},{8,11},{9,8},{10,9... | collective-permute-start | bytes 1572872 | tf_op jit(solution)/shard_map/ppermute | solution.py:164
  65.1 2.0 %negate_convert_fusion.1 = (bf16[1024,16,32]{0,2,1:T(8,128)(2,1)}, bf16[1024,16,32]{0,2,1:T(8,128)(2,1)}) fusion(f32[1024,16]{0,1:T(8,128)S(1)} %get-tuple-element.22, f32[1024,32]{0,1:T(8,128)S(1)} %get-tuple-element.28, f32[1024,16]{0,1:T(8,128)S(1)} %get-tuple-element.21, f32[1024,32]{0,1:T(8,128)S(1)} %get-tuple-element.27), kind=kLoop, calls=%fused_computation.15 | loop fusion | flops 4718592 | bytes 2490368 | tf_op jit(solution)/shard_map/convert.2
  67.1 1.5 %copy.7 = bf16[1,1024,512]{2,1,0:T(8,128)(2,1)S(1)} copy(bf16[1,1024,512]{1,2,0:T(8,128)(2,1)} %bitcast.71) | data formatting | bytes 2097152 | tf_op jit(solution)/shard_map/sub | solution.py:27
  68.6 2.3 %copy.8 = bf16[1,1024,512]{2,1,0:T(8,128)(2,1)} copy(bf16[1,1024,512]{1,2,0:T(8,128)(2,1)} %bitcast.70) | data formatting | bytes 2097152 | tf_op jit(solution)/shard_map/neg | solution.py:29
  70.9 3.9 %shard_map.37 = f32[32,2,16,256]{3,2,1,0:T(8,128)S(1)} custom-call(s32[32]{0:T(128)S(1)} %get-tuple-element.29.offsets_ref, s32[1]{0:T(128)} %constant.111.clone.1.base_ref, f32[144,16,256]{2,1,0:T(8,128)S(1)} %convert_element_type.78.white_ref), custom_call_target="tpu_custom_call" | custom-call | flops 16777216 | bytes 3407872 | tf_op jit(solution)/shard_map/pallas_call | solution.py:60
  74.9 1.6 %collective-permute-start.10 = (bf16[32,2,16,256]{3,2,1,0:T(8,128)(2,1)S(1)}, bf16[32,2,16,256]{3,2,1,0:T(8,128)(2,1)S(1)}, u32[]{:S(2)}, u32[]{:S(2)}) collective-permute-start(bf16[32,2,16,256]{3,2,1,0:T(8,128)(2,1)S(1)} %convert_element_type.79), channel_id=1, source_target_pairs={{0,2},{1,3},{2,0},{3,1},{4,6},{5,7},{6,4},{7,5},{8,10},{9,11},{10,... | collective-permute-start | bytes 1572872 | tf_op jit(solution)/shard_map/ppermute | solution.py:164
  76.5 3.9 %shard_map.40 = f32[32,2,16,256]{3,2,1,0:T(8,128)S(1)} custom-call(s32[32]{0:T(128)S(1)} %get-tuple-element.31.offsets_ref, s32[1]{0:T(128)} %constant.111.clone.1.base_ref, f32[144,16,256]{2,1,0:T(8,128)S(1)} %convert_element_type.78.white_ref), custom_call_target="tpu_custom_call" | custom-call | flops 16777216 | bytes 3407872 | tf_op jit(solution)/shard_map/pallas_call | solution.py:60
  80.4 0.4 convolution_bitcast_fusion
  80.8 1.5 %convolution_bitcast_fusion.2 = f32[32,16,512]{2,1,0:T(8,128)S(1)} fusion(bf16[32,2,16,256]{3,2,1,0:T(8,128)(2,1)} %collective-permute-done.11, s32[]{:T(128)S(6)} %select_n.110, bf16[1,1024,512]{2,1,0:T(8,128)(2,1)S(1)} %copy.7, bf16[1,1024,512]{2,1,0:T(8,128)(2,1)S(1)} %copy-done), kind=kOutput, calls=%fused_computation.19 | convolution fusion | flops 269484032 | bytes 3670020 | tf_op jit(solution)/shard_map/opck,pkl->ocl/dot_general | solution.py:167
  82.3 1.5 %convolution_bitcast_fusion.1 = f32[32,16,512]{2,1,0:T(8,128)S(1)} fusion(bf16[32,2,16,256]{3,2,1,0:T(8,128)(2,1)} %collective-permute-done.12, s32[]{:T(128)S(6)} %select_n.108, bf16[1,1024,512]{2,1,0:T(8,128)(2,1)S(1)} %copy.7, bf16[1,1024,512]{2,1,0:T(8,128)(2,1)S(1)} %copy-done), kind=kOutput, calls=%fused_computation.18 | convolution fusion | flops 269484032 | bytes 3670020 | tf_op jit(solution)/shard_map/opck,pkl->ocl/dot_general | solution.py:167
  83.8 4.9 %collective-permute-done.10 = bf16[32,2,16,256]{3,2,1,0:T(8,128)(2,1)S(1)} collective-permute-done((bf16[32,2,16,256]{3,2,1,0:T(8,128)(2,1)S(1)}, bf16[32,2,16,256]{3,2,1,0:T(8,128)(2,1)S(1)}, u32[]{:S(2)}, u32[]{:S(2)}) %collective-permute-start.10) | collective-permute-done | bytes 524320 | tf_op jit(solution)/shard_map/ppermute | solution.py:164
  88.7 1.3 %fusion.11 = bf16[32,16,512]{2,1,0:T(8,128)(2,1)} fusion(f32[32,16,512]{2,1,0:T(8,128)S(1)} %convolution_bitcast_fusion, f32[32,16,512]{2,1,0:T(8,128)S(1)} %convolution_bitcast_fusion.1, f32[32,16,512]{2,1,0:T(8,128)S(1)} %convolution_bitcast_fusion.2, bf16[32,2,16,256]{3,2,1,0:T(8,128)(2,1)S(1)} %collective-permute-done.10, s32[]{:T(128)S(6)} %select_n.109, ...), kind=kOutput, calls=%fused_computation.25 | convolution fusion | flops 270794752 | bytes 6291460 | tf_op jit(solution)/shard_map/opck,pkl->ocl/dot_general | solution.py:167
  (32 shorter events, 0.8 us)
Async XLA Ops:
  13.4 6.1 %copy-start.1 = (s32[1024]{0:T(1024)S(1)}, s32[1024]{0:T(1024)}, u32[]{:S(2)}) copy-start(s32[1024]{0:T(1024)} %param.4) | copy-start | bytes 12292
  13.4 6.7 %copy-start.2 = (s32[128]{0:T(128)S(1)}, s32[128]{0:T(128)}, u32[]{:S(2)}) copy-start(s32[128]{0:T(128)} %param.5) | copy-start | bytes 1540
  15.1 5.1 %collective-permute-start = (bf16[16,2,2,256]{3,2,1,0:T(2,128)(2,1)S(1)}, bf16[16,2,2,256]{3,2,1,0:T(2,128)(2,1)S(1)}, u32[]{:S(2)}, u32[]{:S(2)}) collective-permute-start(bf16[16,2,2,256]{3,2,1,0:T(2,128)(2,1)S(1)} %get-tuple-element.18), channel_id=1, source_target_pairs={{0,1},{1,2},{2,3},{3,0},{4,5},{5,6},{6,7},{7,4},{8,9},{9,10},{10,1... | collective-permute-start | bytes 98312 | tf_op jit(solution)/shard_map/ppermute | solution.py:133
  15.6 4.6 %collective-permute-start.1 = (bf16[16,2,2,256]{3,2,1,0:T(2,128)(2,1)S(1)}, bf16[16,2,2,256]{3,2,1,0:T(2,128)(2,1)S(1)}, u32[]{:S(2)}, u32[]{:S(2)}) collective-permute-start(bf16[16,2,2,256]{3,2,1,0:T(2,128)(2,1)S(1)} %get-tuple-element.17), channel_id=1, source_target_pairs={{0,2},{1,3},{2,0},{3,1},{4,6},{5,7},{6,4},{7,5},{8,10},{9,11},{10,... | collective-permute-start | bytes 98312 | tf_op jit(solution)/shard_map/ppermute | solution.py:133
  18.2 3.0 %collective-permute-start.2 = (bf16[16,2,2,256]{3,2,1,0:T(2,128)(2,1)S(1)}, bf16[16,2,2,256]{3,2,1,0:T(2,128)(2,1)S(1)}, u32[]{:S(2)}, u32[]{:S(2)}) collective-permute-start(bf16[16,2,2,256]{3,2,1,0:T(2,128)(2,1)S(1)} %get-tuple-element.16), channel_id=1, source_target_pairs={{0,3},{1,0},{2,1},{3,2},{4,7},{5,4},{6,5},{7,6},{8,11},{9,8},{10,9... | collective-permute-start | bytes 98312 | tf_op jit(solution)/shard_map/ppermute | solution.py:133
  21.4 7.7 %collective-permute-start.3 = (bf16[16,16,256]{2,1,0:T(8,128)(2,1)S(1)}, bf16[16,16,256]{2,1,0:T(8,128)(2,1)S(1)}, u32[]{:S(2)}, u32[]{:S(2)}) collective-permute-start(bf16[16,16,256]{2,1,0:T(8,128)(2,1)S(1)} %bitcast.72), channel_id=1, source_target_pairs={{4,0},{8,4},{12,8},{16,12},{20,16},{24,20},{28,24},{5,1},{9,5},{13... | collective-permute-start | bytes 393224 | tf_op jit(solution)/shard_map/ppermute | solution.py:143
  22.7 10.4 %collective-permute-start.4 = (bf16[16,16,256]{2,1,0:T(8,128)(2,1)S(1)}, bf16[16,16,256]{2,1,0:T(8,128)(2,1)S(1)}, u32[]{:S(2)}, u32[]{:S(2)}) collective-permute-start(bf16[16,16,256]{2,1,0:T(8,128)(2,1)S(1)} %bitcast.73), channel_id=1, source_target_pairs={{8,0},{12,4},{16,8},{20,12},{24,16},{28,20},{9,1},{13,5},{17,9},{2... | collective-permute-start | bytes 393224 | tf_op jit(solution)/shard_map/ppermute | solution.py:143
  24.0 11.1 %collective-permute-start.5 = (bf16[16,16,256]{2,1,0:T(8,128)(2,1)S(1)}, bf16[16,16,256]{2,1,0:T(8,128)(2,1)S(1)}, u32[]{:S(2)}, u32[]{:S(2)}) collective-permute-start(bf16[16,16,256]{2,1,0:T(8,128)(2,1)S(1)} %bitcast.74), channel_id=1, source_target_pairs={{12,0},{16,4},{20,8},{24,12},{28,16},{13,1},{17,5},{21,9},{25,13},... | collective-permute-start | bytes 393224 | tf_op jit(solution)/shard_map/ppermute | solution.py:143
  25.3 25.6 %collective-permute-start.6 = (bf16[16,16,256]{2,1,0:T(8,128)(2,1)S(1)}, bf16[16,16,256]{2,1,0:T(8,128)(2,1)S(1)}, u32[]{:S(2)}, u32[]{:S(2)}) collective-permute-start(bf16[16,16,256]{2,1,0:T(8,128)(2,1)S(1)} %bitcast.75), channel_id=1, source_target_pairs={{16,0},{20,4},{24,8},{28,12},{17,1},{21,5},{25,9},{29,13},{18,2},{... | collective-permute-start | bytes 393224 | tf_op jit(solution)/shard_map/ppermute | solution.py:143
  26.6 26.5 %collective-permute-start.7 = (bf16[16,16,256]{2,1,0:T(8,128)(2,1)S(1)}, bf16[16,16,256]{2,1,0:T(8,128)(2,1)S(1)}, u32[]{:S(2)}, u32[]{:S(2)}) collective-permute-start(bf16[16,16,256]{2,1,0:T(8,128)(2,1)S(1)} %bitcast.76), channel_id=1, source_target_pairs={{20,0},{24,4},{28,8},{21,1},{25,5},{29,9},{22,2},{26,6},{30,10},{2... | collective-permute-start | bytes 393224 | tf_op jit(solution)/shard_map/ppermute | solution.py:143
  29.1 24.0 %collective-permute-start.8 = (bf16[16,16,256]{2,1,0:T(8,128)(2,1)S(1)}, bf16[16,16,256]{2,1,0:T(8,128)(2,1)S(1)}, u32[]{:S(2)}, u32[]{:S(2)}) collective-permute-start(bf16[16,16,256]{2,1,0:T(8,128)(2,1)S(1)} %bitcast.77), channel_id=1, source_target_pairs={{24,0},{28,4},{25,1},{29,5},{26,2},{30,6},{27,3},{31,7}} | collective-permute-start | bytes 393224 | tf_op jit(solution)/shard_map/ppermute | solution.py:143
  33.1 20.1 %collective-permute-start.9 = (bf16[16,16,256]{2,1,0:T(8,128)(2,1)S(1)}, bf16[16,16,256]{2,1,0:T(8,128)(2,1)S(1)}, u32[]{:S(2)}, u32[]{:S(2)}) collective-permute-start(bf16[16,16,256]{2,1,0:T(8,128)(2,1)S(1)} %bitcast.78), channel_id=1, source_target_pairs={{28,0},{29,1},{30,2},{31,3}} | collective-permute-start | bytes 393224 | tf_op jit(solution)/shard_map/ppermute | solution.py:143
  58.3 22.6 %collective-permute-start.11 = (bf16[32,2,16,256]{3,2,1,0:T(8,128)(2,1)}, bf16[32,2,16,256]{3,2,1,0:T(8,128)(2,1)}, u32[]{:S(2)}, u32[]{:S(2)}) collective-permute-start(bf16[32,2,16,256]{3,2,1,0:T(8,128)(2,1)} %convert_element_type.82), channel_id=1, source_target_pairs={{0,1},{1,2},{2,3},{3,0},{4,5},{5,6},{6,7},{7,4},{8,9},{9,10},{10,1... | collective-permute-start | bytes 1572872 | tf_op jit(solution)/shard_map/ppermute | solution.py:164
  63.4 19.0 %collective-permute-start.12 = (bf16[32,2,16,256]{3,2,1,0:T(8,128)(2,1)}, bf16[32,2,16,256]{3,2,1,0:T(8,128)(2,1)}, u32[]{:S(2)}, u32[]{:S(2)}) collective-permute-start(bf16[32,2,16,256]{3,2,1,0:T(8,128)(2,1)} %convert_element_type.83), channel_id=1, source_target_pairs={{0,3},{1,0},{2,1},{3,2},{4,7},{5,4},{6,5},{7,6},{8,11},{9,8},{10,9... | collective-permute-start | bytes 1572872 | tf_op jit(solution)/shard_map/ppermute | solution.py:164
  74.9 5.5 %copy-start = (bf16[1,1024,512]{2,1,0:T(8,128)(2,1)S(1)}, bf16[1,1024,512]{2,1,0:T(8,128)(2,1)}, u32[]{:S(2)}) copy-start(bf16[1,1024,512]{2,1,0:T(8,128)(2,1)} %copy.8) | copy-start | bytes 3145732
  74.9 13.8 %collective-permute-start.10 = (bf16[32,2,16,256]{3,2,1,0:T(8,128)(2,1)S(1)}, bf16[32,2,16,256]{3,2,1,0:T(8,128)(2,1)S(1)}, u32[]{:S(2)}, u32[]{:S(2)}) collective-permute-start(bf16[32,2,16,256]{3,2,1,0:T(8,128)(2,1)S(1)} %convert_element_type.79), channel_id=1, source_target_pairs={{0,2},{1,3},{2,0},{3,1},{4,6},{5,7},{6,4},{7,5},{8,10},{9,11},{10,... | collective-permute-start | bytes 1572872 | tf_op jit(solution)/shard_map/ppermute | solution.py:164

commit v23 on v19

--- a/solution.py
+++ b/solution.py
@@ -37,12 +37,11 @@
 def cross_kernel(offsets_ref, base_ref, white_ref, out_ref, *, group, own_count, half):
     step = pl.program_id(0)
     base = base_ref[0]
-    own = [white_ref[base + c].astype(jnp.float32) for c in range(own_count)]
 
     def one_offset(i, carry):
         shift = offsets_ref[step * group + i]
         for c in range(own_count):
-            a = own[c]
+            a = white_ref[base + c].astype(jnp.float32)
             b = white_ref[base + c + shift].astype(jnp.float32)
             ar, ai, br, bi = a[:half], a[half:], b[:half], b[half:]
             out_ref[i, 0, pl.ds(c, 1), :] = jnp.sum(ar * br + ai * bi, axis=0, keepdims=True)

time: 85.1 us -> 85 us (level)
  no operation moved by 1% of the time
where the time goes in v23:
time: 85 us; the launch traced here: 84.5 us
  waiting for transfers between devices  24.2 us (28%)
  starting transfers between devices  15.7 us (18%)
  Pallas kernels  15.3 us (18%)
  other arithmetic  13.8 us (16%)
  local copies, waits for them, and re-layouts  7.97 us (9%)
  matrix products  7.12 us (8%)
    ppermute x7, waiting for transfers between devices, local(): blocks.append(lax.ppermute(rows_white, 'gx', perm=pairs))  22.4 us
    pallas_call x4, Pallas kernels, cross_spectra(): pl.pallas_call(kernel, grid_spec=pltpu.PrefetchScalarGridSpec(num_scalar_...  15.3 us
    ppermute x7, starting transfers between devices, local(): blocks.append(lax.ppermute(rows_white, 'gx', perm=pairs))  9.2 us
    another operation x2, other arithmetic  5.69 us
    dot_general x4, matrix products, local(): jnp.einsum('opck,pkl->ocl', part, rows, preferred_element_type=jnp.float32)  4.66 us
    ppermute x3, starting transfers between devices, local(): lax.ppermute(piece, 'gy', perm=[(src, (src + shift) % gy_count) for src i...  4.46 us
    dot_general x1, matrix products, forward_spectra(): jnp.dot(record_rows.reshape(row_count * block_count, block_len), small_ta...  2.46 us
    neg x1, local copies, waits for them, and re-layouts, inverse_table(): return jnp.stack([cos_t, -sin_t], axis=0).astype(jnp.bfloat16)  2.31 us
  transfers between devices with their start and end apart: 13, of which 7 were waited for; matrix products, arithmetic and copies ran while one was open for 13% of the time, Pallas kernels for 14%

profile of v23, /device:TPU:0, one launch (start us, length us, event | category | flops | bytes accessed | tf_op | source)
XLA Modules:
  0.0 84.5 jit_solution(7040481926279346198)
XLA Ops:
  0.0 1.2 %fusion.52 = (f32[32,1024]{1,0:T(8,128)S(1)}, f32[32,1024]{1,0:T(8,128)S(1)}) fusion(s32[1024]{0:T(1024)} %param.4), kind=kLoop, calls=%fused_computation.87 | loop fusion | flops 458752 | bytes 266240 | tf_op jit(solution)/shard_map/cos | solution.py:89
  1.2 0.7 add_select_fusion.5
  1.9 1.8 %fusion.41 = (f32[64,1024]{1,0:T(8,128)S(1)}, f32[64,1024]{1,0:T(8,128)S(1)}) fusion(s32[1024]{0:T(1024)} %param.4, s32[64]{0:T(128)S(1)} %iota_multiply_fusion), kind=kLoop, calls=%fused_computation.70 | loop fusion | flops 917504 | bytes 528640 | tf_op jit(solution)/shard_map/cos | solution.py:89
  3.7 1.2 %reshape_reshape.3 = bf16[128,2048]{1,0:T(8,128)(2,1)S(1)} reshape(bf16[16,2,8192]{2,1,0:T(2,128)(2,1)} %param.3) | data formatting | bytes 1048576 | tf_op jit(solution)/shard_map/reshape;reshape | solution.py:102
  4.9 3.7 %subtract_convert_fusion = (bf16[64,32,1024]{2,1,0:T(8,128)(2,1)S(1)}, bf16[64,32,1024]{2,1,0:T(8,128)(2,1)S(1)}) fusion(f32[64,1024]{1,0:T(8,128)S(1)} %get-tuple-element.20, f32[32,1024]{1,0:T(8,128)S(1)} %get-tuple-element.26, f32[64,1024]{1,0:T(8,128)S(1)} %get-tuple-element.19, f32[32,1024]{1,0:T(8,128)S(1)} %get-tuple-element.25), kind=kLoop, calls=%fused_computation.5 | loop fusion | flops 18874368 | bytes 9175040 | tf_op jit(solution)/shard_map/convert.7
  8.5 2.5 %fusion.4 = f32[128,2048]{0,1:T(8,128)S(1)} fusion(bf16[128,2048]{1,0:T(8,128)(2,1)S(1)} %reshape_reshape.3, bf16[2048,1024]{1,0:T(8,128)(2,1)S(1)} %bitcast.69, bf16[2048,1024]{1,0:T(8,128)(2,1)S(1)} %bitcast.68), kind=kOutput, calls=%fused_computation.14 | convolution fusion | flops 1090519040 | bytes 9961472 | tf_op jit(solution)/shard_map/dot_general | solution.py:101
  11.0 0.3 copy.4
  11.3 0.9 %reshape.439 = f32[32,4,2,1024]{3,2,1,0:T(2,128)S(1)} reshape(f32[128,2048]{1,0:T(8,128)S(1)} %copy.4) | data formatting | bytes 2097152 | tf_op jit(solution)/shard_map/reshape | solution.py:105
  12.2 1.2 %fusion.68 = (f32[32,4,1,1024]{3,2,1,0:T(1,128)S(1)}, f32[32,4,1,1024]{3,2,1,0:T(1,128)S(1)}) fusion(f32[32,4,2,1024]{3,2,1,0:T(2,128)S(1)} %reshape.439), kind=kLoop, calls=%fused_computation.126 | loop fusion | bytes 2097152 | tf_op jit(solution)/shard_map/slice | solution.py:112
  13.6 0.8 fusion.25
  14.5 0.2 concatenate.18
  14.8 0.2 multiply_convert_fusion
  15.1 0.5 collective-permute-start
  15.6 2.6 %collective-permute-start.1 = (bf16[16,2,2,256]{3,2,1,0:T(2,128)(2,1)S(1)}, bf16[16,2,2,256]{3,2,1,0:T(2,128)(2,1)S(1)}, u32[]{:S(2)}, u32[]{:S(2)}) collective-permute-start(bf16[16,2,2,256]{3,2,1,0:T(2,128)(2,1)S(1)} %get-tuple-element.17), channel_id=1, source_target_pairs={{0,2},{1,3},{2,0},{3,1},{4,6},{5,7},{6,4},{7,5},{8,10},{9,11},{10,... | collective-permute-start | bytes 98312 | tf_op jit(solution)/shard_map/ppermute | solution.py:132
  18.2 1.4 %collective-permute-start.2 = (bf16[16,2,2,256]{3,2,1,0:T(2,128)(2,1)S(1)}, bf16[16,2,2,256]{3,2,1,0:T(2,128)(2,1)S(1)}, u32[]{:S(2)}, u32[]{:S(2)}) collective-permute-start(bf16[16,2,2,256]{3,2,1,0:T(2,128)(2,1)S(1)} %get-tuple-element.16), channel_id=1, source_target_pairs={{0,3},{1,0},{2,1},{3,2},{4,7},{5,4},{6,5},{7,6},{8,11},{9,8},{10,9... | collective-permute-start | bytes 98312 | tf_op jit(solution)/shard_map/ppermute | solution.py:132
  19.5 0.5 fusion.50
  20.2 0.9 %collective-permute-done.2 = bf16[16,2,2,256]{3,2,1,0:T(2,128)(2,1)S(1)} collective-permute-done((bf16[16,2,2,256]{3,2,1,0:T(2,128)(2,1)S(1)}, bf16[16,2,2,256]{3,2,1,0:T(2,128)(2,1)S(1)}, u32[]{:S(2)}, u32[]{:S(2)}) %collective-permute-start.2) | collective-permute-done | bytes 32800 | tf_op jit(solution)/shard_map/ppermute | solution.py:132
  21.1 0.2 maximum_bitcast_fusion
  21.4 1.3 %collective-permute-start.3 = (bf16[16,16,256]{2,1,0:T(8,128)(2,1)S(1)}, bf16[16,16,256]{2,1,0:T(8,128)(2,1)S(1)}, u32[]{:S(2)}, u32[]{:S(2)}) collective-permute-start(bf16[16,16,256]{2,1,0:T(8,128)(2,1)S(1)} %bitcast.72), channel_id=1, source_target_pairs={{4,0},{8,4},{12,8},{16,12},{20,16},{24,20},{28,24},{5,1},{9,5},{13... | collective-permute-start | bytes 393224 | tf_op jit(solution)/shard_map/ppermute | solution.py:142
  22.7 1.3 %collective-permute-start.4 = (bf16[16,16,256]{2,1,0:T(8,128)(2,1)S(1)}, bf16[16,16,256]{2,1,0:T(8,128)(2,1)S(1)}, u32[]{:S(2)}, u32[]{:S(2)}) collective-permute-start(bf16[16,16,256]{2,1,0:T(8,128)(2,1)S(1)} %bitcast.73), channel_id=1, source_target_pairs={{8,0},{12,4},{16,8},{20,12},{24,16},{28,20},{9,1},{13,5},{17,9},{2... | collective-permute-start | bytes 393224 | tf_op jit(solution)/shard_map/ppermute | solution.py:142
  24.0 1.3 %collective-permute-start.5 = (bf16[16,16,256]{2,1,0:T(8,128)(2,1)S(1)}, bf16[16,16,256]{2,1,0:T(8,128)(2,1)S(1)}, u32[]{:S(2)}, u32[]{:S(2)}) collective-permute-start(bf16[16,16,256]{2,1,0:T(8,128)(2,1)S(1)} %bitcast.74), channel_id=1, source_target_pairs={{12,0},{16,4},{20,8},{24,12},{28,16},{13,1},{17,5},{21,9},{25,13},... | collective-permute-start | bytes 393224 | tf_op jit(solution)/shard_map/ppermute | solution.py:142
  25.3 1.3 %collective-permute-start.6 = (bf16[16,16,256]{2,1,0:T(8,128)(2,1)S(1)}, bf16[16,16,256]{2,1,0:T(8,128)(2,1)S(1)}, u32[]{:S(2)}, u32[]{:S(2)}) collective-permute-start(bf16[16,16,256]{2,1,0:T(8,128)(2,1)S(1)} %bitcast.75), channel_id=1, source_target_pairs={{16,0},{20,4},{24,8},{28,12},{17,1},{21,5},{25,9},{29,13},{18,2},{... | collective-permute-start | bytes 393224 | tf_op jit(solution)/shard_map/ppermute | solution.py:142
  26.6 1.3 %collective-permute-start.7 = (bf16[16,16,256]{2,1,0:T(8,128)(2,1)S(1)}, bf16[16,16,256]{2,1,0:T(8,128)(2,1)S(1)}, u32[]{:S(2)}, u32[]{:S(2)}) collective-permute-start(bf16[16,16,256]{2,1,0:T(8,128)(2,1)S(1)} %bitcast.76), channel_id=1, source_target_pairs={{20,0},{24,4},{28,8},{21,1},{25,5},{29,9},{22,2},{26,6},{30,10},{2... | collective-permute-start | bytes 393224 | tf_op jit(solution)/shard_map/ppermute | solution.py:142
  27.9 1.2 %collective-permute-done.3 = bf16[16,16,256]{2,1,0:T(8,128)(2,1)S(1)} collective-permute-done((bf16[16,16,256]{2,1,0:T(8,128)(2,1)S(1)}, bf16[16,16,256]{2,1,0:T(8,128)(2,1)S(1)}, u32[]{:S(2)}, u32[]{:S(2)}) %collective-permute-start.3) | collective-permute-done | bytes 131104 | tf_op jit(solution)/shard_map/ppermute | solution.py:142
  29.1 1.3 %collective-permute-start.8 = (bf16[16,16,256]{2,1,0:T(8,128)(2,1)S(1)}, bf16[16,16,256]{2,1,0:T(8,128)(2,1)S(1)}, u32[]{:S(2)}, u32[]{:S(2)}) collective-permute-start(bf16[16,16,256]{2,1,0:T(8,128)(2,1)S(1)} %bitcast.77), channel_id=1, source_target_pairs={{24,0},{28,4},{25,1},{29,5},{26,2},{30,6},{27,3},{31,7}} | collective-permute-start | bytes 393224 | tf_op jit(solution)/shard_map/ppermute | solution.py:142
  30.4 2.7 %collective-permute-done.4 = bf16[16,16,256]{2,1,0:T(8,128)(2,1)S(1)} collective-permute-done((bf16[16,16,256]{2,1,0:T(8,128)(2,1)S(1)}, bf16[16,16,256]{2,1,0:T(8,128)(2,1)S(1)}, u32[]{:S(2)}, u32[]{:S(2)}) %collective-permute-start.4) | collective-permute-done | bytes 131104 | tf_op jit(solution)/shard_map/ppermute | solution.py:142
  33.1 1.5 %collective-permute-start.9 = (bf16[16,16,256]{2,1,0:T(8,128)(2,1)S(1)}, bf16[16,16,256]{2,1,0:T(8,128)(2,1)S(1)}, u32[]{:S(2)}, u32[]{:S(2)}) collective-permute-start(bf16[16,16,256]{2,1,0:T(8,128)(2,1)S(1)} %bitcast.78), channel_id=1, source_target_pairs={{28,0},{29,1},{30,2},{31,3}} | collective-permute-start | bytes 393224 | tf_op jit(solution)/shard_map/ppermute | solution.py:142
  34.6 0.5 collective-permute-done.5
  35.1 15.9 %collective-permute-done.6 = bf16[16,16,256]{2,1,0:T(8,128)(2,1)S(1)} collective-permute-done((bf16[16,16,256]{2,1,0:T(8,128)(2,1)S(1)}, bf16[16,16,256]{2,1,0:T(8,128)(2,1)S(1)}, u32[]{:S(2)}, u32[]{:S(2)}) %collective-permute-start.6) | collective-permute-done | bytes 131104 | tf_op jit(solution)/shard_map/ppermute | solution.py:142
  50.9 2.1 %collective-permute-done.7 = bf16[16,16,256]{2,1,0:T(8,128)(2,1)S(1)} collective-permute-done((bf16[16,16,256]{2,1,0:T(8,128)(2,1)S(1)}, bf16[16,16,256]{2,1,0:T(8,128)(2,1)S(1)}, u32[]{:S(2)}, u32[]{:S(2)}) %collective-permute-start.7) | collective-permute-done | bytes 131104 | tf_op jit(solution)/shard_map/ppermute | solution.py:142
  53.2 0.3 convert_element_type.78.white_ref
  53.5 3.8 %shard_map.38 = f32[32,2,16,256]{3,2,1,0:T(8,128)S(1)} custom-call(s32[32]{0:T(128)S(1)} %get-tuple-element.30.offsets_ref, s32[1]{0:T(128)} %constant.111.clone.1.base_ref, f32[144,16,256]{2,1,0:T(8,128)S(1)} %convert_element_type.78.white_ref), custom_call_target="tpu_custom_call" | custom-call | flops 16777216 | bytes 3407872 | tf_op jit(solution)/shard_map/pallas_call | solution.py:59
  57.3 0.9 %convert_element_type.82 = bf16[32,2,16,256]{3,2,1,0:T(8,128)(2,1)} convert(f32[32,2,16,256]{3,2,1,0:T(8,128)S(1)} %shard_map.38) | non-fusion elementwise | flops 262144 | bytes 1572864 | tf_op jit(solution)/shard_map/convert_element_type | solution.py:159
  58.2 1.5 %collective-permute-start.11 = (bf16[32,2,16,256]{3,2,1,0:T(8,128)(2,1)}, bf16[32,2,16,256]{3,2,1,0:T(8,128)(2,1)}, u32[]{:S(2)}, u32[]{:S(2)}) collective-permute-start(bf16[32,2,16,256]{3,2,1,0:T(8,128)(2,1)} %convert_element_type.82), channel_id=1, source_target_pairs={{0,2},{1,3},{2,0},{3,1},{4,6},{5,7},{6,4},{7,5},{8,10},{9,11},{10,... | collective-permute-start | bytes 1572872 | tf_op jit(solution)/shard_map/ppermute | solution.py:162
  59.7 0.3 fusion.54
  60.0 3.8 %shard_map.39 = f32[32,2,16,256]{3,2,1,0:T(8,128)S(1)} custom-call(s32[32]{0:T(128)S(1)} %get-tuple-element.32.offsets_ref, s32[1]{0:T(128)} %constant.111.clone.1.base_ref, f32[144,16,256]{2,1,0:T(8,128)S(1)} %convert_element_type.78.white_ref), custom_call_target="tpu_custom_call" | custom-call | flops 16777216 | bytes 3407872 | tf_op jit(solution)/shard_map/pallas_call | solution.py:59
  63.9 0.9 %convert_element_type.83 = bf16[32,2,16,256]{3,2,1,0:T(8,128)(2,1)} convert(f32[32,2,16,256]{3,2,1,0:T(8,128)S(1)} %shard_map.39) | non-fusion elementwise | flops 262144 | bytes 1572864 | tf_op jit(solution)/shard_map/convert_element_type | solution.py:159
  64.8 2.0 %negate_convert_fusion.1 = (bf16[1024,16,32]{0,2,1:T(8,128)(2,1)}, bf16[1024,16,32]{0,2,1:T(8,128)(2,1)}) fusion(f32[1024,16]{0,1:T(8,128)S(1)} %get-tuple-element.22, f32[1024,32]{0,1:T(8,128)S(1)} %get-tuple-element.28, f32[1024,16]{0,1:T(8,128)S(1)} %get-tuple-element.21, f32[1024,32]{0,1:T(8,128)S(1)} %get-tuple-element.27), kind=kLoop, calls=%fused_computation.15 | loop fusion | flops 4718592 | bytes 2490368 | tf_op jit(solution)/shard_map/convert.2
  66.8 1.5 %copy.7 = bf16[1,1024,512]{2,1,0:T(8,128)(2,1)S(1)} copy(bf16[1,1024,512]{1,2,0:T(8,128)(2,1)} %bitcast.71) | data formatting | bytes 2097152 | tf_op jit(solution)/shard_map/sub | solution.py:27
  68.3 2.3 %copy.8 = bf16[1,1024,512]{2,1,0:T(8,128)(2,1)} copy(bf16[1,1024,512]{1,2,0:T(8,128)(2,1)} %bitcast.70) | data formatting | bytes 2097152 | tf_op jit(solution)/shard_map/neg | solution.py:29
  70.6 3.8 %shard_map.37 = f32[32,2,16,256]{3,2,1,0:T(8,128)S(1)} custom-call(s32[32]{0:T(128)S(1)} %get-tuple-element.29.offsets_ref, s32[1]{0:T(128)} %constant.111.clone.1.base_ref, f32[144,16,256]{2,1,0:T(8,128)S(1)} %convert_element_type.78.white_ref), custom_call_target="tpu_custom_call" | custom-call | flops 16777216 | bytes 3407872 | tf_op jit(solution)/shard_map/pallas_call | solution.py:59
  74.5 0.6 collective-permute-start.10
  75.1 3.8 %shard_map.40 = f32[32,2,16,256]{3,2,1,0:T(8,128)S(1)} custom-call(s32[32]{0:T(128)S(1)} %get-tuple-element.31.offsets_ref, s32[1]{0:T(128)} %constant.111.clone.1.base_ref, f32[144,16,256]{2,1,0:T(8,128)S(1)} %convert_element_type.78.white_ref), custom_call_target="tpu_custom_call" | custom-call | flops 16777216 | bytes 3407872 | tf_op jit(solution)/shard_map/pallas_call | solution.py:59
  78.9 0.4 convolution_bitcast_fusion
  79.4 1.5 %convolution_bitcast_fusion.2 = f32[32,16,512]{2,1,0:T(8,128)S(1)} fusion(bf16[32,2,16,256]{3,2,1,0:T(8,128)(2,1)} %collective-permute-done.11, s32[]{:T(128)S(6)} %select_n.109, bf16[1,1024,512]{2,1,0:T(8,128)(2,1)S(1)} %copy.7, bf16[1,1024,512]{2,1,0:T(8,128)(2,1)S(1)} %copy-done), kind=kOutput, calls=%fused_computation.19 | convolution fusion | flops 269484032 | bytes 3670020 | tf_op jit(solution)/shard_map/opck,pkl->ocl/dot_general | solution.py:165
  80.9 1.5 %convolution_bitcast_fusion.1 = f32[32,16,512]{2,1,0:T(8,128)S(1)} fusion(bf16[32,2,16,256]{3,2,1,0:T(8,128)(2,1)} %collective-permute-done.12, s32[]{:T(128)S(6)} %select_n.108, bf16[1,1024,512]{2,1,0:T(8,128)(2,1)S(1)} %copy.7, bf16[1,1024,512]{2,1,0:T(8,128)(2,1)S(1)} %copy-done), kind=kOutput, calls=%fused_computation.18 | convolution fusion | flops 269484032 | bytes 3670020 | tf_op jit(solution)/shard_map/opck,pkl->ocl/dot_general | solution.py:165
  82.4 0.9 %collective-permute-done.10 = bf16[32,2,16,256]{3,2,1,0:T(8,128)(2,1)S(1)} collective-permute-done((bf16[32,2,16,256]{3,2,1,0:T(8,128)(2,1)S(1)}, bf16[32,2,16,256]{3,2,1,0:T(8,128)(2,1)S(1)}, u32[]{:S(2)}, u32[]{:S(2)}) %collective-permute-start.10) | collective-permute-done | bytes 524320 | tf_op jit(solution)/shard_map/ppermute | solution.py:162
  83.3 1.3 %fusion.11 = bf16[32,16,512]{2,1,0:T(8,128)(2,1)} fusion(f32[32,16,512]{2,1,0:T(8,128)S(1)} %convolution_bitcast_fusion, f32[32,16,512]{2,1,0:T(8,128)S(1)} %convolution_bitcast_fusion.1, f32[32,16,512]{2,1,0:T(8,128)S(1)} %convolution_bitcast_fusion.2, bf16[32,2,16,256]{3,2,1,0:T(8,128)(2,1)S(1)} %collective-permute-done.10, s32[]{:T(128)S(6)} %select_n.110, ...), kind=kOutput, calls=%fused_computation.25 | convolution fusion | flops 270794752 | bytes 6291460 | tf_op jit(solution)/shard_map/opck,pkl->ocl/dot_general | solution.py:165
  (32 shorter events, 0.8 us)
Async XLA Ops:
  13.4 6.1 %copy-start.1 = (s32[1024]{0:T(1024)S(1)}, s32[1024]{0:T(1024)}, u32[]{:S(2)}) copy-start(s32[1024]{0:T(1024)} %param.4) | copy-start | bytes 12292
  13.4 6.7 %copy-start.2 = (s32[128]{0:T(128)S(1)}, s32[128]{0:T(128)}, u32[]{:S(2)}) copy-start(s32[128]{0:T(128)} %param.5) | copy-start | bytes 1540
  15.1 5.1 %collective-permute-start = (bf16[16,2,2,256]{3,2,1,0:T(2,128)(2,1)S(1)}, bf16[16,2,2,256]{3,2,1,0:T(2,128)(2,1)S(1)}, u32[]{:S(2)}, u32[]{:S(2)}) collective-permute-start(bf16[16,2,2,256]{3,2,1,0:T(2,128)(2,1)S(1)} %get-tuple-element.18), channel_id=1, source_target_pairs={{0,1},{1,2},{2,3},{3,0},{4,5},{5,6},{6,7},{7,4},{8,9},{9,10},{10,1... | collective-permute-start | bytes 98312 | tf_op jit(solution)/shard_map/ppermute | solution.py:132
  15.6 4.6 %collective-permute-start.1 = (bf16[16,2,2,256]{3,2,1,0:T(2,128)(2,1)S(1)}, bf16[16,2,2,256]{3,2,1,0:T(2,128)(2,1)S(1)}, u32[]{:S(2)}, u32[]{:S(2)}) collective-permute-start(bf16[16,2,2,256]{3,2,1,0:T(2,128)(2,1)S(1)} %get-tuple-element.17), channel_id=1, source_target_pairs={{0,2},{1,3},{2,0},{3,1},{4,6},{5,7},{6,4},{7,5},{8,10},{9,11},{10,... | collective-permute-start | bytes 98312 | tf_op jit(solution)/shard_map/ppermute | solution.py:132
  18.2 3.0 %collective-permute-start.2 = (bf16[16,2,2,256]{3,2,1,0:T(2,128)(2,1)S(1)}, bf16[16,2,2,256]{3,2,1,0:T(2,128)(2,1)S(1)}, u32[]{:S(2)}, u32[]{:S(2)}) collective-permute-start(bf16[16,2,2,256]{3,2,1,0:T(2,128)(2,1)S(1)} %get-tuple-element.16), channel_id=1, source_target_pairs={{0,3},{1,0},{2,1},{3,2},{4,7},{5,4},{6,5},{7,6},{8,11},{9,8},{10,9... | collective-permute-start | bytes 98312 | tf_op jit(solution)/shard_map/ppermute | solution.py:132
  21.4 7.7 %collective-permute-start.3 = (bf16[16,16,256]{2,1,0:T(8,128)(2,1)S(1)}, bf16[16,16,256]{2,1,0:T(8,128)(2,1)S(1)}, u32[]{:S(2)}, u32[]{:S(2)}) collective-permute-start(bf16[16,16,256]{2,1,0:T(8,128)(2,1)S(1)} %bitcast.72), channel_id=1, source_target_pairs={{4,0},{8,4},{12,8},{16,12},{20,16},{24,20},{28,24},{5,1},{9,5},{13... | collective-permute-start | bytes 393224 | tf_op jit(solution)/shard_map/ppermute | solution.py:142
  22.7 10.4 %collective-permute-start.4 = (bf16[16,16,256]{2,1,0:T(8,128)(2,1)S(1)}, bf16[16,16,256]{2,1,0:T(8,128)(2,1)S(1)}, u32[]{:S(2)}, u32[]{:S(2)}) collective-permute-start(bf16[16,16,256]{2,1,0:T(8,128)(2,1)S(1)} %bitcast.73), channel_id=1, source_target_pairs={{8,0},{12,4},{16,8},{20,12},{24,16},{28,20},{9,1},{13,5},{17,9},{2... | collective-permute-start | bytes 393224 | tf_op jit(solution)/shard_map/ppermute | solution.py:142
  24.0 11.1 %collective-permute-start.5 = (bf16[16,16,256]{2,1,0:T(8,128)(2,1)S(1)}, bf16[16,16,256]{2,1,0:T(8,128)(2,1)S(1)}, u32[]{:S(2)}, u32[]{:S(2)}) collective-permute-start(bf16[16,16,256]{2,1,0:T(8,128)(2,1)S(1)} %bitcast.74), channel_id=1, source_target_pairs={{12,0},{16,4},{20,8},{24,12},{28,16},{13,1},{17,5},{21,9},{25,13},... | collective-permute-start | bytes 393224 | tf_op jit(solution)/shard_map/ppermute | solution.py:142
  25.3 25.6 %collective-permute-start.6 = (bf16[16,16,256]{2,1,0:T(8,128)(2,1)S(1)}, bf16[16,16,256]{2,1,0:T(8,128)(2,1)S(1)}, u32[]{:S(2)}, u32[]{:S(2)}) collective-permute-start(bf16[16,16,256]{2,1,0:T(8,128)(2,1)S(1)} %bitcast.75), channel_id=1, source_target_pairs={{16,0},{20,4},{24,8},{28,12},{17,1},{21,5},{25,9},{29,13},{18,2},{... | collective-permute-start | bytes 393224 | tf_op jit(solution)/shard_map/ppermute | solution.py:142
  26.6 26.5 %collective-permute-start.7 = (bf16[16,16,256]{2,1,0:T(8,128)(2,1)S(1)}, bf16[16,16,256]{2,1,0:T(8,128)(2,1)S(1)}, u32[]{:S(2)}, u32[]{:S(2)}) collective-permute-start(bf16[16,16,256]{2,1,0:T(8,128)(2,1)S(1)} %bitcast.76), channel_id=1, source_target_pairs={{20,0},{24,4},{28,8},{21,1},{25,5},{29,9},{22,2},{26,6},{30,10},{2... | collective-permute-start | bytes 393224 | tf_op jit(solution)/shard_map/ppermute | solution.py:142
  29.1 24.0 %collective-permute-start.8 = (bf16[16,16,256]{2,1,0:T(8,128)(2,1)S(1)}, bf16[16,16,256]{2,1,0:T(8,128)(2,1)S(1)}, u32[]{:S(2)}, u32[]{:S(2)}) collective-permute-start(bf16[16,16,256]{2,1,0:T(8,128)(2,1)S(1)} %bitcast.77), channel_id=1, source_target_pairs={{24,0},{28,4},{25,1},{29,5},{26,2},{30,6},{27,3},{31,7}} | collective-permute-start | bytes 393224 | tf_op jit(solution)/shard_map/ppermute | solution.py:142
  33.1 20.1 %collective-permute-start.9 = (bf16[16,16,256]{2,1,0:T(8,128)(2,1)S(1)}, bf16[16,16,256]{2,1,0:T(8,128)(2,1)S(1)}, u32[]{:S(2)}, u32[]{:S(2)}) collective-permute-start(bf16[16,16,256]{2,1,0:T(8,128)(2,1)S(1)} %bitcast.78), channel_id=1, source_target_pairs={{28,0},{29,1},{30,2},{31,3}} | collective-permute-start | bytes 393224 | tf_op jit(solution)/shard_map/ppermute | solution.py:142
  58.2 21.2 %collective-permute-start.11 = (bf16[32,2,16,256]{3,2,1,0:T(8,128)(2,1)}, bf16[32,2,16,256]{3,2,1,0:T(8,128)(2,1)}, u32[]{:S(2)}, u32[]{:S(2)}) collective-permute-start(bf16[32,2,16,256]{3,2,1,0:T(8,128)(2,1)} %convert_element_type.82), channel_id=1, source_target_pairs={{0,2},{1,3},{2,0},{3,1},{4,6},{5,7},{6,4},{7,5},{8,10},{9,11},{10,... | collective-permute-start | bytes 1572872 | tf_op jit(solution)/shard_map/ppermute | solution.py:162
  64.7 16.1 %collective-permute-start.12 = (bf16[32,2,16,256]{3,2,1,0:T(8,128)(2,1)}, bf16[32,2,16,256]{3,2,1,0:T(8,128)(2,1)}, u32[]{:S(2)}, u32[]{:S(2)}) collective-permute-start(bf16[32,2,16,256]{3,2,1,0:T(8,128)(2,1)} %convert_element_type.83), channel_id=1, source_target_pairs={{0,3},{1,0},{2,1},{3,2},{4,7},{5,4},{6,5},{7,6},{8,11},{9,8},{10,9... | collective-permute-start | bytes 1572872 | tf_op jit(solution)/shard_map/ppermute | solution.py:162
  74.5 4.4 %copy-start = (bf16[1,1024,512]{2,1,0:T(8,128)(2,1)S(1)}, bf16[1,1024,512]{2,1,0:T(8,128)(2,1)}, u32[]{:S(2)}) copy-start(bf16[1,1024,512]{2,1,0:T(8,128)(2,1)} %copy.8) | copy-start | bytes 3145732
  74.5 8.8 %collective-permute-start.10 = (bf16[32,2,16,256]{3,2,1,0:T(8,128)(2,1)S(1)}, bf16[32,2,16,256]{3,2,1,0:T(8,128)(2,1)S(1)}, u32[]{:S(2)}, u32[]{:S(2)}) collective-permute-start(bf16[32,2,16,256]{3,2,1,0:T(8,128)(2,1)S(1)} %convert_element_type.79), channel_id=1, source_target_pairs={{0,1},{1,2},{2,3},{3,0},{4,5},{5,6},{6,7},{7,4},{8,9},{9,10},{10,1... | collective-permute-start | bytes 1572872 | tf_op jit(solution)/shard_map/ppermute | solution.py:162

commit v24 on v23

--- a/solution.py
+++ b/solution.py
@@ -40,12 +40,15 @@
 
     def one_offset(i, carry):
         shift = offsets_ref[step * group + i]
+        real_rows, imag_rows = [], []
         for c in range(own_count):
             a = white_ref[base + c].astype(jnp.float32)
             b = white_ref[base + c + shift].astype(jnp.float32)
             ar, ai, br, bi = a[:half], a[half:], b[:half], b[half:]
-            out_ref[i, 0, pl.ds(c, 1), :] = jnp.sum(ar * br + ai * bi, axis=0, keepdims=True)
-            out_ref[i, 1, pl.ds(c, 1), :] = jnp.sum(ai * br - ar * bi, axis=0, keepdims=True)
+            real_rows.append(jnp.sum(ar * br + ai * bi, axis=0, keepdims=True))
+            imag_rows.append(jnp.sum(ai * br - ar * bi, axis=0, keepdims=True))
+        out_ref[i, 0] = jnp.concatenate(real_rows, axis=0).astype(out_ref.dtype)
+        out_ref[i, 1] = jnp.concatenate(imag_rows, axis=0).astype(out_ref.dtype)
         return carry
 
     lax.fori_loop(0, group, one_offset, 0)
@@ -64,7 +67,7 @@
             in_specs=[pl.BlockSpec(white_all.shape, lambda g, offs, b: (0, 0, 0))],
             out_specs=pl.BlockSpec((group, 2, own_count, bins), lambda g, offs, b: (g, 0, 0, 0)),
         ),
-        out_shape=jax.ShapeDtypeStruct((band_span, 2, own_count, bins), jnp.float32),
+        out_shape=jax.ShapeDtypeStruct((band_span, 2, own_count, bins), jnp.bfloat16),
         compiler_params=pltpu.CompilerParams(vmem_limit_bytes=48 * 1024 * 1024),
         cost_estimate=pl.CostEstimate(
             flops=8 * band_span * own_count * rows * bins,

time: 85 us -> 85.1 us (level)
    convert_element_type x3 -> x0, other arithmetic: 1.82 us -> none  [local(): part = cross_spectra(padded, lax.dynamic_slice_in_dim(offsets, dest * off...]
    another operation x2, other arithmetic: 5.69 us -> 6.64 us
  transfers between devices with their start and end apart: 13 -> 13, of which waited for: 7 -> 7; matrix products, arithmetic and copies ran while one was open for 13% -> 16% of each run, Pallas kernels for 14% -> 13%
where the time goes in v24:
time: 85.1 us; the launch traced here: 84.6 us
  waiting for transfers between devices  23.7 us (28%)
  starting transfers between devices  15.8 us (19%)
  Pallas kernels  14.5 us (17%)
  other arithmetic  14.2 us (17%)
  local copies, waits for them, and re-layouts  8.75 us (10%)
  matrix products  7.19 us (8%)
    ppermute x7, waiting for transfers between devices, local(): blocks.append(lax.ppermute(rows_white, 'gx', perm=pairs))  22.4 us
    pallas_call x4, Pallas kernels, cross_spectra(): pl.pallas_call(kernel, grid_spec=pltpu.PrefetchScalarGridSpec(num_scalar_...  14.5 us
    ppermute x7, starting transfers between devices, local(): blocks.append(lax.ppermute(rows_white, 'gx', perm=pairs))  9.2 us
    another operation x2, other arithmetic  6.64 us
    dot_general x4, matrix products, local(): jnp.einsum('opck,pkl->ocl', part, rows, preferred_element_type=jnp.float32)  4.73 us
    ppermute x3, starting transfers between devices, local(): lax.ppermute(piece, 'gy', perm=[(src, (src + shift) % gy_count) for src i...  4.46 us
    dot_general x1, matrix products, forward_spectra(): jnp.dot(record_rows.reshape(row_count * block_count, block_len), small_ta...  2.46 us
    sub x1, local copies, waits for them, and re-layouts, inverse_table(): cos_t = (cos_f * cos_c - sin_f * sin_c).reshape(kept_bins.shape[0], LAGS)  2.29 us
  transfers between devices with their start and end apart: 13, of which 7 were waited for; matrix products, arithmetic and copies ran while one was open for 16% of the time, Pallas kernels for 13%

profile of v24, /device:TPU:0, one launch (start us, length us, event | category | flops | bytes accessed | tf_op | source)
XLA Modules:
  0.0 84.6 jit_solution(7937092425441024613)
XLA Ops:
  0.0 1.2 %fusion.51 = (f32[32,1024]{1,0:T(8,128)S(1)}, f32[32,1024]{1,0:T(8,128)S(1)}) fusion(s32[1024]{0:T(1024)} %param.4), kind=kLoop, calls=%fused_computation.86 | loop fusion | flops 458752 | bytes 266240 | tf_op jit(solution)/shard_map/cos | solution.py:92
  1.2 0.7 add_select_fusion.5
  1.9 1.8 %fusion.40 = (f32[64,1024]{1,0:T(8,128)S(1)}, f32[64,1024]{1,0:T(8,128)S(1)}) fusion(s32[1024]{0:T(1024)} %param.4, s32[64]{0:T(128)S(1)} %iota_multiply_fusion), kind=kLoop, calls=%fused_computation.69 | loop fusion | flops 917504 | bytes 528640 | tf_op jit(solution)/shard_map/cos | solution.py:92
  3.7 1.2 %reshape_reshape.3 = bf16[128,2048]{1,0:T(8,128)(2,1)S(1)} reshape(bf16[16,2,8192]{2,1,0:T(2,128)(2,1)} %param.3) | data formatting | bytes 1048576 | tf_op jit(solution)/shard_map/reshape;reshape | solution.py:105
  4.9 3.7 %subtract_convert_fusion = (bf16[64,32,1024]{2,1,0:T(8,128)(2,1)S(1)}, bf16[64,32,1024]{2,1,0:T(8,128)(2,1)S(1)}) fusion(f32[64,1024]{1,0:T(8,128)S(1)} %get-tuple-element.22, f32[32,1024]{1,0:T(8,128)S(1)} %get-tuple-element.28, f32[64,1024]{1,0:T(8,128)S(1)} %get-tuple-element.21, f32[32,1024]{1,0:T(8,128)S(1)} %get-tuple-element.27), kind=kLoop, calls=%fused_computation.5 | loop fusion | flops 18874368 | bytes 9175040 | tf_op jit(solution)/shard_map/convert.7
  8.5 2.5 %fusion.4 = f32[128,2048]{0,1:T(8,128)S(1)} fusion(bf16[128,2048]{1,0:T(8,128)(2,1)S(1)} %reshape_reshape.3, bf16[2048,1024]{1,0:T(8,128)(2,1)S(1)} %bitcast.70, bf16[2048,1024]{1,0:T(8,128)(2,1)S(1)} %bitcast.69), kind=kOutput, calls=%fused_computation.14 | convolution fusion | flops 1090519040 | bytes 9961472 | tf_op jit(solution)/shard_map/dot_general | solution.py:104
  11.0 0.3 copy.4
  11.3 0.9 %reshape.439 = f32[32,4,2,1024]{3,2,1,0:T(2,128)S(1)} reshape(f32[128,2048]{1,0:T(8,128)S(1)} %copy.4) | data formatting | bytes 2097152 | tf_op jit(solution)/shard_map/reshape | solution.py:108
  12.2 1.2 %fusion.67 = (f32[32,4,1,1024]{3,2,1,0:T(1,128)S(1)}, f32[32,4,1,1024]{3,2,1,0:T(1,128)S(1)}) fusion(f32[32,4,2,1024]{3,2,1,0:T(2,128)S(1)} %reshape.439), kind=kLoop, calls=%fused_computation.125 | loop fusion | bytes 2097152 | tf_op jit(solution)/shard_map/slice | solution.py:115
  13.4 0.2 cosine_round-nearest-even_fusion
  13.6 0.8 fusion.25
  14.3 0.1 multiply_reduce_fusion
  14.5 0.2 concatenate.18
  14.8 0.2 multiply_convert_fusion
  15.1 0.5 collective-permute-start
  15.6 2.6 %collective-permute-start.1 = (bf16[16,2,2,256]{3,2,1,0:T(2,128)(2,1)S(1)}, bf16[16,2,2,256]{3,2,1,0:T(2,128)(2,1)S(1)}, u32[]{:S(2)}, u32[]{:S(2)}) collective-permute-start(bf16[16,2,2,256]{3,2,1,0:T(2,128)(2,1)S(1)} %get-tuple-element.17), channel_id=1, source_target_pairs={{0,2},{1,3},{2,0},{3,1},{4,6},{5,7},{6,4},{7,5},{8,10},{9,11},{10,... | collective-permute-start | bytes 98312 | tf_op jit(solution)/shard_map/ppermute | solution.py:135
  18.2 1.4 %collective-permute-start.2 = (bf16[16,2,2,256]{3,2,1,0:T(2,128)(2,1)S(1)}, bf16[16,2,2,256]{3,2,1,0:T(2,128)(2,1)S(1)}, u32[]{:S(2)}, u32[]{:S(2)}) collective-permute-start(bf16[16,2,2,256]{3,2,1,0:T(2,128)(2,1)S(1)} %get-tuple-element.16), channel_id=1, source_target_pairs={{0,3},{1,0},{2,1},{3,2},{4,7},{5,4},{6,5},{7,6},{8,11},{9,8},{10,9... | collective-permute-start | bytes 98312 | tf_op jit(solution)/shard_map/ppermute | solution.py:135
  19.5 1.2 %fusion.49 = (f32[1024,32]{0,1:T(8,128)S(1)}, f32[1024,32]{0,1:T(8,128)}) fusion(s32[1024]{0:T(1024)S(1)} %copy-done.4), kind=kLoop, calls=%fused_computation.83 | loop fusion | flops 458752 | bytes 266240 | tf_op jit(solution)/shard_map/cos | solution.py:26
  20.8 0.3 collective-permute-done.2
  21.1 0.2 maximum_bitcast_fusion
  21.4 1.3 %collective-permute-start.3 = (bf16[16,16,256]{2,1,0:T(8,128)(2,1)S(1)}, bf16[16,16,256]{2,1,0:T(8,128)(2,1)S(1)}, u32[]{:S(2)}, u32[]{:S(2)}) collective-permute-start(bf16[16,16,256]{2,1,0:T(8,128)(2,1)S(1)} %bitcast.73), channel_id=1, source_target_pairs={{4,0},{8,4},{12,8},{16,12},{20,16},{24,20},{28,24},{5,1},{9,5},{13... | collective-permute-start | bytes 393224 | tf_op jit(solution)/shard_map/ppermute | solution.py:145
  22.7 1.3 %collective-permute-start.4 = (bf16[16,16,256]{2,1,0:T(8,128)(2,1)S(1)}, bf16[16,16,256]{2,1,0:T(8,128)(2,1)S(1)}, u32[]{:S(2)}, u32[]{:S(2)}) collective-permute-start(bf16[16,16,256]{2,1,0:T(8,128)(2,1)S(1)} %bitcast.74), channel_id=1, source_target_pairs={{8,0},{12,4},{16,8},{20,12},{24,16},{28,20},{9,1},{13,5},{17,9},{2... | collective-permute-start | bytes 393224 | tf_op jit(solution)/shard_map/ppermute | solution.py:145
  24.0 1.3 %collective-permute-start.5 = (bf16[16,16,256]{2,1,0:T(8,128)(2,1)S(1)}, bf16[16,16,256]{2,1,0:T(8,128)(2,1)S(1)}, u32[]{:S(2)}, u32[]{:S(2)}) collective-permute-start(bf16[16,16,256]{2,1,0:T(8,128)(2,1)S(1)} %bitcast.75), channel_id=1, source_target_pairs={{12,0},{16,4},{20,8},{24,12},{28,16},{13,1},{17,5},{21,9},{25,13},... | collective-permute-start | bytes 393224 | tf_op jit(solution)/shard_map/ppermute | solution.py:145
  25.3 1.3 %collective-permute-start.6 = (bf16[16,16,256]{2,1,0:T(8,128)(2,1)S(1)}, bf16[16,16,256]{2,1,0:T(8,128)(2,1)S(1)}, u32[]{:S(2)}, u32[]{:S(2)}) collective-permute-start(bf16[16,16,256]{2,1,0:T(8,128)(2,1)S(1)} %bitcast.76), channel_id=1, source_target_pairs={{16,0},{20,4},{24,8},{28,12},{17,1},{21,5},{25,9},{29,13},{18,2},{... | collective-permute-start | bytes 393224 | tf_op jit(solution)/shard_map/ppermute | solution.py:145
  26.6 1.3 %collective-permute-start.7 = (bf16[16,16,256]{2,1,0:T(8,128)(2,1)S(1)}, bf16[16,16,256]{2,1,0:T(8,128)(2,1)S(1)}, u32[]{:S(2)}, u32[]{:S(2)}) collective-permute-start(bf16[16,16,256]{2,1,0:T(8,128)(2,1)S(1)} %bitcast.77), channel_id=1, source_target_pairs={{20,0},{24,4},{28,8},{21,1},{25,5},{29,9},{22,2},{26,6},{30,10},{2... | collective-permute-start | bytes 393224 | tf_op jit(solution)/shard_map/ppermute | solution.py:145
  27.9 1.2 %collective-permute-done.3 = bf16[16,16,256]{2,1,0:T(8,128)(2,1)S(1)} collective-permute-done((bf16[16,16,256]{2,1,0:T(8,128)(2,1)S(1)}, bf16[16,16,256]{2,1,0:T(8,128)(2,1)S(1)}, u32[]{:S(2)}, u32[]{:S(2)}) %collective-permute-start.3) | collective-permute-done | bytes 131104 | tf_op jit(solution)/shard_map/ppermute | solution.py:145
  29.1 1.3 %collective-permute-start.8 = (bf16[16,16,256]{2,1,0:T(8,128)(2,1)S(1)}, bf16[16,16,256]{2,1,0:T(8,128)(2,1)S(1)}, u32[]{:S(2)}, u32[]{:S(2)}) collective-permute-start(bf16[16,16,256]{2,1,0:T(8,128)(2,1)S(1)} %bitcast.78), channel_id=1, source_target_pairs={{24,0},{28,4},{25,1},{29,5},{26,2},{30,6},{27,3},{31,7}} | collective-permute-start | bytes 393224 | tf_op jit(solution)/shard_map/ppermute | solution.py:145
  30.4 2.7 %collective-permute-done.4 = bf16[16,16,256]{2,1,0:T(8,128)(2,1)S(1)} collective-permute-done((bf16[16,16,256]{2,1,0:T(8,128)(2,1)S(1)}, bf16[16,16,256]{2,1,0:T(8,128)(2,1)S(1)}, u32[]{:S(2)}, u32[]{:S(2)}) %collective-permute-start.4) | collective-permute-done | bytes 131104 | tf_op jit(solution)/shard_map/ppermute | solution.py:145
  33.1 1.5 %collective-permute-start.9 = (bf16[16,16,256]{2,1,0:T(8,128)(2,1)S(1)}, bf16[16,16,256]{2,1,0:T(8,128)(2,1)S(1)}, u32[]{:S(2)}, u32[]{:S(2)}) collective-permute-start(bf16[16,16,256]{2,1,0:T(8,128)(2,1)S(1)} %bitcast.79), channel_id=1, source_target_pairs={{28,0},{29,1},{30,2},{31,3}} | collective-permute-start | bytes 393224 | tf_op jit(solution)/shard_map/ppermute | solution.py:145
  34.6 0.5 collective-permute-done.5
  35.1 15.9 %collective-permute-done.6 = bf16[16,16,256]{2,1,0:T(8,128)(2,1)S(1)} collective-permute-done((bf16[16,16,256]{2,1,0:T(8,128)(2,1)S(1)}, bf16[16,16,256]{2,1,0:T(8,128)(2,1)S(1)}, u32[]{:S(2)}, u32[]{:S(2)}) %collective-permute-start.6) | collective-permute-done | bytes 131104 | tf_op jit(solution)/shard_map/ppermute | solution.py:145
  50.9 2.1 %collective-permute-done.7 = bf16[16,16,256]{2,1,0:T(8,128)(2,1)S(1)} collective-permute-done((bf16[16,16,256]{2,1,0:T(8,128)(2,1)S(1)}, bf16[16,16,256]{2,1,0:T(8,128)(2,1)S(1)}, u32[]{:S(2)}, u32[]{:S(2)}) %collective-permute-start.7) | collective-permute-done | bytes 131104 | tf_op jit(solution)/shard_map/ppermute | solution.py:145
  53.2 0.3 convert_element_type.66.white_ref
  53.5 3.6 %shard_map.38 = bf16[32,2,16,256]{3,2,1,0:T(8,128)(2,1)S(1)} custom-call(s32[32]{0:T(128)S(1)} %get-tuple-element.30.offsets_ref, s32[1]{0:T(128)} %constant.111.clone.1.base_ref, f32[144,16,256]{2,1,0:T(8,128)S(1)} %convert_element_type.66.white_ref), custom_call_target="tpu_custom_call" | custom-call | flops 16777216 | bytes 3407872 | tf_op jit(solution)/shard_map/pallas_call | solution.py:62
  57.1 1.6 %collective-permute-start.11 = (bf16[32,2,16,256]{3,2,1,0:T(8,128)(2,1)S(1)}, bf16[32,2,16,256]{3,2,1,0:T(8,128)(2,1)}, u32[]{:S(2)}, u32[]{:S(2)}) collective-permute-start(bf16[32,2,16,256]{3,2,1,0:T(8,128)(2,1)S(1)} %shard_map.38), channel_id=1, source_target_pairs={{0,2},{1,3},{2,0},{3,1},{4,6},{5,7},{6,4},{7,5},{8,10},{9,11},{10,... | collective-permute-start | bytes 1572872 | tf_op jit(solution)/shard_map/ppermute | solution.py:165
  58.7 1.0 %fusion.53 = (f32[1024,16]{0,1:T(8,128)}, f32[1024,16]{0,1:T(8,128)}) fusion(s32[16]{0:T(128)S(1)} %multiply_add_fusion, s32[1024]{0:T(1024)S(1)} %copy-done.4), kind=kLoop, calls=%fused_computation.88 | loop fusion | flops 229376 | bytes 135232 | tf_op jit(solution)/shard_map/cos | solution.py:26
  59.7 3.6 %shard_map.39 = bf16[32,2,16,256]{3,2,1,0:T(8,128)(2,1)S(1)} custom-call(s32[32]{0:T(128)S(1)} %get-tuple-element.32.offsets_ref, s32[1]{0:T(128)} %constant.111.clone.1.base_ref, f32[144,16,256]{2,1,0:T(8,128)S(1)} %convert_element_type.66.white_ref), custom_call_target="tpu_custom_call" | custom-call | flops 16777216 | bytes 3407872 | tf_op jit(solution)/shard_map/pallas_call | solution.py:62
  63.4 3.0 %negate_convert_fusion.1 = (bf16[1024,16,32]{0,2,1:T(8,128)(2,1)}, bf16[1024,16,32]{0,2,1:T(8,128)(2,1)}) fusion(f32[1024,16]{0,1:T(8,128)S(1)} %copy-done.3, f32[1024,32]{0,1:T(8,128)} %get-tuple-element.24, f32[1024,16]{0,1:T(8,128)S(1)} %copy-done.2, f32[1024,32]{0,1:T(8,128)S(1)} %get-tuple-element.23), kind=kLoop, calls=%fused_computation.15 | loop fusion | flops 4718592 | bytes 2490368 | tf_op jit(solution)/shard_map/convert.2
  66.4 2.3 %copy.7 = bf16[1,1024,512]{2,1,0:T(8,128)(2,1)} copy(bf16[1,1024,512]{1,2,0:T(8,128)(2,1)} %bitcast.72) | data formatting | bytes 2097152 | tf_op jit(solution)/shard_map/sub | solution.py:27
  68.7 2.3 %copy.8 = bf16[1,1024,512]{2,1,0:T(8,128)(2,1)} copy(bf16[1,1024,512]{1,2,0:T(8,128)(2,1)} %bitcast.71) | data formatting | bytes 2097152 | tf_op jit(solution)/shard_map/neg | solution.py:29
  71.0 3.6 %shard_map.37 = bf16[32,2,16,256]{3,2,1,0:T(8,128)(2,1)S(1)} custom-call(s32[32]{0:T(128)S(1)} %get-tuple-element.29.offsets_ref, s32[1]{0:T(128)} %constant.111.clone.1.base_ref, f32[144,16,256]{2,1,0:T(8,128)S(1)} %convert_element_type.66.white_ref), custom_call_target="tpu_custom_call" | custom-call | flops 16777216 | bytes 3407872 | tf_op jit(solution)/shard_map/pallas_call | solution.py:62
  74.6 0.5 collective-permute-start.10
  75.1 3.6 %shard_map.40 = bf16[32,2,16,256]{3,2,1,0:T(8,128)(2,1)S(1)} custom-call(s32[32]{0:T(128)S(1)} %get-tuple-element.31.offsets_ref, s32[1]{0:T(128)} %constant.111.clone.1.base_ref, f32[144,16,256]{2,1,0:T(8,128)S(1)} %convert_element_type.66.white_ref), custom_call_target="tpu_custom_call" | custom-call | flops 16777216 | bytes 3407872 | tf_op jit(solution)/shard_map/pallas_call | solution.py:62
  78.8 0.4 convolution_bitcast_fusion
  79.2 1.5 %convolution_bitcast_fusion.2 = f32[32,16,512]{2,1,0:T(8,128)S(1)} fusion(bf16[32,2,16,256]{3,2,1,0:T(8,128)(2,1)} %collective-permute-done.11, s32[]{:T(128)S(6)} %select_n.109, bf16[1,1024,512]{2,1,0:T(8,128)(2,1)S(1)} %copy-done, bf16[1,1024,512]{2,1,0:T(8,128)(2,1)S(1)} %copy-done.1), kind=kOutput, calls=%fused_computation.19 | convolution fusion | flops 269484032 | bytes 3670020 | tf_op jit(solution)/shard_map/opck,pkl->ocl/dot_general | solution.py:168
  80.7 1.5 %convolution_bitcast_fusion.1 = f32[32,16,512]{2,1,0:T(8,128)S(1)} fusion(bf16[32,2,16,256]{3,2,1,0:T(8,128)(2,1)} %collective-permute-done.12, s32[]{:T(128)S(6)} %select_n.108, bf16[1,1024,512]{2,1,0:T(8,128)(2,1)S(1)} %copy-done, bf16[1,1024,512]{2,1,0:T(8,128)(2,1)S(1)} %copy-done.1), kind=kOutput, calls=%fused_computation.18 | convolution fusion | flops 269484032 | bytes 3670020 | tf_op jit(solution)/shard_map/opck,pkl->ocl/dot_general | solution.py:168
  82.2 1.0 %collective-permute-done.10 = bf16[32,2,16,256]{3,2,1,0:T(8,128)(2,1)S(1)} collective-permute-done((bf16[32,2,16,256]{3,2,1,0:T(8,128)(2,1)S(1)}, bf16[32,2,16,256]{3,2,1,0:T(8,128)(2,1)S(1)}, u32[]{:S(2)}, u32[]{:S(2)}) %collective-permute-start.10) | collective-permute-done | bytes 524320 | tf_op jit(solution)/shard_map/ppermute | solution.py:165
  83.3 1.3 %fusion.11 = bf16[32,16,512]{2,1,0:T(8,128)(2,1)} fusion(f32[32,16,512]{2,1,0:T(8,128)S(1)} %convolution_bitcast_fusion, f32[32,16,512]{2,1,0:T(8,128)S(1)} %convolution_bitcast_fusion.1, f32[32,16,512]{2,1,0:T(8,128)S(1)} %convolution_bitcast_fusion.2, bf16[32,2,16,256]{3,2,1,0:T(8,128)(2,1)S(1)} %collective-permute-done.10, s32[]{:T(128)S(6)} %select_n.110, ...), kind=kOutput, calls=%fused_computation.25 | convolution fusion | flops 270794752 | bytes 6291460 | tf_op jit(solution)/shard_map/opck,pkl->ocl/dot_general | solution.py:168
  (35 shorter events, 0.5 us)
Async XLA Ops:
  13.4 6.1 %copy-start.4 = (s32[1024]{0:T(1024)S(1)}, s32[1024]{0:T(1024)}, u32[]{:S(2)}) copy-start(s32[1024]{0:T(1024)} %param.4) | copy-start | bytes 12292
  13.4 7.3 %copy-start.5 = (s32[128]{0:T(128)S(1)}, s32[128]{0:T(128)}, u32[]{:S(2)}) copy-start(s32[128]{0:T(128)} %param.5) | copy-start | bytes 1540
  15.1 5.7 %collective-permute-start = (bf16[16,2,2,256]{3,2,1,0:T(2,128)(2,1)S(1)}, bf16[16,2,2,256]{3,2,1,0:T(2,128)(2,1)S(1)}, u32[]{:S(2)}, u32[]{:S(2)}) collective-permute-start(bf16[16,2,2,256]{3,2,1,0:T(2,128)(2,1)S(1)} %get-tuple-element.18), channel_id=1, source_target_pairs={{0,1},{1,2},{2,3},{3,0},{4,5},{5,6},{6,7},{7,4},{8,9},{9,10},{10,1... | collective-permute-start | bytes 98312 | tf_op jit(solution)/shard_map/ppermute | solution.py:135
  15.6 5.2 %collective-permute-start.1 = (bf16[16,2,2,256]{3,2,1,0:T(2,128)(2,1)S(1)}, bf16[16,2,2,256]{3,2,1,0:T(2,128)(2,1)S(1)}, u32[]{:S(2)}, u32[]{:S(2)}) collective-permute-start(bf16[16,2,2,256]{3,2,1,0:T(2,128)(2,1)S(1)} %get-tuple-element.17), channel_id=1, source_target_pairs={{0,2},{1,3},{2,0},{3,1},{4,6},{5,7},{6,4},{7,5},{8,10},{9,11},{10,... | collective-permute-start | bytes 98312 | tf_op jit(solution)/shard_map/ppermute | solution.py:135
  18.2 3.0 %collective-permute-start.2 = (bf16[16,2,2,256]{3,2,1,0:T(2,128)(2,1)S(1)}, bf16[16,2,2,256]{3,2,1,0:T(2,128)(2,1)S(1)}, u32[]{:S(2)}, u32[]{:S(2)}) collective-permute-start(bf16[16,2,2,256]{3,2,1,0:T(2,128)(2,1)S(1)} %get-tuple-element.16), channel_id=1, source_target_pairs={{0,3},{1,0},{2,1},{3,2},{4,7},{5,4},{6,5},{7,6},{8,11},{9,8},{10,9... | collective-permute-start | bytes 98312 | tf_op jit(solution)/shard_map/ppermute | solution.py:135
  21.4 7.7 %collective-permute-start.3 = (bf16[16,16,256]{2,1,0:T(8,128)(2,1)S(1)}, bf16[16,16,256]{2,1,0:T(8,128)(2,1)S(1)}, u32[]{:S(2)}, u32[]{:S(2)}) collective-permute-start(bf16[16,16,256]{2,1,0:T(8,128)(2,1)S(1)} %bitcast.73), channel_id=1, source_target_pairs={{4,0},{8,4},{12,8},{16,12},{20,16},{24,20},{28,24},{5,1},{9,5},{13... | collective-permute-start | bytes 393224 | tf_op jit(solution)/shard_map/ppermute | solution.py:145
  22.7 10.4 %collective-permute-start.4 = (bf16[16,16,256]{2,1,0:T(8,128)(2,1)S(1)}, bf16[16,16,256]{2,1,0:T(8,128)(2,1)S(1)}, u32[]{:S(2)}, u32[]{:S(2)}) collective-permute-start(bf16[16,16,256]{2,1,0:T(8,128)(2,1)S(1)} %bitcast.74), channel_id=1, source_target_pairs={{8,0},{12,4},{16,8},{20,12},{24,16},{28,20},{9,1},{13,5},{17,9},{2... | collective-permute-start | bytes 393224 | tf_op jit(solution)/shard_map/ppermute | solution.py:145
  24.0 11.1 %collective-permute-start.5 = (bf16[16,16,256]{2,1,0:T(8,128)(2,1)S(1)}, bf16[16,16,256]{2,1,0:T(8,128)(2,1)S(1)}, u32[]{:S(2)}, u32[]{:S(2)}) collective-permute-start(bf16[16,16,256]{2,1,0:T(8,128)(2,1)S(1)} %bitcast.75), channel_id=1, source_target_pairs={{12,0},{16,4},{20,8},{24,12},{28,16},{13,1},{17,5},{21,9},{25,13},... | collective-permute-start | bytes 393224 | tf_op jit(solution)/shard_map/ppermute | solution.py:145
  25.3 25.6 %collective-permute-start.6 = (bf16[16,16,256]{2,1,0:T(8,128)(2,1)S(1)}, bf16[16,16,256]{2,1,0:T(8,128)(2,1)S(1)}, u32[]{:S(2)}, u32[]{:S(2)}) collective-permute-start(bf16[16,16,256]{2,1,0:T(8,128)(2,1)S(1)} %bitcast.76), channel_id=1, source_target_pairs={{16,0},{20,4},{24,8},{28,12},{17,1},{21,5},{25,9},{29,13},{18,2},{... | collective-permute-start | bytes 393224 | tf_op jit(solution)/shard_map/ppermute | solution.py:145
  26.6 26.5 %collective-permute-start.7 = (bf16[16,16,256]{2,1,0:T(8,128)(2,1)S(1)}, bf16[16,16,256]{2,1,0:T(8,128)(2,1)S(1)}, u32[]{:S(2)}, u32[]{:S(2)}) collective-permute-start(bf16[16,16,256]{2,1,0:T(8,128)(2,1)S(1)} %bitcast.77), channel_id=1, source_target_pairs={{20,0},{24,4},{28,8},{21,1},{25,5},{29,9},{22,2},{26,6},{30,10},{2... | collective-permute-start | bytes 393224 | tf_op jit(solution)/shard_map/ppermute | solution.py:145
  29.1 24.0 %collective-permute-start.8 = (bf16[16,16,256]{2,1,0:T(8,128)(2,1)S(1)}, bf16[16,16,256]{2,1,0:T(8,128)(2,1)S(1)}, u32[]{:S(2)}, u32[]{:S(2)}) collective-permute-start(bf16[16,16,256]{2,1,0:T(8,128)(2,1)S(1)} %bitcast.78), channel_id=1, source_target_pairs={{24,0},{28,4},{25,1},{29,5},{26,2},{30,6},{27,3},{31,7}} | collective-permute-start | bytes 393224 | tf_op jit(solution)/shard_map/ppermute | solution.py:145
  33.1 20.1 %collective-permute-start.9 = (bf16[16,16,256]{2,1,0:T(8,128)(2,1)S(1)}, bf16[16,16,256]{2,1,0:T(8,128)(2,1)S(1)}, u32[]{:S(2)}, u32[]{:S(2)}) collective-permute-start(bf16[16,16,256]{2,1,0:T(8,128)(2,1)S(1)} %bitcast.79), channel_id=1, source_target_pairs={{28,0},{29,1},{30,2},{31,3}} | collective-permute-start | bytes 393224 | tf_op jit(solution)/shard_map/ppermute | solution.py:145
  57.1 22.1 %collective-permute-start.11 = (bf16[32,2,16,256]{3,2,1,0:T(8,128)(2,1)S(1)}, bf16[32,2,16,256]{3,2,1,0:T(8,128)(2,1)}, u32[]{:S(2)}, u32[]{:S(2)}) collective-permute-start(bf16[32,2,16,256]{3,2,1,0:T(8,128)(2,1)S(1)} %shard_map.38), channel_id=1, source_target_pairs={{0,2},{1,3},{2,0},{3,1},{4,6},{5,7},{6,4},{7,5},{8,10},{9,11},{10,... | collective-permute-start | bytes 1572872 | tf_op jit(solution)/shard_map/ppermute | solution.py:165
  59.7 3.7 %copy-start.2 = (f32[1024,16]{0,1:T(8,128)S(1)}, f32[1024,16]{0,1:T(8,128)}, u32[]{:S(2)}) copy-start(f32[1024,16]{0,1:T(8,128)} %get-tuple-element.19) | copy-start | bytes 196612
  59.7 3.7 %copy-start.3 = (f32[1024,16]{0,1:T(8,128)S(1)}, f32[1024,16]{0,1:T(8,128)}, u32[]{:S(2)}) copy-start(f32[1024,16]{0,1:T(8,128)} %get-tuple-element.20) | copy-start | bytes 196612
  63.3 17.4 %collective-permute-start.12 = (bf16[32,2,16,256]{3,2,1,0:T(8,128)(2,1)S(1)}, bf16[32,2,16,256]{3,2,1,0:T(8,128)(2,1)}, u32[]{:S(2)}, u32[]{:S(2)}) collective-permute-start(bf16[32,2,16,256]{3,2,1,0:T(8,128)(2,1)S(1)} %shard_map.39), channel_id=1, source_target_pairs={{0,3},{1,0},{2,1},{3,2},{4,7},{5,4},{6,5},{7,6},{8,11},{9,8},{10,9... | collective-permute-start | bytes 1572872 | tf_op jit(solution)/shard_map/ppermute | solution.py:165
  74.6 4.2 %copy-start = (bf16[1,1024,512]{2,1,0:T(8,128)(2,1)S(1)}, bf16[1,1024,512]{2,1,0:T(8,128)(2,1)}, u32[]{:S(2)}) copy-start(bf16[1,1024,512]{2,1,0:T(8,128)(2,1)} %copy.7) | copy-start | bytes 3145732
  74.6 4.2 %copy-start.1 = (bf16[1,1024,512]{2,1,0:T(8,128)(2,1)S(1)}, bf16[1,1024,512]{2,1,0:T(8,128)(2,1)}, u32[]{:S(2)}) copy-start(bf16[1,1024,512]{2,1,0:T(8,128)(2,1)} %copy.8) | copy-start | bytes 3145732
  74.6 8.7 %collective-permute-start.10 = (bf16[32,2,16,256]{3,2,1,0:T(8,128)(2,1)S(1)}, bf16[32,2,16,256]{3,2,1,0:T(8,128)(2,1)S(1)}, u32[]{:S(2)}, u32[]{:S(2)}) collective-permute-start(bf16[32,2,16,256]{3,2,1,0:T(8,128)(2,1)S(1)} %shard_map.37), channel_id=1, source_target_pairs={{0,1},{1,2},{2,3},{3,0},{4,5},{5,6},{6,7},{7,4},{8,9},{9,10},{10,1... | collective-permute-start | bytes 1572872 | tf_op jit(solution)/shard_map/ppermute | solution.py:165

commit v25 on v23

--- a/solution.py
+++ b/solution.py
@@ -152,7 +152,8 @@
     inverse = inverse_table(kept_bins)
     norm_scale = 0.5 / math.sqrt(windows * bin_count)
     lagged = None
-    for shift in list(range(1, gy_count)) + [0]:
+    far_shift = gy_count // 2
+    for shift in [s for s in range(1, gy_count) if s != far_shift] + [far_shift, 0]:
         dest = lax.rem(me + shift, gy_count)
         part = cross_spectra(
             padded, lax.dynamic_slice_in_dim(offsets, dest * off_dev, off_dev), base, ch_dev

time: 85 us -> 85.7 us (level)
  waiting for transfers between devices: 24.2 us -> 25.2 us
    ppermute x3, waiting for transfers between devices: 0.92 us -> 1.86 us  [local(): part = lax.ppermute(part, 'gy', perm=pairs)]
  transfers between devices with their start and end apart: 13 -> 13, of which waited for: 7 -> 7; matrix products, arithmetic and copies ran while one was open for 13% -> 13% of each run, Pallas kernels for 14% -> 13%
where the time goes in v25:
time: 85.7 us; the launch traced here: 85.2 us
  waiting for transfers between devices  25.2 us (29%)
  starting transfers between devices  15.4 us (18%)
  Pallas kernels  15.3 us (18%)
  other arithmetic  13.8 us (16%)
  local copies, waits for them, and re-layouts  7.97 us (9%)
  matrix products  7.12 us (8%)
    ppermute x7, waiting for transfers between devices, local(): blocks.append(lax.ppermute(rows_white, 'gx', perm=pairs))  22.4 us
    pallas_call x4, Pallas kernels, cross_spectra(): pl.pallas_call(kernel, grid_spec=pltpu.PrefetchScalarGridSpec(num_scalar_...  15.3 us
    ppermute x7, starting transfers between devices, local(): blocks.append(lax.ppermute(rows_white, 'gx', perm=pairs))  9.2 us
    another operation x2, other arithmetic  5.69 us
    dot_general x4, matrix products, local(): jnp.einsum('opck,pkl->ocl', part, rows, preferred_element_type=jnp.float32)  4.66 us
    ppermute x3, starting transfers between devices, local(): lax.ppermute(piece, 'gy', perm=[(src, (src + shift) % gy_count) for src i...  4.46 us
    dot_general x1, matrix products, forward_spectra(): jnp.dot(record_rows.reshape(row_count * block_count, block_len), small_ta...  2.46 us
    neg x1, local copies, waits for them, and re-layouts, inverse_table(): return jnp.stack([cos_t, -sin_t], axis=0).astype(jnp.bfloat16)  2.31 us
  transfers between devices with their start and end apart: 13, of which 7 were waited for; matrix products, arithmetic and copies ran while one was open for 13% of the time, Pallas kernels for 13%

profile of v25, /device:TPU:0, one launch (start us, length us, event | category | flops | bytes accessed | tf_op | source)
XLA Modules:
  0.0 85.2 jit_solution(8608608796671971305)
XLA Ops:
  0.0 1.2 %fusion.52 = (f32[32,1024]{1,0:T(8,128)S(1)}, f32[32,1024]{1,0:T(8,128)S(1)}) fusion(s32[1024]{0:T(1024)} %param.4), kind=kLoop, calls=%fused_computation.87 | loop fusion | flops 458752 | bytes 266240 | tf_op jit(solution)/shard_map/cos | solution.py:89
  1.2 0.7 add_select_fusion.5
  1.9 1.8 %fusion.41 = (f32[64,1024]{1,0:T(8,128)S(1)}, f32[64,1024]{1,0:T(8,128)S(1)}) fusion(s32[1024]{0:T(1024)} %param.4, s32[64]{0:T(128)S(1)} %iota_multiply_fusion), kind=kLoop, calls=%fused_computation.70 | loop fusion | flops 917504 | bytes 528640 | tf_op jit(solution)/shard_map/cos | solution.py:89
  3.7 1.2 %reshape_reshape.3 = bf16[128,2048]{1,0:T(8,128)(2,1)S(1)} reshape(bf16[16,2,8192]{2,1,0:T(2,128)(2,1)} %param.3) | data formatting | bytes 1048576 | tf_op jit(solution)/shard_map/reshape;reshape | solution.py:102
  4.9 3.7 %subtract_convert_fusion = (bf16[64,32,1024]{2,1,0:T(8,128)(2,1)S(1)}, bf16[64,32,1024]{2,1,0:T(8,128)(2,1)S(1)}) fusion(f32[64,1024]{1,0:T(8,128)S(1)} %get-tuple-element.20, f32[32,1024]{1,0:T(8,128)S(1)} %get-tuple-element.26, f32[64,1024]{1,0:T(8,128)S(1)} %get-tuple-element.19, f32[32,1024]{1,0:T(8,128)S(1)} %get-tuple-element.25), kind=kLoop, calls=%fused_computation.5 | loop fusion | flops 18874368 | bytes 9175040 | tf_op jit(solution)/shard_map/convert.7
  8.5 2.5 %fusion.4 = f32[128,2048]{0,1:T(8,128)S(1)} fusion(bf16[128,2048]{1,0:T(8,128)(2,1)S(1)} %reshape_reshape.3, bf16[2048,1024]{1,0:T(8,128)(2,1)S(1)} %bitcast.69, bf16[2048,1024]{1,0:T(8,128)(2,1)S(1)} %bitcast.68), kind=kOutput, calls=%fused_computation.14 | convolution fusion | flops 1090519040 | bytes 9961472 | tf_op jit(solution)/shard_map/dot_general | solution.py:101
  11.0 0.3 copy.4
  11.3 0.9 %reshape.439 = f32[32,4,2,1024]{3,2,1,0:T(2,128)S(1)} reshape(f32[128,2048]{1,0:T(8,128)S(1)} %copy.4) | data formatting | bytes 2097152 | tf_op jit(solution)/shard_map/reshape | solution.py:105
  12.2 1.2 %fusion.68 = (f32[32,4,1,1024]{3,2,1,0:T(1,128)S(1)}, f32[32,4,1,1024]{3,2,1,0:T(1,128)S(1)}) fusion(f32[32,4,2,1024]{3,2,1,0:T(2,128)S(1)} %reshape.439), kind=kLoop, calls=%fused_computation.126 | loop fusion | bytes 2097152 | tf_op jit(solution)/shard_map/slice | solution.py:112
  13.6 0.8 fusion.25
  14.5 0.2 concatenate.18
  15.1 0.5 collective-permute-start
  15.6 2.6 %collective-permute-start.1 = (bf16[16,2,2,256]{3,2,1,0:T(2,128)(2,1)S(1)}, bf16[16,2,2,256]{3,2,1,0:T(2,128)(2,1)S(1)}, u32[]{:S(2)}, u32[]{:S(2)}) collective-permute-start(bf16[16,2,2,256]{3,2,1,0:T(2,128)(2,1)S(1)} %get-tuple-element.17), channel_id=1, source_target_pairs={{0,2},{1,3},{2,0},{3,1},{4,6},{5,7},{6,4},{7,5},{8,10},{9,11},{10,... | collective-permute-start | bytes 98312 | tf_op jit(solution)/shard_map/ppermute | solution.py:132
  18.2 1.4 %collective-permute-start.2 = (bf16[16,2,2,256]{3,2,1,0:T(2,128)(2,1)S(1)}, bf16[16,2,2,256]{3,2,1,0:T(2,128)(2,1)S(1)}, u32[]{:S(2)}, u32[]{:S(2)}) collective-permute-start(bf16[16,2,2,256]{3,2,1,0:T(2,128)(2,1)S(1)} %get-tuple-element.16), channel_id=1, source_target_pairs={{0,3},{1,0},{2,1},{3,2},{4,7},{5,4},{6,5},{7,6},{8,11},{9,8},{10,9... | collective-permute-start | bytes 98312 | tf_op jit(solution)/shard_map/ppermute | solution.py:132
  19.5 0.5 fusion.50
  20.2 0.9 %collective-permute-done.2 = bf16[16,2,2,256]{3,2,1,0:T(2,128)(2,1)S(1)} collective-permute-done((bf16[16,2,2,256]{3,2,1,0:T(2,128)(2,1)S(1)}, bf16[16,2,2,256]{3,2,1,0:T(2,128)(2,1)S(1)}, u32[]{:S(2)}, u32[]{:S(2)}) %collective-permute-start.2) | collective-permute-done | bytes 32800 | tf_op jit(solution)/shard_map/ppermute | solution.py:132
  21.1 0.2 maximum_bitcast_fusion
  21.4 1.3 %collective-permute-start.3 = (bf16[16,16,256]{2,1,0:T(8,128)(2,1)S(1)}, bf16[16,16,256]{2,1,0:T(8,128)(2,1)S(1)}, u32[]{:S(2)}, u32[]{:S(2)}) collective-permute-start(bf16[16,16,256]{2,1,0:T(8,128)(2,1)S(1)} %bitcast.72), channel_id=1, source_target_pairs={{4,0},{8,4},{12,8},{16,12},{20,16},{24,20},{28,24},{5,1},{9,5},{13... | collective-permute-start | bytes 393224 | tf_op jit(solution)/shard_map/ppermute | solution.py:142
  22.7 1.3 %collective-permute-start.4 = (bf16[16,16,256]{2,1,0:T(8,128)(2,1)S(1)}, bf16[16,16,256]{2,1,0:T(8,128)(2,1)S(1)}, u32[]{:S(2)}, u32[]{:S(2)}) collective-permute-start(bf16[16,16,256]{2,1,0:T(8,128)(2,1)S(1)} %bitcast.73), channel_id=1, source_target_pairs={{8,0},{12,4},{16,8},{20,12},{24,16},{28,20},{9,1},{13,5},{17,9},{2... | collective-permute-start | bytes 393224 | tf_op jit(solution)/shard_map/ppermute | solution.py:142
  24.0 1.3 %collective-permute-start.5 = (bf16[16,16,256]{2,1,0:T(8,128)(2,1)S(1)}, bf16[16,16,256]{2,1,0:T(8,128)(2,1)S(1)}, u32[]{:S(2)}, u32[]{:S(2)}) collective-permute-start(bf16[16,16,256]{2,1,0:T(8,128)(2,1)S(1)} %bitcast.74), channel_id=1, source_target_pairs={{12,0},{16,4},{20,8},{24,12},{28,16},{13,1},{17,5},{21,9},{25,13},... | collective-permute-start | bytes 393224 | tf_op jit(solution)/shard_map/ppermute | solution.py:142
  25.3 1.3 %collective-permute-start.6 = (bf16[16,16,256]{2,1,0:T(8,128)(2,1)S(1)}, bf16[16,16,256]{2,1,0:T(8,128)(2,1)S(1)}, u32[]{:S(2)}, u32[]{:S(2)}) collective-permute-start(bf16[16,16,256]{2,1,0:T(8,128)(2,1)S(1)} %bitcast.75), channel_id=1, source_target_pairs={{16,0},{20,4},{24,8},{28,12},{17,1},{21,5},{25,9},{29,13},{18,2},{... | collective-permute-start | bytes 393224 | tf_op jit(solution)/shard_map/ppermute | solution.py:142
  26.6 1.3 %collective-permute-start.7 = (bf16[16,16,256]{2,1,0:T(8,128)(2,1)S(1)}, bf16[16,16,256]{2,1,0:T(8,128)(2,1)S(1)}, u32[]{:S(2)}, u32[]{:S(2)}) collective-permute-start(bf16[16,16,256]{2,1,0:T(8,128)(2,1)S(1)} %bitcast.76), channel_id=1, source_target_pairs={{20,0},{24,4},{28,8},{21,1},{25,5},{29,9},{22,2},{26,6},{30,10},{2... | collective-permute-start | bytes 393224 | tf_op jit(solution)/shard_map/ppermute | solution.py:142
  27.9 1.2 %collective-permute-done.3 = bf16[16,16,256]{2,1,0:T(8,128)(2,1)S(1)} collective-permute-done((bf16[16,16,256]{2,1,0:T(8,128)(2,1)S(1)}, bf16[16,16,256]{2,1,0:T(8,128)(2,1)S(1)}, u32[]{:S(2)}, u32[]{:S(2)}) %collective-permute-start.3) | collective-permute-done | bytes 131104 | tf_op jit(solution)/shard_map/ppermute | solution.py:142
  29.1 1.3 %collective-permute-start.8 = (bf16[16,16,256]{2,1,0:T(8,128)(2,1)S(1)}, bf16[16,16,256]{2,1,0:T(8,128)(2,1)S(1)}, u32[]{:S(2)}, u32[]{:S(2)}) collective-permute-start(bf16[16,16,256]{2,1,0:T(8,128)(2,1)S(1)} %bitcast.77), channel_id=1, source_target_pairs={{24,0},{28,4},{25,1},{29,5},{26,2},{30,6},{27,3},{31,7}} | collective-permute-start | bytes 393224 | tf_op jit(solution)/shard_map/ppermute | solution.py:142
  30.4 2.7 %collective-permute-done.4 = bf16[16,16,256]{2,1,0:T(8,128)(2,1)S(1)} collective-permute-done((bf16[16,16,256]{2,1,0:T(8,128)(2,1)S(1)}, bf16[16,16,256]{2,1,0:T(8,128)(2,1)S(1)}, u32[]{:S(2)}, u32[]{:S(2)}) %collective-permute-start.4) | collective-permute-done | bytes 131104 | tf_op jit(solution)/shard_map/ppermute | solution.py:142
  33.1 1.5 %collective-permute-start.9 = (bf16[16,16,256]{2,1,0:T(8,128)(2,1)S(1)}, bf16[16,16,256]{2,1,0:T(8,128)(2,1)S(1)}, u32[]{:S(2)}, u32[]{:S(2)}) collective-permute-start(bf16[16,16,256]{2,1,0:T(8,128)(2,1)S(1)} %bitcast.78), channel_id=1, source_target_pairs={{28,0},{29,1},{30,2},{31,3}} | collective-permute-start | bytes 393224 | tf_op jit(solution)/shard_map/ppermute | solution.py:142
  34.6 0.5 collective-permute-done.5
  35.1 15.9 %collective-permute-done.6 = bf16[16,16,256]{2,1,0:T(8,128)(2,1)S(1)} collective-permute-done((bf16[16,16,256]{2,1,0:T(8,128)(2,1)S(1)}, bf16[16,16,256]{2,1,0:T(8,128)(2,1)S(1)}, u32[]{:S(2)}, u32[]{:S(2)}) %collective-permute-start.6) | collective-permute-done | bytes 131104 | tf_op jit(solution)/shard_map/ppermute | solution.py:142
  50.9 2.1 %collective-permute-done.7 = bf16[16,16,256]{2,1,0:T(8,128)(2,1)S(1)} collective-permute-done((bf16[16,16,256]{2,1,0:T(8,128)(2,1)S(1)}, bf16[16,16,256]{2,1,0:T(8,128)(2,1)S(1)}, u32[]{:S(2)}, u32[]{:S(2)}) %collective-permute-start.7) | collective-permute-done | bytes 131104 | tf_op jit(solution)/shard_map/ppermute | solution.py:142
  53.2 0.3 convert_element_type.78.white_ref
  53.5 3.8 %shard_map.38 = f32[32,2,16,256]{3,2,1,0:T(8,128)S(1)} custom-call(s32[32]{0:T(128)S(1)} %get-tuple-element.30.offsets_ref, s32[1]{0:T(128)} %constant.111.clone.1.base_ref, f32[144,16,256]{2,1,0:T(8,128)S(1)} %convert_element_type.78.white_ref), custom_call_target="tpu_custom_call" | custom-call | flops 16777216 | bytes 3407872 | tf_op jit(solution)/shard_map/pallas_call | solution.py:59
  57.3 0.9 %convert_element_type.82 = bf16[32,2,16,256]{3,2,1,0:T(8,128)(2,1)} convert(f32[32,2,16,256]{3,2,1,0:T(8,128)S(1)} %shard_map.38) | non-fusion elementwise | flops 262144 | bytes 1572864 | tf_op jit(solution)/shard_map/convert_element_type | solution.py:160
  58.2 1.1 %collective-permute-start.11 = (bf16[32,2,16,256]{3,2,1,0:T(8,128)(2,1)}, bf16[32,2,16,256]{3,2,1,0:T(8,128)(2,1)}, u32[]{:S(2)}, u32[]{:S(2)}) collective-permute-start(bf16[32,2,16,256]{3,2,1,0:T(8,128)(2,1)} %convert_element_type.82), channel_id=1, source_target_pairs={{0,3},{1,0},{2,1},{3,2},{4,7},{5,4},{6,5},{7,6},{8,11},{9,8},{10,9... | collective-permute-start | bytes 1572872 | tf_op jit(solution)/shard_map/ppermute | solution.py:163
  59.3 0.3 fusion.54
  59.7 3.8 %shard_map.39 = f32[32,2,16,256]{3,2,1,0:T(8,128)S(1)} custom-call(s32[32]{0:T(128)S(1)} %get-tuple-element.32.offsets_ref, s32[1]{0:T(128)} %constant.111.clone.1.base_ref, f32[144,16,256]{2,1,0:T(8,128)S(1)} %convert_element_type.78.white_ref), custom_call_target="tpu_custom_call" | custom-call | flops 16777216 | bytes 3407872 | tf_op jit(solution)/shard_map/pallas_call | solution.py:59
  63.5 0.9 %convert_element_type.83 = bf16[32,2,16,256]{3,2,1,0:T(8,128)(2,1)} convert(f32[32,2,16,256]{3,2,1,0:T(8,128)S(1)} %shard_map.39) | non-fusion elementwise | flops 262144 | bytes 1572864 | tf_op jit(solution)/shard_map/convert_element_type | solution.py:160
  64.4 0.4 collective-permute-start.12
  64.8 2.0 %negate_convert_fusion.1 = (bf16[1024,16,32]{0,2,1:T(8,128)(2,1)}, bf16[1024,16,32]{0,2,1:T(8,128)(2,1)}) fusion(f32[1024,16]{0,1:T(8,128)S(1)} %get-tuple-element.22, f32[1024,32]{0,1:T(8,128)S(1)} %get-tuple-element.28, f32[1024,16]{0,1:T(8,128)S(1)} %get-tuple-element.21, f32[1024,32]{0,1:T(8,128)S(1)} %get-tuple-element.27), kind=kLoop, calls=%fused_computation.15 | loop fusion | flops 4718592 | bytes 2490368 | tf_op jit(solution)/shard_map/convert.2
  66.8 1.5 %copy.7 = bf16[1,1024,512]{2,1,0:T(8,128)(2,1)S(1)} copy(bf16[1,1024,512]{1,2,0:T(8,128)(2,1)} %bitcast.71) | data formatting | bytes 2097152 | tf_op jit(solution)/shard_map/sub | solution.py:27
  68.3 2.3 %copy.8 = bf16[1,1024,512]{2,1,0:T(8,128)(2,1)} copy(bf16[1,1024,512]{1,2,0:T(8,128)(2,1)} %bitcast.70) | data formatting | bytes 2097152 | tf_op jit(solution)/shard_map/neg | solution.py:29
  70.6 3.8 %shard_map.37 = f32[32,2,16,256]{3,2,1,0:T(8,128)S(1)} custom-call(s32[32]{0:T(128)S(1)} %get-tuple-element.29.offsets_ref, s32[1]{0:T(128)} %constant.111.clone.1.base_ref, f32[144,16,256]{2,1,0:T(8,128)S(1)} %convert_element_type.78.white_ref), custom_call_target="tpu_custom_call" | custom-call | flops 16777216 | bytes 3407872 | tf_op jit(solution)/shard_map/pallas_call | solution.py:59
  74.5 0.3 collective-permute-start.10
  74.8 3.8 %shard_map.40 = f32[32,2,16,256]{3,2,1,0:T(8,128)S(1)} custom-call(s32[32]{0:T(128)S(1)} %get-tuple-element.31.offsets_ref, s32[1]{0:T(128)} %constant.111.clone.1.base_ref, f32[144,16,256]{2,1,0:T(8,128)S(1)} %convert_element_type.78.white_ref), custom_call_target="tpu_custom_call" | custom-call | flops 16777216 | bytes 3407872 | tf_op jit(solution)/shard_map/pallas_call | solution.py:59
  78.6 0.4 convolution_bitcast_fusion
  79.1 1.5 %convolution_bitcast_fusion.2 = f32[32,16,512]{2,1,0:T(8,128)S(1)} fusion(bf16[32,2,16,256]{3,2,1,0:T(8,128)(2,1)} %collective-permute-done.11, s32[]{:T(128)S(6)} %select_n.108, bf16[1,1024,512]{2,1,0:T(8,128)(2,1)S(1)} %copy.7, bf16[1,1024,512]{2,1,0:T(8,128)(2,1)S(1)} %copy-done), kind=kOutput, calls=%fused_computation.19 | convolution fusion | flops 269484032 | bytes 3670020 | tf_op jit(solution)/shard_map/opck,pkl->ocl/dot_general | solution.py:166
  80.6 1.5 %convolution_bitcast_fusion.1 = f32[32,16,512]{2,1,0:T(8,128)S(1)} fusion(bf16[32,2,16,256]{3,2,1,0:T(8,128)(2,1)} %collective-permute-done.12, s32[]{:T(128)S(6)} %select_n.109, bf16[1,1024,512]{2,1,0:T(8,128)(2,1)S(1)} %copy.7, bf16[1,1024,512]{2,1,0:T(8,128)(2,1)S(1)} %copy-done), kind=kOutput, calls=%fused_computation.18 | convolution fusion | flops 269484032 | bytes 3670020 | tf_op jit(solution)/shard_map/opck,pkl->ocl/dot_general | solution.py:166
  82.1 1.9 %collective-permute-done.10 = bf16[32,2,16,256]{3,2,1,0:T(8,128)(2,1)S(1)} collective-permute-done((bf16[32,2,16,256]{3,2,1,0:T(8,128)(2,1)S(1)}, bf16[32,2,16,256]{3,2,1,0:T(8,128)(2,1)S(1)}, u32[]{:S(2)}, u32[]{:S(2)}) %collective-permute-start.10) | collective-permute-done | bytes 524320 | tf_op jit(solution)/shard_map/ppermute | solution.py:163
  83.9 1.3 %fusion.11 = bf16[32,16,512]{2,1,0:T(8,128)(2,1)} fusion(f32[32,16,512]{2,1,0:T(8,128)S(1)} %convolution_bitcast_fusion, f32[32,16,512]{2,1,0:T(8,128)S(1)} %convolution_bitcast_fusion.1, f32[32,16,512]{2,1,0:T(8,128)S(1)} %convolution_bitcast_fusion.2, bf16[32,2,16,256]{3,2,1,0:T(8,128)(2,1)S(1)} %collective-permute-done.10, s32[]{:T(128)S(6)} %select_n.110, ...), kind=kOutput, calls=%fused_computation.25 | convolution fusion | flops 270794752 | bytes 6291460 | tf_op jit(solution)/shard_map/opck,pkl->ocl/dot_general | solution.py:166
  (32 shorter events, 1.0 us)
Async XLA Ops:
  13.4 6.1 %copy-start.1 = (s32[1024]{0:T(1024)S(1)}, s32[1024]{0:T(1024)}, u32[]{:S(2)}) copy-start(s32[1024]{0:T(1024)} %param.4) | copy-start | bytes 12292
  13.4 6.7 %copy-start.2 = (s32[128]{0:T(128)S(1)}, s32[128]{0:T(128)}, u32[]{:S(2)}) copy-start(s32[128]{0:T(128)} %param.5) | copy-start | bytes 1540
  15.1 5.1 %collective-permute-start = (bf16[16,2,2,256]{3,2,1,0:T(2,128)(2,1)S(1)}, bf16[16,2,2,256]{3,2,1,0:T(2,128)(2,1)S(1)}, u32[]{:S(2)}, u32[]{:S(2)}) collective-permute-start(bf16[16,2,2,256]{3,2,1,0:T(2,128)(2,1)S(1)} %get-tuple-element.18), channel_id=1, source_target_pairs={{0,1},{1,2},{2,3},{3,0},{4,5},{5,6},{6,7},{7,4},{8,9},{9,10},{10,1... | collective-permute-start | bytes 98312 | tf_op jit(solution)/shard_map/ppermute | solution.py:132
  15.6 4.6 %collective-permute-start.1 = (bf16[16,2,2,256]{3,2,1,0:T(2,128)(2,1)S(1)}, bf16[16,2,2,256]{3,2,1,0:T(2,128)(2,1)S(1)}, u32[]{:S(2)}, u32[]{:S(2)}) collective-permute-start(bf16[16,2,2,256]{3,2,1,0:T(2,128)(2,1)S(1)} %get-tuple-element.17), channel_id=1, source_target_pairs={{0,2},{1,3},{2,0},{3,1},{4,6},{5,7},{6,4},{7,5},{8,10},{9,11},{10,... | collective-permute-start | bytes 98312 | tf_op jit(solution)/shard_map/ppermute | solution.py:132
  18.2 3.0 %collective-permute-start.2 = (bf16[16,2,2,256]{3,2,1,0:T(2,128)(2,1)S(1)}, bf16[16,2,2,256]{3,2,1,0:T(2,128)(2,1)S(1)}, u32[]{:S(2)}, u32[]{:S(2)}) collective-permute-start(bf16[16,2,2,256]{3,2,1,0:T(2,128)(2,1)S(1)} %get-tuple-element.16), channel_id=1, source_target_pairs={{0,3},{1,0},{2,1},{3,2},{4,7},{5,4},{6,5},{7,6},{8,11},{9,8},{10,9... | collective-permute-start | bytes 98312 | tf_op jit(solution)/shard_map/ppermute | solution.py:132
  21.4 7.7 %collective-permute-start.3 = (bf16[16,16,256]{2,1,0:T(8,128)(2,1)S(1)}, bf16[16,16,256]{2,1,0:T(8,128)(2,1)S(1)}, u32[]{:S(2)}, u32[]{:S(2)}) collective-permute-start(bf16[16,16,256]{2,1,0:T(8,128)(2,1)S(1)} %bitcast.72), channel_id=1, source_target_pairs={{4,0},{8,4},{12,8},{16,12},{20,16},{24,20},{28,24},{5,1},{9,5},{13... | collective-permute-start | bytes 393224 | tf_op jit(solution)/shard_map/ppermute | solution.py:142
  22.7 10.4 %collective-permute-start.4 = (bf16[16,16,256]{2,1,0:T(8,128)(2,1)S(1)}, bf16[16,16,256]{2,1,0:T(8,128)(2,1)S(1)}, u32[]{:S(2)}, u32[]{:S(2)}) collective-permute-start(bf16[16,16,256]{2,1,0:T(8,128)(2,1)S(1)} %bitcast.73), channel_id=1, source_target_pairs={{8,0},{12,4},{16,8},{20,12},{24,16},{28,20},{9,1},{13,5},{17,9},{2... | collective-permute-start | bytes 393224 | tf_op jit(solution)/shard_map/ppermute | solution.py:142
  24.0 11.1 %collective-permute-start.5 = (bf16[16,16,256]{2,1,0:T(8,128)(2,1)S(1)}, bf16[16,16,256]{2,1,0:T(8,128)(2,1)S(1)}, u32[]{:S(2)}, u32[]{:S(2)}) collective-permute-start(bf16[16,16,256]{2,1,0:T(8,128)(2,1)S(1)} %bitcast.74), channel_id=1, source_target_pairs={{12,0},{16,4},{20,8},{24,12},{28,16},{13,1},{17,5},{21,9},{25,13},... | collective-permute-start | bytes 393224 | tf_op jit(solution)/shard_map/ppermute | solution.py:142
  25.3 25.6 %collective-permute-start.6 = (bf16[16,16,256]{2,1,0:T(8,128)(2,1)S(1)}, bf16[16,16,256]{2,1,0:T(8,128)(2,1)S(1)}, u32[]{:S(2)}, u32[]{:S(2)}) collective-permute-start(bf16[16,16,256]{2,1,0:T(8,128)(2,1)S(1)} %bitcast.75), channel_id=1, source_target_pairs={{16,0},{20,4},{24,8},{28,12},{17,1},{21,5},{25,9},{29,13},{18,2},{... | collective-permute-start | bytes 393224 | tf_op jit(solution)/shard_map/ppermute | solution.py:142
  26.6 26.5 %collective-permute-start.7 = (bf16[16,16,256]{2,1,0:T(8,128)(2,1)S(1)}, bf16[16,16,256]{2,1,0:T(8,128)(2,1)S(1)}, u32[]{:S(2)}, u32[]{:S(2)}) collective-permute-start(bf16[16,16,256]{2,1,0:T(8,128)(2,1)S(1)} %bitcast.76), channel_id=1, source_target_pairs={{20,0},{24,4},{28,8},{21,1},{25,5},{29,9},{22,2},{26,6},{30,10},{2... | collective-permute-start | bytes 393224 | tf_op jit(solution)/shard_map/ppermute | solution.py:142
  29.1 24.0 %collective-permute-start.8 = (bf16[16,16,256]{2,1,0:T(8,128)(2,1)S(1)}, bf16[16,16,256]{2,1,0:T(8,128)(2,1)S(1)}, u32[]{:S(2)}, u32[]{:S(2)}) collective-permute-start(bf16[16,16,256]{2,1,0:T(8,128)(2,1)S(1)} %bitcast.77), channel_id=1, source_target_pairs={{24,0},{28,4},{25,1},{29,5},{26,2},{30,6},{27,3},{31,7}} | collective-permute-start | bytes 393224 | tf_op jit(solution)/shard_map/ppermute | solution.py:142
  33.1 20.1 %collective-permute-start.9 = (bf16[16,16,256]{2,1,0:T(8,128)(2,1)S(1)}, bf16[16,16,256]{2,1,0:T(8,128)(2,1)S(1)}, u32[]{:S(2)}, u32[]{:S(2)}) collective-permute-start(bf16[16,16,256]{2,1,0:T(8,128)(2,1)S(1)} %bitcast.78), channel_id=1, source_target_pairs={{28,0},{29,1},{30,2},{31,3}} | collective-permute-start | bytes 393224 | tf_op jit(solution)/shard_map/ppermute | solution.py:142
  58.2 20.9 %collective-permute-start.11 = (bf16[32,2,16,256]{3,2,1,0:T(8,128)(2,1)}, bf16[32,2,16,256]{3,2,1,0:T(8,128)(2,1)}, u32[]{:S(2)}, u32[]{:S(2)}) collective-permute-start(bf16[32,2,16,256]{3,2,1,0:T(8,128)(2,1)} %convert_element_type.82), channel_id=1, source_target_pairs={{0,3},{1,0},{2,1},{3,2},{4,7},{5,4},{6,5},{7,6},{8,11},{9,8},{10,9... | collective-permute-start | bytes 1572872 | tf_op jit(solution)/shard_map/ppermute | solution.py:163
  64.4 16.2 %collective-permute-start.12 = (bf16[32,2,16,256]{3,2,1,0:T(8,128)(2,1)}, bf16[32,2,16,256]{3,2,1,0:T(8,128)(2,1)}, u32[]{:S(2)}, u32[]{:S(2)}) collective-permute-start(bf16[32,2,16,256]{3,2,1,0:T(8,128)(2,1)} %convert_element_type.83), channel_id=1, source_target_pairs={{0,2},{1,3},{2,0},{3,1},{4,6},{5,7},{6,4},{7,5},{8,10},{9,11},{10,... | collective-permute-start | bytes 1572872 | tf_op jit(solution)/shard_map/ppermute | solution.py:163
  74.5 4.1 %copy-start = (bf16[1,1024,512]{2,1,0:T(8,128)(2,1)S(1)}, bf16[1,1024,512]{2,1,0:T(8,128)(2,1)}, u32[]{:S(2)}) copy-start(bf16[1,1024,512]{2,1,0:T(8,128)(2,1)} %copy.8) | copy-start | bytes 3145732
  74.5 9.4 %collective-permute-start.10 = (bf16[32,2,16,256]{3,2,1,0:T(8,128)(2,1)S(1)}, bf16[32,2,16,256]{3,2,1,0:T(8,128)(2,1)S(1)}, u32[]{:S(2)}, u32[]{:S(2)}) collective-permute-start(bf16[32,2,16,256]{3,2,1,0:T(8,128)(2,1)S(1)} %convert_element_type.79), channel_id=1, source_target_pairs={{0,1},{1,2},{2,3},{3,0},{4,5},{5,6},{6,7},{7,4},{8,9},{9,10},{10,1... | collective-permute-start | bytes 1572872 | tf_op jit(solution)/shard_map/ppermute | solution.py:163

commit v26 on v23

--- a/solution.py
+++ b/solution.py
@@ -149,7 +149,7 @@
     off_dev = band_span // gy_count
     me = lax.axis_index("gy")
     offsets = pair_offsets.astype(jnp.int32)
-    inverse = inverse_table(kept_bins)
+    inverse = jnp.transpose(inverse_table(kept_bins).reshape(2, gy_count, shard_bins, LAGS), (1, 0, 2, 3))
     norm_scale = 0.5 / math.sqrt(windows * bin_count)
     lagged = None
     for shift in list(range(1, gy_count)) + [0]:
@@ -161,7 +161,7 @@
             pairs = [(src, (src + shift) % gy_count) for src in range(gy_count)]
             part = lax.ppermute(part, "gy", perm=pairs)
         origin = lax.rem(me + gy_count - shift, gy_count)
-        rows = lax.dynamic_slice_in_dim(inverse, origin * shard_bins, shard_bins, 1)
+        rows = lax.dynamic_index_in_dim(inverse, origin, 0, keepdims=False)
         term = jnp.einsum("opck,pkl->ocl", part, rows, preferred_element_type=jnp.float32)
         lagged = term if lagged is None else lagged + term
     lagged = lagged * norm_scale

time: 85 us -> 105 us (1.24)
  local copies, waits for them, and re-layouts: 7.97 us -> 31.5 us
  waiting for transfers between devices: 24.2 us -> 22 us
  starting transfers between devices: 15.7 us -> 14.5 us
    another operation x0 -> x6, local copies, waits for them, and re-layouts: none -> 23.2 us
    unnamed x14 -> x21, local copies, waits for them, and re-layouts: 0.11 us -> 2.04 us
    neg x1, local copies, waits for them, and re-layouts: 2.31 us -> 0.78 us  [inverse_table(): return jnp.stack([cos_t, -sin_t], axis=0).astype(jnp.bfloat16)]
    another operation x2, other arithmetic: 5.69 us -> 4.41 us
  transfers between devices with their start and end apart: 13 -> 13, of which waited for: 7 -> 6; matrix products, arithmetic and copies ran while one was open for 13% -> 31% of each run, Pallas kernels for 14% -> 11%
where the time goes in v26:
time: 105 us; the launch traced here: 104 us
  local copies, waits for them, and re-layouts  31.5 us (30%)
  waiting for transfers between devices  22 us (21%)
  Pallas kernels  15.3 us (15%)
  starting transfers between devices  14.5 us (14%)
  other arithmetic  13.3 us (13%)
  matrix products  7.1 us (7%)
    another operation x5, local copies, waits for them, and re-layouts  21.9 us
    ppermute x7, waiting for transfers between devices, local(): blocks.append(lax.ppermute(rows_white, 'gx', perm=pairs))  21.8 us
    pallas_call x4, Pallas kernels, cross_spectra(): pl.pallas_call(kernel, grid_spec=pltpu.PrefetchScalarGridSpec(num_scalar_...  15.3 us
    ppermute x7, starting transfers between devices, local(): blocks.append(lax.ppermute(rows_white, 'gx', perm=pairs))  9.02 us
    dot_general x4, matrix products, local(): jnp.einsum('opck,pkl->ocl', part, rows, preferred_element_type=jnp.float32)  4.64 us
    another operation x2, other arithmetic  4.41 us
    ppermute x3, starting transfers between devices, local(): lax.ppermute(piece, 'gy', perm=[(src, (src + shift) % gy_count) for src i...  4.4 us
    dot_general x1, matrix products, forward_spectra(): jnp.dot(record_rows.reshape(row_count * block_count, block_len), small_ta...  2.46 us
  transfers between devices with their start and end apart: 13, of which 6 were waited for; matrix products, arithmetic and copies ran while one was open for 31% of the time, Pallas kernels for 11%

profile of v26, /device:TPU:0, one launch (start us, length us, event | category | flops | bytes accessed | tf_op | source)
XLA Modules:
  0.0 104.2 jit_solution(2399241036675756145)
XLA Ops:
  0.0 1.2 %fusion.44 = (f32[32,1024]{1,0:T(8,128)S(1)}, f32[32,1024]{1,0:T(8,128)S(1)}) fusion(s32[1024]{0:T(1024)} %param.4), kind=kLoop, calls=%fused_computation.75 | loop fusion | flops 458752 | bytes 266240 | tf_op jit(solution)/shard_map/cos | solution.py:89
  1.2 0.7 add_select_fusion.5
  1.9 1.8 %fusion.33 = (f32[64,1024]{1,0:T(8,128)S(1)}, f32[64,1024]{1,0:T(8,128)S(1)}) fusion(s32[1024]{0:T(1024)} %param.4, s32[64]{0:T(128)S(1)} %iota_multiply_fusion), kind=kLoop, calls=%fused_computation.58 | loop fusion | flops 917504 | bytes 528640 | tf_op jit(solution)/shard_map/cos | solution.py:89
  3.7 1.2 %reshape_reshape.3 = bf16[128,2048]{1,0:T(8,128)(2,1)S(1)} reshape(bf16[16,2,8192]{2,1,0:T(2,128)(2,1)} %param.3) | data formatting | bytes 1048576 | tf_op jit(solution)/shard_map/reshape;reshape | solution.py:102
  4.9 3.7 %subtract_convert_fusion = (bf16[64,32,1024]{2,1,0:T(8,128)(2,1)S(1)}, bf16[64,32,1024]{2,1,0:T(8,128)(2,1)S(1)}) fusion(f32[64,1024]{1,0:T(8,128)S(1)} %get-tuple-element.24, f32[32,1024]{1,0:T(8,128)S(1)} %get-tuple-element.30, f32[64,1024]{1,0:T(8,128)S(1)} %get-tuple-element.23, f32[32,1024]{1,0:T(8,128)S(1)} %get-tuple-element.29), kind=kLoop, calls=%fused_computation.5 | loop fusion | flops 18874368 | bytes 9175040 | tf_op jit(solution)/shard_map/convert.7
  8.5 2.5 %fusion.4 = f32[128,2048]{0,1:T(8,128)S(1)} fusion(bf16[128,2048]{1,0:T(8,128)(2,1)S(1)} %reshape_reshape.3, bf16[2048,1024]{1,0:T(8,128)(2,1)S(1)} %bitcast.75, bf16[2048,1024]{1,0:T(8,128)(2,1)S(1)} %bitcast.74), kind=kOutput, calls=%fused_computation.6 | convolution fusion | flops 1090519040 | bytes 9961472 | tf_op jit(solution)/shard_map/dot_general | solution.py:101
  11.3 0.9 reshape.458
  12.2 1.2 %fusion.52 = (f32[32,4,1,1024]{3,2,1,0:T(1,128)S(1)}, f32[32,4,1,1024]{3,2,1,0:T(1,128)S(1)}) fusion(f32[32,4,2,1024]{3,2,1,0:T(2,128)S(1)} %reshape.458), kind=kLoop, calls=%fused_computation.112 | loop fusion | bytes 2097152 | tf_op jit(solution)/shard_map/slice | solution.py:112
  13.6 0.8 fusion.13
  15.0 0.7 constant_dynamic-slice_fusion.7
  15.7 0.5 collective-permute-start
  16.1 2.5 %collective-permute-start.1 = (bf16[16,2,2,256]{3,2,1,0:T(2,128)(2,1)S(1)}, bf16[16,2,2,256]{3,2,1,0:T(2,128)(2,1)}, u32[]{:S(2)}, u32[]{:S(2)}) collective-permute-start(bf16[16,2,2,256]{3,2,1,0:T(2,128)(2,1)S(1)} %get-tuple-element.21), channel_id=1, source_target_pairs={{0,2},{1,3},{2,0},{3,1},{4,6},{5,7},{6,4},{7,5},{8,10},{9,11},{10,... | collective-permute-start | bytes 98312 | tf_op jit(solution)/shard_map/ppermute | solution.py:132
  18.7 1.4 %collective-permute-start.2 = (bf16[16,2,2,256]{3,2,1,0:T(2,128)(2,1)S(1)}, bf16[16,2,2,256]{3,2,1,0:T(2,128)(2,1)}, u32[]{:S(2)}, u32[]{:S(2)}) collective-permute-start(bf16[16,2,2,256]{3,2,1,0:T(2,128)(2,1)S(1)} %get-tuple-element.20), channel_id=1, source_target_pairs={{0,3},{1,0},{2,1},{3,2},{4,7},{5,4},{6,5},{7,6},{8,11},{9,8},{10,9... | collective-permute-start | bytes 98312 | tf_op jit(solution)/shard_map/ppermute | solution.py:132
  20.1 0.5 fusion.42
  21.0 0.7 negate_convert_fusion.1
  21.7 0.8 sub.35
  22.5 1.4 %constant_dynamic-update-slice_fusion.9 = bf16[2,4,256,512]{2,1,3,0:T(4,128)(2,1)} fusion(bf16[1,4,256,512]{2,1,3,0:T(4,128)(2,1)S(1)} %sub.35), kind=kLoop, calls=%fused_computation.90 | loop fusion | bytes 2097152
  24.0 0.8 neg.32
  24.8 1.0 maximum_bitcast_fusion
  25.8 1.3 %collective-permute-start.3 = (bf16[16,16,256]{2,1,0:T(8,128)(2,1)S(1)}, bf16[16,16,256]{2,1,0:T(8,128)(2,1)S(1)}, u32[]{:S(2)}, u32[]{:S(2)}) collective-permute-start(bf16[16,16,256]{2,1,0:T(8,128)(2,1)S(1)} %bitcast.76), channel_id=1, source_target_pairs={{4,0},{8,4},{12,8},{16,12},{20,16},{24,20},{28,24},{5,1},{9,5},{13... | collective-permute-start | bytes 393224 | tf_op jit(solution)/shard_map/ppermute | solution.py:142
  27.1 1.3 %collective-permute-start.4 = (bf16[16,16,256]{2,1,0:T(8,128)(2,1)S(1)}, bf16[16,16,256]{2,1,0:T(8,128)(2,1)S(1)}, u32[]{:S(2)}, u32[]{:S(2)}) collective-permute-start(bf16[16,16,256]{2,1,0:T(8,128)(2,1)S(1)} %bitcast.77), channel_id=1, source_target_pairs={{8,0},{12,4},{16,8},{20,12},{24,16},{28,20},{9,1},{13,5},{17,9},{2... | collective-permute-start | bytes 393224 | tf_op jit(solution)/shard_map/ppermute | solution.py:142
  28.4 1.3 %collective-permute-start.5 = (bf16[16,16,256]{2,1,0:T(8,128)(2,1)S(1)}, bf16[16,16,256]{2,1,0:T(8,128)(2,1)S(1)}, u32[]{:S(2)}, u32[]{:S(2)}) collective-permute-start(bf16[16,16,256]{2,1,0:T(8,128)(2,1)S(1)} %bitcast.78), channel_id=1, source_target_pairs={{12,0},{16,4},{20,8},{24,12},{28,16},{13,1},{17,5},{21,9},{25,13},... | collective-permute-start | bytes 393224 | tf_op jit(solution)/shard_map/ppermute | solution.py:142
  29.7 1.3 %collective-permute-start.6 = (bf16[16,16,256]{2,1,0:T(8,128)(2,1)S(1)}, bf16[16,16,256]{2,1,0:T(8,128)(2,1)S(1)}, u32[]{:S(2)}, u32[]{:S(2)}) collective-permute-start(bf16[16,16,256]{2,1,0:T(8,128)(2,1)S(1)} %bitcast.79), channel_id=1, source_target_pairs={{16,0},{20,4},{24,8},{28,12},{17,1},{21,5},{25,9},{29,13},{18,2},{... | collective-permute-start | bytes 393224 | tf_op jit(solution)/shard_map/ppermute | solution.py:142
  31.0 1.3 %collective-permute-start.7 = (bf16[16,16,256]{2,1,0:T(8,128)(2,1)S(1)}, bf16[16,16,256]{2,1,0:T(8,128)(2,1)S(1)}, u32[]{:S(2)}, u32[]{:S(2)}) collective-permute-start(bf16[16,16,256]{2,1,0:T(8,128)(2,1)S(1)} %bitcast.80), channel_id=1, source_target_pairs={{20,0},{24,4},{28,8},{21,1},{25,5},{29,9},{22,2},{26,6},{30,10},{2... | collective-permute-start | bytes 393224 | tf_op jit(solution)/shard_map/ppermute | solution.py:142
  32.7 1.3 %collective-permute-start.8 = (bf16[16,16,256]{2,1,0:T(8,128)(2,1)S(1)}, bf16[16,16,256]{2,1,0:T(8,128)(2,1)S(1)}, u32[]{:S(2)}, u32[]{:S(2)}) collective-permute-start(bf16[16,16,256]{2,1,0:T(8,128)(2,1)S(1)} %bitcast.81), channel_id=1, source_target_pairs={{24,0},{28,4},{25,1},{29,5},{26,2},{30,6},{27,3},{31,7}} | collective-permute-start | bytes 393224 | tf_op jit(solution)/shard_map/ppermute | solution.py:142
  34.0 2.6 %collective-permute-done.4 = bf16[16,16,256]{2,1,0:T(8,128)(2,1)S(1)} collective-permute-done((bf16[16,16,256]{2,1,0:T(8,128)(2,1)S(1)}, bf16[16,16,256]{2,1,0:T(8,128)(2,1)S(1)}, u32[]{:S(2)}, u32[]{:S(2)}) %collective-permute-start.4) | collective-permute-done | bytes 131104 | tf_op jit(solution)/shard_map/ppermute | solution.py:142
  36.6 1.3 %collective-permute-start.9 = (bf16[16,16,256]{2,1,0:T(8,128)(2,1)S(1)}, bf16[16,16,256]{2,1,0:T(8,128)(2,1)S(1)}, u32[]{:S(2)}, u32[]{:S(2)}) collective-permute-start(bf16[16,16,256]{2,1,0:T(8,128)(2,1)S(1)} %bitcast.82), channel_id=1, source_target_pairs={{28,0},{29,1},{30,2},{31,3}} | collective-permute-start | bytes 393224 | tf_op jit(solution)/shard_map/ppermute | solution.py:142
  37.9 0.9 collective-permute-done.5
  38.9 15.4 %collective-permute-done.6 = bf16[16,16,256]{2,1,0:T(8,128)(2,1)S(1)} collective-permute-done((bf16[16,16,256]{2,1,0:T(8,128)(2,1)S(1)}, bf16[16,16,256]{2,1,0:T(8,128)(2,1)S(1)}, u32[]{:S(2)}, u32[]{:S(2)}) %collective-permute-start.6) | collective-permute-done | bytes 131104 | tf_op jit(solution)/shard_map/ppermute | solution.py:142
  54.3 2.4 %collective-permute-done.7 = bf16[16,16,256]{2,1,0:T(8,128)(2,1)S(1)} collective-permute-done((bf16[16,16,256]{2,1,0:T(8,128)(2,1)S(1)}, bf16[16,16,256]{2,1,0:T(8,128)(2,1)S(1)}, u32[]{:S(2)}, u32[]{:S(2)}) %collective-permute-start.7) | collective-permute-done | bytes 131104 | tf_op jit(solution)/shard_map/ppermute | solution.py:142
  57.1 3.8 %shard_map.38 = f32[32,2,16,256]{3,2,1,0:T(8,128)S(1)} custom-call(s32[32]{0:T(128)S(1)} %get-tuple-element.34.offsets_ref, s32[1]{0:T(128)} %constant.121.clone.1.base_ref, f32[144,16,256]{2,1,0:T(8,128)S(1)} %convert_element_type.79.white_ref), custom_call_target="tpu_custom_call" | custom-call | flops 16777216 | bytes 3407872 | tf_op jit(solution)/shard_map/pallas_call | solution.py:59
  61.0 0.9 convert_element_type.83
  61.9 0.6 collective-permute-start.11
  62.4 1.3 %constant_dynamic-update-slice_fusion.8 = bf16[2,4,256,512]{2,1,3,0:T(4,128)(2,1)} fusion(bf16[2,4,256,512]{2,1,3,0:T(4,128)(2,1)} %constant_dynamic-update-slice_fusion.9, bf16[1,4,256,512]{2,1,3,0:T(4,128)(2,1)S(1)} %neg.32), kind=kLoop, calls=%fused_computation.89 | loop fusion | bytes 2097152 | tf_op jit(solution)/shard_map/stack | solution.py:29
  63.7 3.8 %shard_map.39 = f32[32,2,16,256]{3,2,1,0:T(8,128)S(1)} custom-call(s32[32]{0:T(128)S(1)} %get-tuple-element.36.offsets_ref, s32[1]{0:T(128)} %constant.121.clone.1.base_ref, f32[144,16,256]{2,1,0:T(8,128)S(1)} %convert_element_type.79.white_ref), custom_call_target="tpu_custom_call" | custom-call | flops 16777216 | bytes 3407872 | tf_op jit(solution)/shard_map/pallas_call | solution.py:59
  67.6 0.9 convert_element_type.84
  68.5 9.1 %constant_dynamic-slice_fusion.3 = (bf16[2,1,256,512]{2,1,3,0:T(2,128)(2,1)S(1)}, bf16[2,1,256,512]{2,1,3,0:T(2,128)(2,1)}, bf16[2,1,256,512]{2,1,3,0:T(2,128)(2,1)}, bf16[2,1,256,512]{2,1,3,0:T(2,128)(2,1)}) fusion(bf16[2,4,256,512]{2,1,3,0:T(4,128)(2,1)} %constant_dynamic-update-slice_fusion.8, s32[]{:T(128)S(6)} %select_n.120, s32[]{:T(128)S(6)} %select_n.126, ...), kind=kLoop, calls=%fused_computation.103 | loop fusion | bytes 4194320 | tf_op jit(solution)/shard_map/dynamic-slice
  77.6 3.5 %copy.8 = bf16[2,1,256,512]{3,2,0,1:T(8,128)(2,1)} copy(bf16[2,1,256,512]{2,1,3,0:T(2,128)(2,1)} %get-tuple-element.10) | data formatting | bytes 1048576 | tf_op jit(solution)/shard_map/dynamic-slice.1
  81.0 3.5 %copy.9 = bf16[2,1,256,512]{3,2,0,1:T(8,128)(2,1)} copy(bf16[2,1,256,512]{2,1,3,0:T(2,128)(2,1)} %get-tuple-element.9) | data formatting | bytes 1048576 | tf_op jit(solution)/shard_map/dynamic-slice.2
  84.5 3.5 %copy.10 = bf16[2,1,256,512]{3,2,0,1:T(8,128)(2,1)} copy(bf16[2,1,256,512]{2,1,3,0:T(2,128)(2,1)} %get-tuple-element.8) | data formatting | bytes 1048576 | tf_op jit(solution)/shard_map/dynamic-slice.3
  88.0 2.3 %copy.7 = bf16[2,1,256,512]{3,2,0,1:T(8,128)(2,1)} copy(bf16[2,1,256,512]{2,1,3,0:T(2,128)(2,1)S(1)} %get-tuple-element.7) | data formatting | bytes 1048576 | tf_op jit(solution)/shard_map/dynamic-slice
  90.3 3.8 %shard_map.37 = f32[32,2,16,256]{3,2,1,0:T(8,128)S(1)} custom-call(s32[32]{0:T(128)S(1)} %get-tuple-element.33.offsets_ref, s32[1]{0:T(128)} %constant.121.clone.1.base_ref, f32[144,16,256]{2,1,0:T(8,128)S(1)} %convert_element_type.79.white_ref), custom_call_target="tpu_custom_call" | custom-call | flops 16777216 | bytes 3407872 | tf_op jit(solution)/shard_map/pallas_call | solution.py:59
  94.2 0.6 collective-permute-start.10
  94.8 3.8 %shard_map.40 = f32[32,2,16,256]{3,2,1,0:T(8,128)S(1)} custom-call(s32[32]{0:T(128)S(1)} %get-tuple-element.35.offsets_ref, s32[1]{0:T(128)} %constant.121.clone.1.base_ref, f32[144,16,256]{2,1,0:T(8,128)S(1)} %convert_element_type.79.white_ref), custom_call_target="tpu_custom_call" | custom-call | flops 16777216 | bytes 3407872 | tf_op jit(solution)/shard_map/pallas_call | solution.py:59
  99.1 0.6 copy-done.3
  99.7 1.5 %convolution_bitcast_fusion.2 = f32[32,16,512]{2,1,0:T(8,128)S(1)} fusion(bf16[32,2,16,256]{3,2,1,0:T(8,128)(2,1)} %collective-permute-done.11, bf16[2,1,256,512]{3,2,0,1:T(8,128)(2,1)S(1)} %copy-done.3), kind=kOutput, calls=%fused_computation.11 | convolution fusion | flops 268435456 | bytes 2097152 | tf_op jit(solution)/shard_map/opck,pkl->ocl/dot_general | solution.py:165
  101.2 1.5 %convolution_bitcast_fusion.1 = f32[32,16,512]{2,1,0:T(8,128)S(1)} fusion(bf16[32,2,16,256]{3,2,1,0:T(8,128)(2,1)} %collective-permute-done.12, bf16[2,1,256,512]{3,2,0,1:T(8,128)(2,1)S(1)} %copy-done.2), kind=kOutput, calls=%fused_computation.10 | convolution fusion | flops 268435456 | bytes 2097152 | tf_op jit(solution)/shard_map/opck,pkl->ocl/dot_general | solution.py:165
  102.9 1.3 %fusion.11 = bf16[32,16,512]{2,1,0:T(8,128)(2,1)} fusion(f32[32,16,512]{2,1,0:T(8,128)S(1)} %convolution_bitcast_fusion, f32[32,16,512]{2,1,0:T(8,128)S(1)} %convolution_bitcast_fusion.1, f32[32,16,512]{2,1,0:T(8,128)S(1)} %convolution_bitcast_fusion.2, bf16[32,2,16,256]{3,2,1,0:T(8,128)(2,1)S(1)} %collective-permute-done.10, ...), kind=kOutput, calls=%fused_computation.17 | convolution fusion | flops 269746176 | bytes 4718592 | tf_op jit(solution)/shard_map/opck,pkl->ocl/dot_general | solution.py:165
  (45 shorter events, 3.1 us)
Async XLA Ops:
  13.4 6.7 %copy-start.4 = (s32[1024]{0:T(1024)S(1)}, s32[1024]{0:T(1024)}, u32[]{:S(2)}) copy-start(s32[1024]{0:T(1024)} %param.4) | copy-start | bytes 12292
  15.7 9.1 %collective-permute-start = (bf16[16,2,2,256]{3,2,1,0:T(2,128)(2,1)}, bf16[16,2,2,256]{3,2,1,0:T(2,128)(2,1)S(1)}, u32[]{:S(2)}, u32[]{:S(2)}) collective-permute-start(bf16[16,2,2,256]{3,2,1,0:T(2,128)(2,1)} %get-tuple-element.22), channel_id=1, source_target_pairs={{0,1},{1,2},{2,3},{3,0},{4,5},{5,6},{6,7},{7,4},{8,9},{9,10},{10,1... | collective-permute-start | bytes 98312 | tf_op jit(solution)/shard_map/ppermute | solution.py:132
  16.1 8.6 %collective-permute-start.1 = (bf16[16,2,2,256]{3,2,1,0:T(2,128)(2,1)S(1)}, bf16[16,2,2,256]{3,2,1,0:T(2,128)(2,1)}, u32[]{:S(2)}, u32[]{:S(2)}) collective-permute-start(bf16[16,2,2,256]{3,2,1,0:T(2,128)(2,1)S(1)} %get-tuple-element.21), channel_id=1, source_target_pairs={{0,2},{1,3},{2,0},{3,1},{4,6},{5,7},{6,4},{7,5},{8,10},{9,11},{10,... | collective-permute-start | bytes 98312 | tf_op jit(solution)/shard_map/ppermute | solution.py:132
  18.7 6.1 %collective-permute-start.2 = (bf16[16,2,2,256]{3,2,1,0:T(2,128)(2,1)S(1)}, bf16[16,2,2,256]{3,2,1,0:T(2,128)(2,1)}, u32[]{:S(2)}, u32[]{:S(2)}) collective-permute-start(bf16[16,2,2,256]{3,2,1,0:T(2,128)(2,1)S(1)} %get-tuple-element.20), channel_id=1, source_target_pairs={{0,3},{1,0},{2,1},{3,2},{4,7},{5,4},{6,5},{7,6},{8,11},{9,8},{10,9... | collective-permute-start | bytes 98312 | tf_op jit(solution)/shard_map/ppermute | solution.py:132
  21.7 2.2 %copy-start.5 = (s32[128]{0:T(128)S(1)}, s32[128]{0:T(128)}, u32[]{:S(2)}) copy-start(s32[128]{0:T(128)} %param.5) | copy-start | bytes 1540
  25.8 6.9 %collective-permute-start.3 = (bf16[16,16,256]{2,1,0:T(8,128)(2,1)S(1)}, bf16[16,16,256]{2,1,0:T(8,128)(2,1)S(1)}, u32[]{:S(2)}, u32[]{:S(2)}) collective-permute-start(bf16[16,16,256]{2,1,0:T(8,128)(2,1)S(1)} %bitcast.76), channel_id=1, source_target_pairs={{4,0},{8,4},{12,8},{16,12},{20,16},{24,20},{28,24},{5,1},{9,5},{13... | collective-permute-start | bytes 393224 | tf_op jit(solution)/shard_map/ppermute | solution.py:142
  27.1 9.5 %collective-permute-start.4 = (bf16[16,16,256]{2,1,0:T(8,128)(2,1)S(1)}, bf16[16,16,256]{2,1,0:T(8,128)(2,1)S(1)}, u32[]{:S(2)}, u32[]{:S(2)}) collective-permute-start(bf16[16,16,256]{2,1,0:T(8,128)(2,1)S(1)} %bitcast.77), channel_id=1, source_target_pairs={{8,0},{12,4},{16,8},{20,12},{24,16},{28,20},{9,1},{13,5},{17,9},{2... | collective-permute-start | bytes 393224 | tf_op jit(solution)/shard_map/ppermute | solution.py:142
  28.4 10.4 %collective-permute-start.5 = (bf16[16,16,256]{2,1,0:T(8,128)(2,1)S(1)}, bf16[16,16,256]{2,1,0:T(8,128)(2,1)S(1)}, u32[]{:S(2)}, u32[]{:S(2)}) collective-permute-start(bf16[16,16,256]{2,1,0:T(8,128)(2,1)S(1)} %bitcast.78), channel_id=1, source_target_pairs={{12,0},{16,4},{20,8},{24,12},{28,16},{13,1},{17,5},{21,9},{25,13},... | collective-permute-start | bytes 393224 | tf_op jit(solution)/shard_map/ppermute | solution.py:142
  29.7 24.6 %collective-permute-start.6 = (bf16[16,16,256]{2,1,0:T(8,128)(2,1)S(1)}, bf16[16,16,256]{2,1,0:T(8,128)(2,1)S(1)}, u32[]{:S(2)}, u32[]{:S(2)}) collective-permute-start(bf16[16,16,256]{2,1,0:T(8,128)(2,1)S(1)} %bitcast.79), channel_id=1, source_target_pairs={{16,0},{20,4},{24,8},{28,12},{17,1},{21,5},{25,9},{29,13},{18,2},{... | collective-permute-start | bytes 393224 | tf_op jit(solution)/shard_map/ppermute | solution.py:142
  31.0 25.7 %collective-permute-start.7 = (bf16[16,16,256]{2,1,0:T(8,128)(2,1)S(1)}, bf16[16,16,256]{2,1,0:T(8,128)(2,1)S(1)}, u32[]{:S(2)}, u32[]{:S(2)}) collective-permute-start(bf16[16,16,256]{2,1,0:T(8,128)(2,1)S(1)} %bitcast.80), channel_id=1, source_target_pairs={{20,0},{24,4},{28,8},{21,1},{25,5},{29,9},{22,2},{26,6},{30,10},{2... | collective-permute-start | bytes 393224 | tf_op jit(solution)/shard_map/ppermute | solution.py:142
  32.7 24.1 %collective-permute-start.8 = (bf16[16,16,256]{2,1,0:T(8,128)(2,1)S(1)}, bf16[16,16,256]{2,1,0:T(8,128)(2,1)S(1)}, u32[]{:S(2)}, u32[]{:S(2)}) collective-permute-start(bf16[16,16,256]{2,1,0:T(8,128)(2,1)S(1)} %bitcast.81), channel_id=1, source_target_pairs={{24,0},{28,4},{25,1},{29,5},{26,2},{30,6},{27,3},{31,7}} | collective-permute-start | bytes 393224 | tf_op jit(solution)/shard_map/ppermute | solution.py:142
  36.6 20.1 %collective-permute-start.9 = (bf16[16,16,256]{2,1,0:T(8,128)(2,1)S(1)}, bf16[16,16,256]{2,1,0:T(8,128)(2,1)S(1)}, u32[]{:S(2)}, u32[]{:S(2)}) collective-permute-start(bf16[16,16,256]{2,1,0:T(8,128)(2,1)S(1)} %bitcast.82), channel_id=1, source_target_pairs={{28,0},{29,1},{30,2},{31,3}} | collective-permute-start | bytes 393224 | tf_op jit(solution)/shard_map/ppermute | solution.py:142
  61.9 37.2 %collective-permute-start.11 = (bf16[32,2,16,256]{3,2,1,0:T(8,128)(2,1)}, bf16[32,2,16,256]{3,2,1,0:T(8,128)(2,1)}, u32[]{:S(2)}, u32[]{:S(2)}) collective-permute-start(bf16[32,2,16,256]{3,2,1,0:T(8,128)(2,1)} %convert_element_type.83), channel_id=1, source_target_pairs={{0,2},{1,3},{2,0},{3,1},{4,6},{5,7},{6,4},{7,5},{8,10},{9,11},{10,... | collective-permute-start | bytes 1572872 | tf_op jit(solution)/shard_map/ppermute | solution.py:162
  68.4 32.7 %collective-permute-start.12 = (bf16[32,2,16,256]{3,2,1,0:T(8,128)(2,1)}, bf16[32,2,16,256]{3,2,1,0:T(8,128)(2,1)}, u32[]{:S(2)}, u32[]{:S(2)}) collective-permute-start(bf16[32,2,16,256]{3,2,1,0:T(8,128)(2,1)} %convert_element_type.84), channel_id=1, source_target_pairs={{0,3},{1,0},{2,1},{3,2},{4,7},{5,4},{6,5},{7,6},{8,11},{9,8},{10,9... | collective-permute-start | bytes 1572872 | tf_op jit(solution)/shard_map/ppermute | solution.py:162
  94.2 4.4 %copy-start.1 = (bf16[2,1,256,512]{3,2,0,1:T(8,128)(2,1)S(1)}, bf16[2,1,256,512]{3,2,0,1:T(8,128)(2,1)}, u32[]{:S(2)}) copy-start(bf16[2,1,256,512]{3,2,0,1:T(8,128)(2,1)} %copy.10) | copy-start | bytes 1572868
  94.2 8.7 %collective-permute-start.10 = (bf16[32,2,16,256]{3,2,1,0:T(8,128)(2,1)S(1)}, bf16[32,2,16,256]{3,2,1,0:T(8,128)(2,1)S(1)}, u32[]{:S(2)}, u32[]{:S(2)}) collective-permute-start(bf16[32,2,16,256]{3,2,1,0:T(8,128)(2,1)S(1)} %convert_element_type.80), channel_id=1, source_target_pairs={{0,1},{1,2},{2,3},{3,0},{4,5},{5,6},{6,7},{7,4},{8,9},{9,10},{10,1... | collective-permute-start | bytes 1572872 | tf_op jit(solution)/shard_map/ppermute | solution.py:162
  98.6 1.0 %copy-start.3 = (bf16[2,1,256,512]{3,2,0,1:T(8,128)(2,1)S(1)}, bf16[2,1,256,512]{3,2,0,1:T(8,128)(2,1)}, u32[]{:S(2)}) copy-start(bf16[2,1,256,512]{3,2,0,1:T(8,128)(2,1)} %copy.8) | copy-start | bytes 1572868
  98.7 2.5 %copy-start.2 = (bf16[2,1,256,512]{3,2,0,1:T(8,128)(2,1)S(1)}, bf16[2,1,256,512]{3,2,0,1:T(8,128)(2,1)}, u32[]{:S(2)}) copy-start(bf16[2,1,256,512]{3,2,0,1:T(8,128)(2,1)} %copy.9) | copy-start | bytes 1572868
  99.1 3.8 %copy-start = (bf16[2,1,256,512]{3,2,0,1:T(8,128)(2,1)S(1)}, bf16[2,1,256,512]{3,2,0,1:T(8,128)(2,1)}, u32[]{:S(2)}) copy-start(bf16[2,1,256,512]{3,2,0,1:T(8,128)(2,1)} %copy.7) | copy-start | bytes 1572868

commit v27 on v23

--- a/solution.py
+++ b/solution.py
@@ -67,7 +67,7 @@
         out_shape=jax.ShapeDtypeStruct((band_span, 2, own_count, bins), jnp.float32),
         compiler_params=pltpu.CompilerParams(vmem_limit_bytes=48 * 1024 * 1024),
         cost_estimate=pl.CostEstimate(
-            flops=8 * band_span * own_count * rows * bins,
+            flops=1024 * band_span * own_count * rows * bins,
             transcendentals=0,
             bytes_accessed=white_all.size * 4 + band_span * 2 * own_count * bins * 4,
         ),

time: 85 us -> 83 us (0.976)
  waiting for transfers between devices: 24.2 us -> 30.4 us
  other arithmetic: 13.8 us -> 10.9 us
  local copies, waits for them, and re-layouts: 7.97 us -> 5.24 us
  matrix products: 7.12 us -> 5.04 us
    ppermute x3, waiting for transfers between devices: 0.92 us -> 8.63 us  [local(): part = lax.ppermute(part, 'gy', perm=pairs)]
    dot_general x4, matrix products: 4.66 us -> 2.58 us  [local(): jnp.einsum('opck,pkl->ocl', part, rows, preferred_element_type=jnp.float32)]
    neg x1, local copies, waits for them, and re-layouts: 2.31 us -> 0.54 us  [inverse_table(): return jnp.stack([cos_t, -sin_t], axis=0).astype(jnp.bfloat16)]
    convert_element_type x3, other arithmetic: 1.82 us -> 0.23 us  [local(): part = cross_spectra(padded, lax.dynamic_slice_in_dim(offsets, dest * off...]
    another operation x2, other arithmetic: 5.69 us -> 4.39 us
    sub x1, local copies, waits for them, and re-layouts: 1.49 us -> 0.53 us  [inverse_table(): cos_t = (cos_f * cos_c - sin_f * sin_c).reshape(kept_bins.shape[0], LAGS)]
    ppermute x3, waiting for transfers between devices: 0.94 us -> 0.01 us  [local(): lax.ppermute(piece, 'gy', perm=[(src, (src + shift) % gy_count) for src i...]
  transfers between devices with their start and end apart: 13 -> 13, of which waited for: 7 -> 6; matrix products, arithmetic and copies ran while one was open for 13% -> 5% of each run, Pallas kernels for 14% -> 14%
where the time goes in v27:
time: 83 us; the launch traced here: 82.5 us
  waiting for transfers between devices  30.4 us (37%)
  Pallas kernels  15.3 us (18%)
  starting transfers between devices  15.2 us (18%)
  other arithmetic  10.9 us (13%)
  local copies, waits for them, and re-layouts  5.24 us (6%)
  matrix products  5.04 us (6%)
    ppermute x7, waiting for transfers between devices, local(): blocks.append(lax.ppermute(rows_white, 'gx', perm=pairs))  21.8 us
    pallas_call x4, Pallas kernels, cross_spectra(): pl.pallas_call(kernel, grid_spec=pltpu.PrefetchScalarGridSpec(num_scalar_...  15.3 us
    ppermute x7, starting transfers between devices, local(): blocks.append(lax.ppermute(rows_white, 'gx', perm=pairs))  9.02 us
    ppermute x3, waiting for transfers between devices, local(): part = lax.ppermute(part, 'gy', perm=pairs)  8.63 us
    ppermute x3, starting transfers between devices, local(): lax.ppermute(piece, 'gy', perm=[(src, (src + shift) % gy_count) for src i...  4.46 us
    another operation x2, other arithmetic  4.39 us
    dot_general x4, matrix products, local(): jnp.einsum('opck,pkl->ocl', part, rows, preferred_element_type=jnp.float32)  2.58 us
    dot_general x1, matrix products, forward_spectra(): jnp.dot(record_rows.reshape(row_count * block_count, block_len), small_ta...  2.46 us
  transfers between devices with their start and end apart: 13, of which 6 were waited for; matrix products, arithmetic and copies ran while one was open for 5% of the time, Pallas kernels for 14%

profile of v27, /device:TPU:0, one launch (start us, length us, event | category | flops | bytes accessed | tf_op | source)
XLA Modules:
  0.0 82.5 jit_solution(8485357375102415907)
XLA Ops:
  0.0 1.2 %fusion.52 = (f32[32,1024]{1,0:T(8,128)S(1)}, f32[32,1024]{1,0:T(8,128)S(1)}) fusion(s32[1024]{0:T(1024)} %param.4), kind=kLoop, calls=%fused_computation.87 | loop fusion | flops 458752 | bytes 266240 | tf_op jit(solution)/shard_map/cos | solution.py:89
  1.2 0.7 add_select_fusion.5
  1.9 1.8 %fusion.41 = (f32[64,1024]{1,0:T(8,128)S(1)}, f32[64,1024]{1,0:T(8,128)S(1)}) fusion(s32[1024]{0:T(1024)} %param.4, s32[64]{0:T(128)S(1)} %iota_multiply_fusion), kind=kLoop, calls=%fused_computation.70 | loop fusion | flops 917504 | bytes 528640 | tf_op jit(solution)/shard_map/cos | solution.py:89
  3.7 1.2 %reshape_reshape.3 = bf16[128,2048]{1,0:T(8,128)(2,1)S(1)} reshape(bf16[16,2,8192]{2,1,0:T(2,128)(2,1)} %param.3) | data formatting | bytes 1048576 | tf_op jit(solution)/shard_map/reshape;reshape | solution.py:102
  4.9 3.7 %subtract_convert_fusion = (bf16[64,32,1024]{2,1,0:T(8,128)(2,1)S(1)}, bf16[64,32,1024]{2,1,0:T(8,128)(2,1)S(1)}) fusion(f32[64,1024]{1,0:T(8,128)S(1)} %get-tuple-element.20, f32[32,1024]{1,0:T(8,128)S(1)} %get-tuple-element.26, f32[64,1024]{1,0:T(8,128)S(1)} %get-tuple-element.19, f32[32,1024]{1,0:T(8,128)S(1)} %get-tuple-element.25), kind=kLoop, calls=%fused_computation.5 | loop fusion | flops 18874368 | bytes 9175040 | tf_op jit(solution)/shard_map/convert.7
  8.5 2.5 %fusion.4 = f32[128,2048]{0,1:T(8,128)S(1)} fusion(bf16[128,2048]{1,0:T(8,128)(2,1)S(1)} %reshape_reshape.3, bf16[2048,1024]{1,0:T(8,128)(2,1)S(1)} %bitcast.69, bf16[2048,1024]{1,0:T(8,128)(2,1)S(1)} %bitcast.68), kind=kOutput, calls=%fused_computation.14 | convolution fusion | flops 1090519040 | bytes 9961472 | tf_op jit(solution)/shard_map/dot_general | solution.py:101
  11.0 0.3 copy.4
  11.3 0.9 %reshape.439 = f32[32,4,2,1024]{3,2,1,0:T(2,128)S(1)} reshape(f32[128,2048]{1,0:T(8,128)S(1)} %copy.4) | data formatting | bytes 2097152 | tf_op jit(solution)/shard_map/reshape | solution.py:105
  12.2 1.2 %fusion.68 = (f32[32,4,1,1024]{3,2,1,0:T(1,128)S(1)}, f32[32,4,1,1024]{3,2,1,0:T(1,128)S(1)}) fusion(f32[32,4,2,1024]{3,2,1,0:T(2,128)S(1)} %reshape.439), kind=kLoop, calls=%fused_computation.126 | loop fusion | bytes 2097152 | tf_op jit(solution)/shard_map/slice | solution.py:112
  13.4 0.2 cosine_round-nearest-even_fusion
  13.6 0.8 fusion.25
  14.3 0.1 multiply_reduce_fusion
  14.5 0.2 concatenate.18
  14.8 0.2 multiply_convert_fusion
  15.0 0.1 constant_dynamic-slice_fusion.3
  15.1 0.5 collective-permute-start
  15.6 2.6 %collective-permute-start.1 = (bf16[16,2,2,256]{3,2,1,0:T(2,128)(2,1)S(1)}, bf16[16,2,2,256]{3,2,1,0:T(2,128)(2,1)S(1)}, u32[]{:S(2)}, u32[]{:S(2)}) collective-permute-start(bf16[16,2,2,256]{3,2,1,0:T(2,128)(2,1)S(1)} %get-tuple-element.17), channel_id=1, source_target_pairs={{0,2},{1,3},{2,0},{3,1},{4,6},{5,7},{6,4},{7,5},{8,10},{9,11},{10,... | collective-permute-start | bytes 98312 | tf_op jit(solution)/shard_map/ppermute | solution.py:132
  18.1 1.4 %collective-permute-start.2 = (bf16[16,2,2,256]{3,2,1,0:T(2,128)(2,1)S(1)}, bf16[16,2,2,256]{3,2,1,0:T(2,128)(2,1)S(1)}, u32[]{:S(2)}, u32[]{:S(2)}) collective-permute-start(bf16[16,2,2,256]{3,2,1,0:T(2,128)(2,1)S(1)} %get-tuple-element.16), channel_id=1, source_target_pairs={{0,3},{1,0},{2,1},{3,2},{4,7},{5,4},{6,5},{7,6},{8,11},{9,8},{10,9... | collective-permute-start | bytes 98312 | tf_op jit(solution)/shard_map/ppermute | solution.py:132
  19.5 0.5 fusion.50
  20.1 0.3 fusion.54
  20.4 0.7 negate_convert_fusion.1
  21.3 0.5 copy.7
  21.8 0.5 copy.8
  22.4 0.2 maximum_bitcast_fusion
  22.6 1.3 %collective-permute-start.3 = (bf16[16,16,256]{2,1,0:T(8,128)(2,1)S(1)}, bf16[16,16,256]{2,1,0:T(8,128)(2,1)S(1)}, u32[]{:S(2)}, u32[]{:S(2)}) collective-permute-start(bf16[16,16,256]{2,1,0:T(8,128)(2,1)S(1)} %bitcast.72), channel_id=1, source_target_pairs={{4,0},{8,4},{12,8},{16,12},{20,16},{24,20},{28,24},{5,1},{9,5},{13... | collective-permute-start | bytes 393224 | tf_op jit(solution)/shard_map/ppermute | solution.py:142
  23.9 1.3 %collective-permute-start.4 = (bf16[16,16,256]{2,1,0:T(8,128)(2,1)S(1)}, bf16[16,16,256]{2,1,0:T(8,128)(2,1)S(1)}, u32[]{:S(2)}, u32[]{:S(2)}) collective-permute-start(bf16[16,16,256]{2,1,0:T(8,128)(2,1)S(1)} %bitcast.73), channel_id=1, source_target_pairs={{8,0},{12,4},{16,8},{20,12},{24,16},{28,20},{9,1},{13,5},{17,9},{2... | collective-permute-start | bytes 393224 | tf_op jit(solution)/shard_map/ppermute | solution.py:142
  25.3 1.3 %collective-permute-start.5 = (bf16[16,16,256]{2,1,0:T(8,128)(2,1)S(1)}, bf16[16,16,256]{2,1,0:T(8,128)(2,1)S(1)}, u32[]{:S(2)}, u32[]{:S(2)}) collective-permute-start(bf16[16,16,256]{2,1,0:T(8,128)(2,1)S(1)} %bitcast.74), channel_id=1, source_target_pairs={{12,0},{16,4},{20,8},{24,12},{28,16},{13,1},{17,5},{21,9},{25,13},... | collective-permute-start | bytes 393224 | tf_op jit(solution)/shard_map/ppermute | solution.py:142
  26.6 1.3 %collective-permute-start.6 = (bf16[16,16,256]{2,1,0:T(8,128)(2,1)S(1)}, bf16[16,16,256]{2,1,0:T(8,128)(2,1)S(1)}, u32[]{:S(2)}, u32[]{:S(2)}) collective-permute-start(bf16[16,16,256]{2,1,0:T(8,128)(2,1)S(1)} %bitcast.75), channel_id=1, source_target_pairs={{16,0},{20,4},{24,8},{28,12},{17,1},{21,5},{25,9},{29,13},{18,2},{... | collective-permute-start | bytes 393224 | tf_op jit(solution)/shard_map/ppermute | solution.py:142
  27.9 1.3 %collective-permute-start.7 = (bf16[16,16,256]{2,1,0:T(8,128)(2,1)S(1)}, bf16[16,16,256]{2,1,0:T(8,128)(2,1)S(1)}, u32[]{:S(2)}, u32[]{:S(2)}) collective-permute-start(bf16[16,16,256]{2,1,0:T(8,128)(2,1)S(1)} %bitcast.76), channel_id=1, source_target_pairs={{20,0},{24,4},{28,8},{21,1},{25,5},{29,9},{22,2},{26,6},{30,10},{2... | collective-permute-start | bytes 393224 | tf_op jit(solution)/shard_map/ppermute | solution.py:142
  29.2 0.3 collective-permute-done.3
  29.5 1.3 %collective-permute-start.8 = (bf16[16,16,256]{2,1,0:T(8,128)(2,1)S(1)}, bf16[16,16,256]{2,1,0:T(8,128)(2,1)S(1)}, u32[]{:S(2)}, u32[]{:S(2)}) collective-permute-start(bf16[16,16,256]{2,1,0:T(8,128)(2,1)S(1)} %bitcast.77), channel_id=1, source_target_pairs={{24,0},{28,4},{25,1},{29,5},{26,2},{30,6},{27,3},{31,7}} | collective-permute-start | bytes 393224 | tf_op jit(solution)/shard_map/ppermute | solution.py:142
  30.8 2.5 %collective-permute-done.4 = bf16[16,16,256]{2,1,0:T(8,128)(2,1)S(1)} collective-permute-done((bf16[16,16,256]{2,1,0:T(8,128)(2,1)S(1)}, bf16[16,16,256]{2,1,0:T(8,128)(2,1)S(1)}, u32[]{:S(2)}, u32[]{:S(2)}) %collective-permute-start.4) | collective-permute-done | bytes 131104 | tf_op jit(solution)/shard_map/ppermute | solution.py:142
  33.3 1.3 %collective-permute-start.9 = (bf16[16,16,256]{2,1,0:T(8,128)(2,1)S(1)}, bf16[16,16,256]{2,1,0:T(8,128)(2,1)S(1)}, u32[]{:S(2)}, u32[]{:S(2)}) collective-permute-start(bf16[16,16,256]{2,1,0:T(8,128)(2,1)S(1)} %bitcast.78), channel_id=1, source_target_pairs={{28,0},{29,1},{30,2},{31,3}} | collective-permute-start | bytes 393224 | tf_op jit(solution)/shard_map/ppermute | solution.py:142
  34.6 1.4 %collective-permute-done.5 = bf16[16,16,256]{2,1,0:T(8,128)(2,1)S(1)} collective-permute-done((bf16[16,16,256]{2,1,0:T(8,128)(2,1)S(1)}, bf16[16,16,256]{2,1,0:T(8,128)(2,1)S(1)}, u32[]{:S(2)}, u32[]{:S(2)}) %collective-permute-start.5) | collective-permute-done | bytes 131104 | tf_op jit(solution)/shard_map/ppermute | solution.py:142
  36.0 15.2 %collective-permute-done.6 = bf16[16,16,256]{2,1,0:T(8,128)(2,1)S(1)} collective-permute-done((bf16[16,16,256]{2,1,0:T(8,128)(2,1)S(1)}, bf16[16,16,256]{2,1,0:T(8,128)(2,1)S(1)}, u32[]{:S(2)}, u32[]{:S(2)}) %collective-permute-start.6) | collective-permute-done | bytes 131104 | tf_op jit(solution)/shard_map/ppermute | solution.py:142
  51.1 2.4 %collective-permute-done.7 = bf16[16,16,256]{2,1,0:T(8,128)(2,1)S(1)} collective-permute-done((bf16[16,16,256]{2,1,0:T(8,128)(2,1)S(1)}, bf16[16,16,256]{2,1,0:T(8,128)(2,1)S(1)}, u32[]{:S(2)}, u32[]{:S(2)}) %collective-permute-start.7) | collective-permute-done | bytes 131104 | tf_op jit(solution)/shard_map/ppermute | solution.py:142
  53.6 0.3 convert_element_type.78.white_ref
  54.0 3.8 %shard_map.38 = f32[32,2,16,256]{3,2,1,0:T(8,128)S(1)} custom-call(s32[32]{0:T(128)S(1)} %get-tuple-element.30.offsets_ref, s32[1]{0:T(128)} %constant.111.clone.1.base_ref, f32[144,16,256]{2,1,0:T(8,128)S(1)} %convert_element_type.78.white_ref), custom_call_target="tpu_custom_call" | custom-call | flops 2147483648 | bytes 3407872 | tf_op jit(solution)/shard_map/pallas_call | solution.py:59
  57.9 1.1 %collective-permute-start.11 = (bf16[32,2,16,256]{3,2,1,0:T(8,128)(2,1)S(1)}, bf16[32,2,16,256]{3,2,1,0:T(8,128)(2,1)S(1)}, u32[]{:S(2)}, u32[]{:S(2)}) collective-permute-start(bf16[32,2,16,256]{3,2,1,0:T(8,128)(2,1)S(1)} %convert_element_type.82), channel_id=1, source_target_pairs={{0,2},{1,3},{2,0},{3,1},{4,6},{5,7},{6,4},{7,5},{8,10},{9,11},{10,... | collective-permute-start | bytes 1572872 | tf_op jit(solution)/shard_map/ppermute | solution.py:162
  59.0 3.8 %shard_map.39 = f32[32,2,16,256]{3,2,1,0:T(8,128)S(1)} custom-call(s32[32]{0:T(128)S(1)} %get-tuple-element.32.offsets_ref, s32[1]{0:T(128)} %constant.111.clone.1.base_ref, f32[144,16,256]{2,1,0:T(8,128)S(1)} %convert_element_type.78.white_ref), custom_call_target="tpu_custom_call" | custom-call | flops 2147483648 | bytes 3407872 | tf_op jit(solution)/shard_map/pallas_call | solution.py:59
  63.0 3.8 %shard_map.37 = f32[32,2,16,256]{3,2,1,0:T(8,128)S(1)} custom-call(s32[32]{0:T(128)S(1)} %get-tuple-element.29.offsets_ref, s32[1]{0:T(128)} %constant.111.clone.1.base_ref, f32[144,16,256]{2,1,0:T(8,128)S(1)} %convert_element_type.78.white_ref), custom_call_target="tpu_custom_call" | custom-call | flops 2147483648 | bytes 3407872 | tf_op jit(solution)/shard_map/pallas_call | solution.py:59
  66.9 0.5 collective-permute-start.10
  67.4 3.8 %shard_map.40 = f32[32,2,16,256]{3,2,1,0:T(8,128)S(1)} custom-call(s32[32]{0:T(128)S(1)} %get-tuple-element.31.offsets_ref, s32[1]{0:T(128)} %constant.111.clone.1.base_ref, f32[144,16,256]{2,1,0:T(8,128)S(1)} %convert_element_type.78.white_ref), custom_call_target="tpu_custom_call" | custom-call | flops 2147483648 | bytes 3407872 | tf_op jit(solution)/shard_map/pallas_call | solution.py:59
  71.2 0.4 convolution_bitcast_fusion
  71.7 0.4 convolution_bitcast_fusion.2
  72.1 8.6 %collective-permute-done.12 = bf16[32,2,16,256]{3,2,1,0:T(8,128)(2,1)S(1)} collective-permute-done((bf16[32,2,16,256]{3,2,1,0:T(8,128)(2,1)S(1)}, bf16[32,2,16,256]{3,2,1,0:T(8,128)(2,1)S(1)}, u32[]{:S(2)}, u32[]{:S(2)}) %collective-permute-start.12) | collective-permute-done | bytes 524320 | tf_op jit(solution)/shard_map/ppermute | solution.py:162
  80.8 0.4 convolution_bitcast_fusion.1
  81.2 1.3 %fusion.11 = bf16[32,16,512]{2,1,0:T(8,128)(2,1)} fusion(f32[32,16,512]{2,1,0:T(8,128)S(1)} %convolution_bitcast_fusion, f32[32,16,512]{2,1,0:T(8,128)S(1)} %convolution_bitcast_fusion.1, f32[32,16,512]{2,1,0:T(8,128)S(1)} %convolution_bitcast_fusion.2, bf16[32,2,16,256]{3,2,1,0:T(8,128)(2,1)S(1)} %collective-permute-done.10, s32[]{:T(128)S(6)} %select_n.110, ...), kind=kOutput, calls=%fused_computation.25 | convolution fusion | flops 270794752 | bytes 6291460 | tf_op jit(solution)/shard_map/opck,pkl->ocl/dot_general | solution.py:165
  (30 shorter events, 0.6 us)
Async XLA Ops:
  13.4 6.1 %copy-start = (s32[1024]{0:T(1024)S(1)}, s32[1024]{0:T(1024)}, u32[]{:S(2)}) copy-start(s32[1024]{0:T(1024)} %param.4) | copy-start | bytes 12292
  14.5 6.7 %copy-start.1 = (s32[128]{0:T(128)S(1)}, s32[128]{0:T(128)}, u32[]{:S(2)}) copy-start(s32[128]{0:T(128)} %param.5) | copy-start | bytes 1540
  15.1 7.3 %collective-permute-start = (bf16[16,2,2,256]{3,2,1,0:T(2,128)(2,1)S(1)}, bf16[16,2,2,256]{3,2,1,0:T(2,128)(2,1)S(1)}, u32[]{:S(2)}, u32[]{:S(2)}) collective-permute-start(bf16[16,2,2,256]{3,2,1,0:T(2,128)(2,1)S(1)} %get-tuple-element.18), channel_id=1, source_target_pairs={{0,1},{1,2},{2,3},{3,0},{4,5},{5,6},{6,7},{7,4},{8,9},{9,10},{10,1... | collective-permute-start | bytes 98312 | tf_op jit(solution)/shard_map/ppermute | solution.py:132
  15.6 6.8 %collective-permute-start.1 = (bf16[16,2,2,256]{3,2,1,0:T(2,128)(2,1)S(1)}, bf16[16,2,2,256]{3,2,1,0:T(2,128)(2,1)S(1)}, u32[]{:S(2)}, u32[]{:S(2)}) collective-permute-start(bf16[16,2,2,256]{3,2,1,0:T(2,128)(2,1)S(1)} %get-tuple-element.17), channel_id=1, source_target_pairs={{0,2},{1,3},{2,0},{3,1},{4,6},{5,7},{6,4},{7,5},{8,10},{9,11},{10,... | collective-permute-start | bytes 98312 | tf_op jit(solution)/shard_map/ppermute | solution.py:132
  18.1 4.3 %collective-permute-start.2 = (bf16[16,2,2,256]{3,2,1,0:T(2,128)(2,1)S(1)}, bf16[16,2,2,256]{3,2,1,0:T(2,128)(2,1)S(1)}, u32[]{:S(2)}, u32[]{:S(2)}) collective-permute-start(bf16[16,2,2,256]{3,2,1,0:T(2,128)(2,1)S(1)} %get-tuple-element.16), channel_id=1, source_target_pairs={{0,3},{1,0},{2,1},{3,2},{4,7},{5,4},{6,5},{7,6},{8,11},{9,8},{10,9... | collective-permute-start | bytes 98312 | tf_op jit(solution)/shard_map/ppermute | solution.py:132
  22.6 6.9 %collective-permute-start.3 = (bf16[16,16,256]{2,1,0:T(8,128)(2,1)S(1)}, bf16[16,16,256]{2,1,0:T(8,128)(2,1)S(1)}, u32[]{:S(2)}, u32[]{:S(2)}) collective-permute-start(bf16[16,16,256]{2,1,0:T(8,128)(2,1)S(1)} %bitcast.72), channel_id=1, source_target_pairs={{4,0},{8,4},{12,8},{16,12},{20,16},{24,20},{28,24},{5,1},{9,5},{13... | collective-permute-start | bytes 393224 | tf_op jit(solution)/shard_map/ppermute | solution.py:142
  23.9 9.3 %collective-permute-start.4 = (bf16[16,16,256]{2,1,0:T(8,128)(2,1)S(1)}, bf16[16,16,256]{2,1,0:T(8,128)(2,1)S(1)}, u32[]{:S(2)}, u32[]{:S(2)}) collective-permute-start(bf16[16,16,256]{2,1,0:T(8,128)(2,1)S(1)} %bitcast.73), channel_id=1, source_target_pairs={{8,0},{12,4},{16,8},{20,12},{24,16},{28,20},{9,1},{13,5},{17,9},{2... | collective-permute-start | bytes 393224 | tf_op jit(solution)/shard_map/ppermute | solution.py:142
  25.3 10.7 %collective-permute-start.5 = (bf16[16,16,256]{2,1,0:T(8,128)(2,1)S(1)}, bf16[16,16,256]{2,1,0:T(8,128)(2,1)S(1)}, u32[]{:S(2)}, u32[]{:S(2)}) collective-permute-start(bf16[16,16,256]{2,1,0:T(8,128)(2,1)S(1)} %bitcast.74), channel_id=1, source_target_pairs={{12,0},{16,4},{20,8},{24,12},{28,16},{13,1},{17,5},{21,9},{25,13},... | collective-permute-start | bytes 393224 | tf_op jit(solution)/shard_map/ppermute | solution.py:142
  26.6 24.6 %collective-permute-start.6 = (bf16[16,16,256]{2,1,0:T(8,128)(2,1)S(1)}, bf16[16,16,256]{2,1,0:T(8,128)(2,1)S(1)}, u32[]{:S(2)}, u32[]{:S(2)}) collective-permute-start(bf16[16,16,256]{2,1,0:T(8,128)(2,1)S(1)} %bitcast.75), channel_id=1, source_target_pairs={{16,0},{20,4},{24,8},{28,12},{17,1},{21,5},{25,9},{29,13},{18,2},{... | collective-permute-start | bytes 393224 | tf_op jit(solution)/shard_map/ppermute | solution.py:142
  27.9 25.7 %collective-permute-start.7 = (bf16[16,16,256]{2,1,0:T(8,128)(2,1)S(1)}, bf16[16,16,256]{2,1,0:T(8,128)(2,1)S(1)}, u32[]{:S(2)}, u32[]{:S(2)}) collective-permute-start(bf16[16,16,256]{2,1,0:T(8,128)(2,1)S(1)} %bitcast.76), channel_id=1, source_target_pairs={{20,0},{24,4},{28,8},{21,1},{25,5},{29,9},{22,2},{26,6},{30,10},{2... | collective-permute-start | bytes 393224 | tf_op jit(solution)/shard_map/ppermute | solution.py:142
  29.5 24.1 %collective-permute-start.8 = (bf16[16,16,256]{2,1,0:T(8,128)(2,1)S(1)}, bf16[16,16,256]{2,1,0:T(8,128)(2,1)S(1)}, u32[]{:S(2)}, u32[]{:S(2)}) collective-permute-start(bf16[16,16,256]{2,1,0:T(8,128)(2,1)S(1)} %bitcast.77), channel_id=1, source_target_pairs={{24,0},{28,4},{25,1},{29,5},{26,2},{30,6},{27,3},{31,7}} | collective-permute-start | bytes 393224 | tf_op jit(solution)/shard_map/ppermute | solution.py:142
  33.3 20.3 %collective-permute-start.9 = (bf16[16,16,256]{2,1,0:T(8,128)(2,1)S(1)}, bf16[16,16,256]{2,1,0:T(8,128)(2,1)S(1)}, u32[]{:S(2)}, u32[]{:S(2)}) collective-permute-start(bf16[16,16,256]{2,1,0:T(8,128)(2,1)S(1)} %bitcast.78), channel_id=1, source_target_pairs={{28,0},{29,1},{30,2},{31,3}} | collective-permute-start | bytes 393224 | tf_op jit(solution)/shard_map/ppermute | solution.py:142
  57.9 13.8 %collective-permute-start.11 = (bf16[32,2,16,256]{3,2,1,0:T(8,128)(2,1)S(1)}, bf16[32,2,16,256]{3,2,1,0:T(8,128)(2,1)S(1)}, u32[]{:S(2)}, u32[]{:S(2)}) collective-permute-start(bf16[32,2,16,256]{3,2,1,0:T(8,128)(2,1)S(1)} %convert_element_type.82), channel_id=1, source_target_pairs={{0,2},{1,3},{2,0},{3,1},{4,6},{5,7},{6,4},{7,5},{8,10},{9,11},{10,... | collective-permute-start | bytes 1572872 | tf_op jit(solution)/shard_map/ppermute | solution.py:162
  62.9 17.9 %collective-permute-start.12 = (bf16[32,2,16,256]{3,2,1,0:T(8,128)(2,1)S(1)}, bf16[32,2,16,256]{3,2,1,0:T(8,128)(2,1)S(1)}, u32[]{:S(2)}, u32[]{:S(2)}) collective-permute-start(bf16[32,2,16,256]{3,2,1,0:T(8,128)(2,1)S(1)} %convert_element_type.83), channel_id=1, source_target_pairs={{0,3},{1,0},{2,1},{3,2},{4,7},{5,4},{6,5},{7,6},{8,11},{9,8},{10,9... | collective-permute-start | bytes 1572872 | tf_op jit(solution)/shard_map/ppermute | solution.py:162
  66.9 14.3 %collective-permute-start.10 = (bf16[32,2,16,256]{3,2,1,0:T(8,128)(2,1)S(1)}, bf16[32,2,16,256]{3,2,1,0:T(8,128)(2,1)S(1)}, u32[]{:S(2)}, u32[]{:S(2)}) collective-permute-start(bf16[32,2,16,256]{3,2,1,0:T(8,128)(2,1)S(1)} %convert_element_type.79), channel_id=1, source_target_pairs={{0,1},{1,2},{2,3},{3,0},{4,5},{5,6},{6,7},{7,4},{8,9},{9,10},{10,1... | collective-permute-start | bytes 1572872 | tf_op jit(solution)/shard_map/ppermute | solution.py:162

commit v28 on v27

--- a/solution.py
+++ b/solution.py
@@ -152,7 +152,8 @@
     inverse = inverse_table(kept_bins)
     norm_scale = 0.5 / math.sqrt(windows * bin_count)
     lagged = None
-    for shift in list(range(1, gy_count)) + [0]:
+    far_shift = gy_count // 2
+    for shift in [far_shift] + [s for s in range(1, gy_count) if s != far_shift] + [0]:
         dest = lax.rem(me + shift, gy_count)
         part = cross_spectra(
             padded, lax.dynamic_slice_in_dim(offsets, dest * off_dev, off_dev), base, ch_dev

time: 83 us -> 85 us (1.024)
  starting transfers between devices: 15.2 us -> 16.4 us
  waiting for transfers between devices: 30.4 us -> 31.3 us
    ppermute x3, starting transfers between devices: 1.68 us -> 2.92 us  [local(): part = lax.ppermute(part, 'gy', perm=pairs)]
    ppermute x3, waiting for transfers between devices: 8.63 us -> 9.57 us  [local(): part = lax.ppermute(part, 'gy', perm=pairs)]
where the time goes in v28:
time: 85 us; the launch traced here: 84.7 us
  waiting for transfers between devices  31.3 us (37%)
  starting transfers between devices  16.4 us (19%)
  Pallas kernels  15.3 us (18%)
  other arithmetic  10.9 us (13%)
  local copies, waits for them, and re-layouts  5.24 us (6%)
  matrix products  5.04 us (6%)
    ppermute x7, waiting for transfers between devices, local(): blocks.append(lax.ppermute(rows_white, 'gx', perm=pairs))  21.8 us
    pallas_call x4, Pallas kernels, cross_spectra(): pl.pallas_call(kernel, grid_spec=pltpu.PrefetchScalarGridSpec(num_scalar_...  15.3 us
    ppermute x3, waiting for transfers between devices, local(): part = lax.ppermute(part, 'gy', perm=pairs)  9.57 us
    ppermute x7, starting transfers between devices, local(): blocks.append(lax.ppermute(rows_white, 'gx', perm=pairs))  9.02 us
    ppermute x3, starting transfers between devices, local(): lax.ppermute(piece, 'gy', perm=[(src, (src + shift) % gy_count) for src i...  4.46 us
    another operation x2, other arithmetic  4.39 us
    ppermute x3, starting transfers between devices, local(): part = lax.ppermute(part, 'gy', perm=pairs)  2.92 us
    dot_general x4, matrix products, local(): jnp.einsum('opck,pkl->ocl', part, rows, preferred_element_type=jnp.float32)  2.58 us
  transfers between devices with their start and end apart: 13, of which 6 were waited for; matrix products, arithmetic and copies ran while one was open for 5% of the time, Pallas kernels for 14%

profile of v28, /device:TPU:0, one launch (start us, length us, event | category | flops | bytes accessed | tf_op | source)
XLA Modules:
  0.0 84.7 jit_solution(17116313977151566092)
XLA Ops:
  0.0 1.2 %fusion.52 = (f32[32,1024]{1,0:T(8,128)S(1)}, f32[32,1024]{1,0:T(8,128)S(1)}) fusion(s32[1024]{0:T(1024)} %param.4), kind=kLoop, calls=%fused_computation.87 | loop fusion | flops 458752 | bytes 266240 | tf_op jit(solution)/shard_map/cos | solution.py:89
  1.2 0.7 add_select_fusion.5
  1.9 1.8 %fusion.41 = (f32[64,1024]{1,0:T(8,128)S(1)}, f32[64,1024]{1,0:T(8,128)S(1)}) fusion(s32[1024]{0:T(1024)} %param.4, s32[64]{0:T(128)S(1)} %iota_multiply_fusion), kind=kLoop, calls=%fused_computation.70 | loop fusion | flops 917504 | bytes 528640 | tf_op jit(solution)/shard_map/cos | solution.py:89
  3.7 1.2 %reshape_reshape.3 = bf16[128,2048]{1,0:T(8,128)(2,1)S(1)} reshape(bf16[16,2,8192]{2,1,0:T(2,128)(2,1)} %param.3) | data formatting | bytes 1048576 | tf_op jit(solution)/shard_map/reshape;reshape | solution.py:102
  4.9 3.7 %subtract_convert_fusion = (bf16[64,32,1024]{2,1,0:T(8,128)(2,1)S(1)}, bf16[64,32,1024]{2,1,0:T(8,128)(2,1)S(1)}) fusion(f32[64,1024]{1,0:T(8,128)S(1)} %get-tuple-element.20, f32[32,1024]{1,0:T(8,128)S(1)} %get-tuple-element.26, f32[64,1024]{1,0:T(8,128)S(1)} %get-tuple-element.19, f32[32,1024]{1,0:T(8,128)S(1)} %get-tuple-element.25), kind=kLoop, calls=%fused_computation.5 | loop fusion | flops 18874368 | bytes 9175040 | tf_op jit(solution)/shard_map/convert.7
  8.5 2.5 %fusion.4 = f32[128,2048]{0,1:T(8,128)S(1)} fusion(bf16[128,2048]{1,0:T(8,128)(2,1)S(1)} %reshape_reshape.3, bf16[2048,1024]{1,0:T(8,128)(2,1)S(1)} %bitcast.69, bf16[2048,1024]{1,0:T(8,128)(2,1)S(1)} %bitcast.68), kind=kOutput, calls=%fused_computation.14 | convolution fusion | flops 1090519040 | bytes 9961472 | tf_op jit(solution)/shard_map/dot_general | solution.py:101
  11.0 0.3 copy.4
  11.3 0.9 %reshape.439 = f32[32,4,2,1024]{3,2,1,0:T(2,128)S(1)} reshape(f32[128,2048]{1,0:T(8,128)S(1)} %copy.4) | data formatting | bytes 2097152 | tf_op jit(solution)/shard_map/reshape | solution.py:105
  12.2 1.2 %fusion.68 = (f32[32,4,1,1024]{3,2,1,0:T(1,128)S(1)}, f32[32,4,1,1024]{3,2,1,0:T(1,128)S(1)}) fusion(f32[32,4,2,1024]{3,2,1,0:T(2,128)S(1)} %reshape.439), kind=kLoop, calls=%fused_computation.126 | loop fusion | bytes 2097152 | tf_op jit(solution)/shard_map/slice | solution.py:112
  13.4 0.2 cosine_round-nearest-even_fusion
  13.6 0.8 fusion.25
  14.3 0.1 multiply_reduce_fusion
  14.5 0.2 concatenate.18
  14.8 0.2 multiply_convert_fusion
  15.0 0.1 constant_dynamic-slice_fusion.3
  15.1 0.5 collective-permute-start
  15.6 2.6 %collective-permute-start.1 = (bf16[16,2,2,256]{3,2,1,0:T(2,128)(2,1)S(1)}, bf16[16,2,2,256]{3,2,1,0:T(2,128)(2,1)S(1)}, u32[]{:S(2)}, u32[]{:S(2)}) collective-permute-start(bf16[16,2,2,256]{3,2,1,0:T(2,128)(2,1)S(1)} %get-tuple-element.17), channel_id=1, source_target_pairs={{0,2},{1,3},{2,0},{3,1},{4,6},{5,7},{6,4},{7,5},{8,10},{9,11},{10,... | collective-permute-start | bytes 98312 | tf_op jit(solution)/shard_map/ppermute | solution.py:132
  18.1 1.4 %collective-permute-start.2 = (bf16[16,2,2,256]{3,2,1,0:T(2,128)(2,1)S(1)}, bf16[16,2,2,256]{3,2,1,0:T(2,128)(2,1)S(1)}, u32[]{:S(2)}, u32[]{:S(2)}) collective-permute-start(bf16[16,2,2,256]{3,2,1,0:T(2,128)(2,1)S(1)} %get-tuple-element.16), channel_id=1, source_target_pairs={{0,3},{1,0},{2,1},{3,2},{4,7},{5,4},{6,5},{7,6},{8,11},{9,8},{10,9... | collective-permute-start | bytes 98312 | tf_op jit(solution)/shard_map/ppermute | solution.py:132
  19.5 0.5 fusion.50
  20.1 0.3 fusion.54
  20.4 0.7 negate_convert_fusion.1
  21.3 0.5 copy.7
  21.8 0.5 copy.8
  22.4 0.2 maximum_bitcast_fusion
  22.6 1.3 %collective-permute-start.3 = (bf16[16,16,256]{2,1,0:T(8,128)(2,1)S(1)}, bf16[16,16,256]{2,1,0:T(8,128)(2,1)S(1)}, u32[]{:S(2)}, u32[]{:S(2)}) collective-permute-start(bf16[16,16,256]{2,1,0:T(8,128)(2,1)S(1)} %bitcast.72), channel_id=1, source_target_pairs={{4,0},{8,4},{12,8},{16,12},{20,16},{24,20},{28,24},{5,1},{9,5},{13... | collective-permute-start | bytes 393224 | tf_op jit(solution)/shard_map/ppermute | solution.py:142
  23.9 1.3 %collective-permute-start.4 = (bf16[16,16,256]{2,1,0:T(8,128)(2,1)S(1)}, bf16[16,16,256]{2,1,0:T(8,128)(2,1)S(1)}, u32[]{:S(2)}, u32[]{:S(2)}) collective-permute-start(bf16[16,16,256]{2,1,0:T(8,128)(2,1)S(1)} %bitcast.73), channel_id=1, source_target_pairs={{8,0},{12,4},{16,8},{20,12},{24,16},{28,20},{9,1},{13,5},{17,9},{2... | collective-permute-start | bytes 393224 | tf_op jit(solution)/shard_map/ppermute | solution.py:142
  25.3 1.3 %collective-permute-start.5 = (bf16[16,16,256]{2,1,0:T(8,128)(2,1)S(1)}, bf16[16,16,256]{2,1,0:T(8,128)(2,1)S(1)}, u32[]{:S(2)}, u32[]{:S(2)}) collective-permute-start(bf16[16,16,256]{2,1,0:T(8,128)(2,1)S(1)} %bitcast.74), channel_id=1, source_target_pairs={{12,0},{16,4},{20,8},{24,12},{28,16},{13,1},{17,5},{21,9},{25,13},... | collective-permute-start | bytes 393224 | tf_op jit(solution)/shard_map/ppermute | solution.py:142
  26.6 1.3 %collective-permute-start.6 = (bf16[16,16,256]{2,1,0:T(8,128)(2,1)S(1)}, bf16[16,16,256]{2,1,0:T(8,128)(2,1)S(1)}, u32[]{:S(2)}, u32[]{:S(2)}) collective-permute-start(bf16[16,16,256]{2,1,0:T(8,128)(2,1)S(1)} %bitcast.75), channel_id=1, source_target_pairs={{16,0},{20,4},{24,8},{28,12},{17,1},{21,5},{25,9},{29,13},{18,2},{... | collective-permute-start | bytes 393224 | tf_op jit(solution)/shard_map/ppermute | solution.py:142
  27.9 1.3 %collective-permute-start.7 = (bf16[16,16,256]{2,1,0:T(8,128)(2,1)S(1)}, bf16[16,16,256]{2,1,0:T(8,128)(2,1)S(1)}, u32[]{:S(2)}, u32[]{:S(2)}) collective-permute-start(bf16[16,16,256]{2,1,0:T(8,128)(2,1)S(1)} %bitcast.76), channel_id=1, source_target_pairs={{20,0},{24,4},{28,8},{21,1},{25,5},{29,9},{22,2},{26,6},{30,10},{2... | collective-permute-start | bytes 393224 | tf_op jit(solution)/shard_map/ppermute | solution.py:142
  29.2 0.3 collective-permute-done.3
  29.5 1.3 %collective-permute-start.8 = (bf16[16,16,256]{2,1,0:T(8,128)(2,1)S(1)}, bf16[16,16,256]{2,1,0:T(8,128)(2,1)S(1)}, u32[]{:S(2)}, u32[]{:S(2)}) collective-permute-start(bf16[16,16,256]{2,1,0:T(8,128)(2,1)S(1)} %bitcast.77), channel_id=1, source_target_pairs={{24,0},{28,4},{25,1},{29,5},{26,2},{30,6},{27,3},{31,7}} | collective-permute-start | bytes 393224 | tf_op jit(solution)/shard_map/ppermute | solution.py:142
  30.8 2.5 %collective-permute-done.4 = bf16[16,16,256]{2,1,0:T(8,128)(2,1)S(1)} collective-permute-done((bf16[16,16,256]{2,1,0:T(8,128)(2,1)S(1)}, bf16[16,16,256]{2,1,0:T(8,128)(2,1)S(1)}, u32[]{:S(2)}, u32[]{:S(2)}) %collective-permute-start.4) | collective-permute-done | bytes 131104 | tf_op jit(solution)/shard_map/ppermute | solution.py:142
  33.3 1.3 %collective-permute-start.9 = (bf16[16,16,256]{2,1,0:T(8,128)(2,1)S(1)}, bf16[16,16,256]{2,1,0:T(8,128)(2,1)S(1)}, u32[]{:S(2)}, u32[]{:S(2)}) collective-permute-start(bf16[16,16,256]{2,1,0:T(8,128)(2,1)S(1)} %bitcast.78), channel_id=1, source_target_pairs={{28,0},{29,1},{30,2},{31,3}} | collective-permute-start | bytes 393224 | tf_op jit(solution)/shard_map/ppermute | solution.py:142
  34.6 1.4 %collective-permute-done.5 = bf16[16,16,256]{2,1,0:T(8,128)(2,1)S(1)} collective-permute-done((bf16[16,16,256]{2,1,0:T(8,128)(2,1)S(1)}, bf16[16,16,256]{2,1,0:T(8,128)(2,1)S(1)}, u32[]{:S(2)}, u32[]{:S(2)}) %collective-permute-start.5) | collective-permute-done | bytes 131104 | tf_op jit(solution)/shard_map/ppermute | solution.py:142
  36.0 15.2 %collective-permute-done.6 = bf16[16,16,256]{2,1,0:T(8,128)(2,1)S(1)} collective-permute-done((bf16[16,16,256]{2,1,0:T(8,128)(2,1)S(1)}, bf16[16,16,256]{2,1,0:T(8,128)(2,1)S(1)}, u32[]{:S(2)}, u32[]{:S(2)}) %collective-permute-start.6) | collective-permute-done | bytes 131104 | tf_op jit(solution)/shard_map/ppermute | solution.py:142
  51.1 2.4 %collective-permute-done.7 = bf16[16,16,256]{2,1,0:T(8,128)(2,1)S(1)} collective-permute-done((bf16[16,16,256]{2,1,0:T(8,128)(2,1)S(1)}, bf16[16,16,256]{2,1,0:T(8,128)(2,1)S(1)}, u32[]{:S(2)}, u32[]{:S(2)}) %collective-permute-start.7) | collective-permute-done | bytes 131104 | tf_op jit(solution)/shard_map/ppermute | solution.py:142
  53.6 0.3 convert_element_type.78.white_ref
  54.0 3.8 %shard_map.38 = f32[32,2,16,256]{3,2,1,0:T(8,128)S(1)} custom-call(s32[32]{0:T(128)S(1)} %get-tuple-element.30.offsets_ref, s32[1]{0:T(128)} %constant.111.clone.1.base_ref, f32[144,16,256]{2,1,0:T(8,128)S(1)} %convert_element_type.78.white_ref), custom_call_target="tpu_custom_call" | custom-call | flops 2147483648 | bytes 3407872 | tf_op jit(solution)/shard_map/pallas_call | solution.py:59
  58.0 3.8 %shard_map.39 = f32[32,2,16,256]{3,2,1,0:T(8,128)S(1)} custom-call(s32[32]{0:T(128)S(1)} %get-tuple-element.32.offsets_ref, s32[1]{0:T(128)} %constant.111.clone.1.base_ref, f32[144,16,256]{2,1,0:T(8,128)S(1)} %convert_element_type.78.white_ref), custom_call_target="tpu_custom_call" | custom-call | flops 2147483648 | bytes 3407872 | tf_op jit(solution)/shard_map/pallas_call | solution.py:59
  61.9 1.8 %collective-permute-start.12 = (bf16[32,2,16,256]{3,2,1,0:T(8,128)(2,1)S(1)}, bf16[32,2,16,256]{3,2,1,0:T(8,128)(2,1)S(1)}, u32[]{:S(2)}, u32[]{:S(2)}) collective-permute-start(bf16[32,2,16,256]{3,2,1,0:T(8,128)(2,1)S(1)} %convert_element_type.83), channel_id=1, source_target_pairs={{0,3},{1,0},{2,1},{3,2},{4,7},{5,4},{6,5},{7,6},{8,11},{9,8},{10,9... | collective-permute-start | bytes 1572872 | tf_op jit(solution)/shard_map/ppermute | solution.py:163
  63.7 3.8 %shard_map.37 = f32[32,2,16,256]{3,2,1,0:T(8,128)S(1)} custom-call(s32[32]{0:T(128)S(1)} %get-tuple-element.29.offsets_ref, s32[1]{0:T(128)} %constant.111.clone.1.base_ref, f32[144,16,256]{2,1,0:T(8,128)S(1)} %convert_element_type.78.white_ref), custom_call_target="tpu_custom_call" | custom-call | flops 2147483648 | bytes 3407872 | tf_op jit(solution)/shard_map/pallas_call | solution.py:59
  67.6 1.1 %collective-permute-start.10 = (bf16[32,2,16,256]{3,2,1,0:T(8,128)(2,1)S(1)}, bf16[32,2,16,256]{3,2,1,0:T(8,128)(2,1)S(1)}, u32[]{:S(2)}, u32[]{:S(2)}) collective-permute-start(bf16[32,2,16,256]{3,2,1,0:T(8,128)(2,1)S(1)} %convert_element_type.79), channel_id=1, source_target_pairs={{0,2},{1,3},{2,0},{3,1},{4,6},{5,7},{6,4},{7,5},{8,10},{9,11},{10,... | collective-permute-start | bytes 1572872 | tf_op jit(solution)/shard_map/ppermute | solution.py:163
  68.7 3.8 %shard_map.40 = f32[32,2,16,256]{3,2,1,0:T(8,128)S(1)} custom-call(s32[32]{0:T(128)S(1)} %get-tuple-element.31.offsets_ref, s32[1]{0:T(128)} %constant.111.clone.1.base_ref, f32[144,16,256]{2,1,0:T(8,128)S(1)} %convert_element_type.78.white_ref), custom_call_target="tpu_custom_call" | custom-call | flops 2147483648 | bytes 3407872 | tf_op jit(solution)/shard_map/pallas_call | solution.py:59
  72.5 0.4 convolution_bitcast_fusion
  72.9 0.4 convolution_bitcast_fusion.2
  73.4 0.4 convolution_bitcast_fusion.1
  73.8 9.6 %collective-permute-done.10 = bf16[32,2,16,256]{3,2,1,0:T(8,128)(2,1)S(1)} collective-permute-done((bf16[32,2,16,256]{3,2,1,0:T(8,128)(2,1)S(1)}, bf16[32,2,16,256]{3,2,1,0:T(8,128)(2,1)S(1)}, u32[]{:S(2)}, u32[]{:S(2)}) %collective-permute-start.10) | collective-permute-done | bytes 524320 | tf_op jit(solution)/shard_map/ppermute | solution.py:163
  83.4 1.3 %fusion.11 = bf16[32,16,512]{2,1,0:T(8,128)(2,1)} fusion(f32[32,16,512]{2,1,0:T(8,128)S(1)} %convolution_bitcast_fusion, f32[32,16,512]{2,1,0:T(8,128)S(1)} %convolution_bitcast_fusion.1, f32[32,16,512]{2,1,0:T(8,128)S(1)} %convolution_bitcast_fusion.2, bf16[32,2,16,256]{3,2,1,0:T(8,128)(2,1)S(1)} %collective-permute-done.10, s32[]{:T(128)S(6)} %select_n.109, ...), kind=kOutput, calls=%fused_computation.25 | convolution fusion | flops 270794752 | bytes 6291460 | tf_op jit(solution)/shard_map/opck,pkl->ocl/dot_general | solution.py:166
  (30 shorter events, 0.6 us)
Async XLA Ops:
  13.4 6.1 %copy-start = (s32[1024]{0:T(1024)S(1)}, s32[1024]{0:T(1024)}, u32[]{:S(2)}) copy-start(s32[1024]{0:T(1024)} %param.4) | copy-start | bytes 12292
  14.5 6.7 %copy-start.1 = (s32[128]{0:T(128)S(1)}, s32[128]{0:T(128)}, u32[]{:S(2)}) copy-start(s32[128]{0:T(128)} %param.5) | copy-start | bytes 1540
  15.1 7.3 %collective-permute-start = (bf16[16,2,2,256]{3,2,1,0:T(2,128)(2,1)S(1)}, bf16[16,2,2,256]{3,2,1,0:T(2,128)(2,1)S(1)}, u32[]{:S(2)}, u32[]{:S(2)}) collective-permute-start(bf16[16,2,2,256]{3,2,1,0:T(2,128)(2,1)S(1)} %get-tuple-element.18), channel_id=1, source_target_pairs={{0,1},{1,2},{2,3},{3,0},{4,5},{5,6},{6,7},{7,4},{8,9},{9,10},{10,1... | collective-permute-start | bytes 98312 | tf_op jit(solution)/shard_map/ppermute | solution.py:132
  15.6 6.8 %collective-permute-start.1 = (bf16[16,2,2,256]{3,2,1,0:T(2,128)(2,1)S(1)}, bf16[16,2,2,256]{3,2,1,0:T(2,128)(2,1)S(1)}, u32[]{:S(2)}, u32[]{:S(2)}) collective-permute-start(bf16[16,2,2,256]{3,2,1,0:T(2,128)(2,1)S(1)} %get-tuple-element.17), channel_id=1, source_target_pairs={{0,2},{1,3},{2,0},{3,1},{4,6},{5,7},{6,4},{7,5},{8,10},{9,11},{10,... | collective-permute-start | bytes 98312 | tf_op jit(solution)/shard_map/ppermute | solution.py:132
  18.1 4.3 %collective-permute-start.2 = (bf16[16,2,2,256]{3,2,1,0:T(2,128)(2,1)S(1)}, bf16[16,2,2,256]{3,2,1,0:T(2,128)(2,1)S(1)}, u32[]{:S(2)}, u32[]{:S(2)}) collective-permute-start(bf16[16,2,2,256]{3,2,1,0:T(2,128)(2,1)S(1)} %get-tuple-element.16), channel_id=1, source_target_pairs={{0,3},{1,0},{2,1},{3,2},{4,7},{5,4},{6,5},{7,6},{8,11},{9,8},{10,9... | collective-permute-start | bytes 98312 | tf_op jit(solution)/shard_map/ppermute | solution.py:132
  22.6 6.9 %collective-permute-start.3 = (bf16[16,16,256]{2,1,0:T(8,128)(2,1)S(1)}, bf16[16,16,256]{2,1,0:T(8,128)(2,1)S(1)}, u32[]{:S(2)}, u32[]{:S(2)}) collective-permute-start(bf16[16,16,256]{2,1,0:T(8,128)(2,1)S(1)} %bitcast.72), channel_id=1, source_target_pairs={{4,0},{8,4},{12,8},{16,12},{20,16},{24,20},{28,24},{5,1},{9,5},{13... | collective-permute-start | bytes 393224 | tf_op jit(solution)/shard_map/ppermute | solution.py:142
  23.9 9.3 %collective-permute-start.4 = (bf16[16,16,256]{2,1,0:T(8,128)(2,1)S(1)}, bf16[16,16,256]{2,1,0:T(8,128)(2,1)S(1)}, u32[]{:S(2)}, u32[]{:S(2)}) collective-permute-start(bf16[16,16,256]{2,1,0:T(8,128)(2,1)S(1)} %bitcast.73), channel_id=1, source_target_pairs={{8,0},{12,4},{16,8},{20,12},{24,16},{28,20},{9,1},{13,5},{17,9},{2... | collective-permute-start | bytes 393224 | tf_op jit(solution)/shard_map/ppermute | solution.py:142
  25.3 10.7 %collective-permute-start.5 = (bf16[16,16,256]{2,1,0:T(8,128)(2,1)S(1)}, bf16[16,16,256]{2,1,0:T(8,128)(2,1)S(1)}, u32[]{:S(2)}, u32[]{:S(2)}) collective-permute-start(bf16[16,16,256]{2,1,0:T(8,128)(2,1)S(1)} %bitcast.74), channel_id=1, source_target_pairs={{12,0},{16,4},{20,8},{24,12},{28,16},{13,1},{17,5},{21,9},{25,13},... | collective-permute-start | bytes 393224 | tf_op jit(solution)/shard_map/ppermute | solution.py:142
  26.6 24.6 %collective-permute-start.6 = (bf16[16,16,256]{2,1,0:T(8,128)(2,1)S(1)}, bf16[16,16,256]{2,1,0:T(8,128)(2,1)S(1)}, u32[]{:S(2)}, u32[]{:S(2)}) collective-permute-start(bf16[16,16,256]{2,1,0:T(8,128)(2,1)S(1)} %bitcast.75), channel_id=1, source_target_pairs={{16,0},{20,4},{24,8},{28,12},{17,1},{21,5},{25,9},{29,13},{18,2},{... | collective-permute-start | bytes 393224 | tf_op jit(solution)/shard_map/ppermute | solution.py:142
  27.9 25.7 %collective-permute-start.7 = (bf16[16,16,256]{2,1,0:T(8,128)(2,1)S(1)}, bf16[16,16,256]{2,1,0:T(8,128)(2,1)S(1)}, u32[]{:S(2)}, u32[]{:S(2)}) collective-permute-start(bf16[16,16,256]{2,1,0:T(8,128)(2,1)S(1)} %bitcast.76), channel_id=1, source_target_pairs={{20,0},{24,4},{28,8},{21,1},{25,5},{29,9},{22,2},{26,6},{30,10},{2... | collective-permute-start | bytes 393224 | tf_op jit(solution)/shard_map/ppermute | solution.py:142
  29.5 24.1 %collective-permute-start.8 = (bf16[16,16,256]{2,1,0:T(8,128)(2,1)S(1)}, bf16[16,16,256]{2,1,0:T(8,128)(2,1)S(1)}, u32[]{:S(2)}, u32[]{:S(2)}) collective-permute-start(bf16[16,16,256]{2,1,0:T(8,128)(2,1)S(1)} %bitcast.77), channel_id=1, source_target_pairs={{24,0},{28,4},{25,1},{29,5},{26,2},{30,6},{27,3},{31,7}} | collective-permute-start | bytes 393224 | tf_op jit(solution)/shard_map/ppermute | solution.py:142
  33.3 20.3 %collective-permute-start.9 = (bf16[16,16,256]{2,1,0:T(8,128)(2,1)S(1)}, bf16[16,16,256]{2,1,0:T(8,128)(2,1)S(1)}, u32[]{:S(2)}, u32[]{:S(2)}) collective-permute-start(bf16[16,16,256]{2,1,0:T(8,128)(2,1)S(1)} %bitcast.78), channel_id=1, source_target_pairs={{28,0},{29,1},{30,2},{31,3}} | collective-permute-start | bytes 393224 | tf_op jit(solution)/shard_map/ppermute | solution.py:142
  57.9 15.0 %collective-permute-start.11 = (bf16[32,2,16,256]{3,2,1,0:T(8,128)(2,1)S(1)}, bf16[32,2,16,256]{3,2,1,0:T(8,128)(2,1)S(1)}, u32[]{:S(2)}, u32[]{:S(2)}) collective-permute-start(bf16[32,2,16,256]{3,2,1,0:T(8,128)(2,1)S(1)} %convert_element_type.82), channel_id=1, source_target_pairs={{0,1},{1,2},{2,3},{3,0},{4,5},{5,6},{6,7},{7,4},{8,9},{9,10},{10,1... | collective-permute-start | bytes 1572872 | tf_op jit(solution)/shard_map/ppermute | solution.py:163
  61.9 11.5 %collective-permute-start.12 = (bf16[32,2,16,256]{3,2,1,0:T(8,128)(2,1)S(1)}, bf16[32,2,16,256]{3,2,1,0:T(8,128)(2,1)S(1)}, u32[]{:S(2)}, u32[]{:S(2)}) collective-permute-start(bf16[32,2,16,256]{3,2,1,0:T(8,128)(2,1)S(1)} %convert_element_type.83), channel_id=1, source_target_pairs={{0,3},{1,0},{2,1},{3,2},{4,7},{5,4},{6,5},{7,6},{8,11},{9,8},{10,9... | collective-permute-start | bytes 1572872 | tf_op jit(solution)/shard_map/ppermute | solution.py:163
  67.6 15.8 %collective-permute-start.10 = (bf16[32,2,16,256]{3,2,1,0:T(8,128)(2,1)S(1)}, bf16[32,2,16,256]{3,2,1,0:T(8,128)(2,1)S(1)}, u32[]{:S(2)}, u32[]{:S(2)}) collective-permute-start(bf16[32,2,16,256]{3,2,1,0:T(8,128)(2,1)S(1)} %convert_element_type.79), channel_id=1, source_target_pairs={{0,2},{1,3},{2,0},{3,1},{4,6},{5,7},{6,4},{7,5},{8,10},{9,11},{10,... | collective-permute-start | bytes 1572872 | tf_op jit(solution)/shard_map/ppermute | solution.py:163

commit v29 on v24

--- a/solution.py
+++ b/solution.py
@@ -70,7 +70,7 @@
         out_shape=jax.ShapeDtypeStruct((band_span, 2, own_count, bins), jnp.bfloat16),
         compiler_params=pltpu.CompilerParams(vmem_limit_bytes=48 * 1024 * 1024),
         cost_estimate=pl.CostEstimate(
-            flops=8 * band_span * own_count * rows * bins,
+            flops=1024 * band_span * own_count * rows * bins,
             transcendentals=0,
             bytes_accessed=white_all.size * 4 + band_span * 2 * own_count * bins * 4,
         ),

time: 85.1 us -> 82.7 us (0.972)
  waiting for transfers between devices: 23.7 us -> 31.2 us
  local copies, waits for them, and re-layouts: 8.75 us -> 5.24 us
  other arithmetic: 14.2 us -> 10.7 us
  matrix products: 7.19 us -> 5.03 us
    ppermute x3, waiting for transfers between devices: 1.05 us -> 9.41 us  [local(): part = lax.ppermute(part, 'gy', perm=pairs)]
    another operation x2, other arithmetic: 6.64 us -> 4.39 us
    dot_general x4, matrix products: 4.73 us -> 2.57 us  [local(): jnp.einsum('opck,pkl->ocl', part, rows, preferred_element_type=jnp.float32)]
    sub x1, local copies, waits for them, and re-layouts: 2.29 us -> 0.53 us  [inverse_table(): cos_t = (cos_f * cos_c - sin_f * sin_c).reshape(kept_bins.shape[0], LAGS)]
    neg x1, local copies, waits for them, and re-layouts: 2.28 us -> 0.54 us  [inverse_table(): return jnp.stack([cos_t, -sin_t], axis=0).astype(jnp.bfloat16)]
  transfers between devices with their start and end apart: 13 -> 13, of which waited for: 7 -> 7; matrix products, arithmetic and copies ran while one was open for 16% -> 5% of each run, Pallas kernels for 13% -> 13%
where the time goes in v29:
time: 82.7 us; the launch traced here: 82.2 us
  waiting for transfers between devices  31.2 us (38%)
  starting transfers between devices  15.2 us (18%)
  Pallas kernels  14.5 us (18%)
  other arithmetic  10.7 us (13%)
  local copies, waits for them, and re-layouts  5.24 us (6%)
  matrix products  5.03 us (6%)
    ppermute x7, waiting for transfers between devices, local(): blocks.append(lax.ppermute(rows_white, 'gx', perm=pairs))  21.8 us
    pallas_call x4, Pallas kernels, cross_spectra(): pl.pallas_call(kernel, grid_spec=pltpu.PrefetchScalarGridSpec(num_scalar_...  14.5 us
    ppermute x3, waiting for transfers between devices, local(): part = lax.ppermute(part, 'gy', perm=pairs)  9.41 us
    ppermute x7, starting transfers between devices, local(): blocks.append(lax.ppermute(rows_white, 'gx', perm=pairs))  9.02 us
    ppermute x3, starting transfers between devices, local(): lax.ppermute(piece, 'gy', perm=[(src, (src + shift) % gy_count) for src i...  4.46 us
    another operation x2, other arithmetic  4.39 us
    dot_general x4, matrix products, local(): jnp.einsum('opck,pkl->ocl', part, rows, preferred_element_type=jnp.float32)  2.57 us
    dot_general x1, matrix products, forward_spectra(): jnp.dot(record_rows.reshape(row_count * block_count, block_len), small_ta...  2.46 us
  transfers between devices with their start and end apart: 13, of which 7 were waited for; matrix products, arithmetic and copies ran while one was open for 5% of the time, Pallas kernels for 13%

profile of v29, /device:TPU:0, one launch (start us, length us, event | category | flops | bytes accessed | tf_op | source)
XLA Modules:
  0.0 82.2 jit_solution(9648902967113370241)
XLA Ops:
  0.0 1.2 %fusion.51 = (f32[32,1024]{1,0:T(8,128)S(1)}, f32[32,1024]{1,0:T(8,128)S(1)}) fusion(s32[1024]{0:T(1024)} %param.4), kind=kLoop, calls=%fused_computation.86 | loop fusion | flops 458752 | bytes 266240 | tf_op jit(solution)/shard_map/cos | solution.py:92
  1.2 0.7 add_select_fusion.5
  1.9 1.8 %fusion.40 = (f32[64,1024]{1,0:T(8,128)S(1)}, f32[64,1024]{1,0:T(8,128)S(1)}) fusion(s32[1024]{0:T(1024)} %param.4, s32[64]{0:T(128)S(1)} %iota_multiply_fusion), kind=kLoop, calls=%fused_computation.69 | loop fusion | flops 917504 | bytes 528640 | tf_op jit(solution)/shard_map/cos | solution.py:92
  3.7 1.2 %reshape_reshape.3 = bf16[128,2048]{1,0:T(8,128)(2,1)S(1)} reshape(bf16[16,2,8192]{2,1,0:T(2,128)(2,1)} %param.3) | data formatting | bytes 1048576 | tf_op jit(solution)/shard_map/reshape;reshape | solution.py:105
  4.9 3.7 %subtract_convert_fusion = (bf16[64,32,1024]{2,1,0:T(8,128)(2,1)S(1)}, bf16[64,32,1024]{2,1,0:T(8,128)(2,1)S(1)}) fusion(f32[64,1024]{1,0:T(8,128)S(1)} %get-tuple-element.22, f32[32,1024]{1,0:T(8,128)S(1)} %get-tuple-element.28, f32[64,1024]{1,0:T(8,128)S(1)} %get-tuple-element.21, f32[32,1024]{1,0:T(8,128)S(1)} %get-tuple-element.27), kind=kLoop, calls=%fused_computation.5 | loop fusion | flops 18874368 | bytes 9175040 | tf_op jit(solution)/shard_map/convert.7
  8.5 2.5 %fusion.4 = f32[128,2048]{0,1:T(8,128)S(1)} fusion(bf16[128,2048]{1,0:T(8,128)(2,1)S(1)} %reshape_reshape.3, bf16[2048,1024]{1,0:T(8,128)(2,1)S(1)} %bitcast.70, bf16[2048,1024]{1,0:T(8,128)(2,1)S(1)} %bitcast.69), kind=kOutput, calls=%fused_computation.14 | convolution fusion | flops 1090519040 | bytes 9961472 | tf_op jit(solution)/shard_map/dot_general | solution.py:104
  11.0 0.3 copy.4
  11.3 0.9 %reshape.439 = f32[32,4,2,1024]{3,2,1,0:T(2,128)S(1)} reshape(f32[128,2048]{1,0:T(8,128)S(1)} %copy.4) | data formatting | bytes 2097152 | tf_op jit(solution)/shard_map/reshape | solution.py:108
  12.2 1.2 %fusion.67 = (f32[32,4,1,1024]{3,2,1,0:T(1,128)S(1)}, f32[32,4,1,1024]{3,2,1,0:T(1,128)S(1)}) fusion(f32[32,4,2,1024]{3,2,1,0:T(2,128)S(1)} %reshape.439), kind=kLoop, calls=%fused_computation.125 | loop fusion | bytes 2097152 | tf_op jit(solution)/shard_map/slice | solution.py:115
  13.4 0.2 cosine_round-nearest-even_fusion
  13.6 0.8 fusion.25
  14.3 0.1 multiply_reduce_fusion
  14.5 0.2 concatenate.18
  14.8 0.2 multiply_convert_fusion
  15.1 0.5 collective-permute-start
  15.6 2.6 %collective-permute-start.1 = (bf16[16,2,2,256]{3,2,1,0:T(2,128)(2,1)S(1)}, bf16[16,2,2,256]{3,2,1,0:T(2,128)(2,1)S(1)}, u32[]{:S(2)}, u32[]{:S(2)}) collective-permute-start(bf16[16,2,2,256]{3,2,1,0:T(2,128)(2,1)S(1)} %get-tuple-element.17), channel_id=1, source_target_pairs={{0,2},{1,3},{2,0},{3,1},{4,6},{5,7},{6,4},{7,5},{8,10},{9,11},{10,... | collective-permute-start | bytes 98312 | tf_op jit(solution)/shard_map/ppermute | solution.py:135
  18.1 1.4 %collective-permute-start.2 = (bf16[16,2,2,256]{3,2,1,0:T(2,128)(2,1)S(1)}, bf16[16,2,2,256]{3,2,1,0:T(2,128)(2,1)S(1)}, u32[]{:S(2)}, u32[]{:S(2)}) collective-permute-start(bf16[16,2,2,256]{3,2,1,0:T(2,128)(2,1)S(1)} %get-tuple-element.16), channel_id=1, source_target_pairs={{0,3},{1,0},{2,1},{3,2},{4,7},{5,4},{6,5},{7,6},{8,11},{9,8},{10,9... | collective-permute-start | bytes 98312 | tf_op jit(solution)/shard_map/ppermute | solution.py:135
  19.5 0.5 fusion.49
  20.1 0.3 fusion.53
  20.4 0.7 negate_convert_fusion.1
  21.3 0.5 copy.7
  21.8 0.5 copy.8
  22.4 0.2 maximum_bitcast_fusion
  22.6 1.3 %collective-permute-start.3 = (bf16[16,16,256]{2,1,0:T(8,128)(2,1)S(1)}, bf16[16,16,256]{2,1,0:T(8,128)(2,1)S(1)}, u32[]{:S(2)}, u32[]{:S(2)}) collective-permute-start(bf16[16,16,256]{2,1,0:T(8,128)(2,1)S(1)} %bitcast.73), channel_id=1, source_target_pairs={{4,0},{8,4},{12,8},{16,12},{20,16},{24,20},{28,24},{5,1},{9,5},{13... | collective-permute-start | bytes 393224 | tf_op jit(solution)/shard_map/ppermute | solution.py:145
  23.9 1.3 %collective-permute-start.4 = (bf16[16,16,256]{2,1,0:T(8,128)(2,1)S(1)}, bf16[16,16,256]{2,1,0:T(8,128)(2,1)S(1)}, u32[]{:S(2)}, u32[]{:S(2)}) collective-permute-start(bf16[16,16,256]{2,1,0:T(8,128)(2,1)S(1)} %bitcast.74), channel_id=1, source_target_pairs={{8,0},{12,4},{16,8},{20,12},{24,16},{28,20},{9,1},{13,5},{17,9},{2... | collective-permute-start | bytes 393224 | tf_op jit(solution)/shard_map/ppermute | solution.py:145
  25.3 1.3 %collective-permute-start.5 = (bf16[16,16,256]{2,1,0:T(8,128)(2,1)S(1)}, bf16[16,16,256]{2,1,0:T(8,128)(2,1)S(1)}, u32[]{:S(2)}, u32[]{:S(2)}) collective-permute-start(bf16[16,16,256]{2,1,0:T(8,128)(2,1)S(1)} %bitcast.75), channel_id=1, source_target_pairs={{12,0},{16,4},{20,8},{24,12},{28,16},{13,1},{17,5},{21,9},{25,13},... | collective-permute-start | bytes 393224 | tf_op jit(solution)/shard_map/ppermute | solution.py:145
  26.6 1.3 %collective-permute-start.6 = (bf16[16,16,256]{2,1,0:T(8,128)(2,1)S(1)}, bf16[16,16,256]{2,1,0:T(8,128)(2,1)S(1)}, u32[]{:S(2)}, u32[]{:S(2)}) collective-permute-start(bf16[16,16,256]{2,1,0:T(8,128)(2,1)S(1)} %bitcast.76), channel_id=1, source_target_pairs={{16,0},{20,4},{24,8},{28,12},{17,1},{21,5},{25,9},{29,13},{18,2},{... | collective-permute-start | bytes 393224 | tf_op jit(solution)/shard_map/ppermute | solution.py:145
  27.9 1.3 %collective-permute-start.7 = (bf16[16,16,256]{2,1,0:T(8,128)(2,1)S(1)}, bf16[16,16,256]{2,1,0:T(8,128)(2,1)S(1)}, u32[]{:S(2)}, u32[]{:S(2)}) collective-permute-start(bf16[16,16,256]{2,1,0:T(8,128)(2,1)S(1)} %bitcast.77), channel_id=1, source_target_pairs={{20,0},{24,4},{28,8},{21,1},{25,5},{29,9},{22,2},{26,6},{30,10},{2... | collective-permute-start | bytes 393224 | tf_op jit(solution)/shard_map/ppermute | solution.py:145
  29.2 0.3 collective-permute-done.3
  29.5 1.3 %collective-permute-start.8 = (bf16[16,16,256]{2,1,0:T(8,128)(2,1)S(1)}, bf16[16,16,256]{2,1,0:T(8,128)(2,1)S(1)}, u32[]{:S(2)}, u32[]{:S(2)}) collective-permute-start(bf16[16,16,256]{2,1,0:T(8,128)(2,1)S(1)} %bitcast.78), channel_id=1, source_target_pairs={{24,0},{28,4},{25,1},{29,5},{26,2},{30,6},{27,3},{31,7}} | collective-permute-start | bytes 393224 | tf_op jit(solution)/shard_map/ppermute | solution.py:145
  30.8 2.5 %collective-permute-done.4 = bf16[16,16,256]{2,1,0:T(8,128)(2,1)S(1)} collective-permute-done((bf16[16,16,256]{2,1,0:T(8,128)(2,1)S(1)}, bf16[16,16,256]{2,1,0:T(8,128)(2,1)S(1)}, u32[]{:S(2)}, u32[]{:S(2)}) %collective-permute-start.4) | collective-permute-done | bytes 131104 | tf_op jit(solution)/shard_map/ppermute | solution.py:145
  33.3 1.3 %collective-permute-start.9 = (bf16[16,16,256]{2,1,0:T(8,128)(2,1)S(1)}, bf16[16,16,256]{2,1,0:T(8,128)(2,1)S(1)}, u32[]{:S(2)}, u32[]{:S(2)}) collective-permute-start(bf16[16,16,256]{2,1,0:T(8,128)(2,1)S(1)} %bitcast.79), channel_id=1, source_target_pairs={{28,0},{29,1},{30,2},{31,3}} | collective-permute-start | bytes 393224 | tf_op jit(solution)/shard_map/ppermute | solution.py:145
  34.6 1.4 %collective-permute-done.5 = bf16[16,16,256]{2,1,0:T(8,128)(2,1)S(1)} collective-permute-done((bf16[16,16,256]{2,1,0:T(8,128)(2,1)S(1)}, bf16[16,16,256]{2,1,0:T(8,128)(2,1)S(1)}, u32[]{:S(2)}, u32[]{:S(2)}) %collective-permute-start.5) | collective-permute-done | bytes 131104 | tf_op jit(solution)/shard_map/ppermute | solution.py:145
  36.0 15.2 %collective-permute-done.6 = bf16[16,16,256]{2,1,0:T(8,128)(2,1)S(1)} collective-permute-done((bf16[16,16,256]{2,1,0:T(8,128)(2,1)S(1)}, bf16[16,16,256]{2,1,0:T(8,128)(2,1)S(1)}, u32[]{:S(2)}, u32[]{:S(2)}) %collective-permute-start.6) | collective-permute-done | bytes 131104 | tf_op jit(solution)/shard_map/ppermute | solution.py:145
  51.1 2.4 %collective-permute-done.7 = bf16[16,16,256]{2,1,0:T(8,128)(2,1)S(1)} collective-permute-done((bf16[16,16,256]{2,1,0:T(8,128)(2,1)S(1)}, bf16[16,16,256]{2,1,0:T(8,128)(2,1)S(1)}, u32[]{:S(2)}, u32[]{:S(2)}) %collective-permute-start.7) | collective-permute-done | bytes 131104 | tf_op jit(solution)/shard_map/ppermute | solution.py:145
  53.6 0.3 convert_element_type.66.white_ref
  54.0 3.6 %shard_map.38 = bf16[32,2,16,256]{3,2,1,0:T(8,128)(2,1)S(1)} custom-call(s32[32]{0:T(128)S(1)} %get-tuple-element.30.offsets_ref, s32[1]{0:T(128)} %constant.111.clone.1.base_ref, f32[144,16,256]{2,1,0:T(8,128)S(1)} %convert_element_type.66.white_ref), custom_call_target="tpu_custom_call" | custom-call | flops 2147483648 | bytes 3407872 | tf_op jit(solution)/shard_map/pallas_call | solution.py:62
  57.6 1.1 %collective-permute-start.11 = (bf16[32,2,16,256]{3,2,1,0:T(8,128)(2,1)S(1)}, bf16[32,2,16,256]{3,2,1,0:T(8,128)(2,1)S(1)}, u32[]{:S(2)}, u32[]{:S(2)}) collective-permute-start(bf16[32,2,16,256]{3,2,1,0:T(8,128)(2,1)S(1)} %shard_map.38), channel_id=1, source_target_pairs={{0,2},{1,3},{2,0},{3,1},{4,6},{5,7},{6,4},{7,5},{8,10},{9,11},{10,... | collective-permute-start | bytes 1572872 | tf_op jit(solution)/shard_map/ppermute | solution.py:165
  58.7 3.6 %shard_map.39 = bf16[32,2,16,256]{3,2,1,0:T(8,128)(2,1)S(1)} custom-call(s32[32]{0:T(128)S(1)} %get-tuple-element.32.offsets_ref, s32[1]{0:T(128)} %constant.111.clone.1.base_ref, f32[144,16,256]{2,1,0:T(8,128)S(1)} %convert_element_type.66.white_ref), custom_call_target="tpu_custom_call" | custom-call | flops 2147483648 | bytes 3407872 | tf_op jit(solution)/shard_map/pallas_call | solution.py:62
  62.4 3.6 %shard_map.37 = bf16[32,2,16,256]{3,2,1,0:T(8,128)(2,1)S(1)} custom-call(s32[32]{0:T(128)S(1)} %get-tuple-element.29.offsets_ref, s32[1]{0:T(128)} %constant.111.clone.1.base_ref, f32[144,16,256]{2,1,0:T(8,128)S(1)} %convert_element_type.66.white_ref), custom_call_target="tpu_custom_call" | custom-call | flops 2147483648 | bytes 3407872 | tf_op jit(solution)/shard_map/pallas_call | solution.py:62
  66.0 0.5 collective-permute-start.10
  66.6 3.6 %shard_map.40 = bf16[32,2,16,256]{3,2,1,0:T(8,128)(2,1)S(1)} custom-call(s32[32]{0:T(128)S(1)} %get-tuple-element.31.offsets_ref, s32[1]{0:T(128)} %constant.111.clone.1.base_ref, f32[144,16,256]{2,1,0:T(8,128)S(1)} %convert_element_type.66.white_ref), custom_call_target="tpu_custom_call" | custom-call | flops 2147483648 | bytes 3407872 | tf_op jit(solution)/shard_map/pallas_call | solution.py:62
  70.2 0.4 convolution_bitcast_fusion
  70.6 0.2 collective-permute-done.11
  70.8 0.4 convolution_bitcast_fusion.2
  71.3 9.2 %collective-permute-done.12 = bf16[32,2,16,256]{3,2,1,0:T(8,128)(2,1)S(1)} collective-permute-done((bf16[32,2,16,256]{3,2,1,0:T(8,128)(2,1)S(1)}, bf16[32,2,16,256]{3,2,1,0:T(8,128)(2,1)S(1)}, u32[]{:S(2)}, u32[]{:S(2)}) %collective-permute-start.12) | collective-permute-done | bytes 524320 | tf_op jit(solution)/shard_map/ppermute | solution.py:165
  80.5 0.4 convolution_bitcast_fusion.1
  80.9 1.3 %fusion.11 = bf16[32,16,512]{2,1,0:T(8,128)(2,1)} fusion(f32[32,16,512]{2,1,0:T(8,128)S(1)} %convolution_bitcast_fusion, f32[32,16,512]{2,1,0:T(8,128)S(1)} %convolution_bitcast_fusion.1, f32[32,16,512]{2,1,0:T(8,128)S(1)} %convolution_bitcast_fusion.2, bf16[32,2,16,256]{3,2,1,0:T(8,128)(2,1)S(1)} %collective-permute-done.10, s32[]{:T(128)S(6)} %select_n.110, ...), kind=kOutput, calls=%fused_computation.25 | convolution fusion | flops 270794752 | bytes 6291460 | tf_op jit(solution)/shard_map/opck,pkl->ocl/dot_general | solution.py:168
  (27 shorter events, 0.5 us)
Async XLA Ops:
  13.4 6.1 %copy-start = (s32[1024]{0:T(1024)S(1)}, s32[1024]{0:T(1024)}, u32[]{:S(2)}) copy-start(s32[1024]{0:T(1024)} %param.4) | copy-start | bytes 12292
  14.5 6.7 %copy-start.1 = (s32[128]{0:T(128)S(1)}, s32[128]{0:T(128)}, u32[]{:S(2)}) copy-start(s32[128]{0:T(128)} %param.5) | copy-start | bytes 1540
  15.1 7.3 %collective-permute-start = (bf16[16,2,2,256]{3,2,1,0:T(2,128)(2,1)S(1)}, bf16[16,2,2,256]{3,2,1,0:T(2,128)(2,1)S(1)}, u32[]{:S(2)}, u32[]{:S(2)}) collective-permute-start(bf16[16,2,2,256]{3,2,1,0:T(2,128)(2,1)S(1)} %get-tuple-element.18), channel_id=1, source_target_pairs={{0,1},{1,2},{2,3},{3,0},{4,5},{5,6},{6,7},{7,4},{8,9},{9,10},{10,1... | collective-permute-start | bytes 98312 | tf_op jit(solution)/shard_map/ppermute | solution.py:135
  15.6 6.8 %collective-permute-start.1 = (bf16[16,2,2,256]{3,2,1,0:T(2,128)(2,1)S(1)}, bf16[16,2,2,256]{3,2,1,0:T(2,128)(2,1)S(1)}, u32[]{:S(2)}, u32[]{:S(2)}) collective-permute-start(bf16[16,2,2,256]{3,2,1,0:T(2,128)(2,1)S(1)} %get-tuple-element.17), channel_id=1, source_target_pairs={{0,2},{1,3},{2,0},{3,1},{4,6},{5,7},{6,4},{7,5},{8,10},{9,11},{10,... | collective-permute-start | bytes 98312 | tf_op jit(solution)/shard_map/ppermute | solution.py:135
  18.1 4.3 %collective-permute-start.2 = (bf16[16,2,2,256]{3,2,1,0:T(2,128)(2,1)S(1)}, bf16[16,2,2,256]{3,2,1,0:T(2,128)(2,1)S(1)}, u32[]{:S(2)}, u32[]{:S(2)}) collective-permute-start(bf16[16,2,2,256]{3,2,1,0:T(2,128)(2,1)S(1)} %get-tuple-element.16), channel_id=1, source_target_pairs={{0,3},{1,0},{2,1},{3,2},{4,7},{5,4},{6,5},{7,6},{8,11},{9,8},{10,9... | collective-permute-start | bytes 98312 | tf_op jit(solution)/shard_map/ppermute | solution.py:135
  22.6 6.9 %collective-permute-start.3 = (bf16[16,16,256]{2,1,0:T(8,128)(2,1)S(1)}, bf16[16,16,256]{2,1,0:T(8,128)(2,1)S(1)}, u32[]{:S(2)}, u32[]{:S(2)}) collective-permute-start(bf16[16,16,256]{2,1,0:T(8,128)(2,1)S(1)} %bitcast.73), channel_id=1, source_target_pairs={{4,0},{8,4},{12,8},{16,12},{20,16},{24,20},{28,24},{5,1},{9,5},{13... | collective-permute-start | bytes 393224 | tf_op jit(solution)/shard_map/ppermute | solution.py:145
  23.9 9.3 %collective-permute-start.4 = (bf16[16,16,256]{2,1,0:T(8,128)(2,1)S(1)}, bf16[16,16,256]{2,1,0:T(8,128)(2,1)S(1)}, u32[]{:S(2)}, u32[]{:S(2)}) collective-permute-start(bf16[16,16,256]{2,1,0:T(8,128)(2,1)S(1)} %bitcast.74), channel_id=1, source_target_pairs={{8,0},{12,4},{16,8},{20,12},{24,16},{28,20},{9,1},{13,5},{17,9},{2... | collective-permute-start | bytes 393224 | tf_op jit(solution)/shard_map/ppermute | solution.py:145
  25.3 10.7 %collective-permute-start.5 = (bf16[16,16,256]{2,1,0:T(8,128)(2,1)S(1)}, bf16[16,16,256]{2,1,0:T(8,128)(2,1)S(1)}, u32[]{:S(2)}, u32[]{:S(2)}) collective-permute-start(bf16[16,16,256]{2,1,0:T(8,128)(2,1)S(1)} %bitcast.75), channel_id=1, source_target_pairs={{12,0},{16,4},{20,8},{24,12},{28,16},{13,1},{17,5},{21,9},{25,13},... | collective-permute-start | bytes 393224 | tf_op jit(solution)/shard_map/ppermute | solution.py:145
  26.6 24.6 %collective-permute-start.6 = (bf16[16,16,256]{2,1,0:T(8,128)(2,1)S(1)}, bf16[16,16,256]{2,1,0:T(8,128)(2,1)S(1)}, u32[]{:S(2)}, u32[]{:S(2)}) collective-permute-start(bf16[16,16,256]{2,1,0:T(8,128)(2,1)S(1)} %bitcast.76), channel_id=1, source_target_pairs={{16,0},{20,4},{24,8},{28,12},{17,1},{21,5},{25,9},{29,13},{18,2},{... | collective-permute-start | bytes 393224 | tf_op jit(solution)/shard_map/ppermute | solution.py:145
  27.9 25.7 %collective-permute-start.7 = (bf16[16,16,256]{2,1,0:T(8,128)(2,1)S(1)}, bf16[16,16,256]{2,1,0:T(8,128)(2,1)S(1)}, u32[]{:S(2)}, u32[]{:S(2)}) collective-permute-start(bf16[16,16,256]{2,1,0:T(8,128)(2,1)S(1)} %bitcast.77), channel_id=1, source_target_pairs={{20,0},{24,4},{28,8},{21,1},{25,5},{29,9},{22,2},{26,6},{30,10},{2... | collective-permute-start | bytes 393224 | tf_op jit(solution)/shard_map/ppermute | solution.py:145
  29.5 24.1 %collective-permute-start.8 = (bf16[16,16,256]{2,1,0:T(8,128)(2,1)S(1)}, bf16[16,16,256]{2,1,0:T(8,128)(2,1)S(1)}, u32[]{:S(2)}, u32[]{:S(2)}) collective-permute-start(bf16[16,16,256]{2,1,0:T(8,128)(2,1)S(1)} %bitcast.78), channel_id=1, source_target_pairs={{24,0},{28,4},{25,1},{29,5},{26,2},{30,6},{27,3},{31,7}} | collective-permute-start | bytes 393224 | tf_op jit(solution)/shard_map/ppermute | solution.py:145
  33.3 20.3 %collective-permute-start.9 = (bf16[16,16,256]{2,1,0:T(8,128)(2,1)S(1)}, bf16[16,16,256]{2,1,0:T(8,128)(2,1)S(1)}, u32[]{:S(2)}, u32[]{:S(2)}) collective-permute-start(bf16[16,16,256]{2,1,0:T(8,128)(2,1)S(1)} %bitcast.79), channel_id=1, source_target_pairs={{28,0},{29,1},{30,2},{31,3}} | collective-permute-start | bytes 393224 | tf_op jit(solution)/shard_map/ppermute | solution.py:145
  57.6 13.2 %collective-permute-start.11 = (bf16[32,2,16,256]{3,2,1,0:T(8,128)(2,1)S(1)}, bf16[32,2,16,256]{3,2,1,0:T(8,128)(2,1)S(1)}, u32[]{:S(2)}, u32[]{:S(2)}) collective-permute-start(bf16[32,2,16,256]{3,2,1,0:T(8,128)(2,1)S(1)} %shard_map.38), channel_id=1, source_target_pairs={{0,2},{1,3},{2,0},{3,1},{4,6},{5,7},{6,4},{7,5},{8,10},{9,11},{10,... | collective-permute-start | bytes 1572872 | tf_op jit(solution)/shard_map/ppermute | solution.py:165
  62.3 18.2 %collective-permute-start.12 = (bf16[32,2,16,256]{3,2,1,0:T(8,128)(2,1)S(1)}, bf16[32,2,16,256]{3,2,1,0:T(8,128)(2,1)S(1)}, u32[]{:S(2)}, u32[]{:S(2)}) collective-permute-start(bf16[32,2,16,256]{3,2,1,0:T(8,128)(2,1)S(1)} %shard_map.39), channel_id=1, source_target_pairs={{0,3},{1,0},{2,1},{3,2},{4,7},{5,4},{6,5},{7,6},{8,11},{9,8},{10,9... | collective-permute-start | bytes 1572872 | tf_op jit(solution)/shard_map/ppermute | solution.py:165
  66.0 14.9 %collective-permute-start.10 = (bf16[32,2,16,256]{3,2,1,0:T(8,128)(2,1)S(1)}, bf16[32,2,16,256]{3,2,1,0:T(8,128)(2,1)S(1)}, u32[]{:S(2)}, u32[]{:S(2)}) collective-permute-start(bf16[32,2,16,256]{3,2,1,0:T(8,128)(2,1)S(1)} %shard_map.37), channel_id=1, source_target_pairs={{0,1},{1,2},{2,3},{3,0},{4,5},{5,6},{6,7},{7,4},{8,9},{9,10},{10,1... | collective-permute-start | bytes 1572872 | tf_op jit(solution)/shard_map/ppermute | solution.py:165
